TPU v7x, 512 devices: a whole 4x4x16 slice. The times are simulated.
512 devices in a mesh: row: 32 (over z, y_lo), col: 16 (over x, y_hi, core).
Axes of the slice: x: 4, y: 4 (y_hi: 2, y_lo: 2; y = y_hi * 2 + y_lo), z: 16, core: 2. Of those that a mesh axis runs over, the one named last changes fastest.
Arguments:
- inputs: bfloat16 [1, 256, 256, 1024], P(None, 'row', 'col'), may hold values from -6 to 6
- norm_gain: float32 [1024], replicated, may hold values from 0.1 to 1.9
- w_query: bfloat16 [1024, 512], P('row'), may hold values from -8 to 8
- w_keyvalue: bfloat16 [1024, 1024], P('row'), may hold values from -0.1875 to 0.1875
- w_output: bfloat16 [512, 1024], P('row'), may hold values from -0.25 to 0.25
- out_grad: bfloat16 [1, 256, 256, 1024], P(None, 'row', 'col'), may hold values from -6 to 6
Outputs:
- layer_out: bfloat16 [1, 256, 256, 1024], P(None, 'row', 'col')
- in_grad: bfloat16 [1, 256, 256, 1024], P(None, 'row', 'col')
- keyvalue_grad: float32 [1024, 1024], P('row')
All inputs are finite; a program needn't handle non-finite values.
Results may differ from a plain program's by a relative error of at most 0.012.
The roundings to bfloat16 on the way count: a program that leaves them out, or rounds other values in their place, can miss the bound.
Values may be sent and summed in bfloat16 or wider, within the bound.
No kernel may reach another device: no remote copies, remote signals or barrier semaphores. Data moves between devices by JAX's collectives and lax.ppermute only.
A program may use at most 64 MiB of HBM per device.

v0:
```python
import math

import jax
import jax.numpy as jnp
from jax import lax
from jax.sharding import PartitionSpec as P

HEADS = 8
RADIUS = 6


EPS = 1e-05
MASKED = -1e30


def shifted(value, axis, steps):
    count = lax.axis_size(axis)
    first, last = (max(0, -steps), min(count, count - steps))
    return lax.ppermute(value, axis, [(source, source + steps) for source in range(first, last)])


def with_halo(block, sides, width):
    for axis, dim in sides:
        count = lax.axis_size(axis)
        forward = [(i, i + 1) for i in range(count - 1)]
        backward = [(target, source) for source, target in forward]
        low = lax.ppermute(
            lax.slice_in_dim(block, block.shape[dim] - width, None, axis=dim), axis, forward
        )
        high = lax.ppermute(lax.slice_in_dim(block, 0, width, axis=dim), axis, backward)
        block = jnp.concatenate([low, block, high], axis=dim)
    return block


def normalize(inputs, norm_gain):
    values = inputs.astype(jnp.float32)
    center = values - jnp.mean(values, axis=-1, keepdims=True)
    spread = lax.rsqrt(jnp.mean(center * center, axis=-1, keepdims=True) + EPS)
    standard = center * spread
    return (standard, spread, (standard * norm_gain).astype(jnp.bfloat16))


def window_mask(row_start, col_start, tile_rows, tile_cols, height, map_width):
    ext_rows = tile_rows + 2 * RADIUS
    ext_cols = tile_cols + 2 * RADIUS
    query_pos = jnp.arange(tile_rows * tile_cols, dtype=jnp.int32)
    query_row = query_pos // tile_cols
    query_col = query_pos % tile_cols
    ext_pos = jnp.arange(ext_rows * ext_cols, dtype=jnp.int32)
    ext_row = ext_pos // ext_cols
    ext_col = ext_pos % ext_cols
    nearby = (jnp.abs(ext_row[None, :] - RADIUS - query_row[:, None]) <= RADIUS) & (
        jnp.abs(ext_col[None, :] - RADIUS - query_col[:, None]) <= RADIUS
    )
    global_row = row_start + ext_row - RADIUS
    global_col = col_start + ext_col - RADIUS
    inside = (
        (global_row >= 0) & (global_row < height) & (global_col >= 0) & (global_col < map_width)
    )
    return nearby & inside[None, :]


def tile_forward(queries, keyvalue_ext, allowed):
    batches, query_count, inner_width = queries.shape
    head_size = inner_width // HEADS
    query_heads = queries.reshape(batches, query_count, HEADS, head_size)
    key_heads = keyvalue_ext[:, :, :inner_width].reshape(batches, -1, HEADS, head_size)
    value_heads = keyvalue_ext[:, :, inner_width:].reshape(batches, -1, HEADS, head_size)
    scores = jnp.einsum(
        "bqhd,bkhd->bhqk", query_heads, key_heads, preferred_element_type=jnp.float32
    ) / math.sqrt(head_size)
    scores = jnp.where(allowed, scores, MASKED)
    row_max = jnp.max(scores, axis=-1, keepdims=True)
    exponent = jnp.exp(scores - row_max)
    soft = exponent / jnp.sum(exponent, axis=-1, keepdims=True)
    rounded = soft.astype(jnp.bfloat16)
    attended = jnp.einsum(
        "bhqk,bkhd->bqhd", rounded, value_heads, preferred_element_type=jnp.float32
    )
    return (attended.astype(jnp.bfloat16).reshape(batches, query_count, inner_width), soft, rounded)


def tile_backward(queries, keyvalue_ext, soft, rounded, inner_grad):
    batches, query_count, inner_width = queries.shape
    head_size = inner_width // HEADS
    query_heads = queries.reshape(batches, query_count, HEADS, head_size)
    key_heads = keyvalue_ext[:, :, :inner_width].reshape(batches, -1, HEADS, head_size)
    value_heads = keyvalue_ext[:, :, inner_width:].reshape(batches, -1, HEADS, head_size)
    grad_heads = inner_grad.reshape(batches, query_count, HEADS, head_size)
    prob_grad = jnp.einsum(
        "bqhd,bkhd->bhqk", grad_heads, value_heads, preferred_element_type=jnp.float32
    )
    row_dot = jnp.sum(soft * prob_grad, axis=-1, keepdims=True)
    score_grad = (soft * (prob_grad - row_dot) / math.sqrt(head_size)).astype(jnp.bfloat16)
    query_grad = jnp.einsum(
        "bhqk,bkhd->bqhd", score_grad, key_heads, preferred_element_type=jnp.float32
    )
    key_grad = jnp.einsum(
        "bhqk,bqhd->bkhd", score_grad, query_heads, preferred_element_type=jnp.float32
    )
    value_grad = jnp.einsum(
        "bhqk,bqhd->bkhd", rounded, grad_heads, preferred_element_type=jnp.float32
    )
    ext_count = key_grad.shape[1]
    joined = jnp.concatenate(
        [
            key_grad.reshape(batches, ext_count, inner_width),
            value_grad.reshape(batches, ext_count, inner_width),
        ],
        axis=-1,
    )
    return (query_grad.astype(jnp.bfloat16).reshape(batches, query_count, inner_width), joined)


def fold_cols(extended):
    left_strip = extended[:, :, :RADIUS]
    right_strip = extended[:, :, extended.shape[2] - RADIUS :]
    middle = extended[:, :, RADIUS : extended.shape[2] - RADIUS]
    from_right = shifted(left_strip, "col", -1)
    from_left = shifted(right_strip, "col", 1)
    inner_cols = middle.shape[2]
    return (
        middle
        + jnp.pad(from_left, ((0, 0), (0, 0), (0, inner_cols - RADIUS), (0, 0)))
        + jnp.pad(from_right, ((0, 0), (0, 0), (inner_cols - RADIUS, 0), (0, 0)))
    )


def fold_rows(extended):
    upper_strip = extended[:, :RADIUS]
    lower_strip = extended[:, extended.shape[1] - RADIUS :]
    middle = extended[:, RADIUS : extended.shape[1] - RADIUS]
    from_below = shifted(upper_strip, "row", -1)
    from_above = shifted(lower_strip, "row", 1)
    inner_rows = middle.shape[1]
    return (
        middle
        + jnp.pad(from_above, ((0, 0), (0, inner_rows - RADIUS), (0, 0), (0, 0)))
        + jnp.pad(from_below, ((0, 0), (inner_rows - RADIUS, 0), (0, 0), (0, 0)))
    )


def local(inputs, norm_gain, w_query, w_keyvalue, w_output, out_grad):
    batches, tile_rows, tile_cols, model_width = inputs.shape
    ext_rows = tile_rows + 2 * RADIUS
    ext_cols = tile_cols + 2 * RADIUS
    standard, spread, normed = normalize(inputs, norm_gain)
    flat_norm = normed.reshape(-1, model_width)
    full_query, full_keyvalue, full_output = (
        lax.all_gather(w_query, "row", axis=0, tiled=True),
        lax.all_gather(w_keyvalue, "row", axis=0, tiled=True),
        lax.all_gather(w_output, "row", axis=0, tiled=True),
    )
    inner_width = full_query.shape[1]
    queries = jnp.dot(flat_norm, full_query, preferred_element_type=jnp.float32).astype(
        jnp.bfloat16
    )
    queries = queries.reshape(batches, tile_rows * tile_cols, inner_width)
    keyvalue = jnp.dot(flat_norm, full_keyvalue, preferred_element_type=jnp.float32).astype(
        jnp.bfloat16
    )
    keyvalue = keyvalue.reshape(batches, tile_rows, tile_cols, 2 * inner_width)
    keyvalue_ext = with_halo(keyvalue, (("row", 1), ("col", 2)), RADIUS)
    keyvalue_ext = keyvalue_ext.reshape(batches, ext_rows * ext_cols, 2 * inner_width)
    allowed = window_mask(
        lax.axis_index("row") * tile_rows,
        lax.axis_index("col") * tile_cols,
        tile_rows,
        tile_cols,
        tile_rows * lax.axis_size("row"),
        tile_cols * lax.axis_size("col"),
    )
    attended, soft, rounded = tile_forward(queries, keyvalue_ext, allowed)
    projected = jnp.dot(
        attended.reshape(-1, inner_width), full_output, preferred_element_type=jnp.float32
    )
    layer_out = (inputs.astype(jnp.float32) + projected.reshape(inputs.shape)).astype(jnp.bfloat16)
    flat_grad = out_grad.reshape(-1, model_width)
    inner_grad = lax.dot_general(
        flat_grad, full_output, (((1,), (1,)), ((), ())), preferred_element_type=jnp.float32
    ).astype(jnp.bfloat16)
    inner_grad = inner_grad.reshape(batches, tile_rows * tile_cols, inner_width)
    query_grad, keyvalue_part = tile_backward(queries, keyvalue_ext, soft, rounded, inner_grad)
    keyvalue_part = keyvalue_part.reshape(batches, ext_rows, ext_cols, 2 * inner_width)
    owned = fold_rows(fold_cols(keyvalue_part))
    token_grad = owned.astype(jnp.bfloat16).reshape(-1, 2 * inner_width)
    rows_part = lax.psum_scatter(
        lax.dot_general(
            flat_norm, token_grad, (((0,), (0,)), ((), ())), preferred_element_type=jnp.float32
        ),
        "row",
        scatter_dimension=0,
        tiled=True,
    )
    keyvalue_grad = lax.psum(rows_part, "col")
    normed_grad = lax.dot_general(
        query_grad.reshape(-1, inner_width),
        full_query,
        (((1,), (1,)), ((), ())),
        preferred_element_type=jnp.float32,
    )
    normed_grad = normed_grad + lax.dot_general(
        token_grad, full_keyvalue, (((1,), (1,)), ((), ())), preferred_element_type=jnp.float32
    )
    gained = normed_grad.reshape(inputs.shape) * norm_gain
    in_grad = out_grad.astype(jnp.float32) + spread * (
        gained
        - jnp.mean(gained, axis=-1, keepdims=True)
        - standard * jnp.mean(gained * standard, axis=-1, keepdims=True)
    )
    return (layer_out, in_grad.astype(jnp.bfloat16), keyvalue_grad)


def solution(mesh):
    return jax.shard_map(
        local,
        mesh=mesh,
        in_specs=(
            P(None, "row", "col", None),
            P(),
            P("row", None),
            P("row", None),
            P("row", None),
            P(None, "row", "col", None),
        ),
        out_specs=(P(None, "row", "col", None), P(None, "row", "col", None), P("row", None)),
        check_vma=False,
    )
```

profile of v0, /device:TPU:1, one launch (start us, length us, event | category | flops | bytes accessed | tf_op | source)
XLA Modules:
  0.0 792.2 jit_solution(14434119171756185005)
XLA Ops:
  13.3 115.3 %all-gather.4.cloned.1.call-done = bf16[1024,1024]{1,0:T(8,128)(2,1)} async-done(((bf16[32,1024]{1,0:T(8,128)(2,1)}), bf16[1024,1024]{1,0:T(8,128)(2,1)}) %all-gather.4.cloned.1.call-update) | async-done | bytes 2097168 | tf_op jit(solution)/shard_map/all_gather | solution.py:151
  128.6 2.0 convolution_convert_fusion
  130.7 2.2 collective-permute-start
  132.9 1.3 collective-permute-start.1
  134.2 126.6 %all-gather.8.cloned.1.call-done = bf16[512,1024]{1,0:T(8,128)(2,1)} async-done(((bf16[16,1024]{1,0:T(8,128)(2,1)}), bf16[512,1024]{1,0:T(8,128)(2,1)}) %all-gather.8.cloned.1.call-update) | async-done | bytes 1048592 | tf_op jit(solution)/shard_map/all_gather | solution.py:152
  260.8 1.7 convolution_convert_fusion.1
  262.9 26.0 %collective-permute-start.2 = (bf16[1,20,6,1024]{3,2,1,0:T(8,128)(2,1)S(1)}, bf16[1,20,6,1024]{3,2,1,0:T(8,128)(2,1)S(1)}, u32[]{:S(2)}, u32[]{:S(2)}) collective-permute-start(bf16[1,20,6,1024]{3,2,1,0:T(8,128)(2,1)S(1)} %get-tuple-element.9), channel_id=1, source_target_pairs={{0,1},{1,2},{2,3},{3,4},{4,5},{5,6},{6,7},{7,8},{8,9},{9,10},{10,1... | collective-permute-start | bytes 737288 | tf_op jit(solution)/shard_map/ppermute | solution.py:27
  288.8 1.9 collective-permute-start.3
  290.8 102.0 %all-gather.6.cloned.1.call-done = bf16[1024,512]{1,0:T(8,128)(2,1)} async-done(((bf16[32,512]{1,0:T(8,128)(2,1)}), bf16[1024,512]{1,0:T(8,128)(2,1)}) %all-gather.6.cloned.1.call-update) | async-done | bytes 1048592 | tf_op jit(solution)/shard_map/all_gather | solution.py:150
  392.8 1.5 convolution_convert_fusion.2
  396.1 2.0 fusion.76
  398.1 2.3 fusion.75
  400.5 2.3 convolution_bitcast_fusion.1
  402.8 2.5 copy.31
  405.4 1.4 concatenate.17
  406.8 5.7 fusion.12
  412.4 2.5 copy.30
  415.0 2.4 concatenate.16
  417.4 2.5 constant_dynamic-update-slice_fusion.1
  421.6 26.0 %collective-permute-start.4 = (f32[1,20,6,1024]{3,0,2,1:T(1,128)S(1)}, f32[1,20,6,1024]{3,0,2,1:T(1,128)S(1)}, u32[]{:S(2)}, u32[]{:S(2)}) collective-permute-start(f32[1,20,6,1024]{3,0,2,1:T(1,128)S(1)} %get-tuple-element.3), channel_id=1, source_target_pairs={{0,1},{1,2},{2,3},{3,4},{4,5},{5,6},{6,7},{7,8},{8,9},{9,10},{10,1... | collective-permute-start | bytes 1474568 | tf_op jit(solution)/shard_map/ppermute | solution.py:19
  447.5 2.1 collective-permute-start.5
  449.7 9.1 %collective-permute-done.4 = f32[1,20,6,1024]{3,0,2,1:T(1,128)S(1)} collective-permute-done((f32[1,20,6,1024]{3,0,2,1:T(1,128)S(1)}, f32[1,20,6,1024]{3,0,2,1:T(1,128)S(1)}, u32[]{:S(2)}, u32[]{:S(2)}) %collective-permute-start.4) | collective-permute-done | bytes 491552 | tf_op jit(solution)/shard_map/ppermute | solution.py:19
  459.2 1.5 fusion.15
  461.2 1.3 collective-permute-start.6
  463.8 11.6 %collective-permute-done.6 = f32[1,6,16,1024]{3,0,2,1:T(1,128)S(1)} collective-permute-done((f32[1,6,16,1024]{3,0,2,1:T(1,128)S(1)}, f32[1,6,16,1024]{3,0,2,1:T(1,128)S(1)}, u32[]{:S(2)}, u32[]{:S(2)}) %collective-permute-start.6) | collective-permute-done | bytes 393248 | tf_op jit(solution)/shard_map/ppermute | solution.py:19
  476.9 2.7 convolution_bitcast_fusion
  480.6 2.3 fusion.26
  483.4 5.5 fusion.18
  490.0 1.8 fusion.77
  492.7 116.1 %reduce-scatter.2.cloned.1.call-done = f32[32,1024]{1,0:T(8,128)} async-done(((f32[1024,1024]{1,0:T(8,128)}), f32[32,1024]{1,0:T(8,128)}) %reduce-scatter.2.cloned.1.call-update) | async-done | bytes 131088 | tf_op jit(solution)/shard_map/reduce_scatter | solution.py:187
  609.8 174.3 %all-reduce.6.cloned.1.call-done = f32[32,1024]{1,0:T(8,128)} async-done(((f32[32,1024]{1,0:T(8,128)}), f32[32,1024]{1,0:T(8,128)}) %all-reduce.6.cloned.1.call-update) | async-done | bytes 131088 | tf_op jit(solution)/shard_map/psum | solution.py:195
  784.1 1.6 copy.38
  (82 shorter events, 17.9 us)
Async XLA Ops:
  7.2 121.5 %all-gather.4.cloned.1.call-start = ((), (), s32[]{:S(2)}) async-start(), calls=%async_computation.1 | async-start | bytes 2162688 | tf_op jit(solution)/shard_map/all_gather | solution.py:151
  7.9 252.9 %all-gather.8.cloned.1.call-start = ((), (), s32[]{:S(2)}) async-start(), calls=%async_computation.3 | async-start | bytes 1081344 | tf_op jit(solution)/shard_map/all_gather | solution.py:152
  8.6 384.1 %all-gather.6.cloned.1.call-start = ((), (), s32[]{:S(2)}) async-start(), calls=%async_computation.2 | async-start | bytes 1081344 | tf_op jit(solution)/shard_map/all_gather | solution.py:150
  9.4 599.4 %reduce-scatter.2.cloned.1.call-start = ((), (), s32[]{:S(2)}) async-start(), calls=%async_computation.4 | async-start | bytes 4325376 | tf_op jit(solution)/shard_map/reduce_scatter | solution.py:187
  9.5 251.3 %copy-start.8 = (bf16[1,8,16,1024]{3,2,1,0:T(8,128)(2,1)S(1)}, bf16[1,8,16,1024]{3,2,1,0:T(8,128)(2,1)}, u32[]{:S(2)}) copy-start(bf16[1,8,16,1024]{3,2,1,0:T(8,128)(2,1)} %param.11) | copy-start | bytes 786436
  13.3 379.5 %copy-start.6 = (bf16[1,8,16,1024]{3,2,1,0:T(8,128)(2,1)}, bf16[1,8,16,1024]{3,2,1,0:T(8,128)(2,1)S(1)}, u32[]{:S(2)}) copy-start(bf16[1,8,16,1024]{3,2,1,0:T(8,128)(2,1)S(1)} %fusion.35) | copy-start | bytes 786436
  130.7 131.9 %collective-permute-start = (bf16[1,6,16,1024]{3,2,1,0:T(8,128)(2,1)S(1)}, bf16[1,6,16,1024]{3,2,1,0:T(8,128)(2,1)S(1)}, u32[]{:S(2)}, u32[]{:S(2)}) collective-permute-start(bf16[1,6,16,1024]{3,2,1,0:T(8,128)(2,1)S(1)} %get-tuple-element.11), channel_id=1, source_target_pairs={{0,16},{16,32},{32,48},{48,64},{64,80},{80,96},{96,112},{112,128},... | collective-permute-start | bytes 589832 | tf_op jit(solution)/shard_map/ppermute | solution.py:27
  132.9 129.8 %collective-permute-start.1 = (bf16[1,6,16,1024]{3,2,1,0:T(8,128)(2,1)S(1)}, bf16[1,6,16,1024]{3,2,1,0:T(8,128)(2,1)S(1)}, u32[]{:S(2)}, u32[]{:S(2)}) collective-permute-start(bf16[1,6,16,1024]{3,2,1,0:T(8,128)(2,1)S(1)} %get-tuple-element.12), channel_id=1, source_target_pairs={{16,0},{32,16},{48,32},{64,48},{80,64},{96,80},{112,96},{128,112},... | collective-permute-start | bytes 589832 | tf_op jit(solution)/shard_map/ppermute | solution.py:30
  262.9 131.6 %collective-permute-start.2 = (bf16[1,20,6,1024]{3,2,1,0:T(8,128)(2,1)S(1)}, bf16[1,20,6,1024]{3,2,1,0:T(8,128)(2,1)S(1)}, u32[]{:S(2)}, u32[]{:S(2)}) collective-permute-start(bf16[1,20,6,1024]{3,2,1,0:T(8,128)(2,1)S(1)} %get-tuple-element.9), channel_id=1, source_target_pairs={{0,1},{1,2},{2,3},{3,4},{4,5},{5,6},{6,7},{7,8},{8,9},{9,10},{10,1... | collective-permute-start | bytes 737288 | tf_op jit(solution)/shard_map/ppermute | solution.py:27
  288.8 105.7 %collective-permute-start.3 = (bf16[1,20,6,1024]{3,2,1,0:T(8,128)(2,1)S(1)}, bf16[1,20,6,1024]{3,2,1,0:T(8,128)(2,1)S(1)}, u32[]{:S(2)}, u32[]{:S(2)}) collective-permute-start(bf16[1,20,6,1024]{3,2,1,0:T(8,128)(2,1)S(1)} %get-tuple-element.10), channel_id=1, source_target_pairs={{1,0},{2,1},{3,2},{4,3},{5,4},{6,5},{7,6},{8,7},{9,8},{10,9},{11,1... | collective-permute-start | bytes 737288 | tf_op jit(solution)/shard_map/ppermute | solution.py:30
  394.5 6.0 copy-start.13
  395.8 4.7 copy-start.11
  396.1 4.4 copy-start.4
  421.6 37.2 %collective-permute-start.4 = (f32[1,20,6,1024]{3,0,2,1:T(1,128)S(1)}, f32[1,20,6,1024]{3,0,2,1:T(1,128)S(1)}, u32[]{:S(2)}, u32[]{:S(2)}) collective-permute-start(f32[1,20,6,1024]{3,0,2,1:T(1,128)S(1)} %get-tuple-element.3), channel_id=1, source_target_pairs={{0,1},{1,2},{2,3},{3,4},{4,5},{5,6},{6,7},{7,8},{8,9},{9,10},{10,1... | collective-permute-start | bytes 1474568 | tf_op jit(solution)/shard_map/ppermute | solution.py:19
  447.5 11.7 %collective-permute-start.5 = (f32[1,20,6,1024]{3,0,2,1:T(1,128)S(1)}, f32[1,20,6,1024]{3,0,2,1:T(1,128)S(1)}, u32[]{:S(2)}, u32[]{:S(2)}) collective-permute-start(f32[1,20,6,1024]{3,0,2,1:T(1,128)S(1)} %get-tuple-element.4), channel_id=1, source_target_pairs={{1,0},{2,1},{3,2},{4,3},{5,4},{6,5},{7,6},{8,7},{9,8},{10,9},{11,1... | collective-permute-start | bytes 1474568 | tf_op jit(solution)/shard_map/ppermute | solution.py:19
  460.7 16.2 %copy-start.7 = (bf16[1,8,16,1024]{3,2,1,0:T(8,128)(2,1)S(1)}, bf16[1,8,16,1024]{3,2,1,0:T(8,128)(2,1)}, u32[]{:S(2)}) copy-start(bf16[1,8,16,1024]{3,2,1,0:T(8,128)(2,1)} %copy-done.6) | copy-start | bytes 786436
  461.2 14.2 %collective-permute-start.6 = (f32[1,6,16,1024]{3,0,2,1:T(1,128)S(1)}, f32[1,6,16,1024]{3,0,2,1:T(1,128)S(1)}, u32[]{:S(2)}, u32[]{:S(2)}) collective-permute-start(f32[1,6,16,1024]{3,0,2,1:T(1,128)S(1)} %get-tuple-element.5), channel_id=1, source_target_pairs={{0,16},{16,32},{32,48},{48,64},{64,80},{80,96},{96,112},{112,128},... | collective-permute-start | bytes 1179656 | tf_op jit(solution)/shard_map/ppermute | solution.py:19
  462.5 12.9 %collective-permute-start.7 = (f32[1,6,16,1024]{3,0,2,1:T(1,128)S(1)}, f32[1,6,16,1024]{3,0,2,1:T(1,128)S(1)}, u32[]{:S(2)}, u32[]{:S(2)}) collective-permute-start(f32[1,6,16,1024]{3,0,2,1:T(1,128)S(1)} %get-tuple-element.6), channel_id=1, source_target_pairs={{16,0},{32,16},{48,32},{64,48},{80,64},{96,80},{112,96},{128,112},... | collective-permute-start | bytes 1179656 | tf_op jit(solution)/shard_map/ppermute | solution.py:19
  476.2 0.7 copy-start.10
  479.5 1.1 copy-start.5
  479.5 1.1 copy-start.14
  479.6 304.6 %all-reduce.6.cloned.1.call-start = ((), (), s32[]{:S(2)}) async-start(), calls=%async_computation.5 | async-start | bytes 262144 | tf_op jit(solution)/shard_map/psum | solution.py:195
  483.4 5.6 copy-start
  483.4 5.6 copy-start.3
  483.4 6.6 copy-start.1
  488.9 2.8 copy-start.2
  489.0 2.9 copy-start.12
  489.0 2.8 copy-start.15
  491.8 117.1 %copy-start.9 = (bf16[1,8,16,1024]{3,2,1,0:T(8,128)(2,1)S(1)}, bf16[1,8,16,1024]{3,2,1,0:T(8,128)(2,1)}, u32[]{:S(2)}) copy-start(bf16[1,8,16,1024]{3,2,1,0:T(8,128)(2,1)} %param.11) | copy-start | bytes 786436
Sparse Core Ops, SparseCore 0:
  10.1 118.4 all-gather.3
  130.7 130.0 all-gather.7
  262.9 129.8 all-gather.5
  479.7 129.0 reduce-scatter.1
  611.5 172.5 all-reduce.5
where the time goes:
time: 793 us; the launch traced here: 792 us
  waiting for transfers between devices  658 us (83%)
  starting transfers between devices  62.2 us (8%)
  matrix products  31.5 us (4%)
  local copies, waits for them, and re-layouts  18.8 us (2%)
  between operations  14.3 us (2%)
    psum x1, waiting for transfers between devices, local(): keyvalue_grad = lax.psum(rows_part, 'col')  174 us
    all_gather x1, waiting for transfers between devices, local(): lax.all_gather(w_output, 'row', axis=0, tiled=True)  127 us
    reduce_scatter x1, waiting for transfers between devices, local(): lax.psum_scatter(lax.dot_general(flat_norm, token_grad, (((0,), (0,)), ((...  116 us
    all_gather x1, waiting for transfers between devices, local(): lax.all_gather(w_keyvalue, 'row', axis=0, tiled=True)  115 us
    all_gather x1, waiting for transfers between devices, local(): lax.all_gather(w_query, 'row', axis=0, tiled=True)  102 us
    ppermute x4, starting transfers between devices, shifted(): lax.ppermute(value, axis, [(source, source + steps) for source in range(f...  30.7 us
    ppermute x2, starting transfers between devices, with_halo(): lax.ppermute(lax.slice_in_dim(block, block.shape[dim] - width, None, axis...  28.1 us
    ppermute x4, waiting for transfers between devices, shifted(): lax.ppermute(value, axis, [(source, source + steps) for source in range(f...  21.1 us
  transfers between devices with their start and end apart: 13, of which 8 were waited for; matrix products, arithmetic and copies ran while one was open for 3% of the time, Pallas kernels for 0%

commit v1 on v0

--- a/solution.py
+++ b/solution.py
@@ -30,6 +30,48 @@
         high = lax.ppermute(lax.slice_in_dim(block, 0, width, axis=dim), axis, backward)
         block = jnp.concatenate([low, block, high], axis=dim)
     return block
+
+
+def partner_swap(value, axis, bit):
+    count = lax.axis_size(axis)
+    return lax.ppermute(value, axis, [(i, i ^ (1 << bit)) for i in range(count)])
+
+
+def low_half(axis, bit):
+    return (lax.axis_index(axis) // (1 << bit)) % 2 == 0
+
+
+def gather_by_bits(block, axis, bits, dim=0):
+    count = lax.axis_size(axis)
+    levels = count.bit_length() - 1
+    shape = block.shape
+    held = block.reshape(shape[:dim] + (1,) * levels + shape[dim:])
+    for bit in bits:
+        place = dim + levels - 1 - bit
+        other = partner_swap(held, axis, bit)
+        held = jnp.where(
+            low_half(axis, bit),
+            jnp.concatenate([held, other], place),
+            jnp.concatenate([other, held], place),
+        )
+    return held.reshape(shape[:dim] + (count * shape[dim],) + shape[dim + 1 :])
+
+
+def scatter_by_bits(total, axis, bits, dim=0):
+    count = lax.axis_size(axis)
+    levels = count.bit_length() - 1
+    shape = total.shape
+    piece = shape[dim] // count
+    held = total.reshape(shape[:dim] + (2,) * levels + (piece,) + shape[dim + 1 :])
+    for bit in bits:
+        place = dim + levels - 1 - bit
+        first = lax.index_in_dim(held, 0, place)
+        second = lax.index_in_dim(held, 1, place)
+        low = low_half(axis, bit)
+        keep = jnp.where(low, first, second)
+        send = jnp.where(low, second, first)
+        held = keep + partner_swap(send, axis, bit)
+    return held.reshape(shape[:dim] + (piece,) + shape[dim + 1 :])
 
 
 def normalize(inputs, norm_gain):
@@ -146,11 +188,18 @@
     ext_cols = tile_cols + 2 * RADIUS
     standard, spread, normed = normalize(inputs, norm_gain)
     flat_norm = normed.reshape(-1, model_width)
-    full_query, full_keyvalue, full_output = (
-        lax.all_gather(w_query, "row", axis=0, tiled=True),
-        lax.all_gather(w_keyvalue, "row", axis=0, tiled=True),
-        lax.all_gather(w_output, "row", axis=0, tiled=True),
-    )
+    row_count = lax.axis_size("row")
+    packed = jnp.concatenate(
+        [w_query.reshape(-1), w_keyvalue.reshape(-1), w_output.reshape(-1)]
+    )
+    row_bits = list(range(row_count.bit_length() - 1))
+    gathered = gather_by_bits(packed, "row", row_bits[::-1]).reshape(row_count, -1)
+    query_size, keyvalue_size = w_query.size, w_keyvalue.size
+    full_query = gathered[:, :query_size].reshape(-1, w_query.shape[1])
+    full_keyvalue = gathered[:, query_size : query_size + keyvalue_size].reshape(
+        -1, w_keyvalue.shape[1]
+    )
+    full_output = gathered[:, query_size + keyvalue_size :].reshape(-1, w_output.shape[1])
     inner_width = full_query.shape[1]
     queries = jnp.dot(flat_norm, full_query, preferred_element_type=jnp.float32).astype(
         jnp.bfloat16
@@ -184,15 +233,13 @@
     keyvalue_part = keyvalue_part.reshape(batches, ext_rows, ext_cols, 2 * inner_width)
     owned = fold_rows(fold_cols(keyvalue_part))
     token_grad = owned.astype(jnp.bfloat16).reshape(-1, 2 * inner_width)
-    rows_part = lax.psum_scatter(
-        lax.dot_general(
-            flat_norm, token_grad, (((0,), (0,)), ((), ())), preferred_element_type=jnp.float32
-        ),
-        "row",
-        scatter_dimension=0,
-        tiled=True,
-    )
-    keyvalue_grad = lax.psum(rows_part, "col")
+    partial = lax.dot_general(
+        flat_norm, token_grad, (((0,), (0,)), ((), ())), preferred_element_type=jnp.float32
+    )
+    col_bits = list(range(lax.axis_size("col").bit_length() - 1))
+    col_part = scatter_by_bits(partial, "col", col_bits, dim=1)
+    rows_part = scatter_by_bits(col_part, "row", row_bits, dim=0)
+    keyvalue_grad = gather_by_bits(rows_part, "col", col_bits[::-1], dim=1)
     normed_grad = lax.dot_general(
         query_grad.reshape(-1, inner_width),
         full_query,

time: 793 us -> 493 us (0.62); the launches traced: 792 us -> 484 us
  waiting for transfers between devices: 658 us -> 187 us
  starting transfers between devices: 62.2 us -> 144 us
  local copies, waits for them, and re-layouts: 18.8 us -> 73 us
  other arithmetic: 7.83 us -> 47.5 us
  between operations: 14.3 us -> 1.9 us
    all_gather x3 -> x0, waiting for transfers between devices: 344 us -> none  [the longest x1 127 us: local(): lax.all_gather(w_output, 'row', axis=0, tiled=True)]
    psum x1 -> x0, waiting for transfers between devices: 174 us -> none  [local(): keyvalue_grad = lax.psum(rows_part, 'col')]
    ppermute x0 -> x18, waiting for transfers between devices: none -> 159 us  [partner_swap(): return lax.ppermute(value, axis, [(i, i ^ 1 << bit) for i in range(count)])]
    ppermute x0 -> x18, starting transfers between devices: none -> 120 us  [partner_swap(): return lax.ppermute(value, axis, [(i, i ^ 1 << bit) for i in range(count)])]
    reduce_scatter x1 -> x0, waiting for transfers between devices: 116 us -> none  [local(): lax.psum_scatter(lax.dot_general(flat_norm, token_grad, (((0,), (0,)), ((...]
    select_n x0 -> x20, other arithmetic: none -> 24.5 us  [the longest x11 18.6 us: gather_by_bits(): jnp.where(low_half(axis, bit), jnp.concatenate([held, other], place), jnp...]
    ppermute x4, starting transfers between devices: 30.7 us -> 9.25 us  [shifted(): lax.ppermute(value, axis, [(source, source + steps) for source in range(f...]
    ppermute x2, starting transfers between devices: 28.1 us -> 12 us  [with_halo(): lax.ppermute(lax.slice_in_dim(block, block.shape[dim] - width, None, axis...]
  transfers between devices with their start and end apart: 13 -> 26, of which waited for: 8 -> 23; matrix products, arithmetic and copies ran while one was open for 3% -> 6% of each run, Pallas kernels for 0% -> 0%
where the time goes in v1:
time: 493 us; the launch traced here: 484 us
  waiting for transfers between devices  187 us (38%)
  starting transfers between devices  144 us (29%)
  local copies, waits for them, and re-layouts  73 us (15%)
  other arithmetic  47.5 us (10%)
  matrix products  30.2 us (6%)
    ppermute x18, waiting for transfers between devices, partner_swap(): return lax.ppermute(value, axis, [(i, i ^ 1 << bit) for i in range(count)])  159 us
    ppermute x18, starting transfers between devices, partner_swap(): return lax.ppermute(value, axis, [(i, i ^ 1 << bit) for i in range(count)])  120 us
    select_n x11, other arithmetic, gather_by_bits(): jnp.where(low_half(axis, bit), jnp.concatenate([held, other], place), jnp...  18.6 us
    ppermute x4, waiting for transfers between devices, shifted(): lax.ppermute(value, axis, [(source, source + steps) for source in range(f...  18.3 us
    unnamed x41, local copies, waits for them, and re-layouts  14.7 us
    select_n x6, local copies, waits for them, and re-layouts, gather_by_bits(): jnp.where(low_half(axis, bit), jnp.concatenate([held, other], place), jnp...  14.5 us
    ppermute x2, starting transfers between devices, with_halo(): lax.ppermute(lax.slice_in_dim(block, block.shape[dim] - width, None, axis...  12 us
  transfers between devices with their start and end apart: 26, of which 23 were waited for; matrix products, arithmetic and copies ran while one was open for 6% of the time, Pallas kernels for 0%

profile of v1, /device:TPU:1, one launch (start us, length us, event | category | flops | bytes accessed | tf_op | source)
XLA Modules:
  0.0 484.0 jit_solution(13701351008650403631)
XLA Ops:
  3.2 16.3 %collective-permute-start = (bf16[1,1,1,1,1,65536]{5,0,4,3,2,1:T(2,128)(2,1)S(1)}, bf16[1,1,1,1,1,65536]{5,0,4,3,2,1:T(2,128)(2,1)S(1)}, u32[]{:S(2)}, u32[]{:S(2)}) collective-permute-start(bf16[1,1,1,1,1,65536]{5,0,4,3,2,1:T(2,128)(2,1)S(1)} %reshape.1445), channel_id=1, source_target_pairs={{0,256},{16,272},{32,288},{48,304},{64,320},{80,336},{96,352},{112... | collective-permute-start | bytes 393224 | tf_op jit(solution)/shard_map/ppermute | solution.py:37
  19.8 5.0 %collective-permute-done = bf16[1,1,1,1,1,65536]{5,0,4,3,2,1:T(2,128)(2,1)S(1)} collective-permute-done((bf16[1,1,1,1,1,65536]{5,0,4,3,2,1:T(2,128)(2,1)S(1)}, bf16[1,1,1,1,1,65536]{5,0,4,3,2,1:T(2,128)(2,1)S(1)}, u32[]{:S(2)}, u32[]{:S(2)}) %collective-permute-start) | collective-permute-done | bytes 131104 | tf_op jit(solution)/shard_map/ppermute | solution.py:37
  25.9 18.6 %collective-permute-start.1 = (bf16[2,1,1,1,1,65536]{5,0,4,3,2,1:T(2,128)(2,1)S(1)}, bf16[2,1,1,1,1,65536]{5,0,4,3,2,1:T(2,128)(2,1)S(1)}, u32[]{:S(2)}, u32[]{:S(2)}) collective-permute-start(bf16[2,1,1,1,1,65536]{5,0,4,3,2,1:T(2,128)(2,1)S(1)} %broadcast_select_fusion.6), channel_id=1, source_target_pairs={{0,128},{16,144},{32,160},{48,176},{64,192},{80,208},{96,224},{112... | collective-permute-start | bytes 786440 | tf_op jit(solution)/shard_map/ppermute | solution.py:37
  46.9 20.0 %collective-permute-done.1 = bf16[2,1,1,1,1,65536]{5,0,4,3,2,1:T(2,128)(2,1)S(1)} collective-permute-done((bf16[2,1,1,1,1,65536]{5,0,4,3,2,1:T(2,128)(2,1)S(1)}, bf16[2,1,1,1,1,65536]{5,0,4,3,2,1:T(2,128)(2,1)S(1)}, u32[]{:S(2)}, u32[]{:S(2)}) %collective-permute-start.1) | collective-permute-done | bytes 262176 | tf_op jit(solution)/shard_map/ppermute | solution.py:37
  72.2 19.9 %collective-permute-done.2 = bf16[2,2,1,1,1,65536]{5,0,4,3,2,1:T(2,128)(2,1)S(1)} collective-permute-done((bf16[2,2,1,1,1,65536]{5,0,4,3,2,1:T(2,128)(2,1)S(1)}, bf16[2,2,1,1,1,65536]{5,0,4,3,2,1:T(2,128)(2,1)S(1)}, u32[]{:S(2)}, u32[]{:S(2)}) %collective-permute-start.2) | collective-permute-done | bytes 524320 | tf_op jit(solution)/shard_map/ppermute | solution.py:37
  100.9 20.0 %collective-permute-done.3 = bf16[2,2,2,1,1,65536]{5,0,4,3,2,1:T(2,128)(2,1)S(1)} collective-permute-done((bf16[2,2,2,1,1,65536]{5,0,4,3,2,1:T(2,128)(2,1)S(1)}, bf16[2,2,2,1,1,65536]{5,0,4,3,2,1:T(2,128)(2,1)S(1)}, u32[]{:S(2)}, u32[]{:S(2)}) %collective-permute-start.3) | collective-permute-done | bytes 1048608 | tf_op jit(solution)/shard_map/ppermute | solution.py:37
  129.5 42.3 %collective-permute-done.4 = bf16[2,2,2,2,1,65536]{5,0,4,3,2,1:T(2,128)(2,1)} collective-permute-done((bf16[2,2,2,2,1,65536]{5,0,4,3,2,1:T(2,128)(2,1)S(1)}, bf16[2,2,2,2,1,65536]{5,0,4,3,2,1:T(2,128)(2,1)}, u32[]{:S(2)}, u32[]{:S(2)}) %collective-permute-start.4) | collective-permute-done | bytes 2097184 | tf_op jit(solution)/shard_map/ppermute | solution.py:37
  171.8 9.7 %broadcast_select_fusion = bf16[2,2,2,2,2,65536]{5,0,4,3,2,1:T(2,128)(2,1)S(1)} fusion(pred[]{:T(512)S(6)} %eq.59, bf16[2,2,2,2,1,65536]{5,0,4,3,2,1:T(2,128)(2,1)} %collective-permute-done.4, bf16[2,2,2,2,1,65536]{5,0,4,3,2,1:T(2,128)(2,1)S(1)} %broadcast_select_fusion.1), kind=kLoop, calls=%fused_computation.2 | loop fusion | flops 6291456 | bytes 8388609 | tf_op jit(solution)/shard_map/jit(_where)/select_n | solution.py:52
  181.5 6.3 %copy.46 = bf16[2,2,2,2,2,65536]{5,4,3,2,1,0:T(2,128)(2,1)} copy(bf16[2,2,2,2,2,65536]{5,0,4,3,2,1:T(2,128)(2,1)S(1)} %broadcast_select_fusion) | data formatting | bytes 8388608 | tf_op jit(solution)/shard_map/jit(_where)/select_n | solution.py:52
  187.8 5.4 %select_n.544 = bf16[32,65536]{1,0:T(8,128)(2,1)} reshape(bf16[2,2,2,2,2,65536]{5,4,3,2,1,0:T(2,128)(2,1)} %copy.46) | data formatting | bytes 8388608 | tf_op jit(solution)/shard_map/jit(_where)/select_n | solution.py:52
  203.9 3.9 collective-permute-start.5
  215.8 8.1 %collective-permute-start.7 = (bf16[1,20,6,1024]{3,2,1,0:T(8,128)(2,1)S(1)}, bf16[1,20,6,1024]{3,2,1,0:T(8,128)(2,1)S(1)}, u32[]{:S(2)}, u32[]{:S(2)}) collective-permute-start(bf16[1,20,6,1024]{3,2,1,0:T(8,128)(2,1)S(1)} %get-tuple-element.11), channel_id=1, source_target_pairs={{0,1},{1,2},{2,3},{3,4},{4,5},{5,6},{6,7},{7,8},{8,9},{9,10},{10,1... | collective-permute-start | bytes 737288 | tf_op jit(solution)/shard_map/ppermute | solution.py:27
  227.9 5.9 %collective-permute-done.8 = bf16[1,20,6,1024]{3,2,1,0:T(8,128)(2,1)S(1)} collective-permute-done((bf16[1,20,6,1024]{3,2,1,0:T(8,128)(2,1)S(1)}, bf16[1,20,6,1024]{3,2,1,0:T(8,128)(2,1)S(1)}, u32[]{:S(2)}, u32[]{:S(2)}) %collective-permute-start.8) | collective-permute-done | bytes 245792 | tf_op jit(solution)/shard_map/ppermute | solution.py:30
  258.5 3.6 concatenate.486
  262.1 5.6 %fusion.12 = f32[1,560,8,64]{1,3,2,0:T(8,128)} fusion(bf16[128,8,64]{0,2,1:T(8,128)(2,1)S(1)} %bitcast.154, f32[8,128,560]{1,2,0:T(8,128)} %fusion.78, f32[8,128,560]{1,2,0:T(8,128)} %get-tuple-element.19, f32[8,128]{1,0:T(8,128)S(1)} %get-tuple-element.18), kind=kOutput, calls=%fused_computation.17 | convolution fusion | flops 77415984 | bytes 5869568 | tf_op jit(solution)/shard_map/bhqk,bqhd->bkhd/dot_general | solution.py:140
  270.8 3.6 concatenate.485
  286.3 5.9 %collective-permute-done.10 = f32[1,20,6,1024]{3,0,2,1:T(1,128)S(1)} collective-permute-done((f32[1,20,6,1024]{3,0,2,1:T(1,128)S(1)}, f32[1,20,6,1024]{3,0,2,1:T(1,128)S(1)}, u32[]{:S(2)}, u32[]{:S(2)}) %collective-permute-start.10) | collective-permute-done | bytes 491552 | tf_op jit(solution)/shard_map/ppermute | solution.py:19
  300.9 9.3 %collective-permute-done.11 = f32[1,6,16,1024]{3,0,2,1:T(1,128)} collective-permute-done((f32[1,6,16,1024]{3,0,2,1:T(1,128)}, f32[1,6,16,1024]{3,0,2,1:T(1,128)}, u32[]{:S(2)}, u32[]{:S(2)}) %collective-permute-start.11) | collective-permute-done | bytes 393248 | tf_op jit(solution)/shard_map/ppermute | solution.py:19
  321.0 4.4 collective-permute-done.13
  331.4 9.2 %collective-permute-start.14 = (f32[1024,2,2,1,1,64]{0,5,4,3,2,1:T(8,128)}, f32[1024,2,2,1,1,64]{0,5,4,3,2,1:T(8,128)}, u32[]{:S(2)}, u32[]{:S(2)}) collective-permute-start(f32[1024,2,2,1,1,64]{0,5,4,3,2,1:T(8,128)} %slice_select_fusion.1), channel_id=1, source_target_pairs={{0,2},{1,3},{2,0},{3,1},{4,6},{5,7},{6,4},{7,5},{8,10},{9,11},{10,... | collective-permute-start | bytes 3145736 | tf_op jit(solution)/shard_map/ppermute | solution.py:37
  340.6 23.7 %collective-permute-done.14 = f32[1024,2,2,1,1,64]{0,5,4,3,2,1:T(8,128)} collective-permute-done((f32[1024,2,2,1,1,64]{0,5,4,3,2,1:T(8,128)}, f32[1024,2,2,1,1,64]{0,5,4,3,2,1:T(8,128)}, u32[]{:S(2)}, u32[]{:S(2)}) %collective-permute-start.14) | collective-permute-done | bytes 1048608 | tf_op jit(solution)/shard_map/ppermute | solution.py:37
  368.3 5.7 %collective-permute-start.15 = (f32[1024,2,1,1,1,64]{0,5,4,3,2,1:T(8,128)}, f32[1024,2,1,1,1,64]{0,5,4,3,2,1:T(8,128)}, u32[]{:S(2)}, u32[]{:S(2)}) collective-permute-start(f32[1024,2,1,1,1,64]{0,5,4,3,2,1:T(8,128)} %slice_select_fusion.2), channel_id=1, source_target_pairs={{0,4},{1,5},{2,6},{3,7},{4,0},{5,1},{6,2},{7,3},{8,12},{9,13},{10,... | collective-permute-start | bytes 1572872 | tf_op jit(solution)/shard_map/ppermute | solution.py:37
  381.0 4.9 %collective-permute-done.15 = f32[1024,2,1,1,1,64]{0,5,4,3,2,1:T(8,128)} collective-permute-done((f32[1024,2,1,1,1,64]{0,5,4,3,2,1:T(8,128)}, f32[1024,2,1,1,1,64]{0,5,4,3,2,1:T(8,128)}, u32[]{:S(2)}, u32[]{:S(2)}) %collective-permute-start.15) | collective-permute-done | bytes 524320 | tf_op jit(solution)/shard_map/ppermute | solution.py:37
  387.3 4.6 collective-permute-start.16
  393.0 4.3 collective-permute-done.16
  404.4 4.7 fusion.18
  416.5 4.2 collective-permute-start.19
  422.6 15.3 %collective-permute-start.20 = (f32[2,1,1,1,1,32,64]{6,5,4,3,2,1,0:T(8,128)S(1)}, f32[2,1,1,1,1,32,64]{6,5,4,3,2,1,0:T(8,128)S(1)}, u32[]{:S(2)}, u32[]{:S(2)}) collective-permute-start(f32[2,1,1,1,1,32,64]{6,5,4,3,2,1,0:T(8,128)S(1)} %slice_select_fusion.7), channel_id=1, source_target_pairs={{0,128},{16,144},{32,160},{48,176},{64,192},{80,208},{96,224},{112... | collective-permute-start | bytes 49160 | tf_op jit(solution)/shard_map/ppermute | solution.py:37
  439.2 10.1 %collective-permute-start.21 = (f32[1,1,1,1,1,32,64]{6,5,4,3,2,1,0:T(8,128)S(1)}, f32[1,1,1,1,1,32,64]{6,5,4,3,2,1,0:T(8,128)S(1)}, u32[]{:S(2)}, u32[]{:S(2)}) collective-permute-start(f32[1,1,1,1,1,32,64]{6,5,4,3,2,1,0:T(8,128)S(1)} %slice_select_fusion.8), channel_id=1, source_target_pairs={{0,256},{16,272},{32,288},{48,304},{64,320},{80,336},{96,352},{112... | collective-permute-start | bytes 24584 | tf_op jit(solution)/shard_map/ppermute | solution.py:37
  452.4 4.6 collective-permute-start.22
  465.3 4.5 collective-permute-done.24
  469.7 11.9 %collective-permute-start.25 = (f32[32,2,2,2,1,64]{5,0,4,3,2,1:T(8,128)S(1)}, f32[32,2,2,2,1,64]{5,0,4,3,2,1:T(8,128)S(1)}, u32[]{:S(2)}, u32[]{:S(2)}) collective-permute-start(f32[32,2,2,2,1,64]{5,0,4,3,2,1:T(8,128)S(1)} %maximum_select_fusion.1), channel_id=1, source_target_pairs={{0,1},{1,0},{2,3},{3,2},{4,5},{5,4},{6,7},{7,6},{8,9},{9,8},{10,11... | collective-permute-start | bytes 196616 | tf_op jit(solution)/shard_map/ppermute | solution.py:37
  (161 shorter events, 160.8 us)
Async XLA Ops:
  3.2 21.5 %collective-permute-start = (bf16[1,1,1,1,1,65536]{5,0,4,3,2,1:T(2,128)(2,1)S(1)}, bf16[1,1,1,1,1,65536]{5,0,4,3,2,1:T(2,128)(2,1)S(1)}, u32[]{:S(2)}, u32[]{:S(2)}) collective-permute-start(bf16[1,1,1,1,1,65536]{5,0,4,3,2,1:T(2,128)(2,1)S(1)} %reshape.1445), channel_id=1, source_target_pairs={{0,256},{16,272},{32,288},{48,304},{64,320},{80,336},{96,352},{112... | collective-permute-start | bytes 393224 | tf_op jit(solution)/shard_map/ppermute | solution.py:37
  25.9 41.0 %collective-permute-start.1 = (bf16[2,1,1,1,1,65536]{5,0,4,3,2,1:T(2,128)(2,1)S(1)}, bf16[2,1,1,1,1,65536]{5,0,4,3,2,1:T(2,128)(2,1)S(1)}, u32[]{:S(2)}, u32[]{:S(2)}) collective-permute-start(bf16[2,1,1,1,1,65536]{5,0,4,3,2,1:T(2,128)(2,1)S(1)} %broadcast_select_fusion.6), channel_id=1, source_target_pairs={{0,128},{16,144},{32,160},{48,176},{64,192},{80,208},{96,224},{112... | collective-permute-start | bytes 786440 | tf_op jit(solution)/shard_map/ppermute | solution.py:37
  67.7 24.5 %collective-permute-start.2 = (bf16[2,2,1,1,1,65536]{5,0,4,3,2,1:T(2,128)(2,1)S(1)}, bf16[2,2,1,1,1,65536]{5,0,4,3,2,1:T(2,128)(2,1)S(1)}, u32[]{:S(2)}, u32[]{:S(2)}) collective-permute-start(bf16[2,2,1,1,1,65536]{5,0,4,3,2,1:T(2,128)(2,1)S(1)} %broadcast_select_fusion.4), channel_id=1, source_target_pairs={{0,64},{16,80},{32,96},{48,112},{64,0},{80,16},{96,32},{112,48},{1... | collective-permute-start | bytes 1572872 | tf_op jit(solution)/shard_map/ppermute | solution.py:37
  94.8 26.1 %collective-permute-start.3 = (bf16[2,2,2,1,1,65536]{5,0,4,3,2,1:T(2,128)(2,1)S(1)}, bf16[2,2,2,1,1,65536]{5,0,4,3,2,1:T(2,128)(2,1)S(1)}, u32[]{:S(2)}, u32[]{:S(2)}) collective-permute-start(bf16[2,2,2,1,1,65536]{5,0,4,3,2,1:T(2,128)(2,1)S(1)} %broadcast_select_fusion.2), channel_id=1, source_target_pairs={{0,32},{16,48},{32,0},{48,16},{64,96},{80,112},{96,64},{112,80},{1... | collective-permute-start | bytes 3145736 | tf_op jit(solution)/shard_map/ppermute | solution.py:37
  100.9 26.4 %copy-start.4 = (bf16[1,8,16,1024]{3,2,1,0:T(8,128)(2,1)S(1)}, bf16[1,8,16,1024]{3,2,1,0:T(8,128)(2,1)}, u32[]{:S(2)}) copy-start(bf16[1,8,16,1024]{3,2,1,0:T(8,128)(2,1)} %param.6) | copy-start | bytes 786436
  100.9 27.7 %copy-start.15 = (f32[1024]{0:T(1024)S(1)}, f32[1024]{0:T(1024)}, u32[]{:S(2)}) copy-start(f32[1024]{0:T(1024)} %param.7) | copy-start | bytes 12292
  124.0 47.8 %collective-permute-start.4 = (bf16[2,2,2,2,1,65536]{5,0,4,3,2,1:T(2,128)(2,1)S(1)}, bf16[2,2,2,2,1,65536]{5,0,4,3,2,1:T(2,128)(2,1)}, u32[]{:S(2)}, u32[]{:S(2)}) collective-permute-start(bf16[2,2,2,2,1,65536]{5,0,4,3,2,1:T(2,128)(2,1)S(1)} %broadcast_select_fusion.1), channel_id=1, source_target_pairs={{0,16},{16,0},{32,48},{48,32},{64,80},{80,64},{96,112},{112,96},{1... | collective-permute-start | bytes 6291464 | tf_op jit(solution)/shard_map/ppermute | solution.py:37
  203.9 8.6 %collective-permute-start.5 = (bf16[1,6,16,1024]{3,2,1,0:T(8,128)(2,1)}, bf16[1,6,16,1024]{3,2,1,0:T(8,128)(2,1)}, u32[]{:S(2)}, u32[]{:S(2)}) collective-permute-start(bf16[1,6,16,1024]{3,2,1,0:T(8,128)(2,1)} %get-tuple-element.13), channel_id=1, source_target_pairs={{0,16},{16,32},{32,48},{48,64},{64,80},{80,96},{96,112},{112,128},... | collective-permute-start | bytes 589832 | tf_op jit(solution)/shard_map/ppermute | solution.py:27
  207.8 6.7 %collective-permute-start.6 = (bf16[1,6,16,1024]{3,2,1,0:T(8,128)(2,1)}, bf16[1,6,16,1024]{3,2,1,0:T(8,128)(2,1)}, u32[]{:S(2)}, u32[]{:S(2)}) collective-permute-start(bf16[1,6,16,1024]{3,2,1,0:T(8,128)(2,1)} %get-tuple-element.14), channel_id=1, source_target_pairs={{16,0},{32,16},{48,32},{64,48},{80,64},{96,80},{112,96},{128,112},... | collective-permute-start | bytes 589832 | tf_op jit(solution)/shard_map/ppermute | solution.py:30
  212.5 13.5 %copy-start.10 = (bf16[512,1024]{1,0:T(8,128)(2,1)S(1)}, bf16[512,1024]{1,0:T(8,128)(2,1)}, u32[]{:S(2)}) copy-start(bf16[512,1024]{1,0:T(8,128)(2,1)} %reshape.1454) | copy-start | bytes 3145732
  212.5 13.5 %copy-start.12 = (bf16[1,8,16,1024]{3,2,1,0:T(8,128)(2,1)S(1)}, bf16[1,8,16,1024]{3,2,1,0:T(8,128)(2,1)}, u32[]{:S(2)}) copy-start(bf16[1,8,16,1024]{3,2,1,0:T(8,128)(2,1)} %param.11) | copy-start | bytes 786436
  212.5 21.3 %copy-start.6 = (bf16[128,1024]{1,0:T(8,128)(2,1)S(1)}, bf16[128,1024]{1,0:T(8,128)(2,1)}, u32[]{:S(2)}) copy-start(bf16[128,1024]{1,0:T(8,128)(2,1)} %copy-done.5) | copy-start | bytes 786436
  215.8 12.1 %collective-permute-start.7 = (bf16[1,20,6,1024]{3,2,1,0:T(8,128)(2,1)S(1)}, bf16[1,20,6,1024]{3,2,1,0:T(8,128)(2,1)S(1)}, u32[]{:S(2)}, u32[]{:S(2)}) collective-permute-start(bf16[1,20,6,1024]{3,2,1,0:T(8,128)(2,1)S(1)} %get-tuple-element.11), channel_id=1, source_target_pairs={{0,1},{1,2},{2,3},{3,4},{4,5},{5,6},{6,7},{7,8},{8,9},{9,10},{10,1... | collective-permute-start | bytes 737288 | tf_op jit(solution)/shard_map/ppermute | solution.py:27
  223.9 9.9 %collective-permute-start.8 = (bf16[1,20,6,1024]{3,2,1,0:T(8,128)(2,1)S(1)}, bf16[1,20,6,1024]{3,2,1,0:T(8,128)(2,1)S(1)}, u32[]{:S(2)}, u32[]{:S(2)}) collective-permute-start(bf16[1,20,6,1024]{3,2,1,0:T(8,128)(2,1)S(1)} %get-tuple-element.12), channel_id=1, source_target_pairs={{1,0},{2,1},{3,2},{4,3},{5,4},{6,5},{7,6},{8,7},{9,8},{10,9},{11,1... | collective-permute-start | bytes 737288 | tf_op jit(solution)/shard_map/ppermute | solution.py:30
  278.6 7.7 %collective-permute-start.9 = (f32[1,20,6,1024]{3,0,2,1:T(1,128)S(1)}, f32[1,20,6,1024]{3,0,2,1:T(1,128)S(1)}, u32[]{:S(2)}, u32[]{:S(2)}) collective-permute-start(f32[1,20,6,1024]{3,0,2,1:T(1,128)S(1)} %get-tuple-element.5), channel_id=1, source_target_pairs={{0,1},{1,2},{2,3},{3,4},{4,5},{5,6},{6,7},{7,8},{8,9},{9,10},{10,1... | collective-permute-start | bytes 1474568 | tf_op jit(solution)/shard_map/ppermute | solution.py:19
  280.6 11.7 %collective-permute-start.10 = (f32[1,20,6,1024]{3,0,2,1:T(1,128)S(1)}, f32[1,20,6,1024]{3,0,2,1:T(1,128)S(1)}, u32[]{:S(2)}, u32[]{:S(2)}) collective-permute-start(f32[1,20,6,1024]{3,0,2,1:T(1,128)S(1)} %get-tuple-element.6), channel_id=1, source_target_pairs={{1,0},{2,1},{3,2},{4,3},{5,4},{6,5},{7,6},{8,7},{9,8},{10,9},{11,1... | collective-permute-start | bytes 1474568 | tf_op jit(solution)/shard_map/ppermute | solution.py:19
  296.2 14.0 %collective-permute-start.11 = (f32[1,6,16,1024]{3,0,2,1:T(1,128)}, f32[1,6,16,1024]{3,0,2,1:T(1,128)}, u32[]{:S(2)}, u32[]{:S(2)}) collective-permute-start(f32[1,6,16,1024]{3,0,2,1:T(1,128)} %get-tuple-element.7), channel_id=1, source_target_pairs={{0,16},{16,32},{32,48},{48,64},{64,80},{80,96},{96,112},{112,128},... | collective-permute-start | bytes 1179656 | tf_op jit(solution)/shard_map/ppermute | solution.py:19
  299.6 10.6 %collective-permute-start.12 = (f32[1,6,16,1024]{3,0,2,1:T(1,128)}, f32[1,6,16,1024]{3,0,2,1:T(1,128)}, u32[]{:S(2)}, u32[]{:S(2)}) collective-permute-start(f32[1,6,16,1024]{3,0,2,1:T(1,128)} %get-tuple-element.8), channel_id=1, source_target_pairs={{16,0},{32,16},{48,32},{64,48},{80,64},{96,80},{112,96},{128,112},... | collective-permute-start | bytes 1179656 | tf_op jit(solution)/shard_map/ppermute | solution.py:19
  319.0 6.4 %collective-permute-start.13 = (f32[1024,2,2,2,1,64]{0,5,4,3,2,1:T(8,128)}, f32[1024,2,2,2,1,64]{0,5,4,3,2,1:T(8,128)}, u32[]{:S(2)}, u32[]{:S(2)}) collective-permute-start(f32[1024,2,2,2,1,64]{0,5,4,3,2,1:T(8,128)} %slice_select_fusion), channel_id=1, source_target_pairs={{0,1},{1,0},{2,3},{3,2},{4,5},{5,4},{6,7},{7,6},{8,9},{9,8},{10,11... | collective-permute-start | bytes 6291464 | tf_op jit(solution)/shard_map/ppermute | solution.py:37
  331.4 32.9 %collective-permute-start.14 = (f32[1024,2,2,1,1,64]{0,5,4,3,2,1:T(8,128)}, f32[1024,2,2,1,1,64]{0,5,4,3,2,1:T(8,128)}, u32[]{:S(2)}, u32[]{:S(2)}) collective-permute-start(f32[1024,2,2,1,1,64]{0,5,4,3,2,1:T(8,128)} %slice_select_fusion.1), channel_id=1, source_target_pairs={{0,2},{1,3},{2,0},{3,1},{4,6},{5,7},{6,4},{7,5},{8,10},{9,11},{10,... | collective-permute-start | bytes 3145736 | tf_op jit(solution)/shard_map/ppermute | solution.py:37
  368.3 17.6 %collective-permute-start.15 = (f32[1024,2,1,1,1,64]{0,5,4,3,2,1:T(8,128)}, f32[1024,2,1,1,1,64]{0,5,4,3,2,1:T(8,128)}, u32[]{:S(2)}, u32[]{:S(2)}) collective-permute-start(f32[1024,2,1,1,1,64]{0,5,4,3,2,1:T(8,128)} %slice_select_fusion.2), channel_id=1, source_target_pairs={{0,4},{1,5},{2,6},{3,7},{4,0},{5,1},{6,2},{7,3},{8,12},{9,13},{10,... | collective-permute-start | bytes 1572872 | tf_op jit(solution)/shard_map/ppermute | solution.py:37
  387.3 9.9 %collective-permute-start.16 = (f32[1024,1,1,1,1,64]{0,5,4,3,2,1:T(8,128)S(1)}, f32[1024,1,1,1,1,64]{0,5,4,3,2,1:T(8,128)S(1)}, u32[]{:S(2)}, u32[]{:S(2)}) collective-permute-start(f32[1024,1,1,1,1,64]{0,5,4,3,2,1:T(8,128)S(1)} %slice_select_fusion.4), channel_id=1, source_target_pairs={{0,8},{1,9},{2,10},{3,11},{4,12},{5,13},{6,14},{7,15},{8,0},{9,1},... | collective-permute-start | bytes 786440 | tf_op jit(solution)/shard_map/ppermute | solution.py:37
  401.8 7.8 %collective-permute-start.17 = (f32[2,2,2,2,1,32,64]{6,5,4,3,2,1,0:T(8,128)}, f32[2,2,2,2,1,32,64]{6,5,4,3,2,1,0:T(8,128)}, u32[]{:S(2)}, u32[]{:S(2)}) collective-permute-start(f32[2,2,2,2,1,32,64]{6,5,4,3,2,1,0:T(8,128)} %slice_select_fusion.3), channel_id=1, source_target_pairs={{0,16},{16,0},{32,48},{48,32},{64,80},{80,64},{96,112},{112,96},{1... | collective-permute-start | bytes 393224 | tf_op jit(solution)/shard_map/ppermute | solution.py:37
  410.8 5.7 %collective-permute-start.18 = (f32[2,2,2,1,1,32,64]{6,5,4,3,2,1,0:T(8,128)S(1)}, f32[2,2,2,1,1,32,64]{6,5,4,3,2,1,0:T(8,128)S(1)}, u32[]{:S(2)}, u32[]{:S(2)}) collective-permute-start(f32[2,2,2,1,1,32,64]{6,5,4,3,2,1,0:T(8,128)S(1)} %slice_select_fusion.5), channel_id=1, source_target_pairs={{0,32},{16,48},{32,0},{48,16},{64,96},{80,112},{96,64},{112,80},{1... | collective-permute-start | bytes 196616 | tf_op jit(solution)/shard_map/ppermute | solution.py:37
  416.5 65.1 %copy-start.13 = (bf16[1,8,16,1024]{3,2,1,0:T(8,128)(2,1)S(1)}, bf16[1,8,16,1024]{3,2,1,0:T(8,128)(2,1)}, u32[]{:S(2)}) copy-start(bf16[1,8,16,1024]{3,2,1,0:T(8,128)(2,1)} %param.11) | copy-start | bytes 786436
  416.5 6.0 %collective-permute-start.19 = (f32[2,2,1,1,1,32,64]{6,5,4,3,2,1,0:T(8,128)S(1)}, f32[2,2,1,1,1,32,64]{6,5,4,3,2,1,0:T(8,128)S(1)}, u32[]{:S(2)}, u32[]{:S(2)}) collective-permute-start(f32[2,2,1,1,1,32,64]{6,5,4,3,2,1,0:T(8,128)S(1)} %slice_select_fusion.6), channel_id=1, source_target_pairs={{0,64},{16,80},{32,96},{48,112},{64,0},{80,16},{96,32},{112,48},{1... | collective-permute-start | bytes 98312 | tf_op jit(solution)/shard_map/ppermute | solution.py:37
  422.6 16.5 %collective-permute-start.20 = (f32[2,1,1,1,1,32,64]{6,5,4,3,2,1,0:T(8,128)S(1)}, f32[2,1,1,1,1,32,64]{6,5,4,3,2,1,0:T(8,128)S(1)}, u32[]{:S(2)}, u32[]{:S(2)}) collective-permute-start(f32[2,1,1,1,1,32,64]{6,5,4,3,2,1,0:T(8,128)S(1)} %slice_select_fusion.7), channel_id=1, source_target_pairs={{0,128},{16,144},{32,160},{48,176},{64,192},{80,208},{96,224},{112... | collective-permute-start | bytes 49160 | tf_op jit(solution)/shard_map/ppermute | solution.py:37
  439.2 13.2 %collective-permute-start.21 = (f32[1,1,1,1,1,32,64]{6,5,4,3,2,1,0:T(8,128)S(1)}, f32[1,1,1,1,1,32,64]{6,5,4,3,2,1,0:T(8,128)S(1)}, u32[]{:S(2)}, u32[]{:S(2)}) collective-permute-start(f32[1,1,1,1,1,32,64]{6,5,4,3,2,1,0:T(8,128)S(1)} %slice_select_fusion.8), channel_id=1, source_target_pairs={{0,256},{16,272},{32,288},{48,304},{64,320},{80,336},{96,352},{112... | collective-permute-start | bytes 24584 | tf_op jit(solution)/shard_map/ppermute | solution.py:37
  452.4 6.2 %collective-permute-start.22 = (f32[32,1,1,1,1,64]{5,0,4,3,2,1:T(8,128)S(1)}, f32[32,1,1,1,1,64]{5,0,4,3,2,1:T(8,128)S(1)}, u32[]{:S(2)}, u32[]{:S(2)}) collective-permute-start(f32[32,1,1,1,1,64]{5,0,4,3,2,1:T(8,128)S(1)} %bitcast.147), channel_id=1, source_target_pairs={{0,8},{1,9},{2,10},{3,11},{4,12},{5,13},{6,14},{7,15},{8,0},{9,1},... | collective-permute-start | bytes 24584 | tf_op jit(solution)/shard_map/ppermute | solution.py:37
  458.6 4.6 collective-permute-start.23
  463.2 6.5 %collective-permute-start.24 = (f32[32,2,2,1,1,64]{5,0,4,3,2,1:T(8,128)S(1)}, f32[32,2,2,1,1,64]{5,0,4,3,2,1:T(8,128)S(1)}, u32[]{:S(2)}, u32[]{:S(2)}) collective-permute-start(f32[32,2,2,1,1,64]{5,0,4,3,2,1:T(8,128)S(1)} %maximum_select_fusion.3), channel_id=1, source_target_pairs={{0,2},{1,3},{2,0},{3,1},{4,6},{5,7},{6,4},{7,5},{8,10},{9,11},{10,... | collective-permute-start | bytes 98312 | tf_op jit(solution)/shard_map/ppermute | solution.py:37
  469.7 12.9 %collective-permute-start.25 = (f32[32,2,2,2,1,64]{5,0,4,3,2,1:T(8,128)S(1)}, f32[32,2,2,2,1,64]{5,0,4,3,2,1:T(8,128)S(1)}, u32[]{:S(2)}, u32[]{:S(2)}) collective-permute-start(f32[32,2,2,2,1,64]{5,0,4,3,2,1:T(8,128)S(1)} %maximum_select_fusion.1), channel_id=1, source_target_pairs={{0,1},{1,0},{2,3},{3,2},{4,5},{5,4},{6,7},{7,6},{8,9},{9,8},{10,11... | collective-permute-start | bytes 196616 | tf_op jit(solution)/shard_map/ppermute | solution.py:37
  (10 other events, 35.3 us)

commit v2 on v0

--- a/solution.py
+++ b/solution.py
@@ -30,6 +30,59 @@
         high = lax.ppermute(lax.slice_in_dim(block, 0, width, axis=dim), axis, backward)
         block = jnp.concatenate([low, block, high], axis=dim)
     return block
+
+
+def partner_swap(value, axis, bit):
+    count = lax.axis_size(axis)
+    return lax.ppermute(value, axis, [(i, i ^ (1 << bit)) for i in range(count)])
+
+
+def axis_bit(axis, bit):
+    return (lax.axis_index(axis) // (1 << bit)) % 2
+
+
+def gather_by_bits(block, axis, bits):
+    levels = lax.axis_size(axis).bit_length() - 1
+    mine = [axis_bit(axis, bit) for bit in range(levels)]
+    zero = [0] * block.ndim
+    held = jnp.zeros((2,) * levels + block.shape, block.dtype)
+    held = lax.dynamic_update_slice(
+        held, block.reshape((1,) * levels + block.shape), mine[::-1] + zero
+    )
+    done = set()
+    for bit in bits:
+        start = [0 if b in done else mine[b] for b in range(levels)]
+        size = [2 if b in done else 1 for b in range(levels)]
+        region = lax.dynamic_slice(held, start[::-1] + zero, size[::-1] + list(block.shape))
+        other = partner_swap(region, axis, bit)
+        start[bit] = 1 - mine[bit]
+        held = lax.dynamic_update_slice(held, other, start[::-1] + zero)
+        done.add(bit)
+    return held.reshape((-1,) + block.shape)
+
+
+def scatter_by_bits(total, axis, bits):
+    levels = lax.axis_size(axis).bit_length() - 1
+    held = total.reshape((2,) * levels + (total.shape[0] // 2**levels,) + total.shape[1:])
+    for bit in bits:
+        place = levels - 1 - bit
+        own = axis_bit(axis, bit)
+        keep = lax.dynamic_index_in_dim(held, own, place)
+        send = lax.dynamic_index_in_dim(held, 1 - own, place)
+        held = keep + partner_swap(send, axis, bit)
+    return held.reshape(held.shape[levels:])
+
+
+def gather_weight(shard, row_bits):
+    half = shard.shape[1] // 2
+    own = axis_bit("col", 0)
+    piece = lax.dynamic_slice_in_dim(shard, own * half, half, axis=1)
+    rows = gather_by_bits(piece, "row", row_bits)
+    rows = rows.reshape(-1, half)
+    held = jnp.zeros((2,) + rows.shape, rows.dtype)
+    held = lax.dynamic_update_slice(held, rows[None], (own, 0, 0))
+    held = lax.dynamic_update_slice(held, partner_swap(rows, "col", 0)[None], (1 - own, 0, 0))
+    return jnp.concatenate([held[0], held[1]], axis=1)
 
 
 def normalize(inputs, norm_gain):
@@ -146,11 +199,10 @@
     ext_cols = tile_cols + 2 * RADIUS
     standard, spread, normed = normalize(inputs, norm_gain)
     flat_norm = normed.reshape(-1, model_width)
-    full_query, full_keyvalue, full_output = (
-        lax.all_gather(w_query, "row", axis=0, tiled=True),
-        lax.all_gather(w_keyvalue, "row", axis=0, tiled=True),
-        lax.all_gather(w_output, "row", axis=0, tiled=True),
-    )
+    row_bits = list(range(lax.axis_size("row").bit_length() - 1))
+    full_keyvalue = gather_weight(w_keyvalue, row_bits[::-1])
+    full_query = gather_weight(w_query, row_bits[::-1])
+    full_output = gather_weight(w_output, row_bits[::-1])
     inner_width = full_query.shape[1]
     queries = jnp.dot(flat_norm, full_query, preferred_element_type=jnp.float32).astype(
         jnp.bfloat16
@@ -184,15 +236,21 @@
     keyvalue_part = keyvalue_part.reshape(batches, ext_rows, ext_cols, 2 * inner_width)
     owned = fold_rows(fold_cols(keyvalue_part))
     token_grad = owned.astype(jnp.bfloat16).reshape(-1, 2 * inner_width)
-    rows_part = lax.psum_scatter(
-        lax.dot_general(
-            flat_norm, token_grad, (((0,), (0,)), ((), ())), preferred_element_type=jnp.float32
-        ),
-        "row",
-        scatter_dimension=0,
-        tiled=True,
-    )
-    keyvalue_grad = lax.psum(rows_part, "col")
+    row_count, col_count = lax.axis_size("row"), lax.axis_size("col")
+    col_bits = list(range(col_count.bit_length() - 1))
+    feature_part = model_width // row_count
+    column_part = token_grad.shape[1] // col_count
+    partial = jnp.einsum(
+        "tra,tcb->crab",
+        flat_norm.reshape(-1, row_count, feature_part),
+        token_grad.reshape(-1, col_count, column_part),
+        preferred_element_type=jnp.float32,
+    )
+    col_order = [0] + col_bits[2:3] + col_bits[1:2] + col_bits[3:]
+    col_part = scatter_by_bits(partial, "col", col_order)[0]
+    rows_part = scatter_by_bits(col_part, "row", row_bits)[0]
+    keyvalue_grad = gather_by_bits(rows_part, "col", col_bits[::-1])
+    keyvalue_grad = keyvalue_grad.transpose(1, 0, 2).reshape(feature_part, -1)
     normed_grad = lax.dot_general(
         query_grad.reshape(-1, inner_width),
         full_query,

time: 793 us -> 414 us (0.52)
  waiting for transfers between devices: 658 us -> 146 us
  starting transfers between devices: 62.2 us -> 174 us
  local copies, waits for them, and re-layouts: 18.8 us -> 43.4 us
  between operations: 14.3 us -> 2.52 us
  other arithmetic: 7.83 us -> 19.4 us
    all_gather x3 -> x0, waiting for transfers between devices: 344 us -> none  [the longest x1 127 us: local(): lax.all_gather(w_output, 'row', axis=0, tiled=True)]
    psum x1 -> x0, waiting for transfers between devices: 174 us -> none  [local(): keyvalue_grad = lax.psum(rows_part, 'col')]
    ppermute x0 -> x31, starting transfers between devices: none -> 147 us  [partner_swap(): return lax.ppermute(value, axis, [(i, i ^ 1 << bit) for i in range(count)])]
    ppermute x0 -> x31, waiting for transfers between devices: none -> 119 us  [partner_swap(): return lax.ppermute(value, axis, [(i, i ^ 1 << bit) for i in range(count)])]
    reduce_scatter x1 -> x0, waiting for transfers between devices: 116 us -> none  [local(): lax.psum_scatter(lax.dot_general(flat_norm, token_grad, (((0,), (0,)), ((...]
    ppermute x2, starting transfers between devices: 28.1 us -> 8.86 us  [with_halo(): lax.ppermute(lax.slice_in_dim(block, block.shape[dim] - width, None, axis...]
    ppermute x4, starting transfers between devices: 30.7 us -> 14.2 us  [shifted(): lax.ppermute(value, axis, [(source, source + steps) for source in range(f...]
    add x0 -> x9, other arithmetic: none -> 8.77 us  [scatter_by_bits(): held = keep + partner_swap(send, axis, bit)]
  transfers between devices with their start and end apart: 13 -> 39, of which waited for: 8 -> 23; matrix products, arithmetic and copies ran while one was open for 3% -> 5% of each run, Pallas kernels for 0% -> 0%
where the time goes in v2:
time: 414 us; the launch traced here: 412 us
  starting transfers between devices  174 us (42%)
  waiting for transfers between devices  146 us (35%)
  local copies, waits for them, and re-layouts  43.4 us (10%)
  matrix products  26.9 us (6%)
  other arithmetic  19.4 us (5%)
    ppermute x31, starting transfers between devices, partner_swap(): return lax.ppermute(value, axis, [(i, i ^ 1 << bit) for i in range(count)])  147 us
    ppermute x31, waiting for transfers between devices, partner_swap(): return lax.ppermute(value, axis, [(i, i ^ 1 << bit) for i in range(count)])  119 us
    ppermute x4, waiting for transfers between devices, shifted(): lax.ppermute(value, axis, [(source, source + steps) for source in range(f...  17.4 us
    ppermute x4, starting transfers between devices, shifted(): lax.ppermute(value, axis, [(source, source + steps) for source in range(f...  14.2 us
    unnamed x78, local copies, waits for them, and re-layouts  9.7 us
    ppermute x2, starting transfers between devices, with_halo(): lax.ppermute(lax.slice_in_dim(block, block.shape[dim] - width, None, axis...  8.86 us
    add x9, other arithmetic, scatter_by_bits(): held = keep + partner_swap(send, axis, bit)  8.77 us
  transfers between devices with their start and end apart: 39, of which 23 were waited for; matrix products, arithmetic and copies ran while one was open for 5% of the time, Pallas kernels for 0%

profile of v2, /device:TPU:1, one launch (start us, length us, event | category | flops | bytes accessed | tf_op | source)
XLA Modules:
  0.0 412.0 jit_solution(747685814430213758)
XLA Ops:
  1.7 16.3 %collective-permute-start = (bf16[1,1,1,1,1,32,512]{6,5,4,3,2,1,0:T(8,128)(2,1)S(1)}, bf16[1,1,1,1,1,32,512]{6,5,4,3,2,1,0:T(8,128)(2,1)S(1)}, u32[]{:S(2)}, u32[]{:S(2)}) collective-permute-start(bf16[1,1,1,1,1,32,512]{6,5,4,3,2,1,0:T(8,128)(2,1)S(1)} %constant_dynamic-slice_fusion.27), channel_id=1, source_target_pairs={{0,256},{16,272},{32,288},{48,304},{64,320},{80,336},{96,352},{112... | collective-permute-start | bytes 98312 | tf_op jit(solution)/shard_map/ppermute | solution.py:37
  20.8 12.1 %collective-permute-start.16 = (bf16[1,1,1,1,1,16,512]{6,5,4,3,2,1,0:T(8,128)(2,1)S(1)}, bf16[1,1,1,1,1,16,512]{6,5,4,3,2,1,0:T(8,128)(2,1)S(1)}, u32[]{:S(2)}, u32[]{:S(2)}) collective-permute-start(bf16[1,1,1,1,1,16,512]{6,5,4,3,2,1,0:T(8,128)(2,1)S(1)} %constant_dynamic-slice_fusion.16), channel_id=1, source_target_pairs={{0,256},{16,272},{32,288},{48,304},{64,320},{80,336},{96,352},{112... | collective-permute-start | bytes 49160 | tf_op jit(solution)/shard_map/ppermute | solution.py:37
  34.2 4.0 collective-permute-start.11
  38.3 5.2 %collective-permute-start.17 = (bf16[2,1,1,1,1,16,512]{6,5,4,3,2,1,0:T(8,128)(2,1)S(1)}, bf16[2,1,1,1,1,16,512]{6,5,4,3,2,1,0:T(8,128)(2,1)S(1)}, u32[]{:S(2)}, u32[]{:S(2)}) collective-permute-start(bf16[2,1,1,1,1,16,512]{6,5,4,3,2,1,0:T(8,128)(2,1)S(1)} %constant_dynamic-slice_fusion.15), channel_id=1, source_target_pairs={{0,128},{16,144},{32,160},{48,176},{64,192},{80,208},{96,224},{112... | collective-permute-start | bytes 98312 | tf_op jit(solution)/shard_map/ppermute | solution.py:37
  43.5 4.0 collective-permute-start.1
  68.7 5.3 %collective-permute-done.3 = bf16[2,2,2,1,1,32,512]{6,5,4,3,2,1,0:T(8,128)(2,1)S(1)} collective-permute-done((bf16[2,2,2,1,1,32,512]{6,5,4,3,2,1,0:T(8,128)(2,1)S(1)}, bf16[2,2,2,1,1,32,512]{6,5,4,3,2,1,0:T(8,128)(2,1)S(1)}, u32[]{:S(2)}, u32[]{:S(2)}) %collective-permute-start.3) | collective-permute-done | bytes 262176 | tf_op jit(solution)/shard_map/ppermute | solution.py:37
  80.4 4.8 %collective-permute-start.15 = (bf16[1024,256]{1,0:T(8,128)(2,1)S(1)}, bf16[1024,256]{1,0:T(8,128)(2,1)S(1)}, u32[]{:S(2)}, u32[]{:S(2)}) collective-permute-start(bf16[1024,256]{1,0:T(8,128)(2,1)S(1)} %bitcast.116), channel_id=1, source_target_pairs={{0,1},{1,0},{2,3},{3,2},{4,5},{5,4},{6,7},{7,6},{8,9},{9,8},{10,11... | collective-permute-start | bytes 1572872 | tf_op jit(solution)/shard_map/ppermute | solution.py:37
  85.2 7.5 %collective-permute-done.20 = bf16[2,2,2,2,1,16,512]{6,5,4,3,2,1,0:T(8,128)(2,1)S(1)} collective-permute-done((bf16[2,2,2,2,1,16,512]{6,5,4,3,2,1,0:T(8,128)(2,1)S(1)}, bf16[2,2,2,2,1,16,512]{6,5,4,3,2,1,0:T(8,128)(2,1)S(1)}, u32[]{:S(2)}, u32[]{:S(2)}) %collective-permute-start.20) | collective-permute-done | bytes 262176 | tf_op jit(solution)/shard_map/ppermute | solution.py:37
  92.7 5.2 %collective-permute-start.21 = (bf16[512,512]{1,0:T(8,128)(2,1)S(1)}, bf16[512,512]{1,0:T(8,128)(2,1)S(1)}, u32[]{:S(2)}, u32[]{:S(2)}) collective-permute-start(bf16[512,512]{1,0:T(8,128)(2,1)S(1)} %bitcast.118), channel_id=1, source_target_pairs={{0,1},{1,0},{2,3},{3,2},{4,5},{5,4},{6,7},{7,6},{8,9},{9,8},{10,11... | collective-permute-start | bytes 1572872 | tf_op jit(solution)/shard_map/ppermute | solution.py:37
  112.4 4.7 %collective-permute-done.6 = bf16[1,6,16,1024]{3,2,1,0:T(8,128)(2,1)S(1)} collective-permute-done((bf16[1,6,16,1024]{3,2,1,0:T(8,128)(2,1)S(1)}, bf16[1,6,16,1024]{3,2,1,0:T(8,128)(2,1)S(1)}, u32[]{:S(2)}, u32[]{:S(2)}) %collective-permute-start.6) | collective-permute-done | bytes 196640 | tf_op jit(solution)/shard_map/ppermute | solution.py:27
  119.6 4.9 %collective-permute-start.8 = (bf16[1,20,6,1024]{3,2,1,0:T(8,128)(2,1)S(1)}, bf16[1,20,6,1024]{3,2,1,0:T(8,128)(2,1)}, u32[]{:S(2)}, u32[]{:S(2)}) collective-permute-start(bf16[1,20,6,1024]{3,2,1,0:T(8,128)(2,1)S(1)} %get-tuple-element.17), channel_id=1, source_target_pairs={{0,1},{1,2},{2,3},{3,4},{4,5},{5,6},{6,7},{7,8},{8,9},{9,10},{10,1... | collective-permute-start | bytes 737288 | tf_op jit(solution)/shard_map/ppermute | solution.py:27
  135.8 4.1 %fusion.89 = (f32[8,128]{1,0:T(8,128)S(1)}, f32[8,128,560]{1,2,0:T(8,128)}) fusion(pred[128,560]{0,1:T(8,128)(4,1)S(1)} %copy-done.27, bf16[128,8,64]{0,2,1:T(8,128)(2,1)} %bitcast.140, bf16[560,8,64]{0,2,1:T(8,128)(2,1)} %bitcast.132), kind=kOutput, calls=%fused_computation.183 | convolution fusion | flops 75694640 | bytes 3074048 | tf_op jit(solution)/shard_map/sub | solution.py:127
  143.5 4.3 %fusion.12 = f32[1,560,8,64]{1,3,2,0:T(8,128)} fusion(bf16[128,8,64]{0,2,1:T(8,128)(2,1)S(1)} %bitcast.142, f32[8,128,560]{1,2,0:T(8,128)S(1)} %fusion.90, f32[8,128,560]{1,2,0:T(8,128)} %get-tuple-element.22, f32[8,128]{1,0:T(8,128)S(1)} %get-tuple-element.21), kind=kOutput, calls=%fused_computation.14 | convolution fusion | flops 77415984 | bytes 5869568 | tf_op jit(solution)/shard_map/bhqk,bqhd->bkhd/dot_general | solution.py:151
  167.7 6.2 %collective-permute-start.22 = (f32[1,20,6,1024]{3,0,2,1:T(1,128)S(1)}, f32[1,20,6,1024]{3,0,2,1:T(1,128)S(1)}, u32[]{:S(2)}, u32[]{:S(2)}) collective-permute-start(f32[1,20,6,1024]{3,0,2,1:T(1,128)S(1)} %get-tuple-element.5), channel_id=1, source_target_pairs={{0,1},{1,2},{2,3},{3,4},{4,5},{5,6},{6,7},{7,8},{8,9},{9,10},{10,1... | collective-permute-start | bytes 1474568 | tf_op jit(solution)/shard_map/ppermute | solution.py:19
  174.0 4.3 %collective-permute-done.23 = f32[1,20,6,1024]{3,0,2,1:T(1,128)S(1)} collective-permute-done((f32[1,20,6,1024]{3,0,2,1:T(1,128)S(1)}, f32[1,20,6,1024]{3,0,2,1:T(1,128)S(1)}, u32[]{:S(2)}, u32[]{:S(2)}) %collective-permute-start.23) | collective-permute-done | bytes 491552 | tf_op jit(solution)/shard_map/ppermute | solution.py:19
  178.3 8.8 %collective-permute-done.22 = f32[1,20,6,1024]{3,0,2,1:T(1,128)S(1)} collective-permute-done((f32[1,20,6,1024]{3,0,2,1:T(1,128)S(1)}, f32[1,20,6,1024]{3,0,2,1:T(1,128)S(1)}, u32[]{:S(2)}, u32[]{:S(2)}) %collective-permute-start.22) | collective-permute-done | bytes 491552 | tf_op jit(solution)/shard_map/ppermute | solution.py:19
  192.4 4.8 %collective-permute-start.24 = (f32[1,6,16,1024]{3,0,2,1:T(1,128)}, f32[1,6,16,1024]{3,0,2,1:T(1,128)}, u32[]{:S(2)}, u32[]{:S(2)}) collective-permute-start(f32[1,6,16,1024]{3,0,2,1:T(1,128)} %get-tuple-element.9), channel_id=1, source_target_pairs={{0,16},{16,32},{32,48},{48,64},{64,80},{80,96},{96,112},{112,128},... | collective-permute-start | bytes 1179656 | tf_op jit(solution)/shard_map/ppermute | solution.py:19
  214.4 7.4 %collective-permute-done.26 = f32[2,2,2,1,1,32,32,64]{7,6,5,3,2,1,0,4:T(8,128)} collective-permute-done((f32[2,2,2,1,1,32,32,64]{7,6,5,3,2,1,0,4:T(8,128)}, f32[2,2,2,1,1,32,32,64]{7,6,5,3,2,1,0,4:T(8,128)}, u32[]{:S(2)}, u32[]{:S(2)}) %collective-permute-start.26) | collective-permute-done | bytes 2097184 | tf_op jit(solution)/shard_map/ppermute | solution.py:37
  221.8 4.5 %dynamic-slice_add_fusion = f32[2,2,2,1,1,32,32,64]{7,6,5,3,2,1,0,4:T(8,128)S(1)} fusion(f32[2,2,2,1,1,32,32,64]{7,6,5,3,2,1,0,4:T(8,128)} %collective-permute-done.26, f32[2,2,2,2,1,32,32,64]{7,6,5,3,2,1,0,4:T(8,128)} %bitcast.113, s32[]{:T(128)S(6)} %select_n.408), kind=kLoop, calls=%fused_computation.2 | loop fusion | flops 524288 | bytes 6291460 | tf_op jit(solution)/shard_map/add | solution.py:72
  228.4 9.1 %collective-permute-start.27 = (f32[2,1,2,1,1,32,32,64]{7,6,5,3,2,1,0,4:T(8,128)S(1)}, f32[2,1,2,1,1,32,32,64]{7,6,5,3,2,1,0,4:T(8,128)}, u32[]{:S(2)}, u32[]{:S(2)}) collective-permute-start(f32[2,1,2,1,1,32,32,64]{7,6,5,3,2,1,0,4:T(8,128)S(1)} %constant_dynamic-slice_fusion.10), channel_id=1, source_target_pairs={{0,4},{1,5},{2,6},{3,7},{4,0},{5,1},{6,2},{7,3},{8,12},{9,13},{10,... | collective-permute-start | bytes 3145736 | tf_op jit(solution)/shard_map/ppermute | solution.py:37
  237.6 45.8 %collective-permute-done.27 = f32[2,1,2,1,1,32,32,64]{7,6,5,3,2,1,0,4:T(8,128)} collective-permute-done((f32[2,1,2,1,1,32,32,64]{7,6,5,3,2,1,0,4:T(8,128)S(1)}, f32[2,1,2,1,1,32,32,64]{7,6,5,3,2,1,0,4:T(8,128)}, u32[]{:S(2)}, u32[]{:S(2)}) %collective-permute-start.27) | collective-permute-done | bytes 1048608 | tf_op jit(solution)/shard_map/ppermute | solution.py:37
  288.1 25.4 %collective-permute-done.28 = f32[2,1,1,1,1,32,32,64]{7,6,5,3,2,1,0,4:T(8,128)} collective-permute-done((f32[2,1,1,1,1,32,32,64]{7,6,5,3,2,1,0,4:T(8,128)S(1)}, f32[2,1,1,1,1,32,32,64]{7,6,5,3,2,1,0,4:T(8,128)}, u32[]{:S(2)}, u32[]{:S(2)}) %collective-permute-start.28) | collective-permute-done | bytes 524320 | tf_op jit(solution)/shard_map/ppermute | solution.py:37
  315.0 4.3 %collective-permute-start.29 = (f32[1,1,1,1,1,32,32,64]{7,6,5,3,2,1,0,4:T(8,128)S(1)}, f32[1,1,1,1,1,32,32,64]{7,6,5,3,2,1,0,4:T(8,128)S(1)}, u32[]{:S(2)}, u32[]{:S(2)}) collective-permute-start(f32[1,1,1,1,1,32,32,64]{7,6,5,3,2,1,0,4:T(8,128)S(1)} %constant_dynamic-slice_fusion.8), channel_id=1, source_target_pairs={{0,8},{1,9},{2,10},{3,11},{4,12},{5,13},{6,14},{7,15},{8,0},{9,1},... | collective-permute-start | bytes 786440 | tf_op jit(solution)/shard_map/ppermute | solution.py:37
  319.3 10.8 %collective-permute-done.29 = f32[1,1,1,1,1,32,32,64]{7,6,5,3,2,1,0,4:T(8,128)S(1)} collective-permute-done((f32[1,1,1,1,1,32,32,64]{7,6,5,3,2,1,0,4:T(8,128)S(1)}, f32[1,1,1,1,1,32,32,64]{7,6,5,3,2,1,0,4:T(8,128)S(1)}, u32[]{:S(2)}, u32[]{:S(2)}) %collective-permute-start.29) | collective-permute-done | bytes 262176 | tf_op jit(solution)/shard_map/ppermute | solution.py:37
  330.3 4.1 collective-permute-start.30
  334.4 5.2 %fusion.22 = bf16[8,64,128]{2,1,0:T(8,128)(2,1)} fusion(bf16[560,8,64]{0,2,1:T(8,128)(2,1)S(1)} %bitcast.134, f32[8,128,560]{1,2,0:T(8,128)} %copy-done.5, f32[8,128,560]{1,2,0:T(8,128)} %get-tuple-element.22, f32[8,128]{1,0:T(8,128)S(1)} %copy-done.36), kind=kOutput, calls=%fused_computation.25 | convolution fusion | flops 77481520 | bytes 5296128 | tf_op jit(solution)/shard_map/bhqk,bkhd->bqhd/dot_general | solution.py:148
  345.7 6.9 %collective-permute-start.32 = (f32[2,2,1,1,1,1,32,64]{7,6,4,3,2,1,0,5:T(8,128)S(1)}, f32[2,2,1,1,1,1,32,64]{7,6,4,3,2,1,0,5:T(8,128)S(1)}, u32[]{:S(2)}, u32[]{:S(2)}) collective-permute-start(f32[2,2,1,1,1,1,32,64]{7,6,4,3,2,1,0,5:T(8,128)S(1)} %constant_dynamic-slice_fusion.5), channel_id=1, source_target_pairs={{0,64},{16,80},{32,96},{48,112},{64,0},{80,16},{96,32},{112,48},{1... | collective-permute-start | bytes 98312 | tf_op jit(solution)/shard_map/ppermute | solution.py:37
  354.3 6.3 %collective-permute-start.33 = (f32[2,1,1,1,1,1,32,64]{7,6,4,3,2,1,0,5:T(8,128)S(1)}, f32[2,1,1,1,1,1,32,64]{7,6,4,3,2,1,0,5:T(8,128)S(1)}, u32[]{:S(2)}, u32[]{:S(2)}) collective-permute-start(f32[2,1,1,1,1,1,32,64]{7,6,4,3,2,1,0,5:T(8,128)S(1)} %constant_dynamic-slice_fusion.4), channel_id=1, source_target_pairs={{0,128},{16,144},{32,160},{48,176},{64,192},{80,208},{96,224},{112... | collective-permute-start | bytes 49160 | tf_op jit(solution)/shard_map/ppermute | solution.py:37
  362.9 7.8 %collective-permute-start.34 = (f32[1,1,1,1,1,1,32,64]{7,6,4,3,2,1,0,5:T(8,128)S(1)}, f32[1,1,1,1,1,1,32,64]{7,6,4,3,2,1,0,5:T(8,128)S(1)}, u32[]{:S(2)}, u32[]{:S(2)}) collective-permute-start(f32[1,1,1,1,1,1,32,64]{7,6,4,3,2,1,0,5:T(8,128)S(1)} %constant_dynamic-slice_fusion.3), channel_id=1, source_target_pairs={{0,256},{16,272},{32,288},{48,304},{64,320},{80,336},{96,352},{112... | collective-permute-start | bytes 24584 | tf_op jit(solution)/shard_map/ppermute | solution.py:37
  371.6 4.4 %collective-permute-done.34 = f32[1,1,1,1,1,1,32,64]{7,6,4,3,2,1,0,5:T(8,128)S(1)} collective-permute-done((f32[1,1,1,1,1,1,32,64]{7,6,4,3,2,1,0,5:T(8,128)S(1)}, f32[1,1,1,1,1,1,32,64]{7,6,4,3,2,1,0,5:T(8,128)S(1)}, u32[]{:S(2)}, u32[]{:S(2)}) %collective-permute-start.34) | collective-permute-done | bytes 8224 | tf_op jit(solution)/shard_map/ppermute | solution.py:37
  387.4 5.0 %collective-permute-start.37 = (f32[2,2,1,1,32,64]{5,3,2,1,0,4:T(1,128)S(1)}, f32[2,2,1,1,32,64]{5,3,2,1,0,4:T(1,128)S(1)}, u32[]{:S(2)}, u32[]{:S(2)}) collective-permute-start(f32[2,2,1,1,32,64]{5,3,2,1,0,4:T(1,128)S(1)} %constant_dynamic-slice_fusion), channel_id=1, source_target_pairs={{0,2},{1,3},{2,0},{3,1},{4,6},{5,7},{6,4},{7,5},{8,10},{9,11},{10,... | collective-permute-start | bytes 98312 | tf_op jit(solution)/shard_map/ppermute | solution.py:37
  395.7 11.8 %collective-permute-start.38 = (f32[2,2,2,1,32,64]{5,3,2,1,0,4:T(1,128)S(1)}, f32[2,2,2,1,32,64]{5,3,2,1,0,4:T(1,128)S(1)}, u32[]{:S(2)}, u32[]{:S(2)}) collective-permute-start(f32[2,2,2,1,32,64]{5,3,2,1,0,4:T(1,128)S(1)} %constant_dynamic-slice_fusion.17), channel_id=1, source_target_pairs={{0,1},{1,0},{2,3},{3,2},{4,5},{5,4},{6,7},{7,6},{8,9},{9,8},{10,11... | collective-permute-start | bytes 196616 | tf_op jit(solution)/shard_map/ppermute | solution.py:37
  (249 shorter events, 144.2 us)
Async XLA Ops:
  1.7 41.7 %collective-permute-start = (bf16[1,1,1,1,1,32,512]{6,5,4,3,2,1,0:T(8,128)(2,1)S(1)}, bf16[1,1,1,1,1,32,512]{6,5,4,3,2,1,0:T(8,128)(2,1)S(1)}, u32[]{:S(2)}, u32[]{:S(2)}) collective-permute-start(bf16[1,1,1,1,1,32,512]{6,5,4,3,2,1,0:T(8,128)(2,1)S(1)} %constant_dynamic-slice_fusion.27), channel_id=1, source_target_pairs={{0,256},{16,272},{32,288},{48,304},{64,320},{80,336},{96,352},{112... | collective-permute-start | bytes 98312 | tf_op jit(solution)/shard_map/ppermute | solution.py:37
  18.8 15.3 %collective-permute-start.10 = (bf16[1,1,1,1,1,32,256]{6,5,4,3,2,1,0:T(8,128)(2,1)S(1)}, bf16[1,1,1,1,1,32,256]{6,5,4,3,2,1,0:T(8,128)(2,1)S(1)}, u32[]{:S(2)}, u32[]{:S(2)}) collective-permute-start(bf16[1,1,1,1,1,32,256]{6,5,4,3,2,1,0:T(8,128)(2,1)S(1)} %constant_dynamic-slice_fusion.22), channel_id=1, source_target_pairs={{0,256},{16,272},{32,288},{48,304},{64,320},{80,336},{96,352},{112... | collective-permute-start | bytes 49160 | tf_op jit(solution)/shard_map/ppermute | solution.py:37
  20.8 17.4 %collective-permute-start.16 = (bf16[1,1,1,1,1,16,512]{6,5,4,3,2,1,0:T(8,128)(2,1)S(1)}, bf16[1,1,1,1,1,16,512]{6,5,4,3,2,1,0:T(8,128)(2,1)S(1)}, u32[]{:S(2)}, u32[]{:S(2)}) collective-permute-start(bf16[1,1,1,1,1,16,512]{6,5,4,3,2,1,0:T(8,128)(2,1)S(1)} %constant_dynamic-slice_fusion.16), channel_id=1, source_target_pairs={{0,256},{16,272},{32,288},{48,304},{64,320},{80,336},{96,352},{112... | collective-permute-start | bytes 49160 | tf_op jit(solution)/shard_map/ppermute | solution.py:37
  34.2 13.3 %collective-permute-start.11 = (bf16[2,1,1,1,1,32,256]{6,5,4,3,2,1,0:T(8,128)(2,1)S(1)}, bf16[2,1,1,1,1,32,256]{6,5,4,3,2,1,0:T(8,128)(2,1)S(1)}, u32[]{:S(2)}, u32[]{:S(2)}) collective-permute-start(bf16[2,1,1,1,1,32,256]{6,5,4,3,2,1,0:T(8,128)(2,1)S(1)} %constant_dynamic-slice_fusion.21), channel_id=1, source_target_pairs={{0,128},{16,144},{32,160},{48,176},{64,192},{80,208},{96,224},{112... | collective-permute-start | bytes 98312 | tf_op jit(solution)/shard_map/ppermute | solution.py:37
  38.3 12.4 %collective-permute-start.17 = (bf16[2,1,1,1,1,16,512]{6,5,4,3,2,1,0:T(8,128)(2,1)S(1)}, bf16[2,1,1,1,1,16,512]{6,5,4,3,2,1,0:T(8,128)(2,1)S(1)}, u32[]{:S(2)}, u32[]{:S(2)}) collective-permute-start(bf16[2,1,1,1,1,16,512]{6,5,4,3,2,1,0:T(8,128)(2,1)S(1)} %constant_dynamic-slice_fusion.15), channel_id=1, source_target_pairs={{0,128},{16,144},{32,160},{48,176},{64,192},{80,208},{96,224},{112... | collective-permute-start | bytes 98312 | tf_op jit(solution)/shard_map/ppermute | solution.py:37
  43.5 11.4 %collective-permute-start.1 = (bf16[2,1,1,1,1,32,512]{6,5,4,3,2,1,0:T(8,128)(2,1)S(1)}, bf16[2,1,1,1,1,32,512]{6,5,4,3,2,1,0:T(8,128)(2,1)S(1)}, u32[]{:S(2)}, u32[]{:S(2)}) collective-permute-start(bf16[2,1,1,1,1,32,512]{6,5,4,3,2,1,0:T(8,128)(2,1)S(1)} %constant_dynamic-slice_fusion.26), channel_id=1, source_target_pairs={{0,128},{16,144},{32,160},{48,176},{64,192},{80,208},{96,224},{112... | collective-permute-start | bytes 196616 | tf_op jit(solution)/shard_map/ppermute | solution.py:37
  47.6 9.5 %collective-permute-start.12 = (bf16[2,2,1,1,1,32,256]{6,5,4,3,2,1,0:T(8,128)(2,1)S(1)}, bf16[2,2,1,1,1,32,256]{6,5,4,3,2,1,0:T(8,128)(2,1)S(1)}, u32[]{:S(2)}, u32[]{:S(2)}) collective-permute-start(bf16[2,2,1,1,1,32,256]{6,5,4,3,2,1,0:T(8,128)(2,1)S(1)} %constant_dynamic-slice_fusion.20), channel_id=1, source_target_pairs={{0,64},{16,80},{32,96},{48,112},{64,0},{80,16},{96,32},{112,48},{1... | collective-permute-start | bytes 196616 | tf_op jit(solution)/shard_map/ppermute | solution.py:37
  50.8 9.0 %collective-permute-start.18 = (bf16[2,2,1,1,1,16,512]{6,5,4,3,2,1,0:T(8,128)(2,1)S(1)}, bf16[2,2,1,1,1,16,512]{6,5,4,3,2,1,0:T(8,128)(2,1)S(1)}, u32[]{:S(2)}, u32[]{:S(2)}) collective-permute-start(bf16[2,2,1,1,1,16,512]{6,5,4,3,2,1,0:T(8,128)(2,1)S(1)} %constant_dynamic-slice_fusion.14), channel_id=1, source_target_pairs={{0,64},{16,80},{32,96},{48,112},{64,0},{80,16},{96,32},{112,48},{1... | collective-permute-start | bytes 196616 | tf_op jit(solution)/shard_map/ppermute | solution.py:37
  55.0 8.4 %collective-permute-start.2 = (bf16[2,2,1,1,1,32,512]{6,5,4,3,2,1,0:T(8,128)(2,1)S(1)}, bf16[2,2,1,1,1,32,512]{6,5,4,3,2,1,0:T(8,128)(2,1)S(1)}, u32[]{:S(2)}, u32[]{:S(2)}) collective-permute-start(bf16[2,2,1,1,1,32,512]{6,5,4,3,2,1,0:T(8,128)(2,1)S(1)} %constant_dynamic-slice_fusion.25), channel_id=1, source_target_pairs={{0,64},{16,80},{32,96},{48,112},{64,0},{80,16},{96,32},{112,48},{1... | collective-permute-start | bytes 393224 | tf_op jit(solution)/shard_map/ppermute | solution.py:37
  57.1 8.3 %collective-permute-start.13 = (bf16[2,2,2,1,1,32,256]{6,5,4,3,2,1,0:T(8,128)(2,1)S(1)}, bf16[2,2,2,1,1,32,256]{6,5,4,3,2,1,0:T(8,128)(2,1)S(1)}, u32[]{:S(2)}, u32[]{:S(2)}) collective-permute-start(bf16[2,2,2,1,1,32,256]{6,5,4,3,2,1,0:T(8,128)(2,1)S(1)} %constant_dynamic-slice_fusion.19), channel_id=1, source_target_pairs={{0,32},{16,48},{32,0},{48,16},{64,96},{80,112},{96,64},{112,80},{1... | collective-permute-start | bytes 393224 | tf_op jit(solution)/shard_map/ppermute | solution.py:37
  59.8 8.8 %collective-permute-start.19 = (bf16[2,2,2,1,1,16,512]{6,5,4,3,2,1,0:T(8,128)(2,1)S(1)}, bf16[2,2,2,1,1,16,512]{6,5,4,3,2,1,0:T(8,128)(2,1)S(1)}, u32[]{:S(2)}, u32[]{:S(2)}) collective-permute-start(bf16[2,2,2,1,1,16,512]{6,5,4,3,2,1,0:T(8,128)(2,1)S(1)} %constant_dynamic-slice_fusion.13), channel_id=1, source_target_pairs={{0,32},{16,48},{32,0},{48,16},{64,96},{80,112},{96,64},{112,80},{1... | collective-permute-start | bytes 393224 | tf_op jit(solution)/shard_map/ppermute | solution.py:37
  63.5 10.5 %collective-permute-start.3 = (bf16[2,2,2,1,1,32,512]{6,5,4,3,2,1,0:T(8,128)(2,1)S(1)}, bf16[2,2,2,1,1,32,512]{6,5,4,3,2,1,0:T(8,128)(2,1)S(1)}, u32[]{:S(2)}, u32[]{:S(2)}) collective-permute-start(bf16[2,2,2,1,1,32,512]{6,5,4,3,2,1,0:T(8,128)(2,1)S(1)} %constant_dynamic-slice_fusion.24), channel_id=1, source_target_pairs={{0,32},{16,48},{32,0},{48,16},{64,96},{80,112},{96,64},{112,80},{1... | collective-permute-start | bytes 786440 | tf_op jit(solution)/shard_map/ppermute | solution.py:37
  65.5 14.9 %collective-permute-start.14 = (bf16[2,2,2,2,1,32,256]{6,5,4,3,2,1,0:T(8,128)(2,1)S(1)}, bf16[2,2,2,2,1,32,256]{6,5,4,3,2,1,0:T(8,128)(2,1)S(1)}, u32[]{:S(2)}, u32[]{:S(2)}) collective-permute-start(bf16[2,2,2,2,1,32,256]{6,5,4,3,2,1,0:T(8,128)(2,1)S(1)} %constant_dynamic-slice_fusion.18), channel_id=1, source_target_pairs={{0,16},{16,0},{32,48},{48,32},{64,80},{80,64},{96,112},{112,96},{1... | collective-permute-start | bytes 786440 | tf_op jit(solution)/shard_map/ppermute | solution.py:37
  74.1 23.8 %collective-permute-start.4 = (bf16[2,2,2,2,1,32,512]{6,5,4,3,2,1,0:T(8,128)(2,1)S(1)}, bf16[2,2,2,2,1,32,512]{6,5,4,3,2,1,0:T(8,128)(2,1)S(1)}, u32[]{:S(2)}, u32[]{:S(2)}) collective-permute-start(bf16[2,2,2,2,1,32,512]{6,5,4,3,2,1,0:T(8,128)(2,1)S(1)} %constant_dynamic-slice_fusion.23), channel_id=1, source_target_pairs={{0,16},{16,0},{32,48},{48,32},{64,80},{80,64},{96,112},{112,96},{1... | collective-permute-start | bytes 1572872 | tf_op jit(solution)/shard_map/ppermute | solution.py:37
  77.3 15.4 %collective-permute-start.20 = (bf16[2,2,2,2,1,16,512]{6,5,4,3,2,1,0:T(8,128)(2,1)S(1)}, bf16[2,2,2,2,1,16,512]{6,5,4,3,2,1,0:T(8,128)(2,1)S(1)}, u32[]{:S(2)}, u32[]{:S(2)}) collective-permute-start(bf16[2,2,2,2,1,16,512]{6,5,4,3,2,1,0:T(8,128)(2,1)S(1)} %constant_dynamic-slice_fusion.12), channel_id=1, source_target_pairs={{0,16},{16,0},{32,48},{48,32},{64,80},{80,64},{96,112},{112,96},{1... | collective-permute-start | bytes 786440 | tf_op jit(solution)/shard_map/ppermute | solution.py:37
  80.4 20.0 %collective-permute-start.15 = (bf16[1024,256]{1,0:T(8,128)(2,1)S(1)}, bf16[1024,256]{1,0:T(8,128)(2,1)S(1)}, u32[]{:S(2)}, u32[]{:S(2)}) collective-permute-start(bf16[1024,256]{1,0:T(8,128)(2,1)S(1)} %bitcast.116), channel_id=1, source_target_pairs={{0,1},{1,0},{2,3},{3,2},{4,5},{5,4},{6,7},{7,6},{8,9},{9,8},{10,11... | collective-permute-start | bytes 1572872 | tf_op jit(solution)/shard_map/ppermute | solution.py:37
  105.4 11.6 %collective-permute-start.6 = (bf16[1,6,16,1024]{3,2,1,0:T(8,128)(2,1)S(1)}, bf16[1,6,16,1024]{3,2,1,0:T(8,128)(2,1)S(1)}, u32[]{:S(2)}, u32[]{:S(2)}) collective-permute-start(bf16[1,6,16,1024]{3,2,1,0:T(8,128)(2,1)S(1)} %get-tuple-element.19), channel_id=1, source_target_pairs={{0,16},{16,32},{32,48},{48,64},{64,80},{80,96},{96,112},{112,128},... | collective-permute-start | bytes 589832 | tf_op jit(solution)/shard_map/ppermute | solution.py:27
  117.2 11.0 %collective-permute-start.9 = (bf16[1,20,6,1024]{3,2,1,0:T(8,128)(2,1)S(1)}, bf16[1,20,6,1024]{3,2,1,0:T(8,128)(2,1)S(1)}, u32[]{:S(2)}, u32[]{:S(2)}) collective-permute-start(bf16[1,20,6,1024]{3,2,1,0:T(8,128)(2,1)S(1)} %get-tuple-element.18), channel_id=1, source_target_pairs={{1,0},{2,1},{3,2},{4,3},{5,4},{6,5},{7,6},{8,7},{9,8},{10,9},{11,1... | collective-permute-start | bytes 737288 | tf_op jit(solution)/shard_map/ppermute | solution.py:30
  119.6 11.1 %collective-permute-start.8 = (bf16[1,20,6,1024]{3,2,1,0:T(8,128)(2,1)S(1)}, bf16[1,20,6,1024]{3,2,1,0:T(8,128)(2,1)}, u32[]{:S(2)}, u32[]{:S(2)}) collective-permute-start(bf16[1,20,6,1024]{3,2,1,0:T(8,128)(2,1)S(1)} %get-tuple-element.17), channel_id=1, source_target_pairs={{0,1},{1,2},{2,3},{3,4},{4,5},{5,6},{6,7},{7,8},{8,9},{9,10},{10,1... | collective-permute-start | bytes 737288 | tf_op jit(solution)/shard_map/ppermute | solution.py:27
  165.8 12.5 %collective-permute-start.23 = (f32[1,20,6,1024]{3,0,2,1:T(1,128)S(1)}, f32[1,20,6,1024]{3,0,2,1:T(1,128)S(1)}, u32[]{:S(2)}, u32[]{:S(2)}) collective-permute-start(f32[1,20,6,1024]{3,0,2,1:T(1,128)S(1)} %get-tuple-element.6), channel_id=1, source_target_pairs={{1,0},{2,1},{3,2},{4,3},{5,4},{6,5},{7,6},{8,7},{9,8},{10,9},{11,1... | collective-permute-start | bytes 1474568 | tf_op jit(solution)/shard_map/ppermute | solution.py:19
  167.7 19.4 %collective-permute-start.22 = (f32[1,20,6,1024]{3,0,2,1:T(1,128)S(1)}, f32[1,20,6,1024]{3,0,2,1:T(1,128)S(1)}, u32[]{:S(2)}, u32[]{:S(2)}) collective-permute-start(f32[1,20,6,1024]{3,0,2,1:T(1,128)S(1)} %get-tuple-element.5), channel_id=1, source_target_pairs={{0,1},{1,2},{2,3},{3,4},{4,5},{5,6},{6,7},{7,8},{8,9},{9,10},{10,1... | collective-permute-start | bytes 1474568 | tf_op jit(solution)/shard_map/ppermute | solution.py:19
  191.2 8.7 %collective-permute-start.25 = (f32[1,6,16,1024]{3,0,2,1:T(1,128)}, f32[1,6,16,1024]{3,0,2,1:T(1,128)S(1)}, u32[]{:S(2)}, u32[]{:S(2)}) collective-permute-start(f32[1,6,16,1024]{3,0,2,1:T(1,128)} %get-tuple-element.10), channel_id=1, source_target_pairs={{16,0},{32,16},{48,32},{64,48},{80,64},{96,80},{112,96},{128,112},... | collective-permute-start | bytes 1179656 | tf_op jit(solution)/shard_map/ppermute | solution.py:19
  192.4 10.8 %collective-permute-start.24 = (f32[1,6,16,1024]{3,0,2,1:T(1,128)}, f32[1,6,16,1024]{3,0,2,1:T(1,128)}, u32[]{:S(2)}, u32[]{:S(2)}) collective-permute-start(f32[1,6,16,1024]{3,0,2,1:T(1,128)} %get-tuple-element.9), channel_id=1, source_target_pairs={{0,16},{16,32},{32,48},{48,64},{64,80},{80,96},{96,112},{112,128},... | collective-permute-start | bytes 1179656 | tf_op jit(solution)/shard_map/ppermute | solution.py:19
  212.4 9.4 %collective-permute-start.26 = (f32[2,2,2,1,1,32,32,64]{7,6,5,3,2,1,0,4:T(8,128)}, f32[2,2,2,1,1,32,32,64]{7,6,5,3,2,1,0,4:T(8,128)}, u32[]{:S(2)}, u32[]{:S(2)}) collective-permute-start(f32[2,2,2,1,1,32,32,64]{7,6,5,3,2,1,0,4:T(8,128)} %constant_dynamic-slice_fusion.11), channel_id=1, source_target_pairs={{0,1},{1,0},{2,3},{3,2},{4,5},{5,4},{6,7},{7,6},{8,9},{9,8},{10,11... | collective-permute-start | bytes 6291464 | tf_op jit(solution)/shard_map/ppermute | solution.py:37
  228.4 54.9 %collective-permute-start.27 = (f32[2,1,2,1,1,32,32,64]{7,6,5,3,2,1,0,4:T(8,128)S(1)}, f32[2,1,2,1,1,32,32,64]{7,6,5,3,2,1,0,4:T(8,128)}, u32[]{:S(2)}, u32[]{:S(2)}) collective-permute-start(f32[2,1,2,1,1,32,32,64]{7,6,5,3,2,1,0,4:T(8,128)S(1)} %constant_dynamic-slice_fusion.10), channel_id=1, source_target_pairs={{0,4},{1,5},{2,6},{3,7},{4,0},{5,1},{6,2},{7,3},{8,12},{9,13},{10,... | collective-permute-start | bytes 3145736 | tf_op jit(solution)/shard_map/ppermute | solution.py:37
  286.1 27.3 %collective-permute-start.28 = (f32[2,1,1,1,1,32,32,64]{7,6,5,3,2,1,0,4:T(8,128)S(1)}, f32[2,1,1,1,1,32,32,64]{7,6,5,3,2,1,0,4:T(8,128)}, u32[]{:S(2)}, u32[]{:S(2)}) collective-permute-start(f32[2,1,1,1,1,32,32,64]{7,6,5,3,2,1,0,4:T(8,128)S(1)} %constant_dynamic-slice_fusion.9), channel_id=1, source_target_pairs={{0,2},{1,3},{2,0},{3,1},{4,6},{5,7},{6,4},{7,5},{8,10},{9,11},{10,... | collective-permute-start | bytes 1572872 | tf_op jit(solution)/shard_map/ppermute | solution.py:37
  315.0 15.2 %collective-permute-start.29 = (f32[1,1,1,1,1,32,32,64]{7,6,5,3,2,1,0,4:T(8,128)S(1)}, f32[1,1,1,1,1,32,32,64]{7,6,5,3,2,1,0,4:T(8,128)S(1)}, u32[]{:S(2)}, u32[]{:S(2)}) collective-permute-start(f32[1,1,1,1,1,32,32,64]{7,6,5,3,2,1,0,4:T(8,128)S(1)} %constant_dynamic-slice_fusion.8), channel_id=1, source_target_pairs={{0,8},{1,9},{2,10},{3,11},{4,12},{5,13},{6,14},{7,15},{8,0},{9,1},... | collective-permute-start | bytes 786440 | tf_op jit(solution)/shard_map/ppermute | solution.py:37
  330.3 9.3 %collective-permute-start.30 = (f32[2,2,2,2,1,1,32,64]{7,6,4,3,2,1,0,5:T(8,128)S(1)}, f32[2,2,2,2,1,1,32,64]{7,6,4,3,2,1,0,5:T(8,128)S(1)}, u32[]{:S(2)}, u32[]{:S(2)}) collective-permute-start(f32[2,2,2,2,1,1,32,64]{7,6,4,3,2,1,0,5:T(8,128)S(1)} %constant_dynamic-slice_fusion.7), channel_id=1, source_target_pairs={{0,16},{16,0},{32,48},{48,32},{64,80},{80,64},{96,112},{112,96},{1... | collective-permute-start | bytes 393224 | tf_op jit(solution)/shard_map/ppermute | solution.py:37
  345.7 8.6 %collective-permute-start.32 = (f32[2,2,1,1,1,1,32,64]{7,6,4,3,2,1,0,5:T(8,128)S(1)}, f32[2,2,1,1,1,1,32,64]{7,6,4,3,2,1,0,5:T(8,128)S(1)}, u32[]{:S(2)}, u32[]{:S(2)}) collective-permute-start(f32[2,2,1,1,1,1,32,64]{7,6,4,3,2,1,0,5:T(8,128)S(1)} %constant_dynamic-slice_fusion.5), channel_id=1, source_target_pairs={{0,64},{16,80},{32,96},{48,112},{64,0},{80,16},{96,32},{112,48},{1... | collective-permute-start | bytes 98312 | tf_op jit(solution)/shard_map/ppermute | solution.py:37
  354.3 8.6 %collective-permute-start.33 = (f32[2,1,1,1,1,1,32,64]{7,6,4,3,2,1,0,5:T(8,128)S(1)}, f32[2,1,1,1,1,1,32,64]{7,6,4,3,2,1,0,5:T(8,128)S(1)}, u32[]{:S(2)}, u32[]{:S(2)}) collective-permute-start(f32[2,1,1,1,1,1,32,64]{7,6,4,3,2,1,0,5:T(8,128)S(1)} %constant_dynamic-slice_fusion.4), channel_id=1, source_target_pairs={{0,128},{16,144},{32,160},{48,176},{64,192},{80,208},{96,224},{112... | collective-permute-start | bytes 49160 | tf_op jit(solution)/shard_map/ppermute | solution.py:37
  362.9 13.2 %collective-permute-start.34 = (f32[1,1,1,1,1,1,32,64]{7,6,4,3,2,1,0,5:T(8,128)S(1)}, f32[1,1,1,1,1,1,32,64]{7,6,4,3,2,1,0,5:T(8,128)S(1)}, u32[]{:S(2)}, u32[]{:S(2)}) collective-permute-start(f32[1,1,1,1,1,1,32,64]{7,6,4,3,2,1,0,5:T(8,128)S(1)} %constant_dynamic-slice_fusion.3), channel_id=1, source_target_pairs={{0,256},{16,272},{32,288},{48,304},{64,320},{80,336},{96,352},{112... | collective-permute-start | bytes 24584 | tf_op jit(solution)/shard_map/ppermute | solution.py:37
  395.7 12.8 %collective-permute-start.38 = (f32[2,2,2,1,32,64]{5,3,2,1,0,4:T(1,128)S(1)}, f32[2,2,2,1,32,64]{5,3,2,1,0,4:T(1,128)S(1)}, u32[]{:S(2)}, u32[]{:S(2)}) collective-permute-start(f32[2,2,2,1,32,64]{5,3,2,1,0,4:T(1,128)S(1)} %constant_dynamic-slice_fusion.17), channel_id=1, source_target_pairs={{0,1},{1,0},{2,3},{3,2},{4,5},{5,4},{6,7},{7,6},{8,9},{9,8},{10,11... | collective-permute-start | bytes 196616 | tf_op jit(solution)/shard_map/ppermute | solution.py:37
  (44 other events, 612.8 us)

commit v3 on v2

--- a/solution.py
+++ b/solution.py
@@ -32,16 +32,21 @@
     return block
 
 
-def partner_swap(value, axis, bit):
+def partner_swap(value, axis, mask):
     count = lax.axis_size(axis)
-    return lax.ppermute(value, axis, [(i, i ^ (1 << bit)) for i in range(count)])
+    return lax.ppermute(value, axis, [(i, i ^ mask) for i in range(count)])
 
 
 def axis_bit(axis, bit):
     return (lax.axis_index(axis) // (1 << bit)) % 2
 
 
-def gather_by_bits(block, axis, bits):
+def flips(group):
+    for code in range(1, 1 << len(group)):
+        yield [(code >> k) % 2 for k in range(len(group))]
+
+
+def gather_by_bits(block, axis, groups):
     levels = lax.axis_size(axis).bit_length() - 1
     mine = [axis_bit(axis, bit) for bit in range(levels)]
     zero = [0] * block.ndim
@@ -50,26 +55,41 @@
         held, block.reshape((1,) * levels + block.shape), mine[::-1] + zero
     )
     done = set()
-    for bit in bits:
+    for group in groups:
         start = [0 if b in done else mine[b] for b in range(levels)]
         size = [2 if b in done else 1 for b in range(levels)]
         region = lax.dynamic_slice(held, start[::-1] + zero, size[::-1] + list(block.shape))
-        other = partner_swap(region, axis, bit)
-        start[bit] = 1 - mine[bit]
-        held = lax.dynamic_update_slice(held, other, start[::-1] + zero)
-        done.add(bit)
+        arrived = []
+        for flip in flips(group):
+            mask = sum(f << b for f, b in zip(flip, group))
+            place = list(start)
+            for f, b in zip(flip, group):
+                place[b] = (mine[b] + f) % 2
+            arrived.append((partner_swap(region, axis, mask), place))
+        for other, place in arrived:
+            held = lax.dynamic_update_slice(held, other, place[::-1] + zero)
+        done.update(group)
     return held.reshape((-1,) + block.shape)
 
 
-def scatter_by_bits(total, axis, bits):
+def scatter_by_bits(total, axis, groups):
     levels = lax.axis_size(axis).bit_length() - 1
+    mine = [axis_bit(axis, bit) for bit in range(levels)]
     held = total.reshape((2,) * levels + (total.shape[0] // 2**levels,) + total.shape[1:])
-    for bit in bits:
-        place = levels - 1 - bit
-        own = axis_bit(axis, bit)
-        keep = lax.dynamic_index_in_dim(held, own, place)
-        send = lax.dynamic_index_in_dim(held, 1 - own, place)
-        held = keep + partner_swap(send, axis, bit)
+    rest = [0] * (held.ndim - levels)
+    for group in groups:
+        size = [1 if b in group else held.shape[levels - 1 - b] for b in range(levels)]
+        size = size[::-1] + list(held.shape[levels:])
+        own = [mine[b] if b in group else 0 for b in range(levels)]
+        summed = lax.dynamic_slice(held, own[::-1] + rest, size)
+        for flip in flips(group):
+            mask = sum(f << b for f, b in zip(flip, group))
+            place = list(own)
+            for f, b in zip(flip, group):
+                place[b] = (mine[b] + f) % 2
+            send = lax.dynamic_slice(held, place[::-1] + rest, size)
+            summed = summed + partner_swap(send, axis, mask)
+        held = summed
     return held.reshape(held.shape[levels:])
 
 
@@ -81,7 +101,7 @@
     rows = rows.reshape(-1, half)
     held = jnp.zeros((2,) + rows.shape, rows.dtype)
     held = lax.dynamic_update_slice(held, rows[None], (own, 0, 0))
-    held = lax.dynamic_update_slice(held, partner_swap(rows, "col", 0)[None], (1 - own, 0, 0))
+    held = lax.dynamic_update_slice(held, partner_swap(rows, "col", 1)[None], (1 - own, 0, 0))
     return jnp.concatenate([held[0], held[1]], axis=1)
 
 
@@ -199,10 +219,11 @@
     ext_cols = tile_cols + 2 * RADIUS
     standard, spread, normed = normalize(inputs, norm_gain)
     flat_norm = normed.reshape(-1, model_width)
-    row_bits = list(range(lax.axis_size("row").bit_length() - 1))
-    full_keyvalue = gather_weight(w_keyvalue, row_bits[::-1])
-    full_query = gather_weight(w_query, row_bits[::-1])
-    full_output = gather_weight(w_output, row_bits[::-1])
+    row_levels = lax.axis_size("row").bit_length() - 1
+    row_groups = [list(range(b, min(b + 2, row_levels))) for b in range(0, row_levels, 2)]
+    full_keyvalue = gather_weight(w_keyvalue, row_groups[::-1])
+    full_query = gather_weight(w_query, row_groups[::-1])
+    full_output = gather_weight(w_output, row_groups[::-1])
     inner_width = full_query.shape[1]
     queries = jnp.dot(flat_norm, full_query, preferred_element_type=jnp.float32).astype(
         jnp.bfloat16
@@ -237,7 +258,8 @@
     owned = fold_rows(fold_cols(keyvalue_part))
     token_grad = owned.astype(jnp.bfloat16).reshape(-1, 2 * inner_width)
     row_count, col_count = lax.axis_size("row"), lax.axis_size("col")
-    col_bits = list(range(col_count.bit_length() - 1))
+    col_levels = col_count.bit_length() - 1
+    col_groups = [[0, 2], [1, 3]] if col_levels == 4 else [[b] for b in range(col_levels)]
     feature_part = model_width // row_count
     column_part = token_grad.shape[1] // col_count
     partial = jnp.einsum(
@@ -246,10 +268,9 @@
         token_grad.reshape(-1, col_count, column_part),
         preferred_element_type=jnp.float32,
     )
-    col_order = [0] + col_bits[2:3] + col_bits[1:2] + col_bits[3:]
-    col_part = scatter_by_bits(partial, "col", col_order)[0]
-    rows_part = scatter_by_bits(col_part, "row", row_bits)[0]
-    keyvalue_grad = gather_by_bits(rows_part, "col", col_bits[::-1])
+    col_part = scatter_by_bits(partial, "col", col_groups)[0]
+    rows_part = scatter_by_bits(col_part, "row", row_groups)[0]
+    keyvalue_grad = gather_by_bits(rows_part, "col", col_groups[::-1])
     keyvalue_grad = keyvalue_grad.transpose(1, 0, 2).reshape(feature_part, -1)
     normed_grad = lax.dot_general(
         query_grad.reshape(-1, inner_width),

time: 414 us -> 443 us (1.070)
  starting transfers between devices: 174 us -> 215 us
  waiting for transfers between devices: 146 us -> 141 us
    ppermute x31 -> x43, starting transfers between devices: 147 us -> 188 us  [partner_swap(): return lax.ppermute(value, axis, [(i, i ^ mask) for i in range(count)])]
    ppermute x31 -> x43, waiting for transfers between devices: 119 us -> 115 us  [partner_swap(): return lax.ppermute(value, axis, [(i, i ^ mask) for i in range(count)])]
    unnamed x78 -> x48, local copies, waits for them, and re-layouts: 9.7 us -> 8.47 us
  transfers between devices with their start and end apart: 39 -> 51, of which waited for: 23 -> 18; matrix products, arithmetic and copies ran while one was open for 5% -> 5% of each run, Pallas kernels for 0% -> 0%
where the time goes in v3:
time: 443 us; the launch traced here: 441 us
  starting transfers between devices  215 us (49%)
  waiting for transfers between devices  141 us (32%)
  local copies, waits for them, and re-layouts  41.6 us (9%)
  matrix products  26.2 us (6%)
  other arithmetic  15 us (3%)
    ppermute x43, starting transfers between devices, partner_swap(): return lax.ppermute(value, axis, [(i, i ^ mask) for i in range(count)])  188 us
    ppermute x43, waiting for transfers between devices, partner_swap(): return lax.ppermute(value, axis, [(i, i ^ mask) for i in range(count)])  115 us
    ppermute x4, waiting for transfers between devices, shifted(): lax.ppermute(value, axis, [(source, source + steps) for source in range(f...  17.3 us
    ppermute x4, starting transfers between devices, shifted(): lax.ppermute(value, axis, [(source, source + steps) for source in range(f...  14.2 us
  transfers between devices with their start and end apart: 51, of which 18 were waited for; matrix products, arithmetic and copies ran while one was open for 5% of the time, Pallas kernels for 0%

profile of v3, /device:TPU:1, one launch (start us, length us, event | category | flops | bytes accessed | tf_op | source)
XLA Modules:
  0.0 441.1 jit_solution(4397317879691379959)
XLA Ops:
  1.7 16.3 %collective-permute-start = (bf16[1,1,1,1,1,32,512]{6,5,4,3,2,1,0:T(8,128)(2,1)S(1)}, bf16[1,1,1,1,1,32,512]{6,5,4,3,2,1,0:T(8,128)(2,1)S(1)}, u32[]{:S(2)}, u32[]{:S(2)}) collective-permute-start(bf16[1,1,1,1,1,32,512]{6,5,4,3,2,1,0:T(8,128)(2,1)S(1)} %constant_dynamic-slice_fusion.23), channel_id=1, source_target_pairs={{0,256},{16,272},{32,288},{48,304},{64,320},{80,336},{96,352},{112... | collective-permute-start | bytes 98312 | tf_op jit(solution)/shard_map/ppermute | solution.py:37
  20.8 12.1 %collective-permute-start.20 = (bf16[1,1,1,1,1,16,512]{6,5,4,3,2,1,0:T(8,128)(2,1)S(1)}, bf16[1,1,1,1,1,16,512]{6,5,4,3,2,1,0:T(8,128)(2,1)S(1)}, u32[]{:S(2)}, u32[]{:S(2)}) collective-permute-start(bf16[1,1,1,1,1,16,512]{6,5,4,3,2,1,0:T(8,128)(2,1)S(1)} %constant_dynamic-slice_fusion.17), channel_id=1, source_target_pairs={{0,256},{16,272},{32,288},{48,304},{64,320},{80,336},{96,352},{112... | collective-permute-start | bytes 49160 | tf_op jit(solution)/shard_map/ppermute | solution.py:37
  41.6 6.1 %collective-permute-start.15 = (bf16[2,1,1,1,1,32,256]{6,5,4,3,2,1,0:T(8,128)(2,1)S(1)}, bf16[2,1,1,1,1,32,256]{6,5,4,3,2,1,0:T(8,128)(2,1)S(1)}, u32[]{:S(2)}, u32[]{:S(2)}) collective-permute-start(bf16[2,1,1,1,1,32,256]{6,5,4,3,2,1,0:T(8,128)(2,1)S(1)} %constant_dynamic-slice_fusion.19), channel_id=1, source_target_pairs={{0,192},{16,208},{32,224},{48,240},{64,128},{80,144},{96,160},{112... | collective-permute-start | bytes 98312 | tf_op jit(solution)/shard_map/ppermute | solution.py:37
  49.7 5.2 %collective-permute-start.22 = (bf16[2,1,1,1,1,16,512]{6,5,4,3,2,1,0:T(8,128)(2,1)S(1)}, bf16[2,1,1,1,1,16,512]{6,5,4,3,2,1,0:T(8,128)(2,1)S(1)}, u32[]{:S(2)}, u32[]{:S(2)}) collective-permute-start(bf16[2,1,1,1,1,16,512]{6,5,4,3,2,1,0:T(8,128)(2,1)S(1)} %constant_dynamic-slice_fusion.16), channel_id=1, source_target_pairs={{0,128},{16,144},{32,160},{48,176},{64,192},{80,208},{96,224},{112... | collective-permute-start | bytes 98312 | tf_op jit(solution)/shard_map/ppermute | solution.py:37
  55.0 6.1 %collective-permute-start.23 = (bf16[2,1,1,1,1,16,512]{6,5,4,3,2,1,0:T(8,128)(2,1)S(1)}, bf16[2,1,1,1,1,16,512]{6,5,4,3,2,1,0:T(8,128)(2,1)S(1)}, u32[]{:S(2)}, u32[]{:S(2)}) collective-permute-start(bf16[2,1,1,1,1,16,512]{6,5,4,3,2,1,0:T(8,128)(2,1)S(1)} %constant_dynamic-slice_fusion.16), channel_id=1, source_target_pairs={{0,192},{16,208},{32,224},{48,240},{64,128},{80,144},{96,160},{112... | collective-permute-start | bytes 98312 | tf_op jit(solution)/shard_map/ppermute | solution.py:37
  63.0 5.2 %collective-permute-start.2 = (bf16[2,1,1,1,1,32,512]{6,5,4,3,2,1,0:T(8,128)(2,1)S(1)}, bf16[2,1,1,1,1,32,512]{6,5,4,3,2,1,0:T(8,128)(2,1)S(1)}, u32[]{:S(2)}, u32[]{:S(2)}) collective-permute-start(bf16[2,1,1,1,1,32,512]{6,5,4,3,2,1,0:T(8,128)(2,1)S(1)} %constant_dynamic-slice_fusion.22), channel_id=1, source_target_pairs={{0,128},{16,144},{32,160},{48,176},{64,192},{80,208},{96,224},{112... | collective-permute-start | bytes 196616 | tf_op jit(solution)/shard_map/ppermute | solution.py:37
  68.3 6.1 %collective-permute-start.3 = (bf16[2,1,1,1,1,32,512]{6,5,4,3,2,1,0:T(8,128)(2,1)S(1)}, bf16[2,1,1,1,1,32,512]{6,5,4,3,2,1,0:T(8,128)(2,1)S(1)}, u32[]{:S(2)}, u32[]{:S(2)}) collective-permute-start(bf16[2,1,1,1,1,32,512]{6,5,4,3,2,1,0:T(8,128)(2,1)S(1)} %constant_dynamic-slice_fusion.22), channel_id=1, source_target_pairs={{0,192},{16,208},{32,224},{48,240},{64,128},{80,144},{96,160},{112... | collective-permute-start | bytes 196616 | tf_op jit(solution)/shard_map/ppermute | solution.py:37
  100.0 8.5 %collective-permute-start.19 = (bf16[1024,256]{1,0:T(8,128)(2,1)S(1)}, bf16[1024,256]{1,0:T(8,128)(2,1)S(1)}, u32[]{:S(2)}, u32[]{:S(2)}) collective-permute-start(bf16[1024,256]{1,0:T(8,128)(2,1)S(1)} %bitcast.119), channel_id=1, source_target_pairs={{0,1},{1,0},{2,3},{3,2},{4,5},{5,4},{6,7},{7,6},{8,9},{9,8},{10,11... | collective-permute-start | bytes 1572872 | tf_op jit(solution)/shard_map/ppermute | solution.py:37
  110.6 4.2 collective-permute-start.7
  126.6 4.3 collective-permute-done.8
  133.5 4.8 %collective-permute-start.10 = (bf16[1,20,6,1024]{3,2,1,0:T(8,128)(2,1)S(1)}, bf16[1,20,6,1024]{3,2,1,0:T(8,128)(2,1)}, u32[]{:S(2)}, u32[]{:S(2)}) collective-permute-start(bf16[1,20,6,1024]{3,2,1,0:T(8,128)(2,1)S(1)} %get-tuple-element.23), channel_id=1, source_target_pairs={{0,1},{1,2},{2,3},{3,4},{4,5},{5,6},{6,7},{7,8},{8,9},{9,10},{10,1... | collective-permute-start | bytes 737288 | tf_op jit(solution)/shard_map/ppermute | solution.py:27
  157.2 4.3 fusion.12
  181.5 6.2 %collective-permute-start.28 = (f32[1,20,6,1024]{3,0,2,1:T(1,128)S(1)}, f32[1,20,6,1024]{3,0,2,1:T(1,128)S(1)}, u32[]{:S(2)}, u32[]{:S(2)}) collective-permute-start(f32[1,20,6,1024]{3,0,2,1:T(1,128)S(1)} %get-tuple-element.8), channel_id=1, source_target_pairs={{0,1},{1,2},{2,3},{3,4},{4,5},{5,6},{6,7},{7,8},{8,9},{9,10},{10,1... | collective-permute-start | bytes 1474568 | tf_op jit(solution)/shard_map/ppermute | solution.py:19
  187.7 4.3 collective-permute-done.29
  192.1 8.8 %collective-permute-done.28 = f32[1,20,6,1024]{3,0,2,1:T(1,128)S(1)} collective-permute-done((f32[1,20,6,1024]{3,0,2,1:T(1,128)S(1)}, f32[1,20,6,1024]{3,0,2,1:T(1,128)S(1)}, u32[]{:S(2)}, u32[]{:S(2)}) %collective-permute-start.28) | collective-permute-done | bytes 491552 | tf_op jit(solution)/shard_map/ppermute | solution.py:19
  206.2 4.7 %collective-permute-start.30 = (f32[1,6,16,1024]{3,0,2,1:T(1,128)}, f32[1,6,16,1024]{3,0,2,1:T(1,128)}, u32[]{:S(2)}, u32[]{:S(2)}) collective-permute-start(f32[1,6,16,1024]{3,0,2,1:T(1,128)} %get-tuple-element.15), channel_id=1, source_target_pairs={{0,16},{16,32},{32,48},{48,64},{64,80},{80,96},{96,112},{112,128},... | collective-permute-start | bytes 1179656 | tf_op jit(solution)/shard_map/ppermute | solution.py:19
  227.0 9.3 %collective-permute-start.34 = (f32[2,1,2,1,1,32,32,64]{7,6,5,3,2,1,0,4:T(8,128)}, f32[2,1,2,1,1,32,32,64]{7,6,5,3,2,1,0,4:T(8,128)}, u32[]{:S(2)}, u32[]{:S(2)}) collective-permute-start(f32[2,1,2,1,1,32,32,64]{7,6,5,3,2,1,0,4:T(8,128)} %get-tuple-element.6), channel_id=1, source_target_pairs={{0,5},{1,4},{2,7},{3,6},{4,1},{5,0},{6,3},{7,2},{8,13},{9,12},{10,... | collective-permute-start | bytes 3145736 | tf_op jit(solution)/shard_map/ppermute | solution.py:37
  243.4 4.6 %fusion.22 = bf16[8,64,128]{2,1,0:T(8,128)(2,1)S(1)} fusion(bf16[560,8,64]{0,2,1:T(8,128)(2,1)S(1)} %bitcast.135, f32[8,128,560]{1,2,0:T(8,128)} %copy-done.2, f32[8,128,560]{1,2,0:T(8,128)} %get-tuple-element.34, f32[8,128]{1,0:T(8,128)S(1)} %get-tuple-element.33), kind=kOutput, calls=%fused_computation.24 | convolution fusion | flops 77481520 | bytes 5296128 | tf_op jit(solution)/shard_map/bhqk,bkhd->bqhd/dot_general | solution.py:168
  248.0 34.7 %collective-permute-done.34 = f32[2,1,2,1,1,32,32,64]{7,6,5,3,2,1,0,4:T(8,128)} collective-permute-done((f32[2,1,2,1,1,32,32,64]{7,6,5,3,2,1,0,4:T(8,128)}, f32[2,1,2,1,1,32,32,64]{7,6,5,3,2,1,0,4:T(8,128)}, u32[]{:S(2)}, u32[]{:S(2)}) %collective-permute-start.34) | collective-permute-done | bytes 1048608 | tf_op jit(solution)/shard_map/ppermute | solution.py:37
  282.7 44.3 %collective-permute-done.33 = f32[2,1,2,1,1,32,32,64]{7,6,5,3,2,1,0,4:T(8,128)} collective-permute-done((f32[2,1,2,1,1,32,32,64]{7,6,5,3,2,1,0,4:T(8,128)}, f32[2,1,2,1,1,32,32,64]{7,6,5,3,2,1,0,4:T(8,128)}, u32[]{:S(2)}, u32[]{:S(2)}) %collective-permute-start.33) | collective-permute-done | bytes 1048608 | tf_op jit(solution)/shard_map/ppermute | solution.py:37
  327.0 4.5 %add_add_fusion = f32[2,1,2,1,1,32,32,64]{7,6,5,3,2,1,0,4:T(8,128)S(1)} fusion(f32[2,1,2,1,1,32,32,64]{7,6,5,3,2,1,0,4:T(8,128)} %collective-permute-done.34, f32[2,1,2,1,1,32,32,64]{7,6,5,3,2,1,0,4:T(8,128)} %collective-permute-done.33, f32[2,1,2,1,1,32,32,64]{7,6,5,3,2,1,0,4:T(8,128)} %collective-permute-done.32, ...), kind=kLoop, calls=%fused_computation.8 | loop fusion | flops 786432 | bytes 5242888 | tf_op jit(solution)/shard_map/add | solution.py:91
  334.9 4.2 collective-permute-start.36
  339.1 4.6 %collective-permute-start.35 = (f32[1,1,1,1,1,32,32,64]{7,6,5,3,2,1,0,4:T(8,128)S(1)}, f32[1,1,1,1,1,32,32,64]{7,6,5,3,2,1,0,4:T(8,128)S(1)}, u32[]{:S(2)}, u32[]{:S(2)}) collective-permute-start(f32[1,1,1,1,1,32,32,64]{7,6,5,3,2,1,0,4:T(8,128)S(1)} %get-tuple-element.10), channel_id=1, source_target_pairs={{0,2},{1,3},{2,0},{3,1},{4,6},{5,7},{6,4},{7,5},{8,10},{9,11},{10,... | collective-permute-start | bytes 786440 | tf_op jit(solution)/shard_map/ppermute | solution.py:37
  345.3 4.9 %collective-permute-done.37 = f32[1,1,1,1,1,32,32,64]{7,6,5,3,2,1,0,4:T(8,128)S(1)} collective-permute-done((f32[1,1,1,1,1,32,32,64]{7,6,5,3,2,1,0,4:T(8,128)S(1)}, f32[1,1,1,1,1,32,32,64]{7,6,5,3,2,1,0,4:T(8,128)S(1)}, u32[]{:S(2)}, u32[]{:S(2)}) %collective-permute-start.37) | collective-permute-done | bytes 262176 | tf_op jit(solution)/shard_map/ppermute | solution.py:37
  350.2 9.8 %collective-permute-done.36 = f32[1,1,1,1,1,32,32,64]{7,6,5,3,2,1,0,4:T(8,128)S(1)} collective-permute-done((f32[1,1,1,1,1,32,32,64]{7,6,5,3,2,1,0,4:T(8,128)S(1)}, f32[1,1,1,1,1,32,32,64]{7,6,5,3,2,1,0,4:T(8,128)S(1)}, u32[]{:S(2)}, u32[]{:S(2)}) %collective-permute-start.36) | collective-permute-done | bytes 262176 | tf_op jit(solution)/shard_map/ppermute | solution.py:37
  363.0 4.4 %collective-permute-start.40 = (f32[2,2,2,1,1,1,32,64]{7,6,4,3,2,1,0,5:T(8,128)S(1)}, f32[2,2,2,1,1,1,32,64]{7,6,4,3,2,1,0,5:T(8,128)S(1)}, u32[]{:S(2)}, u32[]{:S(2)}) collective-permute-start(f32[2,2,2,1,1,1,32,64]{7,6,4,3,2,1,0,5:T(8,128)S(1)} %get-tuple-element.26), channel_id=1, source_target_pairs={{0,48},{16,32},{32,16},{48,0},{64,112},{80,96},{96,80},{112,64},{1... | collective-permute-start | bytes 196616 | tf_op jit(solution)/shard_map/ppermute | solution.py:37
  375.9 6.9 %collective-permute-start.43 = (f32[2,1,1,1,1,1,32,64]{7,6,4,3,2,1,0,5:T(8,128)S(1)}, f32[2,1,1,1,1,1,32,64]{7,6,4,3,2,1,0,5:T(8,128)S(1)}, u32[]{:S(2)}, u32[]{:S(2)}) collective-permute-start(f32[2,1,1,1,1,1,32,64]{7,6,4,3,2,1,0,5:T(8,128)S(1)} %get-tuple-element.31), channel_id=1, source_target_pairs={{0,192},{16,208},{32,224},{48,240},{64,128},{80,144},{96,160},{112... | collective-permute-start | bytes 49160 | tf_op jit(solution)/shard_map/ppermute | solution.py:37
  384.7 4.3 collective-permute-start.41
  391.6 4.7 %collective-permute-start.44 = (f32[1,1,1,1,1,1,32,64]{7,6,4,3,2,1,0,5:T(8,128)S(1)}, f32[1,1,1,1,1,1,32,64]{7,6,4,3,2,1,0,5:T(8,128)S(1)}, u32[]{:S(2)}, u32[]{:S(2)}) collective-permute-start(f32[1,1,1,1,1,1,32,64]{7,6,4,3,2,1,0,5:T(8,128)S(1)} %constant_dynamic-slice_fusion.2), channel_id=1, source_target_pairs={{0,256},{16,272},{32,288},{48,304},{64,320},{80,336},{96,352},{112... | collective-permute-start | bytes 24584 | tf_op jit(solution)/shard_map/ppermute | solution.py:37
  396.4 8.5 %collective-permute-done.44 = f32[1,1,1,1,1,1,32,64]{7,6,4,3,2,1,0,5:T(8,128)S(1)} collective-permute-done((f32[1,1,1,1,1,1,32,64]{7,6,4,3,2,1,0,5:T(8,128)S(1)}, f32[1,1,1,1,1,1,32,64]{7,6,4,3,2,1,0,5:T(8,128)S(1)}, u32[]{:S(2)}, u32[]{:S(2)}) %collective-permute-start.44) | collective-permute-done | bytes 8224 | tf_op jit(solution)/shard_map/ppermute | solution.py:37
  412.4 4.6 %collective-permute-start.47 = (f32[1,1,1,1,32,64]{5,3,2,1,0,4:T(1,128)S(1)}, f32[1,1,1,1,32,64]{5,3,2,1,0,4:T(1,128)S(1)}, u32[]{:S(2)}, u32[]{:S(2)}) collective-permute-start(f32[1,1,1,1,32,64]{5,3,2,1,0,4:T(1,128)S(1)} %constant_dynamic-slice_fusion.1), channel_id=1, source_target_pairs={{0,10},{1,11},{2,8},{3,9},{4,14},{5,15},{6,12},{7,13},{8,2},{9,3},... | collective-permute-start | bytes 24584 | tf_op jit(solution)/shard_map/ppermute | solution.py:37
  421.0 8.4 %collective-permute-start.48 = (f32[2,1,2,1,32,64]{5,3,2,1,0,4:T(1,128)S(1)}, f32[2,1,2,1,32,64]{5,3,2,1,0,4:T(1,128)S(1)}, u32[]{:S(2)}, u32[]{:S(2)}) collective-permute-start(f32[2,1,2,1,32,64]{5,3,2,1,0,4:T(1,128)S(1)} %constant_dynamic-slice_fusion), channel_id=1, source_target_pairs={{0,1},{1,0},{2,3},{3,2},{4,5},{5,4},{6,7},{7,6},{8,9},{9,8},{10,11... | collective-permute-start | bytes 98312 | tf_op jit(solution)/shard_map/ppermute | solution.py:37
  (235 shorter events, 168.5 us)
Async XLA Ops:
  1.7 48.0 %collective-permute-start = (bf16[1,1,1,1,1,32,512]{6,5,4,3,2,1,0:T(8,128)(2,1)S(1)}, bf16[1,1,1,1,1,32,512]{6,5,4,3,2,1,0:T(8,128)(2,1)S(1)}, u32[]{:S(2)}, u32[]{:S(2)}) collective-permute-start(bf16[1,1,1,1,1,32,512]{6,5,4,3,2,1,0:T(8,128)(2,1)S(1)} %constant_dynamic-slice_fusion.23), channel_id=1, source_target_pairs={{0,256},{16,272},{32,288},{48,304},{64,320},{80,336},{96,352},{112... | collective-permute-start | bytes 98312 | tf_op jit(solution)/shard_map/ppermute | solution.py:37
  18.8 15.7 %collective-permute-start.12 = (bf16[1,1,1,1,1,32,256]{6,5,4,3,2,1,0:T(8,128)(2,1)S(1)}, bf16[1,1,1,1,1,32,256]{6,5,4,3,2,1,0:T(8,128)(2,1)S(1)}, u32[]{:S(2)}, u32[]{:S(2)}) collective-permute-start(bf16[1,1,1,1,1,32,256]{6,5,4,3,2,1,0:T(8,128)(2,1)S(1)} %constant_dynamic-slice_fusion.20), channel_id=1, source_target_pairs={{0,256},{16,272},{32,288},{48,304},{64,320},{80,336},{96,352},{112... | collective-permute-start | bytes 49160 | tf_op jit(solution)/shard_map/ppermute | solution.py:37
  20.8 26.9 %collective-permute-start.20 = (bf16[1,1,1,1,1,16,512]{6,5,4,3,2,1,0:T(8,128)(2,1)S(1)}, bf16[1,1,1,1,1,16,512]{6,5,4,3,2,1,0:T(8,128)(2,1)S(1)}, u32[]{:S(2)}, u32[]{:S(2)}) collective-permute-start(bf16[1,1,1,1,1,16,512]{6,5,4,3,2,1,0:T(8,128)(2,1)S(1)} %constant_dynamic-slice_fusion.17), channel_id=1, source_target_pairs={{0,256},{16,272},{32,288},{48,304},{64,320},{80,336},{96,352},{112... | collective-permute-start | bytes 49160 | tf_op jit(solution)/shard_map/ppermute | solution.py:37
  34.5 20.5 %collective-permute-start.13 = (bf16[2,1,1,1,1,32,256]{6,5,4,3,2,1,0:T(8,128)(2,1)S(1)}, bf16[2,1,1,1,1,32,256]{6,5,4,3,2,1,0:T(8,128)(2,1)S(1)}, u32[]{:S(2)}, u32[]{:S(2)}) collective-permute-start(bf16[2,1,1,1,1,32,256]{6,5,4,3,2,1,0:T(8,128)(2,1)S(1)} %constant_dynamic-slice_fusion.19), channel_id=1, source_target_pairs={{0,64},{16,80},{32,96},{48,112},{64,0},{80,16},{96,32},{112,48},{1... | collective-permute-start | bytes 98312 | tf_op jit(solution)/shard_map/ppermute | solution.py:37
  37.6 23.5 %collective-permute-start.14 = (bf16[2,1,1,1,1,32,256]{6,5,4,3,2,1,0:T(8,128)(2,1)S(1)}, bf16[2,1,1,1,1,32,256]{6,5,4,3,2,1,0:T(8,128)(2,1)S(1)}, u32[]{:S(2)}, u32[]{:S(2)}) collective-permute-start(bf16[2,1,1,1,1,32,256]{6,5,4,3,2,1,0:T(8,128)(2,1)S(1)} %constant_dynamic-slice_fusion.19), channel_id=1, source_target_pairs={{0,128},{16,144},{32,160},{48,176},{64,192},{80,208},{96,224},{112... | collective-permute-start | bytes 98312 | tf_op jit(solution)/shard_map/ppermute | solution.py:37
  41.6 21.4 %collective-permute-start.15 = (bf16[2,1,1,1,1,32,256]{6,5,4,3,2,1,0:T(8,128)(2,1)S(1)}, bf16[2,1,1,1,1,32,256]{6,5,4,3,2,1,0:T(8,128)(2,1)S(1)}, u32[]{:S(2)}, u32[]{:S(2)}) collective-permute-start(bf16[2,1,1,1,1,32,256]{6,5,4,3,2,1,0:T(8,128)(2,1)S(1)} %constant_dynamic-slice_fusion.19), channel_id=1, source_target_pairs={{0,192},{16,208},{32,224},{48,240},{64,128},{80,144},{96,160},{112... | collective-permute-start | bytes 98312 | tf_op jit(solution)/shard_map/ppermute | solution.py:37
  47.8 20.5 %collective-permute-start.21 = (bf16[2,1,1,1,1,16,512]{6,5,4,3,2,1,0:T(8,128)(2,1)S(1)}, bf16[2,1,1,1,1,16,512]{6,5,4,3,2,1,0:T(8,128)(2,1)S(1)}, u32[]{:S(2)}, u32[]{:S(2)}) collective-permute-start(bf16[2,1,1,1,1,16,512]{6,5,4,3,2,1,0:T(8,128)(2,1)S(1)} %constant_dynamic-slice_fusion.16), channel_id=1, source_target_pairs={{0,64},{16,80},{32,96},{48,112},{64,0},{80,16},{96,32},{112,48},{1... | collective-permute-start | bytes 98312 | tf_op jit(solution)/shard_map/ppermute | solution.py:37
  49.7 24.7 %collective-permute-start.22 = (bf16[2,1,1,1,1,16,512]{6,5,4,3,2,1,0:T(8,128)(2,1)S(1)}, bf16[2,1,1,1,1,16,512]{6,5,4,3,2,1,0:T(8,128)(2,1)S(1)}, u32[]{:S(2)}, u32[]{:S(2)}) collective-permute-start(bf16[2,1,1,1,1,16,512]{6,5,4,3,2,1,0:T(8,128)(2,1)S(1)} %constant_dynamic-slice_fusion.16), channel_id=1, source_target_pairs={{0,128},{16,144},{32,160},{48,176},{64,192},{80,208},{96,224},{112... | collective-permute-start | bytes 98312 | tf_op jit(solution)/shard_map/ppermute | solution.py:37
  55.0 22.7 %collective-permute-start.23 = (bf16[2,1,1,1,1,16,512]{6,5,4,3,2,1,0:T(8,128)(2,1)S(1)}, bf16[2,1,1,1,1,16,512]{6,5,4,3,2,1,0:T(8,128)(2,1)S(1)}, u32[]{:S(2)}, u32[]{:S(2)}) collective-permute-start(bf16[2,1,1,1,1,16,512]{6,5,4,3,2,1,0:T(8,128)(2,1)S(1)} %constant_dynamic-slice_fusion.16), channel_id=1, source_target_pairs={{0,192},{16,208},{32,224},{48,240},{64,128},{80,144},{96,160},{112... | collective-permute-start | bytes 98312 | tf_op jit(solution)/shard_map/ppermute | solution.py:37
  61.1 19.3 %collective-permute-start.1 = (bf16[2,1,1,1,1,32,512]{6,5,4,3,2,1,0:T(8,128)(2,1)S(1)}, bf16[2,1,1,1,1,32,512]{6,5,4,3,2,1,0:T(8,128)(2,1)S(1)}, u32[]{:S(2)}, u32[]{:S(2)}) collective-permute-start(bf16[2,1,1,1,1,32,512]{6,5,4,3,2,1,0:T(8,128)(2,1)S(1)} %constant_dynamic-slice_fusion.22), channel_id=1, source_target_pairs={{0,64},{16,80},{32,96},{48,112},{64,0},{80,16},{96,32},{112,48},{1... | collective-permute-start | bytes 196616 | tf_op jit(solution)/shard_map/ppermute | solution.py:37
  63.0 19.9 %collective-permute-start.2 = (bf16[2,1,1,1,1,32,512]{6,5,4,3,2,1,0:T(8,128)(2,1)S(1)}, bf16[2,1,1,1,1,32,512]{6,5,4,3,2,1,0:T(8,128)(2,1)S(1)}, u32[]{:S(2)}, u32[]{:S(2)}) collective-permute-start(bf16[2,1,1,1,1,32,512]{6,5,4,3,2,1,0:T(8,128)(2,1)S(1)} %constant_dynamic-slice_fusion.22), channel_id=1, source_target_pairs={{0,128},{16,144},{32,160},{48,176},{64,192},{80,208},{96,224},{112... | collective-permute-start | bytes 196616 | tf_op jit(solution)/shard_map/ppermute | solution.py:37
  68.3 17.9 %collective-permute-start.3 = (bf16[2,1,1,1,1,32,512]{6,5,4,3,2,1,0:T(8,128)(2,1)S(1)}, bf16[2,1,1,1,1,32,512]{6,5,4,3,2,1,0:T(8,128)(2,1)S(1)}, u32[]{:S(2)}, u32[]{:S(2)}) collective-permute-start(bf16[2,1,1,1,1,32,512]{6,5,4,3,2,1,0:T(8,128)(2,1)S(1)} %constant_dynamic-slice_fusion.22), channel_id=1, source_target_pairs={{0,192},{16,208},{32,224},{48,240},{64,128},{80,144},{96,160},{112... | collective-permute-start | bytes 196616 | tf_op jit(solution)/shard_map/ppermute | solution.py:37
  74.4 14.5 %collective-permute-start.16 = (bf16[2,2,2,1,1,32,256]{6,5,4,3,2,1,0:T(8,128)(2,1)S(1)}, bf16[2,2,2,1,1,32,256]{6,5,4,3,2,1,0:T(8,128)(2,1)S(1)}, u32[]{:S(2)}, u32[]{:S(2)}) collective-permute-start(bf16[2,2,2,1,1,32,256]{6,5,4,3,2,1,0:T(8,128)(2,1)S(1)} %constant_dynamic-slice_fusion.18), channel_id=1, source_target_pairs={{0,16},{16,0},{32,48},{48,32},{64,80},{80,64},{96,112},{112,96},{1... | collective-permute-start | bytes 393224 | tf_op jit(solution)/shard_map/ppermute | solution.py:37
  77.7 17.1 %collective-permute-start.17 = (bf16[2,2,2,1,1,32,256]{6,5,4,3,2,1,0:T(8,128)(2,1)S(1)}, bf16[2,2,2,1,1,32,256]{6,5,4,3,2,1,0:T(8,128)(2,1)S(1)}, u32[]{:S(2)}, u32[]{:S(2)}) collective-permute-start(bf16[2,2,2,1,1,32,256]{6,5,4,3,2,1,0:T(8,128)(2,1)S(1)} %constant_dynamic-slice_fusion.18), channel_id=1, source_target_pairs={{0,32},{16,48},{32,0},{48,16},{64,96},{80,112},{96,64},{112,80},{1... | collective-permute-start | bytes 393224 | tf_op jit(solution)/shard_map/ppermute | solution.py:37
  80.4 17.0 %collective-permute-start.18 = (bf16[2,2,2,1,1,32,256]{6,5,4,3,2,1,0:T(8,128)(2,1)S(1)}, bf16[2,2,2,1,1,32,256]{6,5,4,3,2,1,0:T(8,128)(2,1)S(1)}, u32[]{:S(2)}, u32[]{:S(2)}) collective-permute-start(bf16[2,2,2,1,1,32,256]{6,5,4,3,2,1,0:T(8,128)(2,1)S(1)} %constant_dynamic-slice_fusion.18), channel_id=1, source_target_pairs={{0,48},{16,32},{32,16},{48,0},{64,112},{80,96},{96,80},{112,64},{1... | collective-permute-start | bytes 393224 | tf_op jit(solution)/shard_map/ppermute | solution.py:37
  86.2 13.8 %collective-permute-start.25 = (bf16[2,2,2,1,1,16,512]{6,5,4,3,2,1,0:T(8,128)(2,1)S(1)}, bf16[2,2,2,1,1,16,512]{6,5,4,3,2,1,0:T(8,128)(2,1)S(1)}, u32[]{:S(2)}, u32[]{:S(2)}) collective-permute-start(bf16[2,2,2,1,1,16,512]{6,5,4,3,2,1,0:T(8,128)(2,1)S(1)} %constant_dynamic-slice_fusion.15), channel_id=1, source_target_pairs={{0,32},{16,48},{32,0},{48,16},{64,96},{80,112},{96,64},{112,80},{1... | collective-permute-start | bytes 393224 | tf_op jit(solution)/shard_map/ppermute | solution.py:37
  88.9 19.6 %collective-permute-start.26 = (bf16[2,2,2,1,1,16,512]{6,5,4,3,2,1,0:T(8,128)(2,1)S(1)}, bf16[2,2,2,1,1,16,512]{6,5,4,3,2,1,0:T(8,128)(2,1)S(1)}, u32[]{:S(2)}, u32[]{:S(2)}) collective-permute-start(bf16[2,2,2,1,1,16,512]{6,5,4,3,2,1,0:T(8,128)(2,1)S(1)} %constant_dynamic-slice_fusion.15), channel_id=1, source_target_pairs={{0,48},{16,32},{32,16},{48,0},{64,112},{80,96},{96,80},{112,64},{1... | collective-permute-start | bytes 393224 | tf_op jit(solution)/shard_map/ppermute | solution.py:37
  91.5 19.0 %collective-permute-start.4 = (bf16[2,2,2,1,1,32,512]{6,5,4,3,2,1,0:T(8,128)(2,1)S(1)}, bf16[2,2,2,1,1,32,512]{6,5,4,3,2,1,0:T(8,128)(2,1)S(1)}, u32[]{:S(2)}, u32[]{:S(2)}) collective-permute-start(bf16[2,2,2,1,1,32,512]{6,5,4,3,2,1,0:T(8,128)(2,1)S(1)} %constant_dynamic-slice_fusion.21), channel_id=1, source_target_pairs={{0,16},{16,0},{32,48},{48,32},{64,80},{80,64},{96,112},{112,96},{1... | collective-permute-start | bytes 786440 | tf_op jit(solution)/shard_map/ppermute | solution.py:37
  94.7 15.8 %collective-permute-start.5 = (bf16[2,2,2,1,1,32,512]{6,5,4,3,2,1,0:T(8,128)(2,1)S(1)}, bf16[2,2,2,1,1,32,512]{6,5,4,3,2,1,0:T(8,128)(2,1)S(1)}, u32[]{:S(2)}, u32[]{:S(2)}) collective-permute-start(bf16[2,2,2,1,1,32,512]{6,5,4,3,2,1,0:T(8,128)(2,1)S(1)} %constant_dynamic-slice_fusion.21), channel_id=1, source_target_pairs={{0,32},{16,48},{32,0},{48,16},{64,96},{80,112},{96,64},{112,80},{1... | collective-permute-start | bytes 786440 | tf_op jit(solution)/shard_map/ppermute | solution.py:37
  97.4 13.1 %collective-permute-start.6 = (bf16[2,2,2,1,1,32,512]{6,5,4,3,2,1,0:T(8,128)(2,1)S(1)}, bf16[2,2,2,1,1,32,512]{6,5,4,3,2,1,0:T(8,128)(2,1)S(1)}, u32[]{:S(2)}, u32[]{:S(2)}) collective-permute-start(bf16[2,2,2,1,1,32,512]{6,5,4,3,2,1,0:T(8,128)(2,1)S(1)} %constant_dynamic-slice_fusion.21), channel_id=1, source_target_pairs={{0,48},{16,32},{32,16},{48,0},{64,112},{80,96},{96,80},{112,64},{1... | collective-permute-start | bytes 786440 | tf_op jit(solution)/shard_map/ppermute | solution.py:37
  100.0 15.3 %collective-permute-start.19 = (bf16[1024,256]{1,0:T(8,128)(2,1)S(1)}, bf16[1024,256]{1,0:T(8,128)(2,1)S(1)}, u32[]{:S(2)}, u32[]{:S(2)}) collective-permute-start(bf16[1024,256]{1,0:T(8,128)(2,1)S(1)} %bitcast.119), channel_id=1, source_target_pairs={{0,1},{1,0},{2,3},{3,2},{4,5},{5,4},{6,7},{7,6},{8,9},{9,8},{10,11... | collective-permute-start | bytes 1572872 | tf_op jit(solution)/shard_map/ppermute | solution.py:37
  179.6 12.5 %collective-permute-start.29 = (f32[1,20,6,1024]{3,0,2,1:T(1,128)S(1)}, f32[1,20,6,1024]{3,0,2,1:T(1,128)S(1)}, u32[]{:S(2)}, u32[]{:S(2)}) collective-permute-start(f32[1,20,6,1024]{3,0,2,1:T(1,128)S(1)} %get-tuple-element.9), channel_id=1, source_target_pairs={{1,0},{2,1},{3,2},{4,3},{5,4},{6,5},{7,6},{8,7},{9,8},{10,9},{11,1... | collective-permute-start | bytes 1474568 | tf_op jit(solution)/shard_map/ppermute | solution.py:19
  181.5 19.4 %collective-permute-start.28 = (f32[1,20,6,1024]{3,0,2,1:T(1,128)S(1)}, f32[1,20,6,1024]{3,0,2,1:T(1,128)S(1)}, u32[]{:S(2)}, u32[]{:S(2)}) collective-permute-start(f32[1,20,6,1024]{3,0,2,1:T(1,128)S(1)} %get-tuple-element.8), channel_id=1, source_target_pairs={{0,1},{1,2},{2,3},{3,4},{4,5},{5,6},{6,7},{7,8},{8,9},{9,10},{10,1... | collective-permute-start | bytes 1474568 | tf_op jit(solution)/shard_map/ppermute | solution.py:19
  227.0 55.7 %collective-permute-start.34 = (f32[2,1,2,1,1,32,32,64]{7,6,5,3,2,1,0,4:T(8,128)}, f32[2,1,2,1,1,32,32,64]{7,6,5,3,2,1,0,4:T(8,128)}, u32[]{:S(2)}, u32[]{:S(2)}) collective-permute-start(f32[2,1,2,1,1,32,32,64]{7,6,5,3,2,1,0,4:T(8,128)} %get-tuple-element.6), channel_id=1, source_target_pairs={{0,5},{1,4},{2,7},{3,6},{4,1},{5,0},{6,3},{7,2},{8,13},{9,12},{10,... | collective-permute-start | bytes 3145736 | tf_op jit(solution)/shard_map/ppermute | solution.py:37
  236.3 90.7 %collective-permute-start.33 = (f32[2,1,2,1,1,32,32,64]{7,6,5,3,2,1,0,4:T(8,128)}, f32[2,1,2,1,1,32,32,64]{7,6,5,3,2,1,0,4:T(8,128)}, u32[]{:S(2)}, u32[]{:S(2)}) collective-permute-start(f32[2,1,2,1,1,32,32,64]{7,6,5,3,2,1,0,4:T(8,128)} %get-tuple-element.7), channel_id=1, source_target_pairs={{0,4},{1,5},{2,6},{3,7},{4,0},{5,1},{6,2},{7,3},{8,12},{9,13},{10,... | collective-permute-start | bytes 3145736 | tf_op jit(solution)/shard_map/ppermute | solution.py:37
  238.2 88.8 %collective-permute-start.32 = (f32[2,1,2,1,1,32,32,64]{7,6,5,3,2,1,0,4:T(8,128)}, f32[2,1,2,1,1,32,32,64]{7,6,5,3,2,1,0,4:T(8,128)}, u32[]{:S(2)}, u32[]{:S(2)}) collective-permute-start(f32[2,1,2,1,1,32,32,64]{7,6,5,3,2,1,0,4:T(8,128)} %get-tuple-element.5), channel_id=1, source_target_pairs={{0,1},{1,0},{2,3},{3,2},{4,5},{5,4},{6,7},{7,6},{8,9},{9,8},{10,11... | collective-permute-start | bytes 3145736 | tf_op jit(solution)/shard_map/ppermute | solution.py:37
  331.7 18.5 %collective-permute-start.37 = (f32[1,1,1,1,1,32,32,64]{7,6,5,3,2,1,0,4:T(8,128)S(1)}, f32[1,1,1,1,1,32,32,64]{7,6,5,3,2,1,0,4:T(8,128)S(1)}, u32[]{:S(2)}, u32[]{:S(2)}) collective-permute-start(f32[1,1,1,1,1,32,32,64]{7,6,5,3,2,1,0,4:T(8,128)S(1)} %get-tuple-element.11), channel_id=1, source_target_pairs={{0,10},{1,11},{2,8},{3,9},{4,14},{5,15},{6,12},{7,13},{8,2},{9,3},... | collective-permute-start | bytes 786440 | tf_op jit(solution)/shard_map/ppermute | solution.py:37
  334.9 25.1 %collective-permute-start.36 = (f32[1,1,1,1,1,32,32,64]{7,6,5,3,2,1,0,4:T(8,128)S(1)}, f32[1,1,1,1,1,32,32,64]{7,6,5,3,2,1,0,4:T(8,128)S(1)}, u32[]{:S(2)}, u32[]{:S(2)}) collective-permute-start(f32[1,1,1,1,1,32,32,64]{7,6,5,3,2,1,0,4:T(8,128)S(1)} %get-tuple-element.12), channel_id=1, source_target_pairs={{0,8},{1,9},{2,10},{3,11},{4,12},{5,13},{6,14},{7,15},{8,0},{9,1},... | collective-permute-start | bytes 786440 | tf_op jit(solution)/shard_map/ppermute | solution.py:37
  339.1 23.6 %collective-permute-start.35 = (f32[1,1,1,1,1,32,32,64]{7,6,5,3,2,1,0,4:T(8,128)S(1)}, f32[1,1,1,1,1,32,32,64]{7,6,5,3,2,1,0,4:T(8,128)S(1)}, u32[]{:S(2)}, u32[]{:S(2)}) collective-permute-start(f32[1,1,1,1,1,32,32,64]{7,6,5,3,2,1,0,4:T(8,128)S(1)} %get-tuple-element.10), channel_id=1, source_target_pairs={{0,2},{1,3},{2,0},{3,1},{4,6},{5,7},{6,4},{7,5},{8,10},{9,11},{10,... | collective-permute-start | bytes 786440 | tf_op jit(solution)/shard_map/ppermute | solution.py:37
  375.9 13.5 %collective-permute-start.43 = (f32[2,1,1,1,1,1,32,64]{7,6,4,3,2,1,0,5:T(8,128)S(1)}, f32[2,1,1,1,1,1,32,64]{7,6,4,3,2,1,0,5:T(8,128)S(1)}, u32[]{:S(2)}, u32[]{:S(2)}) collective-permute-start(f32[2,1,1,1,1,1,32,64]{7,6,4,3,2,1,0,5:T(8,128)S(1)} %get-tuple-element.31), channel_id=1, source_target_pairs={{0,192},{16,208},{32,224},{48,240},{64,128},{80,144},{96,160},{112... | collective-permute-start | bytes 49160 | tf_op jit(solution)/shard_map/ppermute | solution.py:37
  391.6 13.2 %collective-permute-start.44 = (f32[1,1,1,1,1,1,32,64]{7,6,4,3,2,1,0,5:T(8,128)S(1)}, f32[1,1,1,1,1,1,32,64]{7,6,4,3,2,1,0,5:T(8,128)S(1)}, u32[]{:S(2)}, u32[]{:S(2)}) collective-permute-start(f32[1,1,1,1,1,1,32,64]{7,6,4,3,2,1,0,5:T(8,128)S(1)} %constant_dynamic-slice_fusion.2), channel_id=1, source_target_pairs={{0,256},{16,272},{32,288},{48,304},{64,320},{80,336},{96,352},{112... | collective-permute-start | bytes 24584 | tf_op jit(solution)/shard_map/ppermute | solution.py:37
  421.0 14.9 %collective-permute-start.48 = (f32[2,1,2,1,32,64]{5,3,2,1,0,4:T(1,128)S(1)}, f32[2,1,2,1,32,64]{5,3,2,1,0,4:T(1,128)S(1)}, u32[]{:S(2)}, u32[]{:S(2)}) collective-permute-start(f32[2,1,2,1,32,64]{5,3,2,1,0,4:T(1,128)S(1)} %constant_dynamic-slice_fusion), channel_id=1, source_target_pairs={{0,1},{1,0},{2,3},{3,2},{4,5},{5,4},{6,7},{7,6},{8,9},{9,8},{10,11... | collective-permute-start | bytes 98312 | tf_op jit(solution)/shard_map/ppermute | solution.py:37
  (41 other events, 567.7 us)

commit v4 on v3

--- a/solution.py
+++ b/solution.py
@@ -93,16 +93,23 @@
     return held.reshape(held.shape[levels:])
 
 
-def gather_weight(shard, row_bits):
-    half = shard.shape[1] // 2
+def gather_weights(w_query, w_keyvalue, w_output, row_groups):
+    rows, width = w_query.shape
+    kv_pack = w_keyvalue.reshape(rows, 2, width).transpose(1, 0, 2).reshape(2 * rows, width)
+    out_rows = w_output.shape[0]
+    out_pack = w_output.reshape(out_rows, 2, width).transpose(1, 0, 2).reshape(2 * out_rows, width)
+    qo_pack = jnp.concatenate([w_query, out_pack], axis=0)
     own = axis_bit("col", 0)
-    piece = lax.dynamic_slice_in_dim(shard, own * half, half, axis=1)
-    rows = gather_by_bits(piece, "row", row_bits)
-    rows = rows.reshape(-1, half)
-    held = jnp.zeros((2,) + rows.shape, rows.dtype)
-    held = lax.dynamic_update_slice(held, rows[None], (own, 0, 0))
-    held = lax.dynamic_update_slice(held, partner_swap(rows, "col", 1)[None], (1 - own, 0, 0))
-    return jnp.concatenate([held[0], held[1]], axis=1)
+    packed = jnp.where(own == 0, kv_pack, qo_pack)
+    fetched = gather_by_bits(packed, "row", row_groups)
+    held = jnp.zeros((2,) + fetched.shape, fetched.dtype)
+    held = lax.dynamic_update_slice(held, fetched[None], (own, 0, 0, 0))
+    held = lax.dynamic_update_slice(held, partner_swap(fetched, "col", 1)[None], (1 - own, 0, 0, 0))
+    count = fetched.shape[0]
+    kv = held[0].reshape(count, 2, rows, width).transpose(0, 2, 1, 3).reshape(count * rows, 2 * width)
+    query = held[1, :, :rows].reshape(count * rows, width)
+    output = held[1, :, rows:].reshape(count, 2, out_rows, width).transpose(0, 2, 1, 3)
+    return query, kv, output.reshape(count * out_rows, 2 * width)
 
 
 def normalize(inputs, norm_gain):
@@ -220,10 +227,10 @@
     standard, spread, normed = normalize(inputs, norm_gain)
     flat_norm = normed.reshape(-1, model_width)
     row_levels = lax.axis_size("row").bit_length() - 1
-    row_groups = [list(range(b, min(b + 2, row_levels))) for b in range(0, row_levels, 2)]
-    full_keyvalue = gather_weight(w_keyvalue, row_groups[::-1])
-    full_query = gather_weight(w_query, row_groups[::-1])
-    full_output = gather_weight(w_output, row_groups[::-1])
+    row_groups = [[b] for b in range(row_levels)]
+    full_query, full_keyvalue, full_output = gather_weights(
+        w_query, w_keyvalue, w_output, row_groups[::-1]
+    )
     inner_width = full_query.shape[1]
     queries = jnp.dot(flat_norm, full_query, preferred_element_type=jnp.float32).astype(
         jnp.bfloat16
@@ -259,18 +266,20 @@
     token_grad = owned.astype(jnp.bfloat16).reshape(-1, 2 * inner_width)
     row_count, col_count = lax.axis_size("row"), lax.axis_size("col")
     col_levels = col_count.bit_length() - 1
-    col_groups = [[0, 2], [1, 3]] if col_levels == 4 else [[b] for b in range(col_levels)]
+    col_groups = [[0], [2], [1], [3]] if col_levels == 4 else [[b] for b in range(col_levels)]
     feature_part = model_width // row_count
     column_part = token_grad.shape[1] // col_count
-    partial = jnp.einsum(
-        "tra,tcb->crab",
-        flat_norm.reshape(-1, row_count, feature_part),
-        token_grad.reshape(-1, col_count, column_part),
-        preferred_element_type=jnp.float32,
-    )
+    partial = lax.dot_general(
+        token_grad, flat_norm, (((0,), (0,)), ((), ())), preferred_element_type=jnp.float32
+    )
+    partial = partial.reshape(col_count, column_part, model_width)
     col_part = scatter_by_bits(partial, "col", col_groups)[0]
-    rows_part = scatter_by_bits(col_part, "row", row_groups)[0]
+    lanes = 256
+    by_rows = col_part.reshape(column_part, row_count, feature_part).transpose(1, 2, 0)
+    by_rows = by_rows.reshape(row_count, feature_part * column_part // lanes, lanes)
+    rows_part = scatter_by_bits(by_rows, "row", row_groups)[0]
     keyvalue_grad = gather_by_bits(rows_part, "col", col_groups[::-1])
+    keyvalue_grad = keyvalue_grad.reshape(col_count, feature_part, column_part)
     keyvalue_grad = keyvalue_grad.transpose(1, 0, 2).reshape(feature_part, -1)
     normed_grad = lax.dot_general(
         query_grad.reshape(-1, inner_width),

time: 443 us -> 388 us (0.88)
  starting transfers between devices: 215 us -> 126 us
  local copies, waits for them, and re-layouts: 41.6 us -> 60.2 us
  waiting for transfers between devices: 141 us -> 153 us
    ppermute x43 -> x19, starting transfers between devices: 188 us -> 103 us  [partner_swap(): return lax.ppermute(value, axis, [(i, i ^ mask) for i in range(count)])]
    ppermute x2, waiting for transfers between devices: 2.6 us -> 10.5 us  [with_halo(): lax.ppermute(lax.slice_in_dim(block, 0, width, axis=dim), axis, backward)]
    unnamed x48 -> x46, local copies, waits for them, and re-layouts: 8.47 us -> 16 us
    ppermute x43 -> x19, waiting for transfers between devices: 115 us -> 121 us  [partner_swap(): return lax.ppermute(value, axis, [(i, i ^ mask) for i in range(count)])]
    dynamic_update_slice x27 -> x9, local copies, waits for them, and re-layouts: 5.03 us -> 0.22 us  [gather_by_bits(): held = lax.dynamic_update_slice(held, other, place[::-1] + zero)]
    ppermute x4, starting transfers between devices: 14.2 us -> 9.53 us  [shifted(): lax.ppermute(value, axis, [(source, source + steps) for source in range(f...]
  transfers between devices with their start and end apart: 51 -> 27, of which waited for: 18 -> 23; matrix products, arithmetic and copies ran while one was open for 5% -> 5% of each run, Pallas kernels for 0% -> 0%
where the time goes in v4:
time: 388 us; the launch traced here: 386 us
  waiting for transfers between devices  153 us (39%)
  starting transfers between devices  126 us (32%)
  local copies, waits for them, and re-layouts  60.2 us (16%)
  matrix products  28.3 us (7%)
  other arithmetic  17.7 us (5%)
    ppermute x19, waiting for transfers between devices, partner_swap(): return lax.ppermute(value, axis, [(i, i ^ mask) for i in range(count)])  121 us
    ppermute x19, starting transfers between devices, partner_swap(): return lax.ppermute(value, axis, [(i, i ^ mask) for i in range(count)])  103 us
    ppermute x4, waiting for transfers between devices, shifted(): lax.ppermute(value, axis, [(source, source + steps) for source in range(f...  18.6 us
    unnamed x46, local copies, waits for them, and re-layouts  16 us
    ppermute x2, waiting for transfers between devices, with_halo(): lax.ppermute(lax.slice_in_dim(block, 0, width, axis=dim), axis, backward)  10.5 us
    ppermute x2, starting transfers between devices, with_halo(): lax.ppermute(lax.slice_in_dim(block, block.shape[dim] - width, None, axis...  9.8 us
    ppermute x4, starting transfers between devices, shifted(): lax.ppermute(value, axis, [(source, source + steps) for source in range(f...  9.53 us
    concatenate x3, local copies, waits for them, and re-layouts, tile_backward(): jnp.concatenate([key_grad.reshape(batches, ext_count, inner_width), value...  8.26 us
  transfers between devices with their start and end apart: 27, of which 23 were waited for; matrix products, arithmetic and copies ran while one was open for 5% of the time, Pallas kernels for 0%

profile of v4, /device:TPU:1, one launch (start us, length us, event | category | flops | bytes accessed | tf_op | source)
XLA Modules:
  0.0 386.2 jit_solution(8214369933212102769)
XLA Ops:
  2.8 16.3 %collective-permute-start = (bf16[1,1,1,1,1,64,512]{6,5,4,3,2,1,0:T(8,128)(2,1)S(1)}, bf16[1,1,1,1,1,64,512]{6,5,4,3,2,1,0:T(8,128)(2,1)S(1)}, u32[]{:S(2)}, u32[]{:S(2)}) collective-permute-start(bf16[1,1,1,1,1,64,512]{6,5,4,3,2,1,0:T(8,128)(2,1)S(1)} %constant_dynamic-slice_fusion.17), channel_id=1, source_target_pairs={{0,256},{16,272},{32,288},{48,304},{64,320},{80,336},{96,352},{112... | collective-permute-start | bytes 196616 | tf_op jit(solution)/shard_map/ppermute | solution.py:37
  21.0 5.3 %collective-permute-start.1 = (bf16[2,1,1,1,1,64,512]{6,5,4,3,2,1,0:T(8,128)(2,1)S(1)}, bf16[2,1,1,1,1,64,512]{6,5,4,3,2,1,0:T(8,128)(2,1)S(1)}, u32[]{:S(2)}, u32[]{:S(2)}) collective-permute-start(bf16[2,1,1,1,1,64,512]{6,5,4,3,2,1,0:T(8,128)(2,1)S(1)} %constant_dynamic-slice_fusion.16), channel_id=1, source_target_pairs={{0,128},{16,144},{32,160},{48,176},{64,192},{80,208},{96,224},{112... | collective-permute-start | bytes 393224 | tf_op jit(solution)/shard_map/ppermute | solution.py:37
  26.2 13.5 %collective-permute-done.1 = bf16[2,1,1,1,1,64,512]{6,5,4,3,2,1,0:T(8,128)(2,1)S(1)} collective-permute-done((bf16[2,1,1,1,1,64,512]{6,5,4,3,2,1,0:T(8,128)(2,1)S(1)}, bf16[2,1,1,1,1,64,512]{6,5,4,3,2,1,0:T(8,128)(2,1)S(1)}, u32[]{:S(2)}, u32[]{:S(2)}) %collective-permute-start.1) | collective-permute-done | bytes 131104 | tf_op jit(solution)/shard_map/ppermute | solution.py:37
  41.7 13.5 %collective-permute-done.2 = bf16[2,2,1,1,1,64,512]{6,5,4,3,2,1,0:T(8,128)(2,1)S(1)} collective-permute-done((bf16[2,2,1,1,1,64,512]{6,5,4,3,2,1,0:T(8,128)(2,1)S(1)}, bf16[2,2,1,1,1,64,512]{6,5,4,3,2,1,0:T(8,128)(2,1)S(1)}, u32[]{:S(2)}, u32[]{:S(2)}) %collective-permute-start.2) | collective-permute-done | bytes 262176 | tf_op jit(solution)/shard_map/ppermute | solution.py:37
  57.2 13.0 %collective-permute-done.3 = bf16[2,2,2,1,1,64,512]{6,5,4,3,2,1,0:T(8,128)(2,1)S(1)} collective-permute-done((bf16[2,2,2,1,1,64,512]{6,5,4,3,2,1,0:T(8,128)(2,1)S(1)}, bf16[2,2,2,1,1,64,512]{6,5,4,3,2,1,0:T(8,128)(2,1)S(1)}, u32[]{:S(2)}, u32[]{:S(2)}) %collective-permute-start.3) | collective-permute-done | bytes 524320 | tf_op jit(solution)/shard_map/ppermute | solution.py:37
  74.6 22.2 %collective-permute-done.4 = bf16[2,2,2,2,1,64,512]{6,5,4,3,2,1,0:T(8,128)(2,1)S(1)} collective-permute-done((bf16[2,2,2,2,1,64,512]{6,5,4,3,2,1,0:T(8,128)(2,1)}, bf16[2,2,2,2,1,64,512]{6,5,4,3,2,1,0:T(8,128)(2,1)S(1)}, u32[]{:S(2)}, u32[]{:S(2)}) %collective-permute-start.4) | collective-permute-done | bytes 1048608 | tf_op jit(solution)/shard_map/ppermute | solution.py:37
  96.9 4.2 %collective-permute-start.5 = (bf16[32,64,512]{2,1,0:T(8,128)(2,1)S(1)}, bf16[32,64,512]{2,1,0:T(8,128)(2,1)}, u32[]{:S(2)}, u32[]{:S(2)}) collective-permute-start(bf16[32,64,512]{2,1,0:T(8,128)(2,1)S(1)} %bitcast.115), channel_id=1, source_target_pairs={{0,1},{1,0},{2,3},{3,2},{4,5},{5,4},{6,7},{7,6},{8,9},{9,8},{10,11... | collective-permute-start | bytes 6291464 | tf_op jit(solution)/shard_map/ppermute | solution.py:37
  113.1 3.9 %collective-permute-start.6 = (bf16[1,6,16,1024]{3,2,1,0:T(8,128)(2,1)}, bf16[1,6,16,1024]{3,2,1,0:T(8,128)(2,1)}, u32[]{:S(2)}, u32[]{:S(2)}) collective-permute-start(bf16[1,6,16,1024]{3,2,1,0:T(8,128)(2,1)} %get-tuple-element.13), channel_id=1, source_target_pairs={{0,16},{16,32},{32,48},{48,64},{64,80},{80,96},{96,112},{112,128},... | collective-permute-start | bytes 589832 | tf_op jit(solution)/shard_map/ppermute | solution.py:27
  120.4 4.6 %collective-permute-done.7 = bf16[1,6,16,1024]{3,2,1,0:T(8,128)(2,1)} collective-permute-done((bf16[1,6,16,1024]{3,2,1,0:T(8,128)(2,1)}, bf16[1,6,16,1024]{3,2,1,0:T(8,128)(2,1)}, u32[]{:S(2)}, u32[]{:S(2)}) %collective-permute-start.7) | collective-permute-done | bytes 196640 | tf_op jit(solution)/shard_map/ppermute | solution.py:30
  126.3 5.9 %collective-permute-start.8 = (bf16[1,20,6,1024]{3,2,1,0:T(8,128)(2,1)S(1)}, bf16[1,20,6,1024]{3,2,1,0:T(8,128)(2,1)S(1)}, u32[]{:S(2)}, u32[]{:S(2)}) collective-permute-start(bf16[1,20,6,1024]{3,2,1,0:T(8,128)(2,1)S(1)} %get-tuple-element.11), channel_id=1, source_target_pairs={{0,1},{1,2},{2,3},{3,4},{4,5},{5,6},{6,7},{7,8},{8,9},{9,10},{10,1... | collective-permute-start | bytes 737288 | tf_op jit(solution)/shard_map/ppermute | solution.py:27
  136.2 5.9 %collective-permute-done.9 = bf16[1,20,6,1024]{3,2,1,0:T(8,128)(2,1)S(1)} collective-permute-done((bf16[1,20,6,1024]{3,2,1,0:T(8,128)(2,1)S(1)}, bf16[1,20,6,1024]{3,2,1,0:T(8,128)(2,1)S(1)}, u32[]{:S(2)}, u32[]{:S(2)}) %collective-permute-start.9) | collective-permute-done | bytes 245792 | tf_op jit(solution)/shard_map/ppermute | solution.py:30
  166.8 3.6 concatenate.34
  170.4 5.6 %fusion.12 = f32[1,560,8,64]{1,3,2,0:T(8,128)} fusion(bf16[128,8,64]{0,2,1:T(8,128)(2,1)S(1)} %bitcast.152, f32[8,128,560]{1,2,0:T(8,128)} %fusion.77, f32[8,128,560]{1,2,0:T(8,128)} %get-tuple-element.16, f32[8,128]{1,0:T(8,128)S(1)} %get-tuple-element.15), kind=kOutput, calls=%fused_computation.14 | convolution fusion | flops 77415984 | bytes 5869568 | tf_op jit(solution)/shard_map/bhqk,bqhd->bkhd/dot_general | solution.py:178
  179.1 3.6 concatenate.33
  194.7 5.9 %collective-permute-done.11 = f32[1,20,6,1024]{3,0,2,1:T(1,128)S(1)} collective-permute-done((f32[1,20,6,1024]{3,0,2,1:T(1,128)S(1)}, f32[1,20,6,1024]{3,0,2,1:T(1,128)S(1)}, u32[]{:S(2)}, u32[]{:S(2)}) %collective-permute-start.11) | collective-permute-done | bytes 491552 | tf_op jit(solution)/shard_map/ppermute | solution.py:19
  204.5 3.7 collective-permute-start.12
  209.5 9.6 %collective-permute-done.12 = f32[1,6,16,1024]{3,0,2,1:T(1,128)} collective-permute-done((f32[1,6,16,1024]{3,0,2,1:T(1,128)}, f32[1,6,16,1024]{3,0,2,1:T(1,128)}, u32[]{:S(2)}, u32[]{:S(2)}) %collective-permute-start.12) | collective-permute-done | bytes 393248 | tf_op jit(solution)/shard_map/ppermute | solution.py:19
  230.8 4.4 %collective-permute-done.14 = f32[2,2,2,1,1,64,1024]{6,5,2,1,0,4,3:T(8,128)} collective-permute-done((f32[2,2,2,1,1,64,1024]{6,5,2,1,0,4,3:T(8,128)}, f32[2,2,2,1,1,64,1024]{6,5,2,1,0,4,3:T(8,128)}, u32[]{:S(2)}, u32[]{:S(2)}) %collective-permute-start.14) | collective-permute-done | bytes 2097184 | tf_op jit(solution)/shard_map/ppermute | solution.py:37
  240.2 9.3 %collective-permute-start.15 = (f32[2,1,2,1,1,64,1024]{6,5,2,1,0,4,3:T(8,128)}, f32[2,1,2,1,1,64,1024]{6,5,2,1,0,4,3:T(8,128)}, u32[]{:S(2)}, u32[]{:S(2)}) collective-permute-start(f32[2,1,2,1,1,64,1024]{6,5,2,1,0,4,3:T(8,128)} %constant_dynamic-slice_fusion.12), channel_id=1, source_target_pairs={{0,4},{1,5},{2,6},{3,7},{4,0},{5,1},{6,2},{7,3},{8,12},{9,13},{10,... | collective-permute-start | bytes 3145736 | tf_op jit(solution)/shard_map/ppermute | solution.py:37
  249.6 23.7 %collective-permute-done.15 = f32[2,1,2,1,1,64,1024]{6,5,2,1,0,4,3:T(8,128)} collective-permute-done((f32[2,1,2,1,1,64,1024]{6,5,2,1,0,4,3:T(8,128)}, f32[2,1,2,1,1,64,1024]{6,5,2,1,0,4,3:T(8,128)}, u32[]{:S(2)}, u32[]{:S(2)}) %collective-permute-start.15) | collective-permute-done | bytes 1048608 | tf_op jit(solution)/shard_map/ppermute | solution.py:37
  276.7 5.3 %collective-permute-start.16 = (f32[2,1,1,1,1,64,1024]{6,5,2,1,0,4,3:T(8,128)}, f32[2,1,1,1,1,64,1024]{6,5,2,1,0,4,3:T(8,128)}, u32[]{:S(2)}, u32[]{:S(2)}) collective-permute-start(f32[2,1,1,1,1,64,1024]{6,5,2,1,0,4,3:T(8,128)} %constant_dynamic-slice_fusion.11), channel_id=1, source_target_pairs={{0,2},{1,3},{2,0},{3,1},{4,6},{5,7},{6,4},{7,5},{8,10},{9,11},{10,... | collective-permute-start | bytes 1572872 | tf_op jit(solution)/shard_map/ppermute | solution.py:37
  282.1 11.9 %collective-permute-done.16 = f32[2,1,1,1,1,64,1024]{6,5,2,1,0,4,3:T(8,128)} collective-permute-done((f32[2,1,1,1,1,64,1024]{6,5,2,1,0,4,3:T(8,128)}, f32[2,1,1,1,1,64,1024]{6,5,2,1,0,4,3:T(8,128)}, u32[]{:S(2)}, u32[]{:S(2)}) %collective-permute-start.16) | collective-permute-done | bytes 524320 | tf_op jit(solution)/shard_map/ppermute | solution.py:37
  296.7 4.4 %collective-permute-start.17 = (f32[1,1,1,1,1,64,1024]{6,5,2,1,0,4,3:T(8,128)}, f32[1,1,1,1,1,64,1024]{6,5,2,1,0,4,3:T(8,128)}, u32[]{:S(2)}, u32[]{:S(2)}) collective-permute-start(f32[1,1,1,1,1,64,1024]{6,5,2,1,0,4,3:T(8,128)} %constant_dynamic-slice_fusion.10), channel_id=1, source_target_pairs={{0,8},{1,9},{2,10},{3,11},{4,12},{5,13},{6,14},{7,15},{8,0},{9,1},... | collective-permute-start | bytes 786440 | tf_op jit(solution)/shard_map/ppermute | solution.py:37
  302.7 4.3 %collective-permute-done.17 = f32[1,1,1,1,1,64,1024]{6,5,2,1,0,4,3:T(8,128)} collective-permute-done((f32[1,1,1,1,1,64,1024]{6,5,2,1,0,4,3:T(8,128)}, f32[1,1,1,1,1,64,1024]{6,5,2,1,0,4,3:T(8,128)}, u32[]{:S(2)}, u32[]{:S(2)}) %collective-permute-start.17) | collective-permute-done | bytes 262176 | tf_op jit(solution)/shard_map/ppermute | solution.py:37
  318.3 3.6 collective-permute-start.19
  323.6 5.6 %collective-permute-start.20 = (f32[2,2,1,1,1,1,8,256]{7,6,4,3,2,1,0,5:T(8,128)S(1)}, f32[2,2,1,1,1,1,8,256]{7,6,4,3,2,1,0,5:T(8,128)S(1)}, u32[]{:S(2)}, u32[]{:S(2)}) collective-permute-start(f32[2,2,1,1,1,1,8,256]{7,6,4,3,2,1,0,5:T(8,128)S(1)} %constant_dynamic-slice_fusion.7), channel_id=1, source_target_pairs={{0,64},{16,80},{32,96},{48,112},{64,0},{80,16},{96,32},{112,48},{1... | collective-permute-start | bytes 98312 | tf_op jit(solution)/shard_map/ppermute | solution.py:37
  329.2 4.7 %fusion.18 = bf16[8,64,128]{2,1,0:T(8,128)(2,1)S(1)} fusion(bf16[560,8,64]{0,2,1:T(8,128)(2,1)} %bitcast.142, f32[8,128,560]{1,2,0:T(8,128)} %fusion.77, f32[8,128,560]{1,2,0:T(8,128)} %get-tuple-element.16, f32[8,128]{1,0:T(8,128)S(1)} %get-tuple-element.15), kind=kOutput, calls=%fused_computation.23 | convolution fusion | flops 77481520 | bytes 5296128 | tf_op jit(solution)/shard_map/bhqk,bkhd->bqhd/dot_general | solution.py:175
  334.0 8.2 %collective-permute-start.21 = (f32[2,1,1,1,1,1,8,256]{7,6,4,3,2,1,0,5:T(8,128)S(1)}, f32[2,1,1,1,1,1,8,256]{7,6,4,3,2,1,0,5:T(8,128)S(1)}, u32[]{:S(2)}, u32[]{:S(2)}) collective-permute-start(f32[2,1,1,1,1,1,8,256]{7,6,4,3,2,1,0,5:T(8,128)S(1)} %constant_dynamic-slice_fusion.6), channel_id=1, source_target_pairs={{0,128},{16,144},{32,160},{48,176},{64,192},{80,208},{96,224},{112... | collective-permute-start | bytes 49160 | tf_op jit(solution)/shard_map/ppermute | solution.py:37
  343.4 9.0 %collective-permute-start.22 = (f32[1,1,1,1,1,1,8,256]{7,6,4,3,2,1,0,5:T(8,128)S(1)}, f32[1,1,1,1,1,1,8,256]{7,6,4,3,2,1,0,5:T(8,128)S(1)}, u32[]{:S(2)}, u32[]{:S(2)}) collective-permute-start(f32[1,1,1,1,1,1,8,256]{7,6,4,3,2,1,0,5:T(8,128)S(1)} %constant_dynamic-slice_fusion.4), channel_id=1, source_target_pairs={{0,256},{16,272},{32,288},{48,304},{64,320},{80,336},{96,352},{112... | collective-permute-start | bytes 24584 | tf_op jit(solution)/shard_map/ppermute | solution.py:37
  356.6 4.6 %collective-permute-start.23 = (f32[1,1,1,1,8,256]{5,4,3,2,1,0:T(8,128)S(1)}, f32[1,1,1,1,8,256]{5,4,3,2,1,0:T(8,128)S(1)}, u32[]{:S(2)}, u32[]{:S(2)}) collective-permute-start(f32[1,1,1,1,8,256]{5,4,3,2,1,0:T(8,128)S(1)} %constant_dynamic-slice_fusion.3), channel_id=1, source_target_pairs={{0,8},{1,9},{2,10},{3,11},{4,12},{5,13},{6,14},{7,15},{8,0},{9,1},... | collective-permute-start | bytes 24584 | tf_op jit(solution)/shard_map/ppermute | solution.py:37
  364.8 3.6 collective-permute-done.24
  373.1 11.0 %collective-permute-start.26 = (f32[2,2,2,1,8,256]{5,4,3,2,1,0:T(8,128)S(1)}, f32[2,2,2,1,8,256]{5,4,3,2,1,0:T(8,128)S(1)}, u32[]{:S(2)}, u32[]{:S(2)}) collective-permute-start(f32[2,2,2,1,8,256]{5,4,3,2,1,0:T(8,128)S(1)} %constant_dynamic-slice_fusion), channel_id=1, source_target_pairs={{0,1},{1,0},{2,3},{3,2},{4,5},{5,4},{6,7},{7,6},{8,9},{9,8},{10,11... | collective-permute-start | bytes 196616 | tf_op jit(solution)/shard_map/ppermute | solution.py:37
  (170 shorter events, 130.6 us)
Async XLA Ops:
  2.8 18.1 %collective-permute-start = (bf16[1,1,1,1,1,64,512]{6,5,4,3,2,1,0:T(8,128)(2,1)S(1)}, bf16[1,1,1,1,1,64,512]{6,5,4,3,2,1,0:T(8,128)(2,1)S(1)}, u32[]{:S(2)}, u32[]{:S(2)}) collective-permute-start(bf16[1,1,1,1,1,64,512]{6,5,4,3,2,1,0:T(8,128)(2,1)S(1)} %constant_dynamic-slice_fusion.17), channel_id=1, source_target_pairs={{0,256},{16,272},{32,288},{48,304},{64,320},{80,336},{96,352},{112... | collective-permute-start | bytes 196616 | tf_op jit(solution)/shard_map/ppermute | solution.py:37
  21.0 18.7 %collective-permute-start.1 = (bf16[2,1,1,1,1,64,512]{6,5,4,3,2,1,0:T(8,128)(2,1)S(1)}, bf16[2,1,1,1,1,64,512]{6,5,4,3,2,1,0:T(8,128)(2,1)S(1)}, u32[]{:S(2)}, u32[]{:S(2)}) collective-permute-start(bf16[2,1,1,1,1,64,512]{6,5,4,3,2,1,0:T(8,128)(2,1)S(1)} %constant_dynamic-slice_fusion.16), channel_id=1, source_target_pairs={{0,128},{16,144},{32,160},{48,176},{64,192},{80,208},{96,224},{112... | collective-permute-start | bytes 393224 | tf_op jit(solution)/shard_map/ppermute | solution.py:37
  39.8 15.4 %collective-permute-start.2 = (bf16[2,2,1,1,1,64,512]{6,5,4,3,2,1,0:T(8,128)(2,1)S(1)}, bf16[2,2,1,1,1,64,512]{6,5,4,3,2,1,0:T(8,128)(2,1)S(1)}, u32[]{:S(2)}, u32[]{:S(2)}) collective-permute-start(bf16[2,2,1,1,1,64,512]{6,5,4,3,2,1,0:T(8,128)(2,1)S(1)} %constant_dynamic-slice_fusion.15), channel_id=1, source_target_pairs={{0,64},{16,80},{32,96},{48,112},{64,0},{80,16},{96,32},{112,48},{1... | collective-permute-start | bytes 786440 | tf_op jit(solution)/shard_map/ppermute | solution.py:37
  55.3 14.9 %collective-permute-start.3 = (bf16[2,2,2,1,1,64,512]{6,5,4,3,2,1,0:T(8,128)(2,1)S(1)}, bf16[2,2,2,1,1,64,512]{6,5,4,3,2,1,0:T(8,128)(2,1)S(1)}, u32[]{:S(2)}, u32[]{:S(2)}) collective-permute-start(bf16[2,2,2,1,1,64,512]{6,5,4,3,2,1,0:T(8,128)(2,1)S(1)} %constant_dynamic-slice_fusion.14), channel_id=1, source_target_pairs={{0,32},{16,48},{32,0},{48,16},{64,96},{80,112},{96,64},{112,80},{1... | collective-permute-start | bytes 1572872 | tf_op jit(solution)/shard_map/ppermute | solution.py:37
  70.2 30.9 %copy-start.3 = (bf16[1,8,16,1024]{3,2,1,0:T(8,128)(2,1)S(1)}, bf16[1,8,16,1024]{3,2,1,0:T(8,128)(2,1)}, u32[]{:S(2)}) copy-start(bf16[1,8,16,1024]{3,2,1,0:T(8,128)(2,1)} %param.6) | copy-start | bytes 786436
  70.2 32.2 %copy-start.18 = (f32[1024]{0:T(1024)S(1)}, f32[1024]{0:T(1024)}, u32[]{:S(2)}) copy-start(f32[1024]{0:T(1024)} %param.7) | copy-start | bytes 12292
  71.4 25.4 %collective-permute-start.4 = (bf16[2,2,2,2,1,64,512]{6,5,4,3,2,1,0:T(8,128)(2,1)}, bf16[2,2,2,2,1,64,512]{6,5,4,3,2,1,0:T(8,128)(2,1)S(1)}, u32[]{:S(2)}, u32[]{:S(2)}) collective-permute-start(bf16[2,2,2,2,1,64,512]{6,5,4,3,2,1,0:T(8,128)(2,1)} %constant_dynamic-slice_fusion.13), channel_id=1, source_target_pairs={{0,16},{16,0},{32,48},{48,32},{64,80},{80,64},{96,112},{112,96},{1... | collective-permute-start | bytes 3145736 | tf_op jit(solution)/shard_map/ppermute | solution.py:37
  96.9 8.1 %collective-permute-start.5 = (bf16[32,64,512]{2,1,0:T(8,128)(2,1)S(1)}, bf16[32,64,512]{2,1,0:T(8,128)(2,1)}, u32[]{:S(2)}, u32[]{:S(2)}) collective-permute-start(bf16[32,64,512]{2,1,0:T(8,128)(2,1)S(1)} %bitcast.115), channel_id=1, source_target_pairs={{0,1},{1,0},{2,3},{3,2},{4,5},{5,4},{6,7},{7,6},{8,9},{9,8},{10,11... | collective-permute-start | bytes 6291464 | tf_op jit(solution)/shard_map/ppermute | solution.py:37
  113.1 7.3 %collective-permute-start.6 = (bf16[1,6,16,1024]{3,2,1,0:T(8,128)(2,1)}, bf16[1,6,16,1024]{3,2,1,0:T(8,128)(2,1)}, u32[]{:S(2)}, u32[]{:S(2)}) collective-permute-start(bf16[1,6,16,1024]{3,2,1,0:T(8,128)(2,1)} %get-tuple-element.13), channel_id=1, source_target_pairs={{0,16},{16,32},{32,48},{48,64},{64,80},{80,96},{96,112},{112,128},... | collective-permute-start | bytes 589832 | tf_op jit(solution)/shard_map/ppermute | solution.py:27
  117.0 8.0 %collective-permute-start.7 = (bf16[1,6,16,1024]{3,2,1,0:T(8,128)(2,1)}, bf16[1,6,16,1024]{3,2,1,0:T(8,128)(2,1)}, u32[]{:S(2)}, u32[]{:S(2)}) collective-permute-start(bf16[1,6,16,1024]{3,2,1,0:T(8,128)(2,1)} %get-tuple-element.14), channel_id=1, source_target_pairs={{16,0},{32,16},{48,32},{64,48},{80,64},{96,80},{112,96},{128,112},... | collective-permute-start | bytes 589832 | tf_op jit(solution)/shard_map/ppermute | solution.py:30
  119.6 22.5 %copy-start.6 = (bf16[128,1024]{1,0:T(8,128)(2,1)S(1)}, bf16[128,1024]{1,0:T(8,128)(2,1)}, u32[]{:S(2)}) copy-start(bf16[128,1024]{1,0:T(8,128)(2,1)} %copy-done.5) | copy-start | bytes 786436
  126.3 9.9 %collective-permute-start.8 = (bf16[1,20,6,1024]{3,2,1,0:T(8,128)(2,1)S(1)}, bf16[1,20,6,1024]{3,2,1,0:T(8,128)(2,1)S(1)}, u32[]{:S(2)}, u32[]{:S(2)}) collective-permute-start(bf16[1,20,6,1024]{3,2,1,0:T(8,128)(2,1)S(1)} %get-tuple-element.11), channel_id=1, source_target_pairs={{0,1},{1,2},{2,3},{3,4},{4,5},{5,6},{6,7},{7,8},{8,9},{9,10},{10,1... | collective-permute-start | bytes 737288 | tf_op jit(solution)/shard_map/ppermute | solution.py:27
  132.2 9.9 %collective-permute-start.9 = (bf16[1,20,6,1024]{3,2,1,0:T(8,128)(2,1)S(1)}, bf16[1,20,6,1024]{3,2,1,0:T(8,128)(2,1)S(1)}, u32[]{:S(2)}, u32[]{:S(2)}) collective-permute-start(bf16[1,20,6,1024]{3,2,1,0:T(8,128)(2,1)S(1)} %get-tuple-element.12), channel_id=1, source_target_pairs={{1,0},{2,1},{3,2},{4,3},{5,4},{6,5},{7,6},{8,7},{9,8},{10,9},{11,1... | collective-permute-start | bytes 737288 | tf_op jit(solution)/shard_map/ppermute | solution.py:30
  187.0 7.7 %collective-permute-start.10 = (f32[1,20,6,1024]{3,0,2,1:T(1,128)S(1)}, f32[1,20,6,1024]{3,0,2,1:T(1,128)S(1)}, u32[]{:S(2)}, u32[]{:S(2)}) collective-permute-start(f32[1,20,6,1024]{3,0,2,1:T(1,128)S(1)} %get-tuple-element.5), channel_id=1, source_target_pairs={{0,1},{1,2},{2,3},{3,4},{4,5},{5,6},{6,7},{7,8},{8,9},{9,10},{10,1... | collective-permute-start | bytes 1474568 | tf_op jit(solution)/shard_map/ppermute | solution.py:19
  188.9 11.7 %collective-permute-start.11 = (f32[1,20,6,1024]{3,0,2,1:T(1,128)S(1)}, f32[1,20,6,1024]{3,0,2,1:T(1,128)S(1)}, u32[]{:S(2)}, u32[]{:S(2)}) collective-permute-start(f32[1,20,6,1024]{3,0,2,1:T(1,128)S(1)} %get-tuple-element.6), channel_id=1, source_target_pairs={{1,0},{2,1},{3,2},{4,3},{5,4},{6,5},{7,6},{8,7},{9,8},{10,9},{11,1... | collective-permute-start | bytes 1474568 | tf_op jit(solution)/shard_map/ppermute | solution.py:19
  204.5 14.6 %collective-permute-start.12 = (f32[1,6,16,1024]{3,0,2,1:T(1,128)}, f32[1,6,16,1024]{3,0,2,1:T(1,128)}, u32[]{:S(2)}, u32[]{:S(2)}) collective-permute-start(f32[1,6,16,1024]{3,0,2,1:T(1,128)} %get-tuple-element.7), channel_id=1, source_target_pairs={{0,16},{16,32},{32,48},{48,64},{64,80},{80,96},{96,112},{112,128},... | collective-permute-start | bytes 1179656 | tf_op jit(solution)/shard_map/ppermute | solution.py:19
  208.2 10.9 %collective-permute-start.13 = (f32[1,6,16,1024]{3,0,2,1:T(1,128)}, f32[1,6,16,1024]{3,0,2,1:T(1,128)}, u32[]{:S(2)}, u32[]{:S(2)}) collective-permute-start(f32[1,6,16,1024]{3,0,2,1:T(1,128)} %get-tuple-element.8), channel_id=1, source_target_pairs={{16,0},{32,16},{48,32},{64,48},{80,64},{96,80},{112,96},{128,112},... | collective-permute-start | bytes 1179656 | tf_op jit(solution)/shard_map/ppermute | solution.py:19
  228.8 6.4 %collective-permute-start.14 = (f32[2,2,2,1,1,64,1024]{6,5,2,1,0,4,3:T(8,128)}, f32[2,2,2,1,1,64,1024]{6,5,2,1,0,4,3:T(8,128)}, u32[]{:S(2)}, u32[]{:S(2)}) collective-permute-start(f32[2,2,2,1,1,64,1024]{6,5,2,1,0,4,3:T(8,128)} %dynamic-slice_bitcast_fusion), channel_id=1, source_target_pairs={{0,1},{1,0},{2,3},{3,2},{4,5},{5,4},{6,7},{7,6},{8,9},{9,8},{10,11... | collective-permute-start | bytes 6291464 | tf_op jit(solution)/shard_map/ppermute | solution.py:37
  240.2 33.0 %collective-permute-start.15 = (f32[2,1,2,1,1,64,1024]{6,5,2,1,0,4,3:T(8,128)}, f32[2,1,2,1,1,64,1024]{6,5,2,1,0,4,3:T(8,128)}, u32[]{:S(2)}, u32[]{:S(2)}) collective-permute-start(f32[2,1,2,1,1,64,1024]{6,5,2,1,0,4,3:T(8,128)} %constant_dynamic-slice_fusion.12), channel_id=1, source_target_pairs={{0,4},{1,5},{2,6},{3,7},{4,0},{5,1},{6,2},{7,3},{8,12},{9,13},{10,... | collective-permute-start | bytes 3145736 | tf_op jit(solution)/shard_map/ppermute | solution.py:37
  276.7 17.2 %collective-permute-start.16 = (f32[2,1,1,1,1,64,1024]{6,5,2,1,0,4,3:T(8,128)}, f32[2,1,1,1,1,64,1024]{6,5,2,1,0,4,3:T(8,128)}, u32[]{:S(2)}, u32[]{:S(2)}) collective-permute-start(f32[2,1,1,1,1,64,1024]{6,5,2,1,0,4,3:T(8,128)} %constant_dynamic-slice_fusion.11), channel_id=1, source_target_pairs={{0,2},{1,3},{2,0},{3,1},{4,6},{5,7},{6,4},{7,5},{8,10},{9,11},{10,... | collective-permute-start | bytes 1572872 | tf_op jit(solution)/shard_map/ppermute | solution.py:37
  296.7 10.2 %collective-permute-start.17 = (f32[1,1,1,1,1,64,1024]{6,5,2,1,0,4,3:T(8,128)}, f32[1,1,1,1,1,64,1024]{6,5,2,1,0,4,3:T(8,128)}, u32[]{:S(2)}, u32[]{:S(2)}) collective-permute-start(f32[1,1,1,1,1,64,1024]{6,5,2,1,0,4,3:T(8,128)} %constant_dynamic-slice_fusion.10), channel_id=1, source_target_pairs={{0,8},{1,9},{2,10},{3,11},{4,12},{5,13},{6,14},{7,15},{8,0},{9,1},... | collective-permute-start | bytes 786440 | tf_op jit(solution)/shard_map/ppermute | solution.py:37
  309.8 7.5 %collective-permute-start.18 = (f32[2,2,2,2,1,1,8,256]{7,6,4,3,2,1,0,5:T(8,128)}, f32[2,2,2,2,1,1,8,256]{7,6,4,3,2,1,0,5:T(8,128)}, u32[]{:S(2)}, u32[]{:S(2)}) collective-permute-start(f32[2,2,2,2,1,1,8,256]{7,6,4,3,2,1,0,5:T(8,128)} %constant_dynamic-slice_fusion.9), channel_id=1, source_target_pairs={{0,16},{16,0},{32,48},{48,32},{64,80},{80,64},{96,112},{112,96},{1... | collective-permute-start | bytes 393224 | tf_op jit(solution)/shard_map/ppermute | solution.py:37
  318.3 5.3 %collective-permute-start.19 = (f32[2,2,2,1,1,1,8,256]{7,6,4,3,2,1,0,5:T(8,128)S(1)}, f32[2,2,2,1,1,1,8,256]{7,6,4,3,2,1,0,5:T(8,128)S(1)}, u32[]{:S(2)}, u32[]{:S(2)}) collective-permute-start(f32[2,2,2,1,1,1,8,256]{7,6,4,3,2,1,0,5:T(8,128)S(1)} %constant_dynamic-slice_fusion.8), channel_id=1, source_target_pairs={{0,32},{16,48},{32,0},{48,16},{64,96},{80,112},{96,64},{112,80},{1... | collective-permute-start | bytes 196616 | tf_op jit(solution)/shard_map/ppermute | solution.py:37
  323.6 18.7 %copy-start.12 = (bf16[1,8,16,1024]{3,2,0,1:T(8,128)(2,1)S(1)}, bf16[1,8,16,1024]{3,2,0,1:T(8,128)(2,1)}, u32[]{:S(2)}) copy-start(bf16[1,8,16,1024]{3,2,0,1:T(8,128)(2,1)} %copy.41) | copy-start | bytes 786436
  323.6 10.4 %collective-permute-start.20 = (f32[2,2,1,1,1,1,8,256]{7,6,4,3,2,1,0,5:T(8,128)S(1)}, f32[2,2,1,1,1,1,8,256]{7,6,4,3,2,1,0,5:T(8,128)S(1)}, u32[]{:S(2)}, u32[]{:S(2)}) collective-permute-start(f32[2,2,1,1,1,1,8,256]{7,6,4,3,2,1,0,5:T(8,128)S(1)} %constant_dynamic-slice_fusion.7), channel_id=1, source_target_pairs={{0,64},{16,80},{32,96},{48,112},{64,0},{80,16},{96,32},{112,48},{1... | collective-permute-start | bytes 98312 | tf_op jit(solution)/shard_map/ppermute | solution.py:37
  334.0 9.4 %collective-permute-start.21 = (f32[2,1,1,1,1,1,8,256]{7,6,4,3,2,1,0,5:T(8,128)S(1)}, f32[2,1,1,1,1,1,8,256]{7,6,4,3,2,1,0,5:T(8,128)S(1)}, u32[]{:S(2)}, u32[]{:S(2)}) collective-permute-start(f32[2,1,1,1,1,1,8,256]{7,6,4,3,2,1,0,5:T(8,128)S(1)} %constant_dynamic-slice_fusion.6), channel_id=1, source_target_pairs={{0,128},{16,144},{32,160},{48,176},{64,192},{80,208},{96,224},{112... | collective-permute-start | bytes 49160 | tf_op jit(solution)/shard_map/ppermute | solution.py:37
  343.1 41.0 %copy-start.16 = (bf16[1,8,16,1024]{3,2,1,0:T(8,128)(2,1)S(1)}, bf16[1,8,16,1024]{3,2,1,0:T(8,128)(2,1)}, u32[]{:S(2)}) copy-start(bf16[1,8,16,1024]{3,2,1,0:T(8,128)(2,1)} %param.11) | copy-start | bytes 786436
  343.4 13.1 %collective-permute-start.22 = (f32[1,1,1,1,1,1,8,256]{7,6,4,3,2,1,0,5:T(8,128)S(1)}, f32[1,1,1,1,1,1,8,256]{7,6,4,3,2,1,0,5:T(8,128)S(1)}, u32[]{:S(2)}, u32[]{:S(2)}) collective-permute-start(f32[1,1,1,1,1,1,8,256]{7,6,4,3,2,1,0,5:T(8,128)S(1)} %constant_dynamic-slice_fusion.4), channel_id=1, source_target_pairs={{0,256},{16,272},{32,288},{48,304},{64,320},{80,336},{96,352},{112... | collective-permute-start | bytes 24584 | tf_op jit(solution)/shard_map/ppermute | solution.py:37
  356.6 5.9 %collective-permute-start.23 = (f32[1,1,1,1,8,256]{5,4,3,2,1,0:T(8,128)S(1)}, f32[1,1,1,1,8,256]{5,4,3,2,1,0:T(8,128)S(1)}, u32[]{:S(2)}, u32[]{:S(2)}) collective-permute-start(f32[1,1,1,1,8,256]{5,4,3,2,1,0:T(8,128)S(1)} %constant_dynamic-slice_fusion.3), channel_id=1, source_target_pairs={{0,8},{1,9},{2,10},{3,11},{4,12},{5,13},{6,14},{7,15},{8,0},{9,1},... | collective-permute-start | bytes 24584 | tf_op jit(solution)/shard_map/ppermute | solution.py:37
  362.5 6.0 %collective-permute-start.24 = (f32[2,1,1,1,8,256]{5,4,3,2,1,0:T(8,128)S(1)}, f32[2,1,1,1,8,256]{5,4,3,2,1,0:T(8,128)S(1)}, u32[]{:S(2)}, u32[]{:S(2)}) collective-permute-start(f32[2,1,1,1,8,256]{5,4,3,2,1,0:T(8,128)S(1)} %constant_dynamic-slice_fusion.2), channel_id=1, source_target_pairs={{0,2},{1,3},{2,0},{3,1},{4,6},{5,7},{6,4},{7,5},{8,10},{9,11},{10,... | collective-permute-start | bytes 49160 | tf_op jit(solution)/shard_map/ppermute | solution.py:37
  368.4 4.6 %collective-permute-start.25 = (f32[2,1,2,1,8,256]{5,4,3,2,1,0:T(8,128)S(1)}, f32[2,1,2,1,8,256]{5,4,3,2,1,0:T(8,128)S(1)}, u32[]{:S(2)}, u32[]{:S(2)}) collective-permute-start(f32[2,1,2,1,8,256]{5,4,3,2,1,0:T(8,128)S(1)} %constant_dynamic-slice_fusion.1), channel_id=1, source_target_pairs={{0,4},{1,5},{2,6},{3,7},{4,0},{5,1},{6,2},{7,3},{8,12},{9,13},{10,... | collective-permute-start | bytes 98312 | tf_op jit(solution)/shard_map/ppermute | solution.py:37
  373.1 12.0 %collective-permute-start.26 = (f32[2,2,2,1,8,256]{5,4,3,2,1,0:T(8,128)S(1)}, f32[2,2,2,1,8,256]{5,4,3,2,1,0:T(8,128)S(1)}, u32[]{:S(2)}, u32[]{:S(2)}) collective-permute-start(f32[2,2,2,1,8,256]{5,4,3,2,1,0:T(8,128)S(1)} %constant_dynamic-slice_fusion), channel_id=1, source_target_pairs={{0,1},{1,0},{2,3},{3,2},{4,5},{5,4},{6,7},{7,6},{8,9},{9,8},{10,11... | collective-permute-start | bytes 196616 | tf_op jit(solution)/shard_map/ppermute | solution.py:37
  (15 other events, 88.1 us)

commit v5 on v4

--- a/solution.py
+++ b/solution.py
@@ -266,21 +266,25 @@
     token_grad = owned.astype(jnp.bfloat16).reshape(-1, 2 * inner_width)
     row_count, col_count = lax.axis_size("row"), lax.axis_size("col")
     col_levels = col_count.bit_length() - 1
-    col_groups = [[0], [2], [1], [3]] if col_levels == 4 else [[b] for b in range(col_levels)]
     feature_part = model_width // row_count
-    column_part = token_grad.shape[1] // col_count
     partial = lax.dot_general(
-        token_grad, flat_norm, (((0,), (0,)), ((), ())), preferred_element_type=jnp.float32
-    )
-    partial = partial.reshape(col_count, column_part, model_width)
-    col_part = scatter_by_bits(partial, "col", col_groups)[0]
-    lanes = 256
-    by_rows = col_part.reshape(column_part, row_count, feature_part).transpose(1, 2, 0)
-    by_rows = by_rows.reshape(row_count, feature_part * column_part // lanes, lanes)
-    rows_part = scatter_by_bits(by_rows, "row", row_groups)[0]
-    keyvalue_grad = gather_by_bits(rows_part, "col", col_groups[::-1])
-    keyvalue_grad = keyvalue_grad.reshape(col_count, feature_part, column_part)
-    keyvalue_grad = keyvalue_grad.transpose(1, 0, 2).reshape(feature_part, -1)
+        flat_norm, token_grad, (((0,), (0,)), ((), ())), preferred_element_type=jnp.float32
+    )
+    half = partial.shape[1] // 2
+    own = axis_bit("col", 0)
+    halves = partial.reshape(model_width, 2, half)
+    pair_part = lax.dynamic_index_in_dim(halves, own, 1, keepdims=False) + partner_swap(
+        lax.dynamic_index_in_dim(halves, 1 - own, 1, keepdims=False), "col", 1
+    )
+    rows_part = scatter_by_bits(
+        pair_part.reshape(row_count, feature_part, half), "row", row_groups
+    )[0]
+    for bit in range(1, col_levels):
+        rows_part = rows_part + partner_swap(rows_part, "col", 1 << bit)
+    held = jnp.zeros((2,) + rows_part.shape, rows_part.dtype)
+    held = lax.dynamic_update_slice(held, rows_part[None], (own, 0, 0))
+    held = lax.dynamic_update_slice(held, partner_swap(rows_part, "col", 1)[None], (1 - own, 0, 0))
+    keyvalue_grad = held.transpose(1, 0, 2).reshape(feature_part, -1)
     normed_grad = lax.dot_general(
         query_grad.reshape(-1, inner_width),
         full_query,

time: 388 us -> 364 us (0.938)
  starting transfers between devices: 126 us -> 114 us
  local copies, waits for them, and re-layouts: 60.2 us -> 48.7 us
  other arithmetic: 17.7 us -> 10.7 us
    ppermute x19 -> x16, starting transfers between devices: 103 us -> 92.2 us  [partner_swap(): return lax.ppermute(value, axis, [(i, i ^ mask) for i in range(count)])]
    add x8 -> x4, other arithmetic: 7.63 us -> 1.38 us  [scatter_by_bits(): summed = summed + partner_swap(send, axis, mask)]
    unnamed x46 -> x41, local copies, waits for them, and re-layouts: 16 us -> 10.8 us
    ppermute x19 -> x16, waiting for transfers between devices: 121 us -> 124 us  [partner_swap(): return lax.ppermute(value, axis, [(i, i ^ mask) for i in range(count)])]
  transfers between devices with their start and end apart: 27 -> 24, of which waited for: 23 -> 22; matrix products, arithmetic and copies ran while one was open for 5% -> 5% of each run, Pallas kernels for 0% -> 0%
where the time goes in v5:
time: 364 us; the launch traced here: 360 us
  waiting for transfers between devices  156 us (43%)
  starting transfers between devices  114 us (31%)
  local copies, waits for them, and re-layouts  48.7 us (13%)
  matrix products  29 us (8%)
  other arithmetic  10.7 us (3%)
    ppermute x16, waiting for transfers between devices, partner_swap(): return lax.ppermute(value, axis, [(i, i ^ mask) for i in range(count)])  124 us
    ppermute x16, starting transfers between devices, partner_swap(): return lax.ppermute(value, axis, [(i, i ^ mask) for i in range(count)])  92.2 us
    ppermute x4, waiting for transfers between devices, shifted(): lax.ppermute(value, axis, [(source, source + steps) for source in range(f...  19.2 us
    unnamed x41, local copies, waits for them, and re-layouts  10.8 us
    ppermute x2, waiting for transfers between devices, with_halo(): lax.ppermute(lax.slice_in_dim(block, 0, width, axis=dim), axis, backward)  10.5 us
    ppermute x2, starting transfers between devices, with_halo(): lax.ppermute(lax.slice_in_dim(block, block.shape[dim] - width, None, axis...  9.82 us
    ppermute x4, starting transfers between devices, shifted(): lax.ppermute(value, axis, [(source, source + steps) for source in range(f...  8.82 us
    concatenate x3, local copies, waits for them, and re-layouts, tile_backward(): jnp.concatenate([key_grad.reshape(batches, ext_count, inner_width), value...  8.28 us
  transfers between devices with their start and end apart: 24, of which 22 were waited for; matrix products, arithmetic and copies ran while one was open for 5% of the time, Pallas kernels for 0%

profile of v5, /device:TPU:1, one launch (start us, length us, event | category | flops | bytes accessed | tf_op | source)
XLA Modules:
  0.0 360.1 jit_solution(16952331735890770289)
XLA Ops:
  2.8 16.3 %collective-permute-start = (bf16[1,1,1,1,1,64,512]{6,5,4,3,2,1,0:T(8,128)(2,1)S(1)}, bf16[1,1,1,1,1,64,512]{6,5,4,3,2,1,0:T(8,128)(2,1)S(1)}, u32[]{:S(2)}, u32[]{:S(2)}) collective-permute-start(bf16[1,1,1,1,1,64,512]{6,5,4,3,2,1,0:T(8,128)(2,1)S(1)} %constant_dynamic-slice_fusion.9), channel_id=1, source_target_pairs={{0,256},{16,272},{32,288},{48,304},{64,320},{80,336},{96,352},{112... | collective-permute-start | bytes 196616 | tf_op jit(solution)/shard_map/ppermute | solution.py:37
  21.0 5.3 %collective-permute-start.1 = (bf16[2,1,1,1,1,64,512]{6,5,4,3,2,1,0:T(8,128)(2,1)S(1)}, bf16[2,1,1,1,1,64,512]{6,5,4,3,2,1,0:T(8,128)(2,1)S(1)}, u32[]{:S(2)}, u32[]{:S(2)}) collective-permute-start(bf16[2,1,1,1,1,64,512]{6,5,4,3,2,1,0:T(8,128)(2,1)S(1)} %constant_dynamic-slice_fusion.8), channel_id=1, source_target_pairs={{0,128},{16,144},{32,160},{48,176},{64,192},{80,208},{96,224},{112... | collective-permute-start | bytes 393224 | tf_op jit(solution)/shard_map/ppermute | solution.py:37
  26.2 13.5 %collective-permute-done.1 = bf16[2,1,1,1,1,64,512]{6,5,4,3,2,1,0:T(8,128)(2,1)S(1)} collective-permute-done((bf16[2,1,1,1,1,64,512]{6,5,4,3,2,1,0:T(8,128)(2,1)S(1)}, bf16[2,1,1,1,1,64,512]{6,5,4,3,2,1,0:T(8,128)(2,1)S(1)}, u32[]{:S(2)}, u32[]{:S(2)}) %collective-permute-start.1) | collective-permute-done | bytes 131104 | tf_op jit(solution)/shard_map/ppermute | solution.py:37
  41.7 13.5 %collective-permute-done.2 = bf16[2,2,1,1,1,64,512]{6,5,4,3,2,1,0:T(8,128)(2,1)S(1)} collective-permute-done((bf16[2,2,1,1,1,64,512]{6,5,4,3,2,1,0:T(8,128)(2,1)S(1)}, bf16[2,2,1,1,1,64,512]{6,5,4,3,2,1,0:T(8,128)(2,1)S(1)}, u32[]{:S(2)}, u32[]{:S(2)}) %collective-permute-start.2) | collective-permute-done | bytes 262176 | tf_op jit(solution)/shard_map/ppermute | solution.py:37
  57.2 13.0 %collective-permute-done.3 = bf16[2,2,2,1,1,64,512]{6,5,4,3,2,1,0:T(8,128)(2,1)S(1)} collective-permute-done((bf16[2,2,2,1,1,64,512]{6,5,4,3,2,1,0:T(8,128)(2,1)S(1)}, bf16[2,2,2,1,1,64,512]{6,5,4,3,2,1,0:T(8,128)(2,1)S(1)}, u32[]{:S(2)}, u32[]{:S(2)}) %collective-permute-start.3) | collective-permute-done | bytes 524320 | tf_op jit(solution)/shard_map/ppermute | solution.py:37
  74.5 22.2 %collective-permute-done.4 = bf16[2,2,2,2,1,64,512]{6,5,4,3,2,1,0:T(8,128)(2,1)S(1)} collective-permute-done((bf16[2,2,2,2,1,64,512]{6,5,4,3,2,1,0:T(8,128)(2,1)}, bf16[2,2,2,2,1,64,512]{6,5,4,3,2,1,0:T(8,128)(2,1)S(1)}, u32[]{:S(2)}, u32[]{:S(2)}) %collective-permute-start.4) | collective-permute-done | bytes 1048608 | tf_op jit(solution)/shard_map/ppermute | solution.py:37
  96.8 4.2 %collective-permute-start.5 = (bf16[32,64,512]{2,1,0:T(8,128)(2,1)S(1)}, bf16[32,64,512]{2,1,0:T(8,128)(2,1)}, u32[]{:S(2)}, u32[]{:S(2)}) collective-permute-start(bf16[32,64,512]{2,1,0:T(8,128)(2,1)S(1)} %bitcast.110), channel_id=1, source_target_pairs={{0,1},{1,0},{2,3},{3,2},{4,5},{5,4},{6,7},{7,6},{8,9},{9,8},{10,11... | collective-permute-start | bytes 6291464 | tf_op jit(solution)/shard_map/ppermute | solution.py:37
  113.1 3.9 %collective-permute-start.6 = (bf16[1,6,16,1024]{3,2,1,0:T(8,128)(2,1)}, bf16[1,6,16,1024]{3,2,1,0:T(8,128)(2,1)}, u32[]{:S(2)}, u32[]{:S(2)}) collective-permute-start(bf16[1,6,16,1024]{3,2,1,0:T(8,128)(2,1)} %get-tuple-element.13), channel_id=1, source_target_pairs={{0,16},{16,32},{32,48},{48,64},{64,80},{80,96},{96,112},{112,128},... | collective-permute-start | bytes 589832 | tf_op jit(solution)/shard_map/ppermute | solution.py:27
  120.3 4.6 %collective-permute-done.7 = bf16[1,6,16,1024]{3,2,1,0:T(8,128)(2,1)} collective-permute-done((bf16[1,6,16,1024]{3,2,1,0:T(8,128)(2,1)}, bf16[1,6,16,1024]{3,2,1,0:T(8,128)(2,1)}, u32[]{:S(2)}, u32[]{:S(2)}) %collective-permute-start.7) | collective-permute-done | bytes 196640 | tf_op jit(solution)/shard_map/ppermute | solution.py:30
  126.2 5.9 %collective-permute-start.8 = (bf16[1,20,6,1024]{3,2,1,0:T(8,128)(2,1)S(1)}, bf16[1,20,6,1024]{3,2,1,0:T(8,128)(2,1)S(1)}, u32[]{:S(2)}, u32[]{:S(2)}) collective-permute-start(bf16[1,20,6,1024]{3,2,1,0:T(8,128)(2,1)S(1)} %get-tuple-element.11), channel_id=1, source_target_pairs={{0,1},{1,2},{2,3},{3,4},{4,5},{5,6},{6,7},{7,8},{8,9},{9,10},{10,1... | collective-permute-start | bytes 737288 | tf_op jit(solution)/shard_map/ppermute | solution.py:27
  136.2 5.9 %collective-permute-done.9 = bf16[1,20,6,1024]{3,2,1,0:T(8,128)(2,1)S(1)} collective-permute-done((bf16[1,20,6,1024]{3,2,1,0:T(8,128)(2,1)S(1)}, bf16[1,20,6,1024]{3,2,1,0:T(8,128)(2,1)S(1)}, u32[]{:S(2)}, u32[]{:S(2)}) %collective-permute-start.9) | collective-permute-done | bytes 245792 | tf_op jit(solution)/shard_map/ppermute | solution.py:30
  156.7 3.5 fusion.74
  166.7 3.7 %concatenate.34 = f32[1,20,28,512]{3,0,2,1:T(1,128)} reshape(f32[1,560,8,64]{3,2,0,1:T(8,128)} %copy.27) | data formatting | bytes 2293760 | tf_op jit(solution)/shard_map/concatenate | solution.py:185
  170.3 5.6 %fusion.12 = f32[1,560,8,64]{1,3,2,0:T(8,128)} fusion(bf16[128,8,64]{0,2,1:T(8,128)(2,1)S(1)} %bitcast.148, f32[8,128,560]{1,2,0:T(8,128)} %fusion.75, f32[8,128,560]{1,2,0:T(8,128)} %get-tuple-element.16, f32[8,128]{1,0:T(8,128)S(1)} %get-tuple-element.15), kind=kOutput, calls=%fused_computation.14 | convolution fusion | flops 77415984 | bytes 5869568 | tf_op jit(solution)/shard_map/bhqk,bqhd->bkhd/dot_general | solution.py:178
  179.0 3.6 %concatenate.33 = f32[1,20,28,512]{3,0,2,1:T(1,128)} reshape(f32[1,560,8,64]{3,2,0,1:T(8,128)} %copy.26) | data formatting | bytes 2293760 | tf_op jit(solution)/shard_map/concatenate | solution.py:185
  194.6 5.9 %collective-permute-done.11 = f32[1,20,6,1024]{3,0,2,1:T(1,128)S(1)} collective-permute-done((f32[1,20,6,1024]{3,0,2,1:T(1,128)S(1)}, f32[1,20,6,1024]{3,0,2,1:T(1,128)S(1)}, u32[]{:S(2)}, u32[]{:S(2)}) %collective-permute-start.11) | collective-permute-done | bytes 491552 | tf_op jit(solution)/shard_map/ppermute | solution.py:19
  206.8 10.2 %collective-permute-done.12 = f32[1,6,16,1024]{3,0,2,1:T(1,128)S(1)} collective-permute-done((f32[1,6,16,1024]{3,0,2,1:T(1,128)S(1)}, f32[1,6,16,1024]{3,0,2,1:T(1,128)S(1)}, u32[]{:S(2)}, u32[]{:S(2)}) %collective-permute-start.12) | collective-permute-done | bytes 393248 | tf_op jit(solution)/shard_map/ppermute | solution.py:19
  224.1 4.1 %collective-permute-done.14 = f32[1024,512]{1,0:T(8,128)S(1)} collective-permute-done((f32[1024,512]{1,0:T(8,128)S(1)}, f32[1024,512]{1,0:T(8,128)S(1)}, u32[]{:S(2)}, u32[]{:S(2)}) %collective-permute-start.14) | collective-permute-done | bytes 2097184 | tf_op jit(solution)/shard_map/ppermute | solution.py:37
  228.8 3.8 %collective-permute-start.15 = (f32[2,2,2,2,1,1,32,512]{7,6,5,4,3,2,1,0:T(8,128)S(1)}, f32[2,2,2,2,1,1,32,512]{7,6,5,4,3,2,1,0:T(8,128)S(1)}, u32[]{:S(2)}, u32[]{:S(2)}) collective-permute-start(f32[2,2,2,2,1,1,32,512]{7,6,5,4,3,2,1,0:T(8,128)S(1)} %constant_dynamic-slice_fusion.4), channel_id=1, source_target_pairs={{0,16},{16,0},{32,48},{48,32},{64,80},{80,64},{96,112},{112,96},{1... | collective-permute-start | bytes 3145736 | tf_op jit(solution)/shard_map/ppermute | solution.py:37
  232.6 23.4 %collective-permute-done.15 = f32[2,2,2,2,1,1,32,512]{7,6,5,4,3,2,1,0:T(8,128)S(1)} collective-permute-done((f32[2,2,2,2,1,1,32,512]{7,6,5,4,3,2,1,0:T(8,128)S(1)}, f32[2,2,2,2,1,1,32,512]{7,6,5,4,3,2,1,0:T(8,128)S(1)}, u32[]{:S(2)}, u32[]{:S(2)}) %collective-permute-start.15) | collective-permute-done | bytes 1048608 | tf_op jit(solution)/shard_map/ppermute | solution.py:37
  258.1 3.8 %collective-permute-start.16 = (f32[2,2,2,1,1,1,32,512]{7,6,5,4,3,2,1,0:T(8,128)}, f32[2,2,2,1,1,1,32,512]{7,6,5,4,3,2,1,0:T(8,128)}, u32[]{:S(2)}, u32[]{:S(2)}) collective-permute-start(f32[2,2,2,1,1,1,32,512]{7,6,5,4,3,2,1,0:T(8,128)} %constant_dynamic-slice_fusion.3), channel_id=1, source_target_pairs={{0,32},{16,48},{32,0},{48,16},{64,96},{80,112},{96,64},{112,80},{1... | collective-permute-start | bytes 1572872 | tf_op jit(solution)/shard_map/ppermute | solution.py:37
  266.3 5.5 %fusion.18 = bf16[8,64,128]{2,1,0:T(8,128)(2,1)} fusion(bf16[560,8,64]{0,2,1:T(8,128)(2,1)} %bitcast.137, f32[8,128,560]{1,2,0:T(8,128)} %fusion.75, f32[8,128,560]{1,2,0:T(8,128)} %get-tuple-element.16, f32[8,128]{1,0:T(8,128)S(1)} %get-tuple-element.15), kind=kOutput, calls=%fused_computation.23 | convolution fusion | flops 77481520 | bytes 5296128 | tf_op jit(solution)/shard_map/bhqk,bkhd->bqhd/dot_general | solution.py:175
  274.6 4.1 %collective-permute-start.17 = (f32[2,2,1,1,1,1,32,512]{7,6,5,4,3,2,1,0:T(8,128)S(1)}, f32[2,2,1,1,1,1,32,512]{7,6,5,4,3,2,1,0:T(8,128)S(1)}, u32[]{:S(2)}, u32[]{:S(2)}) collective-permute-start(f32[2,2,1,1,1,1,32,512]{7,6,5,4,3,2,1,0:T(8,128)S(1)} %constant_dynamic-slice_fusion.2), channel_id=1, source_target_pairs={{0,64},{16,80},{32,96},{48,112},{64,0},{80,16},{96,32},{112,48},{1... | collective-permute-start | bytes 786440 | tf_op jit(solution)/shard_map/ppermute | solution.py:37
  279.8 10.2 %collective-permute-done.17 = f32[2,2,1,1,1,1,32,512]{7,6,5,4,3,2,1,0:T(8,128)S(1)} collective-permute-done((f32[2,2,1,1,1,1,32,512]{7,6,5,4,3,2,1,0:T(8,128)S(1)}, f32[2,2,1,1,1,1,32,512]{7,6,5,4,3,2,1,0:T(8,128)S(1)}, u32[]{:S(2)}, u32[]{:S(2)}) %collective-permute-start.17) | collective-permute-done | bytes 262176 | tf_op jit(solution)/shard_map/ppermute | solution.py:37
  290.1 8.8 %collective-permute-start.18 = (f32[2,1,1,1,1,1,32,512]{7,6,5,4,3,2,1,0:T(8,128)S(1)}, f32[2,1,1,1,1,1,32,512]{7,6,5,4,3,2,1,0:T(8,128)S(1)}, u32[]{:S(2)}, u32[]{:S(2)}) collective-permute-start(f32[2,1,1,1,1,1,32,512]{7,6,5,4,3,2,1,0:T(8,128)S(1)} %constant_dynamic-slice_fusion.1), channel_id=1, source_target_pairs={{0,128},{16,144},{32,160},{48,176},{64,192},{80,208},{96,224},{112... | collective-permute-start | bytes 393224 | tf_op jit(solution)/shard_map/ppermute | solution.py:37
  299.7 10.4 %collective-permute-done.18 = f32[2,1,1,1,1,1,32,512]{7,6,5,4,3,2,1,0:T(8,128)S(1)} collective-permute-done((f32[2,1,1,1,1,1,32,512]{7,6,5,4,3,2,1,0:T(8,128)S(1)}, f32[2,1,1,1,1,1,32,512]{7,6,5,4,3,2,1,0:T(8,128)S(1)}, u32[]{:S(2)}, u32[]{:S(2)}) %collective-permute-start.18) | collective-permute-done | bytes 131104 | tf_op jit(solution)/shard_map/ppermute | solution.py:37
  310.1 10.3 %collective-permute-start.19 = (f32[1,1,1,1,1,1,32,512]{7,6,5,4,3,2,1,0:T(8,128)S(1)}, f32[1,1,1,1,1,1,32,512]{7,6,5,4,3,2,1,0:T(8,128)S(1)}, u32[]{:S(2)}, u32[]{:S(2)}) collective-permute-start(f32[1,1,1,1,1,1,32,512]{7,6,5,4,3,2,1,0:T(8,128)S(1)} %constant_dynamic-slice_fusion), channel_id=1, source_target_pairs={{0,256},{16,272},{32,288},{48,304},{64,320},{80,336},{96,352},{112... | collective-permute-start | bytes 196616 | tf_op jit(solution)/shard_map/ppermute | solution.py:37
  321.0 4.1 %collective-permute-done.19 = f32[1,1,1,1,1,1,32,512]{7,6,5,4,3,2,1,0:T(8,128)S(1)} collective-permute-done((f32[1,1,1,1,1,1,32,512]{7,6,5,4,3,2,1,0:T(8,128)S(1)}, f32[1,1,1,1,1,1,32,512]{7,6,5,4,3,2,1,0:T(8,128)S(1)}, u32[]{:S(2)}, u32[]{:S(2)}) %collective-permute-start.19) | collective-permute-done | bytes 65568 | tf_op jit(solution)/shard_map/ppermute | solution.py:37
  325.2 6.2 %collective-permute-start.20 = (f32[32,512]{1,0:T(8,128)S(1)}, f32[32,512]{1,0:T(8,128)S(1)}, u32[]{:S(2)}, u32[]{:S(2)}) collective-permute-start(f32[32,512]{1,0:T(8,128)S(1)} %add_bitcast_fusion), channel_id=1, source_target_pairs={{0,2},{1,3},{2,0},{3,1},{4,6},{5,7},{6,4},{7,5},{8,10},{9,11},{10,... | collective-permute-start | bytes 196616 | tf_op jit(solution)/shard_map/ppermute | solution.py:37
  333.0 4.9 %collective-permute-start.21 = (f32[32,512]{1,0:T(8,128)S(1)}, f32[32,512]{1,0:T(8,128)S(1)}, u32[]{:S(2)}, u32[]{:S(2)}) collective-permute-start(f32[32,512]{1,0:T(8,128)S(1)} %add.344), channel_id=1, source_target_pairs={{0,4},{1,5},{2,6},{3,7},{4,0},{5,1},{6,2},{7,3},{8,12},{9,13},{10,... | collective-permute-start | bytes 196616 | tf_op jit(solution)/shard_map/ppermute | solution.py:37
  339.6 9.9 %collective-permute-start.22 = (f32[32,512]{1,0:T(8,128)S(1)}, f32[32,512]{1,0:T(8,128)S(1)}, u32[]{:S(2)}, u32[]{:S(2)}) collective-permute-start(f32[32,512]{1,0:T(8,128)S(1)} %add.345), channel_id=1, source_target_pairs={{0,8},{1,9},{2,10},{3,11},{4,12},{5,13},{6,14},{7,15},{8,0},{9,1},... | collective-permute-start | bytes 196616 | tf_op jit(solution)/shard_map/ppermute | solution.py:37
  351.1 5.8 %collective-permute-start.23 = (f32[32,512]{1,0:T(8,128)S(1)}, f32[32,512]{1,0:T(8,128)S(1)}, u32[]{:S(2)}, u32[]{:S(2)}) collective-permute-start(f32[32,512]{1,0:T(8,128)S(1)} %add.346), channel_id=1, source_target_pairs={{0,1},{1,0},{2,3},{3,2},{4,5},{5,4},{6,7},{7,6},{8,9},{9,8},{10,11... | collective-permute-start | bytes 196616 | tf_op jit(solution)/shard_map/ppermute | solution.py:37
  (147 shorter events, 102.5 us)
Async XLA Ops:
  2.8 18.1 %collective-permute-start = (bf16[1,1,1,1,1,64,512]{6,5,4,3,2,1,0:T(8,128)(2,1)S(1)}, bf16[1,1,1,1,1,64,512]{6,5,4,3,2,1,0:T(8,128)(2,1)S(1)}, u32[]{:S(2)}, u32[]{:S(2)}) collective-permute-start(bf16[1,1,1,1,1,64,512]{6,5,4,3,2,1,0:T(8,128)(2,1)S(1)} %constant_dynamic-slice_fusion.9), channel_id=1, source_target_pairs={{0,256},{16,272},{32,288},{48,304},{64,320},{80,336},{96,352},{112... | collective-permute-start | bytes 196616 | tf_op jit(solution)/shard_map/ppermute | solution.py:37
  21.0 18.7 %collective-permute-start.1 = (bf16[2,1,1,1,1,64,512]{6,5,4,3,2,1,0:T(8,128)(2,1)S(1)}, bf16[2,1,1,1,1,64,512]{6,5,4,3,2,1,0:T(8,128)(2,1)S(1)}, u32[]{:S(2)}, u32[]{:S(2)}) collective-permute-start(bf16[2,1,1,1,1,64,512]{6,5,4,3,2,1,0:T(8,128)(2,1)S(1)} %constant_dynamic-slice_fusion.8), channel_id=1, source_target_pairs={{0,128},{16,144},{32,160},{48,176},{64,192},{80,208},{96,224},{112... | collective-permute-start | bytes 393224 | tf_op jit(solution)/shard_map/ppermute | solution.py:37
  39.8 15.4 %collective-permute-start.2 = (bf16[2,2,1,1,1,64,512]{6,5,4,3,2,1,0:T(8,128)(2,1)S(1)}, bf16[2,2,1,1,1,64,512]{6,5,4,3,2,1,0:T(8,128)(2,1)S(1)}, u32[]{:S(2)}, u32[]{:S(2)}) collective-permute-start(bf16[2,2,1,1,1,64,512]{6,5,4,3,2,1,0:T(8,128)(2,1)S(1)} %constant_dynamic-slice_fusion.7), channel_id=1, source_target_pairs={{0,64},{16,80},{32,96},{48,112},{64,0},{80,16},{96,32},{112,48},{1... | collective-permute-start | bytes 786440 | tf_op jit(solution)/shard_map/ppermute | solution.py:37
  55.3 14.9 %collective-permute-start.3 = (bf16[2,2,2,1,1,64,512]{6,5,4,3,2,1,0:T(8,128)(2,1)S(1)}, bf16[2,2,2,1,1,64,512]{6,5,4,3,2,1,0:T(8,128)(2,1)S(1)}, u32[]{:S(2)}, u32[]{:S(2)}) collective-permute-start(bf16[2,2,2,1,1,64,512]{6,5,4,3,2,1,0:T(8,128)(2,1)S(1)} %constant_dynamic-slice_fusion.6), channel_id=1, source_target_pairs={{0,32},{16,48},{32,0},{48,16},{64,96},{80,112},{96,64},{112,80},{1... | collective-permute-start | bytes 1572872 | tf_op jit(solution)/shard_map/ppermute | solution.py:37
  70.2 30.9 %copy-start.2 = (bf16[1,8,16,1024]{3,2,1,0:T(8,128)(2,1)S(1)}, bf16[1,8,16,1024]{3,2,1,0:T(8,128)(2,1)}, u32[]{:S(2)}) copy-start(bf16[1,8,16,1024]{3,2,1,0:T(8,128)(2,1)} %param.6) | copy-start | bytes 786436
  70.2 32.1 %copy-start.15 = (f32[1024]{0:T(1024)S(1)}, f32[1024]{0:T(1024)}, u32[]{:S(2)}) copy-start(f32[1024]{0:T(1024)} %param.7) | copy-start | bytes 12292
  71.3 25.4 %collective-permute-start.4 = (bf16[2,2,2,2,1,64,512]{6,5,4,3,2,1,0:T(8,128)(2,1)}, bf16[2,2,2,2,1,64,512]{6,5,4,3,2,1,0:T(8,128)(2,1)S(1)}, u32[]{:S(2)}, u32[]{:S(2)}) collective-permute-start(bf16[2,2,2,2,1,64,512]{6,5,4,3,2,1,0:T(8,128)(2,1)} %constant_dynamic-slice_fusion.5), channel_id=1, source_target_pairs={{0,16},{16,0},{32,48},{48,32},{64,80},{80,64},{96,112},{112,96},{1... | collective-permute-start | bytes 3145736 | tf_op jit(solution)/shard_map/ppermute | solution.py:37
  96.8 8.1 %collective-permute-start.5 = (bf16[32,64,512]{2,1,0:T(8,128)(2,1)S(1)}, bf16[32,64,512]{2,1,0:T(8,128)(2,1)}, u32[]{:S(2)}, u32[]{:S(2)}) collective-permute-start(bf16[32,64,512]{2,1,0:T(8,128)(2,1)S(1)} %bitcast.110), channel_id=1, source_target_pairs={{0,1},{1,0},{2,3},{3,2},{4,5},{5,4},{6,7},{7,6},{8,9},{9,8},{10,11... | collective-permute-start | bytes 6291464 | tf_op jit(solution)/shard_map/ppermute | solution.py:37
  102.6 15.6 %copy-start.6 = (bf16[1,8,16,1024]{3,2,1,0:T(8,128)(2,1)}, bf16[1,8,16,1024]{3,2,1,0:T(8,128)(2,1)S(1)}, u32[]{:S(2)}) copy-start(bf16[1,8,16,1024]{3,2,1,0:T(8,128)(2,1)S(1)} %fusion.34) | copy-start | bytes 786436
  113.1 7.3 %collective-permute-start.6 = (bf16[1,6,16,1024]{3,2,1,0:T(8,128)(2,1)}, bf16[1,6,16,1024]{3,2,1,0:T(8,128)(2,1)}, u32[]{:S(2)}, u32[]{:S(2)}) collective-permute-start(bf16[1,6,16,1024]{3,2,1,0:T(8,128)(2,1)} %get-tuple-element.13), channel_id=1, source_target_pairs={{0,16},{16,32},{32,48},{48,64},{64,80},{80,96},{96,112},{112,128},... | collective-permute-start | bytes 589832 | tf_op jit(solution)/shard_map/ppermute | solution.py:27
  117.0 8.0 %collective-permute-start.7 = (bf16[1,6,16,1024]{3,2,1,0:T(8,128)(2,1)}, bf16[1,6,16,1024]{3,2,1,0:T(8,128)(2,1)}, u32[]{:S(2)}, u32[]{:S(2)}) collective-permute-start(bf16[1,6,16,1024]{3,2,1,0:T(8,128)(2,1)} %get-tuple-element.14), channel_id=1, source_target_pairs={{16,0},{32,16},{48,32},{64,48},{80,64},{96,80},{112,96},{128,112},... | collective-permute-start | bytes 589832 | tf_op jit(solution)/shard_map/ppermute | solution.py:30
  119.6 22.5 %copy-start.4 = (bf16[128,1024]{1,0:T(8,128)(2,1)S(1)}, bf16[128,1024]{1,0:T(8,128)(2,1)}, u32[]{:S(2)}) copy-start(bf16[128,1024]{1,0:T(8,128)(2,1)} %copy-done.3) | copy-start | bytes 786436
  126.2 9.9 %collective-permute-start.8 = (bf16[1,20,6,1024]{3,2,1,0:T(8,128)(2,1)S(1)}, bf16[1,20,6,1024]{3,2,1,0:T(8,128)(2,1)S(1)}, u32[]{:S(2)}, u32[]{:S(2)}) collective-permute-start(bf16[1,20,6,1024]{3,2,1,0:T(8,128)(2,1)S(1)} %get-tuple-element.11), channel_id=1, source_target_pairs={{0,1},{1,2},{2,3},{3,4},{4,5},{5,6},{6,7},{7,8},{8,9},{9,10},{10,1... | collective-permute-start | bytes 737288 | tf_op jit(solution)/shard_map/ppermute | solution.py:27
  132.2 9.9 %collective-permute-start.9 = (bf16[1,20,6,1024]{3,2,1,0:T(8,128)(2,1)S(1)}, bf16[1,20,6,1024]{3,2,1,0:T(8,128)(2,1)S(1)}, u32[]{:S(2)}, u32[]{:S(2)}) collective-permute-start(bf16[1,20,6,1024]{3,2,1,0:T(8,128)(2,1)S(1)} %get-tuple-element.12), channel_id=1, source_target_pairs={{1,0},{2,1},{3,2},{4,3},{5,4},{6,5},{7,6},{8,7},{9,8},{10,9},{11,1... | collective-permute-start | bytes 737288 | tf_op jit(solution)/shard_map/ppermute | solution.py:30
  186.9 7.7 %collective-permute-start.10 = (f32[1,20,6,1024]{3,0,2,1:T(1,128)S(1)}, f32[1,20,6,1024]{3,0,2,1:T(1,128)S(1)}, u32[]{:S(2)}, u32[]{:S(2)}) collective-permute-start(f32[1,20,6,1024]{3,0,2,1:T(1,128)S(1)} %get-tuple-element.5), channel_id=1, source_target_pairs={{0,1},{1,2},{2,3},{3,4},{4,5},{5,6},{6,7},{7,8},{8,9},{9,10},{10,1... | collective-permute-start | bytes 1474568 | tf_op jit(solution)/shard_map/ppermute | solution.py:19
  188.8 11.7 %collective-permute-start.11 = (f32[1,20,6,1024]{3,0,2,1:T(1,128)S(1)}, f32[1,20,6,1024]{3,0,2,1:T(1,128)S(1)}, u32[]{:S(2)}, u32[]{:S(2)}) collective-permute-start(f32[1,20,6,1024]{3,0,2,1:T(1,128)S(1)} %get-tuple-element.6), channel_id=1, source_target_pairs={{1,0},{2,1},{3,2},{4,3},{5,4},{6,5},{7,6},{8,7},{9,8},{10,9},{11,1... | collective-permute-start | bytes 1474568 | tf_op jit(solution)/shard_map/ppermute | solution.py:19
  202.6 14.4 %collective-permute-start.12 = (f32[1,6,16,1024]{3,0,2,1:T(1,128)S(1)}, f32[1,6,16,1024]{3,0,2,1:T(1,128)S(1)}, u32[]{:S(2)}, u32[]{:S(2)}) collective-permute-start(f32[1,6,16,1024]{3,0,2,1:T(1,128)S(1)} %get-tuple-element.7), channel_id=1, source_target_pairs={{0,16},{16,32},{32,48},{48,64},{64,80},{80,96},{96,112},{112,128},... | collective-permute-start | bytes 1179656 | tf_op jit(solution)/shard_map/ppermute | solution.py:19
  205.5 11.5 %collective-permute-start.13 = (f32[1,6,16,1024]{3,0,2,1:T(1,128)S(1)}, f32[1,6,16,1024]{3,0,2,1:T(1,128)S(1)}, u32[]{:S(2)}, u32[]{:S(2)}) collective-permute-start(f32[1,6,16,1024]{3,0,2,1:T(1,128)S(1)} %get-tuple-element.8), channel_id=1, source_target_pairs={{16,0},{32,16},{48,32},{64,48},{80,64},{96,80},{112,96},{128,112},... | collective-permute-start | bytes 1179656 | tf_op jit(solution)/shard_map/ppermute | solution.py:19
  222.2 6.1 %collective-permute-start.14 = (f32[1024,512]{1,0:T(8,128)S(1)}, f32[1024,512]{1,0:T(8,128)S(1)}, u32[]{:S(2)}, u32[]{:S(2)}) collective-permute-start(f32[1024,512]{1,0:T(8,128)S(1)} %dynamic-slice_bitcast_fusion), channel_id=1, source_target_pairs={{0,1},{1,0},{2,3},{3,2},{4,5},{5,4},{6,7},{7,6},{8,9},{9,8},{10,11... | collective-permute-start | bytes 6291464 | tf_op jit(solution)/shard_map/ppermute | solution.py:37
  228.8 27.2 %collective-permute-start.15 = (f32[2,2,2,2,1,1,32,512]{7,6,5,4,3,2,1,0:T(8,128)S(1)}, f32[2,2,2,2,1,1,32,512]{7,6,5,4,3,2,1,0:T(8,128)S(1)}, u32[]{:S(2)}, u32[]{:S(2)}) collective-permute-start(f32[2,2,2,2,1,1,32,512]{7,6,5,4,3,2,1,0:T(8,128)S(1)} %constant_dynamic-slice_fusion.4), channel_id=1, source_target_pairs={{0,16},{16,0},{32,48},{48,32},{64,80},{80,64},{96,112},{112,96},{1... | collective-permute-start | bytes 3145736 | tf_op jit(solution)/shard_map/ppermute | solution.py:37
  258.1 15.4 %collective-permute-start.16 = (f32[2,2,2,1,1,1,32,512]{7,6,5,4,3,2,1,0:T(8,128)}, f32[2,2,2,1,1,1,32,512]{7,6,5,4,3,2,1,0:T(8,128)}, u32[]{:S(2)}, u32[]{:S(2)}) collective-permute-start(f32[2,2,2,1,1,1,32,512]{7,6,5,4,3,2,1,0:T(8,128)} %constant_dynamic-slice_fusion.3), channel_id=1, source_target_pairs={{0,32},{16,48},{32,0},{48,16},{64,96},{80,112},{96,64},{112,80},{1... | collective-permute-start | bytes 1572872 | tf_op jit(solution)/shard_map/ppermute | solution.py:37
  271.8 27.0 %copy-start.10 = (bf16[1,8,16,1024]{3,2,0,1:T(8,128)(2,1)S(1)}, bf16[1,8,16,1024]{3,2,0,1:T(8,128)(2,1)}, u32[]{:S(2)}) copy-start(bf16[1,8,16,1024]{3,2,0,1:T(8,128)(2,1)} %copy.34) | copy-start | bytes 786436
  274.6 15.4 %collective-permute-start.17 = (f32[2,2,1,1,1,1,32,512]{7,6,5,4,3,2,1,0:T(8,128)S(1)}, f32[2,2,1,1,1,1,32,512]{7,6,5,4,3,2,1,0:T(8,128)S(1)}, u32[]{:S(2)}, u32[]{:S(2)}) collective-permute-start(f32[2,2,1,1,1,1,32,512]{7,6,5,4,3,2,1,0:T(8,128)S(1)} %constant_dynamic-slice_fusion.2), channel_id=1, source_target_pairs={{0,64},{16,80},{32,96},{48,112},{64,0},{80,16},{96,32},{112,48},{1... | collective-permute-start | bytes 786440 | tf_op jit(solution)/shard_map/ppermute | solution.py:37
  279.8 40.7 %copy-start.1 = (bf16[1,32,32,512]{3,2,1,0:T(8,128)(2,1)S(1)}, bf16[1,32,32,512]{3,2,1,0:T(8,128)(2,1)}, u32[]{:S(2)}) copy-start(bf16[1,32,32,512]{3,2,1,0:T(8,128)(2,1)} %copy-done) | copy-start | bytes 3145732
  279.8 40.7 %copy-start.13 = (bf16[8,64,128]{2,1,0:T(8,128)(2,1)S(1)}, bf16[8,64,128]{2,1,0:T(8,128)(2,1)}, u32[]{:S(2)}) copy-start(bf16[8,64,128]{2,1,0:T(8,128)(2,1)} %fusion.18) | copy-start | bytes 393220
  290.1 20.0 %collective-permute-start.18 = (f32[2,1,1,1,1,1,32,512]{7,6,5,4,3,2,1,0:T(8,128)S(1)}, f32[2,1,1,1,1,1,32,512]{7,6,5,4,3,2,1,0:T(8,128)S(1)}, u32[]{:S(2)}, u32[]{:S(2)}) collective-permute-start(f32[2,1,1,1,1,1,32,512]{7,6,5,4,3,2,1,0:T(8,128)S(1)} %constant_dynamic-slice_fusion.1), channel_id=1, source_target_pairs={{0,128},{16,144},{32,160},{48,176},{64,192},{80,208},{96,224},{112... | collective-permute-start | bytes 393224 | tf_op jit(solution)/shard_map/ppermute | solution.py:37
  299.7 57.3 %copy-start.12 = (bf16[1,8,16,1024]{3,2,1,0:T(8,128)(2,1)S(1)}, bf16[1,8,16,1024]{3,2,1,0:T(8,128)(2,1)}, u32[]{:S(2)}) copy-start(bf16[1,8,16,1024]{3,2,1,0:T(8,128)(2,1)} %param.11) | copy-start | bytes 786436
  310.1 15.0 %collective-permute-start.19 = (f32[1,1,1,1,1,1,32,512]{7,6,5,4,3,2,1,0:T(8,128)S(1)}, f32[1,1,1,1,1,1,32,512]{7,6,5,4,3,2,1,0:T(8,128)S(1)}, u32[]{:S(2)}, u32[]{:S(2)}) collective-permute-start(f32[1,1,1,1,1,1,32,512]{7,6,5,4,3,2,1,0:T(8,128)S(1)} %constant_dynamic-slice_fusion), channel_id=1, source_target_pairs={{0,256},{16,272},{32,288},{48,304},{64,320},{80,336},{96,352},{112... | collective-permute-start | bytes 196616 | tf_op jit(solution)/shard_map/ppermute | solution.py:37
  325.2 7.8 %collective-permute-start.20 = (f32[32,512]{1,0:T(8,128)S(1)}, f32[32,512]{1,0:T(8,128)S(1)}, u32[]{:S(2)}, u32[]{:S(2)}) collective-permute-start(f32[32,512]{1,0:T(8,128)S(1)} %add_bitcast_fusion), channel_id=1, source_target_pairs={{0,2},{1,3},{2,0},{3,1},{4,6},{5,7},{6,4},{7,5},{8,10},{9,11},{10,... | collective-permute-start | bytes 196616 | tf_op jit(solution)/shard_map/ppermute | solution.py:37
  333.0 6.5 %collective-permute-start.21 = (f32[32,512]{1,0:T(8,128)S(1)}, f32[32,512]{1,0:T(8,128)S(1)}, u32[]{:S(2)}, u32[]{:S(2)}) collective-permute-start(f32[32,512]{1,0:T(8,128)S(1)} %add.344), channel_id=1, source_target_pairs={{0,4},{1,5},{2,6},{3,7},{4,0},{5,1},{6,2},{7,3},{8,12},{9,13},{10,... | collective-permute-start | bytes 196616 | tf_op jit(solution)/shard_map/ppermute | solution.py:37
  339.6 11.5 %collective-permute-start.22 = (f32[32,512]{1,0:T(8,128)S(1)}, f32[32,512]{1,0:T(8,128)S(1)}, u32[]{:S(2)}, u32[]{:S(2)}) collective-permute-start(f32[32,512]{1,0:T(8,128)S(1)} %add.345), channel_id=1, source_target_pairs={{0,8},{1,9},{2,10},{3,11},{4,12},{5,13},{6,14},{7,15},{8,0},{9,1},... | collective-permute-start | bytes 196616 | tf_op jit(solution)/shard_map/ppermute | solution.py:37
  351.1 7.6 %collective-permute-start.23 = (f32[32,512]{1,0:T(8,128)S(1)}, f32[32,512]{1,0:T(8,128)S(1)}, u32[]{:S(2)}, u32[]{:S(2)}) collective-permute-start(f32[32,512]{1,0:T(8,128)S(1)} %add.346), channel_id=1, source_target_pairs={{0,1},{1,0},{2,3},{3,2},{4,5},{5,4},{6,7},{7,6},{8,9},{9,8},{10,11... | collective-permute-start | bytes 196616 | tf_op jit(solution)/shard_map/ppermute | solution.py:37
  (9 other events, 50.1 us)

commit v6 on v5

--- a/solution.py
+++ b/solution.py
@@ -240,8 +240,13 @@
         jnp.bfloat16
     )
     keyvalue = keyvalue.reshape(batches, tile_rows, tile_cols, 2 * inner_width)
-    keyvalue_ext = with_halo(keyvalue, (("row", 1), ("col", 2)), RADIUS)
-    keyvalue_ext = keyvalue_ext.reshape(batches, ext_rows * ext_cols, 2 * inner_width)
+    joined_ext = with_halo(
+        jnp.concatenate([keyvalue, normed], axis=-1), (("row", 1), ("col", 2)), RADIUS
+    )
+    keyvalue_ext = joined_ext[..., : 2 * inner_width].reshape(
+        batches, ext_rows * ext_cols, 2 * inner_width
+    )
+    normed_ext = joined_ext[..., 2 * inner_width :].reshape(-1, model_width)
     allowed = window_mask(
         lax.axis_index("row") * tile_rows,
         lax.axis_index("col") * tile_cols,
@@ -268,7 +273,10 @@
     col_levels = col_count.bit_length() - 1
     feature_part = model_width // row_count
     partial = lax.dot_general(
-        flat_norm, token_grad, (((0,), (0,)), ((), ())), preferred_element_type=jnp.float32
+        normed_ext,
+        keyvalue_part.reshape(-1, 2 * inner_width).astype(jnp.bfloat16),
+        (((0,), (0,)), ((), ())),
+        preferred_element_type=jnp.float32,
     )
     half = partial.shape[1] // 2
     own = axis_bit("col", 0)

time: 364 us -> 344 us (0.945)
  waiting for transfers between devices: 156 us -> 117 us
  local copies, waits for them, and re-layouts: 48.7 us -> 62.6 us
  starting transfers between devices: 114 us -> 118 us
    ppermute x16, waiting for transfers between devices: 124 us -> 92.6 us  [partner_swap(): return lax.ppermute(value, axis, [(i, i ^ mask) for i in range(count)])]
    ppermute x2, waiting for transfers between devices: 2.18 us -> 17.7 us  [with_halo(): lax.ppermute(lax.slice_in_dim(block, block.shape[dim] - width, None, axis...]
    ppermute x4, waiting for transfers between devices: 19.2 us -> 3.94 us  [shifted(): lax.ppermute(value, axis, [(source, source + steps) for source in range(f...]
    ppermute x2, waiting for transfers between devices: 10.5 us -> 2.91 us  [with_halo(): lax.ppermute(lax.slice_in_dim(block, 0, width, axis=dim), axis, backward)]
    reshape x1 -> x4, local copies, waits for them, and re-layouts: 2.21 us -> 8.81 us  [the longest x1 2.22 us: local(): normed_ext = joined_ext[..., 2 * inner_width:].reshape(-1, model_width)]
    unnamed x41 -> x51, local copies, waits for them, and re-layouts: 10.8 us -> 11.6 us
  transfers between devices with their start and end apart: 24 -> 24, of which waited for: 22 -> 18; matrix products, arithmetic and copies ran while one was open for 5% -> 14% of each run, Pallas kernels for 0% -> 0%
where the time goes in v6:
time: 344 us; the launch traced here: 342 us
  starting transfers between devices  118 us (34%)
  waiting for transfers between devices  117 us (34%)
  local copies, waits for them, and re-layouts  62.6 us (18%)
  matrix products  29.8 us (9%)
  other arithmetic  12.5 us (4%)
    ppermute x16, starting transfers between devices, partner_swap(): return lax.ppermute(value, axis, [(i, i ^ mask) for i in range(count)])  94.2 us
    ppermute x16, waiting for transfers between devices, partner_swap(): return lax.ppermute(value, axis, [(i, i ^ mask) for i in range(count)])  92.6 us
    ppermute x2, waiting for transfers between devices, with_halo(): lax.ppermute(lax.slice_in_dim(block, block.shape[dim] - width, None, axis...  17.7 us
    ppermute x4, starting transfers between devices, shifted(): lax.ppermute(value, axis, [(source, source + steps) for source in range(f...  12 us
    unnamed x51, local copies, waits for them, and re-layouts  11.6 us
    ppermute x2, starting transfers between devices, with_halo(): lax.ppermute(lax.slice_in_dim(block, block.shape[dim] - width, None, axis...  7.83 us
    concatenate x3, local copies, waits for them, and re-layouts, tile_backward(): jnp.concatenate([key_grad.reshape(batches, ext_count, inner_width), value...  7.43 us
  transfers between devices with their start and end apart: 24, of which 18 were waited for; matrix products, arithmetic and copies ran while one was open for 14% of the time, Pallas kernels for 0%

profile of v6, /device:TPU:1, one launch (start us, length us, event | category | flops | bytes accessed | tf_op | source)
XLA Modules:
  0.0 342.2 jit_solution(15555432470437165701)
XLA Ops:
  2.8 16.3 %collective-permute-start = (bf16[1,1,1,1,1,64,512]{6,5,4,3,2,1,0:T(8,128)(2,1)S(1)}, bf16[1,1,1,1,1,64,512]{6,5,4,3,2,1,0:T(8,128)(2,1)S(1)}, u32[]{:S(2)}, u32[]{:S(2)}) collective-permute-start(bf16[1,1,1,1,1,64,512]{6,5,4,3,2,1,0:T(8,128)(2,1)S(1)} %constant_dynamic-slice_fusion.9), channel_id=1, source_target_pairs={{0,256},{16,272},{32,288},{48,304},{64,320},{80,336},{96,352},{112... | collective-permute-start | bytes 196616 | tf_op jit(solution)/shard_map/ppermute | solution.py:37
  21.0 5.3 %collective-permute-start.1 = (bf16[2,1,1,1,1,64,512]{6,5,4,3,2,1,0:T(8,128)(2,1)S(1)}, bf16[2,1,1,1,1,64,512]{6,5,4,3,2,1,0:T(8,128)(2,1)S(1)}, u32[]{:S(2)}, u32[]{:S(2)}) collective-permute-start(bf16[2,1,1,1,1,64,512]{6,5,4,3,2,1,0:T(8,128)(2,1)S(1)} %constant_dynamic-slice_fusion.8), channel_id=1, source_target_pairs={{0,128},{16,144},{32,160},{48,176},{64,192},{80,208},{96,224},{112... | collective-permute-start | bytes 393224 | tf_op jit(solution)/shard_map/ppermute | solution.py:37
  26.2 13.5 %collective-permute-done.1 = bf16[2,1,1,1,1,64,512]{6,5,4,3,2,1,0:T(8,128)(2,1)S(1)} collective-permute-done((bf16[2,1,1,1,1,64,512]{6,5,4,3,2,1,0:T(8,128)(2,1)S(1)}, bf16[2,1,1,1,1,64,512]{6,5,4,3,2,1,0:T(8,128)(2,1)S(1)}, u32[]{:S(2)}, u32[]{:S(2)}) %collective-permute-start.1) | collective-permute-done | bytes 131104 | tf_op jit(solution)/shard_map/ppermute | solution.py:37
  41.7 13.5 %collective-permute-done.2 = bf16[2,2,1,1,1,64,512]{6,5,4,3,2,1,0:T(8,128)(2,1)S(1)} collective-permute-done((bf16[2,2,1,1,1,64,512]{6,5,4,3,2,1,0:T(8,128)(2,1)S(1)}, bf16[2,2,1,1,1,64,512]{6,5,4,3,2,1,0:T(8,128)(2,1)S(1)}, u32[]{:S(2)}, u32[]{:S(2)}) %collective-permute-start.2) | collective-permute-done | bytes 262176 | tf_op jit(solution)/shard_map/ppermute | solution.py:37
  57.2 13.0 %collective-permute-done.3 = bf16[2,2,2,1,1,64,512]{6,5,4,3,2,1,0:T(8,128)(2,1)S(1)} collective-permute-done((bf16[2,2,2,1,1,64,512]{6,5,4,3,2,1,0:T(8,128)(2,1)S(1)}, bf16[2,2,2,1,1,64,512]{6,5,4,3,2,1,0:T(8,128)(2,1)S(1)}, u32[]{:S(2)}, u32[]{:S(2)}) %collective-permute-start.3) | collective-permute-done | bytes 524320 | tf_op jit(solution)/shard_map/ppermute | solution.py:37
  71.3 3.2 collective-permute-start.4
  74.5 22.2 %collective-permute-done.4 = bf16[2,2,2,2,1,64,512]{6,5,4,3,2,1,0:T(8,128)(2,1)S(1)} collective-permute-done((bf16[2,2,2,2,1,64,512]{6,5,4,3,2,1,0:T(8,128)(2,1)}, bf16[2,2,2,2,1,64,512]{6,5,4,3,2,1,0:T(8,128)(2,1)S(1)}, u32[]{:S(2)}, u32[]{:S(2)}) %collective-permute-start.4) | collective-permute-done | bytes 1048608 | tf_op jit(solution)/shard_map/ppermute | solution.py:37
  96.9 4.2 %collective-permute-start.5 = (bf16[32,64,512]{2,1,0:T(8,128)(2,1)S(1)}, bf16[32,64,512]{2,1,0:T(8,128)(2,1)}, u32[]{:S(2)}, u32[]{:S(2)}) collective-permute-start(bf16[32,64,512]{2,1,0:T(8,128)(2,1)S(1)} %bitcast.113), channel_id=1, source_target_pairs={{0,1},{1,0},{2,3},{3,2},{4,5},{5,4},{6,7},{7,6},{8,9},{9,8},{10,11... | collective-permute-start | bytes 6291464 | tf_op jit(solution)/shard_map/ppermute | solution.py:37
  110.3 3.2 collective-permute-start.6
  117.0 13.0 %collective-permute-done.6 = bf16[1,6,16,2048]{3,2,1,0:T(8,128)(2,1)S(1)} collective-permute-done((bf16[1,6,16,2048]{3,2,1,0:T(8,128)(2,1)S(1)}, bf16[1,6,16,2048]{3,2,1,0:T(8,128)(2,1)S(1)}, u32[]{:S(2)}, u32[]{:S(2)}) %collective-permute-start.6) | collective-permute-done | bytes 393248 | tf_op jit(solution)/shard_map/ppermute | solution.py:27
  133.2 3.1 collective-permute-start.9
  136.3 4.6 %collective-permute-start.8 = (bf16[1,20,6,2048]{3,1,2,0:T(8,128)(2,1)}, bf16[1,20,6,2048]{3,1,2,0:T(8,128)(2,1)}, u32[]{:S(2)}, u32[]{:S(2)}) collective-permute-start(bf16[1,20,6,2048]{3,1,2,0:T(8,128)(2,1)} %copy.34), channel_id=1, source_target_pairs={{0,1},{1,2},{2,3},{3,4},{4,5},{5,6},{6,7},{7,8},{8,9},{9,10},{10,1... | collective-permute-start | bytes 1474568 | tf_op jit(solution)/shard_map/ppermute | solution.py:27
  148.0 4.6 %collective-permute-done.8 = bf16[1,20,6,2048]{3,1,2,0:T(8,128)(2,1)} collective-permute-done((bf16[1,20,6,2048]{3,1,2,0:T(8,128)(2,1)}, bf16[1,20,6,2048]{3,1,2,0:T(8,128)(2,1)}, u32[]{:S(2)}, u32[]{:S(2)}) %collective-permute-start.8) | collective-permute-done | bytes 491552 | tf_op jit(solution)/shard_map/ppermute | solution.py:27
  171.5 3.4 %fusion.78 = (f32[8,128]{1,0:T(8,128)S(1)}, f32[8,128,560]{1,2,0:T(8,128)}) fusion(pred[128,560]{0,1:T(8,128)(4,1)S(1)} %copy-done.19, bf16[128,8,64]{0,2,1:T(8,128)(2,1)S(1)} %bitcast.150, bf16[560,8,64]{0,2,1:T(8,128)(2,1)} %bitcast.135), kind=kOutput, calls=%fused_computation.134 | convolution fusion | flops 75694640 | bytes 3074048 | tf_op jit(solution)/shard_map/sub | solution.py:154
  175.0 3.6 %fusion.79 = (bf16[1,560,8,64]{1,3,2,0:T(8,128)(2,1)}, f32[1,560,8,64]{1,3,2,0:T(8,128)}) fusion(bf16[128,8,64]{0,2,1:T(8,128)(2,1)S(1)} %bitcast.143, f32[8,128]{1,0:T(8,128)S(1)} %get-tuple-element.17, pred[128,560]{0,1:T(8,128)(4,1)S(1)} %copy-done.19, bf16[128,8,64]{0,2,1:T(8,128)(2,1)S(1)} %bitcast.151, bf16[560,8,64]{0,2,1:T(8,128)(2,1)} %bitcast.136), kind=kOutput, calls=%fused_computation.135 | convolution fusion | flops 149956144 | bytes 2631680 | tf_op jit(solution)/shard_map/bhqk,bqhd->bkhd/dot_general | solution.py:181
  178.6 5.9 %fusion.80 = (bf16[1,560,8,64]{1,3,2,0:T(8,128)(2,1)}, f32[1,560,8,64]{1,3,2,0:T(8,128)}) fusion(bf16[128,8,64]{0,2,1:T(8,128)(2,1)S(1)} %bitcast.152, f32[8,128,560]{1,2,0:T(8,128)} %fusion.83, f32[8,128,560]{1,2,0:T(8,128)} %get-tuple-element.18, f32[8,128]{1,0:T(8,128)S(1)} %get-tuple-element.17), kind=kOutput, calls=%fused_computation.136 | convolution fusion | flops 77702704 | bytes 6443008 | tf_op jit(solution)/shard_map/bhqk,bqhd->bkhd/dot_general | solution.py:178
  194.4 4.1 %collective-permute-done.14 = f32[1024,512]{1,0:T(8,128)S(1)} collective-permute-done((f32[1024,512]{1,0:T(8,128)S(1)}, f32[1024,512]{1,0:T(8,128)S(1)}, u32[]{:S(2)}, u32[]{:S(2)}) %collective-permute-start.14) | collective-permute-done | bytes 2097184 | tf_op jit(solution)/shard_map/ppermute | solution.py:37
  201.5 3.7 %collective-permute-start.15 = (f32[2,2,2,2,1,1,32,512]{7,6,5,4,3,2,1,0:T(8,128)}, f32[2,2,2,2,1,1,32,512]{7,6,5,4,3,2,1,0:T(8,128)}, u32[]{:S(2)}, u32[]{:S(2)}) collective-permute-start(f32[2,2,2,2,1,1,32,512]{7,6,5,4,3,2,1,0:T(8,128)} %constant_dynamic-slice_fusion.4), channel_id=1, source_target_pairs={{0,16},{16,0},{32,48},{48,32},{64,80},{80,64},{96,112},{112,96},{1... | collective-permute-start | bytes 3145736 | tf_op jit(solution)/shard_map/ppermute | solution.py:37
  220.1 3.6 %concatenate.40 = f32[1,20,28,512]{3,0,2,1:T(1,128)} reshape(f32[1,560,8,64]{3,2,0,1:T(8,128)} %copy.43) | data formatting | bytes 2293760 | tf_op jit(solution)/shard_map/concatenate | solution.py:185
  227.9 6.8 %collective-permute-start.10 = (f32[1,20,6,1024]{3,0,2,1:T(1,128)S(1)}, f32[1,20,6,1024]{3,0,2,1:T(1,128)S(1)}, u32[]{:S(2)}, u32[]{:S(2)}) collective-permute-start(f32[1,20,6,1024]{3,0,2,1:T(1,128)S(1)} %get-tuple-element.7), channel_id=1, source_target_pairs={{0,1},{1,2},{2,3},{3,4},{4,5},{5,6},{6,7},{7,8},{8,9},{9,10},{10,1... | collective-permute-start | bytes 1474568 | tf_op jit(solution)/shard_map/ppermute | solution.py:19
  242.4 3.3 collective-permute-done.10
  253.7 4.7 %fusion.18 = bf16[8,64,128]{2,1,0:T(8,128)(2,1)S(1)} fusion(bf16[560,8,64]{0,2,1:T(8,128)(2,1)} %bitcast.138, f32[8,128,560]{1,2,0:T(8,128)} %fusion.83, f32[8,128,560]{1,2,0:T(8,128)} %get-tuple-element.18, f32[8,128]{1,0:T(8,128)S(1)} %get-tuple-element.17), kind=kOutput, calls=%fused_computation.24 | convolution fusion | flops 77481520 | bytes 5296128 | tf_op jit(solution)/shard_map/bhqk,bkhd->bqhd/dot_general | solution.py:175
  259.6 6.5 %collective-permute-start.17 = (f32[2,2,1,1,1,1,32,512]{7,6,5,4,3,2,1,0:T(8,128)S(1)}, f32[2,2,1,1,1,1,32,512]{7,6,5,4,3,2,1,0:T(8,128)S(1)}, u32[]{:S(2)}, u32[]{:S(2)}) collective-permute-start(f32[2,2,1,1,1,1,32,512]{7,6,5,4,3,2,1,0:T(8,128)S(1)} %constant_dynamic-slice_fusion.2), channel_id=1, source_target_pairs={{0,64},{16,80},{32,96},{48,112},{64,0},{80,16},{96,32},{112,48},{1... | collective-permute-start | bytes 786440 | tf_op jit(solution)/shard_map/ppermute | solution.py:37
  268.2 6.5 %collective-permute-done.17 = f32[2,2,1,1,1,1,32,512]{7,6,5,4,3,2,1,0:T(8,128)S(1)} collective-permute-done((f32[2,2,1,1,1,1,32,512]{7,6,5,4,3,2,1,0:T(8,128)S(1)}, f32[2,2,1,1,1,1,32,512]{7,6,5,4,3,2,1,0:T(8,128)S(1)}, u32[]{:S(2)}, u32[]{:S(2)}) %collective-permute-start.17) | collective-permute-done | bytes 262176 | tf_op jit(solution)/shard_map/ppermute | solution.py:37
  274.7 7.6 %collective-permute-start.18 = (f32[2,1,1,1,1,1,32,512]{7,6,5,4,3,2,1,0:T(8,128)S(1)}, f32[2,1,1,1,1,1,32,512]{7,6,5,4,3,2,1,0:T(8,128)S(1)}, u32[]{:S(2)}, u32[]{:S(2)}) collective-permute-start(f32[2,1,1,1,1,1,32,512]{7,6,5,4,3,2,1,0:T(8,128)S(1)} %constant_dynamic-slice_fusion.1), channel_id=1, source_target_pairs={{0,128},{16,144},{32,160},{48,176},{64,192},{80,208},{96,224},{112... | collective-permute-start | bytes 393224 | tf_op jit(solution)/shard_map/ppermute | solution.py:37
  283.1 6.8 %collective-permute-done.18 = f32[2,1,1,1,1,1,32,512]{7,6,5,4,3,2,1,0:T(8,128)S(1)} collective-permute-done((f32[2,1,1,1,1,1,32,512]{7,6,5,4,3,2,1,0:T(8,128)S(1)}, f32[2,1,1,1,1,1,32,512]{7,6,5,4,3,2,1,0:T(8,128)S(1)}, u32[]{:S(2)}, u32[]{:S(2)}) %collective-permute-start.18) | collective-permute-done | bytes 131104 | tf_op jit(solution)/shard_map/ppermute | solution.py:37
  290.0 8.9 %collective-permute-start.19 = (f32[1,1,1,1,1,1,32,512]{7,6,5,4,3,2,1,0:T(8,128)S(1)}, f32[1,1,1,1,1,1,32,512]{7,6,5,4,3,2,1,0:T(8,128)S(1)}, u32[]{:S(2)}, u32[]{:S(2)}) collective-permute-start(f32[1,1,1,1,1,1,32,512]{7,6,5,4,3,2,1,0:T(8,128)S(1)} %constant_dynamic-slice_fusion), channel_id=1, source_target_pairs={{0,256},{16,272},{32,288},{48,304},{64,320},{80,336},{96,352},{112... | collective-permute-start | bytes 196616 | tf_op jit(solution)/shard_map/ppermute | solution.py:37
  299.5 4.2 %collective-permute-done.19 = f32[1,1,1,1,1,1,32,512]{7,6,5,4,3,2,1,0:T(8,128)S(1)} collective-permute-done((f32[1,1,1,1,1,1,32,512]{7,6,5,4,3,2,1,0:T(8,128)S(1)}, f32[1,1,1,1,1,1,32,512]{7,6,5,4,3,2,1,0:T(8,128)S(1)}, u32[]{:S(2)}, u32[]{:S(2)}) %collective-permute-start.19) | collective-permute-done | bytes 65568 | tf_op jit(solution)/shard_map/ppermute | solution.py:37
  303.7 12.1 %collective-permute-start.20 = (f32[32,512]{1,0:T(8,128)S(1)}, f32[32,512]{1,0:T(8,128)S(1)}, u32[]{:S(2)}, u32[]{:S(2)}) collective-permute-start(f32[32,512]{1,0:T(8,128)S(1)} %add_bitcast_fusion), channel_id=1, source_target_pairs={{0,2},{1,3},{2,0},{3,1},{4,6},{5,7},{6,4},{7,5},{8,10},{9,11},{10,... | collective-permute-start | bytes 196616 | tf_op jit(solution)/shard_map/ppermute | solution.py:37
  317.5 7.6 %collective-permute-start.21 = (f32[32,512]{1,0:T(8,128)S(1)}, f32[32,512]{1,0:T(8,128)S(1)}, u32[]{:S(2)}, u32[]{:S(2)}) collective-permute-start(f32[32,512]{1,0:T(8,128)S(1)} %add.344), channel_id=1, source_target_pairs={{0,4},{1,5},{2,6},{3,7},{4,0},{5,1},{6,2},{7,3},{8,12},{9,13},{10,... | collective-permute-start | bytes 196616 | tf_op jit(solution)/shard_map/ppermute | solution.py:37
  326.7 4.9 %collective-permute-start.22 = (f32[32,512]{1,0:T(8,128)S(1)}, f32[32,512]{1,0:T(8,128)S(1)}, u32[]{:S(2)}, u32[]{:S(2)}) collective-permute-start(f32[32,512]{1,0:T(8,128)S(1)} %add.345), channel_id=1, source_target_pairs={{0,8},{1,9},{2,10},{3,11},{4,12},{5,13},{6,14},{7,15},{8,0},{9,1},... | collective-permute-start | bytes 196616 | tf_op jit(solution)/shard_map/ppermute | solution.py:37
  333.2 5.9 %collective-permute-start.23 = (f32[32,512]{1,0:T(8,128)S(1)}, f32[32,512]{1,0:T(8,128)S(1)}, u32[]{:S(2)}, u32[]{:S(2)}) collective-permute-start(f32[32,512]{1,0:T(8,128)S(1)} %add.346), channel_id=1, source_target_pairs={{0,1},{1,0},{2,3},{3,2},{4,5},{5,4},{6,7},{7,6},{8,9},{9,8},{10,11... | collective-permute-start | bytes 196616 | tf_op jit(solution)/shard_map/ppermute | solution.py:37
  (165 shorter events, 110.8 us)
Async XLA Ops:
  2.8 18.1 %collective-permute-start = (bf16[1,1,1,1,1,64,512]{6,5,4,3,2,1,0:T(8,128)(2,1)S(1)}, bf16[1,1,1,1,1,64,512]{6,5,4,3,2,1,0:T(8,128)(2,1)S(1)}, u32[]{:S(2)}, u32[]{:S(2)}) collective-permute-start(bf16[1,1,1,1,1,64,512]{6,5,4,3,2,1,0:T(8,128)(2,1)S(1)} %constant_dynamic-slice_fusion.9), channel_id=1, source_target_pairs={{0,256},{16,272},{32,288},{48,304},{64,320},{80,336},{96,352},{112... | collective-permute-start | bytes 196616 | tf_op jit(solution)/shard_map/ppermute | solution.py:37
  21.0 18.7 %collective-permute-start.1 = (bf16[2,1,1,1,1,64,512]{6,5,4,3,2,1,0:T(8,128)(2,1)S(1)}, bf16[2,1,1,1,1,64,512]{6,5,4,3,2,1,0:T(8,128)(2,1)S(1)}, u32[]{:S(2)}, u32[]{:S(2)}) collective-permute-start(bf16[2,1,1,1,1,64,512]{6,5,4,3,2,1,0:T(8,128)(2,1)S(1)} %constant_dynamic-slice_fusion.8), channel_id=1, source_target_pairs={{0,128},{16,144},{32,160},{48,176},{64,192},{80,208},{96,224},{112... | collective-permute-start | bytes 393224 | tf_op jit(solution)/shard_map/ppermute | solution.py:37
  39.8 15.4 %collective-permute-start.2 = (bf16[2,2,1,1,1,64,512]{6,5,4,3,2,1,0:T(8,128)(2,1)S(1)}, bf16[2,2,1,1,1,64,512]{6,5,4,3,2,1,0:T(8,128)(2,1)S(1)}, u32[]{:S(2)}, u32[]{:S(2)}) collective-permute-start(bf16[2,2,1,1,1,64,512]{6,5,4,3,2,1,0:T(8,128)(2,1)S(1)} %constant_dynamic-slice_fusion.7), channel_id=1, source_target_pairs={{0,64},{16,80},{32,96},{48,112},{64,0},{80,16},{96,32},{112,48},{1... | collective-permute-start | bytes 786440 | tf_op jit(solution)/shard_map/ppermute | solution.py:37
  55.3 14.9 %collective-permute-start.3 = (bf16[2,2,2,1,1,64,512]{6,5,4,3,2,1,0:T(8,128)(2,1)S(1)}, bf16[2,2,2,1,1,64,512]{6,5,4,3,2,1,0:T(8,128)(2,1)S(1)}, u32[]{:S(2)}, u32[]{:S(2)}) collective-permute-start(bf16[2,2,2,1,1,64,512]{6,5,4,3,2,1,0:T(8,128)(2,1)S(1)} %constant_dynamic-slice_fusion.6), channel_id=1, source_target_pairs={{0,32},{16,48},{32,0},{48,16},{64,96},{80,112},{96,64},{112,80},{1... | collective-permute-start | bytes 1572872 | tf_op jit(solution)/shard_map/ppermute | solution.py:37
  70.2 30.9 %copy-start.2 = (bf16[1,8,16,1024]{3,2,1,0:T(8,128)(2,1)S(1)}, bf16[1,8,16,1024]{3,2,1,0:T(8,128)(2,1)}, u32[]{:S(2)}) copy-start(bf16[1,8,16,1024]{3,2,1,0:T(8,128)(2,1)} %param.6) | copy-start | bytes 786436
  70.2 31.2 %copy-start.20 = (f32[1024]{0:T(1024)S(1)}, f32[1024]{0:T(1024)}, u32[]{:S(2)}) copy-start(f32[1024]{0:T(1024)} %param.7) | copy-start | bytes 12292
  71.3 25.4 %collective-permute-start.4 = (bf16[2,2,2,2,1,64,512]{6,5,4,3,2,1,0:T(8,128)(2,1)}, bf16[2,2,2,2,1,64,512]{6,5,4,3,2,1,0:T(8,128)(2,1)S(1)}, u32[]{:S(2)}, u32[]{:S(2)}) collective-permute-start(bf16[2,2,2,2,1,64,512]{6,5,4,3,2,1,0:T(8,128)(2,1)} %constant_dynamic-slice_fusion.5), channel_id=1, source_target_pairs={{0,16},{16,0},{32,48},{48,32},{64,80},{80,64},{96,112},{112,96},{1... | collective-permute-start | bytes 3145736 | tf_op jit(solution)/shard_map/ppermute | solution.py:37
  96.9 8.1 %collective-permute-start.5 = (bf16[32,64,512]{2,1,0:T(8,128)(2,1)S(1)}, bf16[32,64,512]{2,1,0:T(8,128)(2,1)}, u32[]{:S(2)}, u32[]{:S(2)}) collective-permute-start(bf16[32,64,512]{2,1,0:T(8,128)(2,1)S(1)} %bitcast.113), channel_id=1, source_target_pairs={{0,1},{1,0},{2,3},{3,2},{4,5},{5,4},{6,7},{7,6},{8,9},{9,8},{10,11... | collective-permute-start | bytes 6291464 | tf_op jit(solution)/shard_map/ppermute | solution.py:37
  110.2 19.9 %copy-start.7 = (bf16[128,1024]{1,0:T(8,128)(2,1)}, bf16[128,1024]{1,0:T(8,128)(2,1)S(1)}, u32[]{:S(2)}) copy-start(bf16[128,1024]{1,0:T(8,128)(2,1)S(1)} %convolution_convert_fusion) | copy-start | bytes 786436
  110.3 19.7 %collective-permute-start.6 = (bf16[1,6,16,2048]{3,2,1,0:T(8,128)(2,1)S(1)}, bf16[1,6,16,2048]{3,2,1,0:T(8,128)(2,1)S(1)}, u32[]{:S(2)}, u32[]{:S(2)}) collective-permute-start(bf16[1,6,16,2048]{3,2,1,0:T(8,128)(2,1)S(1)} %get-tuple-element.15), channel_id=1, source_target_pairs={{0,16},{16,32},{32,48},{48,64},{64,80},{80,96},{96,112},{112,128},... | collective-permute-start | bytes 1179656 | tf_op jit(solution)/shard_map/ppermute | solution.py:27
  113.5 16.5 %collective-permute-start.7 = (bf16[1,6,16,2048]{3,2,1,0:T(8,128)(2,1)S(1)}, bf16[1,6,16,2048]{3,2,1,0:T(8,128)(2,1)S(1)}, u32[]{:S(2)}, u32[]{:S(2)}) collective-permute-start(bf16[1,6,16,2048]{3,2,1,0:T(8,128)(2,1)S(1)} %get-tuple-element.16), channel_id=1, source_target_pairs={{16,0},{32,16},{48,32},{64,48},{80,64},{96,80},{112,96},{128,112},... | collective-permute-start | bytes 1179656 | tf_op jit(solution)/shard_map/ppermute | solution.py:30
  115.9 25.0 %copy-start = (bf16[1,32,32,512]{3,2,1,0:T(8,128)(2,1)}, bf16[1,32,32,512]{3,2,1,0:T(8,128)(2,1)S(1)}, u32[]{:S(2)}) copy-start(bf16[1,32,32,512]{3,2,1,0:T(8,128)(2,1)S(1)} %get-tuple-element.4) | copy-start | bytes 3145732
  133.2 13.5 %collective-permute-start.9 = (bf16[1,20,6,2048]{3,1,2,0:T(8,128)(2,1)}, bf16[1,20,6,2048]{3,1,2,0:T(8,128)(2,1)}, u32[]{:S(2)}, u32[]{:S(2)}) collective-permute-start(bf16[1,20,6,2048]{3,1,2,0:T(8,128)(2,1)} %copy.35), channel_id=1, source_target_pairs={{1,0},{2,1},{3,2},{4,3},{5,4},{6,5},{7,6},{8,7},{9,8},{10,9},{11,1... | collective-permute-start | bytes 1474568 | tf_op jit(solution)/shard_map/ppermute | solution.py:30
  136.3 16.3 %collective-permute-start.8 = (bf16[1,20,6,2048]{3,1,2,0:T(8,128)(2,1)}, bf16[1,20,6,2048]{3,1,2,0:T(8,128)(2,1)}, u32[]{:S(2)}, u32[]{:S(2)}) collective-permute-start(bf16[1,20,6,2048]{3,1,2,0:T(8,128)(2,1)} %copy.34), channel_id=1, source_target_pairs={{0,1},{1,2},{2,3},{3,4},{4,5},{5,6},{6,7},{7,8},{8,9},{9,10},{10,1... | collective-permute-start | bytes 1474568 | tf_op jit(solution)/shard_map/ppermute | solution.py:27
  142.2 11.7 %copy-start.8 = (bf16[128,1024]{1,0:T(8,128)(2,1)S(1)}, bf16[128,1024]{1,0:T(8,128)(2,1)}, u32[]{:S(2)}) copy-start(bf16[128,1024]{1,0:T(8,128)(2,1)} %copy-done.7) | copy-start | bytes 786436
  142.3 11.7 %copy-start.11 = (bf16[1,6,16,2048]{3,2,1,0:T(8,128)(2,1)S(1)}, bf16[1,6,16,2048]{3,2,1,0:T(8,128)(2,1)}, u32[]{:S(2)}) copy-start(bf16[1,6,16,2048]{3,2,1,0:T(8,128)(2,1)} %copy-done.10) | copy-start | bytes 1179652
  192.5 6.1 %collective-permute-start.14 = (f32[1024,512]{1,0:T(8,128)S(1)}, f32[1024,512]{1,0:T(8,128)S(1)}, u32[]{:S(2)}, u32[]{:S(2)}) collective-permute-start(f32[1024,512]{1,0:T(8,128)S(1)} %dynamic-slice_bitcast_fusion), channel_id=1, source_target_pairs={{0,1},{1,0},{2,3},{3,2},{4,5},{5,4},{6,7},{7,6},{8,9},{9,8},{10,11... | collective-permute-start | bytes 6291464 | tf_op jit(solution)/shard_map/ppermute | solution.py:37
  201.5 36.2 %collective-permute-start.15 = (f32[2,2,2,2,1,1,32,512]{7,6,5,4,3,2,1,0:T(8,128)}, f32[2,2,2,2,1,1,32,512]{7,6,5,4,3,2,1,0:T(8,128)}, u32[]{:S(2)}, u32[]{:S(2)}) collective-permute-start(f32[2,2,2,2,1,1,32,512]{7,6,5,4,3,2,1,0:T(8,128)} %constant_dynamic-slice_fusion.4), channel_id=1, source_target_pairs={{0,16},{16,0},{32,48},{48,32},{64,80},{80,64},{96,112},{112,96},{1... | collective-permute-start | bytes 3145736 | tf_op jit(solution)/shard_map/ppermute | solution.py:37
  227.9 17.8 %collective-permute-start.10 = (f32[1,20,6,1024]{3,0,2,1:T(1,128)S(1)}, f32[1,20,6,1024]{3,0,2,1:T(1,128)S(1)}, u32[]{:S(2)}, u32[]{:S(2)}) collective-permute-start(f32[1,20,6,1024]{3,0,2,1:T(1,128)S(1)} %get-tuple-element.7), channel_id=1, source_target_pairs={{0,1},{1,2},{2,3},{3,4},{4,5},{5,6},{6,7},{7,8},{8,9},{9,10},{10,1... | collective-permute-start | bytes 1474568 | tf_op jit(solution)/shard_map/ppermute | solution.py:19
  234.7 11.7 %collective-permute-start.11 = (f32[1,20,6,1024]{3,0,2,1:T(1,128)S(1)}, f32[1,20,6,1024]{3,0,2,1:T(1,128)S(1)}, u32[]{:S(2)}, u32[]{:S(2)}) collective-permute-start(f32[1,20,6,1024]{3,0,2,1:T(1,128)S(1)} %get-tuple-element.8), channel_id=1, source_target_pairs={{1,0},{2,1},{3,2},{4,3},{5,4},{6,5},{7,6},{8,7},{9,8},{10,9},{11,1... | collective-permute-start | bytes 1474568 | tf_op jit(solution)/shard_map/ppermute | solution.py:19
  240.0 18.4 %collective-permute-start.16 = (f32[2,2,2,1,1,1,32,512]{7,6,5,4,3,2,1,0:T(8,128)}, f32[2,2,2,1,1,1,32,512]{7,6,5,4,3,2,1,0:T(8,128)}, u32[]{:S(2)}, u32[]{:S(2)}) collective-permute-start(f32[2,2,2,1,1,1,32,512]{7,6,5,4,3,2,1,0:T(8,128)} %constant_dynamic-slice_fusion.3), channel_id=1, source_target_pairs={{0,32},{16,48},{32,0},{48,16},{64,96},{80,112},{96,64},{112,80},{1... | collective-permute-start | bytes 1572872 | tf_op jit(solution)/shard_map/ppermute | solution.py:37
  250.3 15.8 %collective-permute-start.12 = (f32[1,6,16,1024]{3,0,2,1:T(1,128)}, f32[1,6,16,1024]{3,0,2,1:T(1,128)}, u32[]{:S(2)}, u32[]{:S(2)}) collective-permute-start(f32[1,6,16,1024]{3,0,2,1:T(1,128)} %get-tuple-element.9), channel_id=1, source_target_pairs={{0,16},{16,32},{32,48},{48,64},{64,80},{80,96},{96,112},{112,128},... | collective-permute-start | bytes 1179656 | tf_op jit(solution)/shard_map/ppermute | solution.py:19
  252.4 13.7 %collective-permute-start.13 = (f32[1,6,16,1024]{3,0,2,1:T(1,128)}, f32[1,6,16,1024]{3,0,2,1:T(1,128)}, u32[]{:S(2)}, u32[]{:S(2)}) collective-permute-start(f32[1,6,16,1024]{3,0,2,1:T(1,128)} %get-tuple-element.10), channel_id=1, source_target_pairs={{16,0},{32,16},{48,32},{64,48},{80,64},{96,80},{112,96},{128,112},... | collective-permute-start | bytes 1179656 | tf_op jit(solution)/shard_map/ppermute | solution.py:19
  259.6 15.1 %collective-permute-start.17 = (f32[2,2,1,1,1,1,32,512]{7,6,5,4,3,2,1,0:T(8,128)S(1)}, f32[2,2,1,1,1,1,32,512]{7,6,5,4,3,2,1,0:T(8,128)S(1)}, u32[]{:S(2)}, u32[]{:S(2)}) collective-permute-start(f32[2,2,1,1,1,1,32,512]{7,6,5,4,3,2,1,0:T(8,128)S(1)} %constant_dynamic-slice_fusion.2), channel_id=1, source_target_pairs={{0,64},{16,80},{32,96},{48,112},{64,0},{80,16},{96,32},{112,48},{1... | collective-permute-start | bytes 786440 | tf_op jit(solution)/shard_map/ppermute | solution.py:37
  268.1 30.8 %copy-start.1 = (bf16[1,32,32,512]{3,2,1,0:T(8,128)(2,1)S(1)}, bf16[1,32,32,512]{3,2,1,0:T(8,128)(2,1)}, u32[]{:S(2)}) copy-start(bf16[1,32,32,512]{3,2,1,0:T(8,128)(2,1)} %copy-done) | copy-start | bytes 3145732
  274.7 15.2 %collective-permute-start.18 = (f32[2,1,1,1,1,1,32,512]{7,6,5,4,3,2,1,0:T(8,128)S(1)}, f32[2,1,1,1,1,1,32,512]{7,6,5,4,3,2,1,0:T(8,128)S(1)}, u32[]{:S(2)}, u32[]{:S(2)}) collective-permute-start(f32[2,1,1,1,1,1,32,512]{7,6,5,4,3,2,1,0:T(8,128)S(1)} %constant_dynamic-slice_fusion.1), channel_id=1, source_target_pairs={{0,128},{16,144},{32,160},{48,176},{64,192},{80,208},{96,224},{112... | collective-permute-start | bytes 393224 | tf_op jit(solution)/shard_map/ppermute | solution.py:37
  283.1 56.0 %copy-start.16 = (bf16[1,8,16,1024]{3,2,1,0:T(8,128)(2,1)S(1)}, bf16[1,8,16,1024]{3,2,1,0:T(8,128)(2,1)}, u32[]{:S(2)}) copy-start(bf16[1,8,16,1024]{3,2,1,0:T(8,128)(2,1)} %param.11) | copy-start | bytes 786436
  290.0 13.7 %collective-permute-start.19 = (f32[1,1,1,1,1,1,32,512]{7,6,5,4,3,2,1,0:T(8,128)S(1)}, f32[1,1,1,1,1,1,32,512]{7,6,5,4,3,2,1,0:T(8,128)S(1)}, u32[]{:S(2)}, u32[]{:S(2)}) collective-permute-start(f32[1,1,1,1,1,1,32,512]{7,6,5,4,3,2,1,0:T(8,128)S(1)} %constant_dynamic-slice_fusion), channel_id=1, source_target_pairs={{0,256},{16,272},{32,288},{48,304},{64,320},{80,336},{96,352},{112... | collective-permute-start | bytes 196616 | tf_op jit(solution)/shard_map/ppermute | solution.py:37
  303.7 13.7 %collective-permute-start.20 = (f32[32,512]{1,0:T(8,128)S(1)}, f32[32,512]{1,0:T(8,128)S(1)}, u32[]{:S(2)}, u32[]{:S(2)}) collective-permute-start(f32[32,512]{1,0:T(8,128)S(1)} %add_bitcast_fusion), channel_id=1, source_target_pairs={{0,2},{1,3},{2,0},{3,1},{4,6},{5,7},{6,4},{7,5},{8,10},{9,11},{10,... | collective-permute-start | bytes 196616 | tf_op jit(solution)/shard_map/ppermute | solution.py:37
  317.5 9.2 %collective-permute-start.21 = (f32[32,512]{1,0:T(8,128)S(1)}, f32[32,512]{1,0:T(8,128)S(1)}, u32[]{:S(2)}, u32[]{:S(2)}) collective-permute-start(f32[32,512]{1,0:T(8,128)S(1)} %add.344), channel_id=1, source_target_pairs={{0,4},{1,5},{2,6},{3,7},{4,0},{5,1},{6,2},{7,3},{8,12},{9,13},{10,... | collective-permute-start | bytes 196616 | tf_op jit(solution)/shard_map/ppermute | solution.py:37
  326.7 6.5 %collective-permute-start.22 = (f32[32,512]{1,0:T(8,128)S(1)}, f32[32,512]{1,0:T(8,128)S(1)}, u32[]{:S(2)}, u32[]{:S(2)}) collective-permute-start(f32[32,512]{1,0:T(8,128)S(1)} %add.345), channel_id=1, source_target_pairs={{0,8},{1,9},{2,10},{3,11},{4,12},{5,13},{6,14},{7,15},{8,0},{9,1},... | collective-permute-start | bytes 196616 | tf_op jit(solution)/shard_map/ppermute | solution.py:37
  333.2 7.6 %collective-permute-start.23 = (f32[32,512]{1,0:T(8,128)S(1)}, f32[32,512]{1,0:T(8,128)S(1)}, u32[]{:S(2)}, u32[]{:S(2)}) collective-permute-start(f32[32,512]{1,0:T(8,128)S(1)} %add.346), channel_id=1, source_target_pairs={{0,1},{1,0},{2,3},{3,2},{4,5},{5,4},{6,7},{7,6},{8,9},{9,8},{10,11... | collective-permute-start | bytes 196616 | tf_op jit(solution)/shard_map/ppermute | solution.py:37
  (14 other events, 77.2 us)

commit v7 on v6

--- a/solution.py
+++ b/solution.py
@@ -93,6 +93,19 @@
     return held.reshape(held.shape[levels:])
 
 
+def reduce_over_bits(block, axis, bits):
+    mine = [axis_bit(axis, bit) for bit in bits]
+    code = sum(m * (1 << k) for k, m in enumerate(mine))
+    zero = [0] * block.ndim
+    held = jnp.zeros((1 << len(bits),) + block.shape, block.dtype)
+    held = lax.dynamic_update_slice(held, block[None], [code] + zero)
+    for flip in flips(bits):
+        mask = sum(f << b for f, b in zip(flip, bits))
+        other = sum(((m + f) % 2) * (1 << k) for k, (m, f) in enumerate(zip(mine, flip)))
+        held = lax.dynamic_update_slice(held, partner_swap(block, axis, mask)[None], [other] + zero)
+    return jnp.sum(held, axis=0)
+
+
 def gather_weights(w_query, w_keyvalue, w_output, row_groups):
     rows, width = w_query.shape
     kv_pack = w_keyvalue.reshape(rows, 2, width).transpose(1, 0, 2).reshape(2 * rows, width)
@@ -228,8 +241,9 @@
     flat_norm = normed.reshape(-1, model_width)
     row_levels = lax.axis_size("row").bit_length() - 1
     row_groups = [[b] for b in range(row_levels)]
+    far_groups = [list(range(2, row_levels))] + [[1], [0]] if row_levels > 2 else row_groups[::-1]
     full_query, full_keyvalue, full_output = gather_weights(
-        w_query, w_keyvalue, w_output, row_groups[::-1]
+        w_query, w_keyvalue, w_output, far_groups
     )
     inner_width = full_query.shape[1]
     queries = jnp.dot(flat_norm, full_query, preferred_element_type=jnp.float32).astype(
@@ -287,8 +301,7 @@
     rows_part = scatter_by_bits(
         pair_part.reshape(row_count, feature_part, half), "row", row_groups
     )[0]
-    for bit in range(1, col_levels):
-        rows_part = rows_part + partner_swap(rows_part, "col", 1 << bit)
+    rows_part = reduce_over_bits(rows_part, "col", list(range(1, col_levels)))
     held = jnp.zeros((2,) + rows_part.shape, rows_part.dtype)
     held = lax.dynamic_update_slice(held, rows_part[None], (own, 0, 0))
     held = lax.dynamic_update_slice(held, partner_swap(rows_part, "col", 1)[None], (1 - own, 0, 0))

time: 344 us -> 391 us (1.14)
  waiting for transfers between devices: 117 us -> 138 us
  starting transfers between devices: 118 us -> 138 us
    ppermute x16 -> x24, waiting for transfers between devices: 92.6 us -> 118 us  [partner_swap(): return lax.ppermute(value, axis, [(i, i ^ mask) for i in range(count)])]
    ppermute x16 -> x24, starting transfers between devices: 94.2 us -> 114 us  [partner_swap(): return lax.ppermute(value, axis, [(i, i ^ mask) for i in range(count)])]
    ppermute x4, waiting for transfers between devices: 3.94 us -> 0.01 us  [shifted(): lax.ppermute(value, axis, [(source, source + steps) for source in range(f...]
  transfers between devices with their start and end apart: 24 -> 32, of which waited for: 18 -> 16; matrix products, arithmetic and copies ran while one was open for 14% -> 13% of each run, Pallas kernels for 0% -> 0%
where the time goes in v7:
time: 391 us; the launch traced here: 388 us
  starting transfers between devices  138 us (35%)
  waiting for transfers between devices  138 us (35%)
  local copies, waits for them, and re-layouts  65.5 us (17%)
  matrix products  30.4 us (8%)
  other arithmetic  14 us (4%)
    ppermute x24, waiting for transfers between devices, partner_swap(): return lax.ppermute(value, axis, [(i, i ^ mask) for i in range(count)])  118 us
    ppermute x24, starting transfers between devices, partner_swap(): return lax.ppermute(value, axis, [(i, i ^ mask) for i in range(count)])  114 us
    ppermute x2, waiting for transfers between devices, with_halo(): lax.ppermute(lax.slice_in_dim(block, block.shape[dim] - width, None, axis...  17.6 us
    unnamed x51, local copies, waits for them, and re-layouts  13.8 us
    ppermute x4, starting transfers between devices, shifted(): lax.ppermute(value, axis, [(source, source + steps) for source in range(f...  11.3 us
    ppermute x2, starting transfers between devices, with_halo(): lax.ppermute(lax.slice_in_dim(block, block.shape[dim] - width, None, axis...  7.84 us
  transfers between devices with their start and end apart: 32, of which 16 were waited for; matrix products, arithmetic and copies ran while one was open for 13% of the time, Pallas kernels for 0%

profile of v7, /device:TPU:1, one launch (start us, length us, event | category | flops | bytes accessed | tf_op | source)
XLA Modules:
  0.0 388.2 jit_solution(16433425887765147915)
XLA Ops:
  2.8 5.7 %collective-permute-start = (bf16[1,1,1,1,1,64,512]{6,5,4,3,2,1,0:T(8,128)(2,1)S(1)}, bf16[1,1,1,1,1,64,512]{6,5,4,3,2,1,0:T(8,128)(2,1)S(1)}, u32[]{:S(2)}, u32[]{:S(2)}) collective-permute-start(bf16[1,1,1,1,1,64,512]{6,5,4,3,2,1,0:T(8,128)(2,1)S(1)} %constant_dynamic-slice_fusion.7), channel_id=1, source_target_pairs={{0,64},{16,80},{32,96},{48,112},{64,0},{80,16},{96,32},{112,48},{1... | collective-permute-start | bytes 196616 | tf_op jit(solution)/shard_map/ppermute | solution.py:37
  8.5 9.7 %collective-permute-start.6 = (bf16[1,1,1,1,1,64,512]{6,5,4,3,2,1,0:T(8,128)(2,1)S(1)}, bf16[1,1,1,1,1,64,512]{6,5,4,3,2,1,0:T(8,128)(2,1)S(1)}, u32[]{:S(2)}, u32[]{:S(2)}) collective-permute-start(bf16[1,1,1,1,1,64,512]{6,5,4,3,2,1,0:T(8,128)(2,1)S(1)} %constant_dynamic-slice_fusion.7), channel_id=1, source_target_pairs={{0,448},{16,464},{32,480},{48,496},{64,384},{80,400},{96,416},{112... | collective-permute-start | bytes 196616 | tf_op jit(solution)/shard_map/ppermute | solution.py:37
  21.1 8.5 %collective-permute-start.4 = (bf16[1,1,1,1,1,64,512]{6,5,4,3,2,1,0:T(8,128)(2,1)S(1)}, bf16[1,1,1,1,1,64,512]{6,5,4,3,2,1,0:T(8,128)(2,1)S(1)}, u32[]{:S(2)}, u32[]{:S(2)}) collective-permute-start(bf16[1,1,1,1,1,64,512]{6,5,4,3,2,1,0:T(8,128)(2,1)S(1)} %constant_dynamic-slice_fusion.7), channel_id=1, source_target_pairs={{0,320},{16,336},{32,352},{48,368},{64,256},{80,272},{96,288},{112... | collective-permute-start | bytes 196616 | tf_op jit(solution)/shard_map/ppermute | solution.py:37
  29.6 5.5 %collective-permute-start.3 = (bf16[1,1,1,1,1,64,512]{6,5,4,3,2,1,0:T(8,128)(2,1)S(1)}, bf16[1,1,1,1,1,64,512]{6,5,4,3,2,1,0:T(8,128)(2,1)S(1)}, u32[]{:S(2)}, u32[]{:S(2)}) collective-permute-start(bf16[1,1,1,1,1,64,512]{6,5,4,3,2,1,0:T(8,128)(2,1)S(1)} %constant_dynamic-slice_fusion.7), channel_id=1, source_target_pairs={{0,256},{16,272},{32,288},{48,304},{64,320},{80,336},{96,352},{112... | collective-permute-start | bytes 196616 | tf_op jit(solution)/shard_map/ppermute | solution.py:37
  35.3 5.4 %collective-permute-start.1 = (bf16[1,1,1,1,1,64,512]{6,5,4,3,2,1,0:T(8,128)(2,1)S(1)}, bf16[1,1,1,1,1,64,512]{6,5,4,3,2,1,0:T(8,128)(2,1)S(1)}, u32[]{:S(2)}, u32[]{:S(2)}) collective-permute-start(bf16[1,1,1,1,1,64,512]{6,5,4,3,2,1,0:T(8,128)(2,1)S(1)} %constant_dynamic-slice_fusion.7), channel_id=1, source_target_pairs={{0,128},{16,144},{32,160},{48,176},{64,192},{80,208},{96,224},{112... | collective-permute-start | bytes 196616 | tf_op jit(solution)/shard_map/ppermute | solution.py:37
  40.7 12.0 %collective-permute-done.1 = bf16[1,1,1,1,1,64,512]{6,5,4,3,2,1,0:T(8,128)(2,1)S(1)} collective-permute-done((bf16[1,1,1,1,1,64,512]{6,5,4,3,2,1,0:T(8,128)(2,1)S(1)}, bf16[1,1,1,1,1,64,512]{6,5,4,3,2,1,0:T(8,128)(2,1)S(1)}, u32[]{:S(2)}, u32[]{:S(2)}) %collective-permute-start.1) | collective-permute-done | bytes 65568 | tf_op jit(solution)/shard_map/ppermute | solution.py:37
  54.7 8.8 %collective-permute-done.2 = bf16[1,1,1,1,1,64,512]{6,5,4,3,2,1,0:T(8,128)(2,1)S(1)} collective-permute-done((bf16[1,1,1,1,1,64,512]{6,5,4,3,2,1,0:T(8,128)(2,1)S(1)}, bf16[1,1,1,1,1,64,512]{6,5,4,3,2,1,0:T(8,128)(2,1)S(1)}, u32[]{:S(2)}, u32[]{:S(2)}) %collective-permute-start.2) | collective-permute-done | bytes 65568 | tf_op jit(solution)/shard_map/ppermute | solution.py:37
  65.7 11.8 %collective-permute-done.7 = bf16[2,2,2,1,1,64,512]{6,5,4,3,2,1,0:T(8,128)(2,1)S(1)} collective-permute-done((bf16[2,2,2,1,1,64,512]{6,5,4,3,2,1,0:T(8,128)(2,1)S(1)}, bf16[2,2,2,1,1,64,512]{6,5,4,3,2,1,0:T(8,128)(2,1)S(1)}, u32[]{:S(2)}, u32[]{:S(2)}) %collective-permute-start.7) | collective-permute-done | bytes 524320 | tf_op jit(solution)/shard_map/ppermute | solution.py:37
  81.9 21.1 %collective-permute-done.8 = bf16[2,2,2,2,1,64,512]{6,5,4,3,2,1,0:T(8,128)(2,1)S(1)} collective-permute-done((bf16[2,2,2,2,1,64,512]{6,5,4,3,2,1,0:T(8,128)(2,1)}, bf16[2,2,2,2,1,64,512]{6,5,4,3,2,1,0:T(8,128)(2,1)S(1)}, u32[]{:S(2)}, u32[]{:S(2)}) %collective-permute-start.8) | collective-permute-done | bytes 1048608 | tf_op jit(solution)/shard_map/ppermute | solution.py:37
  103.1 5.3 %collective-permute-start.9 = (bf16[32,64,512]{2,1,0:T(8,128)(2,1)S(1)}, bf16[32,64,512]{2,1,0:T(8,128)(2,1)}, u32[]{:S(2)}, u32[]{:S(2)}) collective-permute-start(bf16[32,64,512]{2,1,0:T(8,128)(2,1)S(1)} %bitcast.129), channel_id=1, source_target_pairs={{0,1},{1,0},{2,3},{3,2},{4,5},{5,4},{6,7},{7,6},{8,9},{9,8},{10,11... | collective-permute-start | bytes 6291464 | tf_op jit(solution)/shard_map/ppermute | solution.py:37
  124.4 13.0 %collective-permute-done.10 = bf16[1,6,16,2048]{3,2,1,0:T(8,128)(2,1)S(1)} collective-permute-done((bf16[1,6,16,2048]{3,2,1,0:T(8,128)(2,1)S(1)}, bf16[1,6,16,2048]{3,2,1,0:T(8,128)(2,1)S(1)}, u32[]{:S(2)}, u32[]{:S(2)}) %collective-permute-start.10) | collective-permute-done | bytes 393248 | tf_op jit(solution)/shard_map/ppermute | solution.py:27
  143.7 4.6 %collective-permute-start.12 = (bf16[1,20,6,2048]{3,1,2,0:T(8,128)(2,1)}, bf16[1,20,6,2048]{3,1,2,0:T(8,128)(2,1)}, u32[]{:S(2)}, u32[]{:S(2)}) collective-permute-start(bf16[1,20,6,2048]{3,1,2,0:T(8,128)(2,1)} %copy.34), channel_id=1, source_target_pairs={{0,1},{1,2},{2,3},{3,4},{4,5},{5,6},{6,7},{7,8},{8,9},{9,10},{10,1... | collective-permute-start | bytes 1474568 | tf_op jit(solution)/shard_map/ppermute | solution.py:27
  155.4 4.6 %collective-permute-done.12 = bf16[1,20,6,2048]{3,1,2,0:T(8,128)(2,1)} collective-permute-done((bf16[1,20,6,2048]{3,1,2,0:T(8,128)(2,1)}, bf16[1,20,6,2048]{3,1,2,0:T(8,128)(2,1)}, u32[]{:S(2)}, u32[]{:S(2)}) %collective-permute-start.12) | collective-permute-done | bytes 491552 | tf_op jit(solution)/shard_map/ppermute | solution.py:27
  178.9 3.5 fusion.79
  182.4 3.6 fusion.80
  186.0 5.8 %fusion.81 = (bf16[1,560,8,64]{1,3,2,0:T(8,128)(2,1)}, f32[1,560,8,64]{1,3,2,0:T(8,128)}) fusion(bf16[128,8,64]{0,2,1:T(8,128)(2,1)S(1)} %bitcast.168, f32[8,128,560]{1,2,0:T(8,128)} %fusion.84, f32[8,128,560]{1,2,0:T(8,128)} %get-tuple-element.18, f32[8,128]{1,0:T(8,128)S(1)} %get-tuple-element.17), kind=kOutput, calls=%fused_computation.147 | convolution fusion | flops 77702704 | bytes 6443008 | tf_op jit(solution)/shard_map/bhqk,bqhd->bkhd/dot_general | solution.py:191
  215.7 3.6 concatenate.40
  225.8 5.9 %collective-permute-start.14 = (f32[1,20,6,1024]{3,0,2,1:T(1,128)}, f32[1,20,6,1024]{3,0,2,1:T(1,128)}, u32[]{:S(2)}, u32[]{:S(2)}) collective-permute-start(f32[1,20,6,1024]{3,0,2,1:T(1,128)} %get-tuple-element.7), channel_id=1, source_target_pairs={{0,1},{1,2},{2,3},{3,4},{4,5},{5,6},{6,7},{7,8},{8,9},{9,10},{10,1... | collective-permute-start | bytes 1474568 | tf_op jit(solution)/shard_map/ppermute | solution.py:19
  233.6 5.4 %fusion.18 = bf16[8,64,128]{2,1,0:T(8,128)(2,1)} fusion(bf16[560,8,64]{0,2,1:T(8,128)(2,1)} %bitcast.153, f32[8,128,560]{1,2,0:T(8,128)} %fusion.84, f32[8,128,560]{1,2,0:T(8,128)} %get-tuple-element.18, f32[8,128]{1,0:T(8,128)S(1)} %get-tuple-element.17), kind=kOutput, calls=%fused_computation.24 | convolution fusion | flops 77481520 | bytes 5296128 | tf_op jit(solution)/shard_map/bhqk,bkhd->bqhd/dot_general | solution.py:188
  244.1 3.6 collective-permute-start.19
  260.5 19.0 %collective-permute-done.19 = f32[2,2,2,2,1,1,32,512]{7,6,4,3,2,1,0,5:T(8,128)} collective-permute-done((f32[2,2,2,2,1,1,32,512]{7,6,4,3,2,1,0,5:T(8,128)}, f32[2,2,2,2,1,1,32,512]{7,6,4,3,2,1,0,5:T(8,128)}, u32[]{:S(2)}, u32[]{:S(2)}) %collective-permute-start.19) | collective-permute-done | bytes 1048608 | tf_op jit(solution)/shard_map/ppermute | solution.py:37
  281.0 5.4 %collective-permute-start.20 = (f32[2,2,2,1,1,1,32,512]{7,6,4,3,2,1,0,5:T(8,128)S(1)}, f32[2,2,2,1,1,1,32,512]{7,6,4,3,2,1,0,5:T(8,128)S(1)}, u32[]{:S(2)}, u32[]{:S(2)}) collective-permute-start(f32[2,2,2,1,1,1,32,512]{7,6,4,3,2,1,0,5:T(8,128)S(1)} %constant_dynamic-slice_fusion.3), channel_id=1, source_target_pairs={{0,32},{16,48},{32,0},{48,16},{64,96},{80,112},{96,64},{112,80},{1... | collective-permute-start | bytes 1572872 | tf_op jit(solution)/shard_map/ppermute | solution.py:37
  288.0 6.8 %collective-permute-done.20 = f32[2,2,2,1,1,1,32,512]{7,6,4,3,2,1,0,5:T(8,128)S(1)} collective-permute-done((f32[2,2,2,1,1,1,32,512]{7,6,4,3,2,1,0,5:T(8,128)S(1)}, f32[2,2,2,1,1,1,32,512]{7,6,4,3,2,1,0,5:T(8,128)S(1)}, u32[]{:S(2)}, u32[]{:S(2)}) %collective-permute-start.20) | collective-permute-done | bytes 524320 | tf_op jit(solution)/shard_map/ppermute | solution.py:37
  297.7 8.2 %collective-permute-done.21 = f32[2,2,1,1,1,1,32,512]{7,6,4,3,2,1,0,5:T(8,128)S(1)} collective-permute-done((f32[2,2,1,1,1,1,32,512]{7,6,4,3,2,1,0,5:T(8,128)S(1)}, f32[2,2,1,1,1,1,32,512]{7,6,4,3,2,1,0,5:T(8,128)S(1)}, u32[]{:S(2)}, u32[]{:S(2)}) %collective-permute-start.21) | collective-permute-done | bytes 262176 | tf_op jit(solution)/shard_map/ppermute | solution.py:37
  306.0 5.1 %collective-permute-start.22 = (f32[2,1,1,1,1,1,32,512]{7,6,4,3,2,1,0,5:T(8,128)S(1)}, f32[2,1,1,1,1,1,32,512]{7,6,4,3,2,1,0,5:T(8,128)S(1)}, u32[]{:S(2)}, u32[]{:S(2)}) collective-permute-start(f32[2,1,1,1,1,1,32,512]{7,6,4,3,2,1,0,5:T(8,128)S(1)} %constant_dynamic-slice_fusion.1), channel_id=1, source_target_pairs={{0,128},{16,144},{32,160},{48,176},{64,192},{80,208},{96,224},{112... | collective-permute-start | bytes 393224 | tf_op jit(solution)/shard_map/ppermute | solution.py:37
  311.1 10.7 %collective-permute-done.22 = f32[2,1,1,1,1,1,32,512]{7,6,4,3,2,1,0,5:T(8,128)S(1)} collective-permute-done((f32[2,1,1,1,1,1,32,512]{7,6,4,3,2,1,0,5:T(8,128)S(1)}, f32[2,1,1,1,1,1,32,512]{7,6,4,3,2,1,0,5:T(8,128)S(1)}, u32[]{:S(2)}, u32[]{:S(2)}) %collective-permute-start.22) | collective-permute-done | bytes 131104 | tf_op jit(solution)/shard_map/ppermute | solution.py:37
  321.8 10.7 %collective-permute-start.23 = (f32[1,1,1,1,1,1,32,512]{7,6,4,3,2,1,0,5:T(8,128)S(1)}, f32[1,1,1,1,1,1,32,512]{7,6,4,3,2,1,0,5:T(8,128)S(1)}, u32[]{:S(2)}, u32[]{:S(2)}) collective-permute-start(f32[1,1,1,1,1,1,32,512]{7,6,4,3,2,1,0,5:T(8,128)S(1)} %constant_dynamic-slice_fusion), channel_id=1, source_target_pairs={{0,256},{16,272},{32,288},{48,304},{64,320},{80,336},{96,352},{112... | collective-permute-start | bytes 196616 | tf_op jit(solution)/shard_map/ppermute | solution.py:37
  342.3 8.9 %collective-permute-start.27 = (f32[32,512]{1,0:T(8,128)S(1)}, f32[32,512]{1,0:T(8,128)S(1)}, u32[]{:S(2)}, u32[]{:S(2)}) collective-permute-start(f32[32,512]{1,0:T(8,128)S(1)} %fusion.52), channel_id=1, source_target_pairs={{0,8},{1,9},{2,10},{3,11},{4,12},{5,13},{6,14},{7,15},{8,0},{9,1},... | collective-permute-start | bytes 196616 | tf_op jit(solution)/shard_map/ppermute | solution.py:37
  353.3 4.5 %collective-permute-done.24 = f32[32,512]{1,0:T(8,128)S(1)} collective-permute-done((f32[32,512]{1,0:T(8,128)S(1)}, f32[32,512]{1,0:T(8,128)S(1)}, u32[]{:S(2)}, u32[]{:S(2)}) %collective-permute-start.24) | collective-permute-done | bytes 65568 | tf_op jit(solution)/shard_map/ppermute | solution.py:37
  359.7 3.7 collective-permute-done.25
  365.4 5.5 %collective-permute-done.26 = f32[32,512]{1,0:T(8,128)S(1)} collective-permute-done((f32[32,512]{1,0:T(8,128)S(1)}, f32[32,512]{1,0:T(8,128)S(1)}, u32[]{:S(2)}, u32[]{:S(2)}) %collective-permute-start.26) | collective-permute-done | bytes 65568 | tf_op jit(solution)/shard_map/ppermute | solution.py:37
  371.0 14.1 %collective-permute-start.31 = (f32[32,512]{1,0:T(8,128)S(1)}, f32[32,512]{1,0:T(8,128)S(1)}, u32[]{:S(2)}, u32[]{:S(2)}) collective-permute-start(f32[32,512]{1,0:T(8,128)S(1)} %reduce_sum.69), channel_id=1, source_target_pairs={{0,1},{1,0},{2,3},{3,2},{4,5},{5,4},{6,7},{7,6},{8,9},{9,8},{10,11... | collective-permute-start | bytes 196616 | tf_op jit(solution)/shard_map/ppermute | solution.py:37
  (190 shorter events, 135.8 us)
Async XLA Ops:
  2.8 32.5 %collective-permute-start = (bf16[1,1,1,1,1,64,512]{6,5,4,3,2,1,0:T(8,128)(2,1)S(1)}, bf16[1,1,1,1,1,64,512]{6,5,4,3,2,1,0:T(8,128)(2,1)S(1)}, u32[]{:S(2)}, u32[]{:S(2)}) collective-permute-start(bf16[1,1,1,1,1,64,512]{6,5,4,3,2,1,0:T(8,128)(2,1)S(1)} %constant_dynamic-slice_fusion.7), channel_id=1, source_target_pairs={{0,64},{16,80},{32,96},{48,112},{64,0},{80,16},{96,32},{112,48},{1... | collective-permute-start | bytes 196616 | tf_op jit(solution)/shard_map/ppermute | solution.py:37
  8.5 55.1 %collective-permute-start.6 = (bf16[1,1,1,1,1,64,512]{6,5,4,3,2,1,0:T(8,128)(2,1)S(1)}, bf16[1,1,1,1,1,64,512]{6,5,4,3,2,1,0:T(8,128)(2,1)S(1)}, u32[]{:S(2)}, u32[]{:S(2)}) collective-permute-start(bf16[1,1,1,1,1,64,512]{6,5,4,3,2,1,0:T(8,128)(2,1)S(1)} %constant_dynamic-slice_fusion.7), channel_id=1, source_target_pairs={{0,448},{16,464},{32,480},{48,496},{64,384},{80,400},{96,416},{112... | collective-permute-start | bytes 196616 | tf_op jit(solution)/shard_map/ppermute | solution.py:37
  18.3 45.4 %collective-permute-start.5 = (bf16[1,1,1,1,1,64,512]{6,5,4,3,2,1,0:T(8,128)(2,1)S(1)}, bf16[1,1,1,1,1,64,512]{6,5,4,3,2,1,0:T(8,128)(2,1)S(1)}, u32[]{:S(2)}, u32[]{:S(2)}) collective-permute-start(bf16[1,1,1,1,1,64,512]{6,5,4,3,2,1,0:T(8,128)(2,1)S(1)} %constant_dynamic-slice_fusion.7), channel_id=1, source_target_pairs={{0,384},{16,400},{32,416},{48,432},{64,448},{80,464},{96,480},{112... | collective-permute-start | bytes 196616 | tf_op jit(solution)/shard_map/ppermute | solution.py:37
  21.1 42.5 %collective-permute-start.4 = (bf16[1,1,1,1,1,64,512]{6,5,4,3,2,1,0:T(8,128)(2,1)S(1)}, bf16[1,1,1,1,1,64,512]{6,5,4,3,2,1,0:T(8,128)(2,1)S(1)}, u32[]{:S(2)}, u32[]{:S(2)}) collective-permute-start(bf16[1,1,1,1,1,64,512]{6,5,4,3,2,1,0:T(8,128)(2,1)S(1)} %constant_dynamic-slice_fusion.7), channel_id=1, source_target_pairs={{0,320},{16,336},{32,352},{48,368},{64,256},{80,272},{96,288},{112... | collective-permute-start | bytes 196616 | tf_op jit(solution)/shard_map/ppermute | solution.py:37
  29.6 34.0 %collective-permute-start.3 = (bf16[1,1,1,1,1,64,512]{6,5,4,3,2,1,0:T(8,128)(2,1)S(1)}, bf16[1,1,1,1,1,64,512]{6,5,4,3,2,1,0:T(8,128)(2,1)S(1)}, u32[]{:S(2)}, u32[]{:S(2)}) collective-permute-start(bf16[1,1,1,1,1,64,512]{6,5,4,3,2,1,0:T(8,128)(2,1)S(1)} %constant_dynamic-slice_fusion.7), channel_id=1, source_target_pairs={{0,256},{16,272},{32,288},{48,304},{64,320},{80,336},{96,352},{112... | collective-permute-start | bytes 196616 | tf_op jit(solution)/shard_map/ppermute | solution.py:37
  35.3 17.5 %collective-permute-start.1 = (bf16[1,1,1,1,1,64,512]{6,5,4,3,2,1,0:T(8,128)(2,1)S(1)}, bf16[1,1,1,1,1,64,512]{6,5,4,3,2,1,0:T(8,128)(2,1)S(1)}, u32[]{:S(2)}, u32[]{:S(2)}) collective-permute-start(bf16[1,1,1,1,1,64,512]{6,5,4,3,2,1,0:T(8,128)(2,1)S(1)} %constant_dynamic-slice_fusion.7), channel_id=1, source_target_pairs={{0,128},{16,144},{32,160},{48,176},{64,192},{80,208},{96,224},{112... | collective-permute-start | bytes 196616 | tf_op jit(solution)/shard_map/ppermute | solution.py:37
  52.8 10.8 %collective-permute-start.2 = (bf16[1,1,1,1,1,64,512]{6,5,4,3,2,1,0:T(8,128)(2,1)S(1)}, bf16[1,1,1,1,1,64,512]{6,5,4,3,2,1,0:T(8,128)(2,1)S(1)}, u32[]{:S(2)}, u32[]{:S(2)}) collective-permute-start(bf16[1,1,1,1,1,64,512]{6,5,4,3,2,1,0:T(8,128)(2,1)S(1)} %constant_dynamic-slice_fusion.7), channel_id=1, source_target_pairs={{0,192},{16,208},{32,224},{48,240},{64,128},{80,144},{96,160},{112... | collective-permute-start | bytes 196616 | tf_op jit(solution)/shard_map/ppermute | solution.py:37
  63.8 13.8 %collective-permute-start.7 = (bf16[2,2,2,1,1,64,512]{6,5,4,3,2,1,0:T(8,128)(2,1)S(1)}, bf16[2,2,2,1,1,64,512]{6,5,4,3,2,1,0:T(8,128)(2,1)S(1)}, u32[]{:S(2)}, u32[]{:S(2)}) collective-permute-start(bf16[2,2,2,1,1,64,512]{6,5,4,3,2,1,0:T(8,128)(2,1)S(1)} %constant_dynamic-slice_fusion.6), channel_id=1, source_target_pairs={{0,32},{16,48},{32,0},{48,16},{64,96},{80,112},{96,64},{112,80},{1... | collective-permute-start | bytes 1572872 | tf_op jit(solution)/shard_map/ppermute | solution.py:37
  78.7 24.3 %collective-permute-start.8 = (bf16[2,2,2,2,1,64,512]{6,5,4,3,2,1,0:T(8,128)(2,1)}, bf16[2,2,2,2,1,64,512]{6,5,4,3,2,1,0:T(8,128)(2,1)S(1)}, u32[]{:S(2)}, u32[]{:S(2)}) collective-permute-start(bf16[2,2,2,2,1,64,512]{6,5,4,3,2,1,0:T(8,128)(2,1)} %constant_dynamic-slice_fusion.5), channel_id=1, source_target_pairs={{0,16},{16,0},{32,48},{48,32},{64,80},{80,64},{96,112},{112,96},{1... | collective-permute-start | bytes 3145736 | tf_op jit(solution)/shard_map/ppermute | solution.py:37
  103.1 9.2 %collective-permute-start.9 = (bf16[32,64,512]{2,1,0:T(8,128)(2,1)S(1)}, bf16[32,64,512]{2,1,0:T(8,128)(2,1)}, u32[]{:S(2)}, u32[]{:S(2)}) collective-permute-start(bf16[32,64,512]{2,1,0:T(8,128)(2,1)S(1)} %bitcast.129), channel_id=1, source_target_pairs={{0,1},{1,0},{2,3},{3,2},{4,5},{5,4},{6,7},{7,6},{8,9},{9,8},{10,11... | collective-permute-start | bytes 6291464 | tf_op jit(solution)/shard_map/ppermute | solution.py:37
  117.7 19.7 %collective-permute-start.10 = (bf16[1,6,16,2048]{3,2,1,0:T(8,128)(2,1)S(1)}, bf16[1,6,16,2048]{3,2,1,0:T(8,128)(2,1)S(1)}, u32[]{:S(2)}, u32[]{:S(2)}) collective-permute-start(bf16[1,6,16,2048]{3,2,1,0:T(8,128)(2,1)S(1)} %get-tuple-element.15), channel_id=1, source_target_pairs={{0,16},{16,32},{32,48},{48,64},{64,80},{80,96},{96,112},{112,128},... | collective-permute-start | bytes 1179656 | tf_op jit(solution)/shard_map/ppermute | solution.py:27
  120.9 16.5 %collective-permute-start.11 = (bf16[1,6,16,2048]{3,2,1,0:T(8,128)(2,1)S(1)}, bf16[1,6,16,2048]{3,2,1,0:T(8,128)(2,1)S(1)}, u32[]{:S(2)}, u32[]{:S(2)}) collective-permute-start(bf16[1,6,16,2048]{3,2,1,0:T(8,128)(2,1)S(1)} %get-tuple-element.16), channel_id=1, source_target_pairs={{16,0},{32,16},{48,32},{64,48},{80,64},{96,80},{112,96},{128,112},... | collective-permute-start | bytes 1179656 | tf_op jit(solution)/shard_map/ppermute | solution.py:30
  140.6 13.5 %collective-permute-start.13 = (bf16[1,20,6,2048]{3,1,2,0:T(8,128)(2,1)}, bf16[1,20,6,2048]{3,1,2,0:T(8,128)(2,1)}, u32[]{:S(2)}, u32[]{:S(2)}) collective-permute-start(bf16[1,20,6,2048]{3,1,2,0:T(8,128)(2,1)} %copy.35), channel_id=1, source_target_pairs={{1,0},{2,1},{3,2},{4,3},{5,4},{6,5},{7,6},{8,7},{9,8},{10,9},{11,1... | collective-permute-start | bytes 1474568 | tf_op jit(solution)/shard_map/ppermute | solution.py:30
  143.7 16.3 %collective-permute-start.12 = (bf16[1,20,6,2048]{3,1,2,0:T(8,128)(2,1)}, bf16[1,20,6,2048]{3,1,2,0:T(8,128)(2,1)}, u32[]{:S(2)}, u32[]{:S(2)}) collective-permute-start(bf16[1,20,6,2048]{3,1,2,0:T(8,128)(2,1)} %copy.34), channel_id=1, source_target_pairs={{0,1},{1,2},{2,3},{3,4},{4,5},{5,6},{6,7},{7,8},{8,9},{9,10},{10,1... | collective-permute-start | bytes 1474568 | tf_op jit(solution)/shard_map/ppermute | solution.py:27
  203.0 36.1 %collective-permute-start.18 = (f32[1024,512]{1,0:T(8,128)}, f32[1024,512]{1,0:T(8,128)}, u32[]{:S(2)}, u32[]{:S(2)}) collective-permute-start(f32[1024,512]{1,0:T(8,128)} %dynamic-slice_bitcast_fusion), channel_id=1, source_target_pairs={{0,1},{1,0},{2,3},{3,2},{4,5},{5,4},{6,7},{7,6},{8,9},{9,8},{10,11... | collective-permute-start | bytes 6291464 | tf_op jit(solution)/shard_map/ppermute | solution.py:37
  225.8 27.6 %collective-permute-start.14 = (f32[1,20,6,1024]{3,0,2,1:T(1,128)}, f32[1,20,6,1024]{3,0,2,1:T(1,128)}, u32[]{:S(2)}, u32[]{:S(2)}) collective-permute-start(f32[1,20,6,1024]{3,0,2,1:T(1,128)} %get-tuple-element.7), channel_id=1, source_target_pairs={{0,1},{1,2},{2,3},{3,4},{4,5},{5,6},{6,7},{7,8},{8,9},{9,10},{10,1... | collective-permute-start | bytes 1474568 | tf_op jit(solution)/shard_map/ppermute | solution.py:19
  231.7 21.8 %collective-permute-start.15 = (f32[1,20,6,1024]{3,0,2,1:T(1,128)}, f32[1,20,6,1024]{3,0,2,1:T(1,128)}, u32[]{:S(2)}, u32[]{:S(2)}) collective-permute-start(f32[1,20,6,1024]{3,0,2,1:T(1,128)} %get-tuple-element.8), channel_id=1, source_target_pairs={{1,0},{2,1},{3,2},{4,3},{5,4},{6,5},{7,6},{8,7},{9,8},{10,9},{11,1... | collective-permute-start | bytes 1474568 | tf_op jit(solution)/shard_map/ppermute | solution.py:19
  244.1 35.4 %collective-permute-start.19 = (f32[2,2,2,2,1,1,32,512]{7,6,4,3,2,1,0,5:T(8,128)}, f32[2,2,2,2,1,1,32,512]{7,6,4,3,2,1,0,5:T(8,128)}, u32[]{:S(2)}, u32[]{:S(2)}) collective-permute-start(f32[2,2,2,2,1,1,32,512]{7,6,4,3,2,1,0,5:T(8,128)} %constant_dynamic-slice_fusion.4), channel_id=1, source_target_pairs={{0,16},{16,0},{32,48},{48,32},{64,80},{80,64},{96,112},{112,96},{1... | collective-permute-start | bytes 3145736 | tf_op jit(solution)/shard_map/ppermute | solution.py:37
  257.0 29.4 %collective-permute-start.16 = (f32[1,6,16,1024]{3,0,2,1:T(1,128)S(1)}, f32[1,6,16,1024]{3,0,2,1:T(1,128)S(1)}, u32[]{:S(2)}, u32[]{:S(2)}) collective-permute-start(f32[1,6,16,1024]{3,0,2,1:T(1,128)S(1)} %get-tuple-element.9), channel_id=1, source_target_pairs={{0,16},{16,32},{32,48},{48,64},{64,80},{80,96},{96,112},{112,128},... | collective-permute-start | bytes 1179656 | tf_op jit(solution)/shard_map/ppermute | solution.py:19
  258.9 27.5 %collective-permute-start.17 = (f32[1,6,16,1024]{3,0,2,1:T(1,128)S(1)}, f32[1,6,16,1024]{3,0,2,1:T(1,128)S(1)}, u32[]{:S(2)}, u32[]{:S(2)}) collective-permute-start(f32[1,6,16,1024]{3,0,2,1:T(1,128)S(1)} %get-tuple-element.10), channel_id=1, source_target_pairs={{16,0},{32,16},{48,32},{64,48},{80,64},{96,80},{112,96},{128,112},... | collective-permute-start | bytes 1179656 | tf_op jit(solution)/shard_map/ppermute | solution.py:19
  281.0 13.8 %collective-permute-start.20 = (f32[2,2,2,1,1,1,32,512]{7,6,4,3,2,1,0,5:T(8,128)S(1)}, f32[2,2,2,1,1,1,32,512]{7,6,4,3,2,1,0,5:T(8,128)S(1)}, u32[]{:S(2)}, u32[]{:S(2)}) collective-permute-start(f32[2,2,2,1,1,1,32,512]{7,6,4,3,2,1,0,5:T(8,128)S(1)} %constant_dynamic-slice_fusion.3), channel_id=1, source_target_pairs={{0,32},{16,48},{32,0},{48,16},{64,96},{80,112},{96,64},{112,80},{1... | collective-permute-start | bytes 1572872 | tf_op jit(solution)/shard_map/ppermute | solution.py:37
  295.0 11.0 %collective-permute-start.21 = (f32[2,2,1,1,1,1,32,512]{7,6,4,3,2,1,0,5:T(8,128)S(1)}, f32[2,2,1,1,1,1,32,512]{7,6,4,3,2,1,0,5:T(8,128)S(1)}, u32[]{:S(2)}, u32[]{:S(2)}) collective-permute-start(f32[2,2,1,1,1,1,32,512]{7,6,4,3,2,1,0,5:T(8,128)S(1)} %constant_dynamic-slice_fusion.2), channel_id=1, source_target_pairs={{0,64},{16,80},{32,96},{48,112},{64,0},{80,16},{96,32},{112,48},{1... | collective-permute-start | bytes 786440 | tf_op jit(solution)/shard_map/ppermute | solution.py:37
  306.0 15.8 %collective-permute-start.22 = (f32[2,1,1,1,1,1,32,512]{7,6,4,3,2,1,0,5:T(8,128)S(1)}, f32[2,1,1,1,1,1,32,512]{7,6,4,3,2,1,0,5:T(8,128)S(1)}, u32[]{:S(2)}, u32[]{:S(2)}) collective-permute-start(f32[2,1,1,1,1,1,32,512]{7,6,4,3,2,1,0,5:T(8,128)S(1)} %constant_dynamic-slice_fusion.1), channel_id=1, source_target_pairs={{0,128},{16,144},{32,160},{48,176},{64,192},{80,208},{96,224},{112... | collective-permute-start | bytes 393224 | tf_op jit(solution)/shard_map/ppermute | solution.py:37
  321.8 13.7 %collective-permute-start.23 = (f32[1,1,1,1,1,1,32,512]{7,6,4,3,2,1,0,5:T(8,128)S(1)}, f32[1,1,1,1,1,1,32,512]{7,6,4,3,2,1,0,5:T(8,128)S(1)}, u32[]{:S(2)}, u32[]{:S(2)}) collective-permute-start(f32[1,1,1,1,1,1,32,512]{7,6,4,3,2,1,0,5:T(8,128)S(1)} %constant_dynamic-slice_fusion), channel_id=1, source_target_pairs={{0,256},{16,272},{32,288},{48,304},{64,320},{80,336},{96,352},{112... | collective-permute-start | bytes 196616 | tf_op jit(solution)/shard_map/ppermute | solution.py:37
  335.6 35.4 %collective-permute-start.30 = (f32[32,512]{1,0:T(8,128)S(1)}, f32[32,512]{1,0:T(8,128)S(1)}, u32[]{:S(2)}, u32[]{:S(2)}) collective-permute-start(f32[32,512]{1,0:T(8,128)S(1)} %fusion.52), channel_id=1, source_target_pairs={{0,14},{1,15},{2,12},{3,13},{4,10},{5,11},{6,8},{7,9},{8,6},{9,7},... | collective-permute-start | bytes 196616 | tf_op jit(solution)/shard_map/ppermute | solution.py:37
  337.5 33.4 %collective-permute-start.29 = (f32[32,512]{1,0:T(8,128)S(1)}, f32[32,512]{1,0:T(8,128)S(1)}, u32[]{:S(2)}, u32[]{:S(2)}) collective-permute-start(f32[32,512]{1,0:T(8,128)S(1)} %fusion.52), channel_id=1, source_target_pairs={{0,12},{1,13},{2,14},{3,15},{4,8},{5,9},{6,10},{7,11},{8,4},{9,5},... | collective-permute-start | bytes 196616 | tf_op jit(solution)/shard_map/ppermute | solution.py:37
  339.4 31.4 %collective-permute-start.28 = (f32[32,512]{1,0:T(8,128)S(1)}, f32[32,512]{1,0:T(8,128)S(1)}, u32[]{:S(2)}, u32[]{:S(2)}) collective-permute-start(f32[32,512]{1,0:T(8,128)S(1)} %fusion.52), channel_id=1, source_target_pairs={{0,10},{1,11},{2,8},{3,9},{4,14},{5,15},{6,12},{7,13},{8,2},{9,3},... | collective-permute-start | bytes 196616 | tf_op jit(solution)/shard_map/ppermute | solution.py:37
  342.3 28.5 %collective-permute-start.27 = (f32[32,512]{1,0:T(8,128)S(1)}, f32[32,512]{1,0:T(8,128)S(1)}, u32[]{:S(2)}, u32[]{:S(2)}) collective-permute-start(f32[32,512]{1,0:T(8,128)S(1)} %fusion.52), channel_id=1, source_target_pairs={{0,8},{1,9},{2,10},{3,11},{4,12},{5,13},{6,14},{7,15},{8,0},{9,1},... | collective-permute-start | bytes 196616 | tf_op jit(solution)/shard_map/ppermute | solution.py:37
  351.3 6.5 %collective-permute-start.24 = (f32[32,512]{1,0:T(8,128)S(1)}, f32[32,512]{1,0:T(8,128)S(1)}, u32[]{:S(2)}, u32[]{:S(2)}) collective-permute-start(f32[32,512]{1,0:T(8,128)S(1)} %fusion.52), channel_id=1, source_target_pairs={{0,2},{1,3},{2,0},{3,1},{4,6},{5,7},{6,4},{7,5},{8,10},{9,11},{10,... | collective-permute-start | bytes 196616 | tf_op jit(solution)/shard_map/ppermute | solution.py:37
  357.8 5.6 %collective-permute-start.25 = (f32[32,512]{1,0:T(8,128)S(1)}, f32[32,512]{1,0:T(8,128)S(1)}, u32[]{:S(2)}, u32[]{:S(2)}) collective-permute-start(f32[32,512]{1,0:T(8,128)S(1)} %fusion.52), channel_id=1, source_target_pairs={{0,4},{1,5},{2,6},{3,7},{4,0},{5,1},{6,2},{7,3},{8,12},{9,13},{10,... | collective-permute-start | bytes 196616 | tf_op jit(solution)/shard_map/ppermute | solution.py:37
  363.4 7.4 %collective-permute-start.26 = (f32[32,512]{1,0:T(8,128)S(1)}, f32[32,512]{1,0:T(8,128)S(1)}, u32[]{:S(2)}, u32[]{:S(2)}) collective-permute-start(f32[32,512]{1,0:T(8,128)S(1)} %fusion.52), channel_id=1, source_target_pairs={{0,6},{1,7},{2,4},{3,5},{4,2},{5,3},{6,0},{7,1},{8,14},{9,15},{10,... | collective-permute-start | bytes 196616 | tf_op jit(solution)/shard_map/ppermute | solution.py:37
  371.0 15.8 %collective-permute-start.31 = (f32[32,512]{1,0:T(8,128)S(1)}, f32[32,512]{1,0:T(8,128)S(1)}, u32[]{:S(2)}, u32[]{:S(2)}) collective-permute-start(f32[32,512]{1,0:T(8,128)S(1)} %reduce_sum.69), channel_id=1, source_target_pairs={{0,1},{1,0},{2,3},{3,2},{4,5},{5,4},{6,7},{7,6},{8,9},{9,8},{10,11... | collective-permute-start | bytes 196616 | tf_op jit(solution)/shard_map/ppermute | solution.py:37
  (22 other events, 312.5 us)

commit v8 on v6

--- a/solution.py
+++ b/solution.py
@@ -72,12 +72,12 @@
     return held.reshape((-1,) + block.shape)
 
 
-def scatter_by_bits(total, axis, groups):
+def scatter_by_bits(total, axis, groups, narrow=0):
     levels = lax.axis_size(axis).bit_length() - 1
     mine = [axis_bit(axis, bit) for bit in range(levels)]
     held = total.reshape((2,) * levels + (total.shape[0] // 2**levels,) + total.shape[1:])
     rest = [0] * (held.ndim - levels)
-    for group in groups:
+    for step, group in enumerate(groups):
         size = [1 if b in group else held.shape[levels - 1 - b] for b in range(levels)]
         size = size[::-1] + list(held.shape[levels:])
         own = [mine[b] if b in group else 0 for b in range(levels)]
@@ -88,7 +88,9 @@
             for f, b in zip(flip, group):
                 place[b] = (mine[b] + f) % 2
             send = lax.dynamic_slice(held, place[::-1] + rest, size)
-            summed = summed + partner_swap(send, axis, mask)
+            if step < narrow:
+                send = send.astype(jnp.bfloat16)
+            summed = summed + partner_swap(send, axis, mask).astype(summed.dtype)
         held = summed
     return held.reshape(held.shape[levels:])
 
@@ -282,10 +284,12 @@
     own = axis_bit("col", 0)
     halves = partial.reshape(model_width, 2, half)
     pair_part = lax.dynamic_index_in_dim(halves, own, 1, keepdims=False) + partner_swap(
-        lax.dynamic_index_in_dim(halves, 1 - own, 1, keepdims=False), "col", 1
-    )
+        lax.dynamic_index_in_dim(halves, 1 - own, 1, keepdims=False).astype(jnp.bfloat16),
+        "col",
+        1,
+    ).astype(jnp.float32)
     rows_part = scatter_by_bits(
-        pair_part.reshape(row_count, feature_part, half), "row", row_groups
+        pair_part.reshape(row_count, feature_part, half), "row", row_groups, narrow=1
     )[0]
     for bit in range(1, col_levels):
         rows_part = rows_part + partner_swap(rows_part, "col", 1 << bit)

time: 344 us -> 350 us (1.017)
  waiting for transfers between devices: 117 us -> 130 us
  starting transfers between devices: 118 us -> 112 us
    ppermute x16, waiting for transfers between devices: 92.6 us -> 104 us  [partner_swap(): return lax.ppermute(value, axis, [(i, i ^ mask) for i in range(count)])]
    ppermute x16, starting transfers between devices: 94.2 us -> 86.9 us  [partner_swap(): return lax.ppermute(value, axis, [(i, i ^ mask) for i in range(count)])]
    unnamed x51 -> x49, local copies, waits for them, and re-layouts: 11.6 us -> 12.3 us
  transfers between devices with their start and end apart: 24 -> 24, of which waited for: 18 -> 17; matrix products, arithmetic and copies ran while one was open for 14% -> 13% of each run, Pallas kernels for 0% -> 0%
where the time goes in v8:
time: 350 us; the launch traced here: 348 us
  waiting for transfers between devices  130 us (37%)
  starting transfers between devices  112 us (32%)
  local copies, waits for them, and re-layouts  62.6 us (18%)
  matrix products  30 us (9%)
  other arithmetic  12.4 us (4%)
    ppermute x16, waiting for transfers between devices, partner_swap(): return lax.ppermute(value, axis, [(i, i ^ mask) for i in range(count)])  104 us
    ppermute x16, starting transfers between devices, partner_swap(): return lax.ppermute(value, axis, [(i, i ^ mask) for i in range(count)])  86.9 us
    ppermute x2, waiting for transfers between devices, with_halo(): lax.ppermute(lax.slice_in_dim(block, block.shape[dim] - width, None, axis...  17.6 us
    ppermute x4, starting transfers between devices, shifted(): lax.ppermute(value, axis, [(source, source + steps) for source in range(f...  12.6 us
    unnamed x49, local copies, waits for them, and re-layouts  12.3 us
    ppermute x2, starting transfers between devices, with_halo(): lax.ppermute(lax.slice_in_dim(block, block.shape[dim] - width, None, axis...  7.83 us
    concatenate x3, local copies, waits for them, and re-layouts, tile_backward(): jnp.concatenate([key_grad.reshape(batches, ext_count, inner_width), value...  7.46 us
  transfers between devices with their start and end apart: 24, of which 17 were waited for; matrix products, arithmetic and copies ran while one was open for 13% of the time, Pallas kernels for 0%

profile of v8, /device:TPU:1, one launch (start us, length us, event | category | flops | bytes accessed | tf_op | source)
XLA Modules:
  0.0 348.5 jit_solution(5201570049006801098)
XLA Ops:
  2.8 16.3 %collective-permute-start = (bf16[1,1,1,1,1,64,512]{6,5,4,3,2,1,0:T(8,128)(2,1)S(1)}, bf16[1,1,1,1,1,64,512]{6,5,4,3,2,1,0:T(8,128)(2,1)S(1)}, u32[]{:S(2)}, u32[]{:S(2)}) collective-permute-start(bf16[1,1,1,1,1,64,512]{6,5,4,3,2,1,0:T(8,128)(2,1)S(1)} %constant_dynamic-slice_fusion.8), channel_id=1, source_target_pairs={{0,256},{16,272},{32,288},{48,304},{64,320},{80,336},{96,352},{112... | collective-permute-start | bytes 196616 | tf_op jit(solution)/shard_map/ppermute | solution.py:37
  21.0 5.3 %collective-permute-start.1 = (bf16[2,1,1,1,1,64,512]{6,5,4,3,2,1,0:T(8,128)(2,1)S(1)}, bf16[2,1,1,1,1,64,512]{6,5,4,3,2,1,0:T(8,128)(2,1)S(1)}, u32[]{:S(2)}, u32[]{:S(2)}) collective-permute-start(bf16[2,1,1,1,1,64,512]{6,5,4,3,2,1,0:T(8,128)(2,1)S(1)} %constant_dynamic-slice_fusion.7), channel_id=1, source_target_pairs={{0,128},{16,144},{32,160},{48,176},{64,192},{80,208},{96,224},{112... | collective-permute-start | bytes 393224 | tf_op jit(solution)/shard_map/ppermute | solution.py:37
  26.2 13.5 %collective-permute-done.1 = bf16[2,1,1,1,1,64,512]{6,5,4,3,2,1,0:T(8,128)(2,1)S(1)} collective-permute-done((bf16[2,1,1,1,1,64,512]{6,5,4,3,2,1,0:T(8,128)(2,1)S(1)}, bf16[2,1,1,1,1,64,512]{6,5,4,3,2,1,0:T(8,128)(2,1)S(1)}, u32[]{:S(2)}, u32[]{:S(2)}) %collective-permute-start.1) | collective-permute-done | bytes 131104 | tf_op jit(solution)/shard_map/ppermute | solution.py:37
  41.7 13.5 %collective-permute-done.2 = bf16[2,2,1,1,1,64,512]{6,5,4,3,2,1,0:T(8,128)(2,1)S(1)} collective-permute-done((bf16[2,2,1,1,1,64,512]{6,5,4,3,2,1,0:T(8,128)(2,1)S(1)}, bf16[2,2,1,1,1,64,512]{6,5,4,3,2,1,0:T(8,128)(2,1)S(1)}, u32[]{:S(2)}, u32[]{:S(2)}) %collective-permute-start.2) | collective-permute-done | bytes 262176 | tf_op jit(solution)/shard_map/ppermute | solution.py:37
  57.2 13.0 %collective-permute-done.3 = bf16[2,2,2,1,1,64,512]{6,5,4,3,2,1,0:T(8,128)(2,1)S(1)} collective-permute-done((bf16[2,2,2,1,1,64,512]{6,5,4,3,2,1,0:T(8,128)(2,1)S(1)}, bf16[2,2,2,1,1,64,512]{6,5,4,3,2,1,0:T(8,128)(2,1)S(1)}, u32[]{:S(2)}, u32[]{:S(2)}) %collective-permute-start.3) | collective-permute-done | bytes 524320 | tf_op jit(solution)/shard_map/ppermute | solution.py:37
  71.4 3.2 collective-permute-start.4
  74.6 22.2 %collective-permute-done.4 = bf16[2,2,2,2,1,64,512]{6,5,4,3,2,1,0:T(8,128)(2,1)S(1)} collective-permute-done((bf16[2,2,2,2,1,64,512]{6,5,4,3,2,1,0:T(8,128)(2,1)}, bf16[2,2,2,2,1,64,512]{6,5,4,3,2,1,0:T(8,128)(2,1)S(1)}, u32[]{:S(2)}, u32[]{:S(2)}) %collective-permute-start.4) | collective-permute-done | bytes 1048608 | tf_op jit(solution)/shard_map/ppermute | solution.py:37
  96.9 4.2 %collective-permute-start.5 = (bf16[32,64,512]{2,1,0:T(8,128)(2,1)S(1)}, bf16[32,64,512]{2,1,0:T(8,128)(2,1)}, u32[]{:S(2)}, u32[]{:S(2)}) collective-permute-start(bf16[32,64,512]{2,1,0:T(8,128)(2,1)S(1)} %bitcast.114), channel_id=1, source_target_pairs={{0,1},{1,0},{2,3},{3,2},{4,5},{5,4},{6,7},{7,6},{8,9},{9,8},{10,11... | collective-permute-start | bytes 6291464 | tf_op jit(solution)/shard_map/ppermute | solution.py:37
  110.3 3.2 collective-permute-start.6
  117.0 13.0 %collective-permute-done.6 = bf16[1,6,16,2048]{3,2,1,0:T(8,128)(2,1)S(1)} collective-permute-done((bf16[1,6,16,2048]{3,2,1,0:T(8,128)(2,1)S(1)}, bf16[1,6,16,2048]{3,2,1,0:T(8,128)(2,1)S(1)}, u32[]{:S(2)}, u32[]{:S(2)}) %collective-permute-start.6) | collective-permute-done | bytes 393248 | tf_op jit(solution)/shard_map/ppermute | solution.py:27
  133.2 3.1 collective-permute-start.9
  136.3 4.6 %collective-permute-start.8 = (bf16[1,20,6,2048]{3,1,2,0:T(8,128)(2,1)}, bf16[1,20,6,2048]{3,1,2,0:T(8,128)(2,1)}, u32[]{:S(2)}, u32[]{:S(2)}) collective-permute-start(bf16[1,20,6,2048]{3,1,2,0:T(8,128)(2,1)} %copy.36), channel_id=1, source_target_pairs={{0,1},{1,2},{2,3},{3,4},{4,5},{5,6},{6,7},{7,8},{8,9},{9,10},{10,1... | collective-permute-start | bytes 1474568 | tf_op jit(solution)/shard_map/ppermute | solution.py:27
  148.1 4.6 %collective-permute-done.8 = bf16[1,20,6,2048]{3,1,2,0:T(8,128)(2,1)} collective-permute-done((bf16[1,20,6,2048]{3,1,2,0:T(8,128)(2,1)}, bf16[1,20,6,2048]{3,1,2,0:T(8,128)(2,1)}, u32[]{:S(2)}, u32[]{:S(2)}) %collective-permute-start.8) | collective-permute-done | bytes 491552 | tf_op jit(solution)/shard_map/ppermute | solution.py:27
  171.7 3.5 fusion.79
  175.2 3.6 %fusion.80 = (bf16[1,560,8,64]{1,3,2,0:T(8,128)(2,1)}, f32[1,560,8,64]{1,3,2,0:T(8,128)}) fusion(bf16[128,8,64]{0,2,1:T(8,128)(2,1)S(1)} %bitcast.144, f32[8,128]{1,0:T(8,128)S(1)} %get-tuple-element.17, pred[128,560]{0,1:T(8,128)(4,1)S(1)} %copy-done.18, bf16[128,8,64]{0,2,1:T(8,128)(2,1)S(1)} %bitcast.152, bf16[560,8,64]{0,2,1:T(8,128)(2,1)} %bitcast.137), kind=kOutput, calls=%fused_computation.136 | convolution fusion | flops 149956144 | bytes 2631680 | tf_op jit(solution)/shard_map/bhqk,bqhd->bkhd/dot_general | solution.py:183
  178.8 5.9 %fusion.81 = (bf16[1,560,8,64]{1,3,2,0:T(8,128)(2,1)}, f32[1,560,8,64]{1,3,2,0:T(8,128)}) fusion(bf16[128,8,64]{0,2,1:T(8,128)(2,1)S(1)} %bitcast.153, f32[8,128,560]{1,2,0:T(8,128)} %fusion.84, f32[8,128,560]{1,2,0:T(8,128)} %get-tuple-element.18, f32[8,128]{1,0:T(8,128)S(1)} %get-tuple-element.17), kind=kOutput, calls=%fused_computation.137 | convolution fusion | flops 77702704 | bytes 6443008 | tf_op jit(solution)/shard_map/bhqk,bqhd->bkhd/dot_general | solution.py:180
  211.8 3.6 %concatenate.40 = f32[1,20,28,512]{3,0,2,1:T(1,128)} reshape(f32[1,560,8,64]{3,2,0,1:T(8,128)} %copy.45) | data formatting | bytes 2293760 | tf_op jit(solution)/shard_map/concatenate | solution.py:187
  220.8 3.6 %collective-permute-start.15 = (bf16[2,2,2,2,1,1,32,512]{7,6,4,3,2,1,0,5:T(8,128)(2,1)S(1)}, bf16[2,2,2,2,1,1,32,512]{7,6,4,3,2,1,0,5:T(8,128)(2,1)S(1)}, u32[]{:S(2)}, u32[]{:S(2)}) collective-permute-start(bf16[2,2,2,2,1,1,32,512]{7,6,4,3,2,1,0,5:T(8,128)(2,1)S(1)} %dynamic-slice_convert_fusion.1), channel_id=1, source_target_pairs={{0,16},{16,0},{32,48},{48,32},{64,80},{80,64},{96,112},{112,96},{1... | collective-permute-start | bytes 1572872 | tf_op jit(solution)/shard_map/ppermute | solution.py:37
  225.1 6.8 %collective-permute-start.10 = (f32[1,20,6,1024]{3,0,2,1:T(1,128)S(1)}, f32[1,20,6,1024]{3,0,2,1:T(1,128)S(1)}, u32[]{:S(2)}, u32[]{:S(2)}) collective-permute-start(f32[1,20,6,1024]{3,0,2,1:T(1,128)S(1)} %get-tuple-element.7), channel_id=1, source_target_pairs={{0,1},{1,2},{2,3},{3,4},{4,5},{5,6},{6,7},{7,8},{8,9},{9,10},{10,1... | collective-permute-start | bytes 1474568 | tf_op jit(solution)/shard_map/ppermute | solution.py:19
  237.2 4.6 %collective-permute-start.16 = (f32[2,2,2,1,1,1,32,512]{7,6,4,3,2,1,0,5:T(8,128)}, f32[2,2,2,1,1,1,32,512]{7,6,4,3,2,1,0,5:T(8,128)}, u32[]{:S(2)}, u32[]{:S(2)}) collective-permute-start(f32[2,2,2,1,1,1,32,512]{7,6,4,3,2,1,0,5:T(8,128)} %constant_dynamic-slice_fusion.3), channel_id=1, source_target_pairs={{0,32},{16,48},{32,0},{48,16},{64,96},{80,112},{96,64},{112,80},{1... | collective-permute-start | bytes 1572872 | tf_op jit(solution)/shard_map/ppermute | solution.py:37
  241.8 4.9 %collective-permute-done.10 = f32[1,20,6,1024]{3,0,2,1:T(1,128)S(1)} collective-permute-done((f32[1,20,6,1024]{3,0,2,1:T(1,128)S(1)}, f32[1,20,6,1024]{3,0,2,1:T(1,128)S(1)}, u32[]{:S(2)}, u32[]{:S(2)}) %collective-permute-start.10) | collective-permute-done | bytes 491552 | tf_op jit(solution)/shard_map/ppermute | solution.py:19
  254.6 4.7 %fusion.18 = bf16[8,64,128]{2,1,0:T(8,128)(2,1)S(1)} fusion(bf16[560,8,64]{0,2,1:T(8,128)(2,1)} %bitcast.139, f32[8,128,560]{1,2,0:T(8,128)} %fusion.84, f32[8,128,560]{1,2,0:T(8,128)} %get-tuple-element.18, f32[8,128]{1,0:T(8,128)S(1)} %get-tuple-element.17), kind=kOutput, calls=%fused_computation.24 | convolution fusion | flops 77481520 | bytes 5296128 | tf_op jit(solution)/shard_map/bhqk,bkhd->bqhd/dot_general | solution.py:177
  260.6 6.8 %collective-permute-start.17 = (f32[2,2,1,1,1,1,32,512]{7,6,4,3,2,1,0,5:T(8,128)S(1)}, f32[2,2,1,1,1,1,32,512]{7,6,4,3,2,1,0,5:T(8,128)S(1)}, u32[]{:S(2)}, u32[]{:S(2)}) collective-permute-start(f32[2,2,1,1,1,1,32,512]{7,6,4,3,2,1,0,5:T(8,128)S(1)} %constant_dynamic-slice_fusion.2), channel_id=1, source_target_pairs={{0,64},{16,80},{32,96},{48,112},{64,0},{80,16},{96,32},{112,48},{1... | collective-permute-start | bytes 786440 | tf_op jit(solution)/shard_map/ppermute | solution.py:37
  269.4 10.0 %collective-permute-done.17 = f32[2,2,1,1,1,1,32,512]{7,6,4,3,2,1,0,5:T(8,128)S(1)} collective-permute-done((f32[2,2,1,1,1,1,32,512]{7,6,4,3,2,1,0,5:T(8,128)S(1)}, f32[2,2,1,1,1,1,32,512]{7,6,4,3,2,1,0,5:T(8,128)S(1)}, u32[]{:S(2)}, u32[]{:S(2)}) %collective-permute-start.17) | collective-permute-done | bytes 262176 | tf_op jit(solution)/shard_map/ppermute | solution.py:37
  279.4 6.5 %collective-permute-start.18 = (f32[2,1,1,1,1,1,32,512]{7,6,4,3,2,1,0,5:T(8,128)S(1)}, f32[2,1,1,1,1,1,32,512]{7,6,4,3,2,1,0,5:T(8,128)S(1)}, u32[]{:S(2)}, u32[]{:S(2)}) collective-permute-start(f32[2,1,1,1,1,1,32,512]{7,6,4,3,2,1,0,5:T(8,128)S(1)} %constant_dynamic-slice_fusion.1), channel_id=1, source_target_pairs={{0,128},{16,144},{32,160},{48,176},{64,192},{80,208},{96,224},{112... | collective-permute-start | bytes 393224 | tf_op jit(solution)/shard_map/ppermute | solution.py:37
  286.8 11.2 %collective-permute-done.18 = f32[2,1,1,1,1,1,32,512]{7,6,4,3,2,1,0,5:T(8,128)S(1)} collective-permute-done((f32[2,1,1,1,1,1,32,512]{7,6,4,3,2,1,0,5:T(8,128)S(1)}, f32[2,1,1,1,1,1,32,512]{7,6,4,3,2,1,0,5:T(8,128)S(1)}, u32[]{:S(2)}, u32[]{:S(2)}) %collective-permute-start.18) | collective-permute-done | bytes 131104 | tf_op jit(solution)/shard_map/ppermute | solution.py:37
  298.1 9.4 %collective-permute-start.19 = (f32[1,1,1,1,1,1,32,512]{7,6,4,3,2,1,0,5:T(8,128)S(1)}, f32[1,1,1,1,1,1,32,512]{7,6,4,3,2,1,0,5:T(8,128)S(1)}, u32[]{:S(2)}, u32[]{:S(2)}) collective-permute-start(f32[1,1,1,1,1,1,32,512]{7,6,4,3,2,1,0,5:T(8,128)S(1)} %constant_dynamic-slice_fusion), channel_id=1, source_target_pairs={{0,256},{16,272},{32,288},{48,304},{64,320},{80,336},{96,352},{112... | collective-permute-start | bytes 196616 | tf_op jit(solution)/shard_map/ppermute | solution.py:37
  308.1 8.2 %collective-permute-done.19 = f32[1,1,1,1,1,1,32,512]{7,6,4,3,2,1,0,5:T(8,128)S(1)} collective-permute-done((f32[1,1,1,1,1,1,32,512]{7,6,4,3,2,1,0,5:T(8,128)S(1)}, f32[1,1,1,1,1,1,32,512]{7,6,4,3,2,1,0,5:T(8,128)S(1)}, u32[]{:S(2)}, u32[]{:S(2)}) %collective-permute-start.19) | collective-permute-done | bytes 65568 | tf_op jit(solution)/shard_map/ppermute | solution.py:37
  318.5 4.3 %collective-permute-done.20 = f32[32,512]{1,0:T(8,128)S(1)} collective-permute-done((f32[32,512]{1,0:T(8,128)S(1)}, f32[32,512]{1,0:T(8,128)S(1)}, u32[]{:S(2)}, u32[]{:S(2)}) %collective-permute-start.20) | collective-permute-done | bytes 65568 | tf_op jit(solution)/shard_map/ppermute | solution.py:37
  322.8 8.7 %collective-permute-start.21 = (f32[32,512]{1,0:T(8,128)S(1)}, f32[32,512]{1,0:T(8,128)S(1)}, u32[]{:S(2)}, u32[]{:S(2)}) collective-permute-start(f32[32,512]{1,0:T(8,128)S(1)} %add.344), channel_id=1, source_target_pairs={{0,4},{1,5},{2,6},{3,7},{4,0},{5,1},{6,2},{7,3},{8,12},{9,13},{10,... | collective-permute-start | bytes 196616 | tf_op jit(solution)/shard_map/ppermute | solution.py:37
  333.2 4.9 %collective-permute-start.22 = (f32[32,512]{1,0:T(8,128)S(1)}, f32[32,512]{1,0:T(8,128)S(1)}, u32[]{:S(2)}, u32[]{:S(2)}) collective-permute-start(f32[32,512]{1,0:T(8,128)S(1)} %add.345), channel_id=1, source_target_pairs={{0,8},{1,9},{2,10},{3,11},{4,12},{5,13},{6,14},{7,15},{8,0},{9,1},... | collective-permute-start | bytes 196616 | tf_op jit(solution)/shard_map/ppermute | solution.py:37
  339.7 5.6 %collective-permute-start.23 = (f32[32,512]{1,0:T(8,128)S(1)}, f32[32,512]{1,0:T(8,128)S(1)}, u32[]{:S(2)}, u32[]{:S(2)}) collective-permute-start(f32[32,512]{1,0:T(8,128)S(1)} %add.346), channel_id=1, source_target_pairs={{0,1},{1,0},{2,3},{3,2},{4,5},{5,4},{6,7},{7,6},{8,9},{9,8},{10,11... | collective-permute-start | bytes 196616 | tf_op jit(solution)/shard_map/ppermute | solution.py:37
  (163 shorter events, 110.2 us)
Async XLA Ops:
  2.8 18.1 %collective-permute-start = (bf16[1,1,1,1,1,64,512]{6,5,4,3,2,1,0:T(8,128)(2,1)S(1)}, bf16[1,1,1,1,1,64,512]{6,5,4,3,2,1,0:T(8,128)(2,1)S(1)}, u32[]{:S(2)}, u32[]{:S(2)}) collective-permute-start(bf16[1,1,1,1,1,64,512]{6,5,4,3,2,1,0:T(8,128)(2,1)S(1)} %constant_dynamic-slice_fusion.8), channel_id=1, source_target_pairs={{0,256},{16,272},{32,288},{48,304},{64,320},{80,336},{96,352},{112... | collective-permute-start | bytes 196616 | tf_op jit(solution)/shard_map/ppermute | solution.py:37
  21.0 18.7 %collective-permute-start.1 = (bf16[2,1,1,1,1,64,512]{6,5,4,3,2,1,0:T(8,128)(2,1)S(1)}, bf16[2,1,1,1,1,64,512]{6,5,4,3,2,1,0:T(8,128)(2,1)S(1)}, u32[]{:S(2)}, u32[]{:S(2)}) collective-permute-start(bf16[2,1,1,1,1,64,512]{6,5,4,3,2,1,0:T(8,128)(2,1)S(1)} %constant_dynamic-slice_fusion.7), channel_id=1, source_target_pairs={{0,128},{16,144},{32,160},{48,176},{64,192},{80,208},{96,224},{112... | collective-permute-start | bytes 393224 | tf_op jit(solution)/shard_map/ppermute | solution.py:37
  39.8 15.4 %collective-permute-start.2 = (bf16[2,2,1,1,1,64,512]{6,5,4,3,2,1,0:T(8,128)(2,1)S(1)}, bf16[2,2,1,1,1,64,512]{6,5,4,3,2,1,0:T(8,128)(2,1)S(1)}, u32[]{:S(2)}, u32[]{:S(2)}) collective-permute-start(bf16[2,2,1,1,1,64,512]{6,5,4,3,2,1,0:T(8,128)(2,1)S(1)} %constant_dynamic-slice_fusion.6), channel_id=1, source_target_pairs={{0,64},{16,80},{32,96},{48,112},{64,0},{80,16},{96,32},{112,48},{1... | collective-permute-start | bytes 786440 | tf_op jit(solution)/shard_map/ppermute | solution.py:37
  55.3 14.9 %collective-permute-start.3 = (bf16[2,2,2,1,1,64,512]{6,5,4,3,2,1,0:T(8,128)(2,1)S(1)}, bf16[2,2,2,1,1,64,512]{6,5,4,3,2,1,0:T(8,128)(2,1)S(1)}, u32[]{:S(2)}, u32[]{:S(2)}) collective-permute-start(bf16[2,2,2,1,1,64,512]{6,5,4,3,2,1,0:T(8,128)(2,1)S(1)} %constant_dynamic-slice_fusion.5), channel_id=1, source_target_pairs={{0,32},{16,48},{32,0},{48,16},{64,96},{80,112},{96,64},{112,80},{1... | collective-permute-start | bytes 1572872 | tf_op jit(solution)/shard_map/ppermute | solution.py:37
  70.2 30.9 %copy-start.2 = (bf16[1,8,16,1024]{3,2,1,0:T(8,128)(2,1)S(1)}, bf16[1,8,16,1024]{3,2,1,0:T(8,128)(2,1)}, u32[]{:S(2)}) copy-start(bf16[1,8,16,1024]{3,2,1,0:T(8,128)(2,1)} %param.6) | copy-start | bytes 786436
  70.2 31.2 %copy-start.19 = (f32[1024]{0:T(1024)S(1)}, f32[1024]{0:T(1024)}, u32[]{:S(2)}) copy-start(f32[1024]{0:T(1024)} %param.7) | copy-start | bytes 12292
  71.4 25.4 %collective-permute-start.4 = (bf16[2,2,2,2,1,64,512]{6,5,4,3,2,1,0:T(8,128)(2,1)}, bf16[2,2,2,2,1,64,512]{6,5,4,3,2,1,0:T(8,128)(2,1)S(1)}, u32[]{:S(2)}, u32[]{:S(2)}) collective-permute-start(bf16[2,2,2,2,1,64,512]{6,5,4,3,2,1,0:T(8,128)(2,1)} %constant_dynamic-slice_fusion.4), channel_id=1, source_target_pairs={{0,16},{16,0},{32,48},{48,32},{64,80},{80,64},{96,112},{112,96},{1... | collective-permute-start | bytes 3145736 | tf_op jit(solution)/shard_map/ppermute | solution.py:37
  96.9 8.1 %collective-permute-start.5 = (bf16[32,64,512]{2,1,0:T(8,128)(2,1)S(1)}, bf16[32,64,512]{2,1,0:T(8,128)(2,1)}, u32[]{:S(2)}, u32[]{:S(2)}) collective-permute-start(bf16[32,64,512]{2,1,0:T(8,128)(2,1)S(1)} %bitcast.114), channel_id=1, source_target_pairs={{0,1},{1,0},{2,3},{3,2},{4,5},{5,4},{6,7},{7,6},{8,9},{9,8},{10,11... | collective-permute-start | bytes 6291464 | tf_op jit(solution)/shard_map/ppermute | solution.py:37
  110.2 19.8 %copy-start.5 = (bf16[128,1024]{1,0:T(8,128)(2,1)}, bf16[128,1024]{1,0:T(8,128)(2,1)S(1)}, u32[]{:S(2)}) copy-start(bf16[128,1024]{1,0:T(8,128)(2,1)S(1)} %convolution_convert_fusion) | copy-start | bytes 786436
  110.3 19.7 %collective-permute-start.6 = (bf16[1,6,16,2048]{3,2,1,0:T(8,128)(2,1)S(1)}, bf16[1,6,16,2048]{3,2,1,0:T(8,128)(2,1)S(1)}, u32[]{:S(2)}, u32[]{:S(2)}) collective-permute-start(bf16[1,6,16,2048]{3,2,1,0:T(8,128)(2,1)S(1)} %get-tuple-element.15), channel_id=1, source_target_pairs={{0,16},{16,32},{32,48},{48,64},{64,80},{80,96},{96,112},{112,128},... | collective-permute-start | bytes 1179656 | tf_op jit(solution)/shard_map/ppermute | solution.py:27
  113.6 16.5 %collective-permute-start.7 = (bf16[1,6,16,2048]{3,2,1,0:T(8,128)(2,1)S(1)}, bf16[1,6,16,2048]{3,2,1,0:T(8,128)(2,1)S(1)}, u32[]{:S(2)}, u32[]{:S(2)}) collective-permute-start(bf16[1,6,16,2048]{3,2,1,0:T(8,128)(2,1)S(1)} %get-tuple-element.16), channel_id=1, source_target_pairs={{16,0},{32,16},{48,32},{64,48},{80,64},{96,80},{112,96},{128,112},... | collective-permute-start | bytes 1179656 | tf_op jit(solution)/shard_map/ppermute | solution.py:30
  115.9 25.0 %copy-start = (bf16[1,32,32,512]{3,2,1,0:T(8,128)(2,1)}, bf16[1,32,32,512]{3,2,1,0:T(8,128)(2,1)S(1)}, u32[]{:S(2)}) copy-start(bf16[1,32,32,512]{3,2,1,0:T(8,128)(2,1)S(1)} %get-tuple-element.4) | copy-start | bytes 3145732
  133.2 13.5 %collective-permute-start.9 = (bf16[1,20,6,2048]{3,1,2,0:T(8,128)(2,1)}, bf16[1,20,6,2048]{3,1,2,0:T(8,128)(2,1)}, u32[]{:S(2)}, u32[]{:S(2)}) collective-permute-start(bf16[1,20,6,2048]{3,1,2,0:T(8,128)(2,1)} %copy.37), channel_id=1, source_target_pairs={{1,0},{2,1},{3,2},{4,3},{5,4},{6,5},{7,6},{8,7},{9,8},{10,9},{11,1... | collective-permute-start | bytes 1474568 | tf_op jit(solution)/shard_map/ppermute | solution.py:30
  136.3 16.3 %collective-permute-start.8 = (bf16[1,20,6,2048]{3,1,2,0:T(8,128)(2,1)}, bf16[1,20,6,2048]{3,1,2,0:T(8,128)(2,1)}, u32[]{:S(2)}, u32[]{:S(2)}) collective-permute-start(bf16[1,20,6,2048]{3,1,2,0:T(8,128)(2,1)} %copy.36), channel_id=1, source_target_pairs={{0,1},{1,2},{2,3},{3,4},{4,5},{5,6},{6,7},{7,8},{8,9},{9,10},{10,1... | collective-permute-start | bytes 1474568 | tf_op jit(solution)/shard_map/ppermute | solution.py:27
  195.5 23.6 %collective-permute-start.14 = (bf16[1024,512]{1,0:T(8,128)(2,1)}, bf16[1024,512]{1,0:T(8,128)(2,1)}, u32[]{:S(2)}, u32[]{:S(2)}) collective-permute-start(bf16[1024,512]{1,0:T(8,128)(2,1)} %fusion.30), channel_id=1, source_target_pairs={{0,1},{1,0},{2,3},{3,2},{4,5},{5,4},{6,7},{7,6},{8,9},{9,8},{10,11... | collective-permute-start | bytes 3145736 | tf_op jit(solution)/shard_map/ppermute | solution.py:37
  220.7 13.2 %copy-start.3 = (bf16[1,8,16,1024]{3,2,1,0:T(8,128)(2,1)S(1)}, bf16[1,8,16,1024]{3,2,1,0:T(8,128)(2,1)}, u32[]{:S(2)}) copy-start(bf16[1,8,16,1024]{3,2,1,0:T(8,128)(2,1)} %param.6) | copy-start | bytes 786436
  220.7 13.2 %copy-start.7 = (bf16[512,1024,1]{1,0,2:T(8,128)(2,1)S(1)}, bf16[512,1024,1]{1,0,2:T(8,128)(2,1)}, u32[]{:S(2)}) copy-start(bf16[512,1024,1]{1,0,2:T(8,128)(2,1)} %reshape.328) | copy-start | bytes 3145732
  220.8 15.3 %collective-permute-start.15 = (bf16[2,2,2,2,1,1,32,512]{7,6,4,3,2,1,0,5:T(8,128)(2,1)S(1)}, bf16[2,2,2,2,1,1,32,512]{7,6,4,3,2,1,0,5:T(8,128)(2,1)S(1)}, u32[]{:S(2)}, u32[]{:S(2)}) collective-permute-start(bf16[2,2,2,2,1,1,32,512]{7,6,4,3,2,1,0,5:T(8,128)(2,1)S(1)} %dynamic-slice_convert_fusion.1), channel_id=1, source_target_pairs={{0,16},{16,0},{32,48},{48,32},{64,80},{80,64},{96,112},{112,96},{1... | collective-permute-start | bytes 1572872 | tf_op jit(solution)/shard_map/ppermute | solution.py:37
  225.1 21.6 %collective-permute-start.10 = (f32[1,20,6,1024]{3,0,2,1:T(1,128)S(1)}, f32[1,20,6,1024]{3,0,2,1:T(1,128)S(1)}, u32[]{:S(2)}, u32[]{:S(2)}) collective-permute-start(f32[1,20,6,1024]{3,0,2,1:T(1,128)S(1)} %get-tuple-element.7), channel_id=1, source_target_pairs={{0,1},{1,2},{2,3},{3,4},{4,5},{5,6},{6,7},{7,8},{8,9},{9,10},{10,1... | collective-permute-start | bytes 1474568 | tf_op jit(solution)/shard_map/ppermute | solution.py:19
  231.9 14.8 %collective-permute-start.11 = (f32[1,20,6,1024]{3,0,2,1:T(1,128)S(1)}, f32[1,20,6,1024]{3,0,2,1:T(1,128)S(1)}, u32[]{:S(2)}, u32[]{:S(2)}) collective-permute-start(f32[1,20,6,1024]{3,0,2,1:T(1,128)S(1)} %get-tuple-element.8), channel_id=1, source_target_pairs={{1,0},{2,1},{3,2},{4,3},{5,4},{6,5},{7,6},{8,7},{9,8},{10,9},{11,1... | collective-permute-start | bytes 1474568 | tf_op jit(solution)/shard_map/ppermute | solution.py:19
  237.2 22.2 %collective-permute-start.16 = (f32[2,2,2,1,1,1,32,512]{7,6,4,3,2,1,0,5:T(8,128)}, f32[2,2,2,1,1,1,32,512]{7,6,4,3,2,1,0,5:T(8,128)}, u32[]{:S(2)}, u32[]{:S(2)}) collective-permute-start(f32[2,2,2,1,1,1,32,512]{7,6,4,3,2,1,0,5:T(8,128)} %constant_dynamic-slice_fusion.3), channel_id=1, source_target_pairs={{0,32},{16,48},{32,0},{48,16},{64,96},{80,112},{96,64},{112,80},{1... | collective-permute-start | bytes 1572872 | tf_op jit(solution)/shard_map/ppermute | solution.py:37
  250.7 16.7 %collective-permute-start.12 = (f32[1,6,16,1024]{3,0,2,1:T(1,128)}, f32[1,6,16,1024]{3,0,2,1:T(1,128)}, u32[]{:S(2)}, u32[]{:S(2)}) collective-permute-start(f32[1,6,16,1024]{3,0,2,1:T(1,128)} %get-tuple-element.9), channel_id=1, source_target_pairs={{0,16},{16,32},{32,48},{48,64},{64,80},{80,96},{96,112},{112,128},... | collective-permute-start | bytes 1179656 | tf_op jit(solution)/shard_map/ppermute | solution.py:19
  253.3 14.0 %collective-permute-start.13 = (f32[1,6,16,1024]{3,0,2,1:T(1,128)}, f32[1,6,16,1024]{3,0,2,1:T(1,128)}, u32[]{:S(2)}, u32[]{:S(2)}) collective-permute-start(f32[1,6,16,1024]{3,0,2,1:T(1,128)} %get-tuple-element.10), channel_id=1, source_target_pairs={{16,0},{32,16},{48,32},{64,48},{80,64},{96,80},{112,96},{128,112},... | collective-permute-start | bytes 1179656 | tf_op jit(solution)/shard_map/ppermute | solution.py:19
  260.6 18.8 %collective-permute-start.17 = (f32[2,2,1,1,1,1,32,512]{7,6,4,3,2,1,0,5:T(8,128)S(1)}, f32[2,2,1,1,1,1,32,512]{7,6,4,3,2,1,0,5:T(8,128)S(1)}, u32[]{:S(2)}, u32[]{:S(2)}) collective-permute-start(f32[2,2,1,1,1,1,32,512]{7,6,4,3,2,1,0,5:T(8,128)S(1)} %constant_dynamic-slice_fusion.2), channel_id=1, source_target_pairs={{0,64},{16,80},{32,96},{48,112},{64,0},{80,16},{96,32},{112,48},{1... | collective-permute-start | bytes 786440 | tf_op jit(solution)/shard_map/ppermute | solution.py:37
  269.4 38.1 %copy-start.1 = (bf16[1,32,32,512]{3,2,1,0:T(8,128)(2,1)S(1)}, bf16[1,32,32,512]{3,2,1,0:T(8,128)(2,1)}, u32[]{:S(2)}) copy-start(bf16[1,32,32,512]{3,2,1,0:T(8,128)(2,1)} %copy-done) | copy-start | bytes 3145732
  279.4 18.6 %collective-permute-start.18 = (f32[2,1,1,1,1,1,32,512]{7,6,4,3,2,1,0,5:T(8,128)S(1)}, f32[2,1,1,1,1,1,32,512]{7,6,4,3,2,1,0,5:T(8,128)S(1)}, u32[]{:S(2)}, u32[]{:S(2)}) collective-permute-start(f32[2,1,1,1,1,1,32,512]{7,6,4,3,2,1,0,5:T(8,128)S(1)} %constant_dynamic-slice_fusion.1), channel_id=1, source_target_pairs={{0,128},{16,144},{32,160},{48,176},{64,192},{80,208},{96,224},{112... | collective-permute-start | bytes 393224 | tf_op jit(solution)/shard_map/ppermute | solution.py:37
  286.8 58.5 %copy-start.16 = (bf16[1,8,16,1024]{3,2,1,0:T(8,128)(2,1)S(1)}, bf16[1,8,16,1024]{3,2,1,0:T(8,128)(2,1)}, u32[]{:S(2)}) copy-start(bf16[1,8,16,1024]{3,2,1,0:T(8,128)(2,1)} %param.11) | copy-start | bytes 786436
  298.1 18.1 %collective-permute-start.19 = (f32[1,1,1,1,1,1,32,512]{7,6,4,3,2,1,0,5:T(8,128)S(1)}, f32[1,1,1,1,1,1,32,512]{7,6,4,3,2,1,0,5:T(8,128)S(1)}, u32[]{:S(2)}, u32[]{:S(2)}) collective-permute-start(f32[1,1,1,1,1,1,32,512]{7,6,4,3,2,1,0,5:T(8,128)S(1)} %constant_dynamic-slice_fusion), channel_id=1, source_target_pairs={{0,256},{16,272},{32,288},{48,304},{64,320},{80,336},{96,352},{112... | collective-permute-start | bytes 196616 | tf_op jit(solution)/shard_map/ppermute | solution.py:37
  316.3 6.5 %collective-permute-start.20 = (f32[32,512]{1,0:T(8,128)S(1)}, f32[32,512]{1,0:T(8,128)S(1)}, u32[]{:S(2)}, u32[]{:S(2)}) collective-permute-start(f32[32,512]{1,0:T(8,128)S(1)} %add_bitcast_fusion), channel_id=1, source_target_pairs={{0,2},{1,3},{2,0},{3,1},{4,6},{5,7},{6,4},{7,5},{8,10},{9,11},{10,... | collective-permute-start | bytes 196616 | tf_op jit(solution)/shard_map/ppermute | solution.py:37
  322.8 10.3 %collective-permute-start.21 = (f32[32,512]{1,0:T(8,128)S(1)}, f32[32,512]{1,0:T(8,128)S(1)}, u32[]{:S(2)}, u32[]{:S(2)}) collective-permute-start(f32[32,512]{1,0:T(8,128)S(1)} %add.344), channel_id=1, source_target_pairs={{0,4},{1,5},{2,6},{3,7},{4,0},{5,1},{6,2},{7,3},{8,12},{9,13},{10,... | collective-permute-start | bytes 196616 | tf_op jit(solution)/shard_map/ppermute | solution.py:37
  333.2 6.5 %collective-permute-start.22 = (f32[32,512]{1,0:T(8,128)S(1)}, f32[32,512]{1,0:T(8,128)S(1)}, u32[]{:S(2)}, u32[]{:S(2)}) collective-permute-start(f32[32,512]{1,0:T(8,128)S(1)} %add.345), channel_id=1, source_target_pairs={{0,8},{1,9},{2,10},{3,11},{4,12},{5,13},{6,14},{7,15},{8,0},{9,1},... | collective-permute-start | bytes 196616 | tf_op jit(solution)/shard_map/ppermute | solution.py:37
  339.7 7.4 %collective-permute-start.23 = (f32[32,512]{1,0:T(8,128)S(1)}, f32[32,512]{1,0:T(8,128)S(1)}, u32[]{:S(2)}, u32[]{:S(2)}) collective-permute-start(f32[32,512]{1,0:T(8,128)S(1)} %add.346), channel_id=1, source_target_pairs={{0,1},{1,0},{2,3},{3,2},{4,5},{5,4},{6,7},{7,6},{8,9},{9,8},{10,11... | collective-permute-start | bytes 196616 | tf_op jit(solution)/shard_map/ppermute | solution.py:37
  (13 other events, 62.5 us)

commit v9 on v6

--- a/solution.py
+++ b/solution.py
@@ -46,7 +46,7 @@
         yield [(code >> k) % 2 for k in range(len(group))]
 
 
-def gather_by_bits(block, axis, groups):
+def gather_by_bits(block, axis, groups, tie=None, tie_at=2):
     levels = lax.axis_size(axis).bit_length() - 1
     mine = [axis_bit(axis, bit) for bit in range(levels)]
     zero = [0] * block.ndim
@@ -55,10 +55,12 @@
         held, block.reshape((1,) * levels + block.shape), mine[::-1] + zero
     )
     done = set()
-    for group in groups:
+    for step, group in enumerate(groups):
         start = [0 if b in done else mine[b] for b in range(levels)]
         size = [2 if b in done else 1 for b in range(levels)]
         region = lax.dynamic_slice(held, start[::-1] + zero, size[::-1] + list(block.shape))
+        if tie is not None and step == tie_at:
+            region, tie = lax.optimization_barrier((region, tie))
         arrived = []
         for flip in flips(group):
             mask = sum(f << b for f, b in zip(flip, group))
@@ -69,7 +71,8 @@
         for other, place in arrived:
             held = lax.dynamic_update_slice(held, other, place[::-1] + zero)
         done.update(group)
-    return held.reshape((-1,) + block.shape)
+    held = held.reshape((-1,) + block.shape)
+    return held if tie is None else (held, tie)
 
 
 def scatter_by_bits(total, axis, groups):
@@ -93,7 +96,7 @@
     return held.reshape(held.shape[levels:])
 
 
-def gather_weights(w_query, w_keyvalue, w_output, row_groups):
+def gather_weights(w_query, w_keyvalue, w_output, row_groups, tie):
     rows, width = w_query.shape
     kv_pack = w_keyvalue.reshape(rows, 2, width).transpose(1, 0, 2).reshape(2 * rows, width)
     out_rows = w_output.shape[0]
@@ -101,7 +104,7 @@
     qo_pack = jnp.concatenate([w_query, out_pack], axis=0)
     own = axis_bit("col", 0)
     packed = jnp.where(own == 0, kv_pack, qo_pack)
-    fetched = gather_by_bits(packed, "row", row_groups)
+    fetched, tie = gather_by_bits(packed, "row", row_groups, tie=tie)
     held = jnp.zeros((2,) + fetched.shape, fetched.dtype)
     held = lax.dynamic_update_slice(held, fetched[None], (own, 0, 0, 0))
     held = lax.dynamic_update_slice(held, partner_swap(fetched, "col", 1)[None], (1 - own, 0, 0, 0))
@@ -109,7 +112,7 @@
     kv = held[0].reshape(count, 2, rows, width).transpose(0, 2, 1, 3).reshape(count * rows, 2 * width)
     query = held[1, :, :rows].reshape(count * rows, width)
     output = held[1, :, rows:].reshape(count, 2, out_rows, width).transpose(0, 2, 1, 3)
-    return query, kv, output.reshape(count * out_rows, 2 * width)
+    return query, kv, output.reshape(count * out_rows, 2 * width), tie
 
 
 def normalize(inputs, norm_gain):
@@ -226,27 +229,21 @@
     ext_cols = tile_cols + 2 * RADIUS
     standard, spread, normed = normalize(inputs, norm_gain)
     flat_norm = normed.reshape(-1, model_width)
+    normed_ext = with_halo(normed, (("row", 1), ("col", 2)), RADIUS).reshape(-1, model_width)
     row_levels = lax.axis_size("row").bit_length() - 1
     row_groups = [[b] for b in range(row_levels)]
-    full_query, full_keyvalue, full_output = gather_weights(
-        w_query, w_keyvalue, w_output, row_groups[::-1]
+    full_query, full_keyvalue, full_output, normed_ext = gather_weights(
+        w_query, w_keyvalue, w_output, row_groups[::-1], normed_ext
     )
     inner_width = full_query.shape[1]
     queries = jnp.dot(flat_norm, full_query, preferred_element_type=jnp.float32).astype(
         jnp.bfloat16
     )
     queries = queries.reshape(batches, tile_rows * tile_cols, inner_width)
-    keyvalue = jnp.dot(flat_norm, full_keyvalue, preferred_element_type=jnp.float32).astype(
-        jnp.bfloat16
-    )
-    keyvalue = keyvalue.reshape(batches, tile_rows, tile_cols, 2 * inner_width)
-    joined_ext = with_halo(
-        jnp.concatenate([keyvalue, normed], axis=-1), (("row", 1), ("col", 2)), RADIUS
-    )
-    keyvalue_ext = joined_ext[..., : 2 * inner_width].reshape(
+    keyvalue_ext = jnp.dot(normed_ext, full_keyvalue, preferred_element_type=jnp.float32)
+    keyvalue_ext = keyvalue_ext.astype(jnp.bfloat16).reshape(
         batches, ext_rows * ext_cols, 2 * inner_width
     )
-    normed_ext = joined_ext[..., 2 * inner_width :].reshape(-1, model_width)
     allowed = window_mask(
         lax.axis_index("row") * tile_rows,
         lax.axis_index("col") * tile_cols,

time: 344 us -> 310 us (0.901)
  waiting for transfers between devices: 117 us -> 91.7 us
  local copies, waits for them, and re-layouts: 62.6 us -> 58.3 us
  starting transfers between devices: 118 us -> 114 us
    ppermute x2, waiting for transfers between devices: 17.7 us -> 0.01 us  [with_halo(): lax.ppermute(lax.slice_in_dim(block, block.shape[dim] - width, None, axis...]
    ppermute x16, waiting for transfers between devices: 92.6 us -> 84.1 us  [partner_swap(): return lax.ppermute(value, axis, [(i, i ^ mask) for i in range(count)])]
    ppermute x16, starting transfers between devices: 94.2 us -> 87.7 us  [partner_swap(): return lax.ppermute(value, axis, [(i, i ^ mask) for i in range(count)])]
    unnamed x51 -> x37, local copies, waits for them, and re-layouts: 11.6 us -> 6.95 us
  transfers between devices with their start and end apart: 24 -> 24, of which waited for: 18 -> 14; matrix products, arithmetic and copies ran while one was open for 14% -> 14% of each run, Pallas kernels for 0% -> 0%
where the time goes in v9:
time: 310 us; the launch traced here: 309 us
  starting transfers between devices  114 us (37%)
  waiting for transfers between devices  91.7 us (30%)
  local copies, waits for them, and re-layouts  58.3 us (19%)
  matrix products  30.4 us (10%)
  other arithmetic  12.2 us (4%)
    ppermute x16, starting transfers between devices, partner_swap(): return lax.ppermute(value, axis, [(i, i ^ mask) for i in range(count)])  87.7 us
    ppermute x16, waiting for transfers between devices, partner_swap(): return lax.ppermute(value, axis, [(i, i ^ mask) for i in range(count)])  84.1 us
    ppermute x4, starting transfers between devices, shifted(): lax.ppermute(value, axis, [(source, source + steps) for source in range(f...  13.7 us
    ppermute x2, starting transfers between devices, with_halo(): lax.ppermute(lax.slice_in_dim(block, block.shape[dim] - width, None, axis...  9.7 us
    concatenate x3, local copies, waits for them, and re-layouts, tile_backward(): jnp.concatenate([key_grad.reshape(batches, ext_count, inner_width), value...  7.45 us
    unnamed x37, local copies, waits for them, and re-layouts  6.95 us
  transfers between devices with their start and end apart: 24, of which 14 were waited for; matrix products, arithmetic and copies ran while one was open for 14% of the time, Pallas kernels for 0%

profile of v9, /device:TPU:1, one launch (start us, length us, event | category | flops | bytes accessed | tf_op | source)
XLA Modules:
  0.0 308.7 jit_solution(16288481651792368711)
XLA Ops:
  2.8 16.3 %collective-permute-start = (bf16[1,1,1,1,1,64,512]{6,5,4,3,2,1,0:T(8,128)(2,1)S(1)}, bf16[1,1,1,1,1,64,512]{6,5,4,3,2,1,0:T(8,128)(2,1)S(1)}, u32[]{:S(2)}, u32[]{:S(2)}) collective-permute-start(bf16[1,1,1,1,1,64,512]{6,5,4,3,2,1,0:T(8,128)(2,1)S(1)} %constant_dynamic-slice_fusion.9), channel_id=1, source_target_pairs={{0,256},{16,272},{32,288},{48,304},{64,320},{80,336},{96,352},{112... | collective-permute-start | bytes 196616 | tf_op jit(solution)/shard_map/ppermute | solution.py:37
  19.7 3.2 %collective-permute-start.2 = (bf16[1,6,16,1024]{3,2,1,0:T(8,128)(2,1)S(1)}, bf16[1,6,16,1024]{3,2,1,0:T(8,128)(2,1)S(1)}, u32[]{:S(2)}, u32[]{:S(2)}) collective-permute-start(bf16[1,6,16,1024]{3,2,1,0:T(8,128)(2,1)S(1)} %get-tuple-element.17), channel_id=1, source_target_pairs={{0,16},{16,32},{32,48},{48,64},{64,80},{80,96},{96,112},{112,128},... | collective-permute-start | bytes 589832 | tf_op jit(solution)/shard_map/ppermute | solution.py:27
  25.0 6.9 %collective-permute-start.1 = (bf16[2,1,1,1,1,64,512]{6,5,4,3,2,1,0:T(8,128)(2,1)}, bf16[2,1,1,1,1,64,512]{6,5,4,3,2,1,0:T(8,128)(2,1)S(1)}, u32[]{:S(2)}, u32[]{:S(2)}) collective-permute-start(bf16[2,1,1,1,1,64,512]{6,5,4,3,2,1,0:T(8,128)(2,1)} %constant_dynamic-slice_fusion.8), channel_id=1, source_target_pairs={{0,128},{16,144},{32,160},{48,176},{64,192},{80,208},{96,224},{112... | collective-permute-start | bytes 393224 | tf_op jit(solution)/shard_map/ppermute | solution.py:37
  33.0 6.5 %collective-permute-start.4 = (bf16[1,20,6,1024]{3,2,1,0:T(8,128)(2,1)}, bf16[1,20,6,1024]{3,2,1,0:T(8,128)(2,1)S(1)}, u32[]{:S(2)}, u32[]{:S(2)}) collective-permute-start(bf16[1,20,6,1024]{3,2,1,0:T(8,128)(2,1)} %get-tuple-element.15), channel_id=1, source_target_pairs={{0,1},{1,2},{2,3},{3,4},{4,5},{5,6},{6,7},{7,8},{8,9},{9,10},{10,1... | collective-permute-start | bytes 737288 | tf_op jit(solution)/shard_map/ppermute | solution.py:27
  41.4 3.6 %collective-permute-done.1 = bf16[2,1,1,1,1,64,512]{6,5,4,3,2,1,0:T(8,128)(2,1)S(1)} collective-permute-done((bf16[2,1,1,1,1,64,512]{6,5,4,3,2,1,0:T(8,128)(2,1)}, bf16[2,1,1,1,1,64,512]{6,5,4,3,2,1,0:T(8,128)(2,1)S(1)}, u32[]{:S(2)}, u32[]{:S(2)}) %collective-permute-start.1) | collective-permute-done | bytes 131104 | tf_op jit(solution)/shard_map/ppermute | solution.py:37
  45.8 3.9 %collective-permute-done.5 = bf16[1,20,6,1024]{3,2,1,0:T(8,128)(2,1)} collective-permute-done((bf16[1,20,6,1024]{3,2,1,0:T(8,128)(2,1)}, bf16[1,20,6,1024]{3,2,1,0:T(8,128)(2,1)}, u32[]{:S(2)}, u32[]{:S(2)}) %collective-permute-start.5) | collective-permute-done | bytes 245792 | tf_op jit(solution)/shard_map/ppermute | solution.py:30
  54.6 4.7 %collective-permute-start.6 = (bf16[2,2,1,1,1,64,512]{6,5,4,3,2,1,0:T(8,128)(2,1)S(1)}, bf16[2,2,1,1,1,64,512]{6,5,4,3,2,1,0:T(8,128)(2,1)S(1)}, u32[]{:S(2)}, u32[]{:S(2)}) collective-permute-start(bf16[2,2,1,1,1,64,512]{6,5,4,3,2,1,0:T(8,128)(2,1)S(1)} %copy-done.12), channel_id=1, source_target_pairs={{0,64},{16,80},{32,96},{48,112},{64,0},{80,16},{96,32},{112,48},{1... | collective-permute-start | bytes 786440 | tf_op jit(solution)/shard_map/ppermute | solution.py:37
  59.3 8.0 %collective-permute-done.6 = bf16[2,2,1,1,1,64,512]{6,5,4,3,2,1,0:T(8,128)(2,1)S(1)} collective-permute-done((bf16[2,2,1,1,1,64,512]{6,5,4,3,2,1,0:T(8,128)(2,1)S(1)}, bf16[2,2,1,1,1,64,512]{6,5,4,3,2,1,0:T(8,128)(2,1)S(1)}, u32[]{:S(2)}, u32[]{:S(2)}) %collective-permute-start.6) | collective-permute-done | bytes 262176 | tf_op jit(solution)/shard_map/ppermute | solution.py:37
  70.2 13.6 %collective-permute-done.7 = bf16[2,2,2,1,1,64,512]{6,5,4,3,2,1,0:T(8,128)(2,1)S(1)} collective-permute-done((bf16[2,2,2,1,1,64,512]{6,5,4,3,2,1,0:T(8,128)(2,1)}, bf16[2,2,2,1,1,64,512]{6,5,4,3,2,1,0:T(8,128)(2,1)S(1)}, u32[]{:S(2)}, u32[]{:S(2)}) %collective-permute-start.7) | collective-permute-done | bytes 524320 | tf_op jit(solution)/shard_map/ppermute | solution.py:37
  87.0 24.5 %collective-permute-done.8 = bf16[2,2,2,2,1,64,512]{6,5,4,3,2,1,0:T(8,128)(2,1)} collective-permute-done((bf16[2,2,2,2,1,64,512]{6,5,4,3,2,1,0:T(8,128)(2,1)}, bf16[2,2,2,2,1,64,512]{6,5,4,3,2,1,0:T(8,128)(2,1)}, u32[]{:S(2)}, u32[]{:S(2)}) %collective-permute-start.8) | collective-permute-done | bytes 1048608 | tf_op jit(solution)/shard_map/ppermute | solution.py:37
  112.8 3.3 %collective-permute-start.9 = (bf16[32,64,512]{2,1,0:T(8,128)(2,1)S(1)}, bf16[32,64,512]{2,1,0:T(8,128)(2,1)}, u32[]{:S(2)}, u32[]{:S(2)}) collective-permute-start(bf16[32,64,512]{2,1,0:T(8,128)(2,1)S(1)} %bitcast.114), channel_id=1, source_target_pairs={{0,1},{1,0},{2,3},{3,2},{4,5},{5,4},{6,7},{7,6},{8,9},{9,8},{10,11... | collective-permute-start | bytes 6291464 | tf_op jit(solution)/shard_map/ppermute | solution.py:37
  127.8 3.8 %copy.21 = bf16[32,2,32,512]{3,1,2,0:T(2,128)(2,1)S(1)} copy(bf16[32,2,32,512]{3,2,1,0:T(8,128)(2,1)} %bitcast.123) | data formatting | bytes 4194304 | tf_op jit(solution)/shard_map/reshape;squeeze | solution.py:112
  141.0 3.1 %fusion.84 = f32[8,128,560]{1,2,0:T(8,128)} fusion(bf16[128,8,64]{0,2,1:T(8,128)(2,1)S(1)} %bitcast.141, bf16[560,8,64]{0,2,1:T(8,128)(2,1)} %bitcast.129), kind=kOutput, calls=%fused_computation.135 | convolution fusion | flops 73400320 | bytes 2998272 | tf_op jit(solution)/shard_map/bqhd,bkhd->bhqk/dot_general | solution.py:173
  144.1 3.3 %fusion.79 = (f32[8,128]{1,0:T(8,128)S(1)}, f32[8,128,560]{1,2,0:T(8,128)}) fusion(pred[128,560]{0,1:T(8,128)(4,1)} %fusion.49, bf16[128,8,64]{0,2,1:T(8,128)(2,1)} %bitcast.148, bf16[560,8,64]{0,2,1:T(8,128)(2,1)S(1)} %bitcast.135), kind=kOutput, calls=%fused_computation.132 | convolution fusion | flops 75694640 | bytes 3074048 | tf_op jit(solution)/shard_map/sub | solution.py:157
  147.5 3.4 %fusion.80 = (bf16[1,560,8,64]{1,3,2,0:T(8,128)(2,1)}, f32[1,560,8,64]{1,3,2,0:T(8,128)}) fusion(bf16[128,8,64]{0,2,1:T(8,128)(2,1)S(1)} %bitcast.142, f32[8,128]{1,0:T(8,128)S(1)} %get-tuple-element.19, pred[128,560]{0,1:T(8,128)(4,1)} %fusion.49, bf16[128,8,64]{0,2,1:T(8,128)(2,1)S(1)} %bitcast.150, bf16[560,8,64]{0,2,1:T(8,128)(2,1)S(1)} %bitcast.136), kind=kOutput, calls=%fused_computation.133 | convolution fusion | flops 149956144 | bytes 2631680 | tf_op jit(solution)/shard_map/bhqk,bqhd->bkhd/dot_general | solution.py:184
  150.9 5.9 %fusion.81 = (bf16[1,560,8,64]{1,3,2,0:T(8,128)(2,1)}, f32[1,560,8,64]{1,3,2,0:T(8,128)}) fusion(bf16[128,8,64]{0,2,1:T(8,128)(2,1)S(1)} %bitcast.151, f32[8,128,560]{1,2,0:T(8,128)} %fusion.84, f32[8,128,560]{1,2,0:T(8,128)} %get-tuple-element.20, f32[8,128]{1,0:T(8,128)S(1)} %get-tuple-element.19), kind=kOutput, calls=%fused_computation.134 | convolution fusion | flops 77702704 | bytes 6443008 | tf_op jit(solution)/shard_map/bhqk,bqhd->bkhd/dot_general | solution.py:181
  165.2 3.8 %collective-permute-done.14 = f32[1024,512]{1,0:T(8,128)S(1)} collective-permute-done((f32[1024,512]{1,0:T(8,128)S(1)}, f32[1024,512]{1,0:T(8,128)S(1)}, u32[]{:S(2)}, u32[]{:S(2)}) %collective-permute-start.14) | collective-permute-done | bytes 2097184 | tf_op jit(solution)/shard_map/ppermute | solution.py:37
  184.2 3.0 copy.27
  187.3 3.6 %concatenate.36 = f32[1,20,28,512]{3,0,2,1:T(1,128)} reshape(f32[1,560,8,64]{3,2,0,1:T(8,128)} %copy.27) | data formatting | bytes 2293760 | tf_op jit(solution)/shard_map/concatenate | solution.py:188
  195.1 7.5 %collective-permute-start.10 = (f32[1,20,6,1024]{3,0,2,1:T(1,128)S(1)}, f32[1,20,6,1024]{3,0,2,1:T(1,128)S(1)}, u32[]{:S(2)}, u32[]{:S(2)}) collective-permute-start(f32[1,20,6,1024]{3,0,2,1:T(1,128)S(1)} %get-tuple-element.9), channel_id=1, source_target_pairs={{0,1},{1,2},{2,3},{3,4},{4,5},{5,6},{6,7},{7,8},{8,9},{9,10},{10,1... | collective-permute-start | bytes 1474568 | tf_op jit(solution)/shard_map/ppermute | solution.py:19
  210.6 3.6 %collective-permute-done.11 = f32[1,20,6,1024]{3,0,2,1:T(1,128)S(1)} collective-permute-done((f32[1,20,6,1024]{3,0,2,1:T(1,128)S(1)}, f32[1,20,6,1024]{3,0,2,1:T(1,128)S(1)}, u32[]{:S(2)}, u32[]{:S(2)}) %collective-permute-start.11) | collective-permute-done | bytes 491552 | tf_op jit(solution)/shard_map/ppermute | solution.py:19
  221.4 4.6 %fusion.19 = bf16[8,64,128]{2,1,0:T(8,128)(2,1)S(1)} fusion(bf16[560,8,64]{0,2,1:T(8,128)(2,1)S(1)} %bitcast.137, f32[8,128,560]{1,2,0:T(8,128)} %fusion.84, f32[8,128,560]{1,2,0:T(8,128)} %get-tuple-element.20, f32[8,128]{1,0:T(8,128)S(1)} %get-tuple-element.19), kind=kOutput, calls=%fused_computation.24 | convolution fusion | flops 77481520 | bytes 5296128 | tf_op jit(solution)/shard_map/bhqk,bkhd->bqhd/dot_general | solution.py:178
  227.3 5.6 %collective-permute-start.17 = (f32[2,2,1,1,1,1,32,512]{7,6,5,4,3,2,1,0:T(8,128)S(1)}, f32[2,2,1,1,1,1,32,512]{7,6,5,4,3,2,1,0:T(8,128)S(1)}, u32[]{:S(2)}, u32[]{:S(2)}) collective-permute-start(f32[2,2,1,1,1,1,32,512]{7,6,5,4,3,2,1,0:T(8,128)S(1)} %constant_dynamic-slice_fusion.2), channel_id=1, source_target_pairs={{0,64},{16,80},{32,96},{48,112},{64,0},{80,16},{96,32},{112,48},{1... | collective-permute-start | bytes 786440 | tf_op jit(solution)/shard_map/ppermute | solution.py:37
  234.8 6.8 %collective-permute-done.17 = f32[2,2,1,1,1,1,32,512]{7,6,5,4,3,2,1,0:T(8,128)S(1)} collective-permute-done((f32[2,2,1,1,1,1,32,512]{7,6,5,4,3,2,1,0:T(8,128)S(1)}, f32[2,2,1,1,1,1,32,512]{7,6,5,4,3,2,1,0:T(8,128)S(1)}, u32[]{:S(2)}, u32[]{:S(2)}) %collective-permute-start.17) | collective-permute-done | bytes 262176 | tf_op jit(solution)/shard_map/ppermute | solution.py:37
  241.6 4.3 %collective-permute-start.18 = (f32[2,1,1,1,1,1,32,512]{7,6,5,4,3,2,1,0:T(8,128)S(1)}, f32[2,1,1,1,1,1,32,512]{7,6,5,4,3,2,1,0:T(8,128)S(1)}, u32[]{:S(2)}, u32[]{:S(2)}) collective-permute-start(f32[2,1,1,1,1,1,32,512]{7,6,5,4,3,2,1,0:T(8,128)S(1)} %constant_dynamic-slice_fusion.1), channel_id=1, source_target_pairs={{0,128},{16,144},{32,160},{48,176},{64,192},{80,208},{96,224},{112... | collective-permute-start | bytes 393224 | tf_op jit(solution)/shard_map/ppermute | solution.py:37
  246.8 8.0 %collective-permute-done.18 = f32[2,1,1,1,1,1,32,512]{7,6,5,4,3,2,1,0:T(8,128)S(1)} collective-permute-done((f32[2,1,1,1,1,1,32,512]{7,6,5,4,3,2,1,0:T(8,128)S(1)}, f32[2,1,1,1,1,1,32,512]{7,6,5,4,3,2,1,0:T(8,128)S(1)}, u32[]{:S(2)}, u32[]{:S(2)}) %collective-permute-start.18) | collective-permute-done | bytes 131104 | tf_op jit(solution)/shard_map/ppermute | solution.py:37
  254.8 7.8 %collective-permute-start.19 = (f32[1,1,1,1,1,1,32,512]{7,6,5,4,3,2,1,0:T(8,128)S(1)}, f32[1,1,1,1,1,1,32,512]{7,6,5,4,3,2,1,0:T(8,128)S(1)}, u32[]{:S(2)}, u32[]{:S(2)}) collective-permute-start(f32[1,1,1,1,1,1,32,512]{7,6,5,4,3,2,1,0:T(8,128)S(1)} %constant_dynamic-slice_fusion), channel_id=1, source_target_pairs={{0,256},{16,272},{32,288},{48,304},{64,320},{80,336},{96,352},{112... | collective-permute-start | bytes 196616 | tf_op jit(solution)/shard_map/ppermute | solution.py:37
  263.2 9.0 %collective-permute-done.19 = f32[1,1,1,1,1,1,32,512]{7,6,5,4,3,2,1,0:T(8,128)S(1)} collective-permute-done((f32[1,1,1,1,1,1,32,512]{7,6,5,4,3,2,1,0:T(8,128)S(1)}, f32[1,1,1,1,1,1,32,512]{7,6,5,4,3,2,1,0:T(8,128)S(1)}, u32[]{:S(2)}, u32[]{:S(2)}) %collective-permute-start.19) | collective-permute-done | bytes 65568 | tf_op jit(solution)/shard_map/ppermute | solution.py:37
  272.2 13.2 %collective-permute-start.20 = (f32[32,512]{1,0:T(8,128)S(1)}, f32[32,512]{1,0:T(8,128)S(1)}, u32[]{:S(2)}, u32[]{:S(2)}) collective-permute-start(f32[32,512]{1,0:T(8,128)S(1)} %add_bitcast_fusion), channel_id=1, source_target_pairs={{0,2},{1,3},{2,0},{3,1},{4,6},{5,7},{6,4},{7,5},{8,10},{9,11},{10,... | collective-permute-start | bytes 196616 | tf_op jit(solution)/shard_map/ppermute | solution.py:37
  287.4 4.4 %collective-permute-start.21 = (f32[32,512]{1,0:T(8,128)S(1)}, f32[32,512]{1,0:T(8,128)S(1)}, u32[]{:S(2)}, u32[]{:S(2)}) collective-permute-start(f32[32,512]{1,0:T(8,128)S(1)} %add.344), channel_id=1, source_target_pairs={{0,4},{1,5},{2,6},{3,7},{4,0},{5,1},{6,2},{7,3},{8,12},{9,13},{10,... | collective-permute-start | bytes 196616 | tf_op jit(solution)/shard_map/ppermute | solution.py:37
  293.4 4.9 %collective-permute-start.22 = (f32[32,512]{1,0:T(8,128)S(1)}, f32[32,512]{1,0:T(8,128)S(1)}, u32[]{:S(2)}, u32[]{:S(2)}) collective-permute-start(f32[32,512]{1,0:T(8,128)S(1)} %add.345), channel_id=1, source_target_pairs={{0,8},{1,9},{2,10},{3,11},{4,12},{5,13},{6,14},{7,15},{8,0},{9,1},... | collective-permute-start | bytes 196616 | tf_op jit(solution)/shard_map/ppermute | solution.py:37
  300.0 5.6 %collective-permute-start.23 = (f32[32,512]{1,0:T(8,128)S(1)}, f32[32,512]{1,0:T(8,128)S(1)}, u32[]{:S(2)}, u32[]{:S(2)}) collective-permute-start(f32[32,512]{1,0:T(8,128)S(1)} %add.346), channel_id=1, source_target_pairs={{0,1},{1,0},{2,3},{3,2},{4,5},{5,4},{6,7},{7,6},{8,9},{9,8},{10,11... | collective-permute-start | bytes 196616 | tf_op jit(solution)/shard_map/ppermute | solution.py:37
  (147 shorter events, 97.4 us)
Async XLA Ops:
  0.6 18.5 %copy-start = (bf16[1,8,16,1024]{3,2,1,0:T(8,128)(2,1)S(1)}, bf16[1,8,16,1024]{3,2,1,0:T(8,128)(2,1)}, u32[]{:S(2)}) copy-start(bf16[1,8,16,1024]{3,2,1,0:T(8,128)(2,1)} %param.6) | copy-start | bytes 786436
  0.7 18.8 %copy-start.14 = (f32[1024]{0:T(1024)S(1)}, f32[1024]{0:T(1024)}, u32[]{:S(2)}) copy-start(f32[1024]{0:T(1024)} %param.7) | copy-start | bytes 12292
  2.8 21.5 %collective-permute-start = (bf16[1,1,1,1,1,64,512]{6,5,4,3,2,1,0:T(8,128)(2,1)S(1)}, bf16[1,1,1,1,1,64,512]{6,5,4,3,2,1,0:T(8,128)(2,1)S(1)}, u32[]{:S(2)}, u32[]{:S(2)}) collective-permute-start(bf16[1,1,1,1,1,64,512]{6,5,4,3,2,1,0:T(8,128)(2,1)S(1)} %constant_dynamic-slice_fusion.9), channel_id=1, source_target_pairs={{0,256},{16,272},{32,288},{48,304},{64,320},{80,336},{96,352},{112... | collective-permute-start | bytes 196616 | tf_op jit(solution)/shard_map/ppermute | solution.py:37
  19.7 12.1 %collective-permute-start.2 = (bf16[1,6,16,1024]{3,2,1,0:T(8,128)(2,1)S(1)}, bf16[1,6,16,1024]{3,2,1,0:T(8,128)(2,1)S(1)}, u32[]{:S(2)}, u32[]{:S(2)}) collective-permute-start(bf16[1,6,16,1024]{3,2,1,0:T(8,128)(2,1)S(1)} %get-tuple-element.17), channel_id=1, source_target_pairs={{0,16},{16,32},{32,48},{48,64},{64,80},{80,96},{96,112},{112,128},... | collective-permute-start | bytes 589832 | tf_op jit(solution)/shard_map/ppermute | solution.py:27
  23.0 8.9 %collective-permute-start.3 = (bf16[1,6,16,1024]{3,2,1,0:T(8,128)(2,1)S(1)}, bf16[1,6,16,1024]{3,2,1,0:T(8,128)(2,1)S(1)}, u32[]{:S(2)}, u32[]{:S(2)}) collective-permute-start(bf16[1,6,16,1024]{3,2,1,0:T(8,128)(2,1)S(1)} %get-tuple-element.18), channel_id=1, source_target_pairs={{16,0},{32,16},{48,32},{64,48},{80,64},{96,80},{112,96},{128,112},... | collective-permute-start | bytes 589832 | tf_op jit(solution)/shard_map/ppermute | solution.py:30
  25.0 20.0 %collective-permute-start.1 = (bf16[2,1,1,1,1,64,512]{6,5,4,3,2,1,0:T(8,128)(2,1)}, bf16[2,1,1,1,1,64,512]{6,5,4,3,2,1,0:T(8,128)(2,1)S(1)}, u32[]{:S(2)}, u32[]{:S(2)}) collective-permute-start(bf16[2,1,1,1,1,64,512]{6,5,4,3,2,1,0:T(8,128)(2,1)} %constant_dynamic-slice_fusion.8), channel_id=1, source_target_pairs={{0,128},{16,144},{32,160},{48,176},{64,192},{80,208},{96,224},{112... | collective-permute-start | bytes 393224 | tf_op jit(solution)/shard_map/ppermute | solution.py:37
  33.0 12.8 %collective-permute-start.4 = (bf16[1,20,6,1024]{3,2,1,0:T(8,128)(2,1)}, bf16[1,20,6,1024]{3,2,1,0:T(8,128)(2,1)S(1)}, u32[]{:S(2)}, u32[]{:S(2)}) collective-permute-start(bf16[1,20,6,1024]{3,2,1,0:T(8,128)(2,1)} %get-tuple-element.15), channel_id=1, source_target_pairs={{0,1},{1,2},{2,3},{3,4},{4,5},{5,6},{6,7},{7,8},{8,9},{9,10},{10,1... | collective-permute-start | bytes 737288 | tf_op jit(solution)/shard_map/ppermute | solution.py:27
  39.5 10.2 %collective-permute-start.5 = (bf16[1,20,6,1024]{3,2,1,0:T(8,128)(2,1)}, bf16[1,20,6,1024]{3,2,1,0:T(8,128)(2,1)}, u32[]{:S(2)}, u32[]{:S(2)}) collective-permute-start(bf16[1,20,6,1024]{3,2,1,0:T(8,128)(2,1)} %get-tuple-element.16), channel_id=1, source_target_pairs={{1,0},{2,1},{3,2},{4,3},{5,4},{6,5},{7,6},{8,7},{9,8},{10,9},{11,1... | collective-permute-start | bytes 737288 | tf_op jit(solution)/shard_map/ppermute | solution.py:30
  54.6 12.7 %collective-permute-start.6 = (bf16[2,2,1,1,1,64,512]{6,5,4,3,2,1,0:T(8,128)(2,1)S(1)}, bf16[2,2,1,1,1,64,512]{6,5,4,3,2,1,0:T(8,128)(2,1)S(1)}, u32[]{:S(2)}, u32[]{:S(2)}) collective-permute-start(bf16[2,2,1,1,1,64,512]{6,5,4,3,2,1,0:T(8,128)(2,1)S(1)} %copy-done.12), channel_id=1, source_target_pairs={{0,64},{16,80},{32,96},{48,112},{64,0},{80,16},{96,32},{112,48},{1... | collective-permute-start | bytes 786440 | tf_op jit(solution)/shard_map/ppermute | solution.py:37
  68.2 15.5 %collective-permute-start.7 = (bf16[2,2,2,1,1,64,512]{6,5,4,3,2,1,0:T(8,128)(2,1)}, bf16[2,2,2,1,1,64,512]{6,5,4,3,2,1,0:T(8,128)(2,1)S(1)}, u32[]{:S(2)}, u32[]{:S(2)}) collective-permute-start(bf16[2,2,2,1,1,64,512]{6,5,4,3,2,1,0:T(8,128)(2,1)} %constant_dynamic-slice_fusion.6), channel_id=1, source_target_pairs={{0,32},{16,48},{32,0},{48,16},{64,96},{80,112},{96,64},{112,80},{1... | collective-permute-start | bytes 1572872 | tf_op jit(solution)/shard_map/ppermute | solution.py:37
  84.9 26.5 %collective-permute-start.8 = (bf16[2,2,2,2,1,64,512]{6,5,4,3,2,1,0:T(8,128)(2,1)}, bf16[2,2,2,2,1,64,512]{6,5,4,3,2,1,0:T(8,128)(2,1)}, u32[]{:S(2)}, u32[]{:S(2)}) collective-permute-start(bf16[2,2,2,2,1,64,512]{6,5,4,3,2,1,0:T(8,128)(2,1)} %constant_dynamic-slice_fusion.5), channel_id=1, source_target_pairs={{0,16},{16,0},{32,48},{48,32},{64,80},{80,64},{96,112},{112,96},{1... | collective-permute-start | bytes 3145736 | tf_op jit(solution)/shard_map/ppermute | solution.py:37
  112.8 7.0 %collective-permute-start.9 = (bf16[32,64,512]{2,1,0:T(8,128)(2,1)S(1)}, bf16[32,64,512]{2,1,0:T(8,128)(2,1)}, u32[]{:S(2)}, u32[]{:S(2)}) collective-permute-start(bf16[32,64,512]{2,1,0:T(8,128)(2,1)S(1)} %bitcast.114), channel_id=1, source_target_pairs={{0,1},{1,0},{2,3},{3,2},{4,5},{5,4},{6,7},{7,6},{8,9},{9,8},{10,11... | collective-permute-start | bytes 6291464 | tf_op jit(solution)/shard_map/ppermute | solution.py:37
  162.9 6.1 %collective-permute-start.14 = (f32[1024,512]{1,0:T(8,128)S(1)}, f32[1024,512]{1,0:T(8,128)S(1)}, u32[]{:S(2)}, u32[]{:S(2)}) collective-permute-start(f32[1024,512]{1,0:T(8,128)S(1)} %dynamic-slice_bitcast_fusion), channel_id=1, source_target_pairs={{0,1},{1,0},{2,3},{3,2},{4,5},{5,4},{6,7},{7,6},{8,9},{9,8},{10,11... | collective-permute-start | bytes 6291464 | tf_op jit(solution)/shard_map/ppermute | solution.py:37
  171.9 33.6 %collective-permute-start.15 = (f32[2,2,2,2,1,1,32,512]{7,6,5,4,3,2,1,0:T(8,128)}, f32[2,2,2,2,1,1,32,512]{7,6,5,4,3,2,1,0:T(8,128)}, u32[]{:S(2)}, u32[]{:S(2)}) collective-permute-start(f32[2,2,2,2,1,1,32,512]{7,6,5,4,3,2,1,0:T(8,128)} %constant_dynamic-slice_fusion.4), channel_id=1, source_target_pairs={{0,16},{16,0},{32,48},{48,32},{64,80},{80,64},{96,112},{112,96},{1... | collective-permute-start | bytes 3145736 | tf_op jit(solution)/shard_map/ppermute | solution.py:37
  193.4 11.1 %copy-start.11 = (bf16[8,16,512]{2,1,0:T(8,128)(2,1)S(1)}, bf16[8,16,512]{2,1,0:T(8,128)(2,1)}, u32[]{:S(2)}) copy-start(bf16[8,16,512]{2,1,0:T(8,128)(2,1)} %reshape.314) | copy-start | bytes 393220
  194.4 11.1 %copy-start.2 = (f32[1024,512]{1,0:T(8,128)S(1)}, f32[1024,512]{1,0:T(8,128)}, u32[]{:S(2)}) copy-start(f32[1024,512]{1,0:T(8,128)} %copy-done.1) | copy-start | bytes 6291460
  195.1 15.5 %collective-permute-start.10 = (f32[1,20,6,1024]{3,0,2,1:T(1,128)S(1)}, f32[1,20,6,1024]{3,0,2,1:T(1,128)S(1)}, u32[]{:S(2)}, u32[]{:S(2)}) collective-permute-start(f32[1,20,6,1024]{3,0,2,1:T(1,128)S(1)} %get-tuple-element.9), channel_id=1, source_target_pairs={{0,1},{1,2},{2,3},{3,4},{4,5},{5,6},{6,7},{7,8},{8,9},{9,10},{10,1... | collective-permute-start | bytes 1474568 | tf_op jit(solution)/shard_map/ppermute | solution.py:19
  202.5 11.7 %collective-permute-start.11 = (f32[1,20,6,1024]{3,0,2,1:T(1,128)S(1)}, f32[1,20,6,1024]{3,0,2,1:T(1,128)S(1)}, u32[]{:S(2)}, u32[]{:S(2)}) collective-permute-start(f32[1,20,6,1024]{3,0,2,1:T(1,128)S(1)} %get-tuple-element.10), channel_id=1, source_target_pairs={{1,0},{2,1},{3,2},{4,3},{5,4},{6,5},{7,6},{8,7},{9,8},{10,9},{11,1... | collective-permute-start | bytes 1474568 | tf_op jit(solution)/shard_map/ppermute | solution.py:19
  207.0 3.6 %copy-start.5 = (f32[2,2,2,2,1,1,32,512]{7,6,5,4,3,2,1,0:T(8,128)}, f32[2,2,2,2,1,1,32,512]{7,6,5,4,3,2,1,0:T(8,128)S(1)}, u32[]{:S(2)}) copy-start(f32[2,2,2,2,1,1,32,512]{7,6,5,4,3,2,1,0:T(8,128)S(1)} %dynamic-slice_add_fusion) | copy-start | bytes 3145732
  207.9 13.5 %copy-start.10 = (bf16[1,560,512]{1,2,0:T(8,128)(2,1)S(1)}, bf16[1,560,512]{1,2,0:T(8,128)(2,1)}, u32[]{:S(2)}) copy-start(bf16[1,560,512]{1,2,0:T(8,128)(2,1)} %copy.24) | copy-start | bytes 1720324
  207.9 18.0 %collective-permute-start.16 = (f32[2,2,2,1,1,1,32,512]{7,6,5,4,3,2,1,0:T(8,128)}, f32[2,2,2,1,1,1,32,512]{7,6,5,4,3,2,1,0:T(8,128)}, u32[]{:S(2)}, u32[]{:S(2)}) collective-permute-start(f32[2,2,2,1,1,1,32,512]{7,6,5,4,3,2,1,0:T(8,128)} %constant_dynamic-slice_fusion.3), channel_id=1, source_target_pairs={{0,32},{16,48},{32,0},{48,16},{64,96},{80,112},{96,64},{112,80},{1... | collective-permute-start | bytes 1572872 | tf_op jit(solution)/shard_map/ppermute | solution.py:37
  217.1 15.8 %collective-permute-start.12 = (f32[1,6,16,1024]{3,0,2,1:T(1,128)}, f32[1,6,16,1024]{3,0,2,1:T(1,128)}, u32[]{:S(2)}, u32[]{:S(2)}) collective-permute-start(f32[1,6,16,1024]{3,0,2,1:T(1,128)} %get-tuple-element.11), channel_id=1, source_target_pairs={{0,16},{16,32},{32,48},{48,64},{64,80},{80,96},{96,112},{112,128},... | collective-permute-start | bytes 1179656 | tf_op jit(solution)/shard_map/ppermute | solution.py:19
  220.1 12.8 %collective-permute-start.13 = (f32[1,6,16,1024]{3,0,2,1:T(1,128)}, f32[1,6,16,1024]{3,0,2,1:T(1,128)}, u32[]{:S(2)}, u32[]{:S(2)}) collective-permute-start(f32[1,6,16,1024]{3,0,2,1:T(1,128)} %get-tuple-element.12), channel_id=1, source_target_pairs={{16,0},{32,16},{48,32},{64,48},{80,64},{96,80},{112,96},{128,112},... | collective-permute-start | bytes 1179656 | tf_op jit(solution)/shard_map/ppermute | solution.py:19
  227.3 18.6 %copy-start.4 = (bf16[128,8,2,512]{3,1,2,0:T(8,128)(2,1)S(1)}, bf16[128,8,2,512]{3,1,2,0:T(8,128)(2,1)}, u32[]{:S(2)}) copy-start(bf16[128,8,2,512]{3,1,2,0:T(8,128)(2,1)} %copy-done.3) | copy-start | bytes 6291460
  227.3 14.2 %collective-permute-start.17 = (f32[2,2,1,1,1,1,32,512]{7,6,5,4,3,2,1,0:T(8,128)S(1)}, f32[2,2,1,1,1,1,32,512]{7,6,5,4,3,2,1,0:T(8,128)S(1)}, u32[]{:S(2)}, u32[]{:S(2)}) collective-permute-start(f32[2,2,1,1,1,1,32,512]{7,6,5,4,3,2,1,0:T(8,128)S(1)} %constant_dynamic-slice_fusion.2), channel_id=1, source_target_pairs={{0,64},{16,80},{32,96},{48,112},{64,0},{80,16},{96,32},{112,48},{1... | collective-permute-start | bytes 786440 | tf_op jit(solution)/shard_map/ppermute | solution.py:37
  241.6 13.2 %collective-permute-start.18 = (f32[2,1,1,1,1,1,32,512]{7,6,5,4,3,2,1,0:T(8,128)S(1)}, f32[2,1,1,1,1,1,32,512]{7,6,5,4,3,2,1,0:T(8,128)S(1)}, u32[]{:S(2)}, u32[]{:S(2)}) collective-permute-start(f32[2,1,1,1,1,1,32,512]{7,6,5,4,3,2,1,0:T(8,128)S(1)} %constant_dynamic-slice_fusion.1), channel_id=1, source_target_pairs={{0,128},{16,144},{32,160},{48,176},{64,192},{80,208},{96,224},{112... | collective-permute-start | bytes 393224 | tf_op jit(solution)/shard_map/ppermute | solution.py:37
  246.7 58.8 %copy-start.8 = (bf16[1,8,16,1024]{3,2,1,0:T(8,128)(2,1)S(1)}, bf16[1,8,16,1024]{3,2,1,0:T(8,128)(2,1)}, u32[]{:S(2)}) copy-start(bf16[1,8,16,1024]{3,2,1,0:T(8,128)(2,1)} %param.11) | copy-start | bytes 786436
  254.8 17.3 %collective-permute-start.19 = (f32[1,1,1,1,1,1,32,512]{7,6,5,4,3,2,1,0:T(8,128)S(1)}, f32[1,1,1,1,1,1,32,512]{7,6,5,4,3,2,1,0:T(8,128)S(1)}, u32[]{:S(2)}, u32[]{:S(2)}) collective-permute-start(f32[1,1,1,1,1,1,32,512]{7,6,5,4,3,2,1,0:T(8,128)S(1)} %constant_dynamic-slice_fusion), channel_id=1, source_target_pairs={{0,256},{16,272},{32,288},{48,304},{64,320},{80,336},{96,352},{112... | collective-permute-start | bytes 196616 | tf_op jit(solution)/shard_map/ppermute | solution.py:37
  272.2 15.2 %collective-permute-start.20 = (f32[32,512]{1,0:T(8,128)S(1)}, f32[32,512]{1,0:T(8,128)S(1)}, u32[]{:S(2)}, u32[]{:S(2)}) collective-permute-start(f32[32,512]{1,0:T(8,128)S(1)} %add_bitcast_fusion), channel_id=1, source_target_pairs={{0,2},{1,3},{2,0},{3,1},{4,6},{5,7},{6,4},{7,5},{8,10},{9,11},{10,... | collective-permute-start | bytes 196616 | tf_op jit(solution)/shard_map/ppermute | solution.py:37
  287.4 6.0 %collective-permute-start.21 = (f32[32,512]{1,0:T(8,128)S(1)}, f32[32,512]{1,0:T(8,128)S(1)}, u32[]{:S(2)}, u32[]{:S(2)}) collective-permute-start(f32[32,512]{1,0:T(8,128)S(1)} %add.344), channel_id=1, source_target_pairs={{0,4},{1,5},{2,6},{3,7},{4,0},{5,1},{6,2},{7,3},{8,12},{9,13},{10,... | collective-permute-start | bytes 196616 | tf_op jit(solution)/shard_map/ppermute | solution.py:37
  293.4 6.5 %collective-permute-start.22 = (f32[32,512]{1,0:T(8,128)S(1)}, f32[32,512]{1,0:T(8,128)S(1)}, u32[]{:S(2)}, u32[]{:S(2)}) collective-permute-start(f32[32,512]{1,0:T(8,128)S(1)} %add.345), channel_id=1, source_target_pairs={{0,8},{1,9},{2,10},{3,11},{4,12},{5,13},{6,14},{7,15},{8,0},{9,1},... | collective-permute-start | bytes 196616 | tf_op jit(solution)/shard_map/ppermute | solution.py:37
  300.0 7.3 %collective-permute-start.23 = (f32[32,512]{1,0:T(8,128)S(1)}, f32[32,512]{1,0:T(8,128)S(1)}, u32[]{:S(2)}, u32[]{:S(2)}) collective-permute-start(f32[32,512]{1,0:T(8,128)S(1)} %add.346), channel_id=1, source_target_pairs={{0,1},{1,0},{2,3},{3,2},{4,5},{5,4},{6,7},{7,6},{8,9},{9,8},{10,11... | collective-permute-start | bytes 196616 | tf_op jit(solution)/shard_map/ppermute | solution.py:37
  (8 other events, 16.7 us)

commit v10 on v9

--- a/solution.py
+++ b/solution.py
@@ -98,21 +98,21 @@
 
 def gather_weights(w_query, w_keyvalue, w_output, row_groups, tie):
     rows, width = w_query.shape
-    kv_pack = w_keyvalue.reshape(rows, 2, width).transpose(1, 0, 2).reshape(2 * rows, width)
+    kv_rows, kv_width = w_keyvalue.shape
     out_rows = w_output.shape[0]
-    out_pack = w_output.reshape(out_rows, 2, width).transpose(1, 0, 2).reshape(2 * out_rows, width)
-    qo_pack = jnp.concatenate([w_query, out_pack], axis=0)
+    qo_pack = jnp.concatenate([w_query.reshape(-1, kv_width), w_output], axis=0)
     own = axis_bit("col", 0)
-    packed = jnp.where(own == 0, kv_pack, qo_pack)
+    packed = jnp.where(own == 0, w_keyvalue, qo_pack)
     fetched, tie = gather_by_bits(packed, "row", row_groups, tie=tie)
     held = jnp.zeros((2,) + fetched.shape, fetched.dtype)
     held = lax.dynamic_update_slice(held, fetched[None], (own, 0, 0, 0))
     held = lax.dynamic_update_slice(held, partner_swap(fetched, "col", 1)[None], (1 - own, 0, 0, 0))
     count = fetched.shape[0]
-    kv = held[0].reshape(count, 2, rows, width).transpose(0, 2, 1, 3).reshape(count * rows, 2 * width)
-    query = held[1, :, :rows].reshape(count * rows, width)
-    output = held[1, :, rows:].reshape(count, 2, out_rows, width).transpose(0, 2, 1, 3)
-    return query, kv, output.reshape(count * out_rows, 2 * width), tie
+    query_rows = kv_rows - out_rows
+    kv = held[0].reshape(count * kv_rows, kv_width)
+    query = held[1, :, :query_rows].reshape(count * rows, width)
+    output = held[1, :, query_rows:].reshape(count * out_rows, kv_width)
+    return query, kv, output, tie
 
 
 def normalize(inputs, norm_gain):

time: 310 us -> 302 us (0.974)
  local copies, waits for them, and re-layouts: 58.3 us -> 49 us
    unnamed x37 -> x31, local copies, waits for them, and re-layouts: 6.95 us -> 4.77 us
where the time goes in v10:
time: 302 us; the launch traced here: 301 us
  starting transfers between devices  114 us (38%)
  waiting for transfers between devices  91.8 us (30%)
  local copies, waits for them, and re-layouts  49 us (16%)
  matrix products  30 us (10%)
  other arithmetic  13.5 us (4%)
    ppermute x16, starting transfers between devices, partner_swap(): return lax.ppermute(value, axis, [(i, i ^ mask) for i in range(count)])  87.9 us
    ppermute x16, waiting for transfers between devices, partner_swap(): return lax.ppermute(value, axis, [(i, i ^ mask) for i in range(count)])  84 us
    ppermute x4, starting transfers between devices, shifted(): lax.ppermute(value, axis, [(source, source + steps) for source in range(f...  13.6 us
    ppermute x2, starting transfers between devices, with_halo(): lax.ppermute(lax.slice_in_dim(block, block.shape[dim] - width, None, axis...  9.7 us
    concatenate x3, local copies, waits for them, and re-layouts, tile_backward(): jnp.concatenate([key_grad.reshape(batches, ext_count, inner_width), value...  7.45 us
  transfers between devices with their start and end apart: 24, of which 14 were waited for; matrix products, arithmetic and copies ran while one was open for 14% of the time, Pallas kernels for 0%

profile of v10, /device:TPU:1, one launch (start us, length us, event | category | flops | bytes accessed | tf_op | source)
XLA Modules:
  0.0 300.5 jit_solution(5894600486712306432)
XLA Ops:
  2.0 16.3 %collective-permute-start = (bf16[1,1,1,1,1,32,1024]{6,5,4,3,2,1,0:T(8,128)(2,1)S(1)}, bf16[1,1,1,1,1,32,1024]{6,5,4,3,2,1,0:T(8,128)(2,1)S(1)}, u32[]{:S(2)}, u32[]{:S(2)}) collective-permute-start(bf16[1,1,1,1,1,32,1024]{6,5,4,3,2,1,0:T(8,128)(2,1)S(1)} %constant_dynamic-slice_fusion.9), channel_id=1, source_target_pairs={{0,256},{16,272},{32,288},{48,304},{64,320},{80,336},{96,352},{112... | collective-permute-start | bytes 196616 | tf_op jit(solution)/shard_map/ppermute | solution.py:37
  18.9 3.2 %collective-permute-start.2 = (bf16[1,6,16,1024]{3,2,1,0:T(8,128)(2,1)S(1)}, bf16[1,6,16,1024]{3,2,1,0:T(8,128)(2,1)S(1)}, u32[]{:S(2)}, u32[]{:S(2)}) collective-permute-start(bf16[1,6,16,1024]{3,2,1,0:T(8,128)(2,1)S(1)} %get-tuple-element.17), channel_id=1, source_target_pairs={{0,16},{16,32},{32,48},{48,64},{64,80},{80,96},{96,112},{112,128},... | collective-permute-start | bytes 589832 | tf_op jit(solution)/shard_map/ppermute | solution.py:27
  24.1 6.9 %collective-permute-start.1 = (bf16[2,1,1,1,1,32,1024]{6,5,4,3,2,1,0:T(8,128)(2,1)}, bf16[2,1,1,1,1,32,1024]{6,5,4,3,2,1,0:T(8,128)(2,1)S(1)}, u32[]{:S(2)}, u32[]{:S(2)}) collective-permute-start(bf16[2,1,1,1,1,32,1024]{6,5,4,3,2,1,0:T(8,128)(2,1)} %constant_dynamic-slice_fusion.8), channel_id=1, source_target_pairs={{0,128},{16,144},{32,160},{48,176},{64,192},{80,208},{96,224},{112... | collective-permute-start | bytes 393224 | tf_op jit(solution)/shard_map/ppermute | solution.py:37
  32.1 6.5 %collective-permute-start.4 = (bf16[1,20,6,1024]{3,2,1,0:T(8,128)(2,1)}, bf16[1,20,6,1024]{3,2,1,0:T(8,128)(2,1)S(1)}, u32[]{:S(2)}, u32[]{:S(2)}) collective-permute-start(bf16[1,20,6,1024]{3,2,1,0:T(8,128)(2,1)} %get-tuple-element.15), channel_id=1, source_target_pairs={{0,1},{1,2},{2,3},{3,4},{4,5},{5,6},{6,7},{7,8},{8,9},{9,10},{10,1... | collective-permute-start | bytes 737288 | tf_op jit(solution)/shard_map/ppermute | solution.py:27
  40.5 3.6 %collective-permute-done.1 = bf16[2,1,1,1,1,32,1024]{6,5,4,3,2,1,0:T(8,128)(2,1)S(1)} collective-permute-done((bf16[2,1,1,1,1,32,1024]{6,5,4,3,2,1,0:T(8,128)(2,1)}, bf16[2,1,1,1,1,32,1024]{6,5,4,3,2,1,0:T(8,128)(2,1)S(1)}, u32[]{:S(2)}, u32[]{:S(2)}) %collective-permute-start.1) | collective-permute-done | bytes 131104 | tf_op jit(solution)/shard_map/ppermute | solution.py:37
  44.9 3.9 %collective-permute-done.5 = bf16[1,20,6,1024]{3,2,1,0:T(8,128)(2,1)} collective-permute-done((bf16[1,20,6,1024]{3,2,1,0:T(8,128)(2,1)}, bf16[1,20,6,1024]{3,2,1,0:T(8,128)(2,1)}, u32[]{:S(2)}, u32[]{:S(2)}) %collective-permute-start.5) | collective-permute-done | bytes 245792 | tf_op jit(solution)/shard_map/ppermute | solution.py:30
  53.7 4.7 %collective-permute-start.6 = (bf16[2,2,1,1,1,32,1024]{6,5,4,3,2,1,0:T(8,128)(2,1)S(1)}, bf16[2,2,1,1,1,32,1024]{6,5,4,3,2,1,0:T(8,128)(2,1)S(1)}, u32[]{:S(2)}, u32[]{:S(2)}) collective-permute-start(bf16[2,2,1,1,1,32,1024]{6,5,4,3,2,1,0:T(8,128)(2,1)S(1)} %copy-done.10), channel_id=1, source_target_pairs={{0,64},{16,80},{32,96},{48,112},{64,0},{80,16},{96,32},{112,48},{1... | collective-permute-start | bytes 786440 | tf_op jit(solution)/shard_map/ppermute | solution.py:37
  58.4 8.1 %collective-permute-done.6 = bf16[2,2,1,1,1,32,1024]{6,5,4,3,2,1,0:T(8,128)(2,1)S(1)} collective-permute-done((bf16[2,2,1,1,1,32,1024]{6,5,4,3,2,1,0:T(8,128)(2,1)S(1)}, bf16[2,2,1,1,1,32,1024]{6,5,4,3,2,1,0:T(8,128)(2,1)S(1)}, u32[]{:S(2)}, u32[]{:S(2)}) %collective-permute-start.6) | collective-permute-done | bytes 262176 | tf_op jit(solution)/shard_map/ppermute | solution.py:37
  69.3 13.7 %collective-permute-done.7 = bf16[2,2,2,1,1,32,1024]{6,5,4,3,2,1,0:T(8,128)(2,1)S(1)} collective-permute-done((bf16[2,2,2,1,1,32,1024]{6,5,4,3,2,1,0:T(8,128)(2,1)}, bf16[2,2,2,1,1,32,1024]{6,5,4,3,2,1,0:T(8,128)(2,1)S(1)}, u32[]{:S(2)}, u32[]{:S(2)}) %collective-permute-start.7) | collective-permute-done | bytes 524320 | tf_op jit(solution)/shard_map/ppermute | solution.py:37
  86.1 24.6 %collective-permute-done.8 = bf16[2,2,2,2,1,32,1024]{6,5,4,3,2,1,0:T(8,128)(2,1)} collective-permute-done((bf16[2,2,2,2,1,32,1024]{6,5,4,3,2,1,0:T(8,128)(2,1)}, bf16[2,2,2,2,1,32,1024]{6,5,4,3,2,1,0:T(8,128)(2,1)}, u32[]{:S(2)}, u32[]{:S(2)}) %collective-permute-start.8) | collective-permute-done | bytes 1048608 | tf_op jit(solution)/shard_map/ppermute | solution.py:37
  112.0 3.3 %collective-permute-start.9 = (bf16[32,32,1024]{2,1,0:T(8,128)(2,1)S(1)}, bf16[32,32,1024]{2,1,0:T(8,128)(2,1)}, u32[]{:S(2)}, u32[]{:S(2)}) collective-permute-start(bf16[32,32,1024]{2,1,0:T(8,128)(2,1)S(1)} %bitcast.107), channel_id=1, source_target_pairs={{0,1},{1,0},{2,3},{3,2},{4,5},{5,4},{6,7},{7,6},{8,9},{9,8},{10,11... | collective-permute-start | bytes 6291464 | tf_op jit(solution)/shard_map/ppermute | solution.py:37
  125.7 3.3 %fusion.15 = bf16[1,560,1024]{2,1,0:T(8,128)(2,1)S(1)} fusion(bf16[560,1024]{1,0:T(8,128)(2,1)} %reshape.257, bf16[1024,1024]{1,0:T(8,128)(2,1)} %bitcast.113), kind=kOutput, calls=%fused_computation.16 | convolution fusion | flops 1174978560 | bytes 4390912 | tf_op jit(solution)/shard_map/dot_general | solution.py:243
  134.7 3.5 %fusion.80 = (f32[8,128]{1,0:T(8,128)S(1)}, f32[8,128,560]{1,2,0:T(8,128)}) fusion(pred[128,560]{0,1:T(8,128)(4,1)} %fusion.49, bf16[128,8,64]{0,2,1:T(8,128)(2,1)S(1)} %bitcast.133, bf16[560,8,64]{0,2,1:T(8,128)(2,1)} %bitcast.122), kind=kOutput, calls=%fused_computation.133 | convolution fusion | flops 75694640 | bytes 3074048 | tf_op jit(solution)/shard_map/sub | solution.py:157
  138.2 3.7 %fusion.81 = (bf16[1,560,8,64]{1,3,2,0:T(8,128)(2,1)}, f32[1,560,8,64]{1,3,2,0:T(8,128)}) fusion(bf16[128,8,64]{0,2,1:T(8,128)(2,1)S(1)} %bitcast.130, f32[8,128]{1,0:T(8,128)S(1)} %get-tuple-element.19, pred[128,560]{0,1:T(8,128)(4,1)} %fusion.49, bf16[128,8,64]{0,2,1:T(8,128)(2,1)S(1)} %bitcast.134, bf16[560,8,64]{0,2,1:T(8,128)(2,1)} %bitcast.123), kind=kOutput, calls=%fused_computation.134 | convolution fusion | flops 149956144 | bytes 2631680 | tf_op jit(solution)/shard_map/bhqk,bqhd->bkhd/dot_general | solution.py:184
  141.9 5.8 %fusion.82 = (bf16[1,560,8,64]{1,3,2,0:T(8,128)(2,1)}, f32[1,560,8,64]{1,3,2,0:T(8,128)}) fusion(bf16[128,8,64]{0,2,1:T(8,128)(2,1)S(1)} %bitcast.135, f32[8,128,560]{1,2,0:T(8,128)} %fusion.85, f32[8,128,560]{1,2,0:T(8,128)} %get-tuple-element.20, f32[8,128]{1,0:T(8,128)S(1)} %get-tuple-element.19), kind=kOutput, calls=%fused_computation.135 | convolution fusion | flops 77702704 | bytes 6443008 | tf_op jit(solution)/shard_map/bhqk,bqhd->bkhd/dot_general | solution.py:181
  157.9 3.8 %collective-permute-done.14 = f32[1024,512]{1,0:T(8,128)S(1)} collective-permute-done((f32[1024,512]{1,0:T(8,128)S(1)}, f32[1024,512]{1,0:T(8,128)S(1)}, u32[]{:S(2)}, u32[]{:S(2)}) %collective-permute-start.14) | collective-permute-done | bytes 2097184 | tf_op jit(solution)/shard_map/ppermute | solution.py:37
  170.1 3.0 %copy.22 = f32[1,560,8,64]{3,2,0,1:T(8,128)} copy(f32[1,560,8,64]{1,3,2,0:T(8,128)} %get-tuple-element.24) | data formatting | bytes 2293760 | tf_op jit(solution)/shard_map/bhqk,bqhd->bkhd/transpose | solution.py:184
  176.0 3.0 %copy.21 = f32[1,560,8,64]{3,2,0,1:T(8,128)} copy(f32[1,560,8,64]{1,3,2,0:T(8,128)} %get-tuple-element.26) | data formatting | bytes 2293760 | tf_op jit(solution)/shard_map/bhqk,bqhd->bkhd/transpose | solution.py:181
  179.0 3.6 %concatenate.23 = f32[1,20,28,512]{3,0,2,1:T(1,128)} reshape(f32[1,560,8,64]{3,2,0,1:T(8,128)} %copy.21) | data formatting | bytes 2293760 | tf_op jit(solution)/shard_map/concatenate | solution.py:188
  186.8 7.5 %collective-permute-start.10 = (f32[1,20,6,1024]{3,0,2,1:T(1,128)S(1)}, f32[1,20,6,1024]{3,0,2,1:T(1,128)S(1)}, u32[]{:S(2)}, u32[]{:S(2)}) collective-permute-start(f32[1,20,6,1024]{3,0,2,1:T(1,128)S(1)} %get-tuple-element.9), channel_id=1, source_target_pairs={{0,1},{1,2},{2,3},{3,4},{4,5},{5,6},{6,7},{7,8},{8,9},{9,10},{10,1... | collective-permute-start | bytes 1474568 | tf_op jit(solution)/shard_map/ppermute | solution.py:19
  202.0 3.9 %collective-permute-done.11 = f32[1,20,6,1024]{3,0,2,1:T(1,128)S(1)} collective-permute-done((f32[1,20,6,1024]{3,0,2,1:T(1,128)S(1)}, f32[1,20,6,1024]{3,0,2,1:T(1,128)S(1)}, u32[]{:S(2)}, u32[]{:S(2)}) %collective-permute-start.11) | collective-permute-done | bytes 491552 | tf_op jit(solution)/shard_map/ppermute | solution.py:19
  213.1 4.6 %fusion.19 = bf16[8,64,128]{2,1,0:T(8,128)(2,1)S(1)} fusion(bf16[560,8,64]{0,2,1:T(8,128)(2,1)S(1)} %bitcast.125, f32[8,128,560]{1,2,0:T(8,128)} %fusion.85, f32[8,128,560]{1,2,0:T(8,128)} %get-tuple-element.20, f32[8,128]{1,0:T(8,128)S(1)} %get-tuple-element.19), kind=kOutput, calls=%fused_computation.24 | convolution fusion | flops 77481520 | bytes 5296128 | tf_op jit(solution)/shard_map/bhqk,bkhd->bqhd/dot_general | solution.py:178
  219.0 5.6 %collective-permute-start.17 = (f32[2,2,1,1,1,1,32,512]{7,6,5,4,3,2,1,0:T(8,128)S(1)}, f32[2,2,1,1,1,1,32,512]{7,6,5,4,3,2,1,0:T(8,128)S(1)}, u32[]{:S(2)}, u32[]{:S(2)}) collective-permute-start(f32[2,2,1,1,1,1,32,512]{7,6,5,4,3,2,1,0:T(8,128)S(1)} %constant_dynamic-slice_fusion.2), channel_id=1, source_target_pairs={{0,64},{16,80},{32,96},{48,112},{64,0},{80,16},{96,32},{112,48},{1... | collective-permute-start | bytes 786440 | tf_op jit(solution)/shard_map/ppermute | solution.py:37
  226.5 6.8 %collective-permute-done.17 = f32[2,2,1,1,1,1,32,512]{7,6,5,4,3,2,1,0:T(8,128)S(1)} collective-permute-done((f32[2,2,1,1,1,1,32,512]{7,6,5,4,3,2,1,0:T(8,128)S(1)}, f32[2,2,1,1,1,1,32,512]{7,6,5,4,3,2,1,0:T(8,128)S(1)}, u32[]{:S(2)}, u32[]{:S(2)}) %collective-permute-start.17) | collective-permute-done | bytes 262176 | tf_op jit(solution)/shard_map/ppermute | solution.py:37
  233.3 4.5 %collective-permute-start.18 = (f32[2,1,1,1,1,1,32,512]{7,6,5,4,3,2,1,0:T(8,128)S(1)}, f32[2,1,1,1,1,1,32,512]{7,6,5,4,3,2,1,0:T(8,128)S(1)}, u32[]{:S(2)}, u32[]{:S(2)}) collective-permute-start(f32[2,1,1,1,1,1,32,512]{7,6,5,4,3,2,1,0:T(8,128)S(1)} %constant_dynamic-slice_fusion.1), channel_id=1, source_target_pairs={{0,128},{16,144},{32,160},{48,176},{64,192},{80,208},{96,224},{112... | collective-permute-start | bytes 393224 | tf_op jit(solution)/shard_map/ppermute | solution.py:37
  238.7 7.8 %collective-permute-done.18 = f32[2,1,1,1,1,1,32,512]{7,6,5,4,3,2,1,0:T(8,128)S(1)} collective-permute-done((f32[2,1,1,1,1,1,32,512]{7,6,5,4,3,2,1,0:T(8,128)S(1)}, f32[2,1,1,1,1,1,32,512]{7,6,5,4,3,2,1,0:T(8,128)S(1)}, u32[]{:S(2)}, u32[]{:S(2)}) %collective-permute-start.18) | collective-permute-done | bytes 131104 | tf_op jit(solution)/shard_map/ppermute | solution.py:37
  246.6 7.8 %collective-permute-start.19 = (f32[1,1,1,1,1,1,32,512]{7,6,5,4,3,2,1,0:T(8,128)S(1)}, f32[1,1,1,1,1,1,32,512]{7,6,5,4,3,2,1,0:T(8,128)S(1)}, u32[]{:S(2)}, u32[]{:S(2)}) collective-permute-start(f32[1,1,1,1,1,1,32,512]{7,6,5,4,3,2,1,0:T(8,128)S(1)} %constant_dynamic-slice_fusion), channel_id=1, source_target_pairs={{0,256},{16,272},{32,288},{48,304},{64,320},{80,336},{96,352},{112... | collective-permute-start | bytes 196616 | tf_op jit(solution)/shard_map/ppermute | solution.py:37
  254.9 8.9 %collective-permute-done.19 = f32[1,1,1,1,1,1,32,512]{7,6,5,4,3,2,1,0:T(8,128)S(1)} collective-permute-done((f32[1,1,1,1,1,1,32,512]{7,6,5,4,3,2,1,0:T(8,128)S(1)}, f32[1,1,1,1,1,1,32,512]{7,6,5,4,3,2,1,0:T(8,128)S(1)}, u32[]{:S(2)}, u32[]{:S(2)}) %collective-permute-start.19) | collective-permute-done | bytes 65568 | tf_op jit(solution)/shard_map/ppermute | solution.py:37
  263.9 13.0 %collective-permute-start.20 = (f32[32,512]{1,0:T(8,128)S(1)}, f32[32,512]{1,0:T(8,128)S(1)}, u32[]{:S(2)}, u32[]{:S(2)}) collective-permute-start(f32[32,512]{1,0:T(8,128)S(1)} %add_bitcast_fusion), channel_id=1, source_target_pairs={{0,2},{1,3},{2,0},{3,1},{4,6},{5,7},{6,4},{7,5},{8,10},{9,11},{10,... | collective-permute-start | bytes 196616 | tf_op jit(solution)/shard_map/ppermute | solution.py:37
  278.9 4.7 %collective-permute-start.21 = (f32[32,512]{1,0:T(8,128)S(1)}, f32[32,512]{1,0:T(8,128)S(1)}, u32[]{:S(2)}, u32[]{:S(2)}) collective-permute-start(f32[32,512]{1,0:T(8,128)S(1)} %add.344), channel_id=1, source_target_pairs={{0,4},{1,5},{2,6},{3,7},{4,0},{5,1},{6,2},{7,3},{8,12},{9,13},{10,... | collective-permute-start | bytes 196616 | tf_op jit(solution)/shard_map/ppermute | solution.py:37
  285.3 4.9 %collective-permute-start.22 = (f32[32,512]{1,0:T(8,128)S(1)}, f32[32,512]{1,0:T(8,128)S(1)}, u32[]{:S(2)}, u32[]{:S(2)}) collective-permute-start(f32[32,512]{1,0:T(8,128)S(1)} %add.345), channel_id=1, source_target_pairs={{0,8},{1,9},{2,10},{3,11},{4,12},{5,13},{6,14},{7,15},{8,0},{9,1},... | collective-permute-start | bytes 196616 | tf_op jit(solution)/shard_map/ppermute | solution.py:37
  291.8 5.6 %collective-permute-start.23 = (f32[32,512]{1,0:T(8,128)S(1)}, f32[32,512]{1,0:T(8,128)S(1)}, u32[]{:S(2)}, u32[]{:S(2)}) collective-permute-start(f32[32,512]{1,0:T(8,128)S(1)} %add.346), channel_id=1, source_target_pairs={{0,1},{1,0},{2,3},{3,2},{4,5},{5,4},{6,7},{7,6},{8,9},{9,8},{10,11... | collective-permute-start | bytes 196616 | tf_op jit(solution)/shard_map/ppermute | solution.py:37
  (136 shorter events, 88.9 us)
Async XLA Ops:
  0.7 17.6 %copy-start = (bf16[1,8,16,1024]{3,2,1,0:T(8,128)(2,1)S(1)}, bf16[1,8,16,1024]{3,2,1,0:T(8,128)(2,1)}, u32[]{:S(2)}) copy-start(bf16[1,8,16,1024]{3,2,1,0:T(8,128)(2,1)} %param.6) | copy-start | bytes 786436
  0.7 17.9 %copy-start.11 = (f32[1024]{0:T(1024)S(1)}, f32[1024]{0:T(1024)}, u32[]{:S(2)}) copy-start(f32[1024]{0:T(1024)} %param.7) | copy-start | bytes 12292
  2.0 21.5 %collective-permute-start = (bf16[1,1,1,1,1,32,1024]{6,5,4,3,2,1,0:T(8,128)(2,1)S(1)}, bf16[1,1,1,1,1,32,1024]{6,5,4,3,2,1,0:T(8,128)(2,1)S(1)}, u32[]{:S(2)}, u32[]{:S(2)}) collective-permute-start(bf16[1,1,1,1,1,32,1024]{6,5,4,3,2,1,0:T(8,128)(2,1)S(1)} %constant_dynamic-slice_fusion.9), channel_id=1, source_target_pairs={{0,256},{16,272},{32,288},{48,304},{64,320},{80,336},{96,352},{112... | collective-permute-start | bytes 196616 | tf_op jit(solution)/shard_map/ppermute | solution.py:37
  18.9 12.1 %collective-permute-start.2 = (bf16[1,6,16,1024]{3,2,1,0:T(8,128)(2,1)S(1)}, bf16[1,6,16,1024]{3,2,1,0:T(8,128)(2,1)S(1)}, u32[]{:S(2)}, u32[]{:S(2)}) collective-permute-start(bf16[1,6,16,1024]{3,2,1,0:T(8,128)(2,1)S(1)} %get-tuple-element.17), channel_id=1, source_target_pairs={{0,16},{16,32},{32,48},{48,64},{64,80},{80,96},{96,112},{112,128},... | collective-permute-start | bytes 589832 | tf_op jit(solution)/shard_map/ppermute | solution.py:27
  22.1 8.9 %collective-permute-start.3 = (bf16[1,6,16,1024]{3,2,1,0:T(8,128)(2,1)S(1)}, bf16[1,6,16,1024]{3,2,1,0:T(8,128)(2,1)S(1)}, u32[]{:S(2)}, u32[]{:S(2)}) collective-permute-start(bf16[1,6,16,1024]{3,2,1,0:T(8,128)(2,1)S(1)} %get-tuple-element.18), channel_id=1, source_target_pairs={{16,0},{32,16},{48,32},{64,48},{80,64},{96,80},{112,96},{128,112},... | collective-permute-start | bytes 589832 | tf_op jit(solution)/shard_map/ppermute | solution.py:30
  24.1 20.0 %collective-permute-start.1 = (bf16[2,1,1,1,1,32,1024]{6,5,4,3,2,1,0:T(8,128)(2,1)}, bf16[2,1,1,1,1,32,1024]{6,5,4,3,2,1,0:T(8,128)(2,1)S(1)}, u32[]{:S(2)}, u32[]{:S(2)}) collective-permute-start(bf16[2,1,1,1,1,32,1024]{6,5,4,3,2,1,0:T(8,128)(2,1)} %constant_dynamic-slice_fusion.8), channel_id=1, source_target_pairs={{0,128},{16,144},{32,160},{48,176},{64,192},{80,208},{96,224},{112... | collective-permute-start | bytes 393224 | tf_op jit(solution)/shard_map/ppermute | solution.py:37
  32.1 12.8 %collective-permute-start.4 = (bf16[1,20,6,1024]{3,2,1,0:T(8,128)(2,1)}, bf16[1,20,6,1024]{3,2,1,0:T(8,128)(2,1)S(1)}, u32[]{:S(2)}, u32[]{:S(2)}) collective-permute-start(bf16[1,20,6,1024]{3,2,1,0:T(8,128)(2,1)} %get-tuple-element.15), channel_id=1, source_target_pairs={{0,1},{1,2},{2,3},{3,4},{4,5},{5,6},{6,7},{7,8},{8,9},{9,10},{10,1... | collective-permute-start | bytes 737288 | tf_op jit(solution)/shard_map/ppermute | solution.py:27
  38.6 10.2 %collective-permute-start.5 = (bf16[1,20,6,1024]{3,2,1,0:T(8,128)(2,1)}, bf16[1,20,6,1024]{3,2,1,0:T(8,128)(2,1)}, u32[]{:S(2)}, u32[]{:S(2)}) collective-permute-start(bf16[1,20,6,1024]{3,2,1,0:T(8,128)(2,1)} %get-tuple-element.16), channel_id=1, source_target_pairs={{1,0},{2,1},{3,2},{4,3},{5,4},{6,5},{7,6},{8,7},{9,8},{10,9},{11,1... | collective-permute-start | bytes 737288 | tf_op jit(solution)/shard_map/ppermute | solution.py:30
  53.7 12.7 %collective-permute-start.6 = (bf16[2,2,1,1,1,32,1024]{6,5,4,3,2,1,0:T(8,128)(2,1)S(1)}, bf16[2,2,1,1,1,32,1024]{6,5,4,3,2,1,0:T(8,128)(2,1)S(1)}, u32[]{:S(2)}, u32[]{:S(2)}) collective-permute-start(bf16[2,2,1,1,1,32,1024]{6,5,4,3,2,1,0:T(8,128)(2,1)S(1)} %copy-done.10), channel_id=1, source_target_pairs={{0,64},{16,80},{32,96},{48,112},{64,0},{80,16},{96,32},{112,48},{1... | collective-permute-start | bytes 786440 | tf_op jit(solution)/shard_map/ppermute | solution.py:37
  67.4 15.6 %collective-permute-start.7 = (bf16[2,2,2,1,1,32,1024]{6,5,4,3,2,1,0:T(8,128)(2,1)}, bf16[2,2,2,1,1,32,1024]{6,5,4,3,2,1,0:T(8,128)(2,1)S(1)}, u32[]{:S(2)}, u32[]{:S(2)}) collective-permute-start(bf16[2,2,2,1,1,32,1024]{6,5,4,3,2,1,0:T(8,128)(2,1)} %constant_dynamic-slice_fusion.6), channel_id=1, source_target_pairs={{0,32},{16,48},{32,0},{48,16},{64,96},{80,112},{96,64},{112,80},{1... | collective-permute-start | bytes 1572872 | tf_op jit(solution)/shard_map/ppermute | solution.py:37
  84.1 26.5 %collective-permute-start.8 = (bf16[2,2,2,2,1,32,1024]{6,5,4,3,2,1,0:T(8,128)(2,1)}, bf16[2,2,2,2,1,32,1024]{6,5,4,3,2,1,0:T(8,128)(2,1)}, u32[]{:S(2)}, u32[]{:S(2)}) collective-permute-start(bf16[2,2,2,2,1,32,1024]{6,5,4,3,2,1,0:T(8,128)(2,1)} %constant_dynamic-slice_fusion.5), channel_id=1, source_target_pairs={{0,16},{16,0},{32,48},{48,32},{64,80},{80,64},{96,112},{112,96},{1... | collective-permute-start | bytes 3145736 | tf_op jit(solution)/shard_map/ppermute | solution.py:37
  112.0 7.0 %collective-permute-start.9 = (bf16[32,32,1024]{2,1,0:T(8,128)(2,1)S(1)}, bf16[32,32,1024]{2,1,0:T(8,128)(2,1)}, u32[]{:S(2)}, u32[]{:S(2)}) collective-permute-start(bf16[32,32,1024]{2,1,0:T(8,128)(2,1)S(1)} %bitcast.107), channel_id=1, source_target_pairs={{0,1},{1,0},{2,3},{3,2},{4,5},{5,4},{6,7},{7,6},{8,9},{9,8},{10,11... | collective-permute-start | bytes 6291464 | tf_op jit(solution)/shard_map/ppermute | solution.py:37
  129.0 3.4 %copy-start.6 = (bf16[1,8,16,1024]{3,2,1,0:T(8,128)(2,1)S(1)}, bf16[1,8,16,1024]{3,2,1,0:T(8,128)(2,1)}, u32[]{:S(2)}) copy-start(bf16[1,8,16,1024]{3,2,1,0:T(8,128)(2,1)} %param.11) | copy-start | bytes 786436
  155.6 6.1 %collective-permute-start.14 = (f32[1024,512]{1,0:T(8,128)S(1)}, f32[1024,512]{1,0:T(8,128)S(1)}, u32[]{:S(2)}, u32[]{:S(2)}) collective-permute-start(f32[1024,512]{1,0:T(8,128)S(1)} %dynamic-slice_bitcast_fusion), channel_id=1, source_target_pairs={{0,1},{1,0},{2,3},{3,2},{4,5},{5,4},{6,7},{7,6},{8,9},{9,8},{10,11... | collective-permute-start | bytes 6291464 | tf_op jit(solution)/shard_map/ppermute | solution.py:37
  164.5 32.7 %collective-permute-start.15 = (f32[2,2,2,2,1,1,32,512]{7,6,5,4,3,2,1,0:T(8,128)}, f32[2,2,2,2,1,1,32,512]{7,6,5,4,3,2,1,0:T(8,128)}, u32[]{:S(2)}, u32[]{:S(2)}) collective-permute-start(f32[2,2,2,2,1,1,32,512]{7,6,5,4,3,2,1,0:T(8,128)} %constant_dynamic-slice_fusion.4), channel_id=1, source_target_pairs={{0,16},{16,0},{32,48},{48,32},{64,80},{80,64},{96,112},{112,96},{1... | collective-permute-start | bytes 3145736 | tf_op jit(solution)/shard_map/ppermute | solution.py:37
  185.1 11.1 %copy-start.9 = (bf16[8,16,512]{2,1,0:T(8,128)(2,1)S(1)}, bf16[8,16,512]{2,1,0:T(8,128)(2,1)}, u32[]{:S(2)}) copy-start(bf16[8,16,512]{2,1,0:T(8,128)(2,1)} %reshape.264) | copy-start | bytes 393220
  186.1 11.1 %copy-start.2 = (f32[1024,512]{1,0:T(8,128)S(1)}, f32[1024,512]{1,0:T(8,128)}, u32[]{:S(2)}) copy-start(f32[1024,512]{1,0:T(8,128)} %copy-done.1) | copy-start | bytes 6291460
  186.8 15.2 %collective-permute-start.10 = (f32[1,20,6,1024]{3,0,2,1:T(1,128)S(1)}, f32[1,20,6,1024]{3,0,2,1:T(1,128)S(1)}, u32[]{:S(2)}, u32[]{:S(2)}) collective-permute-start(f32[1,20,6,1024]{3,0,2,1:T(1,128)S(1)} %get-tuple-element.9), channel_id=1, source_target_pairs={{0,1},{1,2},{2,3},{3,4},{4,5},{5,6},{6,7},{7,8},{8,9},{9,10},{10,1... | collective-permute-start | bytes 1474568 | tf_op jit(solution)/shard_map/ppermute | solution.py:19
  194.3 11.7 %collective-permute-start.11 = (f32[1,20,6,1024]{3,0,2,1:T(1,128)S(1)}, f32[1,20,6,1024]{3,0,2,1:T(1,128)S(1)}, u32[]{:S(2)}, u32[]{:S(2)}) collective-permute-start(f32[1,20,6,1024]{3,0,2,1:T(1,128)S(1)} %get-tuple-element.10), channel_id=1, source_target_pairs={{1,0},{2,1},{3,2},{4,3},{5,4},{6,5},{7,6},{8,7},{9,8},{10,9},{11,1... | collective-permute-start | bytes 1474568 | tf_op jit(solution)/shard_map/ppermute | solution.py:19
  199.7 13.4 %copy-start.8 = (bf16[1,560,512]{1,2,0:T(8,128)(2,1)S(1)}, bf16[1,560,512]{1,2,0:T(8,128)(2,1)}, u32[]{:S(2)}) copy-start(bf16[1,560,512]{1,2,0:T(8,128)(2,1)} %copy.19) | copy-start | bytes 1720324
  199.7 18.0 %collective-permute-start.16 = (f32[2,2,2,1,1,1,32,512]{7,6,5,4,3,2,1,0:T(8,128)}, f32[2,2,2,1,1,1,32,512]{7,6,5,4,3,2,1,0:T(8,128)}, u32[]{:S(2)}, u32[]{:S(2)}) collective-permute-start(f32[2,2,2,1,1,1,32,512]{7,6,5,4,3,2,1,0:T(8,128)} %constant_dynamic-slice_fusion.3), channel_id=1, source_target_pairs={{0,32},{16,48},{32,0},{48,16},{64,96},{80,112},{96,64},{112,80},{1... | collective-permute-start | bytes 1572872 | tf_op jit(solution)/shard_map/ppermute | solution.py:37
  208.8 15.8 %collective-permute-start.12 = (f32[1,6,16,1024]{3,0,2,1:T(1,128)}, f32[1,6,16,1024]{3,0,2,1:T(1,128)}, u32[]{:S(2)}, u32[]{:S(2)}) collective-permute-start(f32[1,6,16,1024]{3,0,2,1:T(1,128)} %get-tuple-element.11), channel_id=1, source_target_pairs={{0,16},{16,32},{32,48},{48,64},{64,80},{80,96},{96,112},{112,128},... | collective-permute-start | bytes 1179656 | tf_op jit(solution)/shard_map/ppermute | solution.py:19
  211.8 12.9 %collective-permute-start.13 = (f32[1,6,16,1024]{3,0,2,1:T(1,128)}, f32[1,6,16,1024]{3,0,2,1:T(1,128)}, u32[]{:S(2)}, u32[]{:S(2)}) collective-permute-start(f32[1,6,16,1024]{3,0,2,1:T(1,128)} %get-tuple-element.12), channel_id=1, source_target_pairs={{16,0},{32,16},{48,32},{64,48},{80,64},{96,80},{112,96},{128,112},... | collective-permute-start | bytes 1179656 | tf_op jit(solution)/shard_map/ppermute | solution.py:19
  219.0 18.9 %copy-start.3 = (bf16[1,32,32,1024]{3,2,1,0:T(8,128)(2,1)S(1)}, bf16[1,32,32,1024]{3,2,1,0:T(8,128)(2,1)}, u32[]{:S(2)}) copy-start(bf16[1,32,32,1024]{3,2,1,0:T(8,128)(2,1)} %slice.66) | copy-start | bytes 6291460
  219.0 14.3 %collective-permute-start.17 = (f32[2,2,1,1,1,1,32,512]{7,6,5,4,3,2,1,0:T(8,128)S(1)}, f32[2,2,1,1,1,1,32,512]{7,6,5,4,3,2,1,0:T(8,128)S(1)}, u32[]{:S(2)}, u32[]{:S(2)}) collective-permute-start(f32[2,2,1,1,1,1,32,512]{7,6,5,4,3,2,1,0:T(8,128)S(1)} %constant_dynamic-slice_fusion.2), channel_id=1, source_target_pairs={{0,64},{16,80},{32,96},{48,112},{64,0},{80,16},{96,32},{112,48},{1... | collective-permute-start | bytes 786440 | tf_op jit(solution)/shard_map/ppermute | solution.py:37
  233.3 13.2 %collective-permute-start.18 = (f32[2,1,1,1,1,1,32,512]{7,6,5,4,3,2,1,0:T(8,128)S(1)}, f32[2,1,1,1,1,1,32,512]{7,6,5,4,3,2,1,0:T(8,128)S(1)}, u32[]{:S(2)}, u32[]{:S(2)}) collective-permute-start(f32[2,1,1,1,1,1,32,512]{7,6,5,4,3,2,1,0:T(8,128)S(1)} %constant_dynamic-slice_fusion.1), channel_id=1, source_target_pairs={{0,128},{16,144},{32,160},{48,176},{64,192},{80,208},{96,224},{112... | collective-permute-start | bytes 393224 | tf_op jit(solution)/shard_map/ppermute | solution.py:37
  238.7 58.7 %copy-start.7 = (bf16[1,8,16,1024]{3,2,1,0:T(8,128)(2,1)S(1)}, bf16[1,8,16,1024]{3,2,1,0:T(8,128)(2,1)}, u32[]{:S(2)}) copy-start(bf16[1,8,16,1024]{3,2,1,0:T(8,128)(2,1)} %param.11) | copy-start | bytes 786436
  246.6 17.3 %collective-permute-start.19 = (f32[1,1,1,1,1,1,32,512]{7,6,5,4,3,2,1,0:T(8,128)S(1)}, f32[1,1,1,1,1,1,32,512]{7,6,5,4,3,2,1,0:T(8,128)S(1)}, u32[]{:S(2)}, u32[]{:S(2)}) collective-permute-start(f32[1,1,1,1,1,1,32,512]{7,6,5,4,3,2,1,0:T(8,128)S(1)} %constant_dynamic-slice_fusion), channel_id=1, source_target_pairs={{0,256},{16,272},{32,288},{48,304},{64,320},{80,336},{96,352},{112... | collective-permute-start | bytes 196616 | tf_op jit(solution)/shard_map/ppermute | solution.py:37
  263.9 15.0 %collective-permute-start.20 = (f32[32,512]{1,0:T(8,128)S(1)}, f32[32,512]{1,0:T(8,128)S(1)}, u32[]{:S(2)}, u32[]{:S(2)}) collective-permute-start(f32[32,512]{1,0:T(8,128)S(1)} %add_bitcast_fusion), channel_id=1, source_target_pairs={{0,2},{1,3},{2,0},{3,1},{4,6},{5,7},{6,4},{7,5},{8,10},{9,11},{10,... | collective-permute-start | bytes 196616 | tf_op jit(solution)/shard_map/ppermute | solution.py:37
  278.9 6.4 %collective-permute-start.21 = (f32[32,512]{1,0:T(8,128)S(1)}, f32[32,512]{1,0:T(8,128)S(1)}, u32[]{:S(2)}, u32[]{:S(2)}) collective-permute-start(f32[32,512]{1,0:T(8,128)S(1)} %add.344), channel_id=1, source_target_pairs={{0,4},{1,5},{2,6},{3,7},{4,0},{5,1},{6,2},{7,3},{8,12},{9,13},{10,... | collective-permute-start | bytes 196616 | tf_op jit(solution)/shard_map/ppermute | solution.py:37
  285.3 6.5 %collective-permute-start.22 = (f32[32,512]{1,0:T(8,128)S(1)}, f32[32,512]{1,0:T(8,128)S(1)}, u32[]{:S(2)}, u32[]{:S(2)}) collective-permute-start(f32[32,512]{1,0:T(8,128)S(1)} %add.345), channel_id=1, source_target_pairs={{0,8},{1,9},{2,10},{3,11},{4,12},{5,13},{6,14},{7,15},{8,0},{9,1},... | collective-permute-start | bytes 196616 | tf_op jit(solution)/shard_map/ppermute | solution.py:37
  291.8 7.3 %collective-permute-start.23 = (f32[32,512]{1,0:T(8,128)S(1)}, f32[32,512]{1,0:T(8,128)S(1)}, u32[]{:S(2)}, u32[]{:S(2)}) collective-permute-start(f32[32,512]{1,0:T(8,128)S(1)} %add.346), channel_id=1, source_target_pairs={{0,1},{1,0},{2,3},{3,2},{4,5},{5,4},{6,7},{7,6},{8,9},{9,8},{10,11... | collective-permute-start | bytes 196616 | tf_op jit(solution)/shard_map/ppermute | solution.py:37
  (6 other events, 11.0 us)

commit v11 on v10

--- a/solution.py
+++ b/solution.py
@@ -147,10 +147,10 @@
     batches, query_count, inner_width = queries.shape
     head_size = inner_width // HEADS
     query_heads = queries.reshape(batches, query_count, HEADS, head_size)
-    key_heads = keyvalue_ext[:, :, :inner_width].reshape(batches, -1, HEADS, head_size)
-    value_heads = keyvalue_ext[:, :, inner_width:].reshape(batches, -1, HEADS, head_size)
+    key_heads = keyvalue_ext[:HEADS]
+    value_heads = keyvalue_ext[HEADS:]
     scores = jnp.einsum(
-        "bqhd,bkhd->bhqk", query_heads, key_heads, preferred_element_type=jnp.float32
+        "bqhd,hkd->bhqk", query_heads, key_heads, preferred_element_type=jnp.float32
     ) / math.sqrt(head_size)
     scores = jnp.where(allowed, scores, MASKED)
     row_max = jnp.max(scores, axis=-1, keepdims=True)
@@ -158,7 +158,7 @@
     soft = exponent / jnp.sum(exponent, axis=-1, keepdims=True)
     rounded = soft.astype(jnp.bfloat16)
     attended = jnp.einsum(
-        "bhqk,bkhd->bqhd", rounded, value_heads, preferred_element_type=jnp.float32
+        "bhqk,hkd->bqhd", rounded, value_heads, preferred_element_type=jnp.float32
     )
     return (attended.astype(jnp.bfloat16).reshape(batches, query_count, inner_width), soft, rounded)
 
@@ -167,16 +167,16 @@
     batches, query_count, inner_width = queries.shape
     head_size = inner_width // HEADS
     query_heads = queries.reshape(batches, query_count, HEADS, head_size)
-    key_heads = keyvalue_ext[:, :, :inner_width].reshape(batches, -1, HEADS, head_size)
-    value_heads = keyvalue_ext[:, :, inner_width:].reshape(batches, -1, HEADS, head_size)
+    key_heads = keyvalue_ext[:HEADS]
+    value_heads = keyvalue_ext[HEADS:]
     grad_heads = inner_grad.reshape(batches, query_count, HEADS, head_size)
     prob_grad = jnp.einsum(
-        "bqhd,bkhd->bhqk", grad_heads, value_heads, preferred_element_type=jnp.float32
+        "bqhd,hkd->bhqk", grad_heads, value_heads, preferred_element_type=jnp.float32
     )
     row_dot = jnp.sum(soft * prob_grad, axis=-1, keepdims=True)
     score_grad = (soft * (prob_grad - row_dot) / math.sqrt(head_size)).astype(jnp.bfloat16)
     query_grad = jnp.einsum(
-        "bhqk,bkhd->bqhd", score_grad, key_heads, preferred_element_type=jnp.float32
+        "bhqk,hkd->bqhd", score_grad, key_heads, preferred_element_type=jnp.float32
     )
     key_grad = jnp.einsum(
         "bhqk,bqhd->bkhd", score_grad, query_heads, preferred_element_type=jnp.float32
@@ -240,10 +240,12 @@
         jnp.bfloat16
     )
     queries = queries.reshape(batches, tile_rows * tile_cols, inner_width)
-    keyvalue_ext = jnp.dot(normed_ext, full_keyvalue, preferred_element_type=jnp.float32)
-    keyvalue_ext = keyvalue_ext.astype(jnp.bfloat16).reshape(
-        batches, ext_rows * ext_cols, 2 * inner_width
-    )
+    keyvalue_ext = jnp.einsum(
+        "tf,fhd->htd",
+        normed_ext,
+        full_keyvalue.reshape(model_width, 2 * HEADS, -1),
+        preferred_element_type=jnp.float32,
+    ).astype(jnp.bfloat16)
     allowed = window_mask(
         lax.axis_index("row") * tile_rows,
         lax.axis_index("col") * tile_cols,

time: 302 us -> 309 us (1.023)
  waiting for transfers between devices: 91.8 us -> 117 us
  starting transfers between devices: 114 us -> 98.9 us
  matrix products: 30 us -> 19.1 us
  local copies, waits for them, and re-layouts: 49 us -> 53.7 us
    ppermute x16, waiting for transfers between devices: 84 us -> 101 us  [partner_swap(): return lax.ppermute(value, axis, [(i, i ^ mask) for i in range(count)])]
    ppermute x16, starting transfers between devices: 87.9 us -> 73.3 us  [partner_swap(): return lax.ppermute(value, axis, [(i, i ^ mask) for i in range(count)])]
    ppermute x4, waiting for transfers between devices: 3.91 us -> 12.3 us  [shifted(): lax.ppermute(value, axis, [(source, source + steps) for source in range(f...]
    ppermute x2, waiting for transfers between devices: 0.01 us -> 4.19 us  [with_halo(): lax.ppermute(lax.slice_in_dim(block, block.shape[dim] - width, None, axis...]
    dot_general x1, matrix products: 5.84 us -> 1.84 us  [tile_backward(): jnp.einsum('bhqk,bqhd->bkhd', score_grad, query_heads, preferred_element_...]
    another operation x1 -> x2, local copies, waits for them, and re-layouts: 0.87 us -> 4.82 us  [the longest x1 3.95 us: local(): full_keyvalue.reshape(model_width, 2 * HEADS, -1)]
    ppermute x2, waiting for transfers between devices: 3.9 us -> 0.01 us  [with_halo(): lax.ppermute(lax.slice_in_dim(block, 0, width, axis=dim), axis, backward)]
    sub x1 -> x0, matrix products: 3.45 us -> none  [tile_forward(): exponent = jnp.exp(scores - row_max)]
  transfers between devices with their start and end apart: 24 -> 24, of which waited for: 14 -> 17; matrix products, arithmetic and copies ran while one was open for 14% -> 12% of each run, Pallas kernels for 0% -> 0%
where the time goes in v11:
time: 309 us; the launch traced here: 307 us
  waiting for transfers between devices  117 us (38%)
  starting transfers between devices  98.9 us (32%)
  local copies, waits for them, and re-layouts  53.7 us (17%)
  matrix products  19.1 us (6%)
  other arithmetic  16.3 us (5%)
    ppermute x16, waiting for transfers between devices, partner_swap(): return lax.ppermute(value, axis, [(i, i ^ mask) for i in range(count)])  101 us
    ppermute x16, starting transfers between devices, partner_swap(): return lax.ppermute(value, axis, [(i, i ^ mask) for i in range(count)])  73.3 us
    ppermute x4, starting transfers between devices, shifted(): lax.ppermute(value, axis, [(source, source + steps) for source in range(f...  12.5 us
    ppermute x4, waiting for transfers between devices, shifted(): lax.ppermute(value, axis, [(source, source + steps) for source in range(f...  12.3 us
    ppermute x2, starting transfers between devices, with_halo(): lax.ppermute(lax.slice_in_dim(block, block.shape[dim] - width, None, axis...  8.69 us
    concatenate x3, local copies, waits for them, and re-layouts, tile_backward(): jnp.concatenate([key_grad.reshape(batches, ext_count, inner_width), value...  8.2 us
    unnamed x51, local copies, waits for them, and re-layouts  8.14 us
  transfers between devices with their start and end apart: 24, of which 17 were waited for; matrix products, arithmetic and copies ran while one was open for 12% of the time, Pallas kernels for 0%

profile of v11, /device:TPU:1, one launch (start us, length us, event | category | flops | bytes accessed | tf_op | source)
XLA Modules:
  0.0 307.2 jit_solution(2030416129135364186)
XLA Ops:
  2.0 16.3 %collective-permute-start = (bf16[1,1,1,1,1,32,1024]{6,5,4,3,2,1,0:T(8,128)(2,1)S(1)}, bf16[1,1,1,1,1,32,1024]{6,5,4,3,2,1,0:T(8,128)(2,1)S(1)}, u32[]{:S(2)}, u32[]{:S(2)}) collective-permute-start(bf16[1,1,1,1,1,32,1024]{6,5,4,3,2,1,0:T(8,128)(2,1)S(1)} %constant_dynamic-slice_fusion.9), channel_id=1, source_target_pairs={{0,256},{16,272},{32,288},{48,304},{64,320},{80,336},{96,352},{112... | collective-permute-start | bytes 196616 | tf_op jit(solution)/shard_map/ppermute | solution.py:37
  20.2 4.0 %collective-permute-start.2 = (bf16[1,6,16,1024]{3,2,1,0:T(8,128)(2,1)S(1)}, bf16[1,6,16,1024]{3,2,1,0:T(8,128)(2,1)S(1)}, u32[]{:S(2)}, u32[]{:S(2)}) collective-permute-start(bf16[1,6,16,1024]{3,2,1,0:T(8,128)(2,1)S(1)} %get-tuple-element.15), channel_id=1, source_target_pairs={{0,16},{16,32},{32,48},{48,64},{64,80},{80,96},{96,112},{112,128},... | collective-permute-start | bytes 589832 | tf_op jit(solution)/shard_map/ppermute | solution.py:27
  24.9 5.5 %collective-permute-start.1 = (bf16[2,1,1,1,1,32,1024]{6,5,4,3,2,1,0:T(8,128)(2,1)}, bf16[2,1,1,1,1,32,1024]{6,5,4,3,2,1,0:T(8,128)(2,1)S(1)}, u32[]{:S(2)}, u32[]{:S(2)}) collective-permute-start(bf16[2,1,1,1,1,32,1024]{6,5,4,3,2,1,0:T(8,128)(2,1)} %constant_dynamic-slice_fusion.8), channel_id=1, source_target_pairs={{0,128},{16,144},{32,160},{48,176},{64,192},{80,208},{96,224},{112... | collective-permute-start | bytes 393224 | tf_op jit(solution)/shard_map/ppermute | solution.py:37
  33.1 3.1 %collective-permute-start.5 = (bf16[1,20,6,1024]{3,2,1,0:T(8,128)(2,1)}, bf16[1,20,6,1024]{3,2,1,0:T(8,128)(2,1)S(1)}, u32[]{:S(2)}, u32[]{:S(2)}) collective-permute-start(bf16[1,20,6,1024]{3,2,1,0:T(8,128)(2,1)} %get-tuple-element.14), channel_id=1, source_target_pairs={{1,0},{2,1},{3,2},{4,3},{5,4},{6,5},{7,6},{8,7},{9,8},{10,9},{11,1... | collective-permute-start | bytes 737288 | tf_op jit(solution)/shard_map/ppermute | solution.py:30
  36.2 4.7 %collective-permute-start.4 = (bf16[1,20,6,1024]{3,2,1,0:T(8,128)(2,1)S(1)}, bf16[1,20,6,1024]{3,2,1,0:T(8,128)(2,1)}, u32[]{:S(2)}, u32[]{:S(2)}) collective-permute-start(bf16[1,20,6,1024]{3,2,1,0:T(8,128)(2,1)S(1)} %get-tuple-element.13), channel_id=1, source_target_pairs={{0,1},{1,2},{2,3},{3,4},{4,5},{5,6},{6,7},{7,8},{8,9},{9,10},{10,1... | collective-permute-start | bytes 737288 | tf_op jit(solution)/shard_map/ppermute | solution.py:27
  40.9 3.0 collective-permute-done.1
  52.0 3.4 %collective-permute-start.6 = (bf16[2,2,1,1,1,32,1024]{6,5,4,3,2,1,0:T(8,128)(2,1)S(1)}, bf16[2,2,1,1,1,32,1024]{6,5,4,3,2,1,0:T(8,128)(2,1)S(1)}, u32[]{:S(2)}, u32[]{:S(2)}) collective-permute-start(bf16[2,2,1,1,1,32,1024]{6,5,4,3,2,1,0:T(8,128)(2,1)S(1)} %copy-done.20), channel_id=1, source_target_pairs={{0,64},{16,80},{32,96},{48,112},{64,0},{80,16},{96,32},{112,48},{1... | collective-permute-start | bytes 786440 | tf_op jit(solution)/shard_map/ppermute | solution.py:37
  55.4 10.7 %collective-permute-done.6 = bf16[2,2,1,1,1,32,1024]{6,5,4,3,2,1,0:T(8,128)(2,1)S(1)} collective-permute-done((bf16[2,2,1,1,1,32,1024]{6,5,4,3,2,1,0:T(8,128)(2,1)S(1)}, bf16[2,2,1,1,1,32,1024]{6,5,4,3,2,1,0:T(8,128)(2,1)S(1)}, u32[]{:S(2)}, u32[]{:S(2)}) %collective-permute-start.6) | collective-permute-done | bytes 262176 | tf_op jit(solution)/shard_map/ppermute | solution.py:37
  68.1 13.1 %collective-permute-done.7 = bf16[2,2,2,1,1,32,1024]{6,5,4,3,2,1,0:T(8,128)(2,1)S(1)} collective-permute-done((bf16[2,2,2,1,1,32,1024]{6,5,4,3,2,1,0:T(8,128)(2,1)S(1)}, bf16[2,2,2,1,1,32,1024]{6,5,4,3,2,1,0:T(8,128)(2,1)S(1)}, u32[]{:S(2)}, u32[]{:S(2)}) %collective-permute-start.7) | collective-permute-done | bytes 524320 | tf_op jit(solution)/shard_map/ppermute | solution.py:37
  82.3 3.9 %collective-permute-start.8 = (bf16[2,2,2,2,1,32,1024]{6,5,4,3,2,1,0:T(8,128)(2,1)}, bf16[2,2,2,2,1,32,1024]{6,5,4,3,2,1,0:T(8,128)(2,1)S(1)}, u32[]{:S(2)}, u32[]{:S(2)}) collective-permute-start(bf16[2,2,2,2,1,32,1024]{6,5,4,3,2,1,0:T(8,128)(2,1)} %constant_dynamic-slice_fusion.5), channel_id=1, source_target_pairs={{0,16},{16,0},{32,48},{48,32},{64,80},{80,64},{96,112},{112,96},{1... | collective-permute-start | bytes 3145736 | tf_op jit(solution)/shard_map/ppermute | solution.py:37
  86.2 22.4 %collective-permute-done.8 = bf16[2,2,2,2,1,32,1024]{6,5,4,3,2,1,0:T(8,128)(2,1)S(1)} collective-permute-done((bf16[2,2,2,2,1,32,1024]{6,5,4,3,2,1,0:T(8,128)(2,1)}, bf16[2,2,2,2,1,32,1024]{6,5,4,3,2,1,0:T(8,128)(2,1)S(1)}, u32[]{:S(2)}, u32[]{:S(2)}) %collective-permute-start.8) | collective-permute-done | bytes 1048608 | tf_op jit(solution)/shard_map/ppermute | solution.py:37
  108.8 3.8 %collective-permute-start.9 = (bf16[32,32,1024]{2,1,0:T(8,128)(2,1)S(1)}, bf16[32,32,1024]{2,1,0:T(8,128)(2,1)}, u32[]{:S(2)}, u32[]{:S(2)}) collective-permute-start(bf16[32,32,1024]{2,1,0:T(8,128)(2,1)S(1)} %bitcast.156), channel_id=1, source_target_pairs={{0,1},{1,0},{2,3},{3,2},{4,5},{5,4},{6,7},{7,6},{8,9},{9,8},{10,11... | collective-permute-start | bytes 6291464 | tf_op jit(solution)/shard_map/ppermute | solution.py:37
  120.1 4.0 %reshape_reshape_squeeze.3 = bf16[1024,16,64]{2,1,0:T(8,128)(2,1)} reshape(bf16[1,32,32,1024]{3,2,1,0:T(8,128)(2,1)S(1)} %slice.66) | data formatting | bytes 4194304 | tf_op jit(solution)/shard_map/reshape;reshape;squeeze | solution.py:246
  128.2 6.0 %fusion.12 = bf16[16,560,64]{1,2,0:T(8,128)(2,1)S(1)} fusion(bf16[1024,16,64]{2,1,0:T(8,128)(2,1)} %reshape_reshape_squeeze.3, bf16[560,1024]{1,0:T(8,128)(2,1)} %reshape.229), kind=kOutput, calls=%fused_computation.19 | convolution fusion | flops 1174978560 | bytes 4390912 | tf_op jit(solution)/shard_map/tf,fhd->htd/dot_general | solution.py:243
  157.7 3.3 %copy.28 = f32[1,560,8,64]{3,2,0,1:T(8,128)} copy(f32[1,560,8,64]{1,3,2,0:T(8,128)} %get-tuple-element.26) | data formatting | bytes 2293760 | tf_op jit(solution)/shard_map/bhqk,bqhd->bkhd/transpose | solution.py:181
  161.0 3.6 %concatenate.23 = f32[1,20,28,512]{3,0,2,1:T(1,128)} reshape(f32[1,560,8,64]{3,2,0,1:T(8,128)} %copy.28) | data formatting | bytes 2293760 | tf_op jit(solution)/shard_map/concatenate | solution.py:188
  164.6 3.1 copy.29
  167.7 3.6 %concatenate.24 = f32[1,20,28,512]{3,0,2,1:T(1,128)} reshape(f32[1,560,8,64]{3,2,0,1:T(8,128)} %copy.29) | data formatting | bytes 2293760 | tf_op jit(solution)/shard_map/concatenate | solution.py:188
  174.9 3.5 %bitcast_add_fusion = f32[1024,512]{1,0:T(8,128)S(1)} fusion(f32[1024,512]{1,0:T(8,128)} %collective-permute-done.14, f32[1024,2,512]{2,0,1:T(8,128)} %copy-done.14, s32[]{:T(128)S(6)} %select_n.253), kind=kLoop, calls=%fused_computation.10 | loop fusion | flops 524288 | bytes 6291460 | tf_op jit(solution)/shard_map/add | solution.py:283
  179.5 3.5 %collective-permute-start.15 = (f32[2,2,2,2,1,1,32,512]{7,6,5,4,3,2,1,0:T(8,128)}, f32[2,2,2,2,1,1,32,512]{7,6,5,4,3,2,1,0:T(8,128)}, u32[]{:S(2)}, u32[]{:S(2)}) collective-permute-start(f32[2,2,2,2,1,1,32,512]{7,6,5,4,3,2,1,0:T(8,128)} %constant_dynamic-slice_fusion.4), channel_id=1, source_target_pairs={{0,16},{16,0},{32,48},{48,32},{64,80},{80,64},{96,112},{112,96},{1... | collective-permute-start | bytes 3145736 | tf_op jit(solution)/shard_map/ppermute | solution.py:37
  187.0 4.9 %collective-permute-start.10 = (f32[1,20,6,1024]{3,0,2,1:T(1,128)}, f32[1,20,6,1024]{3,0,2,1:T(1,128)}, u32[]{:S(2)}, u32[]{:S(2)}) collective-permute-start(f32[1,20,6,1024]{3,0,2,1:T(1,128)} %get-tuple-element.9), channel_id=1, source_target_pairs={{0,1},{1,2},{2,3},{3,4},{4,5},{5,6},{6,7},{7,8},{8,9},{9,10},{10,1... | collective-permute-start | bytes 1474568 | tf_op jit(solution)/shard_map/ppermute | solution.py:19
  195.7 16.1 %collective-permute-done.15 = f32[2,2,2,2,1,1,32,512]{7,6,5,4,3,2,1,0:T(8,128)} collective-permute-done((f32[2,2,2,2,1,1,32,512]{7,6,5,4,3,2,1,0:T(8,128)}, f32[2,2,2,2,1,1,32,512]{7,6,5,4,3,2,1,0:T(8,128)}, u32[]{:S(2)}, u32[]{:S(2)}) %collective-permute-start.15) | collective-permute-done | bytes 1048608 | tf_op jit(solution)/shard_map/ppermute | solution.py:37
  221.2 4.0 %collective-permute-start.12 = (f32[1,6,16,1024]{3,0,2,1:T(1,128)S(1)}, f32[1,6,16,1024]{3,0,2,1:T(1,128)S(1)}, u32[]{:S(2)}, u32[]{:S(2)}) collective-permute-start(f32[1,6,16,1024]{3,0,2,1:T(1,128)S(1)} %get-tuple-element.11), channel_id=1, source_target_pairs={{0,16},{16,32},{32,48},{48,64},{64,80},{80,96},{96,112},{112,128},... | collective-permute-start | bytes 1179656 | tf_op jit(solution)/shard_map/ppermute | solution.py:19
  231.5 9.8 %collective-permute-done.12 = f32[1,6,16,1024]{3,0,2,1:T(1,128)S(1)} collective-permute-done((f32[1,6,16,1024]{3,0,2,1:T(1,128)S(1)}, f32[1,6,16,1024]{3,0,2,1:T(1,128)S(1)}, u32[]{:S(2)}, u32[]{:S(2)}) %collective-permute-start.12) | collective-permute-done | bytes 393248 | tf_op jit(solution)/shard_map/ppermute | solution.py:19
  242.1 2.8 collective-permute-start.18
  245.8 15.9 %collective-permute-done.18 = f32[2,1,1,1,1,1,32,512]{7,6,5,4,3,2,1,0:T(8,128)S(1)} collective-permute-done((f32[2,1,1,1,1,1,32,512]{7,6,5,4,3,2,1,0:T(8,128)S(1)}, f32[2,1,1,1,1,1,32,512]{7,6,5,4,3,2,1,0:T(8,128)S(1)}, u32[]{:S(2)}, u32[]{:S(2)}) %collective-permute-start.18) | collective-permute-done | bytes 131104 | tf_op jit(solution)/shard_map/ppermute | solution.py:37
  261.7 7.1 %collective-permute-start.19 = (f32[1,1,1,1,1,1,32,512]{7,6,5,4,3,2,1,0:T(8,128)S(1)}, f32[1,1,1,1,1,1,32,512]{7,6,5,4,3,2,1,0:T(8,128)S(1)}, u32[]{:S(2)}, u32[]{:S(2)}) collective-permute-start(f32[1,1,1,1,1,1,32,512]{7,6,5,4,3,2,1,0:T(8,128)S(1)} %constant_dynamic-slice_fusion), channel_id=1, source_target_pairs={{0,256},{16,272},{32,288},{48,304},{64,320},{80,336},{96,352},{112... | collective-permute-start | bytes 196616 | tf_op jit(solution)/shard_map/ppermute | solution.py:37
  269.4 8.3 %collective-permute-done.19 = f32[1,1,1,1,1,1,32,512]{7,6,5,4,3,2,1,0:T(8,128)S(1)} collective-permute-done((f32[1,1,1,1,1,1,32,512]{7,6,5,4,3,2,1,0:T(8,128)S(1)}, f32[1,1,1,1,1,1,32,512]{7,6,5,4,3,2,1,0:T(8,128)S(1)}, u32[]{:S(2)}, u32[]{:S(2)}) %collective-permute-start.19) | collective-permute-done | bytes 65568 | tf_op jit(solution)/shard_map/ppermute | solution.py:37
  279.8 4.3 %collective-permute-done.20 = f32[32,512]{1,0:T(8,128)S(1)} collective-permute-done((f32[32,512]{1,0:T(8,128)S(1)}, f32[32,512]{1,0:T(8,128)S(1)}, u32[]{:S(2)}, u32[]{:S(2)}) %collective-permute-start.20) | collective-permute-done | bytes 65568 | tf_op jit(solution)/shard_map/ppermute | solution.py:37
  284.2 6.0 %collective-permute-start.21 = (f32[32,512]{1,0:T(8,128)S(1)}, f32[32,512]{1,0:T(8,128)S(1)}, u32[]{:S(2)}, u32[]{:S(2)}) collective-permute-start(f32[32,512]{1,0:T(8,128)S(1)} %add.344), channel_id=1, source_target_pairs={{0,4},{1,5},{2,6},{3,7},{4,0},{5,1},{6,2},{7,3},{8,12},{9,13},{10,... | collective-permute-start | bytes 196616 | tf_op jit(solution)/shard_map/ppermute | solution.py:37
  291.9 4.9 %collective-permute-start.22 = (f32[32,512]{1,0:T(8,128)S(1)}, f32[32,512]{1,0:T(8,128)S(1)}, u32[]{:S(2)}, u32[]{:S(2)}) collective-permute-start(f32[32,512]{1,0:T(8,128)S(1)} %add.345), channel_id=1, source_target_pairs={{0,8},{1,9},{2,10},{3,11},{4,12},{5,13},{6,14},{7,15},{8,0},{9,1},... | collective-permute-start | bytes 196616 | tf_op jit(solution)/shard_map/ppermute | solution.py:37
  298.5 5.6 %collective-permute-start.23 = (f32[32,512]{1,0:T(8,128)S(1)}, f32[32,512]{1,0:T(8,128)S(1)}, u32[]{:S(2)}, u32[]{:S(2)}) collective-permute-start(f32[32,512]{1,0:T(8,128)S(1)} %add.346), channel_id=1, source_target_pairs={{0,1},{1,0},{2,3},{3,2},{4,5},{5,4},{6,7},{7,6},{8,9},{9,8},{10,11... | collective-permute-start | bytes 196616 | tf_op jit(solution)/shard_map/ppermute | solution.py:37
  (156 shorter events, 91.4 us)
Async XLA Ops:
  0.7 17.6 %copy-start.6 = (bf16[1,8,16,1024]{3,2,1,0:T(8,128)(2,1)S(1)}, bf16[1,8,16,1024]{3,2,1,0:T(8,128)(2,1)}, u32[]{:S(2)}) copy-start(bf16[1,8,16,1024]{3,2,1,0:T(8,128)(2,1)} %param.6) | copy-start | bytes 786436
  0.7 17.9 %copy-start.21 = (f32[1024]{0:T(1024)S(1)}, f32[1024]{0:T(1024)}, u32[]{:S(2)}) copy-start(f32[1024]{0:T(1024)} %param.7) | copy-start | bytes 12292
  2.0 22.2 %collective-permute-start = (bf16[1,1,1,1,1,32,1024]{6,5,4,3,2,1,0:T(8,128)(2,1)S(1)}, bf16[1,1,1,1,1,32,1024]{6,5,4,3,2,1,0:T(8,128)(2,1)S(1)}, u32[]{:S(2)}, u32[]{:S(2)}) collective-permute-start(bf16[1,1,1,1,1,32,1024]{6,5,4,3,2,1,0:T(8,128)(2,1)S(1)} %constant_dynamic-slice_fusion.9), channel_id=1, source_target_pairs={{0,256},{16,272},{32,288},{48,304},{64,320},{80,336},{96,352},{112... | collective-permute-start | bytes 196616 | tf_op jit(solution)/shard_map/ppermute | solution.py:37
  18.9 11.5 %collective-permute-start.3 = (bf16[1,6,16,1024]{3,2,1,0:T(8,128)(2,1)S(1)}, bf16[1,6,16,1024]{3,2,1,0:T(8,128)(2,1)S(1)}, u32[]{:S(2)}, u32[]{:S(2)}) collective-permute-start(bf16[1,6,16,1024]{3,2,1,0:T(8,128)(2,1)S(1)} %get-tuple-element.16), channel_id=1, source_target_pairs={{16,0},{32,16},{48,32},{64,48},{80,64},{96,80},{112,96},{128,112},... | collective-permute-start | bytes 589832 | tf_op jit(solution)/shard_map/ppermute | solution.py:30
  20.2 12.0 %collective-permute-start.2 = (bf16[1,6,16,1024]{3,2,1,0:T(8,128)(2,1)S(1)}, bf16[1,6,16,1024]{3,2,1,0:T(8,128)(2,1)S(1)}, u32[]{:S(2)}, u32[]{:S(2)}) collective-permute-start(bf16[1,6,16,1024]{3,2,1,0:T(8,128)(2,1)S(1)} %get-tuple-element.15), channel_id=1, source_target_pairs={{0,16},{16,32},{32,48},{48,64},{64,80},{80,96},{96,112},{112,128},... | collective-permute-start | bytes 589832 | tf_op jit(solution)/shard_map/ppermute | solution.py:27
  24.9 19.0 %collective-permute-start.1 = (bf16[2,1,1,1,1,32,1024]{6,5,4,3,2,1,0:T(8,128)(2,1)}, bf16[2,1,1,1,1,32,1024]{6,5,4,3,2,1,0:T(8,128)(2,1)S(1)}, u32[]{:S(2)}, u32[]{:S(2)}) collective-permute-start(bf16[2,1,1,1,1,32,1024]{6,5,4,3,2,1,0:T(8,128)(2,1)} %constant_dynamic-slice_fusion.8), channel_id=1, source_target_pairs={{0,128},{16,144},{32,160},{48,176},{64,192},{80,208},{96,224},{112... | collective-permute-start | bytes 393224 | tf_op jit(solution)/shard_map/ppermute | solution.py:37
  33.1 11.6 %collective-permute-start.5 = (bf16[1,20,6,1024]{3,2,1,0:T(8,128)(2,1)}, bf16[1,20,6,1024]{3,2,1,0:T(8,128)(2,1)S(1)}, u32[]{:S(2)}, u32[]{:S(2)}) collective-permute-start(bf16[1,20,6,1024]{3,2,1,0:T(8,128)(2,1)} %get-tuple-element.14), channel_id=1, source_target_pairs={{1,0},{2,1},{3,2},{4,3},{5,4},{6,5},{7,6},{8,7},{9,8},{10,9},{11,1... | collective-permute-start | bytes 737288 | tf_op jit(solution)/shard_map/ppermute | solution.py:30
  36.2 10.9 %collective-permute-start.4 = (bf16[1,20,6,1024]{3,2,1,0:T(8,128)(2,1)S(1)}, bf16[1,20,6,1024]{3,2,1,0:T(8,128)(2,1)}, u32[]{:S(2)}, u32[]{:S(2)}) collective-permute-start(bf16[1,20,6,1024]{3,2,1,0:T(8,128)(2,1)S(1)} %get-tuple-element.13), channel_id=1, source_target_pairs={{0,1},{1,2},{2,3},{3,4},{4,5},{5,6},{6,7},{7,8},{8,9},{9,10},{10,1... | collective-permute-start | bytes 737288 | tf_op jit(solution)/shard_map/ppermute | solution.py:27
  52.0 14.1 %collective-permute-start.6 = (bf16[2,2,1,1,1,32,1024]{6,5,4,3,2,1,0:T(8,128)(2,1)S(1)}, bf16[2,2,1,1,1,32,1024]{6,5,4,3,2,1,0:T(8,128)(2,1)S(1)}, u32[]{:S(2)}, u32[]{:S(2)}) collective-permute-start(bf16[2,2,1,1,1,32,1024]{6,5,4,3,2,1,0:T(8,128)(2,1)S(1)} %copy-done.20), channel_id=1, source_target_pairs={{0,64},{16,80},{32,96},{48,112},{64,0},{80,16},{96,32},{112,48},{1... | collective-permute-start | bytes 786440 | tf_op jit(solution)/shard_map/ppermute | solution.py:37
  66.2 15.0 %collective-permute-start.7 = (bf16[2,2,2,1,1,32,1024]{6,5,4,3,2,1,0:T(8,128)(2,1)S(1)}, bf16[2,2,2,1,1,32,1024]{6,5,4,3,2,1,0:T(8,128)(2,1)S(1)}, u32[]{:S(2)}, u32[]{:S(2)}) collective-permute-start(bf16[2,2,2,1,1,32,1024]{6,5,4,3,2,1,0:T(8,128)(2,1)S(1)} %constant_dynamic-slice_fusion.6), channel_id=1, source_target_pairs={{0,32},{16,48},{32,0},{48,16},{64,96},{80,112},{96,64},{112,80},{1... | collective-permute-start | bytes 1572872 | tf_op jit(solution)/shard_map/ppermute | solution.py:37
  82.3 26.3 %collective-permute-start.8 = (bf16[2,2,2,2,1,32,1024]{6,5,4,3,2,1,0:T(8,128)(2,1)}, bf16[2,2,2,2,1,32,1024]{6,5,4,3,2,1,0:T(8,128)(2,1)S(1)}, u32[]{:S(2)}, u32[]{:S(2)}) collective-permute-start(bf16[2,2,2,2,1,32,1024]{6,5,4,3,2,1,0:T(8,128)(2,1)} %constant_dynamic-slice_fusion.5), channel_id=1, source_target_pairs={{0,16},{16,0},{32,48},{48,32},{64,80},{80,64},{96,112},{112,96},{1... | collective-permute-start | bytes 3145736 | tf_op jit(solution)/shard_map/ppermute | solution.py:37
  108.8 7.7 %collective-permute-start.9 = (bf16[32,32,1024]{2,1,0:T(8,128)(2,1)S(1)}, bf16[32,32,1024]{2,1,0:T(8,128)(2,1)}, u32[]{:S(2)}, u32[]{:S(2)}) collective-permute-start(bf16[32,32,1024]{2,1,0:T(8,128)(2,1)S(1)} %bitcast.156), channel_id=1, source_target_pairs={{0,1},{1,0},{2,3},{3,2},{4,5},{5,4},{6,7},{7,6},{8,9},{9,8},{10,11... | collective-permute-start | bytes 6291464 | tf_op jit(solution)/shard_map/ppermute | solution.py:37
  155.4 19.5 %collective-permute-start.14 = (f32[1024,512]{1,0:T(8,128)}, f32[1024,512]{1,0:T(8,128)}, u32[]{:S(2)}, u32[]{:S(2)}) collective-permute-start(f32[1024,512]{1,0:T(8,128)} %dynamic-slice_bitcast_fusion), channel_id=1, source_target_pairs={{0,1},{1,0},{2,3},{3,2},{4,5},{5,4},{6,7},{7,6},{8,9},{9,8},{10,11... | collective-permute-start | bytes 6291464 | tf_op jit(solution)/shard_map/ppermute | solution.py:37
  178.4 14.9 %copy-start.10 = (f32[1024,512]{1,0:T(8,128)}, f32[1024,512]{1,0:T(8,128)S(1)}, u32[]{:S(2)}) copy-start(f32[1024,512]{1,0:T(8,128)S(1)} %bitcast_add_fusion) | copy-start | bytes 6291460
  178.4 13.4 %copy-start.9 = (f32[8,560,128]{2,1,0:T(8,128)S(1)}, f32[8,560,128]{2,1,0:T(8,128)}, u32[]{:S(2)}) copy-start(f32[8,560,128]{2,1,0:T(8,128)} %copy-done.8) | copy-start | bytes 6881284
  179.5 32.2 %collective-permute-start.15 = (f32[2,2,2,2,1,1,32,512]{7,6,5,4,3,2,1,0:T(8,128)}, f32[2,2,2,2,1,1,32,512]{7,6,5,4,3,2,1,0:T(8,128)}, u32[]{:S(2)}, u32[]{:S(2)}) collective-permute-start(f32[2,2,2,2,1,1,32,512]{7,6,5,4,3,2,1,0:T(8,128)} %constant_dynamic-slice_fusion.4), channel_id=1, source_target_pairs={{0,16},{16,0},{32,48},{48,32},{64,80},{80,64},{96,112},{112,96},{1... | collective-permute-start | bytes 3145736 | tf_op jit(solution)/shard_map/ppermute | solution.py:37
  184.6 31.3 %collective-permute-start.11 = (f32[1,20,6,1024]{3,0,2,1:T(1,128)}, f32[1,20,6,1024]{3,0,2,1:T(1,128)}, u32[]{:S(2)}, u32[]{:S(2)}) collective-permute-start(f32[1,20,6,1024]{3,0,2,1:T(1,128)} %get-tuple-element.10), channel_id=1, source_target_pairs={{1,0},{2,1},{3,2},{4,3},{5,4},{6,5},{7,6},{8,7},{9,8},{10,9},{11,1... | collective-permute-start | bytes 1474568 | tf_op jit(solution)/shard_map/ppermute | solution.py:19
  187.0 29.8 %collective-permute-start.10 = (f32[1,20,6,1024]{3,0,2,1:T(1,128)}, f32[1,20,6,1024]{3,0,2,1:T(1,128)}, u32[]{:S(2)}, u32[]{:S(2)}) collective-permute-start(f32[1,20,6,1024]{3,0,2,1:T(1,128)} %get-tuple-element.9), channel_id=1, source_target_pairs={{0,1},{1,2},{2,3},{3,4},{4,5},{5,6},{6,7},{7,8},{8,9},{9,10},{10,1... | collective-permute-start | bytes 1474568 | tf_op jit(solution)/shard_map/ppermute | solution.py:19
  195.7 21.1 %copy-start.12 = (f32[1,20,28,1024]{3,0,2,1:T(1,128)S(1)}, f32[1,20,28,1024]{3,0,2,1:T(1,128)}, u32[]{:S(2)}) copy-start(f32[1,20,28,1024]{3,0,2,1:T(1,128)} %copy-done.11) | copy-start | bytes 6881284
  213.6 11.7 %copy-start.5 = (bf16[1,32,16,1024]{3,2,1,0:T(8,128)(2,1)S(1)}, bf16[1,32,16,1024]{3,2,1,0:T(8,128)(2,1)}, u32[]{:S(2)}) copy-start(bf16[1,32,16,1024]{3,2,1,0:T(8,128)(2,1)} %get-tuple-element.7) | copy-start | bytes 3145732
  213.6 13.9 %collective-permute-start.16 = (f32[2,2,2,1,1,1,32,512]{7,6,5,4,3,2,1,0:T(8,128)S(1)}, f32[2,2,2,1,1,1,32,512]{7,6,5,4,3,2,1,0:T(8,128)S(1)}, u32[]{:S(2)}, u32[]{:S(2)}) collective-permute-start(f32[2,2,2,1,1,1,32,512]{7,6,5,4,3,2,1,0:T(8,128)S(1)} %constant_dynamic-slice_fusion.3), channel_id=1, source_target_pairs={{0,32},{16,48},{32,0},{48,16},{64,96},{80,112},{96,64},{112,80},{1... | collective-permute-start | bytes 1572872 | tf_op jit(solution)/shard_map/ppermute | solution.py:37
  219.9 11.5 %collective-permute-start.13 = (f32[1,6,16,1024]{3,0,2,1:T(1,128)S(1)}, f32[1,6,16,1024]{3,0,2,1:T(1,128)S(1)}, u32[]{:S(2)}, u32[]{:S(2)}) collective-permute-start(f32[1,6,16,1024]{3,0,2,1:T(1,128)S(1)} %get-tuple-element.12), channel_id=1, source_target_pairs={{16,0},{32,16},{48,32},{64,48},{80,64},{96,80},{112,96},{128,112},... | collective-permute-start | bytes 1179656 | tf_op jit(solution)/shard_map/ppermute | solution.py:19
  221.2 20.0 %collective-permute-start.12 = (f32[1,6,16,1024]{3,0,2,1:T(1,128)S(1)}, f32[1,6,16,1024]{3,0,2,1:T(1,128)S(1)}, u32[]{:S(2)}, u32[]{:S(2)}) collective-permute-start(f32[1,6,16,1024]{3,0,2,1:T(1,128)S(1)} %get-tuple-element.11), channel_id=1, source_target_pairs={{0,16},{16,32},{32,48},{48,64},{64,80},{80,96},{96,112},{112,128},... | collective-permute-start | bytes 1179656 | tf_op jit(solution)/shard_map/ppermute | solution.py:19
  227.7 14.3 %collective-permute-start.17 = (f32[2,2,1,1,1,1,32,512]{7,6,5,4,3,2,1,0:T(8,128)S(1)}, f32[2,2,1,1,1,1,32,512]{7,6,5,4,3,2,1,0:T(8,128)S(1)}, u32[]{:S(2)}, u32[]{:S(2)}) collective-permute-start(f32[2,2,1,1,1,1,32,512]{7,6,5,4,3,2,1,0:T(8,128)S(1)} %constant_dynamic-slice_fusion.2), channel_id=1, source_target_pairs={{0,64},{16,80},{32,96},{48,112},{64,0},{80,16},{96,32},{112,48},{1... | collective-permute-start | bytes 786440 | tf_op jit(solution)/shard_map/ppermute | solution.py:37
  242.0 26.8 %copy-start.3 = (bf16[1024,512]{1,0:T(8,128)(2,1)S(1)}, bf16[1024,512]{1,0:T(8,128)(2,1)}, u32[]{:S(2)}) copy-start(bf16[1024,512]{1,0:T(8,128)(2,1)} %copy-done.2) | copy-start | bytes 3145732
  242.1 19.5 %collective-permute-start.18 = (f32[2,1,1,1,1,1,32,512]{7,6,5,4,3,2,1,0:T(8,128)S(1)}, f32[2,1,1,1,1,1,32,512]{7,6,5,4,3,2,1,0:T(8,128)S(1)}, u32[]{:S(2)}, u32[]{:S(2)}) collective-permute-start(f32[2,1,1,1,1,1,32,512]{7,6,5,4,3,2,1,0:T(8,128)S(1)} %constant_dynamic-slice_fusion.1), channel_id=1, source_target_pairs={{0,128},{16,144},{32,160},{48,176},{64,192},{80,208},{96,224},{112... | collective-permute-start | bytes 393224 | tf_op jit(solution)/shard_map/ppermute | solution.py:37
  245.8 58.3 %copy-start.17 = (bf16[1,8,16,1024]{3,2,1,0:T(8,128)(2,1)S(1)}, bf16[1,8,16,1024]{3,2,1,0:T(8,128)(2,1)}, u32[]{:S(2)}) copy-start(bf16[1,8,16,1024]{3,2,1,0:T(8,128)(2,1)} %param.11) | copy-start | bytes 786436
  261.7 16.0 %collective-permute-start.19 = (f32[1,1,1,1,1,1,32,512]{7,6,5,4,3,2,1,0:T(8,128)S(1)}, f32[1,1,1,1,1,1,32,512]{7,6,5,4,3,2,1,0:T(8,128)S(1)}, u32[]{:S(2)}, u32[]{:S(2)}) collective-permute-start(f32[1,1,1,1,1,1,32,512]{7,6,5,4,3,2,1,0:T(8,128)S(1)} %constant_dynamic-slice_fusion), channel_id=1, source_target_pairs={{0,256},{16,272},{32,288},{48,304},{64,320},{80,336},{96,352},{112... | collective-permute-start | bytes 196616 | tf_op jit(solution)/shard_map/ppermute | solution.py:37
  277.7 6.5 %collective-permute-start.20 = (f32[32,512]{1,0:T(8,128)S(1)}, f32[32,512]{1,0:T(8,128)S(1)}, u32[]{:S(2)}, u32[]{:S(2)}) collective-permute-start(f32[32,512]{1,0:T(8,128)S(1)} %add_bitcast_fusion), channel_id=1, source_target_pairs={{0,2},{1,3},{2,0},{3,1},{4,6},{5,7},{6,4},{7,5},{8,10},{9,11},{10,... | collective-permute-start | bytes 196616 | tf_op jit(solution)/shard_map/ppermute | solution.py:37
  284.2 7.7 %collective-permute-start.21 = (f32[32,512]{1,0:T(8,128)S(1)}, f32[32,512]{1,0:T(8,128)S(1)}, u32[]{:S(2)}, u32[]{:S(2)}) collective-permute-start(f32[32,512]{1,0:T(8,128)S(1)} %add.344), channel_id=1, source_target_pairs={{0,4},{1,5},{2,6},{3,7},{4,0},{5,1},{6,2},{7,3},{8,12},{9,13},{10,... | collective-permute-start | bytes 196616 | tf_op jit(solution)/shard_map/ppermute | solution.py:37
  291.9 6.6 %collective-permute-start.22 = (f32[32,512]{1,0:T(8,128)S(1)}, f32[32,512]{1,0:T(8,128)S(1)}, u32[]{:S(2)}, u32[]{:S(2)}) collective-permute-start(f32[32,512]{1,0:T(8,128)S(1)} %add.345), channel_id=1, source_target_pairs={{0,8},{1,9},{2,10},{3,11},{4,12},{5,13},{6,14},{7,15},{8,0},{9,1},... | collective-permute-start | bytes 196616 | tf_op jit(solution)/shard_map/ppermute | solution.py:37
  298.5 7.3 %collective-permute-start.23 = (f32[32,512]{1,0:T(8,128)S(1)}, f32[32,512]{1,0:T(8,128)S(1)}, u32[]{:S(2)}, u32[]{:S(2)}) collective-permute-start(f32[32,512]{1,0:T(8,128)S(1)} %add.346), channel_id=1, source_target_pairs={{0,1},{1,0},{2,3},{3,2},{4,5},{5,4},{6,7},{7,6},{8,9},{9,8},{10,11... | collective-permute-start | bytes 196616 | tf_op jit(solution)/shard_map/ppermute | solution.py:37
  (16 other events, 69.3 us)

commit v12 on v10

--- a/solution.py
+++ b/solution.py
@@ -96,6 +96,43 @@
     return held.reshape(held.shape[levels:])
 
 
+def split_swap(value, low_mask, high_mask):
+    rows, cols = lax.axis_size("row"), lax.axis_size("col")
+    pairs = []
+    for r in range(rows):
+        for c in range(cols):
+            mask = low_mask if c % 2 == 0 else high_mask
+            pairs.append((r * cols + c, (r ^ mask) * cols + c))
+    return lax.ppermute(value, ("row", "col"), pairs)
+
+
+def split_scatter(total):
+    levels = lax.axis_size("row").bit_length() - 1
+    core = axis_bit("col", 0)
+    low, high = axis_bit("row", 0), axis_bit("row", 1)
+    held = total.reshape((2,) * (levels - 2) + (4,) + total.shape[1:])
+    place = levels - 2
+    even = core == 0
+    keep_at = jnp.where(even, jnp.stack([low, 2 + low]), jnp.stack([2 * high, 2 * high + 1]))
+    send_at = jnp.where(
+        even, jnp.stack([1 - low, 3 - low]), jnp.stack([2 * (1 - high), 2 * (1 - high) + 1])
+    )
+    held = jnp.take(held, keep_at, axis=place) + split_swap(
+        jnp.take(held, send_at, axis=place), 1, 2
+    )
+    rest = jnp.where(even, high, low)
+    held = lax.dynamic_index_in_dim(held, rest, place) + split_swap(
+        lax.dynamic_index_in_dim(held, 1 - rest, place), 2, 1
+    )
+    for bit in range(2, levels):
+        axis = levels - 1 - bit
+        own = axis_bit("row", bit)
+        keep = lax.dynamic_index_in_dim(held, own, axis)
+        send = lax.dynamic_index_in_dim(held, 1 - own, axis)
+        held = keep + partner_swap(send, "row", 1 << bit)
+    return held.reshape(total.shape[1:])
+
+
 def gather_weights(w_query, w_keyvalue, w_output, row_groups, tie):
     rows, width = w_query.shape
     kv_rows, kv_width = w_keyvalue.shape
@@ -281,9 +318,7 @@
     pair_part = lax.dynamic_index_in_dim(halves, own, 1, keepdims=False) + partner_swap(
         lax.dynamic_index_in_dim(halves, 1 - own, 1, keepdims=False), "col", 1
     )
-    rows_part = scatter_by_bits(
-        pair_part.reshape(row_count, feature_part, half), "row", row_groups
-    )[0]
+    rows_part = split_scatter(pair_part.reshape(row_count, feature_part, half))
     for bit in range(1, col_levels):
         rows_part = rows_part + partner_swap(rows_part, "col", 1 << bit)
     held = jnp.zeros((2,) + rows_part.shape, rows_part.dtype)

time: 302 us -> 315 us (1.043)
  waiting for transfers between devices: 91.8 us -> 79.9 us
  starting transfers between devices: 114 us -> 125 us
  other arithmetic: 13.5 us -> 20.9 us
  local copies, waits for them, and re-layouts: 49 us -> 55.5 us
    ppermute x16 -> x14, waiting for transfers between devices: 84 us -> 71.3 us  [partner_swap(): return lax.ppermute(value, axis, [(i, i ^ mask) for i in range(count)])]
    ppermute x16 -> x14, starting transfers between devices: 87.9 us -> 93.8 us  [partner_swap(): return lax.ppermute(value, axis, [(i, i ^ mask) for i in range(count)])]
    ppermute x0 -> x2, starting transfers between devices: none -> 4.45 us  [split_swap(): return lax.ppermute(value, ('row', 'col'), pairs)]
    gather x0 -> x2, local copies, waits for them, and re-layouts: none -> 4.44 us  [the longest x1 2.24 us: split_scatter(): jnp.take(held, send_at, axis=place)]
    add x1, other arithmetic: 0.48 us -> 4.11 us  [local(): lax.dynamic_index_in_dim(halves, own, 1, keepdims=False)]
    unnamed x31 -> x45, local copies, waits for them, and re-layouts: 4.77 us -> 7.79 us
  transfers between devices with their start and end apart: 24 -> 24, of which waited for: 14 -> 15; matrix products, arithmetic and copies ran while one was open for 14% -> 15% of each run, Pallas kernels for 0% -> 0%
where the time goes in v12:
time: 315 us; the launch traced here: 313 us
  starting transfers between devices  125 us (40%)
  waiting for transfers between devices  79.9 us (25%)
  local copies, waits for them, and re-layouts  55.5 us (18%)
  matrix products  30.3 us (10%)
  other arithmetic  20.9 us (7%)
    ppermute x14, starting transfers between devices, partner_swap(): return lax.ppermute(value, axis, [(i, i ^ mask) for i in range(count)])  93.8 us
    ppermute x14, waiting for transfers between devices, partner_swap(): return lax.ppermute(value, axis, [(i, i ^ mask) for i in range(count)])  71.3 us
    ppermute x4, starting transfers between devices, shifted(): lax.ppermute(value, axis, [(source, source + steps) for source in range(f...  13.8 us
    ppermute x2, starting transfers between devices, with_halo(): lax.ppermute(lax.slice_in_dim(block, block.shape[dim] - width, None, axis...  9.7 us
    unnamed x45, local copies, waits for them, and re-layouts  7.79 us
    concatenate x3, local copies, waits for them, and re-layouts, tile_backward(): jnp.concatenate([key_grad.reshape(batches, ext_count, inner_width), value...  7.43 us
  transfers between devices with their start and end apart: 24, of which 15 were waited for; matrix products, arithmetic and copies ran while one was open for 15% of the time, Pallas kernels for 0%

profile of v12, /device:TPU:1, one launch (start us, length us, event | category | flops | bytes accessed | tf_op | source)
XLA Modules:
  0.0 313.4 jit_solution(2574559955234183957)
XLA Ops:
  2.0 16.3 %collective-permute-start = (bf16[1,1,1,1,1,32,1024]{6,5,4,3,2,1,0:T(8,128)(2,1)S(1)}, bf16[1,1,1,1,1,32,1024]{6,5,4,3,2,1,0:T(8,128)(2,1)S(1)}, u32[]{:S(2)}, u32[]{:S(2)}) collective-permute-start(bf16[1,1,1,1,1,32,1024]{6,5,4,3,2,1,0:T(8,128)(2,1)S(1)} %constant_dynamic-slice_fusion.8), channel_id=1, source_target_pairs={{0,256},{16,272},{32,288},{48,304},{64,320},{80,336},{96,352},{112... | collective-permute-start | bytes 196616 | tf_op jit(solution)/shard_map/ppermute | solution.py:37
  18.9 3.2 %collective-permute-start.2 = (bf16[1,6,16,1024]{3,2,1,0:T(8,128)(2,1)S(1)}, bf16[1,6,16,1024]{3,2,1,0:T(8,128)(2,1)S(1)}, u32[]{:S(2)}, u32[]{:S(2)}) collective-permute-start(bf16[1,6,16,1024]{3,2,1,0:T(8,128)(2,1)S(1)} %get-tuple-element.24), channel_id=1, source_target_pairs={{0,16},{16,32},{32,48},{48,64},{64,80},{80,96},{96,112},{112,128},... | collective-permute-start | bytes 589832 | tf_op jit(solution)/shard_map/ppermute | solution.py:27
  24.1 6.9 %collective-permute-start.1 = (bf16[2,1,1,1,1,32,1024]{6,5,4,3,2,1,0:T(8,128)(2,1)}, bf16[2,1,1,1,1,32,1024]{6,5,4,3,2,1,0:T(8,128)(2,1)S(1)}, u32[]{:S(2)}, u32[]{:S(2)}) collective-permute-start(bf16[2,1,1,1,1,32,1024]{6,5,4,3,2,1,0:T(8,128)(2,1)} %constant_dynamic-slice_fusion.7), channel_id=1, source_target_pairs={{0,128},{16,144},{32,160},{48,176},{64,192},{80,208},{96,224},{112... | collective-permute-start | bytes 393224 | tf_op jit(solution)/shard_map/ppermute | solution.py:37
  32.1 6.5 %collective-permute-start.4 = (bf16[1,20,6,1024]{3,2,1,0:T(8,128)(2,1)}, bf16[1,20,6,1024]{3,2,1,0:T(8,128)(2,1)S(1)}, u32[]{:S(2)}, u32[]{:S(2)}) collective-permute-start(bf16[1,20,6,1024]{3,2,1,0:T(8,128)(2,1)} %get-tuple-element.22), channel_id=1, source_target_pairs={{0,1},{1,2},{2,3},{3,4},{4,5},{5,6},{6,7},{7,8},{8,9},{9,10},{10,1... | collective-permute-start | bytes 737288 | tf_op jit(solution)/shard_map/ppermute | solution.py:27
  40.5 3.6 %collective-permute-done.1 = bf16[2,1,1,1,1,32,1024]{6,5,4,3,2,1,0:T(8,128)(2,1)S(1)} collective-permute-done((bf16[2,1,1,1,1,32,1024]{6,5,4,3,2,1,0:T(8,128)(2,1)}, bf16[2,1,1,1,1,32,1024]{6,5,4,3,2,1,0:T(8,128)(2,1)S(1)}, u32[]{:S(2)}, u32[]{:S(2)}) %collective-permute-start.1) | collective-permute-done | bytes 131104 | tf_op jit(solution)/shard_map/ppermute | solution.py:37
  44.9 3.9 %collective-permute-done.5 = bf16[1,20,6,1024]{3,2,1,0:T(8,128)(2,1)} collective-permute-done((bf16[1,20,6,1024]{3,2,1,0:T(8,128)(2,1)}, bf16[1,20,6,1024]{3,2,1,0:T(8,128)(2,1)}, u32[]{:S(2)}, u32[]{:S(2)}) %collective-permute-start.5) | collective-permute-done | bytes 245792 | tf_op jit(solution)/shard_map/ppermute | solution.py:30
  53.8 4.7 %collective-permute-start.6 = (bf16[2,2,1,1,1,32,1024]{6,5,4,3,2,1,0:T(8,128)(2,1)S(1)}, bf16[2,2,1,1,1,32,1024]{6,5,4,3,2,1,0:T(8,128)(2,1)S(1)}, u32[]{:S(2)}, u32[]{:S(2)}) collective-permute-start(bf16[2,2,1,1,1,32,1024]{6,5,4,3,2,1,0:T(8,128)(2,1)S(1)} %copy-done.12), channel_id=1, source_target_pairs={{0,64},{16,80},{32,96},{48,112},{64,0},{80,16},{96,32},{112,48},{1... | collective-permute-start | bytes 786440 | tf_op jit(solution)/shard_map/ppermute | solution.py:37
  58.4 8.1 %collective-permute-done.6 = bf16[2,2,1,1,1,32,1024]{6,5,4,3,2,1,0:T(8,128)(2,1)S(1)} collective-permute-done((bf16[2,2,1,1,1,32,1024]{6,5,4,3,2,1,0:T(8,128)(2,1)S(1)}, bf16[2,2,1,1,1,32,1024]{6,5,4,3,2,1,0:T(8,128)(2,1)S(1)}, u32[]{:S(2)}, u32[]{:S(2)}) %collective-permute-start.6) | collective-permute-done | bytes 262176 | tf_op jit(solution)/shard_map/ppermute | solution.py:37
  69.3 13.7 %collective-permute-done.7 = bf16[2,2,2,1,1,32,1024]{6,5,4,3,2,1,0:T(8,128)(2,1)S(1)} collective-permute-done((bf16[2,2,2,1,1,32,1024]{6,5,4,3,2,1,0:T(8,128)(2,1)}, bf16[2,2,2,1,1,32,1024]{6,5,4,3,2,1,0:T(8,128)(2,1)S(1)}, u32[]{:S(2)}, u32[]{:S(2)}) %collective-permute-start.7) | collective-permute-done | bytes 524320 | tf_op jit(solution)/shard_map/ppermute | solution.py:37
  86.1 24.6 %collective-permute-done.8 = bf16[2,2,2,2,1,32,1024]{6,5,4,3,2,1,0:T(8,128)(2,1)} collective-permute-done((bf16[2,2,2,2,1,32,1024]{6,5,4,3,2,1,0:T(8,128)(2,1)}, bf16[2,2,2,2,1,32,1024]{6,5,4,3,2,1,0:T(8,128)(2,1)}, u32[]{:S(2)}, u32[]{:S(2)}) %collective-permute-start.8) | collective-permute-done | bytes 1048608 | tf_op jit(solution)/shard_map/ppermute | solution.py:37
  112.1 3.3 %collective-permute-start.9 = (bf16[32,32,1024]{2,1,0:T(8,128)(2,1)S(1)}, bf16[32,32,1024]{2,1,0:T(8,128)(2,1)}, u32[]{:S(2)}, u32[]{:S(2)}) collective-permute-start(bf16[32,32,1024]{2,1,0:T(8,128)(2,1)S(1)} %bitcast.121), channel_id=1, source_target_pairs={{0,1},{1,0},{2,3},{3,2},{4,5},{5,4},{6,7},{7,6},{8,9},{9,8},{10,11... | collective-permute-start | bytes 6291464 | tf_op jit(solution)/shard_map/ppermute | solution.py:37
  125.6 3.3 %fusion.15 = bf16[1,560,1024]{2,1,0:T(8,128)(2,1)S(1)} fusion(bf16[560,1024]{1,0:T(8,128)(2,1)} %reshape.265, bf16[1024,1024]{1,0:T(8,128)(2,1)} %bitcast.127), kind=kOutput, calls=%fused_computation.18 | convolution fusion | flops 1174978560 | bytes 4390912 | tf_op jit(solution)/shard_map/dot_general | solution.py:280
  134.8 3.5 %fusion.80 = (f32[8,128]{1,0:T(8,128)S(1)}, f32[8,128,560]{1,2,0:T(8,128)}) fusion(pred[128,560]{0,1:T(8,128)(4,1)} %fusion.49, bf16[128,8,64]{0,2,1:T(8,128)(2,1)S(1)} %bitcast.146, bf16[560,8,64]{0,2,1:T(8,128)(2,1)} %bitcast.136), kind=kOutput, calls=%fused_computation.144 | convolution fusion | flops 75694640 | bytes 3074048 | tf_op jit(solution)/shard_map/sub | solution.py:194
  138.3 3.6 %fusion.81 = (bf16[1,560,8,64]{1,3,2,0:T(8,128)(2,1)}, f32[1,560,8,64]{1,3,2,0:T(8,128)}) fusion(bf16[128,8,64]{0,2,1:T(8,128)(2,1)S(1)} %bitcast.144, f32[8,128]{1,0:T(8,128)S(1)} %get-tuple-element.26, pred[128,560]{0,1:T(8,128)(4,1)} %fusion.49, bf16[128,8,64]{0,2,1:T(8,128)(2,1)S(1)} %bitcast.147, bf16[560,8,64]{0,2,1:T(8,128)(2,1)} %bitcast.137), kind=kOutput, calls=%fused_computation.145 | convolution fusion | flops 149956144 | bytes 2631680 | tf_op jit(solution)/shard_map/bhqk,bqhd->bkhd/dot_general | solution.py:221
  141.9 5.8 %fusion.82 = (bf16[1,560,8,64]{1,3,2,0:T(8,128)(2,1)}, f32[1,560,8,64]{1,3,2,0:T(8,128)}) fusion(bf16[128,8,64]{0,2,1:T(8,128)(2,1)S(1)} %bitcast.148, f32[8,128,560]{1,2,0:T(8,128)} %fusion.85, f32[8,128,560]{1,2,0:T(8,128)} %get-tuple-element.27, f32[8,128]{1,0:T(8,128)S(1)} %get-tuple-element.26), kind=kOutput, calls=%fused_computation.146 | convolution fusion | flops 77702704 | bytes 6443008 | tf_op jit(solution)/shard_map/bhqk,bqhd->bkhd/dot_general | solution.py:218
  163.4 4.1 %bitcast_add_fusion = f32[1024,512]{1,0:T(8,128)} fusion(f32[1024,512]{1,0:T(8,128)} %collective-permute-done.14, f32[1024,2,512]{2,0,1:T(8,128)} %copy-done.4, s32[]{:T(128)S(6)} %select_n.281), kind=kLoop, calls=%fused_computation.9 | loop fusion | flops 524288 | bytes 6291460 | tf_op jit(solution)/shard_map/add | solution.py:318
  178.0 3.0 copy.22
  183.9 3.1 copy.21
  186.9 3.6 %concatenate.23 = f32[1,20,28,512]{3,0,2,1:T(1,128)} reshape(f32[1,560,8,64]{3,2,0,1:T(8,128)} %copy.21) | data formatting | bytes 2293760 | tf_op jit(solution)/shard_map/concatenate | solution.py:225
  197.0 7.6 %collective-permute-start.10 = (f32[1,20,6,1024]{3,0,2,1:T(1,128)}, f32[1,20,6,1024]{3,0,2,1:T(1,128)}, u32[]{:S(2)}, u32[]{:S(2)}) collective-permute-start(f32[1,20,6,1024]{3,0,2,1:T(1,128)} %get-tuple-element.16), channel_id=1, source_target_pairs={{0,1},{1,2},{2,3},{3,4},{4,5},{5,6},{6,7},{7,8},{8,9},{9,10},{10,1... | collective-permute-start | bytes 1474568 | tf_op jit(solution)/shard_map/ppermute | solution.py:19
  220.7 3.0 collective-permute-start.12
  224.9 4.5 %fusion.19 = bf16[8,64,128]{2,1,0:T(8,128)(2,1)S(1)} fusion(bf16[560,8,64]{0,2,1:T(8,128)(2,1)S(1)} %bitcast.139, f32[8,128,560]{1,2,0:T(8,128)} %fusion.85, f32[8,128,560]{1,2,0:T(8,128)} %get-tuple-element.27, f32[8,128]{1,0:T(8,128)S(1)} %copy-done.20), kind=kOutput, calls=%fused_computation.26 | convolution fusion | flops 77481520 | bytes 5296128 | tf_op jit(solution)/shard_map/bhqk,bkhd->bqhd/dot_general | solution.py:215
  229.5 2.9 collective-permute-done.16
  233.7 8.0 %collective-permute-start.17 = (f32[2,2,1,1,32,512]{5,4,2,1,0,3:T(8,128)S(1)}, f32[2,2,1,1,32,512]{5,4,2,1,0,3:T(8,128)S(1)}, u32[]{:S(2)}, u32[]{:S(2)}) collective-permute-start(f32[2,2,1,1,32,512]{5,4,2,1,0,3:T(8,128)S(1)} %constant_dynamic-slice_fusion.2), channel_id=1, source_target_pairs={{0,64},{16,80},{32,96},{48,112},{64,0},{80,16},{96,32},{112,48},{1... | collective-permute-start | bytes 786440 | tf_op jit(solution)/shard_map/ppermute | solution.py:37
  243.6 4.4 %collective-permute-done.17 = f32[2,2,1,1,32,512]{5,4,2,1,0,3:T(8,128)S(1)} collective-permute-done((f32[2,2,1,1,32,512]{5,4,2,1,0,3:T(8,128)S(1)}, f32[2,2,1,1,32,512]{5,4,2,1,0,3:T(8,128)S(1)}, u32[]{:S(2)}, u32[]{:S(2)}) %collective-permute-start.17) | collective-permute-done | bytes 262176 | tf_op jit(solution)/shard_map/ppermute | solution.py:37
  248.1 8.3 %collective-permute-start.18 = (f32[2,1,1,1,32,512]{5,4,2,1,0,3:T(8,128)S(1)}, f32[2,1,1,1,32,512]{5,4,2,1,0,3:T(8,128)S(1)}, u32[]{:S(2)}, u32[]{:S(2)}) collective-permute-start(f32[2,1,1,1,32,512]{5,4,2,1,0,3:T(8,128)S(1)} %constant_dynamic-slice_fusion.1), channel_id=1, source_target_pairs={{0,128},{16,144},{32,160},{48,176},{64,192},{80,208},{96,224},{112... | collective-permute-start | bytes 393224 | tf_op jit(solution)/shard_map/ppermute | solution.py:37
  259.5 8.1 %collective-permute-start.19 = (f32[1,1,1,1,32,512]{5,4,2,1,0,3:T(8,128)S(1)}, f32[1,1,1,1,32,512]{5,4,2,1,0,3:T(8,128)S(1)}, u32[]{:S(2)}, u32[]{:S(2)}) collective-permute-start(f32[1,1,1,1,32,512]{5,4,2,1,0,3:T(8,128)S(1)} %constant_dynamic-slice_fusion), channel_id=1, source_target_pairs={{0,256},{16,272},{32,288},{48,304},{64,320},{80,336},{96,352},{112... | collective-permute-start | bytes 196616 | tf_op jit(solution)/shard_map/ppermute | solution.py:37
  268.2 5.1 %collective-permute-done.19 = f32[1,1,1,1,32,512]{5,4,2,1,0,3:T(8,128)S(1)} collective-permute-done((f32[1,1,1,1,32,512]{5,4,2,1,0,3:T(8,128)S(1)}, f32[1,1,1,1,32,512]{5,4,2,1,0,3:T(8,128)S(1)}, u32[]{:S(2)}, u32[]{:S(2)}) %collective-permute-start.19) | collective-permute-done | bytes 65568 | tf_op jit(solution)/shard_map/ppermute | solution.py:37
  273.3 17.1 %collective-permute-start.20 = (f32[32,512]{1,0:T(8,128)S(1)}, f32[32,512]{1,0:T(8,128)S(1)}, u32[]{:S(2)}, u32[]{:S(2)}) collective-permute-start(f32[32,512]{1,0:T(8,128)S(1)} %add_bitcast_fusion), channel_id=1, source_target_pairs={{0,2},{1,3},{2,0},{3,1},{4,6},{5,7},{6,4},{7,5},{8,10},{9,11},{10,... | collective-permute-start | bytes 196616 | tf_op jit(solution)/shard_map/ppermute | solution.py:37
  292.4 4.7 %collective-permute-start.21 = (f32[32,512]{1,0:T(8,128)S(1)}, f32[32,512]{1,0:T(8,128)S(1)}, u32[]{:S(2)}, u32[]{:S(2)}) collective-permute-start(f32[32,512]{1,0:T(8,128)S(1)} %add.368), channel_id=1, source_target_pairs={{0,4},{1,5},{2,6},{3,7},{4,0},{5,1},{6,2},{7,3},{8,12},{9,13},{10,... | collective-permute-start | bytes 196616 | tf_op jit(solution)/shard_map/ppermute | solution.py:37
  298.8 4.8 %collective-permute-start.22 = (f32[32,512]{1,0:T(8,128)S(1)}, f32[32,512]{1,0:T(8,128)S(1)}, u32[]{:S(2)}, u32[]{:S(2)}) collective-permute-start(f32[32,512]{1,0:T(8,128)S(1)} %add.369), channel_id=1, source_target_pairs={{0,8},{1,9},{2,10},{3,11},{4,12},{5,13},{6,14},{7,15},{8,0},{9,1},... | collective-permute-start | bytes 196616 | tf_op jit(solution)/shard_map/ppermute | solution.py:37
  305.3 5.6 %collective-permute-start.23 = (f32[32,512]{1,0:T(8,128)S(1)}, f32[32,512]{1,0:T(8,128)S(1)}, u32[]{:S(2)}, u32[]{:S(2)}) collective-permute-start(f32[32,512]{1,0:T(8,128)S(1)} %get-tuple-element.9), channel_id=1, source_target_pairs={{0,1},{1,0},{2,3},{3,2},{4,5},{5,4},{6,7},{7,6},{8,9},{9,8},{10,11... | collective-permute-start | bytes 196616 | tf_op jit(solution)/shard_map/ppermute | solution.py:37
  (155 shorter events, 102.7 us)
Async XLA Ops:
  0.7 17.6 %copy-start = (bf16[1,8,16,1024]{3,2,1,0:T(8,128)(2,1)S(1)}, bf16[1,8,16,1024]{3,2,1,0:T(8,128)(2,1)}, u32[]{:S(2)}) copy-start(bf16[1,8,16,1024]{3,2,1,0:T(8,128)(2,1)} %param.8) | copy-start | bytes 786436
  0.7 17.9 %copy-start.15 = (f32[1024]{0:T(1024)S(1)}, f32[1024]{0:T(1024)}, u32[]{:S(2)}) copy-start(f32[1024]{0:T(1024)} %param.9) | copy-start | bytes 12292
  2.0 21.5 %collective-permute-start = (bf16[1,1,1,1,1,32,1024]{6,5,4,3,2,1,0:T(8,128)(2,1)S(1)}, bf16[1,1,1,1,1,32,1024]{6,5,4,3,2,1,0:T(8,128)(2,1)S(1)}, u32[]{:S(2)}, u32[]{:S(2)}) collective-permute-start(bf16[1,1,1,1,1,32,1024]{6,5,4,3,2,1,0:T(8,128)(2,1)S(1)} %constant_dynamic-slice_fusion.8), channel_id=1, source_target_pairs={{0,256},{16,272},{32,288},{48,304},{64,320},{80,336},{96,352},{112... | collective-permute-start | bytes 196616 | tf_op jit(solution)/shard_map/ppermute | solution.py:37
  18.9 12.1 %collective-permute-start.2 = (bf16[1,6,16,1024]{3,2,1,0:T(8,128)(2,1)S(1)}, bf16[1,6,16,1024]{3,2,1,0:T(8,128)(2,1)S(1)}, u32[]{:S(2)}, u32[]{:S(2)}) collective-permute-start(bf16[1,6,16,1024]{3,2,1,0:T(8,128)(2,1)S(1)} %get-tuple-element.24), channel_id=1, source_target_pairs={{0,16},{16,32},{32,48},{48,64},{64,80},{80,96},{96,112},{112,128},... | collective-permute-start | bytes 589832 | tf_op jit(solution)/shard_map/ppermute | solution.py:27
  22.1 8.9 %collective-permute-start.3 = (bf16[1,6,16,1024]{3,2,1,0:T(8,128)(2,1)S(1)}, bf16[1,6,16,1024]{3,2,1,0:T(8,128)(2,1)S(1)}, u32[]{:S(2)}, u32[]{:S(2)}) collective-permute-start(bf16[1,6,16,1024]{3,2,1,0:T(8,128)(2,1)S(1)} %get-tuple-element.25), channel_id=1, source_target_pairs={{16,0},{32,16},{48,32},{64,48},{80,64},{96,80},{112,96},{128,112},... | collective-permute-start | bytes 589832 | tf_op jit(solution)/shard_map/ppermute | solution.py:30
  24.1 20.0 %collective-permute-start.1 = (bf16[2,1,1,1,1,32,1024]{6,5,4,3,2,1,0:T(8,128)(2,1)}, bf16[2,1,1,1,1,32,1024]{6,5,4,3,2,1,0:T(8,128)(2,1)S(1)}, u32[]{:S(2)}, u32[]{:S(2)}) collective-permute-start(bf16[2,1,1,1,1,32,1024]{6,5,4,3,2,1,0:T(8,128)(2,1)} %constant_dynamic-slice_fusion.7), channel_id=1, source_target_pairs={{0,128},{16,144},{32,160},{48,176},{64,192},{80,208},{96,224},{112... | collective-permute-start | bytes 393224 | tf_op jit(solution)/shard_map/ppermute | solution.py:37
  32.1 12.8 %collective-permute-start.4 = (bf16[1,20,6,1024]{3,2,1,0:T(8,128)(2,1)}, bf16[1,20,6,1024]{3,2,1,0:T(8,128)(2,1)S(1)}, u32[]{:S(2)}, u32[]{:S(2)}) collective-permute-start(bf16[1,20,6,1024]{3,2,1,0:T(8,128)(2,1)} %get-tuple-element.22), channel_id=1, source_target_pairs={{0,1},{1,2},{2,3},{3,4},{4,5},{5,6},{6,7},{7,8},{8,9},{9,10},{10,1... | collective-permute-start | bytes 737288 | tf_op jit(solution)/shard_map/ppermute | solution.py:27
  38.6 10.2 %collective-permute-start.5 = (bf16[1,20,6,1024]{3,2,1,0:T(8,128)(2,1)}, bf16[1,20,6,1024]{3,2,1,0:T(8,128)(2,1)}, u32[]{:S(2)}, u32[]{:S(2)}) collective-permute-start(bf16[1,20,6,1024]{3,2,1,0:T(8,128)(2,1)} %get-tuple-element.23), channel_id=1, source_target_pairs={{1,0},{2,1},{3,2},{4,3},{5,4},{6,5},{7,6},{8,7},{9,8},{10,9},{11,1... | collective-permute-start | bytes 737288 | tf_op jit(solution)/shard_map/ppermute | solution.py:30
  53.8 12.7 %collective-permute-start.6 = (bf16[2,2,1,1,1,32,1024]{6,5,4,3,2,1,0:T(8,128)(2,1)S(1)}, bf16[2,2,1,1,1,32,1024]{6,5,4,3,2,1,0:T(8,128)(2,1)S(1)}, u32[]{:S(2)}, u32[]{:S(2)}) collective-permute-start(bf16[2,2,1,1,1,32,1024]{6,5,4,3,2,1,0:T(8,128)(2,1)S(1)} %copy-done.12), channel_id=1, source_target_pairs={{0,64},{16,80},{32,96},{48,112},{64,0},{80,16},{96,32},{112,48},{1... | collective-permute-start | bytes 786440 | tf_op jit(solution)/shard_map/ppermute | solution.py:37
  67.4 15.6 %collective-permute-start.7 = (bf16[2,2,2,1,1,32,1024]{6,5,4,3,2,1,0:T(8,128)(2,1)}, bf16[2,2,2,1,1,32,1024]{6,5,4,3,2,1,0:T(8,128)(2,1)S(1)}, u32[]{:S(2)}, u32[]{:S(2)}) collective-permute-start(bf16[2,2,2,1,1,32,1024]{6,5,4,3,2,1,0:T(8,128)(2,1)} %constant_dynamic-slice_fusion.5), channel_id=1, source_target_pairs={{0,32},{16,48},{32,0},{48,16},{64,96},{80,112},{96,64},{112,80},{1... | collective-permute-start | bytes 1572872 | tf_op jit(solution)/shard_map/ppermute | solution.py:37
  84.2 26.5 %collective-permute-start.8 = (bf16[2,2,2,2,1,32,1024]{6,5,4,3,2,1,0:T(8,128)(2,1)}, bf16[2,2,2,2,1,32,1024]{6,5,4,3,2,1,0:T(8,128)(2,1)}, u32[]{:S(2)}, u32[]{:S(2)}) collective-permute-start(bf16[2,2,2,2,1,32,1024]{6,5,4,3,2,1,0:T(8,128)(2,1)} %constant_dynamic-slice_fusion.4), channel_id=1, source_target_pairs={{0,16},{16,0},{32,48},{48,32},{64,80},{80,64},{96,112},{112,96},{1... | collective-permute-start | bytes 3145736 | tf_op jit(solution)/shard_map/ppermute | solution.py:37
  112.1 7.0 %collective-permute-start.9 = (bf16[32,32,1024]{2,1,0:T(8,128)(2,1)S(1)}, bf16[32,32,1024]{2,1,0:T(8,128)(2,1)}, u32[]{:S(2)}, u32[]{:S(2)}) collective-permute-start(bf16[32,32,1024]{2,1,0:T(8,128)(2,1)S(1)} %bitcast.121), channel_id=1, source_target_pairs={{0,1},{1,0},{2,3},{3,2},{4,5},{5,4},{6,7},{7,6},{8,9},{9,8},{10,11... | collective-permute-start | bytes 6291464 | tf_op jit(solution)/shard_map/ppermute | solution.py:37
  125.6 16.3 %copy-start.13 = (bf16[128,512]{0,1:T(8,128)(2,1)}, bf16[128,512]{0,1:T(8,128)(2,1)S(1)}, u32[]{:S(2)}) copy-start(bf16[128,512]{0,1:T(8,128)(2,1)S(1)} %copy.18) | copy-start | bytes 393220
  157.0 6.4 %collective-permute-start.14 = (f32[1024,512]{1,0:T(8,128)}, f32[1024,512]{1,0:T(8,128)}, u32[]{:S(2)}, u32[]{:S(2)}) collective-permute-start(f32[1024,512]{1,0:T(8,128)} %dynamic-slice_bitcast_fusion), channel_id=1, source_target_pairs={{0,1},{1,0},{2,3},{3,2},{4,5},{5,4},{6,7},{7,6},{8,9},{9,8},{10,11... | collective-permute-start | bytes 6291464 | tf_op jit(solution)/shard_map/ppermute | solution.py:37
  171.6 38.2 %collective-permute-start.15 = (f32[2,2,2,2,32,512]{5,4,2,1,0,3:T(8,128)}, f32[2,2,2,2,32,512]{5,4,2,1,0,3:T(8,128)}, u32[]{:S(2)}, u32[]{:S(2)}) collective-permute-start(f32[2,2,2,2,32,512]{5,4,2,1,0,3:T(8,128)} %select_bitcast_fusion), channel_id=1, source_target_pairs={{0,16},{1,33},{2,18},{3,35},{4,20},{5,37},{6,22},{7,39},{8,24},{9,... | collective-permute-start | bytes 3145736 | tf_op jit(solution)/shard_map/ppermute | solution.py:106
  193.0 13.6 %copy-start.11 = (bf16[8,16,512]{2,1,0:T(8,128)(2,1)S(1)}, bf16[8,16,512]{2,1,0:T(8,128)(2,1)}, u32[]{:S(2)}) copy-start(bf16[8,16,512]{2,1,0:T(8,128)(2,1)} %reshape.272) | copy-start | bytes 393220
  197.0 12.8 %copy-start.18 = (pred[2]{0:T(512)(128)(4,1)S(1)}, pred[2]{0:T(512)(128)(4,1)}, u32[]{:S(2)}) copy-start(pred[2]{0:T(512)(128)(4,1)} %get-tuple-element.10) | copy-start | bytes 10
  197.0 17.8 %collective-permute-start.10 = (f32[1,20,6,1024]{3,0,2,1:T(1,128)}, f32[1,20,6,1024]{3,0,2,1:T(1,128)}, u32[]{:S(2)}, u32[]{:S(2)}) collective-permute-start(f32[1,20,6,1024]{3,0,2,1:T(1,128)} %get-tuple-element.16), channel_id=1, source_target_pairs={{0,1},{1,2},{2,3},{3,4},{4,5},{5,6},{6,7},{7,8},{8,9},{9,10},{10,1... | collective-permute-start | bytes 1474568 | tf_op jit(solution)/shard_map/ppermute | solution.py:19
  204.7 12.0 %collective-permute-start.11 = (f32[1,20,6,1024]{3,0,2,1:T(1,128)}, f32[1,20,6,1024]{3,0,2,1:T(1,128)}, u32[]{:S(2)}, u32[]{:S(2)}) collective-permute-start(f32[1,20,6,1024]{3,0,2,1:T(1,128)} %get-tuple-element.17), channel_id=1, source_target_pairs={{1,0},{2,1},{3,2},{4,3},{5,4},{6,5},{7,6},{8,7},{9,8},{10,9},{11,1... | collective-permute-start | bytes 1474568 | tf_op jit(solution)/shard_map/ppermute | solution.py:19
  212.5 12.4 %copy-start.20 = (f32[8,128]{1,0:T(8,128)S(1)}, f32[8,128]{1,0:T(8,128)}, u32[]{:S(2)}) copy-start(f32[8,128]{1,0:T(8,128)} %copy-done.19) | copy-start | bytes 12292
  212.5 19.9 %collective-permute-start.16 = (f32[2,2,2,1,32,512]{5,4,2,1,0,3:T(8,128)}, f32[2,2,2,1,32,512]{5,4,2,1,0,3:T(8,128)}, u32[]{:S(2)}, u32[]{:S(2)}) collective-permute-start(f32[2,2,2,1,32,512]{5,4,2,1,0,3:T(8,128)} %constant_dynamic-slice_fusion.3), channel_id=1, source_target_pairs={{0,32},{1,17},{2,34},{3,19},{4,36},{5,21},{6,38},{7,23},{8,40},{9,... | collective-permute-start | bytes 1572872 | tf_op jit(solution)/shard_map/ppermute | solution.py:106
  220.7 21.1 %collective-permute-start.12 = (f32[1,6,16,1024]{3,0,2,1:T(1,128)}, f32[1,6,16,1024]{3,0,2,1:T(1,128)}, u32[]{:S(2)}, u32[]{:S(2)}) collective-permute-start(f32[1,6,16,1024]{3,0,2,1:T(1,128)} %get-tuple-element.18), channel_id=1, source_target_pairs={{0,16},{16,32},{32,48},{48,64},{64,80},{80,96},{96,112},{112,128},... | collective-permute-start | bytes 1179656 | tf_op jit(solution)/shard_map/ppermute | solution.py:19
  223.6 18.1 %collective-permute-start.13 = (f32[1,6,16,1024]{3,0,2,1:T(1,128)}, f32[1,6,16,1024]{3,0,2,1:T(1,128)}, u32[]{:S(2)}, u32[]{:S(2)}) collective-permute-start(f32[1,6,16,1024]{3,0,2,1:T(1,128)} %get-tuple-element.19), channel_id=1, source_target_pairs={{16,0},{32,16},{48,32},{64,48},{80,64},{96,80},{112,96},{128,112},... | collective-permute-start | bytes 1179656 | tf_op jit(solution)/shard_map/ppermute | solution.py:19
  233.7 22.8 %copy-start.1 = (bf16[1,32,32,1024]{3,2,1,0:T(8,128)(2,1)S(1)}, bf16[1,32,32,1024]{3,2,1,0:T(8,128)(2,1)}, u32[]{:S(2)}) copy-start(bf16[1,32,32,1024]{3,2,1,0:T(8,128)(2,1)} %slice.70) | copy-start | bytes 6291460
  233.7 14.3 %collective-permute-start.17 = (f32[2,2,1,1,32,512]{5,4,2,1,0,3:T(8,128)S(1)}, f32[2,2,1,1,32,512]{5,4,2,1,0,3:T(8,128)S(1)}, u32[]{:S(2)}, u32[]{:S(2)}) collective-permute-start(f32[2,2,1,1,32,512]{5,4,2,1,0,3:T(8,128)S(1)} %constant_dynamic-slice_fusion.2), channel_id=1, source_target_pairs={{0,64},{16,80},{32,96},{48,112},{64,0},{80,16},{96,32},{112,48},{1... | collective-permute-start | bytes 786440 | tf_op jit(solution)/shard_map/ppermute | solution.py:37
  248.1 11.3 %collective-permute-start.18 = (f32[2,1,1,1,32,512]{5,4,2,1,0,3:T(8,128)S(1)}, f32[2,1,1,1,32,512]{5,4,2,1,0,3:T(8,128)S(1)}, u32[]{:S(2)}, u32[]{:S(2)}) collective-permute-start(f32[2,1,1,1,32,512]{5,4,2,1,0,3:T(8,128)S(1)} %constant_dynamic-slice_fusion.1), channel_id=1, source_target_pairs={{0,128},{16,144},{32,160},{48,176},{64,192},{80,208},{96,224},{112... | collective-permute-start | bytes 393224 | tf_op jit(solution)/shard_map/ppermute | solution.py:37
  257.3 53.6 %copy-start.9 = (bf16[1,8,16,1024]{3,2,1,0:T(8,128)(2,1)S(1)}, bf16[1,8,16,1024]{3,2,1,0:T(8,128)(2,1)}, u32[]{:S(2)}) copy-start(bf16[1,8,16,1024]{3,2,1,0:T(8,128)(2,1)} %param.13) | copy-start | bytes 786436
  259.5 13.8 %collective-permute-start.19 = (f32[1,1,1,1,32,512]{5,4,2,1,0,3:T(8,128)S(1)}, f32[1,1,1,1,32,512]{5,4,2,1,0,3:T(8,128)S(1)}, u32[]{:S(2)}, u32[]{:S(2)}) collective-permute-start(f32[1,1,1,1,32,512]{5,4,2,1,0,3:T(8,128)S(1)} %constant_dynamic-slice_fusion), channel_id=1, source_target_pairs={{0,256},{16,272},{32,288},{48,304},{64,320},{80,336},{96,352},{112... | collective-permute-start | bytes 196616 | tf_op jit(solution)/shard_map/ppermute | solution.py:37
  273.3 19.1 %collective-permute-start.20 = (f32[32,512]{1,0:T(8,128)S(1)}, f32[32,512]{1,0:T(8,128)S(1)}, u32[]{:S(2)}, u32[]{:S(2)}) collective-permute-start(f32[32,512]{1,0:T(8,128)S(1)} %add_bitcast_fusion), channel_id=1, source_target_pairs={{0,2},{1,3},{2,0},{3,1},{4,6},{5,7},{6,4},{7,5},{8,10},{9,11},{10,... | collective-permute-start | bytes 196616 | tf_op jit(solution)/shard_map/ppermute | solution.py:37
  292.4 6.3 %collective-permute-start.21 = (f32[32,512]{1,0:T(8,128)S(1)}, f32[32,512]{1,0:T(8,128)S(1)}, u32[]{:S(2)}, u32[]{:S(2)}) collective-permute-start(f32[32,512]{1,0:T(8,128)S(1)} %add.368), channel_id=1, source_target_pairs={{0,4},{1,5},{2,6},{3,7},{4,0},{5,1},{6,2},{7,3},{8,12},{9,13},{10,... | collective-permute-start | bytes 196616 | tf_op jit(solution)/shard_map/ppermute | solution.py:37
  298.8 6.5 %collective-permute-start.22 = (f32[32,512]{1,0:T(8,128)S(1)}, f32[32,512]{1,0:T(8,128)S(1)}, u32[]{:S(2)}, u32[]{:S(2)}) collective-permute-start(f32[32,512]{1,0:T(8,128)S(1)} %add.369), channel_id=1, source_target_pairs={{0,8},{1,9},{2,10},{3,11},{4,12},{5,13},{6,14},{7,15},{8,0},{9,1},... | collective-permute-start | bytes 196616 | tf_op jit(solution)/shard_map/ppermute | solution.py:37
  305.3 6.7 %collective-permute-start.23 = (f32[32,512]{1,0:T(8,128)S(1)}, f32[32,512]{1,0:T(8,128)S(1)}, u32[]{:S(2)}, u32[]{:S(2)}) collective-permute-start(f32[32,512]{1,0:T(8,128)S(1)} %get-tuple-element.9), channel_id=1, source_target_pairs={{0,1},{1,0},{2,3},{3,2},{4,5},{5,4},{6,7},{7,6},{8,9},{9,8},{10,11... | collective-permute-start | bytes 196616 | tf_op jit(solution)/shard_map/ppermute | solution.py:37
  (13 other events, 51.7 us)

commit v13 on v10

--- a/solution.py
+++ b/solution.py
@@ -46,7 +46,7 @@
         yield [(code >> k) % 2 for k in range(len(group))]
 
 
-def gather_by_bits(block, axis, groups, tie=None, tie_at=2):
+def gather_by_bits(block, axis, groups, tie=None, tie_at=3):
     levels = lax.axis_size(axis).bit_length() - 1
     mine = [axis_bit(axis, bit) for bit in range(levels)]
     zero = [0] * block.ndim

time: 302 us -> 296 us (0.980)
  waiting for transfers between devices: 91.8 us -> 87.8 us
  transfers between devices with their start and end apart: 24 -> 24, of which waited for: 14 -> 15; matrix products, arithmetic and copies ran while one was open for 14% -> 16% of each run, Pallas kernels for 0% -> 0%
where the time goes in v13:
time: 296 us; the launch traced here: 294 us
  starting transfers between devices  112 us (38%)
  waiting for transfers between devices  87.8 us (30%)
  local copies, waits for them, and re-layouts  49.2 us (17%)
  matrix products  30 us (10%)
  other arithmetic  13.5 us (5%)
    ppermute x16, starting transfers between devices, partner_swap(): return lax.ppermute(value, axis, [(i, i ^ mask) for i in range(count)])  87 us
    ppermute x16, waiting for transfers between devices, partner_swap(): return lax.ppermute(value, axis, [(i, i ^ mask) for i in range(count)])  81.7 us
    ppermute x4, starting transfers between devices, shifted(): lax.ppermute(value, axis, [(source, source + steps) for source in range(f...  12 us
    ppermute x2, starting transfers between devices, with_halo(): lax.ppermute(lax.slice_in_dim(block, block.shape[dim] - width, None, axis...  9.7 us
    concatenate x3, local copies, waits for them, and re-layouts, tile_backward(): jnp.concatenate([key_grad.reshape(batches, ext_count, inner_width), value...  7.45 us
  transfers between devices with their start and end apart: 24, of which 15 were waited for; matrix products, arithmetic and copies ran while one was open for 16% of the time, Pallas kernels for 0%

profile of v13, /device:TPU:1, one launch (start us, length us, event | category | flops | bytes accessed | tf_op | source)
XLA Modules:
  0.0 294.2 jit_solution(4816943222514992483)
XLA Ops:
  2.0 16.3 %collective-permute-start = (bf16[1,1,1,1,1,32,1024]{6,5,4,3,2,1,0:T(8,128)(2,1)S(1)}, bf16[1,1,1,1,1,32,1024]{6,5,4,3,2,1,0:T(8,128)(2,1)S(1)}, u32[]{:S(2)}, u32[]{:S(2)}) collective-permute-start(bf16[1,1,1,1,1,32,1024]{6,5,4,3,2,1,0:T(8,128)(2,1)S(1)} %constant_dynamic-slice_fusion.9), channel_id=1, source_target_pairs={{0,256},{16,272},{32,288},{48,304},{64,320},{80,336},{96,352},{112... | collective-permute-start | bytes 196616 | tf_op jit(solution)/shard_map/ppermute | solution.py:37
  18.9 3.2 %collective-permute-start.3 = (bf16[1,6,16,1024]{3,2,1,0:T(8,128)(2,1)S(1)}, bf16[1,6,16,1024]{3,2,1,0:T(8,128)(2,1)S(1)}, u32[]{:S(2)}, u32[]{:S(2)}) collective-permute-start(bf16[1,6,16,1024]{3,2,1,0:T(8,128)(2,1)S(1)} %get-tuple-element.17), channel_id=1, source_target_pairs={{0,16},{16,32},{32,48},{48,64},{64,80},{80,96},{96,112},{112,128},... | collective-permute-start | bytes 589832 | tf_op jit(solution)/shard_map/ppermute | solution.py:27
  23.5 6.9 %collective-permute-start.1 = (bf16[2,1,1,1,1,32,1024]{6,5,4,3,2,1,0:T(8,128)(2,1)S(1)}, bf16[2,1,1,1,1,32,1024]{6,5,4,3,2,1,0:T(8,128)(2,1)S(1)}, u32[]{:S(2)}, u32[]{:S(2)}) collective-permute-start(bf16[2,1,1,1,1,32,1024]{6,5,4,3,2,1,0:T(8,128)(2,1)S(1)} %constant_dynamic-slice_fusion.8), channel_id=1, source_target_pairs={{0,128},{16,144},{32,160},{48,176},{64,192},{80,208},{96,224},{112... | collective-permute-start | bytes 393224 | tf_op jit(solution)/shard_map/ppermute | solution.py:37
  31.4 6.5 %collective-permute-start.5 = (bf16[1,20,6,1024]{3,2,1,0:T(8,128)(2,1)}, bf16[1,20,6,1024]{3,2,1,0:T(8,128)(2,1)S(1)}, u32[]{:S(2)}, u32[]{:S(2)}) collective-permute-start(bf16[1,20,6,1024]{3,2,1,0:T(8,128)(2,1)} %get-tuple-element.15), channel_id=1, source_target_pairs={{0,1},{1,2},{2,3},{3,4},{4,5},{5,6},{6,7},{7,8},{8,9},{9,10},{10,1... | collective-permute-start | bytes 737288 | tf_op jit(solution)/shard_map/ppermute | solution.py:27
  39.9 3.1 %collective-permute-done.1 = bf16[2,1,1,1,1,32,1024]{6,5,4,3,2,1,0:T(8,128)(2,1)S(1)} collective-permute-done((bf16[2,1,1,1,1,32,1024]{6,5,4,3,2,1,0:T(8,128)(2,1)S(1)}, bf16[2,1,1,1,1,32,1024]{6,5,4,3,2,1,0:T(8,128)(2,1)S(1)}, u32[]{:S(2)}, u32[]{:S(2)}) %collective-permute-start.1) | collective-permute-done | bytes 131104 | tf_op jit(solution)/shard_map/ppermute | solution.py:37
  53.1 6.7 %collective-permute-done.2 = bf16[2,2,1,1,1,32,1024]{6,5,4,3,2,1,0:T(8,128)(2,1)} collective-permute-done((bf16[2,2,1,1,1,32,1024]{6,5,4,3,2,1,0:T(8,128)(2,1)}, bf16[2,2,1,1,1,32,1024]{6,5,4,3,2,1,0:T(8,128)(2,1)}, u32[]{:S(2)}, u32[]{:S(2)}) %collective-permute-start.2) | collective-permute-done | bytes 262176 | tf_op jit(solution)/shard_map/ppermute | solution.py:37
  63.6 13.2 %collective-permute-done.7 = bf16[2,2,2,1,1,32,1024]{6,5,4,3,2,1,0:T(8,128)(2,1)S(1)} collective-permute-done((bf16[2,2,2,1,1,32,1024]{6,5,4,3,2,1,0:T(8,128)(2,1)}, bf16[2,2,2,1,1,32,1024]{6,5,4,3,2,1,0:T(8,128)(2,1)S(1)}, u32[]{:S(2)}, u32[]{:S(2)}) %collective-permute-start.7) | collective-permute-done | bytes 524320 | tf_op jit(solution)/shard_map/ppermute | solution.py:37
  79.8 23.6 %collective-permute-done.8 = bf16[2,2,2,2,1,32,1024]{6,5,4,3,2,1,0:T(8,128)(2,1)} collective-permute-done((bf16[2,2,2,2,1,32,1024]{6,5,4,3,2,1,0:T(8,128)(2,1)}, bf16[2,2,2,2,1,32,1024]{6,5,4,3,2,1,0:T(8,128)(2,1)}, u32[]{:S(2)}, u32[]{:S(2)}) %collective-permute-start.8) | collective-permute-done | bytes 1048608 | tf_op jit(solution)/shard_map/ppermute | solution.py:37
  104.7 4.3 %collective-permute-start.9 = (bf16[32,32,1024]{2,1,0:T(8,128)(2,1)S(1)}, bf16[32,32,1024]{2,1,0:T(8,128)(2,1)}, u32[]{:S(2)}, u32[]{:S(2)}) collective-permute-start(bf16[32,32,1024]{2,1,0:T(8,128)(2,1)S(1)} %bitcast.107), channel_id=1, source_target_pairs={{0,1},{1,0},{2,3},{3,2},{4,5},{5,4},{6,7},{7,6},{8,9},{9,8},{10,11... | collective-permute-start | bytes 6291464 | tf_op jit(solution)/shard_map/ppermute | solution.py:37
  119.4 3.3 %fusion.15 = bf16[1,560,1024]{2,1,0:T(8,128)(2,1)S(1)} fusion(bf16[560,1024]{1,0:T(8,128)(2,1)} %reshape.257, bf16[1024,1024]{1,0:T(8,128)(2,1)} %bitcast.113), kind=kOutput, calls=%fused_computation.16 | convolution fusion | flops 1174978560 | bytes 4390912 | tf_op jit(solution)/shard_map/dot_general | solution.py:243
  128.5 3.4 %fusion.80 = (f32[8,128]{1,0:T(8,128)S(1)}, f32[8,128,560]{1,2,0:T(8,128)}) fusion(pred[128,560]{0,1:T(8,128)(4,1)} %fusion.49, bf16[128,8,64]{0,2,1:T(8,128)(2,1)S(1)} %bitcast.133, bf16[560,8,64]{0,2,1:T(8,128)(2,1)} %bitcast.122), kind=kOutput, calls=%fused_computation.133 | convolution fusion | flops 75694640 | bytes 3074048 | tf_op jit(solution)/shard_map/sub | solution.py:157
  131.9 3.6 %fusion.81 = (bf16[1,560,8,64]{1,3,2,0:T(8,128)(2,1)}, f32[1,560,8,64]{1,3,2,0:T(8,128)}) fusion(bf16[128,8,64]{0,2,1:T(8,128)(2,1)S(1)} %bitcast.130, f32[8,128]{1,0:T(8,128)S(1)} %get-tuple-element.19, pred[128,560]{0,1:T(8,128)(4,1)} %fusion.49, bf16[128,8,64]{0,2,1:T(8,128)(2,1)S(1)} %bitcast.134, bf16[560,8,64]{0,2,1:T(8,128)(2,1)} %bitcast.123), kind=kOutput, calls=%fused_computation.134 | convolution fusion | flops 149956144 | bytes 2631680 | tf_op jit(solution)/shard_map/bhqk,bqhd->bkhd/dot_general | solution.py:184
  135.6 5.8 %fusion.82 = (bf16[1,560,8,64]{1,3,2,0:T(8,128)(2,1)}, f32[1,560,8,64]{1,3,2,0:T(8,128)}) fusion(bf16[128,8,64]{0,2,1:T(8,128)(2,1)S(1)} %bitcast.135, f32[8,128,560]{1,2,0:T(8,128)} %fusion.85, f32[8,128,560]{1,2,0:T(8,128)} %get-tuple-element.20, f32[8,128]{1,0:T(8,128)S(1)} %get-tuple-element.19), kind=kOutput, calls=%fused_computation.135 | convolution fusion | flops 77702704 | bytes 6443008 | tf_op jit(solution)/shard_map/bhqk,bqhd->bkhd/dot_general | solution.py:181
  151.6 3.8 %collective-permute-done.14 = f32[1024,512]{1,0:T(8,128)S(1)} collective-permute-done((f32[1024,512]{1,0:T(8,128)S(1)}, f32[1024,512]{1,0:T(8,128)S(1)}, u32[]{:S(2)}, u32[]{:S(2)}) %collective-permute-start.14) | collective-permute-done | bytes 2097184 | tf_op jit(solution)/shard_map/ppermute | solution.py:37
  163.7 3.0 %copy.22 = f32[1,560,8,64]{3,2,0,1:T(8,128)} copy(f32[1,560,8,64]{1,3,2,0:T(8,128)} %get-tuple-element.24) | data formatting | bytes 2293760 | tf_op jit(solution)/shard_map/bhqk,bqhd->bkhd/transpose | solution.py:184
  166.8 2.8 concatenate.24
  169.6 3.1 %copy.21 = f32[1,560,8,64]{3,2,0,1:T(8,128)} copy(f32[1,560,8,64]{1,3,2,0:T(8,128)} %get-tuple-element.26) | data formatting | bytes 2293760 | tf_op jit(solution)/shard_map/bhqk,bqhd->bkhd/transpose | solution.py:181
  172.7 3.6 %concatenate.23 = f32[1,20,28,512]{3,0,2,1:T(1,128)} reshape(f32[1,560,8,64]{3,2,0,1:T(8,128)} %copy.21) | data formatting | bytes 2293760 | tf_op jit(solution)/shard_map/concatenate | solution.py:188
  180.5 5.2 %collective-permute-start.10 = (f32[1,20,6,1024]{3,0,2,1:T(1,128)S(1)}, f32[1,20,6,1024]{3,0,2,1:T(1,128)S(1)}, u32[]{:S(2)}, u32[]{:S(2)}) collective-permute-start(f32[1,20,6,1024]{3,0,2,1:T(1,128)S(1)} %get-tuple-element.9), channel_id=1, source_target_pairs={{0,1},{1,2},{2,3},{3,4},{4,5},{5,6},{6,7},{7,8},{8,9},{9,10},{10,1... | collective-permute-start | bytes 1474568 | tf_op jit(solution)/shard_map/ppermute | solution.py:19
  193.5 3.3 %collective-permute-done.10 = f32[1,20,6,1024]{3,0,2,1:T(1,128)S(1)} collective-permute-done((f32[1,20,6,1024]{3,0,2,1:T(1,128)S(1)}, f32[1,20,6,1024]{3,0,2,1:T(1,128)S(1)}, u32[]{:S(2)}, u32[]{:S(2)}) %collective-permute-start.10) | collective-permute-done | bytes 491552 | tf_op jit(solution)/shard_map/ppermute | solution.py:19
  200.3 3.5 %collective-permute-start.12 = (f32[1,6,16,1024]{3,0,2,1:T(1,128)}, f32[1,6,16,1024]{3,0,2,1:T(1,128)}, u32[]{:S(2)}, u32[]{:S(2)}) collective-permute-start(f32[1,6,16,1024]{3,0,2,1:T(1,128)} %get-tuple-element.11), channel_id=1, source_target_pairs={{0,16},{16,32},{32,48},{48,64},{64,80},{80,96},{96,112},{112,128},... | collective-permute-start | bytes 1179656 | tf_op jit(solution)/shard_map/ppermute | solution.py:19
  205.1 4.5 %fusion.19 = bf16[8,64,128]{2,1,0:T(8,128)(2,1)S(1)} fusion(bf16[560,8,64]{0,2,1:T(8,128)(2,1)S(1)} %bitcast.125, f32[8,128,560]{1,2,0:T(8,128)} %fusion.85, f32[8,128,560]{1,2,0:T(8,128)} %get-tuple-element.20, f32[8,128]{1,0:T(8,128)S(1)} %get-tuple-element.19), kind=kOutput, calls=%fused_computation.24 | convolution fusion | flops 77481520 | bytes 5296128 | tf_op jit(solution)/shard_map/bhqk,bkhd->bqhd/dot_general | solution.py:178
  211.0 7.4 %collective-permute-start.17 = (f32[2,2,1,1,1,1,32,512]{7,6,5,4,3,2,1,0:T(8,128)S(1)}, f32[2,2,1,1,1,1,32,512]{7,6,5,4,3,2,1,0:T(8,128)S(1)}, u32[]{:S(2)}, u32[]{:S(2)}) collective-permute-start(f32[2,2,1,1,1,1,32,512]{7,6,5,4,3,2,1,0:T(8,128)S(1)} %constant_dynamic-slice_fusion.2), channel_id=1, source_target_pairs={{0,64},{16,80},{32,96},{48,112},{64,0},{80,16},{96,32},{112,48},{1... | collective-permute-start | bytes 786440 | tf_op jit(solution)/shard_map/ppermute | solution.py:37
  220.2 6.8 %collective-permute-done.17 = f32[2,2,1,1,1,1,32,512]{7,6,5,4,3,2,1,0:T(8,128)S(1)} collective-permute-done((f32[2,2,1,1,1,1,32,512]{7,6,5,4,3,2,1,0:T(8,128)S(1)}, f32[2,2,1,1,1,1,32,512]{7,6,5,4,3,2,1,0:T(8,128)S(1)}, u32[]{:S(2)}, u32[]{:S(2)}) %collective-permute-start.17) | collective-permute-done | bytes 262176 | tf_op jit(solution)/shard_map/ppermute | solution.py:37
  227.1 4.1 %collective-permute-start.18 = (f32[2,1,1,1,1,1,32,512]{7,6,5,4,3,2,1,0:T(8,128)S(1)}, f32[2,1,1,1,1,1,32,512]{7,6,5,4,3,2,1,0:T(8,128)S(1)}, u32[]{:S(2)}, u32[]{:S(2)}) collective-permute-start(f32[2,1,1,1,1,1,32,512]{7,6,5,4,3,2,1,0:T(8,128)S(1)} %constant_dynamic-slice_fusion.1), channel_id=1, source_target_pairs={{0,128},{16,144},{32,160},{48,176},{64,192},{80,208},{96,224},{112... | collective-permute-start | bytes 393224 | tf_op jit(solution)/shard_map/ppermute | solution.py:37
  232.0 8.3 %collective-permute-done.18 = f32[2,1,1,1,1,1,32,512]{7,6,5,4,3,2,1,0:T(8,128)S(1)} collective-permute-done((f32[2,1,1,1,1,1,32,512]{7,6,5,4,3,2,1,0:T(8,128)S(1)}, f32[2,1,1,1,1,1,32,512]{7,6,5,4,3,2,1,0:T(8,128)S(1)}, u32[]{:S(2)}, u32[]{:S(2)}) %collective-permute-start.18) | collective-permute-done | bytes 131104 | tf_op jit(solution)/shard_map/ppermute | solution.py:37
  240.3 5.6 %collective-permute-start.19 = (f32[1,1,1,1,1,1,32,512]{7,6,5,4,3,2,1,0:T(8,128)S(1)}, f32[1,1,1,1,1,1,32,512]{7,6,5,4,3,2,1,0:T(8,128)S(1)}, u32[]{:S(2)}, u32[]{:S(2)}) collective-permute-start(f32[1,1,1,1,1,1,32,512]{7,6,5,4,3,2,1,0:T(8,128)S(1)} %constant_dynamic-slice_fusion), channel_id=1, source_target_pairs={{0,256},{16,272},{32,288},{48,304},{64,320},{80,336},{96,352},{112... | collective-permute-start | bytes 196616 | tf_op jit(solution)/shard_map/ppermute | solution.py:37
  246.5 9.9 %collective-permute-done.19 = f32[1,1,1,1,1,1,32,512]{7,6,5,4,3,2,1,0:T(8,128)S(1)} collective-permute-done((f32[1,1,1,1,1,1,32,512]{7,6,5,4,3,2,1,0:T(8,128)S(1)}, f32[1,1,1,1,1,1,32,512]{7,6,5,4,3,2,1,0:T(8,128)S(1)}, u32[]{:S(2)}, u32[]{:S(2)}) %collective-permute-start.19) | collective-permute-done | bytes 65568 | tf_op jit(solution)/shard_map/ppermute | solution.py:37
  256.4 12.0 %collective-permute-start.20 = (f32[32,512]{1,0:T(8,128)S(1)}, f32[32,512]{1,0:T(8,128)S(1)}, u32[]{:S(2)}, u32[]{:S(2)}) collective-permute-start(f32[32,512]{1,0:T(8,128)S(1)} %add_bitcast_fusion), channel_id=1, source_target_pairs={{0,2},{1,3},{2,0},{3,1},{4,6},{5,7},{6,4},{7,5},{8,10},{9,11},{10,... | collective-permute-start | bytes 196616 | tf_op jit(solution)/shard_map/ppermute | solution.py:37
  270.0 6.1 %collective-permute-start.21 = (f32[32,512]{1,0:T(8,128)S(1)}, f32[32,512]{1,0:T(8,128)S(1)}, u32[]{:S(2)}, u32[]{:S(2)}) collective-permute-start(f32[32,512]{1,0:T(8,128)S(1)} %add.344), channel_id=1, source_target_pairs={{0,4},{1,5},{2,6},{3,7},{4,0},{5,1},{6,2},{7,3},{8,12},{9,13},{10,... | collective-permute-start | bytes 196616 | tf_op jit(solution)/shard_map/ppermute | solution.py:37
  277.8 4.9 %collective-permute-start.22 = (f32[32,512]{1,0:T(8,128)S(1)}, f32[32,512]{1,0:T(8,128)S(1)}, u32[]{:S(2)}, u32[]{:S(2)}) collective-permute-start(f32[32,512]{1,0:T(8,128)S(1)} %add.345), channel_id=1, source_target_pairs={{0,8},{1,9},{2,10},{3,11},{4,12},{5,13},{6,14},{7,15},{8,0},{9,1},... | collective-permute-start | bytes 196616 | tf_op jit(solution)/shard_map/ppermute | solution.py:37
  284.3 6.7 %collective-permute-start.23 = (f32[32,512]{1,0:T(8,128)S(1)}, f32[32,512]{1,0:T(8,128)S(1)}, u32[]{:S(2)}, u32[]{:S(2)}) collective-permute-start(f32[32,512]{1,0:T(8,128)S(1)} %add.346), channel_id=1, source_target_pairs={{0,1},{1,0},{2,3},{3,2},{4,5},{5,4},{6,7},{7,6},{8,9},{9,8},{10,11... | collective-permute-start | bytes 196616 | tf_op jit(solution)/shard_map/ppermute | solution.py:37
  (134 shorter events, 87.9 us)
Async XLA Ops:
  0.7 17.6 %copy-start = (bf16[1,8,16,1024]{3,2,1,0:T(8,128)(2,1)S(1)}, bf16[1,8,16,1024]{3,2,1,0:T(8,128)(2,1)}, u32[]{:S(2)}) copy-start(bf16[1,8,16,1024]{3,2,1,0:T(8,128)(2,1)} %param.6) | copy-start | bytes 786436
  0.7 17.9 %copy-start.10 = (f32[1024]{0:T(1024)S(1)}, f32[1024]{0:T(1024)}, u32[]{:S(2)}) copy-start(f32[1024]{0:T(1024)} %param.7) | copy-start | bytes 12292
  2.0 21.5 %collective-permute-start = (bf16[1,1,1,1,1,32,1024]{6,5,4,3,2,1,0:T(8,128)(2,1)S(1)}, bf16[1,1,1,1,1,32,1024]{6,5,4,3,2,1,0:T(8,128)(2,1)S(1)}, u32[]{:S(2)}, u32[]{:S(2)}) collective-permute-start(bf16[1,1,1,1,1,32,1024]{6,5,4,3,2,1,0:T(8,128)(2,1)S(1)} %constant_dynamic-slice_fusion.9), channel_id=1, source_target_pairs={{0,256},{16,272},{32,288},{48,304},{64,320},{80,336},{96,352},{112... | collective-permute-start | bytes 196616 | tf_op jit(solution)/shard_map/ppermute | solution.py:37
  18.9 11.5 %collective-permute-start.3 = (bf16[1,6,16,1024]{3,2,1,0:T(8,128)(2,1)S(1)}, bf16[1,6,16,1024]{3,2,1,0:T(8,128)(2,1)S(1)}, u32[]{:S(2)}, u32[]{:S(2)}) collective-permute-start(bf16[1,6,16,1024]{3,2,1,0:T(8,128)(2,1)S(1)} %get-tuple-element.17), channel_id=1, source_target_pairs={{0,16},{16,32},{32,48},{48,64},{64,80},{80,96},{96,112},{112,128},... | collective-permute-start | bytes 589832 | tf_op jit(solution)/shard_map/ppermute | solution.py:27
  22.1 8.3 %collective-permute-start.4 = (bf16[1,6,16,1024]{3,2,1,0:T(8,128)(2,1)S(1)}, bf16[1,6,16,1024]{3,2,1,0:T(8,128)(2,1)S(1)}, u32[]{:S(2)}, u32[]{:S(2)}) collective-permute-start(bf16[1,6,16,1024]{3,2,1,0:T(8,128)(2,1)S(1)} %get-tuple-element.18), channel_id=1, source_target_pairs={{16,0},{32,16},{48,32},{64,48},{80,64},{96,80},{112,96},{128,112},... | collective-permute-start | bytes 589832 | tf_op jit(solution)/shard_map/ppermute | solution.py:30
  23.5 19.5 %collective-permute-start.1 = (bf16[2,1,1,1,1,32,1024]{6,5,4,3,2,1,0:T(8,128)(2,1)S(1)}, bf16[2,1,1,1,1,32,1024]{6,5,4,3,2,1,0:T(8,128)(2,1)S(1)}, u32[]{:S(2)}, u32[]{:S(2)}) collective-permute-start(bf16[2,1,1,1,1,32,1024]{6,5,4,3,2,1,0:T(8,128)(2,1)S(1)} %constant_dynamic-slice_fusion.8), channel_id=1, source_target_pairs={{0,128},{16,144},{32,160},{48,176},{64,192},{80,208},{96,224},{112... | collective-permute-start | bytes 393224 | tf_op jit(solution)/shard_map/ppermute | solution.py:37
  31.4 14.5 %collective-permute-start.5 = (bf16[1,20,6,1024]{3,2,1,0:T(8,128)(2,1)}, bf16[1,20,6,1024]{3,2,1,0:T(8,128)(2,1)S(1)}, u32[]{:S(2)}, u32[]{:S(2)}) collective-permute-start(bf16[1,20,6,1024]{3,2,1,0:T(8,128)(2,1)} %get-tuple-element.15), channel_id=1, source_target_pairs={{0,1},{1,2},{2,3},{3,4},{4,5},{5,6},{6,7},{7,8},{8,9},{9,10},{10,1... | collective-permute-start | bytes 737288 | tf_op jit(solution)/shard_map/ppermute | solution.py:27
  37.9 10.2 %collective-permute-start.6 = (bf16[1,20,6,1024]{3,2,1,0:T(8,128)(2,1)}, bf16[1,20,6,1024]{3,2,1,0:T(8,128)(2,1)}, u32[]{:S(2)}, u32[]{:S(2)}) collective-permute-start(bf16[1,20,6,1024]{3,2,1,0:T(8,128)(2,1)} %get-tuple-element.16), channel_id=1, source_target_pairs={{1,0},{2,1},{3,2},{4,3},{5,4},{6,5},{7,6},{8,7},{9,8},{10,9},{11,1... | collective-permute-start | bytes 737288 | tf_op jit(solution)/shard_map/ppermute | solution.py:30
  43.7 16.0 %collective-permute-start.2 = (bf16[2,2,1,1,1,32,1024]{6,5,4,3,2,1,0:T(8,128)(2,1)}, bf16[2,2,1,1,1,32,1024]{6,5,4,3,2,1,0:T(8,128)(2,1)}, u32[]{:S(2)}, u32[]{:S(2)}) collective-permute-start(bf16[2,2,1,1,1,32,1024]{6,5,4,3,2,1,0:T(8,128)(2,1)} %constant_dynamic-slice_fusion.7), channel_id=1, source_target_pairs={{0,64},{16,80},{32,96},{48,112},{64,0},{80,16},{96,32},{112,48},{1... | collective-permute-start | bytes 786440 | tf_op jit(solution)/shard_map/ppermute | solution.py:37
  61.6 15.1 %collective-permute-start.7 = (bf16[2,2,2,1,1,32,1024]{6,5,4,3,2,1,0:T(8,128)(2,1)}, bf16[2,2,2,1,1,32,1024]{6,5,4,3,2,1,0:T(8,128)(2,1)S(1)}, u32[]{:S(2)}, u32[]{:S(2)}) collective-permute-start(bf16[2,2,2,1,1,32,1024]{6,5,4,3,2,1,0:T(8,128)(2,1)} %constant_dynamic-slice_fusion.6), channel_id=1, source_target_pairs={{0,32},{16,48},{32,0},{48,16},{64,96},{80,112},{96,64},{112,80},{1... | collective-permute-start | bytes 1572872 | tf_op jit(solution)/shard_map/ppermute | solution.py:37
  77.9 25.5 %collective-permute-start.8 = (bf16[2,2,2,2,1,32,1024]{6,5,4,3,2,1,0:T(8,128)(2,1)}, bf16[2,2,2,2,1,32,1024]{6,5,4,3,2,1,0:T(8,128)(2,1)}, u32[]{:S(2)}, u32[]{:S(2)}) collective-permute-start(bf16[2,2,2,2,1,32,1024]{6,5,4,3,2,1,0:T(8,128)(2,1)} %constant_dynamic-slice_fusion.5), channel_id=1, source_target_pairs={{0,16},{16,0},{32,48},{48,32},{64,80},{80,64},{96,112},{112,96},{1... | collective-permute-start | bytes 3145736 | tf_op jit(solution)/shard_map/ppermute | solution.py:37
  104.7 8.1 %collective-permute-start.9 = (bf16[32,32,1024]{2,1,0:T(8,128)(2,1)S(1)}, bf16[32,32,1024]{2,1,0:T(8,128)(2,1)}, u32[]{:S(2)}, u32[]{:S(2)}) collective-permute-start(bf16[32,32,1024]{2,1,0:T(8,128)(2,1)S(1)} %bitcast.107), channel_id=1, source_target_pairs={{0,1},{1,0},{2,3},{3,2},{4,5},{5,4},{6,7},{7,6},{8,9},{9,8},{10,11... | collective-permute-start | bytes 6291464 | tf_op jit(solution)/shard_map/ppermute | solution.py:37
  149.3 6.1 %collective-permute-start.14 = (f32[1024,512]{1,0:T(8,128)S(1)}, f32[1024,512]{1,0:T(8,128)S(1)}, u32[]{:S(2)}, u32[]{:S(2)}) collective-permute-start(f32[1024,512]{1,0:T(8,128)S(1)} %dynamic-slice_bitcast_fusion), channel_id=1, source_target_pairs={{0,1},{1,0},{2,3},{3,2},{4,5},{5,4},{6,7},{7,6},{8,9},{9,8},{10,11... | collective-permute-start | bytes 6291464 | tf_op jit(solution)/shard_map/ppermute | solution.py:37
  158.2 30.5 %collective-permute-start.15 = (f32[2,2,2,2,1,1,32,512]{7,6,5,4,3,2,1,0:T(8,128)}, f32[2,2,2,2,1,1,32,512]{7,6,5,4,3,2,1,0:T(8,128)}, u32[]{:S(2)}, u32[]{:S(2)}) collective-permute-start(f32[2,2,2,2,1,1,32,512]{7,6,5,4,3,2,1,0:T(8,128)} %constant_dynamic-slice_fusion.4), channel_id=1, source_target_pairs={{0,16},{16,0},{32,48},{48,32},{64,80},{80,64},{96,112},{112,96},{1... | collective-permute-start | bytes 3145736 | tf_op jit(solution)/shard_map/ppermute | solution.py:37
  178.8 8.9 %copy-start.9 = (bf16[8,16,512]{2,1,0:T(8,128)(2,1)S(1)}, bf16[8,16,512]{2,1,0:T(8,128)(2,1)}, u32[]{:S(2)}) copy-start(bf16[8,16,512]{2,1,0:T(8,128)(2,1)} %reshape.264) | copy-start | bytes 393220
  179.8 8.9 %copy-start.2 = (f32[1024,512]{1,0:T(8,128)S(1)}, f32[1024,512]{1,0:T(8,128)}, u32[]{:S(2)}) copy-start(f32[1024,512]{1,0:T(8,128)} %copy-done.1) | copy-start | bytes 6291460
  180.5 16.3 %collective-permute-start.10 = (f32[1,20,6,1024]{3,0,2,1:T(1,128)S(1)}, f32[1,20,6,1024]{3,0,2,1:T(1,128)S(1)}, u32[]{:S(2)}, u32[]{:S(2)}) collective-permute-start(f32[1,20,6,1024]{3,0,2,1:T(1,128)S(1)} %get-tuple-element.9), channel_id=1, source_target_pairs={{0,1},{1,2},{2,3},{3,4},{4,5},{5,6},{6,7},{7,8},{8,9},{9,10},{10,1... | collective-permute-start | bytes 1474568 | tf_op jit(solution)/shard_map/ppermute | solution.py:19
  185.7 11.7 %collective-permute-start.11 = (f32[1,20,6,1024]{3,0,2,1:T(1,128)S(1)}, f32[1,20,6,1024]{3,0,2,1:T(1,128)S(1)}, u32[]{:S(2)}, u32[]{:S(2)}) collective-permute-start(f32[1,20,6,1024]{3,0,2,1:T(1,128)S(1)} %get-tuple-element.10), channel_id=1, source_target_pairs={{1,0},{2,1},{3,2},{4,3},{5,4},{6,5},{7,6},{8,7},{9,8},{10,9},{11,1... | collective-permute-start | bytes 1474568 | tf_op jit(solution)/shard_map/ppermute | solution.py:19
  190.1 6.6 %copy-start.4 = (f32[2,2,2,2,1,1,32,512]{7,6,5,4,3,2,1,0:T(8,128)}, f32[2,2,2,2,1,1,32,512]{7,6,5,4,3,2,1,0:T(8,128)S(1)}, u32[]{:S(2)}) copy-start(f32[2,2,2,2,1,1,32,512]{7,6,5,4,3,2,1,0:T(8,128)S(1)} %dynamic-slice_add_fusion) | copy-start | bytes 3145732
  191.1 14.0 %copy-start.8 = (bf16[1,560,512]{1,2,0:T(8,128)(2,1)S(1)}, bf16[1,560,512]{1,2,0:T(8,128)(2,1)}, u32[]{:S(2)}) copy-start(bf16[1,560,512]{1,2,0:T(8,128)(2,1)} %copy.19) | copy-start | bytes 1720324
  191.1 18.5 %collective-permute-start.16 = (f32[2,2,2,1,1,1,32,512]{7,6,5,4,3,2,1,0:T(8,128)}, f32[2,2,2,1,1,1,32,512]{7,6,5,4,3,2,1,0:T(8,128)}, u32[]{:S(2)}, u32[]{:S(2)}) collective-permute-start(f32[2,2,2,1,1,1,32,512]{7,6,5,4,3,2,1,0:T(8,128)} %constant_dynamic-slice_fusion.3), channel_id=1, source_target_pairs={{0,32},{16,48},{32,0},{48,16},{64,96},{80,112},{96,64},{112,80},{1... | collective-permute-start | bytes 1572872 | tf_op jit(solution)/shard_map/ppermute | solution.py:37
  200.3 18.1 %collective-permute-start.12 = (f32[1,6,16,1024]{3,0,2,1:T(1,128)}, f32[1,6,16,1024]{3,0,2,1:T(1,128)}, u32[]{:S(2)}, u32[]{:S(2)}) collective-permute-start(f32[1,6,16,1024]{3,0,2,1:T(1,128)} %get-tuple-element.11), channel_id=1, source_target_pairs={{0,16},{16,32},{32,48},{48,64},{64,80},{80,96},{96,112},{112,128},... | collective-permute-start | bytes 1179656 | tf_op jit(solution)/shard_map/ppermute | solution.py:19
  203.8 14.6 %collective-permute-start.13 = (f32[1,6,16,1024]{3,0,2,1:T(1,128)}, f32[1,6,16,1024]{3,0,2,1:T(1,128)}, u32[]{:S(2)}, u32[]{:S(2)}) collective-permute-start(f32[1,6,16,1024]{3,0,2,1:T(1,128)} %get-tuple-element.12), channel_id=1, source_target_pairs={{16,0},{32,16},{48,32},{64,48},{80,64},{96,80},{112,96},{128,112},... | collective-permute-start | bytes 1179656 | tf_op jit(solution)/shard_map/ppermute | solution.py:19
  210.9 20.2 %copy-start.3 = (bf16[1,32,32,1024]{3,2,1,0:T(8,128)(2,1)S(1)}, bf16[1,32,32,1024]{3,2,1,0:T(8,128)(2,1)}, u32[]{:S(2)}) copy-start(bf16[1,32,32,1024]{3,2,1,0:T(8,128)(2,1)} %slice.66) | copy-start | bytes 6291460
  211.0 16.0 %collective-permute-start.17 = (f32[2,2,1,1,1,1,32,512]{7,6,5,4,3,2,1,0:T(8,128)S(1)}, f32[2,2,1,1,1,1,32,512]{7,6,5,4,3,2,1,0:T(8,128)S(1)}, u32[]{:S(2)}, u32[]{:S(2)}) collective-permute-start(f32[2,2,1,1,1,1,32,512]{7,6,5,4,3,2,1,0:T(8,128)S(1)} %constant_dynamic-slice_fusion.2), channel_id=1, source_target_pairs={{0,64},{16,80},{32,96},{48,112},{64,0},{80,16},{96,32},{112,48},{1... | collective-permute-start | bytes 786440 | tf_op jit(solution)/shard_map/ppermute | solution.py:37
  227.1 13.2 %collective-permute-start.18 = (f32[2,1,1,1,1,1,32,512]{7,6,5,4,3,2,1,0:T(8,128)S(1)}, f32[2,1,1,1,1,1,32,512]{7,6,5,4,3,2,1,0:T(8,128)S(1)}, u32[]{:S(2)}, u32[]{:S(2)}) collective-permute-start(f32[2,1,1,1,1,1,32,512]{7,6,5,4,3,2,1,0:T(8,128)S(1)} %constant_dynamic-slice_fusion.1), channel_id=1, source_target_pairs={{0,128},{16,144},{32,160},{48,176},{64,192},{80,208},{96,224},{112... | collective-permute-start | bytes 393224 | tf_op jit(solution)/shard_map/ppermute | solution.py:37
  232.0 59.1 %copy-start.7 = (bf16[1,8,16,1024]{3,2,1,0:T(8,128)(2,1)S(1)}, bf16[1,8,16,1024]{3,2,1,0:T(8,128)(2,1)}, u32[]{:S(2)}) copy-start(bf16[1,8,16,1024]{3,2,1,0:T(8,128)(2,1)} %param.11) | copy-start | bytes 786436
  240.3 16.0 %collective-permute-start.19 = (f32[1,1,1,1,1,1,32,512]{7,6,5,4,3,2,1,0:T(8,128)S(1)}, f32[1,1,1,1,1,1,32,512]{7,6,5,4,3,2,1,0:T(8,128)S(1)}, u32[]{:S(2)}, u32[]{:S(2)}) collective-permute-start(f32[1,1,1,1,1,1,32,512]{7,6,5,4,3,2,1,0:T(8,128)S(1)} %constant_dynamic-slice_fusion), channel_id=1, source_target_pairs={{0,256},{16,272},{32,288},{48,304},{64,320},{80,336},{96,352},{112... | collective-permute-start | bytes 196616 | tf_op jit(solution)/shard_map/ppermute | solution.py:37
  256.4 13.6 %collective-permute-start.20 = (f32[32,512]{1,0:T(8,128)S(1)}, f32[32,512]{1,0:T(8,128)S(1)}, u32[]{:S(2)}, u32[]{:S(2)}) collective-permute-start(f32[32,512]{1,0:T(8,128)S(1)} %add_bitcast_fusion), channel_id=1, source_target_pairs={{0,2},{1,3},{2,0},{3,1},{4,6},{5,7},{6,4},{7,5},{8,10},{9,11},{10,... | collective-permute-start | bytes 196616 | tf_op jit(solution)/shard_map/ppermute | solution.py:37
  270.0 7.8 %collective-permute-start.21 = (f32[32,512]{1,0:T(8,128)S(1)}, f32[32,512]{1,0:T(8,128)S(1)}, u32[]{:S(2)}, u32[]{:S(2)}) collective-permute-start(f32[32,512]{1,0:T(8,128)S(1)} %add.344), channel_id=1, source_target_pairs={{0,4},{1,5},{2,6},{3,7},{4,0},{5,1},{6,2},{7,3},{8,12},{9,13},{10,... | collective-permute-start | bytes 196616 | tf_op jit(solution)/shard_map/ppermute | solution.py:37
  277.8 6.5 %collective-permute-start.22 = (f32[32,512]{1,0:T(8,128)S(1)}, f32[32,512]{1,0:T(8,128)S(1)}, u32[]{:S(2)}, u32[]{:S(2)}) collective-permute-start(f32[32,512]{1,0:T(8,128)S(1)} %add.345), channel_id=1, source_target_pairs={{0,8},{1,9},{2,10},{3,11},{4,12},{5,13},{6,14},{7,15},{8,0},{9,1},... | collective-permute-start | bytes 196616 | tf_op jit(solution)/shard_map/ppermute | solution.py:37
  284.3 8.5 %collective-permute-start.23 = (f32[32,512]{1,0:T(8,128)S(1)}, f32[32,512]{1,0:T(8,128)S(1)}, u32[]{:S(2)}, u32[]{:S(2)}) collective-permute-start(f32[32,512]{1,0:T(8,128)S(1)} %add.346), channel_id=1, source_target_pairs={{0,1},{1,0},{2,3},{3,2},{4,5},{5,4},{6,7},{7,6},{8,9},{9,8},{10,11... | collective-permute-start | bytes 196616 | tf_op jit(solution)/shard_map/ppermute | solution.py:37
  (5 other events, 8.8 us)

commit v14 on v13

--- a/solution.py
+++ b/solution.py
@@ -104,14 +104,13 @@
     own = axis_bit("col", 0)
     packed = jnp.where(own == 0, w_keyvalue, qo_pack)
     fetched, tie = gather_by_bits(packed, "row", row_groups, tie=tie)
-    held = jnp.zeros((2,) + fetched.shape, fetched.dtype)
-    held = lax.dynamic_update_slice(held, fetched[None], (own, 0, 0, 0))
-    held = lax.dynamic_update_slice(held, partner_swap(fetched, "col", 1)[None], (1 - own, 0, 0, 0))
+    swapped = partner_swap(fetched, "col", 1)
     count = fetched.shape[0]
     query_rows = kv_rows - out_rows
-    kv = held[0].reshape(count * kv_rows, kv_width)
-    query = held[1, :, :query_rows].reshape(count * rows, width)
-    output = held[1, :, query_rows:].reshape(count * out_rows, kv_width)
+    kv = jnp.where(own == 0, fetched, swapped).reshape(count * kv_rows, kv_width)
+    qo = jnp.where(own == 0, swapped, fetched)
+    query = qo[:, :query_rows].reshape(count * rows, width)
+    output = qo[:, query_rows:].reshape(count * out_rows, kv_width)
     return query, kv, output, tie
 
 

time: 296 us -> 300 us (1.014)
  other arithmetic: 13.5 us -> 18.9 us
    select_n x0 -> x1, other arithmetic: none -> 3.19 us  [gather_weights(): qo = jnp.where(own == 0, swapped, fetched)]
  transfers between devices with their start and end apart: 24 -> 24, of which waited for: 15 -> 15; matrix products, arithmetic and copies ran while one was open for 16% -> 15% of each run, Pallas kernels for 0% -> 0%
where the time goes in v14:
time: 300 us; the launch traced here: 299 us
  starting transfers between devices  112 us (37%)
  waiting for transfers between devices  89.1 us (30%)
  local copies, waits for them, and re-layouts  47.4 us (16%)
  matrix products  30.1 us (10%)
  other arithmetic  18.9 us (6%)
    ppermute x16, starting transfers between devices, partner_swap(): return lax.ppermute(value, axis, [(i, i ^ mask) for i in range(count)])  87 us
    ppermute x16, waiting for transfers between devices, partner_swap(): return lax.ppermute(value, axis, [(i, i ^ mask) for i in range(count)])  82.9 us
    ppermute x4, starting transfers between devices, shifted(): lax.ppermute(value, axis, [(source, source + steps) for source in range(f...  11.9 us
    ppermute x2, starting transfers between devices, with_halo(): lax.ppermute(lax.slice_in_dim(block, block.shape[dim] - width, None, axis...  9.7 us
    concatenate x3, local copies, waits for them, and re-layouts, tile_backward(): jnp.concatenate([key_grad.reshape(batches, ext_count, inner_width), value...  7.45 us
  transfers between devices with their start and end apart: 24, of which 15 were waited for; matrix products, arithmetic and copies ran while one was open for 15% of the time, Pallas kernels for 0%

profile of v14, /device:TPU:1, one launch (start us, length us, event | category | flops | bytes accessed | tf_op | source)
XLA Modules:
  0.0 299.0 jit_solution(4516381992190905073)
XLA Ops:
  2.0 16.3 %collective-permute-start = (bf16[1,1,1,1,1,32,1024]{6,5,4,3,2,1,0:T(8,128)(2,1)S(1)}, bf16[1,1,1,1,1,32,1024]{6,5,4,3,2,1,0:T(8,128)(2,1)S(1)}, u32[]{:S(2)}, u32[]{:S(2)}) collective-permute-start(bf16[1,1,1,1,1,32,1024]{6,5,4,3,2,1,0:T(8,128)(2,1)S(1)} %constant_dynamic-slice_fusion.9), channel_id=1, source_target_pairs={{0,256},{16,272},{32,288},{48,304},{64,320},{80,336},{96,352},{112... | collective-permute-start | bytes 196616 | tf_op jit(solution)/shard_map/ppermute | solution.py:37
  18.9 3.2 %collective-permute-start.3 = (bf16[1,6,16,1024]{3,2,1,0:T(8,128)(2,1)S(1)}, bf16[1,6,16,1024]{3,2,1,0:T(8,128)(2,1)S(1)}, u32[]{:S(2)}, u32[]{:S(2)}) collective-permute-start(bf16[1,6,16,1024]{3,2,1,0:T(8,128)(2,1)S(1)} %get-tuple-element.19), channel_id=1, source_target_pairs={{0,16},{16,32},{32,48},{48,64},{64,80},{80,96},{96,112},{112,128},... | collective-permute-start | bytes 589832 | tf_op jit(solution)/shard_map/ppermute | solution.py:27
  23.5 6.9 %collective-permute-start.1 = (bf16[2,1,1,1,1,32,1024]{6,5,4,3,2,1,0:T(8,128)(2,1)S(1)}, bf16[2,1,1,1,1,32,1024]{6,5,4,3,2,1,0:T(8,128)(2,1)S(1)}, u32[]{:S(2)}, u32[]{:S(2)}) collective-permute-start(bf16[2,1,1,1,1,32,1024]{6,5,4,3,2,1,0:T(8,128)(2,1)S(1)} %constant_dynamic-slice_fusion.8), channel_id=1, source_target_pairs={{0,128},{16,144},{32,160},{48,176},{64,192},{80,208},{96,224},{112... | collective-permute-start | bytes 393224 | tf_op jit(solution)/shard_map/ppermute | solution.py:37
  31.5 6.5 %collective-permute-start.5 = (bf16[1,20,6,1024]{3,2,1,0:T(8,128)(2,1)}, bf16[1,20,6,1024]{3,2,1,0:T(8,128)(2,1)S(1)}, u32[]{:S(2)}, u32[]{:S(2)}) collective-permute-start(bf16[1,20,6,1024]{3,2,1,0:T(8,128)(2,1)} %get-tuple-element.17), channel_id=1, source_target_pairs={{0,1},{1,2},{2,3},{3,4},{4,5},{5,6},{6,7},{7,8},{8,9},{9,10},{10,1... | collective-permute-start | bytes 737288 | tf_op jit(solution)/shard_map/ppermute | solution.py:27
  39.9 3.1 %collective-permute-done.1 = bf16[2,1,1,1,1,32,1024]{6,5,4,3,2,1,0:T(8,128)(2,1)S(1)} collective-permute-done((bf16[2,1,1,1,1,32,1024]{6,5,4,3,2,1,0:T(8,128)(2,1)S(1)}, bf16[2,1,1,1,1,32,1024]{6,5,4,3,2,1,0:T(8,128)(2,1)S(1)}, u32[]{:S(2)}, u32[]{:S(2)}) %collective-permute-start.1) | collective-permute-done | bytes 131104 | tf_op jit(solution)/shard_map/ppermute | solution.py:37
  53.1 6.7 %collective-permute-done.2 = bf16[2,2,1,1,1,32,1024]{6,5,4,3,2,1,0:T(8,128)(2,1)} collective-permute-done((bf16[2,2,1,1,1,32,1024]{6,5,4,3,2,1,0:T(8,128)(2,1)}, bf16[2,2,1,1,1,32,1024]{6,5,4,3,2,1,0:T(8,128)(2,1)}, u32[]{:S(2)}, u32[]{:S(2)}) %collective-permute-start.2) | collective-permute-done | bytes 262176 | tf_op jit(solution)/shard_map/ppermute | solution.py:37
  63.6 13.2 %collective-permute-done.7 = bf16[2,2,2,1,1,32,1024]{6,5,4,3,2,1,0:T(8,128)(2,1)S(1)} collective-permute-done((bf16[2,2,2,1,1,32,1024]{6,5,4,3,2,1,0:T(8,128)(2,1)}, bf16[2,2,2,1,1,32,1024]{6,5,4,3,2,1,0:T(8,128)(2,1)S(1)}, u32[]{:S(2)}, u32[]{:S(2)}) %collective-permute-start.7) | collective-permute-done | bytes 524320 | tf_op jit(solution)/shard_map/ppermute | solution.py:37
  79.9 23.6 %collective-permute-done.8 = bf16[2,2,2,2,1,32,1024]{6,5,4,3,2,1,0:T(8,128)(2,1)} collective-permute-done((bf16[2,2,2,2,1,32,1024]{6,5,4,3,2,1,0:T(8,128)(2,1)}, bf16[2,2,2,2,1,32,1024]{6,5,4,3,2,1,0:T(8,128)(2,1)}, u32[]{:S(2)}, u32[]{:S(2)}) %collective-permute-start.8) | collective-permute-done | bytes 1048608 | tf_op jit(solution)/shard_map/ppermute | solution.py:37
  104.8 4.3 %collective-permute-start.9 = (bf16[32,32,1024]{2,1,0:T(8,128)(2,1)S(1)}, bf16[32,32,1024]{2,1,0:T(8,128)(2,1)}, u32[]{:S(2)}, u32[]{:S(2)}) collective-permute-start(bf16[32,32,1024]{2,1,0:T(8,128)(2,1)S(1)} %bitcast.104), channel_id=1, source_target_pairs={{0,1},{1,0},{2,3},{3,2},{4,5},{5,4},{6,7},{7,6},{8,9},{9,8},{10,11... | collective-permute-start | bytes 6291464 | tf_op jit(solution)/shard_map/ppermute | solution.py:37
  112.9 3.2 %broadcast_select_fusion = (bf16[32,32,1024]{2,1,0:T(8,128)(2,1)S(1)}, bf16[32,32,1024]{2,1,0:T(8,128)(2,1)}) fusion(bf16[32,32,1024]{2,1,0:T(8,128)(2,1)} %collective-permute-done.9, pred[]{:T(512)S(6)} %eq.32, bf16[2,2,2,2,2,32,1024]{6,5,4,3,2,1,0:T(8,128)(2,1)S(1)} %constant_dynamic-update-slice_fusion.2), kind=kLoop, calls=%fused_computation.9 | loop fusion | flops 2097152 | bytes 8388609 | tf_op jit(solution)/shard_map/jit(_where)/select_n | solution.py:111
  119.1 3.3 %fusion.15 = bf16[1,560,1024]{2,1,0:T(8,128)(2,1)S(1)} fusion(bf16[560,1024]{1,0:T(8,128)(2,1)} %reshape.266, bf16[1024,1024]{1,0:T(8,128)(2,1)} %bitcast.109), kind=kOutput, calls=%fused_computation.17 | convolution fusion | flops 1174978560 | bytes 4390912 | tf_op jit(solution)/shard_map/dot_general | solution.py:242
  128.3 3.5 %fusion.80 = (f32[8,128]{1,0:T(8,128)S(1)}, f32[8,128,560]{1,2,0:T(8,128)}) fusion(pred[128,560]{0,1:T(8,128)(4,1)S(1)} %copy-done.11, bf16[128,8,64]{0,2,1:T(8,128)(2,1)S(1)} %bitcast.129, bf16[560,8,64]{0,2,1:T(8,128)(2,1)} %bitcast.118), kind=kOutput, calls=%fused_computation.133 | convolution fusion | flops 75694640 | bytes 3074048 | tf_op jit(solution)/shard_map/sub | solution.py:156
  131.7 3.6 %fusion.81 = (bf16[1,560,8,64]{1,3,2,0:T(8,128)(2,1)}, f32[1,560,8,64]{1,3,2,0:T(8,128)}) fusion(bf16[128,8,64]{0,2,1:T(8,128)(2,1)S(1)} %bitcast.126, f32[8,128]{1,0:T(8,128)S(1)} %get-tuple-element.21, pred[128,560]{0,1:T(8,128)(4,1)S(1)} %copy-done.11, bf16[128,8,64]{0,2,1:T(8,128)(2,1)S(1)} %bitcast.130, bf16[560,8,64]{0,2,1:T(8,128)(2,1)} %bitcast.119), kind=kOutput, calls=%fused_computation.134 | convolution fusion | flops 149956144 | bytes 2631680 | tf_op jit(solution)/shard_map/bhqk,bqhd->bkhd/dot_general | solution.py:183
  135.4 5.8 %fusion.82 = (bf16[1,560,8,64]{1,3,2,0:T(8,128)(2,1)}, f32[1,560,8,64]{1,3,2,0:T(8,128)}) fusion(bf16[128,8,64]{0,2,1:T(8,128)(2,1)S(1)} %bitcast.131, f32[8,128,560]{1,2,0:T(8,128)} %fusion.85, f32[8,128,560]{1,2,0:T(8,128)} %get-tuple-element.22, f32[8,128]{1,0:T(8,128)S(1)} %get-tuple-element.21), kind=kOutput, calls=%fused_computation.135 | convolution fusion | flops 77702704 | bytes 6443008 | tf_op jit(solution)/shard_map/bhqk,bqhd->bkhd/dot_general | solution.py:180
  153.8 4.1 %collective-permute-done.14 = f32[1024,512]{1,0:T(8,128)} collective-permute-done((f32[1024,512]{1,0:T(8,128)}, f32[1024,512]{1,0:T(8,128)}, u32[]{:S(2)}, u32[]{:S(2)}) %collective-permute-start.14) | collective-permute-done | bytes 2097184 | tf_op jit(solution)/shard_map/ppermute | solution.py:37
  168.6 3.0 %copy.22 = f32[1,560,8,64]{3,2,0,1:T(8,128)} copy(f32[1,560,8,64]{1,3,2,0:T(8,128)} %get-tuple-element.26) | data formatting | bytes 2293760 | tf_op jit(solution)/shard_map/bhqk,bqhd->bkhd/transpose | solution.py:183
  174.4 3.0 %copy.21 = f32[1,560,8,64]{3,2,0,1:T(8,128)} copy(f32[1,560,8,64]{1,3,2,0:T(8,128)} %get-tuple-element.28) | data formatting | bytes 2293760 | tf_op jit(solution)/shard_map/bhqk,bqhd->bkhd/transpose | solution.py:180
  177.5 3.6 %concatenate.23 = f32[1,20,28,512]{3,0,2,1:T(1,128)} reshape(f32[1,560,8,64]{3,2,0,1:T(8,128)} %copy.21) | data formatting | bytes 2293760 | tf_op jit(solution)/shard_map/concatenate | solution.py:187
  185.3 5.2 %collective-permute-start.10 = (f32[1,20,6,1024]{3,0,2,1:T(1,128)S(1)}, f32[1,20,6,1024]{3,0,2,1:T(1,128)S(1)}, u32[]{:S(2)}, u32[]{:S(2)}) collective-permute-start(f32[1,20,6,1024]{3,0,2,1:T(1,128)S(1)} %get-tuple-element.9), channel_id=1, source_target_pairs={{0,1},{1,2},{2,3},{3,4},{4,5},{5,6},{6,7},{7,8},{8,9},{9,10},{10,1... | collective-permute-start | bytes 1474568 | tf_op jit(solution)/shard_map/ppermute | solution.py:19
  198.2 3.3 %collective-permute-done.10 = f32[1,20,6,1024]{3,0,2,1:T(1,128)S(1)} collective-permute-done((f32[1,20,6,1024]{3,0,2,1:T(1,128)S(1)}, f32[1,20,6,1024]{3,0,2,1:T(1,128)S(1)}, u32[]{:S(2)}, u32[]{:S(2)}) %collective-permute-start.10) | collective-permute-done | bytes 491552 | tf_op jit(solution)/shard_map/ppermute | solution.py:19
  205.0 3.5 %collective-permute-start.12 = (f32[1,6,16,1024]{3,0,2,1:T(1,128)}, f32[1,6,16,1024]{3,0,2,1:T(1,128)}, u32[]{:S(2)}, u32[]{:S(2)}) collective-permute-start(f32[1,6,16,1024]{3,0,2,1:T(1,128)} %get-tuple-element.13), channel_id=1, source_target_pairs={{0,16},{16,32},{32,48},{48,64},{64,80},{80,96},{96,112},{112,128},... | collective-permute-start | bytes 1179656 | tf_op jit(solution)/shard_map/ppermute | solution.py:19
  209.8 4.6 %fusion.19 = bf16[8,64,128]{2,1,0:T(8,128)(2,1)S(1)} fusion(bf16[560,8,64]{0,2,1:T(8,128)(2,1)S(1)} %bitcast.121, f32[8,128,560]{1,2,0:T(8,128)} %fusion.85, f32[8,128,560]{1,2,0:T(8,128)} %get-tuple-element.22, f32[8,128]{1,0:T(8,128)S(1)} %get-tuple-element.21), kind=kOutput, calls=%fused_computation.25 | convolution fusion | flops 77481520 | bytes 5296128 | tf_op jit(solution)/shard_map/bhqk,bkhd->bqhd/dot_general | solution.py:177
  215.8 7.4 %collective-permute-start.17 = (f32[2,2,1,1,1,1,32,512]{7,6,5,4,3,2,1,0:T(8,128)S(1)}, f32[2,2,1,1,1,1,32,512]{7,6,5,4,3,2,1,0:T(8,128)S(1)}, u32[]{:S(2)}, u32[]{:S(2)}) collective-permute-start(f32[2,2,1,1,1,1,32,512]{7,6,5,4,3,2,1,0:T(8,128)S(1)} %constant_dynamic-slice_fusion.2), channel_id=1, source_target_pairs={{0,64},{16,80},{32,96},{48,112},{64,0},{80,16},{96,32},{112,48},{1... | collective-permute-start | bytes 786440 | tf_op jit(solution)/shard_map/ppermute | solution.py:37
  225.1 6.8 %collective-permute-done.17 = f32[2,2,1,1,1,1,32,512]{7,6,5,4,3,2,1,0:T(8,128)S(1)} collective-permute-done((f32[2,2,1,1,1,1,32,512]{7,6,5,4,3,2,1,0:T(8,128)S(1)}, f32[2,2,1,1,1,1,32,512]{7,6,5,4,3,2,1,0:T(8,128)S(1)}, u32[]{:S(2)}, u32[]{:S(2)}) %collective-permute-start.17) | collective-permute-done | bytes 262176 | tf_op jit(solution)/shard_map/ppermute | solution.py:37
  231.9 4.0 %collective-permute-start.18 = (f32[2,1,1,1,1,1,32,512]{7,6,5,4,3,2,1,0:T(8,128)S(1)}, f32[2,1,1,1,1,1,32,512]{7,6,5,4,3,2,1,0:T(8,128)S(1)}, u32[]{:S(2)}, u32[]{:S(2)}) collective-permute-start(f32[2,1,1,1,1,1,32,512]{7,6,5,4,3,2,1,0:T(8,128)S(1)} %constant_dynamic-slice_fusion.1), channel_id=1, source_target_pairs={{0,128},{16,144},{32,160},{48,176},{64,192},{80,208},{96,224},{112... | collective-permute-start | bytes 393224 | tf_op jit(solution)/shard_map/ppermute | solution.py:37
  236.8 8.3 %collective-permute-done.18 = f32[2,1,1,1,1,1,32,512]{7,6,5,4,3,2,1,0:T(8,128)S(1)} collective-permute-done((f32[2,1,1,1,1,1,32,512]{7,6,5,4,3,2,1,0:T(8,128)S(1)}, f32[2,1,1,1,1,1,32,512]{7,6,5,4,3,2,1,0:T(8,128)S(1)}, u32[]{:S(2)}, u32[]{:S(2)}) %collective-permute-start.18) | collective-permute-done | bytes 131104 | tf_op jit(solution)/shard_map/ppermute | solution.py:37
  245.1 5.5 %collective-permute-start.19 = (f32[1,1,1,1,1,1,32,512]{7,6,5,4,3,2,1,0:T(8,128)S(1)}, f32[1,1,1,1,1,1,32,512]{7,6,5,4,3,2,1,0:T(8,128)S(1)}, u32[]{:S(2)}, u32[]{:S(2)}) collective-permute-start(f32[1,1,1,1,1,1,32,512]{7,6,5,4,3,2,1,0:T(8,128)S(1)} %constant_dynamic-slice_fusion), channel_id=1, source_target_pairs={{0,256},{16,272},{32,288},{48,304},{64,320},{80,336},{96,352},{112... | collective-permute-start | bytes 196616 | tf_op jit(solution)/shard_map/ppermute | solution.py:37
  251.2 9.9 %collective-permute-done.19 = f32[1,1,1,1,1,1,32,512]{7,6,5,4,3,2,1,0:T(8,128)S(1)} collective-permute-done((f32[1,1,1,1,1,1,32,512]{7,6,5,4,3,2,1,0:T(8,128)S(1)}, f32[1,1,1,1,1,1,32,512]{7,6,5,4,3,2,1,0:T(8,128)S(1)}, u32[]{:S(2)}, u32[]{:S(2)}) %collective-permute-start.19) | collective-permute-done | bytes 65568 | tf_op jit(solution)/shard_map/ppermute | solution.py:37
  261.1 12.0 %collective-permute-start.20 = (f32[32,512]{1,0:T(8,128)S(1)}, f32[32,512]{1,0:T(8,128)S(1)}, u32[]{:S(2)}, u32[]{:S(2)}) collective-permute-start(f32[32,512]{1,0:T(8,128)S(1)} %add_bitcast_fusion), channel_id=1, source_target_pairs={{0,2},{1,3},{2,0},{3,1},{4,6},{5,7},{6,4},{7,5},{8,10},{9,11},{10,... | collective-permute-start | bytes 196616 | tf_op jit(solution)/shard_map/ppermute | solution.py:37
  274.8 6.1 %collective-permute-start.21 = (f32[32,512]{1,0:T(8,128)S(1)}, f32[32,512]{1,0:T(8,128)S(1)}, u32[]{:S(2)}, u32[]{:S(2)}) collective-permute-start(f32[32,512]{1,0:T(8,128)S(1)} %add.342), channel_id=1, source_target_pairs={{0,4},{1,5},{2,6},{3,7},{4,0},{5,1},{6,2},{7,3},{8,12},{9,13},{10,... | collective-permute-start | bytes 196616 | tf_op jit(solution)/shard_map/ppermute | solution.py:37
  282.6 4.9 %collective-permute-start.22 = (f32[32,512]{1,0:T(8,128)S(1)}, f32[32,512]{1,0:T(8,128)S(1)}, u32[]{:S(2)}, u32[]{:S(2)}) collective-permute-start(f32[32,512]{1,0:T(8,128)S(1)} %add.343), channel_id=1, source_target_pairs={{0,8},{1,9},{2,10},{3,11},{4,12},{5,13},{6,14},{7,15},{8,0},{9,1},... | collective-permute-start | bytes 196616 | tf_op jit(solution)/shard_map/ppermute | solution.py:37
  289.1 6.7 %collective-permute-start.23 = (f32[32,512]{1,0:T(8,128)S(1)}, f32[32,512]{1,0:T(8,128)S(1)}, u32[]{:S(2)}, u32[]{:S(2)}) collective-permute-start(f32[32,512]{1,0:T(8,128)S(1)} %add.344), channel_id=1, source_target_pairs={{0,1},{1,0},{2,3},{3,2},{4,5},{5,4},{6,7},{7,6},{8,9},{9,8},{10,11... | collective-permute-start | bytes 196616 | tf_op jit(solution)/shard_map/ppermute | solution.py:37
  (135 shorter events, 92.1 us)
Async XLA Ops:
  0.7 17.6 %copy-start = (bf16[1,8,16,1024]{3,2,1,0:T(8,128)(2,1)S(1)}, bf16[1,8,16,1024]{3,2,1,0:T(8,128)(2,1)}, u32[]{:S(2)}) copy-start(bf16[1,8,16,1024]{3,2,1,0:T(8,128)(2,1)} %param.6) | copy-start | bytes 786436
  0.7 17.9 %copy-start.12 = (f32[1024]{0:T(1024)S(1)}, f32[1024]{0:T(1024)}, u32[]{:S(2)}) copy-start(f32[1024]{0:T(1024)} %param.7) | copy-start | bytes 12292
  2.0 21.5 %collective-permute-start = (bf16[1,1,1,1,1,32,1024]{6,5,4,3,2,1,0:T(8,128)(2,1)S(1)}, bf16[1,1,1,1,1,32,1024]{6,5,4,3,2,1,0:T(8,128)(2,1)S(1)}, u32[]{:S(2)}, u32[]{:S(2)}) collective-permute-start(bf16[1,1,1,1,1,32,1024]{6,5,4,3,2,1,0:T(8,128)(2,1)S(1)} %constant_dynamic-slice_fusion.9), channel_id=1, source_target_pairs={{0,256},{16,272},{32,288},{48,304},{64,320},{80,336},{96,352},{112... | collective-permute-start | bytes 196616 | tf_op jit(solution)/shard_map/ppermute | solution.py:37
  18.9 11.5 %collective-permute-start.3 = (bf16[1,6,16,1024]{3,2,1,0:T(8,128)(2,1)S(1)}, bf16[1,6,16,1024]{3,2,1,0:T(8,128)(2,1)S(1)}, u32[]{:S(2)}, u32[]{:S(2)}) collective-permute-start(bf16[1,6,16,1024]{3,2,1,0:T(8,128)(2,1)S(1)} %get-tuple-element.19), channel_id=1, source_target_pairs={{0,16},{16,32},{32,48},{48,64},{64,80},{80,96},{96,112},{112,128},... | collective-permute-start | bytes 589832 | tf_op jit(solution)/shard_map/ppermute | solution.py:27
  22.1 8.3 %collective-permute-start.4 = (bf16[1,6,16,1024]{3,2,1,0:T(8,128)(2,1)S(1)}, bf16[1,6,16,1024]{3,2,1,0:T(8,128)(2,1)S(1)}, u32[]{:S(2)}, u32[]{:S(2)}) collective-permute-start(bf16[1,6,16,1024]{3,2,1,0:T(8,128)(2,1)S(1)} %get-tuple-element.20), channel_id=1, source_target_pairs={{16,0},{32,16},{48,32},{64,48},{80,64},{96,80},{112,96},{128,112},... | collective-permute-start | bytes 589832 | tf_op jit(solution)/shard_map/ppermute | solution.py:30
  23.5 19.5 %collective-permute-start.1 = (bf16[2,1,1,1,1,32,1024]{6,5,4,3,2,1,0:T(8,128)(2,1)S(1)}, bf16[2,1,1,1,1,32,1024]{6,5,4,3,2,1,0:T(8,128)(2,1)S(1)}, u32[]{:S(2)}, u32[]{:S(2)}) collective-permute-start(bf16[2,1,1,1,1,32,1024]{6,5,4,3,2,1,0:T(8,128)(2,1)S(1)} %constant_dynamic-slice_fusion.8), channel_id=1, source_target_pairs={{0,128},{16,144},{32,160},{48,176},{64,192},{80,208},{96,224},{112... | collective-permute-start | bytes 393224 | tf_op jit(solution)/shard_map/ppermute | solution.py:37
  31.5 14.5 %collective-permute-start.5 = (bf16[1,20,6,1024]{3,2,1,0:T(8,128)(2,1)}, bf16[1,20,6,1024]{3,2,1,0:T(8,128)(2,1)S(1)}, u32[]{:S(2)}, u32[]{:S(2)}) collective-permute-start(bf16[1,20,6,1024]{3,2,1,0:T(8,128)(2,1)} %get-tuple-element.17), channel_id=1, source_target_pairs={{0,1},{1,2},{2,3},{3,4},{4,5},{5,6},{6,7},{7,8},{8,9},{9,10},{10,1... | collective-permute-start | bytes 737288 | tf_op jit(solution)/shard_map/ppermute | solution.py:27
  38.0 10.2 %collective-permute-start.6 = (bf16[1,20,6,1024]{3,2,1,0:T(8,128)(2,1)}, bf16[1,20,6,1024]{3,2,1,0:T(8,128)(2,1)}, u32[]{:S(2)}, u32[]{:S(2)}) collective-permute-start(bf16[1,20,6,1024]{3,2,1,0:T(8,128)(2,1)} %get-tuple-element.18), channel_id=1, source_target_pairs={{1,0},{2,1},{3,2},{4,3},{5,4},{6,5},{7,6},{8,7},{9,8},{10,9},{11,1... | collective-permute-start | bytes 737288 | tf_op jit(solution)/shard_map/ppermute | solution.py:30
  43.7 16.1 %collective-permute-start.2 = (bf16[2,2,1,1,1,32,1024]{6,5,4,3,2,1,0:T(8,128)(2,1)}, bf16[2,2,1,1,1,32,1024]{6,5,4,3,2,1,0:T(8,128)(2,1)}, u32[]{:S(2)}, u32[]{:S(2)}) collective-permute-start(bf16[2,2,1,1,1,32,1024]{6,5,4,3,2,1,0:T(8,128)(2,1)} %constant_dynamic-slice_fusion.7), channel_id=1, source_target_pairs={{0,64},{16,80},{32,96},{48,112},{64,0},{80,16},{96,32},{112,48},{1... | collective-permute-start | bytes 786440 | tf_op jit(solution)/shard_map/ppermute | solution.py:37
  61.7 15.1 %collective-permute-start.7 = (bf16[2,2,2,1,1,32,1024]{6,5,4,3,2,1,0:T(8,128)(2,1)}, bf16[2,2,2,1,1,32,1024]{6,5,4,3,2,1,0:T(8,128)(2,1)S(1)}, u32[]{:S(2)}, u32[]{:S(2)}) collective-permute-start(bf16[2,2,2,1,1,32,1024]{6,5,4,3,2,1,0:T(8,128)(2,1)} %constant_dynamic-slice_fusion.6), channel_id=1, source_target_pairs={{0,32},{16,48},{32,0},{48,16},{64,96},{80,112},{96,64},{112,80},{1... | collective-permute-start | bytes 1572872 | tf_op jit(solution)/shard_map/ppermute | solution.py:37
  77.9 25.5 %collective-permute-start.8 = (bf16[2,2,2,2,1,32,1024]{6,5,4,3,2,1,0:T(8,128)(2,1)}, bf16[2,2,2,2,1,32,1024]{6,5,4,3,2,1,0:T(8,128)(2,1)}, u32[]{:S(2)}, u32[]{:S(2)}) collective-permute-start(bf16[2,2,2,2,1,32,1024]{6,5,4,3,2,1,0:T(8,128)(2,1)} %constant_dynamic-slice_fusion.5), channel_id=1, source_target_pairs={{0,16},{16,0},{32,48},{48,32},{64,80},{80,64},{96,112},{112,96},{1... | collective-permute-start | bytes 3145736 | tf_op jit(solution)/shard_map/ppermute | solution.py:37
  104.8 8.1 %collective-permute-start.9 = (bf16[32,32,1024]{2,1,0:T(8,128)(2,1)S(1)}, bf16[32,32,1024]{2,1,0:T(8,128)(2,1)}, u32[]{:S(2)}, u32[]{:S(2)}) collective-permute-start(bf16[32,32,1024]{2,1,0:T(8,128)(2,1)S(1)} %bitcast.104), channel_id=1, source_target_pairs={{0,1},{1,0},{2,3},{3,2},{4,5},{5,4},{6,7},{7,6},{8,9},{9,8},{10,11... | collective-permute-start | bytes 6291464 | tf_op jit(solution)/shard_map/ppermute | solution.py:37
  151.5 6.4 %collective-permute-start.14 = (f32[1024,512]{1,0:T(8,128)}, f32[1024,512]{1,0:T(8,128)}, u32[]{:S(2)}, u32[]{:S(2)}) collective-permute-start(f32[1024,512]{1,0:T(8,128)} %dynamic-slice_bitcast_fusion), channel_id=1, source_target_pairs={{0,1},{1,0},{2,3},{3,2},{4,5},{5,4},{6,7},{7,6},{8,9},{9,8},{10,11... | collective-permute-start | bytes 6291464 | tf_op jit(solution)/shard_map/ppermute | solution.py:37
  163.0 30.4 %collective-permute-start.15 = (f32[2,2,2,2,1,1,32,512]{7,6,5,4,3,2,1,0:T(8,128)}, f32[2,2,2,2,1,1,32,512]{7,6,5,4,3,2,1,0:T(8,128)}, u32[]{:S(2)}, u32[]{:S(2)}) collective-permute-start(f32[2,2,2,2,1,1,32,512]{7,6,5,4,3,2,1,0:T(8,128)} %constant_dynamic-slice_fusion.4), channel_id=1, source_target_pairs={{0,16},{16,0},{32,48},{48,32},{64,80},{80,64},{96,112},{112,96},{1... | collective-permute-start | bytes 3145736 | tf_op jit(solution)/shard_map/ppermute | solution.py:37
  183.6 8.8 %copy-start.10 = (bf16[8,16,512]{2,1,0:T(8,128)(2,1)S(1)}, bf16[8,16,512]{2,1,0:T(8,128)(2,1)}, u32[]{:S(2)}) copy-start(bf16[8,16,512]{2,1,0:T(8,128)(2,1)} %reshape.275) | copy-start | bytes 393220
  184.6 8.9 %copy-start.2 = (f32[1024,512]{1,0:T(8,128)S(1)}, f32[1024,512]{1,0:T(8,128)}, u32[]{:S(2)}) copy-start(f32[1024,512]{1,0:T(8,128)} %copy-done.1) | copy-start | bytes 6291460
  185.3 16.2 %collective-permute-start.10 = (f32[1,20,6,1024]{3,0,2,1:T(1,128)S(1)}, f32[1,20,6,1024]{3,0,2,1:T(1,128)S(1)}, u32[]{:S(2)}, u32[]{:S(2)}) collective-permute-start(f32[1,20,6,1024]{3,0,2,1:T(1,128)S(1)} %get-tuple-element.9), channel_id=1, source_target_pairs={{0,1},{1,2},{2,3},{3,4},{4,5},{5,6},{6,7},{7,8},{8,9},{9,10},{10,1... | collective-permute-start | bytes 1474568 | tf_op jit(solution)/shard_map/ppermute | solution.py:19
  190.5 11.7 %collective-permute-start.11 = (f32[1,20,6,1024]{3,0,2,1:T(1,128)S(1)}, f32[1,20,6,1024]{3,0,2,1:T(1,128)S(1)}, u32[]{:S(2)}, u32[]{:S(2)}) collective-permute-start(f32[1,20,6,1024]{3,0,2,1:T(1,128)S(1)} %get-tuple-element.10), channel_id=1, source_target_pairs={{1,0},{2,1},{3,2},{4,3},{5,4},{6,5},{7,6},{8,7},{9,8},{10,9},{11,1... | collective-permute-start | bytes 1474568 | tf_op jit(solution)/shard_map/ppermute | solution.py:19
  194.9 6.6 %copy-start.5 = (f32[2,2,2,2,1,1,32,512]{7,6,5,4,3,2,1,0:T(8,128)}, f32[2,2,2,2,1,1,32,512]{7,6,5,4,3,2,1,0:T(8,128)S(1)}, u32[]{:S(2)}) copy-start(f32[2,2,2,2,1,1,32,512]{7,6,5,4,3,2,1,0:T(8,128)S(1)} %dynamic-slice_add_fusion) | copy-start | bytes 3145732
  195.8 14.0 %copy-start.9 = (bf16[1,560,512]{1,2,0:T(8,128)(2,1)S(1)}, bf16[1,560,512]{1,2,0:T(8,128)(2,1)}, u32[]{:S(2)}) copy-start(bf16[1,560,512]{1,2,0:T(8,128)(2,1)} %copy.19) | copy-start | bytes 1720324
  195.8 18.6 %collective-permute-start.16 = (f32[2,2,2,1,1,1,32,512]{7,6,5,4,3,2,1,0:T(8,128)}, f32[2,2,2,1,1,1,32,512]{7,6,5,4,3,2,1,0:T(8,128)}, u32[]{:S(2)}, u32[]{:S(2)}) collective-permute-start(f32[2,2,2,1,1,1,32,512]{7,6,5,4,3,2,1,0:T(8,128)} %constant_dynamic-slice_fusion.3), channel_id=1, source_target_pairs={{0,32},{16,48},{32,0},{48,16},{64,96},{80,112},{96,64},{112,80},{1... | collective-permute-start | bytes 1572872 | tf_op jit(solution)/shard_map/ppermute | solution.py:37
  205.0 18.2 %collective-permute-start.12 = (f32[1,6,16,1024]{3,0,2,1:T(1,128)}, f32[1,6,16,1024]{3,0,2,1:T(1,128)}, u32[]{:S(2)}, u32[]{:S(2)}) collective-permute-start(f32[1,6,16,1024]{3,0,2,1:T(1,128)} %get-tuple-element.13), channel_id=1, source_target_pairs={{0,16},{16,32},{32,48},{48,64},{64,80},{80,96},{96,112},{112,128},... | collective-permute-start | bytes 1179656 | tf_op jit(solution)/shard_map/ppermute | solution.py:19
  208.6 14.7 %collective-permute-start.13 = (f32[1,6,16,1024]{3,0,2,1:T(1,128)}, f32[1,6,16,1024]{3,0,2,1:T(1,128)}, u32[]{:S(2)}, u32[]{:S(2)}) collective-permute-start(f32[1,6,16,1024]{3,0,2,1:T(1,128)} %get-tuple-element.14), channel_id=1, source_target_pairs={{16,0},{32,16},{48,32},{64,48},{80,64},{96,80},{112,96},{128,112},... | collective-permute-start | bytes 1179656 | tf_op jit(solution)/shard_map/ppermute | solution.py:19
  215.7 20.2 %copy-start.3 = (bf16[32,32,1024]{2,1,0:T(8,128)(2,1)S(1)}, bf16[32,32,1024]{2,1,0:T(8,128)(2,1)}, u32[]{:S(2)}) copy-start(bf16[32,32,1024]{2,1,0:T(8,128)(2,1)} %get-tuple-element.8) | copy-start | bytes 6291460
  215.8 16.1 %collective-permute-start.17 = (f32[2,2,1,1,1,1,32,512]{7,6,5,4,3,2,1,0:T(8,128)S(1)}, f32[2,2,1,1,1,1,32,512]{7,6,5,4,3,2,1,0:T(8,128)S(1)}, u32[]{:S(2)}, u32[]{:S(2)}) collective-permute-start(f32[2,2,1,1,1,1,32,512]{7,6,5,4,3,2,1,0:T(8,128)S(1)} %constant_dynamic-slice_fusion.2), channel_id=1, source_target_pairs={{0,64},{16,80},{32,96},{48,112},{64,0},{80,16},{96,32},{112,48},{1... | collective-permute-start | bytes 786440 | tf_op jit(solution)/shard_map/ppermute | solution.py:37
  231.9 13.2 %collective-permute-start.18 = (f32[2,1,1,1,1,1,32,512]{7,6,5,4,3,2,1,0:T(8,128)S(1)}, f32[2,1,1,1,1,1,32,512]{7,6,5,4,3,2,1,0:T(8,128)S(1)}, u32[]{:S(2)}, u32[]{:S(2)}) collective-permute-start(f32[2,1,1,1,1,1,32,512]{7,6,5,4,3,2,1,0:T(8,128)S(1)} %constant_dynamic-slice_fusion.1), channel_id=1, source_target_pairs={{0,128},{16,144},{32,160},{48,176},{64,192},{80,208},{96,224},{112... | collective-permute-start | bytes 393224 | tf_op jit(solution)/shard_map/ppermute | solution.py:37
  236.7 59.1 %copy-start.8 = (bf16[1,8,16,1024]{3,2,1,0:T(8,128)(2,1)S(1)}, bf16[1,8,16,1024]{3,2,1,0:T(8,128)(2,1)}, u32[]{:S(2)}) copy-start(bf16[1,8,16,1024]{3,2,1,0:T(8,128)(2,1)} %param.11) | copy-start | bytes 786436
  245.1 16.0 %collective-permute-start.19 = (f32[1,1,1,1,1,1,32,512]{7,6,5,4,3,2,1,0:T(8,128)S(1)}, f32[1,1,1,1,1,1,32,512]{7,6,5,4,3,2,1,0:T(8,128)S(1)}, u32[]{:S(2)}, u32[]{:S(2)}) collective-permute-start(f32[1,1,1,1,1,1,32,512]{7,6,5,4,3,2,1,0:T(8,128)S(1)} %constant_dynamic-slice_fusion), channel_id=1, source_target_pairs={{0,256},{16,272},{32,288},{48,304},{64,320},{80,336},{96,352},{112... | collective-permute-start | bytes 196616 | tf_op jit(solution)/shard_map/ppermute | solution.py:37
  261.1 13.6 %collective-permute-start.20 = (f32[32,512]{1,0:T(8,128)S(1)}, f32[32,512]{1,0:T(8,128)S(1)}, u32[]{:S(2)}, u32[]{:S(2)}) collective-permute-start(f32[32,512]{1,0:T(8,128)S(1)} %add_bitcast_fusion), channel_id=1, source_target_pairs={{0,2},{1,3},{2,0},{3,1},{4,6},{5,7},{6,4},{7,5},{8,10},{9,11},{10,... | collective-permute-start | bytes 196616 | tf_op jit(solution)/shard_map/ppermute | solution.py:37
  274.8 7.8 %collective-permute-start.21 = (f32[32,512]{1,0:T(8,128)S(1)}, f32[32,512]{1,0:T(8,128)S(1)}, u32[]{:S(2)}, u32[]{:S(2)}) collective-permute-start(f32[32,512]{1,0:T(8,128)S(1)} %add.342), channel_id=1, source_target_pairs={{0,4},{1,5},{2,6},{3,7},{4,0},{5,1},{6,2},{7,3},{8,12},{9,13},{10,... | collective-permute-start | bytes 196616 | tf_op jit(solution)/shard_map/ppermute | solution.py:37
  282.6 6.5 %collective-permute-start.22 = (f32[32,512]{1,0:T(8,128)S(1)}, f32[32,512]{1,0:T(8,128)S(1)}, u32[]{:S(2)}, u32[]{:S(2)}) collective-permute-start(f32[32,512]{1,0:T(8,128)S(1)} %add.343), channel_id=1, source_target_pairs={{0,8},{1,9},{2,10},{3,11},{4,12},{5,13},{6,14},{7,15},{8,0},{9,1},... | collective-permute-start | bytes 196616 | tf_op jit(solution)/shard_map/ppermute | solution.py:37
  289.1 8.5 %collective-permute-start.23 = (f32[32,512]{1,0:T(8,128)S(1)}, f32[32,512]{1,0:T(8,128)S(1)}, u32[]{:S(2)}, u32[]{:S(2)}) collective-permute-start(f32[32,512]{1,0:T(8,128)S(1)} %add.344), channel_id=1, source_target_pairs={{0,1},{1,0},{2,3},{3,2},{4,5},{5,4},{6,7},{7,6},{8,9},{9,8},{10,11... | collective-permute-start | bytes 196616 | tf_op jit(solution)/shard_map/ppermute | solution.py:37
  (7 other events, 13.5 us)

commit v15 on v13

--- a/solution.py
+++ b/solution.py
@@ -286,10 +286,6 @@
     )[0]
     for bit in range(1, col_levels):
         rows_part = rows_part + partner_swap(rows_part, "col", 1 << bit)
-    held = jnp.zeros((2,) + rows_part.shape, rows_part.dtype)
-    held = lax.dynamic_update_slice(held, rows_part[None], (own, 0, 0))
-    held = lax.dynamic_update_slice(held, partner_swap(rows_part, "col", 1)[None], (1 - own, 0, 0))
-    keyvalue_grad = held.transpose(1, 0, 2).reshape(feature_part, -1)
     normed_grad = lax.dot_general(
         query_grad.reshape(-1, inner_width),
         full_query,
@@ -305,7 +301,15 @@
         - jnp.mean(gained, axis=-1, keepdims=True)
         - standard * jnp.mean(gained * standard, axis=-1, keepdims=True)
     )
-    return (layer_out, in_grad.astype(jnp.bfloat16), keyvalue_grad)
+    in_grad = in_grad.astype(jnp.bfloat16)
+    rows_part, in_grad = lax.optimization_barrier((rows_part, in_grad))
+    other = partner_swap(rows_part, "col", 1)
+    keyvalue_grad = jnp.where(
+        own == 0,
+        jnp.concatenate([rows_part, other], axis=1),
+        jnp.concatenate([other, rows_part], axis=1),
+    )
+    return (layer_out, in_grad, keyvalue_grad)
 
 
 def solution(mesh):

time: 296 us -> 316 us (1.068)
  waiting for transfers between devices: 87.8 us -> 114 us
  starting transfers between devices: 112 us -> 104 us
    ppermute x16, waiting for transfers between devices: 81.7 us -> 104 us  [partner_swap(): return lax.ppermute(value, axis, [(i, i ^ mask) for i in range(count)])]
    ppermute x16, starting transfers between devices: 87 us -> 81 us  [partner_swap(): return lax.ppermute(value, axis, [(i, i ^ mask) for i in range(count)])]
    ppermute x4, waiting for transfers between devices: 3.9 us -> 8.47 us  [shifted(): lax.ppermute(value, axis, [(source, source + steps) for source in range(f...]
  transfers between devices with their start and end apart: 24 -> 24, of which waited for: 15 -> 15; matrix products, arithmetic and copies ran while one was open for 16% -> 15% of each run, Pallas kernels for 0% -> 0%
where the time goes in v15:
time: 316 us; the launch traced here: 315 us
  waiting for transfers between devices  114 us (36%)
  starting transfers between devices  104 us (33%)
  local copies, waits for them, and re-layouts  50.5 us (16%)
  matrix products  29.6 us (9%)
  other arithmetic  14.8 us (5%)
    ppermute x16, waiting for transfers between devices, partner_swap(): return lax.ppermute(value, axis, [(i, i ^ mask) for i in range(count)])  104 us
    ppermute x16, starting transfers between devices, partner_swap(): return lax.ppermute(value, axis, [(i, i ^ mask) for i in range(count)])  81 us
    ppermute x4, starting transfers between devices, shifted(): lax.ppermute(value, axis, [(source, source + steps) for source in range(f...  9.96 us
    ppermute x2, starting transfers between devices, with_halo(): lax.ppermute(lax.slice_in_dim(block, block.shape[dim] - width, None, axis...  9.7 us
    ppermute x4, waiting for transfers between devices, shifted(): lax.ppermute(value, axis, [(source, source + steps) for source in range(f...  8.47 us
    concatenate x3, local copies, waits for them, and re-layouts, tile_backward(): jnp.concatenate([key_grad.reshape(batches, ext_count, inner_width), value...  8.23 us
  transfers between devices with their start and end apart: 24, of which 15 were waited for; matrix products, arithmetic and copies ran while one was open for 15% of the time, Pallas kernels for 0%

profile of v15, /device:TPU:1, one launch (start us, length us, event | category | flops | bytes accessed | tf_op | source)
XLA Modules:
  0.0 314.7 jit_solution(3550006491901168174)
XLA Ops:
  1.9 16.3 %collective-permute-start = (bf16[1,1,1,1,1,32,1024]{6,5,4,3,2,1,0:T(8,128)(2,1)S(1)}, bf16[1,1,1,1,1,32,1024]{6,5,4,3,2,1,0:T(8,128)(2,1)S(1)}, u32[]{:S(2)}, u32[]{:S(2)}) collective-permute-start(bf16[1,1,1,1,1,32,1024]{6,5,4,3,2,1,0:T(8,128)(2,1)S(1)} %constant_dynamic-slice_fusion.9), channel_id=1, source_target_pairs={{0,256},{16,272},{32,288},{48,304},{64,320},{80,336},{96,352},{112... | collective-permute-start | bytes 196616 | tf_op jit(solution)/shard_map/ppermute | solution.py:37
  18.9 3.2 %collective-permute-start.3 = (bf16[1,6,16,1024]{3,2,1,0:T(8,128)(2,1)S(1)}, bf16[1,6,16,1024]{3,2,1,0:T(8,128)(2,1)S(1)}, u32[]{:S(2)}, u32[]{:S(2)}) collective-permute-start(bf16[1,6,16,1024]{3,2,1,0:T(8,128)(2,1)S(1)} %get-tuple-element.21), channel_id=1, source_target_pairs={{0,16},{16,32},{32,48},{48,64},{64,80},{80,96},{96,112},{112,128},... | collective-permute-start | bytes 589832 | tf_op jit(solution)/shard_map/ppermute | solution.py:27
  23.5 6.9 %collective-permute-start.1 = (bf16[2,1,1,1,1,32,1024]{6,5,4,3,2,1,0:T(8,128)(2,1)S(1)}, bf16[2,1,1,1,1,32,1024]{6,5,4,3,2,1,0:T(8,128)(2,1)S(1)}, u32[]{:S(2)}, u32[]{:S(2)}) collective-permute-start(bf16[2,1,1,1,1,32,1024]{6,5,4,3,2,1,0:T(8,128)(2,1)S(1)} %constant_dynamic-slice_fusion.8), channel_id=1, source_target_pairs={{0,128},{16,144},{32,160},{48,176},{64,192},{80,208},{96,224},{112... | collective-permute-start | bytes 393224 | tf_op jit(solution)/shard_map/ppermute | solution.py:37
  31.5 6.5 %collective-permute-start.5 = (bf16[1,20,6,1024]{3,2,1,0:T(8,128)(2,1)}, bf16[1,20,6,1024]{3,2,1,0:T(8,128)(2,1)S(1)}, u32[]{:S(2)}, u32[]{:S(2)}) collective-permute-start(bf16[1,20,6,1024]{3,2,1,0:T(8,128)(2,1)} %get-tuple-element.19), channel_id=1, source_target_pairs={{0,1},{1,2},{2,3},{3,4},{4,5},{5,6},{6,7},{7,8},{8,9},{9,10},{10,1... | collective-permute-start | bytes 737288 | tf_op jit(solution)/shard_map/ppermute | solution.py:27
  39.9 3.1 collective-permute-done.1
  48.2 2.7 pad_maximum_fusion
  53.1 6.7 %collective-permute-done.2 = bf16[2,2,1,1,1,32,1024]{6,5,4,3,2,1,0:T(8,128)(2,1)} collective-permute-done((bf16[2,2,1,1,1,32,1024]{6,5,4,3,2,1,0:T(8,128)(2,1)}, bf16[2,2,1,1,1,32,1024]{6,5,4,3,2,1,0:T(8,128)(2,1)}, u32[]{:S(2)}, u32[]{:S(2)}) %collective-permute-start.2) | collective-permute-done | bytes 262176 | tf_op jit(solution)/shard_map/ppermute | solution.py:37
  63.6 13.2 %collective-permute-done.7 = bf16[2,2,2,1,1,32,1024]{6,5,4,3,2,1,0:T(8,128)(2,1)S(1)} collective-permute-done((bf16[2,2,2,1,1,32,1024]{6,5,4,3,2,1,0:T(8,128)(2,1)}, bf16[2,2,2,1,1,32,1024]{6,5,4,3,2,1,0:T(8,128)(2,1)S(1)}, u32[]{:S(2)}, u32[]{:S(2)}) %collective-permute-start.7) | collective-permute-done | bytes 524320 | tf_op jit(solution)/shard_map/ppermute | solution.py:37
  79.8 23.6 %collective-permute-done.8 = bf16[2,2,2,2,1,32,1024]{6,5,4,3,2,1,0:T(8,128)(2,1)} collective-permute-done((bf16[2,2,2,2,1,32,1024]{6,5,4,3,2,1,0:T(8,128)(2,1)}, bf16[2,2,2,2,1,32,1024]{6,5,4,3,2,1,0:T(8,128)(2,1)}, u32[]{:S(2)}, u32[]{:S(2)}) %collective-permute-start.8) | collective-permute-done | bytes 1048608 | tf_op jit(solution)/shard_map/ppermute | solution.py:37
  104.8 4.3 %collective-permute-start.9 = (bf16[32,32,1024]{2,1,0:T(8,128)(2,1)S(1)}, bf16[32,32,1024]{2,1,0:T(8,128)(2,1)}, u32[]{:S(2)}, u32[]{:S(2)}) collective-permute-start(bf16[32,32,1024]{2,1,0:T(8,128)(2,1)S(1)} %bitcast.103), channel_id=1, source_target_pairs={{0,1},{1,0},{2,3},{3,2},{4,5},{5,4},{6,7},{7,6},{8,9},{9,8},{10,11... | collective-permute-start | bytes 6291464 | tf_op jit(solution)/shard_map/ppermute | solution.py:37
  127.6 3.5 %fusion.80 = (f32[8,128]{1,0:T(8,128)S(1)}, f32[8,128,560]{1,2,0:T(8,128)}) fusion(pred[128,560]{0,1:T(8,128)(4,1)} %fusion.49, bf16[128,8,64]{0,2,1:T(8,128)(2,1)S(1)} %bitcast.127, bf16[560,8,64]{0,2,1:T(8,128)(2,1)} %bitcast.118), kind=kOutput, calls=%fused_computation.134 | convolution fusion | flops 75694640 | bytes 3074048 | tf_op jit(solution)/shard_map/sub | solution.py:157
  131.1 3.6 %fusion.81 = (bf16[1,560,8,64]{1,3,2,0:T(8,128)(2,1)}, f32[1,560,8,64]{1,3,2,0:T(8,128)}) fusion(bf16[128,8,64]{0,2,1:T(8,128)(2,1)S(1)} %bitcast.125, f32[8,128]{1,0:T(8,128)S(1)} %get-tuple-element.23, pred[128,560]{0,1:T(8,128)(4,1)} %fusion.49, bf16[128,8,64]{0,2,1:T(8,128)(2,1)S(1)} %bitcast.128, bf16[560,8,64]{0,2,1:T(8,128)(2,1)} %bitcast.119), kind=kOutput, calls=%fused_computation.135 | convolution fusion | flops 149956144 | bytes 2631680 | tf_op jit(solution)/shard_map/bhqk,bqhd->bkhd/dot_general | solution.py:184
  134.7 5.8 %fusion.82 = (bf16[1,560,8,64]{1,3,2,0:T(8,128)(2,1)}, f32[1,560,8,64]{1,3,2,0:T(8,128)}) fusion(bf16[128,8,64]{0,2,1:T(8,128)(2,1)S(1)} %bitcast.129, f32[8,128,560]{1,2,0:T(8,128)} %fusion.85, f32[8,128,560]{1,2,0:T(8,128)} %get-tuple-element.24, f32[8,128]{1,0:T(8,128)S(1)} %get-tuple-element.23), kind=kOutput, calls=%fused_computation.136 | convolution fusion | flops 77702704 | bytes 6443008 | tf_op jit(solution)/shard_map/bhqk,bqhd->bkhd/dot_general | solution.py:181
  154.2 3.0 copy.23
  157.2 3.6 %concatenate.30 = f32[1,20,28,512]{3,0,2,1:T(1,128)} reshape(f32[1,560,8,64]{3,2,0,1:T(8,128)} %copy.23) | data formatting | bytes 2293760 | tf_op jit(solution)/shard_map/concatenate | solution.py:188
  160.9 3.0 copy.24
  163.9 3.6 %concatenate.31 = f32[1,20,28,512]{3,0,2,1:T(1,128)} reshape(f32[1,560,8,64]{3,2,0,1:T(8,128)} %copy.24) | data formatting | bytes 2293760 | tf_op jit(solution)/shard_map/concatenate | solution.py:188
  171.8 4.7 %collective-permute-start.19 = (f32[1,20,6,1024]{3,0,2,1:T(1,128)S(1)}, f32[1,20,6,1024]{3,0,2,1:T(1,128)S(1)}, u32[]{:S(2)}, u32[]{:S(2)}) collective-permute-start(f32[1,20,6,1024]{3,0,2,1:T(1,128)S(1)} %get-tuple-element.13), channel_id=1, source_target_pairs={{0,1},{1,2},{2,3},{3,4},{4,5},{5,6},{6,7},{7,8},{8,9},{9,10},{10,1... | collective-permute-start | bytes 1474568 | tf_op jit(solution)/shard_map/ppermute | solution.py:19
  182.6 6.5 %collective-permute-done.19 = f32[1,20,6,1024]{3,0,2,1:T(1,128)S(1)} collective-permute-done((f32[1,20,6,1024]{3,0,2,1:T(1,128)S(1)}, f32[1,20,6,1024]{3,0,2,1:T(1,128)S(1)}, u32[]{:S(2)}, u32[]{:S(2)}) %collective-permute-start.19) | collective-permute-done | bytes 491552 | tf_op jit(solution)/shard_map/ppermute | solution.py:19
  197.3 22.7 %collective-permute-done.11 = f32[2,2,2,2,1,1,32,512]{7,6,5,4,3,2,1,0:T(8,128)S(1)} collective-permute-done((f32[2,2,2,2,1,1,32,512]{7,6,5,4,3,2,1,0:T(8,128)S(1)}, f32[2,2,2,2,1,1,32,512]{7,6,5,4,3,2,1,0:T(8,128)S(1)}, u32[]{:S(2)}, u32[]{:S(2)}) %collective-permute-start.11) | collective-permute-done | bytes 1048608 | tf_op jit(solution)/shard_map/ppermute | solution.py:37
  223.9 3.0 fusion.31
  228.8 4.7 %fusion.19 = bf16[8,64,128]{2,1,0:T(8,128)(2,1)S(1)} fusion(bf16[560,8,64]{0,2,1:T(8,128)(2,1)} %bitcast.121, f32[8,128,560]{1,2,0:T(8,128)} %fusion.85, f32[8,128,560]{1,2,0:T(8,128)} %get-tuple-element.24, f32[8,128]{1,0:T(8,128)S(1)} %get-tuple-element.23), kind=kOutput, calls=%fused_computation.24 | convolution fusion | flops 77481520 | bytes 5296128 | tf_op jit(solution)/shard_map/bhqk,bkhd->bqhd/dot_general | solution.py:178
  237.1 9.6 %collective-permute-start.13 = (f32[2,2,1,1,1,1,32,512]{7,6,5,4,3,2,1,0:T(8,128)S(1)}, f32[2,2,1,1,1,1,32,512]{7,6,5,4,3,2,1,0:T(8,128)S(1)}, u32[]{:S(2)}, u32[]{:S(2)}) collective-permute-start(f32[2,2,1,1,1,1,32,512]{7,6,5,4,3,2,1,0:T(8,128)S(1)} %constant_dynamic-slice_fusion.2), channel_id=1, source_target_pairs={{0,64},{16,80},{32,96},{48,112},{64,0},{80,16},{96,32},{112,48},{1... | collective-permute-start | bytes 786440 | tf_op jit(solution)/shard_map/ppermute | solution.py:37
  247.5 5.7 %collective-permute-done.13 = f32[2,2,1,1,1,1,32,512]{7,6,5,4,3,2,1,0:T(8,128)S(1)} collective-permute-done((f32[2,2,1,1,1,1,32,512]{7,6,5,4,3,2,1,0:T(8,128)S(1)}, f32[2,2,1,1,1,1,32,512]{7,6,5,4,3,2,1,0:T(8,128)S(1)}, u32[]{:S(2)}, u32[]{:S(2)}) %collective-permute-start.13) | collective-permute-done | bytes 262176 | tf_op jit(solution)/shard_map/ppermute | solution.py:37
  253.3 7.0 %collective-permute-start.14 = (f32[2,1,1,1,1,1,32,512]{7,6,5,4,3,2,1,0:T(8,128)S(1)}, f32[2,1,1,1,1,1,32,512]{7,6,5,4,3,2,1,0:T(8,128)S(1)}, u32[]{:S(2)}, u32[]{:S(2)}) collective-permute-start(f32[2,1,1,1,1,1,32,512]{7,6,5,4,3,2,1,0:T(8,128)S(1)} %constant_dynamic-slice_fusion.1), channel_id=1, source_target_pairs={{0,128},{16,144},{32,160},{48,176},{64,192},{80,208},{96,224},{112... | collective-permute-start | bytes 393224 | tf_op jit(solution)/shard_map/ppermute | solution.py:37
  260.8 10.2 %collective-permute-done.14 = f32[2,1,1,1,1,1,32,512]{7,6,5,4,3,2,1,0:T(8,128)S(1)} collective-permute-done((f32[2,1,1,1,1,1,32,512]{7,6,5,4,3,2,1,0:T(8,128)S(1)}, f32[2,1,1,1,1,1,32,512]{7,6,5,4,3,2,1,0:T(8,128)S(1)}, u32[]{:S(2)}, u32[]{:S(2)}) %collective-permute-start.14) | collective-permute-done | bytes 131104 | tf_op jit(solution)/shard_map/ppermute | solution.py:37
  271.1 5.9 %collective-permute-start.15 = (f32[1,1,1,1,1,1,32,512]{7,6,5,4,3,2,1,0:T(8,128)S(1)}, f32[1,1,1,1,1,1,32,512]{7,6,5,4,3,2,1,0:T(8,128)S(1)}, u32[]{:S(2)}, u32[]{:S(2)}) collective-permute-start(f32[1,1,1,1,1,1,32,512]{7,6,5,4,3,2,1,0:T(8,128)S(1)} %constant_dynamic-slice_fusion), channel_id=1, source_target_pairs={{0,256},{16,272},{32,288},{48,304},{64,320},{80,336},{96,352},{112... | collective-permute-start | bytes 196616 | tf_op jit(solution)/shard_map/ppermute | solution.py:37
  277.2 9.9 %collective-permute-done.15 = f32[1,1,1,1,1,1,32,512]{7,6,5,4,3,2,1,0:T(8,128)S(1)} collective-permute-done((f32[1,1,1,1,1,1,32,512]{7,6,5,4,3,2,1,0:T(8,128)S(1)}, f32[1,1,1,1,1,1,32,512]{7,6,5,4,3,2,1,0:T(8,128)S(1)}, u32[]{:S(2)}, u32[]{:S(2)}) %collective-permute-start.15) | collective-permute-done | bytes 65568 | tf_op jit(solution)/shard_map/ppermute | solution.py:37
  289.4 4.2 %collective-permute-done.16 = f32[32,512]{1,0:T(8,128)S(1)} collective-permute-done((f32[32,512]{1,0:T(8,128)S(1)}, f32[32,512]{1,0:T(8,128)S(1)}, u32[]{:S(2)}, u32[]{:S(2)}) %collective-permute-start.16) | collective-permute-done | bytes 65568 | tf_op jit(solution)/shard_map/ppermute | solution.py:37
  293.6 4.3 %collective-permute-start.17 = (f32[32,512]{1,0:T(8,128)S(1)}, f32[32,512]{1,0:T(8,128)S(1)}, u32[]{:S(2)}, u32[]{:S(2)}) collective-permute-start(f32[32,512]{1,0:T(8,128)S(1)} %add.336), channel_id=1, source_target_pairs={{0,4},{1,5},{2,6},{3,7},{4,0},{5,1},{6,2},{7,3},{8,12},{9,13},{10,... | collective-permute-start | bytes 196616 | tf_op jit(solution)/shard_map/ppermute | solution.py:37
  299.6 4.6 %collective-permute-start.18 = (f32[32,512]{1,0:T(8,128)S(1)}, f32[32,512]{1,0:T(8,128)S(1)}, u32[]{:S(2)}, u32[]{:S(2)}) collective-permute-start(f32[32,512]{1,0:T(8,128)S(1)} %add.337), channel_id=1, source_target_pairs={{0,8},{1,9},{2,10},{3,11},{4,12},{5,13},{6,14},{7,15},{8,0},{9,1},... | collective-permute-start | bytes 196616 | tf_op jit(solution)/shard_map/ppermute | solution.py:37
  306.1 6.9 %collective-permute-start.23 = (f32[32,512]{1,0:T(8,128)S(1)}, f32[32,512]{1,0:T(8,128)S(1)}, u32[]{:S(2)}, u32[]{:S(2)}) collective-permute-start(f32[32,512]{1,0:T(8,128)S(1)} %add.338), channel_id=1, source_target_pairs={{0,1},{1,0},{2,3},{3,2},{4,5},{5,4},{6,7},{7,6},{8,9},{9,8},{10,11... | collective-permute-start | bytes 196616 | tf_op jit(solution)/shard_map/ppermute | solution.py:37
  (133 shorter events, 90.5 us)
Async XLA Ops:
  0.7 17.6 %copy-start = (bf16[1,8,16,1024]{3,2,1,0:T(8,128)(2,1)S(1)}, bf16[1,8,16,1024]{3,2,1,0:T(8,128)(2,1)}, u32[]{:S(2)}) copy-start(bf16[1,8,16,1024]{3,2,1,0:T(8,128)(2,1)} %param.6) | copy-start | bytes 786436
  0.7 17.9 %copy-start.12 = (f32[1024]{0:T(1024)S(1)}, f32[1024]{0:T(1024)}, u32[]{:S(2)}) copy-start(f32[1024]{0:T(1024)} %param.7) | copy-start | bytes 12292
  1.9 21.5 %collective-permute-start = (bf16[1,1,1,1,1,32,1024]{6,5,4,3,2,1,0:T(8,128)(2,1)S(1)}, bf16[1,1,1,1,1,32,1024]{6,5,4,3,2,1,0:T(8,128)(2,1)S(1)}, u32[]{:S(2)}, u32[]{:S(2)}) collective-permute-start(bf16[1,1,1,1,1,32,1024]{6,5,4,3,2,1,0:T(8,128)(2,1)S(1)} %constant_dynamic-slice_fusion.9), channel_id=1, source_target_pairs={{0,256},{16,272},{32,288},{48,304},{64,320},{80,336},{96,352},{112... | collective-permute-start | bytes 196616 | tf_op jit(solution)/shard_map/ppermute | solution.py:37
  18.9 11.5 %collective-permute-start.3 = (bf16[1,6,16,1024]{3,2,1,0:T(8,128)(2,1)S(1)}, bf16[1,6,16,1024]{3,2,1,0:T(8,128)(2,1)S(1)}, u32[]{:S(2)}, u32[]{:S(2)}) collective-permute-start(bf16[1,6,16,1024]{3,2,1,0:T(8,128)(2,1)S(1)} %get-tuple-element.21), channel_id=1, source_target_pairs={{0,16},{16,32},{32,48},{48,64},{64,80},{80,96},{96,112},{112,128},... | collective-permute-start | bytes 589832 | tf_op jit(solution)/shard_map/ppermute | solution.py:27
  22.1 8.3 %collective-permute-start.4 = (bf16[1,6,16,1024]{3,2,1,0:T(8,128)(2,1)S(1)}, bf16[1,6,16,1024]{3,2,1,0:T(8,128)(2,1)S(1)}, u32[]{:S(2)}, u32[]{:S(2)}) collective-permute-start(bf16[1,6,16,1024]{3,2,1,0:T(8,128)(2,1)S(1)} %get-tuple-element.22), channel_id=1, source_target_pairs={{16,0},{32,16},{48,32},{64,48},{80,64},{96,80},{112,96},{128,112},... | collective-permute-start | bytes 589832 | tf_op jit(solution)/shard_map/ppermute | solution.py:30
  23.5 19.5 %collective-permute-start.1 = (bf16[2,1,1,1,1,32,1024]{6,5,4,3,2,1,0:T(8,128)(2,1)S(1)}, bf16[2,1,1,1,1,32,1024]{6,5,4,3,2,1,0:T(8,128)(2,1)S(1)}, u32[]{:S(2)}, u32[]{:S(2)}) collective-permute-start(bf16[2,1,1,1,1,32,1024]{6,5,4,3,2,1,0:T(8,128)(2,1)S(1)} %constant_dynamic-slice_fusion.8), channel_id=1, source_target_pairs={{0,128},{16,144},{32,160},{48,176},{64,192},{80,208},{96,224},{112... | collective-permute-start | bytes 393224 | tf_op jit(solution)/shard_map/ppermute | solution.py:37
  31.5 14.5 %collective-permute-start.5 = (bf16[1,20,6,1024]{3,2,1,0:T(8,128)(2,1)}, bf16[1,20,6,1024]{3,2,1,0:T(8,128)(2,1)S(1)}, u32[]{:S(2)}, u32[]{:S(2)}) collective-permute-start(bf16[1,20,6,1024]{3,2,1,0:T(8,128)(2,1)} %get-tuple-element.19), channel_id=1, source_target_pairs={{0,1},{1,2},{2,3},{3,4},{4,5},{5,6},{6,7},{7,8},{8,9},{9,10},{10,1... | collective-permute-start | bytes 737288 | tf_op jit(solution)/shard_map/ppermute | solution.py:27
  38.0 10.2 %collective-permute-start.6 = (bf16[1,20,6,1024]{3,2,1,0:T(8,128)(2,1)}, bf16[1,20,6,1024]{3,2,1,0:T(8,128)(2,1)}, u32[]{:S(2)}, u32[]{:S(2)}) collective-permute-start(bf16[1,20,6,1024]{3,2,1,0:T(8,128)(2,1)} %get-tuple-element.20), channel_id=1, source_target_pairs={{1,0},{2,1},{3,2},{4,3},{5,4},{6,5},{7,6},{8,7},{9,8},{10,9},{11,1... | collective-permute-start | bytes 737288 | tf_op jit(solution)/shard_map/ppermute | solution.py:30
  43.7 16.1 %collective-permute-start.2 = (bf16[2,2,1,1,1,32,1024]{6,5,4,3,2,1,0:T(8,128)(2,1)}, bf16[2,2,1,1,1,32,1024]{6,5,4,3,2,1,0:T(8,128)(2,1)}, u32[]{:S(2)}, u32[]{:S(2)}) collective-permute-start(bf16[2,2,1,1,1,32,1024]{6,5,4,3,2,1,0:T(8,128)(2,1)} %constant_dynamic-slice_fusion.7), channel_id=1, source_target_pairs={{0,64},{16,80},{32,96},{48,112},{64,0},{80,16},{96,32},{112,48},{1... | collective-permute-start | bytes 786440 | tf_op jit(solution)/shard_map/ppermute | solution.py:37
  61.7 15.1 %collective-permute-start.7 = (bf16[2,2,2,1,1,32,1024]{6,5,4,3,2,1,0:T(8,128)(2,1)}, bf16[2,2,2,1,1,32,1024]{6,5,4,3,2,1,0:T(8,128)(2,1)S(1)}, u32[]{:S(2)}, u32[]{:S(2)}) collective-permute-start(bf16[2,2,2,1,1,32,1024]{6,5,4,3,2,1,0:T(8,128)(2,1)} %constant_dynamic-slice_fusion.6), channel_id=1, source_target_pairs={{0,32},{16,48},{32,0},{48,16},{64,96},{80,112},{96,64},{112,80},{1... | collective-permute-start | bytes 1572872 | tf_op jit(solution)/shard_map/ppermute | solution.py:37
  77.9 25.5 %collective-permute-start.8 = (bf16[2,2,2,2,1,32,1024]{6,5,4,3,2,1,0:T(8,128)(2,1)}, bf16[2,2,2,2,1,32,1024]{6,5,4,3,2,1,0:T(8,128)(2,1)}, u32[]{:S(2)}, u32[]{:S(2)}) collective-permute-start(bf16[2,2,2,2,1,32,1024]{6,5,4,3,2,1,0:T(8,128)(2,1)} %constant_dynamic-slice_fusion.5), channel_id=1, source_target_pairs={{0,16},{16,0},{32,48},{48,32},{64,80},{80,64},{96,112},{112,96},{1... | collective-permute-start | bytes 3145736 | tf_op jit(solution)/shard_map/ppermute | solution.py:37
  104.8 8.1 %collective-permute-start.9 = (bf16[32,32,1024]{2,1,0:T(8,128)(2,1)S(1)}, bf16[32,32,1024]{2,1,0:T(8,128)(2,1)}, u32[]{:S(2)}, u32[]{:S(2)}) collective-permute-start(bf16[32,32,1024]{2,1,0:T(8,128)(2,1)S(1)} %bitcast.103), channel_id=1, source_target_pairs={{0,1},{1,0},{2,3},{3,2},{4,5},{5,4},{6,7},{7,6},{8,9},{9,8},{10,11... | collective-permute-start | bytes 6291464 | tf_op jit(solution)/shard_map/ppermute | solution.py:37
  114.9 3.5 %copy-start.1 = (bf16[1,32,32,1024]{3,2,1,0:T(8,128)(2,1)}, bf16[1,32,32,1024]{3,2,1,0:T(8,128)(2,1)S(1)}, u32[]{:S(2)}) copy-start(bf16[1,32,32,1024]{3,2,1,0:T(8,128)(2,1)S(1)} %slice.66) | copy-start | bytes 6291460
  120.7 4.5 %copy-start.10 = (bf16[1,8,16,1024]{3,2,1,0:T(8,128)(2,1)S(1)}, bf16[1,8,16,1024]{3,2,1,0:T(8,128)(2,1)}, u32[]{:S(2)}) copy-start(bf16[1,8,16,1024]{3,2,1,0:T(8,128)(2,1)} %param.11) | copy-start | bytes 786436
  151.7 26.7 %collective-permute-start.10 = (f32[1024,512]{1,0:T(8,128)}, f32[1024,512]{1,0:T(8,128)}, u32[]{:S(2)}, u32[]{:S(2)}) collective-permute-start(f32[1024,512]{1,0:T(8,128)} %dynamic-slice_bitcast_fusion), channel_id=1, source_target_pairs={{0,1},{1,0},{2,3},{3,2},{4,5},{5,4},{6,7},{7,6},{8,9},{9,8},{10,11... | collective-permute-start | bytes 6291464 | tf_op jit(solution)/shard_map/ppermute | solution.py:37
  170.1 8.3 %copy-start.6 = (f32[1024,2,512]{2,0,1:T(8,128)S(1)}, f32[1024,2,512]{2,0,1:T(8,128)}, u32[]{:S(2)}) copy-start(f32[1024,2,512]{2,0,1:T(8,128)} %copy-done.5) | copy-start | bytes 12582916
  171.8 17.3 %collective-permute-start.19 = (f32[1,20,6,1024]{3,0,2,1:T(1,128)S(1)}, f32[1,20,6,1024]{3,0,2,1:T(1,128)S(1)}, u32[]{:S(2)}, u32[]{:S(2)}) collective-permute-start(f32[1,20,6,1024]{3,0,2,1:T(1,128)S(1)} %get-tuple-element.13), channel_id=1, source_target_pairs={{0,1},{1,2},{2,3},{3,4},{4,5},{5,6},{6,7},{7,8},{8,9},{9,10},{10,1... | collective-permute-start | bytes 1474568 | tf_op jit(solution)/shard_map/ppermute | solution.py:19
  176.5 14.5 %collective-permute-start.20 = (f32[1,20,6,1024]{3,0,2,1:T(1,128)S(1)}, f32[1,20,6,1024]{3,0,2,1:T(1,128)S(1)}, u32[]{:S(2)}, u32[]{:S(2)}) collective-permute-start(f32[1,20,6,1024]{3,0,2,1:T(1,128)S(1)} %get-tuple-element.14), channel_id=1, source_target_pairs={{1,0},{2,1},{3,2},{4,3},{5,4},{6,5},{7,6},{8,7},{9,8},{10,9},{11,1... | collective-permute-start | bytes 1474568 | tf_op jit(solution)/shard_map/ppermute | solution.py:19
  180.6 39.4 %collective-permute-start.11 = (f32[2,2,2,2,1,1,32,512]{7,6,5,4,3,2,1,0:T(8,128)S(1)}, f32[2,2,2,2,1,1,32,512]{7,6,5,4,3,2,1,0:T(8,128)S(1)}, u32[]{:S(2)}, u32[]{:S(2)}) collective-permute-start(f32[2,2,2,2,1,1,32,512]{7,6,5,4,3,2,1,0:T(8,128)S(1)} %constant_dynamic-slice_fusion.4), channel_id=1, source_target_pairs={{0,16},{16,0},{32,48},{48,32},{64,80},{80,64},{96,112},{112,96},{1... | collective-permute-start | bytes 3145736 | tf_op jit(solution)/shard_map/ppermute | solution.py:37
  192.5 27.7 %copy-start.3 = (f32[1,20,16,1024]{3,0,2,1:T(1,128)}, f32[1,20,16,1024]{3,0,2,1:T(1,128)S(1)}, u32[]{:S(2)}) copy-start(f32[1,20,16,1024]{3,0,2,1:T(1,128)S(1)} %fusion.16) | copy-start | bytes 3932164
  193.9 39.6 %collective-permute-start.21 = (f32[1,6,16,1024]{3,0,2,1:T(1,128)}, f32[1,6,16,1024]{3,0,2,1:T(1,128)}, u32[]{:S(2)}, u32[]{:S(2)}) collective-permute-start(f32[1,6,16,1024]{3,0,2,1:T(1,128)} %get-tuple-element.15), channel_id=1, source_target_pairs={{0,16},{16,32},{32,48},{48,64},{64,80},{80,96},{96,112},{112,128},... | collective-permute-start | bytes 1179656 | tf_op jit(solution)/shard_map/ppermute | solution.py:19
  196.0 37.6 %collective-permute-start.22 = (f32[1,6,16,1024]{3,0,2,1:T(1,128)}, f32[1,6,16,1024]{3,0,2,1:T(1,128)}, u32[]{:S(2)}, u32[]{:S(2)}) collective-permute-start(f32[1,6,16,1024]{3,0,2,1:T(1,128)} %get-tuple-element.16), channel_id=1, source_target_pairs={{16,0},{32,16},{48,32},{64,48},{80,64},{96,80},{112,96},{128,112},... | collective-permute-start | bytes 1179656 | tf_op jit(solution)/shard_map/ppermute | solution.py:19
  221.4 14.3 %collective-permute-start.12 = (f32[2,2,2,1,1,1,32,512]{7,6,5,4,3,2,1,0:T(8,128)}, f32[2,2,2,1,1,1,32,512]{7,6,5,4,3,2,1,0:T(8,128)}, u32[]{:S(2)}, u32[]{:S(2)}) collective-permute-start(f32[2,2,2,1,1,1,32,512]{7,6,5,4,3,2,1,0:T(8,128)} %constant_dynamic-slice_fusion.3), channel_id=1, source_target_pairs={{0,32},{16,48},{32,0},{48,16},{64,96},{80,112},{96,64},{112,80},{1... | collective-permute-start | bytes 1572872 | tf_op jit(solution)/shard_map/ppermute | solution.py:37
  233.6 13.1 %copy-start.2 = (bf16[1,32,32,1024]{3,2,1,0:T(8,128)(2,1)S(1)}, bf16[1,32,32,1024]{3,2,1,0:T(8,128)(2,1)}, u32[]{:S(2)}) copy-start(bf16[1,32,32,1024]{3,2,1,0:T(8,128)(2,1)} %copy-done.1) | copy-start | bytes 6291460
  237.1 16.2 %collective-permute-start.13 = (f32[2,2,1,1,1,1,32,512]{7,6,5,4,3,2,1,0:T(8,128)S(1)}, f32[2,2,1,1,1,1,32,512]{7,6,5,4,3,2,1,0:T(8,128)S(1)}, u32[]{:S(2)}, u32[]{:S(2)}) collective-permute-start(f32[2,2,1,1,1,1,32,512]{7,6,5,4,3,2,1,0:T(8,128)S(1)} %constant_dynamic-slice_fusion.2), channel_id=1, source_target_pairs={{0,64},{16,80},{32,96},{48,112},{64,0},{80,16},{96,32},{112,48},{1... | collective-permute-start | bytes 786440 | tf_op jit(solution)/shard_map/ppermute | solution.py:37
  253.3 17.7 %collective-permute-start.14 = (f32[2,1,1,1,1,1,32,512]{7,6,5,4,3,2,1,0:T(8,128)S(1)}, f32[2,1,1,1,1,1,32,512]{7,6,5,4,3,2,1,0:T(8,128)S(1)}, u32[]{:S(2)}, u32[]{:S(2)}) collective-permute-start(f32[2,1,1,1,1,1,32,512]{7,6,5,4,3,2,1,0:T(8,128)S(1)} %constant_dynamic-slice_fusion.1), channel_id=1, source_target_pairs={{0,128},{16,144},{32,160},{48,176},{64,192},{80,208},{96,224},{112... | collective-permute-start | bytes 393224 | tf_op jit(solution)/shard_map/ppermute | solution.py:37
  260.3 52.8 %copy-start.11 = (bf16[8,16,512]{2,1,0:T(8,128)(2,1)S(1)}, bf16[8,16,512]{2,1,0:T(8,128)(2,1)}, u32[]{:S(2)}) copy-start(bf16[8,16,512]{2,1,0:T(8,128)(2,1)} %reshape.261) | copy-start | bytes 393220
  271.1 16.0 %collective-permute-start.15 = (f32[1,1,1,1,1,1,32,512]{7,6,5,4,3,2,1,0:T(8,128)S(1)}, f32[1,1,1,1,1,1,32,512]{7,6,5,4,3,2,1,0:T(8,128)S(1)}, u32[]{:S(2)}, u32[]{:S(2)}) collective-permute-start(f32[1,1,1,1,1,1,32,512]{7,6,5,4,3,2,1,0:T(8,128)S(1)} %constant_dynamic-slice_fusion), channel_id=1, source_target_pairs={{0,256},{16,272},{32,288},{48,304},{64,320},{80,336},{96,352},{112... | collective-permute-start | bytes 196616 | tf_op jit(solution)/shard_map/ppermute | solution.py:37
  287.1 6.5 %collective-permute-start.16 = (f32[32,512]{1,0:T(8,128)S(1)}, f32[32,512]{1,0:T(8,128)S(1)}, u32[]{:S(2)}, u32[]{:S(2)}) collective-permute-start(f32[32,512]{1,0:T(8,128)S(1)} %add_bitcast_fusion), channel_id=1, source_target_pairs={{0,2},{1,3},{2,0},{3,1},{4,6},{5,7},{6,4},{7,5},{8,10},{9,11},{10,... | collective-permute-start | bytes 196616 | tf_op jit(solution)/shard_map/ppermute | solution.py:37
  293.6 5.9 %collective-permute-start.17 = (f32[32,512]{1,0:T(8,128)S(1)}, f32[32,512]{1,0:T(8,128)S(1)}, u32[]{:S(2)}, u32[]{:S(2)}) collective-permute-start(f32[32,512]{1,0:T(8,128)S(1)} %add.336), channel_id=1, source_target_pairs={{0,4},{1,5},{2,6},{3,7},{4,0},{5,1},{6,2},{7,3},{8,12},{9,13},{10,... | collective-permute-start | bytes 196616 | tf_op jit(solution)/shard_map/ppermute | solution.py:37
  299.6 6.5 %collective-permute-start.18 = (f32[32,512]{1,0:T(8,128)S(1)}, f32[32,512]{1,0:T(8,128)S(1)}, u32[]{:S(2)}, u32[]{:S(2)}) collective-permute-start(f32[32,512]{1,0:T(8,128)S(1)} %add.337), channel_id=1, source_target_pairs={{0,8},{1,9},{2,10},{3,11},{4,12},{5,13},{6,14},{7,15},{8,0},{9,1},... | collective-permute-start | bytes 196616 | tf_op jit(solution)/shard_map/ppermute | solution.py:37
  306.1 8.0 %collective-permute-start.23 = (f32[32,512]{1,0:T(8,128)S(1)}, f32[32,512]{1,0:T(8,128)S(1)}, u32[]{:S(2)}, u32[]{:S(2)}) collective-permute-start(f32[32,512]{1,0:T(8,128)S(1)} %add.338), channel_id=1, source_target_pairs={{0,1},{1,0},{2,3},{3,2},{4,5},{5,4},{6,7},{7,6},{8,9},{9,8},{10,11... | collective-permute-start | bytes 196616 | tf_op jit(solution)/shard_map/ppermute | solution.py:37
  (7 other events, 11.9 us)

commit v16 on v13

--- a/solution.py
+++ b/solution.py
@@ -75,12 +75,14 @@
     return held if tie is None else (held, tie)
 
 
-def scatter_by_bits(total, axis, groups):
+def scatter_by_bits(total, axis, groups, tie=None, tie_at=2):
     levels = lax.axis_size(axis).bit_length() - 1
     mine = [axis_bit(axis, bit) for bit in range(levels)]
     held = total.reshape((2,) * levels + (total.shape[0] // 2**levels,) + total.shape[1:])
     rest = [0] * (held.ndim - levels)
-    for group in groups:
+    for step, group in enumerate(groups):
+        if tie is not None and step == tie_at:
+            held, tie = lax.optimization_barrier((held, tie))
         size = [1 if b in group else held.shape[levels - 1 - b] for b in range(levels)]
         size = size[::-1] + list(held.shape[levels:])
         own = [mine[b] if b in group else 0 for b in range(levels)]
@@ -93,7 +95,8 @@
             send = lax.dynamic_slice(held, place[::-1] + rest, size)
             summed = summed + partner_swap(send, axis, mask)
         held = summed
-    return held.reshape(held.shape[levels:])
+    held = held.reshape(held.shape[levels:])
+    return held if tie is None else (held, tie)
 
 
 def gather_weights(w_query, w_keyvalue, w_output, row_groups, tie):
@@ -264,8 +267,7 @@
     inner_grad = inner_grad.reshape(batches, tile_rows * tile_cols, inner_width)
     query_grad, keyvalue_part = tile_backward(queries, keyvalue_ext, soft, rounded, inner_grad)
     keyvalue_part = keyvalue_part.reshape(batches, ext_rows, ext_cols, 2 * inner_width)
-    owned = fold_rows(fold_cols(keyvalue_part))
-    token_grad = owned.astype(jnp.bfloat16).reshape(-1, 2 * inner_width)
+    cols_folded = fold_cols(keyvalue_part)
     row_count, col_count = lax.axis_size("row"), lax.axis_size("col")
     col_levels = col_count.bit_length() - 1
     feature_part = model_width // row_count
@@ -281,9 +283,12 @@
     pair_part = lax.dynamic_index_in_dim(halves, own, 1, keepdims=False) + partner_swap(
         lax.dynamic_index_in_dim(halves, 1 - own, 1, keepdims=False), "col", 1
     )
-    rows_part = scatter_by_bits(
-        pair_part.reshape(row_count, feature_part, half), "row", row_groups
-    )[0]
+    rows_part, cols_folded = scatter_by_bits(
+        pair_part.reshape(row_count, feature_part, half), "row", row_groups, tie=cols_folded
+    )
+    rows_part = rows_part[0]
+    owned = fold_rows(cols_folded)
+    token_grad = owned.astype(jnp.bfloat16).reshape(-1, 2 * inner_width)
     for bit in range(1, col_levels):
         rows_part = rows_part + partner_swap(rows_part, "col", 1 << bit)
     held = jnp.zeros((2,) + rows_part.shape, rows_part.dtype)

time: 296 us -> 285 us (0.963)
  starting transfers between devices: 112 us -> 99 us
    ppermute x16, starting transfers between devices: 87 us -> 75.3 us  [partner_swap(): return lax.ppermute(value, axis, [(i, i ^ mask) for i in range(count)])]
    ppermute x4, waiting for transfers between devices: 3.9 us -> 0.83 us  [shifted(): lax.ppermute(value, axis, [(source, source + steps) for source in range(f...]
  transfers between devices with their start and end apart: 24 -> 24, of which waited for: 15 -> 16; matrix products, arithmetic and copies ran while one was open for 16% -> 18% of each run, Pallas kernels for 0% -> 0%
where the time goes in v16:
time: 285 us; the launch traced here: 283 us
  starting transfers between devices  99 us (35%)
  waiting for transfers between devices  86.4 us (30%)
  local copies, waits for them, and re-layouts  51.1 us (18%)
  matrix products  30.3 us (11%)
  other arithmetic  14.2 us (5%)
    ppermute x16, waiting for transfers between devices, partner_swap(): return lax.ppermute(value, axis, [(i, i ^ mask) for i in range(count)])  83.3 us
    ppermute x16, starting transfers between devices, partner_swap(): return lax.ppermute(value, axis, [(i, i ^ mask) for i in range(count)])  75.3 us
    ppermute x4, starting transfers between devices, shifted(): lax.ppermute(value, axis, [(source, source + steps) for source in range(f...  10.8 us
    ppermute x2, starting transfers between devices, with_halo(): lax.ppermute(lax.slice_in_dim(block, block.shape[dim] - width, None, axis...  9.7 us
    concatenate x3, local copies, waits for them, and re-layouts, tile_backward(): jnp.concatenate([key_grad.reshape(batches, ext_count, inner_width), value...  7.45 us
    dot_general x1, matrix products, tile_backward(): jnp.einsum('bhqk,bqhd->bkhd', score_grad, query_heads, preferred_element_...  5.84 us
    unnamed x33, local copies, waits for them, and re-layouts  5.72 us
  transfers between devices with their start and end apart: 24, of which 16 were waited for; matrix products, arithmetic and copies ran while one was open for 18% of the time, Pallas kernels for 0%

profile of v16, /device:TPU:1, one launch (start us, length us, event | category | flops | bytes accessed | tf_op | source)
XLA Modules:
  0.0 282.8 jit_solution(14239920468996388534)
XLA Ops:
  2.0 16.3 %collective-permute-start = (bf16[1,1,1,1,1,32,1024]{6,5,4,3,2,1,0:T(8,128)(2,1)S(1)}, bf16[1,1,1,1,1,32,1024]{6,5,4,3,2,1,0:T(8,128)(2,1)S(1)}, u32[]{:S(2)}, u32[]{:S(2)}) collective-permute-start(bf16[1,1,1,1,1,32,1024]{6,5,4,3,2,1,0:T(8,128)(2,1)S(1)} %constant_dynamic-slice_fusion.9), channel_id=1, source_target_pairs={{0,256},{16,272},{32,288},{48,304},{64,320},{80,336},{96,352},{112... | collective-permute-start | bytes 196616 | tf_op jit(solution)/shard_map/ppermute | solution.py:37
  18.9 3.2 %collective-permute-start.3 = (bf16[1,6,16,1024]{3,2,1,0:T(8,128)(2,1)S(1)}, bf16[1,6,16,1024]{3,2,1,0:T(8,128)(2,1)S(1)}, u32[]{:S(2)}, u32[]{:S(2)}) collective-permute-start(bf16[1,6,16,1024]{3,2,1,0:T(8,128)(2,1)S(1)} %get-tuple-element.21), channel_id=1, source_target_pairs={{0,16},{16,32},{32,48},{48,64},{64,80},{80,96},{96,112},{112,128},... | collective-permute-start | bytes 589832 | tf_op jit(solution)/shard_map/ppermute | solution.py:27
  23.5 6.9 %collective-permute-start.1 = (bf16[2,1,1,1,1,32,1024]{6,5,4,3,2,1,0:T(8,128)(2,1)S(1)}, bf16[2,1,1,1,1,32,1024]{6,5,4,3,2,1,0:T(8,128)(2,1)S(1)}, u32[]{:S(2)}, u32[]{:S(2)}) collective-permute-start(bf16[2,1,1,1,1,32,1024]{6,5,4,3,2,1,0:T(8,128)(2,1)S(1)} %constant_dynamic-slice_fusion.8), channel_id=1, source_target_pairs={{0,128},{16,144},{32,160},{48,176},{64,192},{80,208},{96,224},{112... | collective-permute-start | bytes 393224 | tf_op jit(solution)/shard_map/ppermute | solution.py:37
  31.5 6.5 %collective-permute-start.5 = (bf16[1,20,6,1024]{3,2,1,0:T(8,128)(2,1)}, bf16[1,20,6,1024]{3,2,1,0:T(8,128)(2,1)S(1)}, u32[]{:S(2)}, u32[]{:S(2)}) collective-permute-start(bf16[1,20,6,1024]{3,2,1,0:T(8,128)(2,1)} %get-tuple-element.19), channel_id=1, source_target_pairs={{0,1},{1,2},{2,3},{3,4},{4,5},{5,6},{6,7},{7,8},{8,9},{9,10},{10,1... | collective-permute-start | bytes 737288 | tf_op jit(solution)/shard_map/ppermute | solution.py:27
  39.9 3.1 %collective-permute-done.1 = bf16[2,1,1,1,1,32,1024]{6,5,4,3,2,1,0:T(8,128)(2,1)S(1)} collective-permute-done((bf16[2,1,1,1,1,32,1024]{6,5,4,3,2,1,0:T(8,128)(2,1)S(1)}, bf16[2,1,1,1,1,32,1024]{6,5,4,3,2,1,0:T(8,128)(2,1)S(1)}, u32[]{:S(2)}, u32[]{:S(2)}) %collective-permute-start.1) | collective-permute-done | bytes 131104 | tf_op jit(solution)/shard_map/ppermute | solution.py:37
  53.1 6.7 %collective-permute-done.2 = bf16[2,2,1,1,1,32,1024]{6,5,4,3,2,1,0:T(8,128)(2,1)} collective-permute-done((bf16[2,2,1,1,1,32,1024]{6,5,4,3,2,1,0:T(8,128)(2,1)}, bf16[2,2,1,1,1,32,1024]{6,5,4,3,2,1,0:T(8,128)(2,1)}, u32[]{:S(2)}, u32[]{:S(2)}) %collective-permute-start.2) | collective-permute-done | bytes 262176 | tf_op jit(solution)/shard_map/ppermute | solution.py:37
  63.6 13.2 %collective-permute-done.7 = bf16[2,2,2,1,1,32,1024]{6,5,4,3,2,1,0:T(8,128)(2,1)S(1)} collective-permute-done((bf16[2,2,2,1,1,32,1024]{6,5,4,3,2,1,0:T(8,128)(2,1)}, bf16[2,2,2,1,1,32,1024]{6,5,4,3,2,1,0:T(8,128)(2,1)S(1)}, u32[]{:S(2)}, u32[]{:S(2)}) %collective-permute-start.7) | collective-permute-done | bytes 524320 | tf_op jit(solution)/shard_map/ppermute | solution.py:37
  79.8 23.6 %collective-permute-done.8 = bf16[2,2,2,2,1,32,1024]{6,5,4,3,2,1,0:T(8,128)(2,1)} collective-permute-done((bf16[2,2,2,2,1,32,1024]{6,5,4,3,2,1,0:T(8,128)(2,1)}, bf16[2,2,2,2,1,32,1024]{6,5,4,3,2,1,0:T(8,128)(2,1)}, u32[]{:S(2)}, u32[]{:S(2)}) %collective-permute-start.8) | collective-permute-done | bytes 1048608 | tf_op jit(solution)/shard_map/ppermute | solution.py:37
  104.8 4.3 %collective-permute-start.9 = (bf16[32,32,1024]{2,1,0:T(8,128)(2,1)S(1)}, bf16[32,32,1024]{2,1,0:T(8,128)(2,1)}, u32[]{:S(2)}, u32[]{:S(2)}) collective-permute-start(bf16[32,32,1024]{2,1,0:T(8,128)(2,1)S(1)} %bitcast.107), channel_id=1, source_target_pairs={{0,1},{1,0},{2,3},{3,2},{4,5},{5,4},{6,7},{7,6},{8,9},{9,8},{10,11... | collective-permute-start | bytes 6291464 | tf_op jit(solution)/shard_map/ppermute | solution.py:37
  119.4 3.3 %fusion.15 = bf16[1,560,1024]{2,1,0:T(8,128)(2,1)S(1)} fusion(bf16[560,1024]{1,0:T(8,128)(2,1)} %reshape.257, bf16[1024,1024]{1,0:T(8,128)(2,1)} %bitcast.113), kind=kOutput, calls=%fused_computation.16 | convolution fusion | flops 1174978560 | bytes 4390912 | tf_op jit(solution)/shard_map/dot_general | solution.py:246
  128.5 3.4 %fusion.78 = (f32[8,128]{1,0:T(8,128)S(1)}, f32[8,128,560]{1,2,0:T(8,128)}) fusion(pred[128,560]{0,1:T(8,128)(4,1)} %fusion.47, bf16[128,8,64]{0,2,1:T(8,128)(2,1)S(1)} %bitcast.133, bf16[560,8,64]{0,2,1:T(8,128)(2,1)} %bitcast.122), kind=kOutput, calls=%fused_computation.131 | convolution fusion | flops 75694640 | bytes 3074048 | tf_op jit(solution)/shard_map/sub | solution.py:160
  132.0 3.6 %fusion.79 = (bf16[1,560,8,64]{1,3,2,0:T(8,128)(2,1)}, f32[1,560,8,64]{1,3,2,0:T(8,128)}) fusion(bf16[128,8,64]{0,2,1:T(8,128)(2,1)S(1)} %bitcast.130, f32[8,128]{1,0:T(8,128)S(1)} %get-tuple-element.23, pred[128,560]{0,1:T(8,128)(4,1)} %fusion.47, bf16[128,8,64]{0,2,1:T(8,128)(2,1)S(1)} %bitcast.134, bf16[560,8,64]{0,2,1:T(8,128)(2,1)} %bitcast.123), kind=kOutput, calls=%fused_computation.132 | convolution fusion | flops 149956144 | bytes 2631680 | tf_op jit(solution)/shard_map/bhqk,bqhd->bkhd/dot_general | solution.py:187
  135.7 5.8 %fusion.80 = (bf16[1,560,8,64]{1,3,2,0:T(8,128)(2,1)}, f32[1,560,8,64]{1,3,2,0:T(8,128)}) fusion(bf16[128,8,64]{0,2,1:T(8,128)(2,1)S(1)} %bitcast.135, f32[8,128,560]{1,2,0:T(8,128)} %fusion.83, f32[8,128,560]{1,2,0:T(8,128)} %get-tuple-element.24, f32[8,128]{1,0:T(8,128)S(1)} %get-tuple-element.23), kind=kOutput, calls=%fused_computation.133 | convolution fusion | flops 77702704 | bytes 6443008 | tf_op jit(solution)/shard_map/bhqk,bqhd->bkhd/dot_general | solution.py:184
  149.7 3.8 %collective-permute-done.10 = f32[1024,512]{1,0:T(8,128)S(1)} collective-permute-done((f32[1024,512]{1,0:T(8,128)S(1)}, f32[1024,512]{1,0:T(8,128)S(1)}, u32[]{:S(2)}, u32[]{:S(2)}) %collective-permute-start.10) | collective-permute-done | bytes 2097184 | tf_op jit(solution)/shard_map/ppermute | solution.py:37
  158.5 3.0 %copy.25 = f32[1,560,8,64]{3,2,0,1:T(8,128)} copy(f32[1,560,8,64]{1,3,2,0:T(8,128)} %get-tuple-element.26) | data formatting | bytes 2293760 | tf_op jit(solution)/shard_map/bhqk,bqhd->bkhd/transpose | solution.py:187
  161.5 2.8 %concatenate.25 = f32[1,20,28,512]{3,0,2,1:T(1,128)S(1)} reshape(f32[1,560,8,64]{3,2,0,1:T(8,128)} %copy.25) | data formatting | bytes 2293760 | tf_op jit(solution)/shard_map/concatenate | solution.py:191
  164.4 3.0 %copy.24 = f32[1,560,8,64]{3,2,0,1:T(8,128)} copy(f32[1,560,8,64]{1,3,2,0:T(8,128)} %get-tuple-element.28) | data formatting | bytes 2293760 | tf_op jit(solution)/shard_map/bhqk,bqhd->bkhd/transpose | solution.py:184
  167.4 3.6 %concatenate.24 = f32[1,20,28,512]{3,0,2,1:T(1,128)} reshape(f32[1,560,8,64]{3,2,0,1:T(8,128)} %copy.24) | data formatting | bytes 2293760 | tf_op jit(solution)/shard_map/concatenate | solution.py:191
  176.3 5.2 %collective-permute-start.13 = (f32[1,20,6,1024]{3,0,2,1:T(1,128)}, f32[1,20,6,1024]{3,0,2,1:T(1,128)}, u32[]{:S(2)}, u32[]{:S(2)}) collective-permute-start(f32[1,20,6,1024]{3,0,2,1:T(1,128)} %get-tuple-element.13), channel_id=1, source_target_pairs={{0,1},{1,2},{2,3},{3,4},{4,5},{5,6},{6,7},{7,8},{8,9},{9,10},{10,1... | collective-permute-start | bytes 1474568 | tf_op jit(solution)/shard_map/ppermute | solution.py:19
  193.5 2.8 fusion.16
  196.3 4.4 %collective-permute-done.12 = f32[2,2,2,1,1,1,32,512]{7,6,5,4,3,2,1,0:T(8,128)} collective-permute-done((f32[2,2,2,1,1,1,32,512]{7,6,5,4,3,2,1,0:T(8,128)}, f32[2,2,2,1,1,1,32,512]{7,6,5,4,3,2,1,0:T(8,128)}, u32[]{:S(2)}, u32[]{:S(2)}) %collective-permute-start.12) | collective-permute-done | bytes 524320 | tf_op jit(solution)/shard_map/ppermute | solution.py:37
  201.9 5.5 %collective-permute-start.17 = (f32[2,2,1,1,1,1,32,512]{7,6,5,4,3,2,1,0:T(8,128)S(1)}, f32[2,2,1,1,1,1,32,512]{7,6,5,4,3,2,1,0:T(8,128)S(1)}, u32[]{:S(2)}, u32[]{:S(2)}) collective-permute-start(f32[2,2,1,1,1,1,32,512]{7,6,5,4,3,2,1,0:T(8,128)S(1)} %constant_dynamic-slice_fusion.2), channel_id=1, source_target_pairs={{0,64},{16,80},{32,96},{48,112},{64,0},{80,16},{96,32},{112,48},{1... | collective-permute-start | bytes 786440 | tf_op jit(solution)/shard_map/ppermute | solution.py:37
  213.5 5.5 %collective-permute-done.17 = f32[2,2,1,1,1,1,32,512]{7,6,5,4,3,2,1,0:T(8,128)S(1)} collective-permute-done((f32[2,2,1,1,1,1,32,512]{7,6,5,4,3,2,1,0:T(8,128)S(1)}, f32[2,2,1,1,1,1,32,512]{7,6,5,4,3,2,1,0:T(8,128)S(1)}, u32[]{:S(2)}, u32[]{:S(2)}) %collective-permute-start.17) | collective-permute-done | bytes 262176 | tf_op jit(solution)/shard_map/ppermute | solution.py:37
  219.8 4.4 %collective-permute-start.18 = (f32[2,1,1,1,1,1,32,512]{7,6,5,4,3,2,1,0:T(8,128)}, f32[2,1,1,1,1,1,32,512]{7,6,5,4,3,2,1,0:T(8,128)}, u32[]{:S(2)}, u32[]{:S(2)}) collective-permute-start(f32[2,1,1,1,1,1,32,512]{7,6,5,4,3,2,1,0:T(8,128)} %constant_dynamic-slice_fusion.1), channel_id=1, source_target_pairs={{0,128},{16,144},{32,160},{48,176},{64,192},{80,208},{96,224},{112... | collective-permute-start | bytes 393224 | tf_op jit(solution)/shard_map/ppermute | solution.py:37
  224.1 4.6 %fusion.19 = bf16[8,64,128]{2,1,0:T(8,128)(2,1)S(1)} fusion(bf16[560,8,64]{0,2,1:T(8,128)(2,1)S(1)} %bitcast.125, f32[8,128,560]{1,2,0:T(8,128)} %fusion.83, f32[8,128,560]{1,2,0:T(8,128)} %get-tuple-element.24, f32[8,128]{1,0:T(8,128)S(1)} %get-tuple-element.23), kind=kOutput, calls=%fused_computation.24 | convolution fusion | flops 77481520 | bytes 5296128 | tf_op jit(solution)/shard_map/bhqk,bkhd->bqhd/dot_general | solution.py:181
  228.7 9.4 %collective-permute-done.18 = f32[2,1,1,1,1,1,32,512]{7,6,5,4,3,2,1,0:T(8,128)} collective-permute-done((f32[2,1,1,1,1,1,32,512]{7,6,5,4,3,2,1,0:T(8,128)}, f32[2,1,1,1,1,1,32,512]{7,6,5,4,3,2,1,0:T(8,128)}, u32[]{:S(2)}, u32[]{:S(2)}) %collective-permute-start.18) | collective-permute-done | bytes 131104 | tf_op jit(solution)/shard_map/ppermute | solution.py:37
  239.1 7.4 %collective-permute-start.19 = (f32[1,1,1,1,1,1,32,512]{7,6,5,4,3,2,1,0:T(8,128)S(1)}, f32[1,1,1,1,1,1,32,512]{7,6,5,4,3,2,1,0:T(8,128)S(1)}, u32[]{:S(2)}, u32[]{:S(2)}) collective-permute-start(f32[1,1,1,1,1,1,32,512]{7,6,5,4,3,2,1,0:T(8,128)S(1)} %constant_dynamic-slice_fusion), channel_id=1, source_target_pairs={{0,256},{16,272},{32,288},{48,304},{64,320},{80,336},{96,352},{112... | collective-permute-start | bytes 196616 | tf_op jit(solution)/shard_map/ppermute | solution.py:37
  249.7 4.4 %collective-permute-done.19 = f32[1,1,1,1,1,1,32,512]{7,6,5,4,3,2,1,0:T(8,128)S(1)} collective-permute-done((f32[1,1,1,1,1,1,32,512]{7,6,5,4,3,2,1,0:T(8,128)S(1)}, f32[1,1,1,1,1,1,32,512]{7,6,5,4,3,2,1,0:T(8,128)S(1)}, u32[]{:S(2)}, u32[]{:S(2)}) %collective-permute-start.19) | collective-permute-done | bytes 65568 | tf_op jit(solution)/shard_map/ppermute | solution.py:37
  254.1 5.0 %collective-permute-start.20 = (f32[32,512]{1,0:T(8,128)S(1)}, f32[32,512]{1,0:T(8,128)S(1)}, u32[]{:S(2)}, u32[]{:S(2)}) collective-permute-start(f32[32,512]{1,0:T(8,128)S(1)} %add_bitcast_fusion), channel_id=1, source_target_pairs={{0,2},{1,3},{2,0},{3,1},{4,6},{5,7},{6,4},{7,5},{8,10},{9,11},{10,... | collective-permute-start | bytes 196616 | tf_op jit(solution)/shard_map/ppermute | solution.py:37
  265.8 3.4 %collective-permute-start.22 = (f32[32,512]{1,0:T(8,128)S(1)}, f32[32,512]{1,0:T(8,128)S(1)}, u32[]{:S(2)}, u32[]{:S(2)}) collective-permute-start(f32[32,512]{1,0:T(8,128)S(1)} %add.345), channel_id=1, source_target_pairs={{0,8},{1,9},{2,10},{3,11},{4,12},{5,13},{6,14},{7,15},{8,0},{9,1},... | collective-permute-start | bytes 196616 | tf_op jit(solution)/shard_map/ppermute | solution.py:37
  269.3 3.4 %collective-permute-done.22 = f32[32,512]{1,0:T(8,128)S(1)} collective-permute-done((f32[32,512]{1,0:T(8,128)S(1)}, f32[32,512]{1,0:T(8,128)S(1)}, u32[]{:S(2)}, u32[]{:S(2)}) %collective-permute-start.22) | collective-permute-done | bytes 65568 | tf_op jit(solution)/shard_map/ppermute | solution.py:37
  272.7 7.0 %collective-permute-start.23 = (f32[32,512]{1,0:T(8,128)S(1)}, f32[32,512]{1,0:T(8,128)S(1)}, u32[]{:S(2)}, u32[]{:S(2)}) collective-permute-start(f32[32,512]{1,0:T(8,128)S(1)} %add.346), channel_id=1, source_target_pairs={{0,1},{1,0},{2,3},{3,2},{4,5},{5,4},{6,7},{7,6},{8,9},{9,8},{10,11... | collective-permute-start | bytes 196616 | tf_op jit(solution)/shard_map/ppermute | solution.py:37
  (138 shorter events, 92.3 us)
Async XLA Ops:
  0.7 17.6 %copy-start = (bf16[1,8,16,1024]{3,2,1,0:T(8,128)(2,1)S(1)}, bf16[1,8,16,1024]{3,2,1,0:T(8,128)(2,1)}, u32[]{:S(2)}) copy-start(bf16[1,8,16,1024]{3,2,1,0:T(8,128)(2,1)} %param.6) | copy-start | bytes 786436
  0.7 17.9 %copy-start.12 = (f32[1024]{0:T(1024)S(1)}, f32[1024]{0:T(1024)}, u32[]{:S(2)}) copy-start(f32[1024]{0:T(1024)} %param.7) | copy-start | bytes 12292
  2.0 21.5 %collective-permute-start = (bf16[1,1,1,1,1,32,1024]{6,5,4,3,2,1,0:T(8,128)(2,1)S(1)}, bf16[1,1,1,1,1,32,1024]{6,5,4,3,2,1,0:T(8,128)(2,1)S(1)}, u32[]{:S(2)}, u32[]{:S(2)}) collective-permute-start(bf16[1,1,1,1,1,32,1024]{6,5,4,3,2,1,0:T(8,128)(2,1)S(1)} %constant_dynamic-slice_fusion.9), channel_id=1, source_target_pairs={{0,256},{16,272},{32,288},{48,304},{64,320},{80,336},{96,352},{112... | collective-permute-start | bytes 196616 | tf_op jit(solution)/shard_map/ppermute | solution.py:37
  18.9 11.5 %collective-permute-start.3 = (bf16[1,6,16,1024]{3,2,1,0:T(8,128)(2,1)S(1)}, bf16[1,6,16,1024]{3,2,1,0:T(8,128)(2,1)S(1)}, u32[]{:S(2)}, u32[]{:S(2)}) collective-permute-start(bf16[1,6,16,1024]{3,2,1,0:T(8,128)(2,1)S(1)} %get-tuple-element.21), channel_id=1, source_target_pairs={{0,16},{16,32},{32,48},{48,64},{64,80},{80,96},{96,112},{112,128},... | collective-permute-start | bytes 589832 | tf_op jit(solution)/shard_map/ppermute | solution.py:27
  22.1 8.3 %collective-permute-start.4 = (bf16[1,6,16,1024]{3,2,1,0:T(8,128)(2,1)S(1)}, bf16[1,6,16,1024]{3,2,1,0:T(8,128)(2,1)S(1)}, u32[]{:S(2)}, u32[]{:S(2)}) collective-permute-start(bf16[1,6,16,1024]{3,2,1,0:T(8,128)(2,1)S(1)} %get-tuple-element.22), channel_id=1, source_target_pairs={{16,0},{32,16},{48,32},{64,48},{80,64},{96,80},{112,96},{128,112},... | collective-permute-start | bytes 589832 | tf_op jit(solution)/shard_map/ppermute | solution.py:30
  23.5 19.5 %collective-permute-start.1 = (bf16[2,1,1,1,1,32,1024]{6,5,4,3,2,1,0:T(8,128)(2,1)S(1)}, bf16[2,1,1,1,1,32,1024]{6,5,4,3,2,1,0:T(8,128)(2,1)S(1)}, u32[]{:S(2)}, u32[]{:S(2)}) collective-permute-start(bf16[2,1,1,1,1,32,1024]{6,5,4,3,2,1,0:T(8,128)(2,1)S(1)} %constant_dynamic-slice_fusion.8), channel_id=1, source_target_pairs={{0,128},{16,144},{32,160},{48,176},{64,192},{80,208},{96,224},{112... | collective-permute-start | bytes 393224 | tf_op jit(solution)/shard_map/ppermute | solution.py:37
  31.5 14.5 %collective-permute-start.5 = (bf16[1,20,6,1024]{3,2,1,0:T(8,128)(2,1)}, bf16[1,20,6,1024]{3,2,1,0:T(8,128)(2,1)S(1)}, u32[]{:S(2)}, u32[]{:S(2)}) collective-permute-start(bf16[1,20,6,1024]{3,2,1,0:T(8,128)(2,1)} %get-tuple-element.19), channel_id=1, source_target_pairs={{0,1},{1,2},{2,3},{3,4},{4,5},{5,6},{6,7},{7,8},{8,9},{9,10},{10,1... | collective-permute-start | bytes 737288 | tf_op jit(solution)/shard_map/ppermute | solution.py:27
  38.0 10.2 %collective-permute-start.6 = (bf16[1,20,6,1024]{3,2,1,0:T(8,128)(2,1)}, bf16[1,20,6,1024]{3,2,1,0:T(8,128)(2,1)}, u32[]{:S(2)}, u32[]{:S(2)}) collective-permute-start(bf16[1,20,6,1024]{3,2,1,0:T(8,128)(2,1)} %get-tuple-element.20), channel_id=1, source_target_pairs={{1,0},{2,1},{3,2},{4,3},{5,4},{6,5},{7,6},{8,7},{9,8},{10,9},{11,1... | collective-permute-start | bytes 737288 | tf_op jit(solution)/shard_map/ppermute | solution.py:30
  43.7 16.1 %collective-permute-start.2 = (bf16[2,2,1,1,1,32,1024]{6,5,4,3,2,1,0:T(8,128)(2,1)}, bf16[2,2,1,1,1,32,1024]{6,5,4,3,2,1,0:T(8,128)(2,1)}, u32[]{:S(2)}, u32[]{:S(2)}) collective-permute-start(bf16[2,2,1,1,1,32,1024]{6,5,4,3,2,1,0:T(8,128)(2,1)} %constant_dynamic-slice_fusion.7), channel_id=1, source_target_pairs={{0,64},{16,80},{32,96},{48,112},{64,0},{80,16},{96,32},{112,48},{1... | collective-permute-start | bytes 786440 | tf_op jit(solution)/shard_map/ppermute | solution.py:37
  61.7 15.1 %collective-permute-start.7 = (bf16[2,2,2,1,1,32,1024]{6,5,4,3,2,1,0:T(8,128)(2,1)}, bf16[2,2,2,1,1,32,1024]{6,5,4,3,2,1,0:T(8,128)(2,1)S(1)}, u32[]{:S(2)}, u32[]{:S(2)}) collective-permute-start(bf16[2,2,2,1,1,32,1024]{6,5,4,3,2,1,0:T(8,128)(2,1)} %constant_dynamic-slice_fusion.6), channel_id=1, source_target_pairs={{0,32},{16,48},{32,0},{48,16},{64,96},{80,112},{96,64},{112,80},{1... | collective-permute-start | bytes 1572872 | tf_op jit(solution)/shard_map/ppermute | solution.py:37
  77.9 25.5 %collective-permute-start.8 = (bf16[2,2,2,2,1,32,1024]{6,5,4,3,2,1,0:T(8,128)(2,1)}, bf16[2,2,2,2,1,32,1024]{6,5,4,3,2,1,0:T(8,128)(2,1)}, u32[]{:S(2)}, u32[]{:S(2)}) collective-permute-start(bf16[2,2,2,2,1,32,1024]{6,5,4,3,2,1,0:T(8,128)(2,1)} %constant_dynamic-slice_fusion.5), channel_id=1, source_target_pairs={{0,16},{16,0},{32,48},{48,32},{64,80},{80,64},{96,112},{112,96},{1... | collective-permute-start | bytes 3145736 | tf_op jit(solution)/shard_map/ppermute | solution.py:37
  104.8 8.1 %collective-permute-start.9 = (bf16[32,32,1024]{2,1,0:T(8,128)(2,1)S(1)}, bf16[32,32,1024]{2,1,0:T(8,128)(2,1)}, u32[]{:S(2)}, u32[]{:S(2)}) collective-permute-start(bf16[32,32,1024]{2,1,0:T(8,128)(2,1)S(1)} %bitcast.107), channel_id=1, source_target_pairs={{0,1},{1,0},{2,3},{3,2},{4,5},{5,4},{6,7},{7,6},{8,9},{9,8},{10,11... | collective-permute-start | bytes 6291464 | tf_op jit(solution)/shard_map/ppermute | solution.py:37
  119.4 16.2 %copy-start.11 = (bf16[128,512]{0,1:T(8,128)(2,1)}, bf16[128,512]{0,1:T(8,128)(2,1)S(1)}, u32[]{:S(2)}) copy-start(bf16[128,512]{0,1:T(8,128)(2,1)S(1)} %copy.18) | copy-start | bytes 393220
  147.4 6.1 %collective-permute-start.10 = (f32[1024,512]{1,0:T(8,128)S(1)}, f32[1024,512]{1,0:T(8,128)S(1)}, u32[]{:S(2)}, u32[]{:S(2)}) collective-permute-start(f32[1024,512]{1,0:T(8,128)S(1)} %dynamic-slice_bitcast_fusion), channel_id=1, source_target_pairs={{0,1},{1,0},{2,3},{3,2},{4,5},{5,4},{6,7},{7,6},{8,9},{9,8},{10,11... | collective-permute-start | bytes 6291464 | tf_op jit(solution)/shard_map/ppermute | solution.py:37
  156.3 27.1 %collective-permute-start.11 = (f32[2,2,2,2,1,1,32,512]{7,6,5,4,3,2,1,0:T(8,128)}, f32[2,2,2,2,1,1,32,512]{7,6,5,4,3,2,1,0:T(8,128)}, u32[]{:S(2)}, u32[]{:S(2)}) collective-permute-start(f32[2,2,2,2,1,1,32,512]{7,6,5,4,3,2,1,0:T(8,128)} %constant_dynamic-slice_fusion.4), channel_id=1, source_target_pairs={{0,16},{16,0},{32,48},{48,32},{64,80},{80,64},{96,112},{112,96},{1... | collective-permute-start | bytes 3145736 | tf_op jit(solution)/shard_map/ppermute | solution.py:37
  174.5 10.4 %copy-start.5 = (f32[1,20,28,1024]{3,0,2,1:T(1,128)}, f32[1,20,28,1024]{3,0,2,1:T(1,128)S(1)}, u32[]{:S(2)}) copy-start(f32[1,20,28,1024]{3,0,2,1:T(1,128)S(1)} %constant_dynamic-update-slice_fusion.6) | copy-start | bytes 6881284
  176.3 16.6 %collective-permute-start.13 = (f32[1,20,6,1024]{3,0,2,1:T(1,128)}, f32[1,20,6,1024]{3,0,2,1:T(1,128)}, u32[]{:S(2)}, u32[]{:S(2)}) collective-permute-start(f32[1,20,6,1024]{3,0,2,1:T(1,128)} %get-tuple-element.13), channel_id=1, source_target_pairs={{0,1},{1,2},{2,3},{3,4},{4,5},{5,6},{6,7},{7,8},{8,9},{9,10},{10,1... | collective-permute-start | bytes 1474568 | tf_op jit(solution)/shard_map/ppermute | solution.py:19
  181.5 12.0 %collective-permute-start.14 = (f32[1,20,6,1024]{3,0,2,1:T(1,128)}, f32[1,20,6,1024]{3,0,2,1:T(1,128)}, u32[]{:S(2)}, u32[]{:S(2)}) collective-permute-start(f32[1,20,6,1024]{3,0,2,1:T(1,128)} %get-tuple-element.14), channel_id=1, source_target_pairs={{1,0},{2,1},{3,2},{4,3},{5,4},{6,5},{7,6},{8,7},{9,8},{10,9},{11,1... | collective-permute-start | bytes 1474568 | tf_op jit(solution)/shard_map/ppermute | solution.py:19
  185.8 15.0 %collective-permute-start.12 = (f32[2,2,2,1,1,1,32,512]{7,6,5,4,3,2,1,0:T(8,128)}, f32[2,2,2,1,1,1,32,512]{7,6,5,4,3,2,1,0:T(8,128)}, u32[]{:S(2)}, u32[]{:S(2)}) collective-permute-start(f32[2,2,2,1,1,1,32,512]{7,6,5,4,3,2,1,0:T(8,128)} %constant_dynamic-slice_fusion.3), channel_id=1, source_target_pairs={{0,32},{16,48},{32,0},{48,16},{64,96},{80,112},{96,64},{112,80},{1... | collective-permute-start | bytes 1572872 | tf_op jit(solution)/shard_map/ppermute | solution.py:37
  196.3 13.5 %copy-start.4 = (f32[1,20,16,1024]{3,0,2,1:T(1,128)}, f32[1,20,16,1024]{3,0,2,1:T(1,128)S(1)}, u32[]{:S(2)}) copy-start(f32[1,20,16,1024]{3,0,2,1:T(1,128)S(1)} %fusion.16) | copy-start | bytes 3932164
  201.9 22.2 %copy-start.10 = (bf16[1,560,512]{1,2,0:T(8,128)(2,1)S(1)}, bf16[1,560,512]{1,2,0:T(8,128)(2,1)}, u32[]{:S(2)}) copy-start(bf16[1,560,512]{1,2,0:T(8,128)(2,1)} %copy.19) | copy-start | bytes 1720324
  201.9 17.1 %collective-permute-start.17 = (f32[2,2,1,1,1,1,32,512]{7,6,5,4,3,2,1,0:T(8,128)S(1)}, f32[2,2,1,1,1,1,32,512]{7,6,5,4,3,2,1,0:T(8,128)S(1)}, u32[]{:S(2)}, u32[]{:S(2)}) collective-permute-start(f32[2,2,1,1,1,1,32,512]{7,6,5,4,3,2,1,0:T(8,128)S(1)} %constant_dynamic-slice_fusion.2), channel_id=1, source_target_pairs={{0,64},{16,80},{32,96},{48,112},{64,0},{80,16},{96,32},{112,48},{1... | collective-permute-start | bytes 786440 | tf_op jit(solution)/shard_map/ppermute | solution.py:37
  209.8 36.7 %collective-permute-start.15 = (f32[1,6,16,1024]{3,0,2,1:T(1,128)}, f32[1,6,16,1024]{3,0,2,1:T(1,128)S(1)}, u32[]{:S(2)}, u32[]{:S(2)}) collective-permute-start(f32[1,6,16,1024]{3,0,2,1:T(1,128)} %get-tuple-element.15), channel_id=1, source_target_pairs={{0,16},{16,32},{32,48},{48,64},{64,80},{80,96},{96,112},{112,128},... | collective-permute-start | bytes 1179656 | tf_op jit(solution)/shard_map/ppermute | solution.py:19
  212.2 34.3 %collective-permute-start.16 = (f32[1,6,16,1024]{3,0,2,1:T(1,128)S(1)}, f32[1,6,16,1024]{3,0,2,1:T(1,128)S(1)}, u32[]{:S(2)}, u32[]{:S(2)}) collective-permute-start(f32[1,6,16,1024]{3,0,2,1:T(1,128)S(1)} %get-tuple-element.16), channel_id=1, source_target_pairs={{16,0},{32,16},{48,32},{64,48},{80,64},{96,80},{112,96},{128,112},... | collective-permute-start | bytes 1179656 | tf_op jit(solution)/shard_map/ppermute | solution.py:19
  219.8 18.4 %collective-permute-start.18 = (f32[2,1,1,1,1,1,32,512]{7,6,5,4,3,2,1,0:T(8,128)}, f32[2,1,1,1,1,1,32,512]{7,6,5,4,3,2,1,0:T(8,128)}, u32[]{:S(2)}, u32[]{:S(2)}) collective-permute-start(f32[2,1,1,1,1,1,32,512]{7,6,5,4,3,2,1,0:T(8,128)} %constant_dynamic-slice_fusion.1), channel_id=1, source_target_pairs={{0,128},{16,144},{32,160},{48,176},{64,192},{80,208},{96,224},{112... | collective-permute-start | bytes 393224 | tf_op jit(solution)/shard_map/ppermute | solution.py:37
  228.7 19.6 %copy-start.3 = (bf16[1,32,32,1024]{3,2,1,0:T(8,128)(2,1)S(1)}, bf16[1,32,32,1024]{3,2,1,0:T(8,128)(2,1)}, u32[]{:S(2)}) copy-start(bf16[1,32,32,1024]{3,2,1,0:T(8,128)(2,1)} %slice.66) | copy-start | bytes 6291460
  239.1 15.0 %collective-permute-start.19 = (f32[1,1,1,1,1,1,32,512]{7,6,5,4,3,2,1,0:T(8,128)S(1)}, f32[1,1,1,1,1,1,32,512]{7,6,5,4,3,2,1,0:T(8,128)S(1)}, u32[]{:S(2)}, u32[]{:S(2)}) collective-permute-start(f32[1,1,1,1,1,1,32,512]{7,6,5,4,3,2,1,0:T(8,128)S(1)} %constant_dynamic-slice_fusion), channel_id=1, source_target_pairs={{0,256},{16,272},{32,288},{48,304},{64,320},{80,336},{96,352},{112... | collective-permute-start | bytes 196616 | tf_op jit(solution)/shard_map/ppermute | solution.py:37
  249.1 30.6 %copy-start.9 = (bf16[1,8,16,1024]{3,2,1,0:T(8,128)(2,1)S(1)}, bf16[1,8,16,1024]{3,2,1,0:T(8,128)(2,1)}, u32[]{:S(2)}) copy-start(bf16[1,8,16,1024]{3,2,1,0:T(8,128)(2,1)} %param.11) | copy-start | bytes 786436
  254.1 6.7 %collective-permute-start.20 = (f32[32,512]{1,0:T(8,128)S(1)}, f32[32,512]{1,0:T(8,128)S(1)}, u32[]{:S(2)}, u32[]{:S(2)}) collective-permute-start(f32[32,512]{1,0:T(8,128)S(1)} %add_bitcast_fusion), channel_id=1, source_target_pairs={{0,2},{1,3},{2,0},{3,1},{4,6},{5,7},{6,4},{7,5},{8,10},{9,11},{10,... | collective-permute-start | bytes 196616 | tf_op jit(solution)/shard_map/ppermute | solution.py:37
  260.8 5.0 %collective-permute-start.21 = (f32[32,512]{1,0:T(8,128)S(1)}, f32[32,512]{1,0:T(8,128)S(1)}, u32[]{:S(2)}, u32[]{:S(2)}) collective-permute-start(f32[32,512]{1,0:T(8,128)S(1)} %add.344), channel_id=1, source_target_pairs={{0,4},{1,5},{2,6},{3,7},{4,0},{5,1},{6,2},{7,3},{8,12},{9,13},{10,... | collective-permute-start | bytes 196616 | tf_op jit(solution)/shard_map/ppermute | solution.py:37
  265.8 6.9 %collective-permute-start.22 = (f32[32,512]{1,0:T(8,128)S(1)}, f32[32,512]{1,0:T(8,128)S(1)}, u32[]{:S(2)}, u32[]{:S(2)}) collective-permute-start(f32[32,512]{1,0:T(8,128)S(1)} %add.345), channel_id=1, source_target_pairs={{0,8},{1,9},{2,10},{3,11},{4,12},{5,13},{6,14},{7,15},{8,0},{9,1},... | collective-permute-start | bytes 196616 | tf_op jit(solution)/shard_map/ppermute | solution.py:37
  272.7 8.7 %collective-permute-start.23 = (f32[32,512]{1,0:T(8,128)S(1)}, f32[32,512]{1,0:T(8,128)S(1)}, u32[]{:S(2)}, u32[]{:S(2)}) collective-permute-start(f32[32,512]{1,0:T(8,128)S(1)} %add.346), channel_id=1, source_target_pairs={{0,1},{1,0},{2,3},{3,2},{4,5},{5,4},{6,7},{7,6},{8,9},{9,8},{10,11... | collective-permute-start | bytes 196616 | tf_op jit(solution)/shard_map/ppermute | solution.py:37
  (7 other events, 24.2 us)

commit v17 on v16

--- a/solution.py
+++ b/solution.py
@@ -75,7 +75,7 @@
     return held if tie is None else (held, tie)
 
 
-def scatter_by_bits(total, axis, groups, tie=None, tie_at=2):
+def scatter_by_bits(total, axis, groups, tie=None, tie_at=3):
     levels = lax.axis_size(axis).bit_length() - 1
     mine = [axis_bit(axis, bit) for bit in range(levels)]
     held = total.reshape((2,) * levels + (total.shape[0] // 2**levels,) + total.shape[1:])

time: 285 us -> 291 us (1.021)
  waiting for transfers between devices: 86.4 us -> 96.2 us
    ppermute x16, waiting for transfers between devices: 83.3 us -> 90.9 us  [partner_swap(): return lax.ppermute(value, axis, [(i, i ^ mask) for i in range(count)])]
  transfers between devices with their start and end apart: 24 -> 24, of which waited for: 16 -> 15; matrix products, arithmetic and copies ran while one was open for 18% -> 15% of each run, Pallas kernels for 0% -> 0%
where the time goes in v17:
time: 291 us; the launch traced here: 289 us
  starting transfers between devices  99.4 us (34%)
  waiting for transfers between devices  96.2 us (33%)
  local copies, waits for them, and re-layouts  48.9 us (17%)
  matrix products  30.1 us (10%)
  other arithmetic  12.9 us (4%)
    ppermute x16, waiting for transfers between devices, partner_swap(): return lax.ppermute(value, axis, [(i, i ^ mask) for i in range(count)])  90.9 us
    ppermute x16, starting transfers between devices, partner_swap(): return lax.ppermute(value, axis, [(i, i ^ mask) for i in range(count)])  74.5 us
    ppermute x4, starting transfers between devices, shifted(): lax.ppermute(value, axis, [(source, source + steps) for source in range(f...  12 us
    ppermute x2, starting transfers between devices, with_halo(): lax.ppermute(lax.slice_in_dim(block, block.shape[dim] - width, None, axis...  9.7 us
    concatenate x3, local copies, waits for them, and re-layouts, tile_backward(): jnp.concatenate([key_grad.reshape(batches, ext_count, inner_width), value...  7.45 us
    unnamed x33, local copies, waits for them, and re-layouts  5.87 us
    dot_general x1, matrix products, tile_backward(): jnp.einsum('bhqk,bqhd->bkhd', score_grad, query_heads, preferred_element_...  5.84 us
  transfers between devices with their start and end apart: 24, of which 15 were waited for; matrix products, arithmetic and copies ran while one was open for 15% of the time, Pallas kernels for 0%

profile of v17, /device:TPU:1, one launch (start us, length us, event | category | flops | bytes accessed | tf_op | source)
XLA Modules:
  0.0 289.3 jit_solution(18327489051362118226)
XLA Ops:
  2.0 16.3 %collective-permute-start = (bf16[1,1,1,1,1,32,1024]{6,5,4,3,2,1,0:T(8,128)(2,1)S(1)}, bf16[1,1,1,1,1,32,1024]{6,5,4,3,2,1,0:T(8,128)(2,1)S(1)}, u32[]{:S(2)}, u32[]{:S(2)}) collective-permute-start(bf16[1,1,1,1,1,32,1024]{6,5,4,3,2,1,0:T(8,128)(2,1)S(1)} %constant_dynamic-slice_fusion.9), channel_id=1, source_target_pairs={{0,256},{16,272},{32,288},{48,304},{64,320},{80,336},{96,352},{112... | collective-permute-start | bytes 196616 | tf_op jit(solution)/shard_map/ppermute | solution.py:37
  18.9 3.2 %collective-permute-start.3 = (bf16[1,6,16,1024]{3,2,1,0:T(8,128)(2,1)S(1)}, bf16[1,6,16,1024]{3,2,1,0:T(8,128)(2,1)S(1)}, u32[]{:S(2)}, u32[]{:S(2)}) collective-permute-start(bf16[1,6,16,1024]{3,2,1,0:T(8,128)(2,1)S(1)} %get-tuple-element.21), channel_id=1, source_target_pairs={{0,16},{16,32},{32,48},{48,64},{64,80},{80,96},{96,112},{112,128},... | collective-permute-start | bytes 589832 | tf_op jit(solution)/shard_map/ppermute | solution.py:27
  23.5 6.9 %collective-permute-start.1 = (bf16[2,1,1,1,1,32,1024]{6,5,4,3,2,1,0:T(8,128)(2,1)S(1)}, bf16[2,1,1,1,1,32,1024]{6,5,4,3,2,1,0:T(8,128)(2,1)S(1)}, u32[]{:S(2)}, u32[]{:S(2)}) collective-permute-start(bf16[2,1,1,1,1,32,1024]{6,5,4,3,2,1,0:T(8,128)(2,1)S(1)} %constant_dynamic-slice_fusion.8), channel_id=1, source_target_pairs={{0,128},{16,144},{32,160},{48,176},{64,192},{80,208},{96,224},{112... | collective-permute-start | bytes 393224 | tf_op jit(solution)/shard_map/ppermute | solution.py:37
  31.5 6.5 %collective-permute-start.5 = (bf16[1,20,6,1024]{3,2,1,0:T(8,128)(2,1)}, bf16[1,20,6,1024]{3,2,1,0:T(8,128)(2,1)S(1)}, u32[]{:S(2)}, u32[]{:S(2)}) collective-permute-start(bf16[1,20,6,1024]{3,2,1,0:T(8,128)(2,1)} %get-tuple-element.19), channel_id=1, source_target_pairs={{0,1},{1,2},{2,3},{3,4},{4,5},{5,6},{6,7},{7,8},{8,9},{9,10},{10,1... | collective-permute-start | bytes 737288 | tf_op jit(solution)/shard_map/ppermute | solution.py:27
  39.9 3.1 %collective-permute-done.1 = bf16[2,1,1,1,1,32,1024]{6,5,4,3,2,1,0:T(8,128)(2,1)S(1)} collective-permute-done((bf16[2,1,1,1,1,32,1024]{6,5,4,3,2,1,0:T(8,128)(2,1)S(1)}, bf16[2,1,1,1,1,32,1024]{6,5,4,3,2,1,0:T(8,128)(2,1)S(1)}, u32[]{:S(2)}, u32[]{:S(2)}) %collective-permute-start.1) | collective-permute-done | bytes 131104 | tf_op jit(solution)/shard_map/ppermute | solution.py:37
  53.1 6.7 %collective-permute-done.2 = bf16[2,2,1,1,1,32,1024]{6,5,4,3,2,1,0:T(8,128)(2,1)} collective-permute-done((bf16[2,2,1,1,1,32,1024]{6,5,4,3,2,1,0:T(8,128)(2,1)}, bf16[2,2,1,1,1,32,1024]{6,5,4,3,2,1,0:T(8,128)(2,1)}, u32[]{:S(2)}, u32[]{:S(2)}) %collective-permute-start.2) | collective-permute-done | bytes 262176 | tf_op jit(solution)/shard_map/ppermute | solution.py:37
  63.6 13.2 %collective-permute-done.7 = bf16[2,2,2,1,1,32,1024]{6,5,4,3,2,1,0:T(8,128)(2,1)S(1)} collective-permute-done((bf16[2,2,2,1,1,32,1024]{6,5,4,3,2,1,0:T(8,128)(2,1)}, bf16[2,2,2,1,1,32,1024]{6,5,4,3,2,1,0:T(8,128)(2,1)S(1)}, u32[]{:S(2)}, u32[]{:S(2)}) %collective-permute-start.7) | collective-permute-done | bytes 524320 | tf_op jit(solution)/shard_map/ppermute | solution.py:37
  79.8 23.6 %collective-permute-done.8 = bf16[2,2,2,2,1,32,1024]{6,5,4,3,2,1,0:T(8,128)(2,1)} collective-permute-done((bf16[2,2,2,2,1,32,1024]{6,5,4,3,2,1,0:T(8,128)(2,1)}, bf16[2,2,2,2,1,32,1024]{6,5,4,3,2,1,0:T(8,128)(2,1)}, u32[]{:S(2)}, u32[]{:S(2)}) %collective-permute-start.8) | collective-permute-done | bytes 1048608 | tf_op jit(solution)/shard_map/ppermute | solution.py:37
  104.8 4.3 %collective-permute-start.9 = (bf16[32,32,1024]{2,1,0:T(8,128)(2,1)S(1)}, bf16[32,32,1024]{2,1,0:T(8,128)(2,1)}, u32[]{:S(2)}, u32[]{:S(2)}) collective-permute-start(bf16[32,32,1024]{2,1,0:T(8,128)(2,1)S(1)} %bitcast.107), channel_id=1, source_target_pairs={{0,1},{1,0},{2,3},{3,2},{4,5},{5,4},{6,7},{7,6},{8,9},{9,8},{10,11... | collective-permute-start | bytes 6291464 | tf_op jit(solution)/shard_map/ppermute | solution.py:37
  119.4 3.3 %fusion.15 = bf16[1,560,1024]{2,1,0:T(8,128)(2,1)S(1)} fusion(bf16[560,1024]{1,0:T(8,128)(2,1)} %reshape.257, bf16[1024,1024]{1,0:T(8,128)(2,1)} %bitcast.113), kind=kOutput, calls=%fused_computation.16 | convolution fusion | flops 1174978560 | bytes 4390912 | tf_op jit(solution)/shard_map/dot_general | solution.py:246
  128.5 3.4 %fusion.78 = (f32[8,128]{1,0:T(8,128)S(1)}, f32[8,128,560]{1,2,0:T(8,128)}) fusion(pred[128,560]{0,1:T(8,128)(4,1)} %fusion.47, bf16[128,8,64]{0,2,1:T(8,128)(2,1)S(1)} %bitcast.133, bf16[560,8,64]{0,2,1:T(8,128)(2,1)} %bitcast.122), kind=kOutput, calls=%fused_computation.131 | convolution fusion | flops 75694640 | bytes 3074048 | tf_op jit(solution)/shard_map/sub | solution.py:160
  132.0 3.6 %fusion.79 = (bf16[1,560,8,64]{1,3,2,0:T(8,128)(2,1)}, f32[1,560,8,64]{1,3,2,0:T(8,128)}) fusion(bf16[128,8,64]{0,2,1:T(8,128)(2,1)S(1)} %bitcast.130, f32[8,128]{1,0:T(8,128)S(1)} %get-tuple-element.23, pred[128,560]{0,1:T(8,128)(4,1)} %fusion.47, bf16[128,8,64]{0,2,1:T(8,128)(2,1)S(1)} %bitcast.134, bf16[560,8,64]{0,2,1:T(8,128)(2,1)} %bitcast.123), kind=kOutput, calls=%fused_computation.132 | convolution fusion | flops 149956144 | bytes 2631680 | tf_op jit(solution)/shard_map/bhqk,bqhd->bkhd/dot_general | solution.py:187
  135.7 5.8 %fusion.80 = (bf16[1,560,8,64]{1,3,2,0:T(8,128)(2,1)}, f32[1,560,8,64]{1,3,2,0:T(8,128)}) fusion(bf16[128,8,64]{0,2,1:T(8,128)(2,1)S(1)} %bitcast.135, f32[8,128,560]{1,2,0:T(8,128)} %fusion.83, f32[8,128,560]{1,2,0:T(8,128)} %get-tuple-element.24, f32[8,128]{1,0:T(8,128)S(1)} %get-tuple-element.23), kind=kOutput, calls=%fused_computation.133 | convolution fusion | flops 77702704 | bytes 6443008 | tf_op jit(solution)/shard_map/bhqk,bqhd->bkhd/dot_general | solution.py:184
  149.7 3.8 %collective-permute-done.10 = f32[1024,512]{1,0:T(8,128)S(1)} collective-permute-done((f32[1024,512]{1,0:T(8,128)S(1)}, f32[1024,512]{1,0:T(8,128)S(1)}, u32[]{:S(2)}, u32[]{:S(2)}) %collective-permute-start.10) | collective-permute-done | bytes 2097184 | tf_op jit(solution)/shard_map/ppermute | solution.py:37
  158.5 3.0 %copy.25 = f32[1,560,8,64]{3,2,0,1:T(8,128)} copy(f32[1,560,8,64]{1,3,2,0:T(8,128)} %get-tuple-element.26) | data formatting | bytes 2293760 | tf_op jit(solution)/shard_map/bhqk,bqhd->bkhd/transpose | solution.py:187
  161.5 2.8 concatenate.25
  164.4 3.0 %copy.24 = f32[1,560,8,64]{3,2,0,1:T(8,128)} copy(f32[1,560,8,64]{1,3,2,0:T(8,128)} %get-tuple-element.28) | data formatting | bytes 2293760 | tf_op jit(solution)/shard_map/bhqk,bqhd->bkhd/transpose | solution.py:184
  167.4 3.6 %concatenate.24 = f32[1,20,28,512]{3,0,2,1:T(1,128)} reshape(f32[1,560,8,64]{3,2,0,1:T(8,128)} %copy.24) | data formatting | bytes 2293760 | tf_op jit(solution)/shard_map/concatenate | solution.py:191
  173.7 9.2 %collective-permute-done.11 = f32[2,2,2,2,1,1,32,512]{7,6,5,4,3,2,1,0:T(8,128)} collective-permute-done((f32[2,2,2,2,1,1,32,512]{7,6,5,4,3,2,1,0:T(8,128)}, f32[2,2,2,2,1,1,32,512]{7,6,5,4,3,2,1,0:T(8,128)}, u32[]{:S(2)}, u32[]{:S(2)}) %collective-permute-start.11) | collective-permute-done | bytes 1048608 | tf_op jit(solution)/shard_map/ppermute | solution.py:37
  188.3 6.1 %collective-permute-start.14 = (f32[1,20,6,1024]{3,0,2,1:T(1,128)S(1)}, f32[1,20,6,1024]{3,0,2,1:T(1,128)S(1)}, u32[]{:S(2)}, u32[]{:S(2)}) collective-permute-start(f32[1,20,6,1024]{3,0,2,1:T(1,128)S(1)} %get-tuple-element.13), channel_id=1, source_target_pairs={{0,1},{1,2},{2,3},{3,4},{4,5},{5,6},{6,7},{7,8},{8,9},{9,10},{10,1... | collective-permute-start | bytes 1474568 | tf_op jit(solution)/shard_map/ppermute | solution.py:19
  198.7 4.2 %collective-permute-start.13 = (f32[2,2,1,1,1,1,32,512]{7,6,5,4,3,2,1,0:T(8,128)S(1)}, f32[2,2,1,1,1,1,32,512]{7,6,5,4,3,2,1,0:T(8,128)S(1)}, u32[]{:S(2)}, u32[]{:S(2)}) collective-permute-start(f32[2,2,1,1,1,1,32,512]{7,6,5,4,3,2,1,0:T(8,128)S(1)} %constant_dynamic-slice_fusion.2), channel_id=1, source_target_pairs={{0,64},{16,80},{32,96},{48,112},{64,0},{80,16},{96,32},{112,48},{1... | collective-permute-start | bytes 786440 | tf_op jit(solution)/shard_map/ppermute | solution.py:37
  208.4 7.0 %collective-permute-done.13 = f32[2,2,1,1,1,1,32,512]{7,6,5,4,3,2,1,0:T(8,128)S(1)} collective-permute-done((f32[2,2,1,1,1,1,32,512]{7,6,5,4,3,2,1,0:T(8,128)S(1)}, f32[2,2,1,1,1,1,32,512]{7,6,5,4,3,2,1,0:T(8,128)S(1)}, u32[]{:S(2)}, u32[]{:S(2)}) %collective-permute-start.13) | collective-permute-done | bytes 262176 | tf_op jit(solution)/shard_map/ppermute | solution.py:37
  215.4 6.5 %collective-permute-start.18 = (f32[2,1,1,1,1,1,32,512]{7,6,5,4,3,2,1,0:T(8,128)S(1)}, f32[2,1,1,1,1,1,32,512]{7,6,5,4,3,2,1,0:T(8,128)S(1)}, u32[]{:S(2)}, u32[]{:S(2)}) collective-permute-start(f32[2,1,1,1,1,1,32,512]{7,6,5,4,3,2,1,0:T(8,128)S(1)} %constant_dynamic-slice_fusion.1), channel_id=1, source_target_pairs={{0,128},{16,144},{32,160},{48,176},{64,192},{80,208},{96,224},{112... | collective-permute-start | bytes 393224 | tf_op jit(solution)/shard_map/ppermute | solution.py:37
  222.0 11.3 %collective-permute-done.18 = f32[2,1,1,1,1,1,32,512]{7,6,5,4,3,2,1,0:T(8,128)S(1)} collective-permute-done((f32[2,1,1,1,1,1,32,512]{7,6,5,4,3,2,1,0:T(8,128)S(1)}, f32[2,1,1,1,1,1,32,512]{7,6,5,4,3,2,1,0:T(8,128)S(1)}, u32[]{:S(2)}, u32[]{:S(2)}) %collective-permute-start.18) | collective-permute-done | bytes 131104 | tf_op jit(solution)/shard_map/ppermute | solution.py:37
  234.0 3.9 %collective-permute-start.19 = (f32[1,1,1,1,1,1,32,512]{7,6,5,4,3,2,1,0:T(8,128)}, f32[1,1,1,1,1,1,32,512]{7,6,5,4,3,2,1,0:T(8,128)}, u32[]{:S(2)}, u32[]{:S(2)}) collective-permute-start(f32[1,1,1,1,1,1,32,512]{7,6,5,4,3,2,1,0:T(8,128)} %constant_dynamic-slice_fusion), channel_id=1, source_target_pairs={{0,256},{16,272},{32,288},{48,304},{64,320},{80,336},{96,352},{112... | collective-permute-start | bytes 196616 | tf_op jit(solution)/shard_map/ppermute | solution.py:37
  240.6 8.1 %collective-permute-done.19 = f32[1,1,1,1,1,1,32,512]{7,6,5,4,3,2,1,0:T(8,128)} collective-permute-done((f32[1,1,1,1,1,1,32,512]{7,6,5,4,3,2,1,0:T(8,128)}, f32[1,1,1,1,1,1,32,512]{7,6,5,4,3,2,1,0:T(8,128)}, u32[]{:S(2)}, u32[]{:S(2)}) %collective-permute-start.19) | collective-permute-done | bytes 65568 | tf_op jit(solution)/shard_map/ppermute | solution.py:37
  249.6 5.3 %collective-permute-start.20 = (f32[32,512]{1,0:T(8,128)S(1)}, f32[32,512]{1,0:T(8,128)S(1)}, u32[]{:S(2)}, u32[]{:S(2)}) collective-permute-start(f32[32,512]{1,0:T(8,128)S(1)} %add_bitcast_fusion), channel_id=1, source_target_pairs={{0,2},{1,3},{2,0},{3,1},{4,6},{5,7},{6,4},{7,5},{8,10},{9,11},{10,... | collective-permute-start | bytes 196616 | tf_op jit(solution)/shard_map/ppermute | solution.py:37
  257.4 2.8 collective-permute-start.16
  261.5 3.2 %collective-permute-start.21 = (f32[32,512]{1,0:T(8,128)S(1)}, f32[32,512]{1,0:T(8,128)S(1)}, u32[]{:S(2)}, u32[]{:S(2)}) collective-permute-start(f32[32,512]{1,0:T(8,128)S(1)} %add.344), channel_id=1, source_target_pairs={{0,4},{1,5},{2,6},{3,7},{4,0},{5,1},{6,2},{7,3},{8,12},{9,13},{10,... | collective-permute-start | bytes 196616 | tf_op jit(solution)/shard_map/ppermute | solution.py:37
  266.5 4.8 %collective-permute-start.22 = (f32[32,512]{1,0:T(8,128)S(1)}, f32[32,512]{1,0:T(8,128)S(1)}, u32[]{:S(2)}, u32[]{:S(2)}) collective-permute-start(f32[32,512]{1,0:T(8,128)S(1)} %add.345), channel_id=1, source_target_pairs={{0,8},{1,9},{2,10},{3,11},{4,12},{5,13},{6,14},{7,15},{8,0},{9,1},... | collective-permute-start | bytes 196616 | tf_op jit(solution)/shard_map/ppermute | solution.py:37
  271.3 4.5 %fusion.19 = bf16[8,64,128]{2,1,0:T(8,128)(2,1)S(1)} fusion(bf16[560,8,64]{0,2,1:T(8,128)(2,1)S(1)} %bitcast.125, f32[8,128,560]{1,2,0:T(8,128)} %fusion.83, f32[8,128,560]{1,2,0:T(8,128)} %get-tuple-element.24, f32[8,128]{1,0:T(8,128)S(1)} %get-tuple-element.23), kind=kOutput, calls=%fused_computation.24 | convolution fusion | flops 77481520 | bytes 5296128 | tf_op jit(solution)/shard_map/bhqk,bkhd->bqhd/dot_general | solution.py:181
  275.9 6.4 %collective-permute-start.23 = (f32[32,512]{1,0:T(8,128)S(1)}, f32[32,512]{1,0:T(8,128)S(1)}, u32[]{:S(2)}, u32[]{:S(2)}) collective-permute-start(f32[32,512]{1,0:T(8,128)S(1)} %add.346), channel_id=1, source_target_pairs={{0,1},{1,0},{2,3},{3,2},{4,5},{5,4},{6,7},{7,6},{8,9},{9,8},{10,11... | collective-permute-start | bytes 196616 | tf_op jit(solution)/shard_map/ppermute | solution.py:37
  (138 shorter events, 87.8 us)
Async XLA Ops:
  0.7 17.6 %copy-start = (bf16[1,8,16,1024]{3,2,1,0:T(8,128)(2,1)S(1)}, bf16[1,8,16,1024]{3,2,1,0:T(8,128)(2,1)}, u32[]{:S(2)}) copy-start(bf16[1,8,16,1024]{3,2,1,0:T(8,128)(2,1)} %param.6) | copy-start | bytes 786436
  0.7 17.9 %copy-start.12 = (f32[1024]{0:T(1024)S(1)}, f32[1024]{0:T(1024)}, u32[]{:S(2)}) copy-start(f32[1024]{0:T(1024)} %param.7) | copy-start | bytes 12292
  2.0 21.5 %collective-permute-start = (bf16[1,1,1,1,1,32,1024]{6,5,4,3,2,1,0:T(8,128)(2,1)S(1)}, bf16[1,1,1,1,1,32,1024]{6,5,4,3,2,1,0:T(8,128)(2,1)S(1)}, u32[]{:S(2)}, u32[]{:S(2)}) collective-permute-start(bf16[1,1,1,1,1,32,1024]{6,5,4,3,2,1,0:T(8,128)(2,1)S(1)} %constant_dynamic-slice_fusion.9), channel_id=1, source_target_pairs={{0,256},{16,272},{32,288},{48,304},{64,320},{80,336},{96,352},{112... | collective-permute-start | bytes 196616 | tf_op jit(solution)/shard_map/ppermute | solution.py:37
  18.9 11.5 %collective-permute-start.3 = (bf16[1,6,16,1024]{3,2,1,0:T(8,128)(2,1)S(1)}, bf16[1,6,16,1024]{3,2,1,0:T(8,128)(2,1)S(1)}, u32[]{:S(2)}, u32[]{:S(2)}) collective-permute-start(bf16[1,6,16,1024]{3,2,1,0:T(8,128)(2,1)S(1)} %get-tuple-element.21), channel_id=1, source_target_pairs={{0,16},{16,32},{32,48},{48,64},{64,80},{80,96},{96,112},{112,128},... | collective-permute-start | bytes 589832 | tf_op jit(solution)/shard_map/ppermute | solution.py:27
  22.1 8.3 %collective-permute-start.4 = (bf16[1,6,16,1024]{3,2,1,0:T(8,128)(2,1)S(1)}, bf16[1,6,16,1024]{3,2,1,0:T(8,128)(2,1)S(1)}, u32[]{:S(2)}, u32[]{:S(2)}) collective-permute-start(bf16[1,6,16,1024]{3,2,1,0:T(8,128)(2,1)S(1)} %get-tuple-element.22), channel_id=1, source_target_pairs={{16,0},{32,16},{48,32},{64,48},{80,64},{96,80},{112,96},{128,112},... | collective-permute-start | bytes 589832 | tf_op jit(solution)/shard_map/ppermute | solution.py:30
  23.5 19.5 %collective-permute-start.1 = (bf16[2,1,1,1,1,32,1024]{6,5,4,3,2,1,0:T(8,128)(2,1)S(1)}, bf16[2,1,1,1,1,32,1024]{6,5,4,3,2,1,0:T(8,128)(2,1)S(1)}, u32[]{:S(2)}, u32[]{:S(2)}) collective-permute-start(bf16[2,1,1,1,1,32,1024]{6,5,4,3,2,1,0:T(8,128)(2,1)S(1)} %constant_dynamic-slice_fusion.8), channel_id=1, source_target_pairs={{0,128},{16,144},{32,160},{48,176},{64,192},{80,208},{96,224},{112... | collective-permute-start | bytes 393224 | tf_op jit(solution)/shard_map/ppermute | solution.py:37
  31.5 14.5 %collective-permute-start.5 = (bf16[1,20,6,1024]{3,2,1,0:T(8,128)(2,1)}, bf16[1,20,6,1024]{3,2,1,0:T(8,128)(2,1)S(1)}, u32[]{:S(2)}, u32[]{:S(2)}) collective-permute-start(bf16[1,20,6,1024]{3,2,1,0:T(8,128)(2,1)} %get-tuple-element.19), channel_id=1, source_target_pairs={{0,1},{1,2},{2,3},{3,4},{4,5},{5,6},{6,7},{7,8},{8,9},{9,10},{10,1... | collective-permute-start | bytes 737288 | tf_op jit(solution)/shard_map/ppermute | solution.py:27
  38.0 10.2 %collective-permute-start.6 = (bf16[1,20,6,1024]{3,2,1,0:T(8,128)(2,1)}, bf16[1,20,6,1024]{3,2,1,0:T(8,128)(2,1)}, u32[]{:S(2)}, u32[]{:S(2)}) collective-permute-start(bf16[1,20,6,1024]{3,2,1,0:T(8,128)(2,1)} %get-tuple-element.20), channel_id=1, source_target_pairs={{1,0},{2,1},{3,2},{4,3},{5,4},{6,5},{7,6},{8,7},{9,8},{10,9},{11,1... | collective-permute-start | bytes 737288 | tf_op jit(solution)/shard_map/ppermute | solution.py:30
  43.7 16.1 %collective-permute-start.2 = (bf16[2,2,1,1,1,32,1024]{6,5,4,3,2,1,0:T(8,128)(2,1)}, bf16[2,2,1,1,1,32,1024]{6,5,4,3,2,1,0:T(8,128)(2,1)}, u32[]{:S(2)}, u32[]{:S(2)}) collective-permute-start(bf16[2,2,1,1,1,32,1024]{6,5,4,3,2,1,0:T(8,128)(2,1)} %constant_dynamic-slice_fusion.7), channel_id=1, source_target_pairs={{0,64},{16,80},{32,96},{48,112},{64,0},{80,16},{96,32},{112,48},{1... | collective-permute-start | bytes 786440 | tf_op jit(solution)/shard_map/ppermute | solution.py:37
  61.7 15.1 %collective-permute-start.7 = (bf16[2,2,2,1,1,32,1024]{6,5,4,3,2,1,0:T(8,128)(2,1)}, bf16[2,2,2,1,1,32,1024]{6,5,4,3,2,1,0:T(8,128)(2,1)S(1)}, u32[]{:S(2)}, u32[]{:S(2)}) collective-permute-start(bf16[2,2,2,1,1,32,1024]{6,5,4,3,2,1,0:T(8,128)(2,1)} %constant_dynamic-slice_fusion.6), channel_id=1, source_target_pairs={{0,32},{16,48},{32,0},{48,16},{64,96},{80,112},{96,64},{112,80},{1... | collective-permute-start | bytes 1572872 | tf_op jit(solution)/shard_map/ppermute | solution.py:37
  77.9 25.5 %collective-permute-start.8 = (bf16[2,2,2,2,1,32,1024]{6,5,4,3,2,1,0:T(8,128)(2,1)}, bf16[2,2,2,2,1,32,1024]{6,5,4,3,2,1,0:T(8,128)(2,1)}, u32[]{:S(2)}, u32[]{:S(2)}) collective-permute-start(bf16[2,2,2,2,1,32,1024]{6,5,4,3,2,1,0:T(8,128)(2,1)} %constant_dynamic-slice_fusion.5), channel_id=1, source_target_pairs={{0,16},{16,0},{32,48},{48,32},{64,80},{80,64},{96,112},{112,96},{1... | collective-permute-start | bytes 3145736 | tf_op jit(solution)/shard_map/ppermute | solution.py:37
  104.8 8.1 %collective-permute-start.9 = (bf16[32,32,1024]{2,1,0:T(8,128)(2,1)S(1)}, bf16[32,32,1024]{2,1,0:T(8,128)(2,1)}, u32[]{:S(2)}, u32[]{:S(2)}) collective-permute-start(bf16[32,32,1024]{2,1,0:T(8,128)(2,1)S(1)} %bitcast.107), channel_id=1, source_target_pairs={{0,1},{1,0},{2,3},{3,2},{4,5},{5,4},{6,7},{7,6},{8,9},{9,8},{10,11... | collective-permute-start | bytes 6291464 | tf_op jit(solution)/shard_map/ppermute | solution.py:37
  119.4 16.2 %copy-start.10 = (bf16[128,512]{0,1:T(8,128)(2,1)}, bf16[128,512]{0,1:T(8,128)(2,1)S(1)}, u32[]{:S(2)}) copy-start(bf16[128,512]{0,1:T(8,128)(2,1)S(1)} %copy.18) | copy-start | bytes 393220
  147.4 6.1 %collective-permute-start.10 = (f32[1024,512]{1,0:T(8,128)S(1)}, f32[1024,512]{1,0:T(8,128)S(1)}, u32[]{:S(2)}, u32[]{:S(2)}) collective-permute-start(f32[1024,512]{1,0:T(8,128)S(1)} %dynamic-slice_bitcast_fusion), channel_id=1, source_target_pairs={{0,1},{1,0},{2,3},{3,2},{4,5},{5,4},{6,7},{7,6},{8,9},{9,8},{10,11... | collective-permute-start | bytes 6291464 | tf_op jit(solution)/shard_map/ppermute | solution.py:37
  156.3 26.6 %collective-permute-start.11 = (f32[2,2,2,2,1,1,32,512]{7,6,5,4,3,2,1,0:T(8,128)}, f32[2,2,2,2,1,1,32,512]{7,6,5,4,3,2,1,0:T(8,128)}, u32[]{:S(2)}, u32[]{:S(2)}) collective-permute-start(f32[2,2,2,2,1,1,32,512]{7,6,5,4,3,2,1,0:T(8,128)} %constant_dynamic-slice_fusion.4), channel_id=1, source_target_pairs={{0,16},{16,0},{32,48},{48,32},{64,80},{80,64},{96,112},{112,96},{1... | collective-permute-start | bytes 3145736 | tf_op jit(solution)/shard_map/ppermute | solution.py:37
  171.0 11.9 %copy-start.2 = (f32[1024,512]{1,0:T(8,128)S(1)}, f32[1024,512]{1,0:T(8,128)}, u32[]{:S(2)}) copy-start(f32[1024,512]{1,0:T(8,128)} %copy-done.1) | copy-start | bytes 6291460
  184.4 14.1 %collective-permute-start.12 = (f32[2,2,2,1,1,1,32,512]{7,6,5,4,3,2,1,0:T(8,128)S(1)}, f32[2,2,2,1,1,1,32,512]{7,6,5,4,3,2,1,0:T(8,128)S(1)}, u32[]{:S(2)}, u32[]{:S(2)}) collective-permute-start(f32[2,2,2,1,1,1,32,512]{7,6,5,4,3,2,1,0:T(8,128)S(1)} %constant_dynamic-slice_fusion.3), channel_id=1, source_target_pairs={{0,32},{16,48},{32,0},{48,16},{64,96},{80,112},{96,64},{112,80},{1... | collective-permute-start | bytes 1572872 | tf_op jit(solution)/shard_map/ppermute | solution.py:37
  188.3 17.1 %collective-permute-start.14 = (f32[1,20,6,1024]{3,0,2,1:T(1,128)S(1)}, f32[1,20,6,1024]{3,0,2,1:T(1,128)S(1)}, u32[]{:S(2)}, u32[]{:S(2)}) collective-permute-start(f32[1,20,6,1024]{3,0,2,1:T(1,128)S(1)} %get-tuple-element.13), channel_id=1, source_target_pairs={{0,1},{1,2},{2,3},{3,4},{4,5},{5,6},{6,7},{7,8},{8,9},{9,10},{10,1... | collective-permute-start | bytes 1474568 | tf_op jit(solution)/shard_map/ppermute | solution.py:19
  194.4 11.7 %collective-permute-start.15 = (f32[1,20,6,1024]{3,0,2,1:T(1,128)S(1)}, f32[1,20,6,1024]{3,0,2,1:T(1,128)S(1)}, u32[]{:S(2)}, u32[]{:S(2)}) collective-permute-start(f32[1,20,6,1024]{3,0,2,1:T(1,128)S(1)} %get-tuple-element.14), channel_id=1, source_target_pairs={{1,0},{2,1},{3,2},{4,3},{5,4},{6,5},{7,6},{8,7},{9,8},{10,9},{11,1... | collective-permute-start | bytes 1474568 | tf_op jit(solution)/shard_map/ppermute | solution.py:19
  198.6 39.2 %copy-start.5 = (bf16[1,560,512]{1,2,0:T(8,128)(2,1)S(1)}, bf16[1,560,512]{1,2,0:T(8,128)(2,1)}, u32[]{:S(2)}) copy-start(bf16[1,560,512]{1,2,0:T(8,128)(2,1)} %copy-done.4) | copy-start | bytes 1720324
  198.6 39.2 %copy-start.11 = (bf16[128,512]{0,1:T(8,128)(2,1)S(1)}, bf16[128,512]{0,1:T(8,128)(2,1)}, u32[]{:S(2)}) copy-start(bf16[128,512]{0,1:T(8,128)(2,1)} %copy-done.10) | copy-start | bytes 393220
  198.7 16.7 %collective-permute-start.13 = (f32[2,2,1,1,1,1,32,512]{7,6,5,4,3,2,1,0:T(8,128)S(1)}, f32[2,2,1,1,1,1,32,512]{7,6,5,4,3,2,1,0:T(8,128)S(1)}, u32[]{:S(2)}, u32[]{:S(2)}) collective-permute-start(f32[2,2,1,1,1,1,32,512]{7,6,5,4,3,2,1,0:T(8,128)S(1)} %constant_dynamic-slice_fusion.2), channel_id=1, source_target_pairs={{0,64},{16,80},{32,96},{48,112},{64,0},{80,16},{96,32},{112,48},{1... | collective-permute-start | bytes 786440 | tf_op jit(solution)/shard_map/ppermute | solution.py:37
  215.4 17.8 %collective-permute-start.18 = (f32[2,1,1,1,1,1,32,512]{7,6,5,4,3,2,1,0:T(8,128)S(1)}, f32[2,1,1,1,1,1,32,512]{7,6,5,4,3,2,1,0:T(8,128)S(1)}, u32[]{:S(2)}, u32[]{:S(2)}) collective-permute-start(f32[2,1,1,1,1,1,32,512]{7,6,5,4,3,2,1,0:T(8,128)S(1)} %constant_dynamic-slice_fusion.1), channel_id=1, source_target_pairs={{0,128},{16,144},{32,160},{48,176},{64,192},{80,208},{96,224},{112... | collective-permute-start | bytes 393224 | tf_op jit(solution)/shard_map/ppermute | solution.py:37
  234.0 14.8 %collective-permute-start.19 = (f32[1,1,1,1,1,1,32,512]{7,6,5,4,3,2,1,0:T(8,128)}, f32[1,1,1,1,1,1,32,512]{7,6,5,4,3,2,1,0:T(8,128)}, u32[]{:S(2)}, u32[]{:S(2)}) collective-permute-start(f32[1,1,1,1,1,1,32,512]{7,6,5,4,3,2,1,0:T(8,128)} %constant_dynamic-slice_fusion), channel_id=1, source_target_pairs={{0,256},{16,272},{32,288},{48,304},{64,320},{80,336},{96,352},{112... | collective-permute-start | bytes 196616 | tf_op jit(solution)/shard_map/ppermute | solution.py:37
  240.2 31.1 %copy-start.9 = (bf16[1,560,512]{1,2,0:T(8,128)(2,1)S(1)}, bf16[1,560,512]{1,2,0:T(8,128)(2,1)}, u32[]{:S(2)}) copy-start(bf16[1,560,512]{1,2,0:T(8,128)(2,1)} %copy.19) | copy-start | bytes 1720324
  249.6 11.9 %collective-permute-start.20 = (f32[32,512]{1,0:T(8,128)S(1)}, f32[32,512]{1,0:T(8,128)S(1)}, u32[]{:S(2)}, u32[]{:S(2)}) collective-permute-start(f32[32,512]{1,0:T(8,128)S(1)} %add_bitcast_fusion), channel_id=1, source_target_pairs={{0,2},{1,3},{2,0},{3,1},{4,6},{5,7},{6,4},{7,5},{8,10},{9,11},{10,... | collective-permute-start | bytes 196616 | tf_op jit(solution)/shard_map/ppermute | solution.py:37
  257.4 24.9 %collective-permute-start.16 = (f32[1,6,16,1024]{3,0,2,1:T(1,128)}, f32[1,6,16,1024]{3,0,2,1:T(1,128)}, u32[]{:S(2)}, u32[]{:S(2)}) collective-permute-start(f32[1,6,16,1024]{3,0,2,1:T(1,128)} %get-tuple-element.15), channel_id=1, source_target_pairs={{0,16},{16,32},{32,48},{48,64},{64,80},{80,96},{96,112},{112,128},... | collective-permute-start | bytes 1179656 | tf_op jit(solution)/shard_map/ppermute | solution.py:19
  260.2 22.1 %collective-permute-start.17 = (f32[1,6,16,1024]{3,0,2,1:T(1,128)}, f32[1,6,16,1024]{3,0,2,1:T(1,128)}, u32[]{:S(2)}, u32[]{:S(2)}) collective-permute-start(f32[1,6,16,1024]{3,0,2,1:T(1,128)} %get-tuple-element.16), channel_id=1, source_target_pairs={{16,0},{32,16},{48,32},{64,48},{80,64},{96,80},{112,96},{128,112},... | collective-permute-start | bytes 1179656 | tf_op jit(solution)/shard_map/ppermute | solution.py:19
  261.5 5.0 %collective-permute-start.21 = (f32[32,512]{1,0:T(8,128)S(1)}, f32[32,512]{1,0:T(8,128)S(1)}, u32[]{:S(2)}, u32[]{:S(2)}) collective-permute-start(f32[32,512]{1,0:T(8,128)S(1)} %add.344), channel_id=1, source_target_pairs={{0,4},{1,5},{2,6},{3,7},{4,0},{5,1},{6,2},{7,3},{8,12},{9,13},{10,... | collective-permute-start | bytes 196616 | tf_op jit(solution)/shard_map/ppermute | solution.py:37
  266.5 9.3 %collective-permute-start.22 = (f32[32,512]{1,0:T(8,128)S(1)}, f32[32,512]{1,0:T(8,128)S(1)}, u32[]{:S(2)}, u32[]{:S(2)}) collective-permute-start(f32[32,512]{1,0:T(8,128)S(1)} %add.345), channel_id=1, source_target_pairs={{0,8},{1,9},{2,10},{3,11},{4,12},{5,13},{6,14},{7,15},{8,0},{9,1},... | collective-permute-start | bytes 196616 | tf_op jit(solution)/shard_map/ppermute | solution.py:37
  275.9 8.5 %copy-start.3 = (bf16[1,32,32,1024]{3,2,1,0:T(8,128)(2,1)S(1)}, bf16[1,32,32,1024]{3,2,1,0:T(8,128)(2,1)}, u32[]{:S(2)}) copy-start(bf16[1,32,32,1024]{3,2,1,0:T(8,128)(2,1)} %slice.66) | copy-start | bytes 6291460
  275.9 12.0 %collective-permute-start.23 = (f32[32,512]{1,0:T(8,128)S(1)}, f32[32,512]{1,0:T(8,128)S(1)}, u32[]{:S(2)}, u32[]{:S(2)}) collective-permute-start(f32[32,512]{1,0:T(8,128)S(1)} %add.346), channel_id=1, source_target_pairs={{0,1},{1,0},{2,3},{3,2},{4,5},{5,4},{6,7},{7,6},{8,9},{9,8},{10,11... | collective-permute-start | bytes 196616 | tf_op jit(solution)/shard_map/ppermute | solution.py:37
  (7 other events, 16.1 us)

commit v18 on v17

--- a/solution.py
+++ b/solution.py
@@ -75,7 +75,7 @@
     return held if tie is None else (held, tie)
 
 
-def scatter_by_bits(total, axis, groups, tie=None, tie_at=3):
+def scatter_by_bits(total, axis, groups, tie=None, tie_at=1):
     levels = lax.axis_size(axis).bit_length() - 1
     mine = [axis_bit(axis, bit) for bit in range(levels)]
     held = total.reshape((2,) * levels + (total.shape[0] // 2**levels,) + total.shape[1:])

time: 291 us -> 312 us (1.072)
  waiting for transfers between devices: 96.2 us -> 106 us
  starting transfers between devices: 99.4 us -> 103 us
  other arithmetic: 12.9 us -> 16.3 us
  local copies, waits for them, and re-layouts: 48.9 us -> 52.3 us
    ppermute x4, waiting for transfers between devices: 3.15 us -> 22.5 us  [shifted(): lax.ppermute(value, axis, [(source, source + steps) for source in range(f...]
    ppermute x16, waiting for transfers between devices: 90.9 us -> 81.7 us  [partner_swap(): return lax.ppermute(value, axis, [(i, i ^ mask) for i in range(count)])]
    ppermute x16, starting transfers between devices: 74.5 us -> 78.4 us  [partner_swap(): return lax.ppermute(value, axis, [(i, i ^ mask) for i in range(count)])]
    unnamed x33 -> x39, local copies, waits for them, and re-layouts: 5.87 us -> 7.82 us
  transfers between devices with their start and end apart: 24 -> 24, of which waited for: 15 -> 13; matrix products, arithmetic and copies ran while one was open for 15% -> 15% of each run, Pallas kernels for 0% -> 0%
where the time goes in v18:
time: 312 us; the launch traced here: 310 us
  waiting for transfers between devices  106 us (34%)
  starting transfers between devices  103 us (33%)
  local copies, waits for them, and re-layouts  52.3 us (17%)
  matrix products  30.4 us (10%)
  other arithmetic  16.3 us (5%)
    ppermute x16, waiting for transfers between devices, partner_swap(): return lax.ppermute(value, axis, [(i, i ^ mask) for i in range(count)])  81.7 us
    ppermute x16, starting transfers between devices, partner_swap(): return lax.ppermute(value, axis, [(i, i ^ mask) for i in range(count)])  78.4 us
    ppermute x4, waiting for transfers between devices, shifted(): lax.ppermute(value, axis, [(source, source + steps) for source in range(f...  22.5 us
    ppermute x4, starting transfers between devices, shifted(): lax.ppermute(value, axis, [(source, source + steps) for source in range(f...  11.6 us
    ppermute x2, starting transfers between devices, with_halo(): lax.ppermute(lax.slice_in_dim(block, block.shape[dim] - width, None, axis...  9.7 us
    unnamed x39, local copies, waits for them, and re-layouts  7.82 us
    concatenate x3, local copies, waits for them, and re-layouts, tile_backward(): jnp.concatenate([key_grad.reshape(batches, ext_count, inner_width), value...  7.43 us
  transfers between devices with their start and end apart: 24, of which 13 were waited for; matrix products, arithmetic and copies ran while one was open for 15% of the time, Pallas kernels for 0%

profile of v18, /device:TPU:1, one launch (start us, length us, event | category | flops | bytes accessed | tf_op | source)
XLA Modules:
  0.0 310.1 jit_solution(16610317009141418044)
XLA Ops:
  2.0 16.3 %collective-permute-start = (bf16[1,1,1,1,1,32,1024]{6,5,4,3,2,1,0:T(8,128)(2,1)S(1)}, bf16[1,1,1,1,1,32,1024]{6,5,4,3,2,1,0:T(8,128)(2,1)S(1)}, u32[]{:S(2)}, u32[]{:S(2)}) collective-permute-start(bf16[1,1,1,1,1,32,1024]{6,5,4,3,2,1,0:T(8,128)(2,1)S(1)} %constant_dynamic-slice_fusion.9), channel_id=1, source_target_pairs={{0,256},{16,272},{32,288},{48,304},{64,320},{80,336},{96,352},{112... | collective-permute-start | bytes 196616 | tf_op jit(solution)/shard_map/ppermute | solution.py:37
  18.9 3.2 %collective-permute-start.3 = (bf16[1,6,16,1024]{3,2,1,0:T(8,128)(2,1)S(1)}, bf16[1,6,16,1024]{3,2,1,0:T(8,128)(2,1)S(1)}, u32[]{:S(2)}, u32[]{:S(2)}) collective-permute-start(bf16[1,6,16,1024]{3,2,1,0:T(8,128)(2,1)S(1)} %get-tuple-element.21), channel_id=1, source_target_pairs={{0,16},{16,32},{32,48},{48,64},{64,80},{80,96},{96,112},{112,128},... | collective-permute-start | bytes 589832 | tf_op jit(solution)/shard_map/ppermute | solution.py:27
  23.5 6.9 %collective-permute-start.1 = (bf16[2,1,1,1,1,32,1024]{6,5,4,3,2,1,0:T(8,128)(2,1)S(1)}, bf16[2,1,1,1,1,32,1024]{6,5,4,3,2,1,0:T(8,128)(2,1)S(1)}, u32[]{:S(2)}, u32[]{:S(2)}) collective-permute-start(bf16[2,1,1,1,1,32,1024]{6,5,4,3,2,1,0:T(8,128)(2,1)S(1)} %constant_dynamic-slice_fusion.8), channel_id=1, source_target_pairs={{0,128},{16,144},{32,160},{48,176},{64,192},{80,208},{96,224},{112... | collective-permute-start | bytes 393224 | tf_op jit(solution)/shard_map/ppermute | solution.py:37
  31.5 6.5 %collective-permute-start.5 = (bf16[1,20,6,1024]{3,2,1,0:T(8,128)(2,1)}, bf16[1,20,6,1024]{3,2,1,0:T(8,128)(2,1)S(1)}, u32[]{:S(2)}, u32[]{:S(2)}) collective-permute-start(bf16[1,20,6,1024]{3,2,1,0:T(8,128)(2,1)} %get-tuple-element.19), channel_id=1, source_target_pairs={{0,1},{1,2},{2,3},{3,4},{4,5},{5,6},{6,7},{7,8},{8,9},{9,10},{10,1... | collective-permute-start | bytes 737288 | tf_op jit(solution)/shard_map/ppermute | solution.py:27
  39.9 3.1 collective-permute-done.1
  53.1 6.8 %collective-permute-done.2 = bf16[2,2,1,1,1,32,1024]{6,5,4,3,2,1,0:T(8,128)(2,1)} collective-permute-done((bf16[2,2,1,1,1,32,1024]{6,5,4,3,2,1,0:T(8,128)(2,1)}, bf16[2,2,1,1,1,32,1024]{6,5,4,3,2,1,0:T(8,128)(2,1)}, u32[]{:S(2)}, u32[]{:S(2)}) %collective-permute-start.2) | collective-permute-done | bytes 262176 | tf_op jit(solution)/shard_map/ppermute | solution.py:37
  63.6 13.2 %collective-permute-done.7 = bf16[2,2,2,1,1,32,1024]{6,5,4,3,2,1,0:T(8,128)(2,1)S(1)} collective-permute-done((bf16[2,2,2,1,1,32,1024]{6,5,4,3,2,1,0:T(8,128)(2,1)}, bf16[2,2,2,1,1,32,1024]{6,5,4,3,2,1,0:T(8,128)(2,1)S(1)}, u32[]{:S(2)}, u32[]{:S(2)}) %collective-permute-start.7) | collective-permute-done | bytes 524320 | tf_op jit(solution)/shard_map/ppermute | solution.py:37
  79.9 23.6 %collective-permute-done.8 = bf16[2,2,2,2,1,32,1024]{6,5,4,3,2,1,0:T(8,128)(2,1)} collective-permute-done((bf16[2,2,2,2,1,32,1024]{6,5,4,3,2,1,0:T(8,128)(2,1)}, bf16[2,2,2,2,1,32,1024]{6,5,4,3,2,1,0:T(8,128)(2,1)}, u32[]{:S(2)}, u32[]{:S(2)}) %collective-permute-start.8) | collective-permute-done | bytes 1048608 | tf_op jit(solution)/shard_map/ppermute | solution.py:37
  104.8 4.3 %collective-permute-start.9 = (bf16[32,32,1024]{2,1,0:T(8,128)(2,1)S(1)}, bf16[32,32,1024]{2,1,0:T(8,128)(2,1)}, u32[]{:S(2)}, u32[]{:S(2)}) collective-permute-start(bf16[32,32,1024]{2,1,0:T(8,128)(2,1)S(1)} %bitcast.107), channel_id=1, source_target_pairs={{0,1},{1,0},{2,3},{3,2},{4,5},{5,4},{6,7},{7,6},{8,9},{9,8},{10,11... | collective-permute-start | bytes 6291464 | tf_op jit(solution)/shard_map/ppermute | solution.py:37
  119.5 3.3 %fusion.15 = bf16[1,560,1024]{2,1,0:T(8,128)(2,1)S(1)} fusion(bf16[560,1024]{1,0:T(8,128)(2,1)} %reshape.257, bf16[1024,1024]{1,0:T(8,128)(2,1)} %bitcast.113), kind=kOutput, calls=%fused_computation.16 | convolution fusion | flops 1174978560 | bytes 4390912 | tf_op jit(solution)/shard_map/dot_general | solution.py:246
  128.7 3.5 %fusion.78 = (f32[8,128]{1,0:T(8,128)S(1)}, f32[8,128,560]{1,2,0:T(8,128)}) fusion(pred[128,560]{0,1:T(8,128)(4,1)} %fusion.47, bf16[128,8,64]{0,2,1:T(8,128)(2,1)S(1)} %bitcast.133, bf16[560,8,64]{0,2,1:T(8,128)(2,1)} %bitcast.122), kind=kOutput, calls=%fused_computation.131 | convolution fusion | flops 75694640 | bytes 3074048 | tf_op jit(solution)/shard_map/sub | solution.py:160
  132.2 3.6 %fusion.79 = (bf16[1,560,8,64]{1,3,2,0:T(8,128)(2,1)}, f32[1,560,8,64]{1,3,2,0:T(8,128)}) fusion(bf16[128,8,64]{0,2,1:T(8,128)(2,1)S(1)} %bitcast.130, f32[8,128]{1,0:T(8,128)S(1)} %get-tuple-element.23, pred[128,560]{0,1:T(8,128)(4,1)} %fusion.47, bf16[128,8,64]{0,2,1:T(8,128)(2,1)S(1)} %bitcast.134, bf16[560,8,64]{0,2,1:T(8,128)(2,1)} %bitcast.123), kind=kOutput, calls=%fused_computation.132 | convolution fusion | flops 149956144 | bytes 2631680 | tf_op jit(solution)/shard_map/bhqk,bqhd->bkhd/dot_general | solution.py:187
  135.8 5.9 %fusion.80 = (bf16[1,560,8,64]{1,3,2,0:T(8,128)(2,1)}, f32[1,560,8,64]{1,3,2,0:T(8,128)}) fusion(bf16[128,8,64]{0,2,1:T(8,128)(2,1)S(1)} %bitcast.135, f32[8,128,560]{1,2,0:T(8,128)} %fusion.83, f32[8,128,560]{1,2,0:T(8,128)} %get-tuple-element.24, f32[8,128]{1,0:T(8,128)S(1)} %get-tuple-element.23), kind=kOutput, calls=%fused_computation.133 | convolution fusion | flops 77702704 | bytes 6443008 | tf_op jit(solution)/shard_map/bhqk,bqhd->bkhd/dot_general | solution.py:184
  153.3 3.0 copy.25
  156.4 2.8 concatenate.25
  159.2 3.0 copy.24
  162.2 3.6 %concatenate.24 = f32[1,20,28,512]{3,0,2,1:T(1,128)} reshape(f32[1,560,8,64]{3,2,0,1:T(8,128)} %copy.24) | data formatting | bytes 2293760 | tf_op jit(solution)/shard_map/concatenate | solution.py:191
  169.5 2.9 bitcast_add_fusion
  178.4 5.0 %collective-permute-start.12 = (f32[1,20,6,1024]{3,0,2,1:T(1,128)}, f32[1,20,6,1024]{3,0,2,1:T(1,128)}, u32[]{:S(2)}, u32[]{:S(2)}) collective-permute-start(f32[1,20,6,1024]{3,0,2,1:T(1,128)} %get-tuple-element.13), channel_id=1, source_target_pairs={{0,1},{1,2},{2,3},{3,4},{4,5},{5,6},{6,7},{7,8},{8,9},{9,10},{10,1... | collective-permute-start | bytes 1474568 | tf_op jit(solution)/shard_map/ppermute | solution.py:19
  188.0 22.5 %collective-permute-done.12 = f32[1,20,6,1024]{3,0,2,1:T(1,128)} collective-permute-done((f32[1,20,6,1024]{3,0,2,1:T(1,128)}, f32[1,20,6,1024]{3,0,2,1:T(1,128)}, u32[]{:S(2)}, u32[]{:S(2)}) %collective-permute-start.12) | collective-permute-done | bytes 491552 | tf_op jit(solution)/shard_map/ppermute | solution.py:19
  220.8 3.4 %collective-permute-start.14 = (f32[1,6,16,1024]{3,0,2,1:T(1,128)}, f32[1,6,16,1024]{3,0,2,1:T(1,128)S(1)}, u32[]{:S(2)}, u32[]{:S(2)}) collective-permute-start(f32[1,6,16,1024]{3,0,2,1:T(1,128)} %get-tuple-element.15), channel_id=1, source_target_pairs={{0,16},{16,32},{32,48},{48,64},{64,80},{80,96},{96,112},{112,128},... | collective-permute-start | bytes 1179656 | tf_op jit(solution)/shard_map/ppermute | solution.py:19
  225.5 4.8 %fusion.19 = bf16[8,64,128]{2,1,0:T(8,128)(2,1)S(1)} fusion(bf16[560,8,64]{0,2,1:T(8,128)(2,1)} %bitcast.125, f32[8,128,560]{1,2,0:T(8,128)} %fusion.83, f32[8,128,560]{1,2,0:T(8,128)} %get-tuple-element.24, f32[8,128]{1,0:T(8,128)S(1)} %get-tuple-element.23), kind=kOutput, calls=%fused_computation.24 | convolution fusion | flops 77481520 | bytes 5296128 | tf_op jit(solution)/shard_map/bhqk,bkhd->bqhd/dot_general | solution.py:181
  231.5 7.6 %collective-permute-start.17 = (f32[2,2,1,1,1,1,32,512]{7,6,5,4,3,2,1,0:T(8,128)S(1)}, f32[2,2,1,1,1,1,32,512]{7,6,5,4,3,2,1,0:T(8,128)S(1)}, u32[]{:S(2)}, u32[]{:S(2)}) collective-permute-start(f32[2,2,1,1,1,1,32,512]{7,6,5,4,3,2,1,0:T(8,128)S(1)} %constant_dynamic-slice_fusion.2), channel_id=1, source_target_pairs={{0,64},{16,80},{32,96},{48,112},{64,0},{80,16},{96,32},{112,48},{1... | collective-permute-start | bytes 786440 | tf_op jit(solution)/shard_map/ppermute | solution.py:37
  241.0 6.4 %collective-permute-done.17 = f32[2,2,1,1,1,1,32,512]{7,6,5,4,3,2,1,0:T(8,128)S(1)} collective-permute-done((f32[2,2,1,1,1,1,32,512]{7,6,5,4,3,2,1,0:T(8,128)S(1)}, f32[2,2,1,1,1,1,32,512]{7,6,5,4,3,2,1,0:T(8,128)S(1)}, u32[]{:S(2)}, u32[]{:S(2)}) %collective-permute-start.17) | collective-permute-done | bytes 262176 | tf_op jit(solution)/shard_map/ppermute | solution.py:37
  247.5 5.4 %collective-permute-start.18 = (f32[2,1,1,1,1,1,32,512]{7,6,5,4,3,2,1,0:T(8,128)S(1)}, f32[2,1,1,1,1,1,32,512]{7,6,5,4,3,2,1,0:T(8,128)S(1)}, u32[]{:S(2)}, u32[]{:S(2)}) collective-permute-start(f32[2,1,1,1,1,1,32,512]{7,6,5,4,3,2,1,0:T(8,128)S(1)} %constant_dynamic-slice_fusion.1), channel_id=1, source_target_pairs={{0,128},{16,144},{32,160},{48,176},{64,192},{80,208},{96,224},{112... | collective-permute-start | bytes 393224 | tf_op jit(solution)/shard_map/ppermute | solution.py:37
  253.8 8.9 %collective-permute-done.18 = f32[2,1,1,1,1,1,32,512]{7,6,5,4,3,2,1,0:T(8,128)S(1)} collective-permute-done((f32[2,1,1,1,1,1,32,512]{7,6,5,4,3,2,1,0:T(8,128)S(1)}, f32[2,1,1,1,1,1,32,512]{7,6,5,4,3,2,1,0:T(8,128)S(1)}, u32[]{:S(2)}, u32[]{:S(2)}) %collective-permute-start.18) | collective-permute-done | bytes 131104 | tf_op jit(solution)/shard_map/ppermute | solution.py:37
  262.7 4.7 %collective-permute-start.19 = (f32[1,1,1,1,1,1,32,512]{7,6,5,4,3,2,1,0:T(8,128)S(1)}, f32[1,1,1,1,1,1,32,512]{7,6,5,4,3,2,1,0:T(8,128)S(1)}, u32[]{:S(2)}, u32[]{:S(2)}) collective-permute-start(f32[1,1,1,1,1,1,32,512]{7,6,5,4,3,2,1,0:T(8,128)S(1)} %constant_dynamic-slice_fusion), channel_id=1, source_target_pairs={{0,256},{16,272},{32,288},{48,304},{64,320},{80,336},{96,352},{112... | collective-permute-start | bytes 196616 | tf_op jit(solution)/shard_map/ppermute | solution.py:37
  268.0 10.5 %collective-permute-done.19 = f32[1,1,1,1,1,1,32,512]{7,6,5,4,3,2,1,0:T(8,128)S(1)} collective-permute-done((f32[1,1,1,1,1,1,32,512]{7,6,5,4,3,2,1,0:T(8,128)S(1)}, f32[1,1,1,1,1,1,32,512]{7,6,5,4,3,2,1,0:T(8,128)S(1)}, u32[]{:S(2)}, u32[]{:S(2)}) %collective-permute-start.19) | collective-permute-done | bytes 65568 | tf_op jit(solution)/shard_map/ppermute | solution.py:37
  280.6 4.3 %collective-permute-done.20 = f32[32,512]{1,0:T(8,128)S(1)} collective-permute-done((f32[32,512]{1,0:T(8,128)S(1)}, f32[32,512]{1,0:T(8,128)S(1)}, u32[]{:S(2)}, u32[]{:S(2)}) %collective-permute-start.20) | collective-permute-done | bytes 65568 | tf_op jit(solution)/shard_map/ppermute | solution.py:37
  285.0 5.7 %collective-permute-start.21 = (f32[32,512]{1,0:T(8,128)S(1)}, f32[32,512]{1,0:T(8,128)S(1)}, u32[]{:S(2)}, u32[]{:S(2)}) collective-permute-start(f32[32,512]{1,0:T(8,128)S(1)} %add.344), channel_id=1, source_target_pairs={{0,4},{1,5},{2,6},{3,7},{4,0},{5,1},{6,2},{7,3},{8,12},{9,13},{10,... | collective-permute-start | bytes 196616 | tf_op jit(solution)/shard_map/ppermute | solution.py:37
  292.3 4.9 %collective-permute-start.22 = (f32[32,512]{1,0:T(8,128)S(1)}, f32[32,512]{1,0:T(8,128)S(1)}, u32[]{:S(2)}, u32[]{:S(2)}) collective-permute-start(f32[32,512]{1,0:T(8,128)S(1)} %add.345), channel_id=1, source_target_pairs={{0,8},{1,9},{2,10},{3,11},{4,12},{5,13},{6,14},{7,15},{8,0},{9,1},... | collective-permute-start | bytes 196616 | tf_op jit(solution)/shard_map/ppermute | solution.py:37
  298.9 8.1 %collective-permute-start.23 = (f32[32,512]{1,0:T(8,128)S(1)}, f32[32,512]{1,0:T(8,128)S(1)}, u32[]{:S(2)}, u32[]{:S(2)}) collective-permute-start(f32[32,512]{1,0:T(8,128)S(1)} %add.346), channel_id=1, source_target_pairs={{0,1},{1,0},{2,3},{3,2},{4,5},{5,4},{6,7},{7,6},{8,9},{9,8},{10,11... | collective-permute-start | bytes 196616 | tf_op jit(solution)/shard_map/ppermute | solution.py:37
  (144 shorter events, 90.7 us)
Async XLA Ops:
  0.7 17.6 %copy-start = (bf16[1,8,16,1024]{3,2,1,0:T(8,128)(2,1)S(1)}, bf16[1,8,16,1024]{3,2,1,0:T(8,128)(2,1)}, u32[]{:S(2)}) copy-start(bf16[1,8,16,1024]{3,2,1,0:T(8,128)(2,1)} %param.6) | copy-start | bytes 786436
  0.7 17.9 %copy-start.15 = (f32[1024]{0:T(1024)S(1)}, f32[1024]{0:T(1024)}, u32[]{:S(2)}) copy-start(f32[1024]{0:T(1024)} %param.7) | copy-start | bytes 12292
  2.0 21.5 %collective-permute-start = (bf16[1,1,1,1,1,32,1024]{6,5,4,3,2,1,0:T(8,128)(2,1)S(1)}, bf16[1,1,1,1,1,32,1024]{6,5,4,3,2,1,0:T(8,128)(2,1)S(1)}, u32[]{:S(2)}, u32[]{:S(2)}) collective-permute-start(bf16[1,1,1,1,1,32,1024]{6,5,4,3,2,1,0:T(8,128)(2,1)S(1)} %constant_dynamic-slice_fusion.9), channel_id=1, source_target_pairs={{0,256},{16,272},{32,288},{48,304},{64,320},{80,336},{96,352},{112... | collective-permute-start | bytes 196616 | tf_op jit(solution)/shard_map/ppermute | solution.py:37
  18.9 11.5 %collective-permute-start.3 = (bf16[1,6,16,1024]{3,2,1,0:T(8,128)(2,1)S(1)}, bf16[1,6,16,1024]{3,2,1,0:T(8,128)(2,1)S(1)}, u32[]{:S(2)}, u32[]{:S(2)}) collective-permute-start(bf16[1,6,16,1024]{3,2,1,0:T(8,128)(2,1)S(1)} %get-tuple-element.21), channel_id=1, source_target_pairs={{0,16},{16,32},{32,48},{48,64},{64,80},{80,96},{96,112},{112,128},... | collective-permute-start | bytes 589832 | tf_op jit(solution)/shard_map/ppermute | solution.py:27
  22.1 8.3 %collective-permute-start.4 = (bf16[1,6,16,1024]{3,2,1,0:T(8,128)(2,1)S(1)}, bf16[1,6,16,1024]{3,2,1,0:T(8,128)(2,1)S(1)}, u32[]{:S(2)}, u32[]{:S(2)}) collective-permute-start(bf16[1,6,16,1024]{3,2,1,0:T(8,128)(2,1)S(1)} %get-tuple-element.22), channel_id=1, source_target_pairs={{16,0},{32,16},{48,32},{64,48},{80,64},{96,80},{112,96},{128,112},... | collective-permute-start | bytes 589832 | tf_op jit(solution)/shard_map/ppermute | solution.py:30
  23.5 19.5 %collective-permute-start.1 = (bf16[2,1,1,1,1,32,1024]{6,5,4,3,2,1,0:T(8,128)(2,1)S(1)}, bf16[2,1,1,1,1,32,1024]{6,5,4,3,2,1,0:T(8,128)(2,1)S(1)}, u32[]{:S(2)}, u32[]{:S(2)}) collective-permute-start(bf16[2,1,1,1,1,32,1024]{6,5,4,3,2,1,0:T(8,128)(2,1)S(1)} %constant_dynamic-slice_fusion.8), channel_id=1, source_target_pairs={{0,128},{16,144},{32,160},{48,176},{64,192},{80,208},{96,224},{112... | collective-permute-start | bytes 393224 | tf_op jit(solution)/shard_map/ppermute | solution.py:37
  31.5 14.5 %collective-permute-start.5 = (bf16[1,20,6,1024]{3,2,1,0:T(8,128)(2,1)}, bf16[1,20,6,1024]{3,2,1,0:T(8,128)(2,1)S(1)}, u32[]{:S(2)}, u32[]{:S(2)}) collective-permute-start(bf16[1,20,6,1024]{3,2,1,0:T(8,128)(2,1)} %get-tuple-element.19), channel_id=1, source_target_pairs={{0,1},{1,2},{2,3},{3,4},{4,5},{5,6},{6,7},{7,8},{8,9},{9,10},{10,1... | collective-permute-start | bytes 737288 | tf_op jit(solution)/shard_map/ppermute | solution.py:27
  38.0 10.2 %collective-permute-start.6 = (bf16[1,20,6,1024]{3,2,1,0:T(8,128)(2,1)}, bf16[1,20,6,1024]{3,2,1,0:T(8,128)(2,1)}, u32[]{:S(2)}, u32[]{:S(2)}) collective-permute-start(bf16[1,20,6,1024]{3,2,1,0:T(8,128)(2,1)} %get-tuple-element.20), channel_id=1, source_target_pairs={{1,0},{2,1},{3,2},{4,3},{5,4},{6,5},{7,6},{8,7},{9,8},{10,9},{11,1... | collective-permute-start | bytes 737288 | tf_op jit(solution)/shard_map/ppermute | solution.py:30
  43.7 16.1 %collective-permute-start.2 = (bf16[2,2,1,1,1,32,1024]{6,5,4,3,2,1,0:T(8,128)(2,1)}, bf16[2,2,1,1,1,32,1024]{6,5,4,3,2,1,0:T(8,128)(2,1)}, u32[]{:S(2)}, u32[]{:S(2)}) collective-permute-start(bf16[2,2,1,1,1,32,1024]{6,5,4,3,2,1,0:T(8,128)(2,1)} %constant_dynamic-slice_fusion.7), channel_id=1, source_target_pairs={{0,64},{16,80},{32,96},{48,112},{64,0},{80,16},{96,32},{112,48},{1... | collective-permute-start | bytes 786440 | tf_op jit(solution)/shard_map/ppermute | solution.py:37
  61.7 15.1 %collective-permute-start.7 = (bf16[2,2,2,1,1,32,1024]{6,5,4,3,2,1,0:T(8,128)(2,1)}, bf16[2,2,2,1,1,32,1024]{6,5,4,3,2,1,0:T(8,128)(2,1)S(1)}, u32[]{:S(2)}, u32[]{:S(2)}) collective-permute-start(bf16[2,2,2,1,1,32,1024]{6,5,4,3,2,1,0:T(8,128)(2,1)} %constant_dynamic-slice_fusion.6), channel_id=1, source_target_pairs={{0,32},{16,48},{32,0},{48,16},{64,96},{80,112},{96,64},{112,80},{1... | collective-permute-start | bytes 1572872 | tf_op jit(solution)/shard_map/ppermute | solution.py:37
  77.9 25.5 %collective-permute-start.8 = (bf16[2,2,2,2,1,32,1024]{6,5,4,3,2,1,0:T(8,128)(2,1)}, bf16[2,2,2,2,1,32,1024]{6,5,4,3,2,1,0:T(8,128)(2,1)}, u32[]{:S(2)}, u32[]{:S(2)}) collective-permute-start(bf16[2,2,2,2,1,32,1024]{6,5,4,3,2,1,0:T(8,128)(2,1)} %constant_dynamic-slice_fusion.5), channel_id=1, source_target_pairs={{0,16},{16,0},{32,48},{48,32},{64,80},{80,64},{96,112},{112,96},{1... | collective-permute-start | bytes 3145736 | tf_op jit(solution)/shard_map/ppermute | solution.py:37
  104.8 8.1 %collective-permute-start.9 = (bf16[32,32,1024]{2,1,0:T(8,128)(2,1)S(1)}, bf16[32,32,1024]{2,1,0:T(8,128)(2,1)}, u32[]{:S(2)}, u32[]{:S(2)}) collective-permute-start(bf16[32,32,1024]{2,1,0:T(8,128)(2,1)S(1)} %bitcast.107), channel_id=1, source_target_pairs={{0,1},{1,0},{2,3},{3,2},{4,5},{5,4},{6,7},{7,6},{8,9},{9,8},{10,11... | collective-permute-start | bytes 6291464 | tf_op jit(solution)/shard_map/ppermute | solution.py:37
  119.5 16.3 %copy-start.13 = (bf16[128,512]{0,1:T(8,128)(2,1)}, bf16[128,512]{0,1:T(8,128)(2,1)S(1)}, u32[]{:S(2)}) copy-start(bf16[128,512]{0,1:T(8,128)(2,1)S(1)} %copy.18) | copy-start | bytes 393220
  150.8 18.7 %collective-permute-start.10 = (f32[1024,512]{1,0:T(8,128)}, f32[1024,512]{1,0:T(8,128)}, u32[]{:S(2)}, u32[]{:S(2)}) collective-permute-start(f32[1024,512]{1,0:T(8,128)} %dynamic-slice_bitcast_fusion), channel_id=1, source_target_pairs={{0,1},{1,0},{2,3},{3,2},{4,5},{5,4},{6,7},{7,6},{8,9},{9,8},{10,11... | collective-permute-start | bytes 6291464 | tf_op jit(solution)/shard_map/ppermute | solution.py:37
  172.4 12.9 %copy-start.9 = (bf16[1,560,512]{1,2,0:T(8,128)(2,1)S(1)}, bf16[1,560,512]{1,2,0:T(8,128)(2,1)}, u32[]{:S(2)}) copy-start(bf16[1,560,512]{1,2,0:T(8,128)(2,1)} %copy-done.8) | copy-start | bytes 1720324
  172.4 12.9 %copy-start.14 = (bf16[128,512]{0,1:T(8,128)(2,1)S(1)}, bf16[128,512]{0,1:T(8,128)(2,1)}, u32[]{:S(2)}) copy-start(bf16[128,512]{0,1:T(8,128)(2,1)} %copy-done.13) | copy-start | bytes 393220
  174.8 38.6 %collective-permute-start.11 = (f32[2,2,2,2,1,1,32,512]{7,6,5,4,3,2,1,0:T(8,128)}, f32[2,2,2,2,1,1,32,512]{7,6,5,4,3,2,1,0:T(8,128)}, u32[]{:S(2)}, u32[]{:S(2)}) collective-permute-start(f32[2,2,2,2,1,1,32,512]{7,6,5,4,3,2,1,0:T(8,128)} %constant_dynamic-slice_fusion.4), channel_id=1, source_target_pairs={{0,16},{16,0},{32,48},{48,32},{64,80},{80,64},{96,112},{112,96},{1... | collective-permute-start | bytes 3145736 | tf_op jit(solution)/shard_map/ppermute | solution.py:37
  178.4 32.1 %collective-permute-start.12 = (f32[1,20,6,1024]{3,0,2,1:T(1,128)}, f32[1,20,6,1024]{3,0,2,1:T(1,128)}, u32[]{:S(2)}, u32[]{:S(2)}) collective-permute-start(f32[1,20,6,1024]{3,0,2,1:T(1,128)} %get-tuple-element.13), channel_id=1, source_target_pairs={{0,1},{1,2},{2,3},{3,4},{4,5},{5,6},{6,7},{7,8},{8,9},{9,10},{10,1... | collective-permute-start | bytes 1474568 | tf_op jit(solution)/shard_map/ppermute | solution.py:19
  183.4 27.1 %collective-permute-start.13 = (f32[1,20,6,1024]{3,0,2,1:T(1,128)}, f32[1,20,6,1024]{3,0,2,1:T(1,128)}, u32[]{:S(2)}, u32[]{:S(2)}) collective-permute-start(f32[1,20,6,1024]{3,0,2,1:T(1,128)} %get-tuple-element.14), channel_id=1, source_target_pairs={{1,0},{2,1},{3,2},{4,3},{5,4},{6,5},{7,6},{8,7},{9,8},{10,9},{11,1... | collective-permute-start | bytes 1474568 | tf_op jit(solution)/shard_map/ppermute | solution.py:19
  188.0 25.3 %copy-start.2 = (f32[1024,512]{1,0:T(8,128)S(1)}, f32[1024,512]{1,0:T(8,128)}, u32[]{:S(2)}) copy-start(f32[1024,512]{1,0:T(8,128)} %copy-done.1) | copy-start | bytes 6291460
  216.1 14.2 %collective-permute-start.16 = (f32[2,2,2,1,1,1,32,512]{7,6,5,4,3,2,1,0:T(8,128)}, f32[2,2,2,1,1,1,32,512]{7,6,5,4,3,2,1,0:T(8,128)}, u32[]{:S(2)}, u32[]{:S(2)}) collective-permute-start(f32[2,2,2,1,1,1,32,512]{7,6,5,4,3,2,1,0:T(8,128)} %constant_dynamic-slice_fusion.3), channel_id=1, source_target_pairs={{0,32},{16,48},{32,0},{48,16},{64,96},{80,112},{96,64},{112,80},{1... | collective-permute-start | bytes 1572872 | tf_op jit(solution)/shard_map/ppermute | solution.py:37
  220.8 18.2 %collective-permute-start.14 = (f32[1,6,16,1024]{3,0,2,1:T(1,128)}, f32[1,6,16,1024]{3,0,2,1:T(1,128)S(1)}, u32[]{:S(2)}, u32[]{:S(2)}) collective-permute-start(f32[1,6,16,1024]{3,0,2,1:T(1,128)} %get-tuple-element.15), channel_id=1, source_target_pairs={{0,16},{16,32},{32,48},{48,64},{64,80},{80,96},{96,112},{112,128},... | collective-permute-start | bytes 1179656 | tf_op jit(solution)/shard_map/ppermute | solution.py:19
  224.2 14.9 %collective-permute-start.15 = (f32[1,6,16,1024]{3,0,2,1:T(1,128)}, f32[1,6,16,1024]{3,0,2,1:T(1,128)}, u32[]{:S(2)}, u32[]{:S(2)}) collective-permute-start(f32[1,6,16,1024]{3,0,2,1:T(1,128)} %get-tuple-element.16), channel_id=1, source_target_pairs={{16,0},{32,16},{48,32},{64,48},{80,64},{96,80},{112,96},{128,112},... | collective-permute-start | bytes 1179656 | tf_op jit(solution)/shard_map/ppermute | solution.py:19
  231.5 21.4 %copy-start.3 = (bf16[1,32,32,1024]{3,2,1,0:T(8,128)(2,1)S(1)}, bf16[1,32,32,1024]{3,2,1,0:T(8,128)(2,1)}, u32[]{:S(2)}) copy-start(bf16[1,32,32,1024]{3,2,1,0:T(8,128)(2,1)} %slice.66) | copy-start | bytes 6291460
  231.5 15.9 %collective-permute-start.17 = (f32[2,2,1,1,1,1,32,512]{7,6,5,4,3,2,1,0:T(8,128)S(1)}, f32[2,2,1,1,1,1,32,512]{7,6,5,4,3,2,1,0:T(8,128)S(1)}, u32[]{:S(2)}, u32[]{:S(2)}) collective-permute-start(f32[2,2,1,1,1,1,32,512]{7,6,5,4,3,2,1,0:T(8,128)S(1)} %constant_dynamic-slice_fusion.2), channel_id=1, source_target_pairs={{0,64},{16,80},{32,96},{48,112},{64,0},{80,16},{96,32},{112,48},{1... | collective-permute-start | bytes 786440 | tf_op jit(solution)/shard_map/ppermute | solution.py:37
  247.5 15.1 %collective-permute-start.18 = (f32[2,1,1,1,1,1,32,512]{7,6,5,4,3,2,1,0:T(8,128)S(1)}, f32[2,1,1,1,1,1,32,512]{7,6,5,4,3,2,1,0:T(8,128)S(1)}, u32[]{:S(2)}, u32[]{:S(2)}) collective-permute-start(f32[2,1,1,1,1,1,32,512]{7,6,5,4,3,2,1,0:T(8,128)S(1)} %constant_dynamic-slice_fusion.1), channel_id=1, source_target_pairs={{0,128},{16,144},{32,160},{48,176},{64,192},{80,208},{96,224},{112... | collective-permute-start | bytes 393224 | tf_op jit(solution)/shard_map/ppermute | solution.py:37
  253.7 53.2 %copy-start.12 = (bf16[1,8,16,1024]{3,2,1,0:T(8,128)(2,1)S(1)}, bf16[1,8,16,1024]{3,2,1,0:T(8,128)(2,1)}, u32[]{:S(2)}) copy-start(bf16[1,8,16,1024]{3,2,1,0:T(8,128)(2,1)} %param.11) | copy-start | bytes 786436
  262.7 15.7 %collective-permute-start.19 = (f32[1,1,1,1,1,1,32,512]{7,6,5,4,3,2,1,0:T(8,128)S(1)}, f32[1,1,1,1,1,1,32,512]{7,6,5,4,3,2,1,0:T(8,128)S(1)}, u32[]{:S(2)}, u32[]{:S(2)}) collective-permute-start(f32[1,1,1,1,1,1,32,512]{7,6,5,4,3,2,1,0:T(8,128)S(1)} %constant_dynamic-slice_fusion), channel_id=1, source_target_pairs={{0,256},{16,272},{32,288},{48,304},{64,320},{80,336},{96,352},{112... | collective-permute-start | bytes 196616 | tf_op jit(solution)/shard_map/ppermute | solution.py:37
  278.4 6.5 %collective-permute-start.20 = (f32[32,512]{1,0:T(8,128)S(1)}, f32[32,512]{1,0:T(8,128)S(1)}, u32[]{:S(2)}, u32[]{:S(2)}) collective-permute-start(f32[32,512]{1,0:T(8,128)S(1)} %add_bitcast_fusion), channel_id=1, source_target_pairs={{0,2},{1,3},{2,0},{3,1},{4,6},{5,7},{6,4},{7,5},{8,10},{9,11},{10,... | collective-permute-start | bytes 196616 | tf_op jit(solution)/shard_map/ppermute | solution.py:37
  285.0 7.3 %collective-permute-start.21 = (f32[32,512]{1,0:T(8,128)S(1)}, f32[32,512]{1,0:T(8,128)S(1)}, u32[]{:S(2)}, u32[]{:S(2)}) collective-permute-start(f32[32,512]{1,0:T(8,128)S(1)} %add.344), channel_id=1, source_target_pairs={{0,4},{1,5},{2,6},{3,7},{4,0},{5,1},{6,2},{7,3},{8,12},{9,13},{10,... | collective-permute-start | bytes 196616 | tf_op jit(solution)/shard_map/ppermute | solution.py:37
  292.3 6.5 %collective-permute-start.22 = (f32[32,512]{1,0:T(8,128)S(1)}, f32[32,512]{1,0:T(8,128)S(1)}, u32[]{:S(2)}, u32[]{:S(2)}) collective-permute-start(f32[32,512]{1,0:T(8,128)S(1)} %add.345), channel_id=1, source_target_pairs={{0,8},{1,9},{2,10},{3,11},{4,12},{5,13},{6,14},{7,15},{8,0},{9,1},... | collective-permute-start | bytes 196616 | tf_op jit(solution)/shard_map/ppermute | solution.py:37
  298.9 9.8 %collective-permute-start.23 = (f32[32,512]{1,0:T(8,128)S(1)}, f32[32,512]{1,0:T(8,128)S(1)}, u32[]{:S(2)}, u32[]{:S(2)}) collective-permute-start(f32[32,512]{1,0:T(8,128)S(1)} %add.346), channel_id=1, source_target_pairs={{0,1},{1,0},{2,3},{3,2},{4,5},{5,4},{6,7},{7,6},{8,9},{9,8},{10,11... | collective-permute-start | bytes 196616 | tf_op jit(solution)/shard_map/ppermute | solution.py:37
  (10 other events, 33.3 us)
